TPU v7x, 32 devices: a whole 2x2x4 slice. The times are simulated.
32 devices in a mesh: gx: 8 (over z, x), gy: 4 (over y, core).
Axes of the slice: x: 2, y: 2, z: 4, core: 2. Of those that a mesh axis runs over, the one named last changes fastest.
Arguments:
- patches: bfloat16 [128, 64, 256], P('gx', 'gy'), may hold values from -9 to 9
- w_query: bfloat16 [256, 256], replicated, may hold values from -2 to 2
- w_key: bfloat16 [256, 256], replicated, may hold values from -2 to 2
- w_value: bfloat16 [256, 256], replicated, may hold values from -0.375 to 0.375
- w_out: bfloat16 [256, 256], replicated, may hold values from -0.375 to 0.375
- region_memory: bfloat16 [8, 4, 4, 64, 512], P('gx', 'gy'), may hold values from -6 to 6
- region_owner: int32 [8, 4, 4, 2], P('gx', 'gy'), may hold values from 0 to 7, all different within a row; in each aligned block of 4 rows (0 to 3, 4 to 7, ..., all dimensions but the last counted through in order) at most 2 rows name the same one
- region_local: int32 [8, 4, 4, 2], P('gx', 'gy'), may hold values from 0 to 3
- grad_out: bfloat16 [128, 64, 256], P('gx', 'gy'), may hold values from -6 to 6
Outputs:
- layer_out: bfloat16 [128, 64, 256], P('gx', 'gy')
- grad_patches: bfloat16 [128, 64, 256], P('gx', 'gy')
- grad_w_query: float32 [256, 256], replicated
- grad_w_key: float32 [256, 256], replicated
- grad_w_value: float32 [256, 256], replicated
- grad_w_out: float32 [256, 256], replicated
Inputs may be any that keep to these rules, and one draw needn't show every extreme that they name: `region_owner`: each block names two different owner tiles. The blocks of one tile name one owner at most 2 times, a bound that some tile reaches.
All inputs are finite; a program needn't handle non-finite values.
Results may differ from a plain program's by a relative error of at most 0.02.
Values may be sent and summed in bfloat16 or wider, within the bound.
No kernel may reach another device: no remote copies, remote signals or barrier semaphores. Data moves between devices by JAX's collectives and lax.ppermute only.
A program may use at most 64 MiB of HBM per device.

v0:
```python
import math

import jax
import jax.numpy as jnp
from jax import lax
from jax.sharding import PartitionSpec as P

D = 256
HEADS = 2
HEAD_DIM = 128
BSIDE = 8
BT = 64


masked_score = -1000000000.0


def padded(block, sides, width):
    for axis, dim in sides:
        count = lax.axis_size(axis)
        forward = [(i, i + 1) for i in range(count - 1)]
        backward = [(target, source) for source, target in forward]
        low = lax.ppermute(
            lax.slice_in_dim(block, block.shape[dim] - width, None, axis=dim), axis, forward
        )
        high = lax.ppermute(lax.slice_in_dim(block, 0, width, axis=dim), axis, backward)
        block = jnp.concatenate([low, block, high], axis=dim)
    return block


def to_blocks(grid_array):
    grid_rows, grid_cols, feature_width = grid_array.shape
    shaped = grid_array.reshape(grid_rows // BSIDE, BSIDE, grid_cols // BSIDE, BSIDE, feature_width)
    return shaped.transpose(0, 2, 1, 3, 4).reshape(
        grid_rows // BSIDE, grid_cols // BSIDE, BSIDE * BSIDE, feature_width
    )


def from_blocks(block_array):
    block_rows, block_cols, block_tokens, feature_width = block_array.shape
    shaped = block_array.reshape(block_rows, block_cols, BSIDE, BSIDE, feature_width)
    return shaped.transpose(0, 2, 1, 3, 4).reshape(
        block_rows * BSIDE, block_cols * BSIDE, feature_width
    )


def split_heads(source):
    return source.reshape(source.shape[:-1] + (HEADS, source.shape[-1] // HEADS))


def key_pieces(keyval_pad, key_valid, region_keyval):
    block_rows, block_cols = (region_keyval.shape[0], region_keyval.shape[1])
    pieces = []
    for row_off in range(3):
        for col_off in range(3):
            key_block = keyval_pad[row_off : row_off + block_rows, col_off : col_off + block_cols]
            valid_mask = key_valid[row_off : row_off + block_rows, col_off : col_off + block_cols]
            pieces.append((key_block[..., :D], key_block[..., D:], valid_mask))
    merged = region_keyval.reshape(block_rows, block_cols, 2 * BT, 2 * D)
    pieces.append(
        (merged[..., :D], merged[..., D:], jnp.ones((block_rows, block_cols), dtype=jnp.bool_))
    )
    return pieces


def piece_scores(query_heads, key_part, valid_mask):
    scores = jnp.einsum(
        "abqhe,abkhe->abhqk", query_heads, split_heads(key_part), preferred_element_type=jnp.float32
    )
    scores = scores * (1.0 / math.sqrt(HEAD_DIM))
    return jnp.where(valid_mask[:, :, None, None, None], scores, masked_score)


def attend_forward(query_blocks, keyval_pad, key_valid, region_keyval):
    query_heads = split_heads(query_blocks)
    pieces = key_pieces(keyval_pad, key_valid, region_keyval)
    scores = [
        piece_scores(query_heads, key_part, valid_mask)
        for key_part, value_part, valid_mask in pieces
    ]
    row_top = jnp.max(jnp.concatenate(scores, -1), -1, keepdims=True)
    row_total = sum(
        (jnp.sum(jnp.exp(part_scores - row_top), -1, keepdims=True) for part_scores in scores)
    )
    log_total = row_top + jnp.log(row_total)
    mixed_sum = jnp.zeros(query_heads.shape, jnp.float32)
    for part_scores, (key_part, value_part, valid_mask) in zip(scores, pieces):
        weights = jnp.exp(part_scores - log_total).astype(jnp.bfloat16)
        mixed_sum = mixed_sum + jnp.einsum(
            "abhqk,abkhe->abqhe",
            weights,
            split_heads(value_part),
            preferred_element_type=jnp.float32,
        )
    output = mixed_sum.reshape(query_blocks.shape).astype(jnp.bfloat16)
    return (output, log_total[..., 0])


def query_grads(
    query_blocks, keyval_pad, key_valid, region_keyval, log_total, dout_blocks, delta_rows
):
    query_heads = split_heads(query_blocks)
    dout_heads = split_heads(dout_blocks)
    accum_sum = jnp.zeros(query_heads.shape, jnp.float32)
    for key_part, value_part, valid_mask in key_pieces(keyval_pad, key_valid, region_keyval):
        part_scores = piece_scores(query_heads, key_part, valid_mask)
        prob_part = jnp.exp(part_scores - log_total[..., None])
        grad_prob = jnp.einsum(
            "abqhe,abkhe->abhqk",
            dout_heads,
            split_heads(value_part),
            preferred_element_type=jnp.float32,
        )
        grad_score = (prob_part * (grad_prob - delta_rows[..., None])).astype(jnp.bfloat16)
        accum_sum = accum_sum + jnp.einsum(
            "abhqk,abkhe->abqhe",
            grad_score,
            split_heads(key_part),
            preferred_element_type=jnp.float32,
        )
    return (
        (accum_sum * (1.0 / math.sqrt(HEAD_DIM))).reshape(query_blocks.shape).astype(jnp.bfloat16)
    )


def key_grads(keyval_center, query_pad, dout_pad, log_pad, delta_pad, query_valid):
    block_rows, block_cols = (keyval_center.shape[0], keyval_center.shape[1])
    key_heads = split_heads(keyval_center[..., :D])
    value_heads = split_heads(keyval_center[..., D:])
    grad_key = jnp.zeros(key_heads.shape, jnp.float32)
    grad_value = jnp.zeros(key_heads.shape, jnp.float32)
    for row_off in range(3):
        for col_off in range(3):
            query_heads = split_heads(
                query_pad[row_off : row_off + block_rows, col_off : col_off + block_cols]
            )
            dout_heads = split_heads(
                dout_pad[row_off : row_off + block_rows, col_off : col_off + block_cols]
            )
            log_part = log_pad[row_off : row_off + block_rows, col_off : col_off + block_cols]
            delta_part = delta_pad[row_off : row_off + block_rows, col_off : col_off + block_cols]
            valid_mask = query_valid[row_off : row_off + block_rows, col_off : col_off + block_cols]
            part_scores = jnp.einsum(
                "abqhe,abkhe->abhqk", query_heads, key_heads, preferred_element_type=jnp.float32
            )
            part_scores = part_scores * (1.0 / math.sqrt(HEAD_DIM))
            prob_part = jnp.where(
                valid_mask[:, :, None, None, None], jnp.exp(part_scores - log_part[..., None]), 0.0
            )
            grad_prob = jnp.einsum(
                "abqhe,abkhe->abhqk", dout_heads, value_heads, preferred_element_type=jnp.float32
            )
            grad_score = (prob_part * (grad_prob - delta_part[..., None])).astype(jnp.bfloat16)
            grad_key = grad_key + jnp.einsum(
                "abhqk,abqhe->abkhe", grad_score, query_heads, preferred_element_type=jnp.float32
            )
            rounded_prob = prob_part.astype(jnp.bfloat16)
            grad_value = grad_value + jnp.einsum(
                "abhqk,abqhe->abkhe", rounded_prob, dout_heads, preferred_element_type=jnp.float32
            )
    out_shape = (block_rows, block_cols, BT, D)
    grad_key = (grad_key * (1.0 / math.sqrt(HEAD_DIM))).reshape(out_shape).astype(jnp.bfloat16)
    return (grad_key, grad_value.reshape(out_shape).astype(jnp.bfloat16))


def inner_rows(left_rows, right_rows):
    return lax.dot_general(
        left_rows, right_rows, (((0,), (0,)), ((), ())), preferred_element_type=jnp.float32
    )


def on_device(
    patches, w_query, w_key, w_value, w_out, region_memory, region_owner, region_local, grad_out
):
    tile_rows, tile_cols, model_width = patches.shape
    block_rows, block_cols = (tile_rows // BSIDE, tile_cols // BSIDE)
    block_count = block_rows * block_cols
    flat_in = patches.reshape(-1, model_width)
    w_pair = jnp.concatenate([w_key, w_value], 1)
    queries = jnp.dot(flat_in, w_query, preferred_element_type=jnp.float32).astype(jnp.bfloat16)
    keyvals = jnp.dot(flat_in, w_pair, preferred_element_type=jnp.float32).astype(jnp.bfloat16)
    keyvals = keyvals.reshape(tile_rows, tile_cols, 2 * model_width)
    keyval_grid = padded(keyvals, (("gx", 0), ("gy", 1)), BSIDE)
    keyval_pad = to_blocks(keyval_grid)
    gx_count = lax.axis_size("gx")
    gy_count = lax.axis_size("gy")
    row_ids = lax.axis_index("gx") * block_rows - 1 + jnp.arange(block_rows + 2, dtype=jnp.int32)
    col_ids = lax.axis_index("gy") * block_cols - 1 + jnp.arange(block_cols + 2, dtype=jnp.int32)
    row_valid = (row_ids >= 0) & (row_ids < block_rows * gx_count)
    col_valid = (col_ids >= 0) & (col_ids < block_cols * gy_count)
    key_valid = row_valid[:, None] & col_valid[None, :]
    owners = region_owner.reshape(2 * block_count)
    local_ids = region_local.reshape(2 * block_count)
    memory_local = region_memory.reshape(
        region_memory.shape[2], region_memory.shape[3], region_memory.shape[4]
    )
    region_count = memory_local.shape[0]
    row_tables = lax.all_gather(memory_local, "gx", axis=0, tiled=True)
    fetched = jnp.take(row_tables, owners * region_count + local_ids, axis=0)
    region_keyval = fetched.reshape(
        block_rows, block_cols, 2, memory_local.shape[1], memory_local.shape[2]
    )
    query_blocks = to_blocks(queries.reshape(tile_rows, tile_cols, model_width))
    outputs, log_totals = attend_forward(query_blocks, keyval_pad, key_valid, region_keyval)
    attended = from_blocks(outputs).reshape(-1, model_width)
    layer_out = jnp.dot(attended, w_out, preferred_element_type=jnp.float32).astype(jnp.bfloat16)
    grad_flat = grad_out.reshape(-1, model_width)
    d_attended = jnp.dot(grad_flat, w_out.T, preferred_element_type=jnp.float32).astype(
        jnp.bfloat16
    )
    grad_out_local = inner_rows(attended, grad_flat)
    dout_blocks = to_blocks(d_attended.reshape(tile_rows, tile_cols, model_width))
    delta_rows = jnp.sum(
        split_heads(dout_blocks).astype(jnp.float32) * split_heads(outputs).astype(jnp.float32), -1
    )
    delta_rows = delta_rows.transpose(0, 1, 3, 2)
    d_queries = query_grads(
        query_blocks, keyval_pad, key_valid, region_keyval, log_totals, dout_blocks, delta_rows
    )
    query_grid = jnp.concatenate(
        [
            queries.reshape(tile_rows, tile_cols, model_width),
            d_attended.reshape(tile_rows, tile_cols, model_width),
        ],
        -1,
    )
    query_halo = padded(query_grid, (("gx", 0), ("gy", 1)), BSIDE)
    stat_grid = from_blocks(jnp.concatenate([log_totals, delta_rows], 2).transpose(0, 1, 3, 2))
    stat_halo = padded(stat_grid, (("gx", 0), ("gy", 1)), BSIDE)
    query_all = to_blocks(query_halo)
    stat_pad = to_blocks(stat_halo).transpose(0, 1, 3, 2)
    d_keys, d_values = key_grads(
        keyval_pad[1:-1, 1:-1],
        query_all[..., :model_width],
        query_all[..., model_width:],
        stat_pad[:, :, :HEADS],
        stat_pad[:, :, HEADS:],
        key_valid,
    )
    dq_flat = from_blocks(d_queries).reshape(-1, model_width)
    dk_flat = from_blocks(d_keys).reshape(-1, model_width)
    dv_flat = from_blocks(d_values).reshape(-1, model_width)
    grads_joined = jnp.concatenate([dq_flat, dk_flat, dv_flat], 1)
    w_stacked = jnp.concatenate([w_query.T, w_key.T, w_value.T], 0)
    grad_patches = jnp.dot(grads_joined, w_stacked, preferred_element_type=jnp.float32).astype(
        jnp.bfloat16
    )
    summed = lax.psum(
        (
            inner_rows(flat_in, dq_flat),
            inner_rows(flat_in, dk_flat),
            inner_rows(flat_in, dv_flat),
            grad_out_local,
        ),
        ("gx", "gy"),
    )
    return (
        layer_out.reshape(tile_rows, tile_cols, model_width),
        grad_patches.reshape(tile_rows, tile_cols, model_width),
        summed[0],
        summed[1],
        summed[2],
        summed[3],
    )


def solution(mesh):
    return jax.shard_map(
        on_device,
        mesh=mesh,
        in_specs=(
            P("gx", "gy", None),
            P(),
            P(),
            P(),
            P(),
            P("gx", "gy", None, None, None),
            P("gx", "gy", None, None),
            P("gx", "gy", None, None),
            P("gx", "gy", None),
        ),
        out_specs=(P("gx", "gy", None), P("gx", "gy", None), P(), P(), P(), P()),
        check_vma=False,
    )
```

profile of v0, /device:TPU:0, one launch (start us, length us, event | category | flops | bytes accessed | tf_op | source)
XLA Modules:
  0.0 271.7 jit_solution(11771590287470757042)
XLA Ops:
  8.1 1.2 convolution_convert_fusion
  9.3 1.3 collective-permute-start.1
  10.6 5.5 %collective-permute-start = (bf16[8,16,512]{2,1,0:T(8,128)(2,1)S(1)}, bf16[8,16,512]{2,1,0:T(8,128)(2,1)S(1)}, u32[]{:S(2)}, u32[]{:S(2)}) collective-permute-start(bf16[8,16,512]{2,1,0:T(8,128)(2,1)S(1)} %bitcast.503), channel_id=1, source_target_pairs={{0,4},{4,8},{8,12},{12,16},{16,20},{20,24},{24,28},{1,5},{5,9},{9,... | collective-permute-start | bytes 393224 | tf_op jit(solution)/shard_map/ppermute | solution.py:23
  16.1 1.1 convolution_convert_fusion.4
  17.2 1.2 convolution_convert_fusion.2
  18.4 4.8 %collective-permute-start.4 = (bf16[8,16,512]{2,1,0:T(8,128)(2,1)S(1)}, bf16[8,16,512]{2,1,0:T(8,128)(2,1)S(1)}, u32[]{:S(2)}, u32[]{:S(2)}) collective-permute-start(bf16[8,16,512]{2,1,0:T(8,128)(2,1)S(1)} %get-tuple-element.85), channel_id=1, source_target_pairs={{0,4},{4,8},{8,12},{12,16},{16,20},{20,24},{24,28},{1,5},{5,9},{9,... | collective-permute-start | bytes 393224 | tf_op jit(solution)/shard_map/ppermute | solution.py:23
  23.2 1.3 collective-permute-start.5
  25.1 3.5 %collective-permute-done.4 = bf16[8,16,512]{2,1,0:T(8,128)(2,1)S(1)} collective-permute-done((bf16[8,16,512]{2,1,0:T(8,128)(2,1)S(1)}, bf16[8,16,512]{2,1,0:T(8,128)(2,1)S(1)}, u32[]{:S(2)}, u32[]{:S(2)}) %collective-permute-start.4) | collective-permute-done | bytes 131104 | tf_op jit(solution)/shard_map/ppermute | solution.py:23
  28.6 1.5 collective-permute-done.5
  30.2 1.3 collective-permute-start.6
  31.5 1.3 collective-permute-start.7
  33.0 4.8 %collective-permute-start.2 = (bf16[32,8,512]{2,1,0:T(8,128)(2,1)S(1)}, bf16[32,8,512]{2,1,0:T(8,128)(2,1)S(1)}, u32[]{:S(2)}, u32[]{:S(2)}) collective-permute-start(bf16[32,8,512]{2,1,0:T(8,128)(2,1)S(1)} %get-tuple-element.83), channel_id=1, source_target_pairs={{0,1},{1,2},{2,3},{4,5},{5,6},{6,7},{8,9},{9,10},{10,11},{12,13},{... | collective-permute-start | bytes 786440 | tf_op jit(solution)/shard_map/ppermute | solution.py:23
  37.7 1.3 collective-permute-start.3
  39.7 2.8 %collective-permute-done.3 = bf16[32,8,512]{2,1,0:T(8,128)(2,1)} collective-permute-done((bf16[32,8,512]{2,1,0:T(8,128)(2,1)S(1)}, bf16[32,8,512]{2,1,0:T(8,128)(2,1)}, u32[]{:S(2)}, u32[]{:S(2)}) %collective-permute-start.3) | collective-permute-done | bytes 262176 | tf_op jit(solution)/shard_map/ppermute | solution.py:26
  42.5 1.1 pad_maximum_fusion
  43.7 1.2 slice_bitcast_fusion.18
  50.2 1.5 slice_bitcast_fusion
  51.7 13.7 %all-gather.3.cloned.1.call-done = bf16[1,1,32,64,512]{4,3,1,0,2:T(8,128)(2,1)} async-done(((bf16[1,1,4,64,512]{4,3,1,0,2:T(8,128)(2,1)}), bf16[1,1,32,64,512]{4,3,1,0,2:T(8,128)(2,1)}) %all-gather.3.cloned.1.call-update) | async-done | bytes 2097168 | tf_op jit(solution)/shard_map/all_gather | solution.py:198
  65.4 2.2 gather_fusion
  68.1 1.2 fusion.445
  70.9 1.2 fusion.118
  74.2 1.0 multiply_reduce_fusion
  75.2 2.1 fusion.84
  77.3 2.2 convolution_add_fusion.24
  79.5 2.2 convolution_add_fusion.23
  81.7 1.4 convolution_add_fusion.22
  83.2 1.3 convolution_add_fusion.21
  84.5 1.3 convolution_add_fusion.20
  85.9 1.3 convolution_add_fusion.19
  88.7 2.4 collective-permute-start.8
  93.0 1.3 collective-permute-start.9
  94.3 4.7 %collective-permute-done.9 = f32[8,16,4]{1,0,2:T(8,128)S(1)} collective-permute-done((f32[8,16,4]{1,0,2:T(8,128)S(1)}, f32[8,16,4]{1,0,2:T(8,128)S(1)}, u32[]{:S(2)}, u32[]{:S(2)}) %collective-permute-start.9) | collective-permute-done | bytes 2080 | tf_op jit(solution)/shard_map/ppermute | solution.py:26
  99.0 1.3 collective-permute-start.10
  100.3 1.5 collective-permute-start.11
  102.8 2.4 collective-permute-done.11
  111.9 1.6 convert_element_type.219
  113.5 1.6 copy.530
  115.1 2.0 convolution_add_fusion.15
  117.1 1.3 convolution_add_fusion.14
  118.5 1.3 convolution_add_fusion.13
  119.7 1.3 convolution_add_fusion.12
  121.0 1.2 convolution_add_fusion.11
  126.3 1.0 convolution_convert_fusion.1
  127.3 130.5 %all-reduce.3.cloned.1.call-done = (f32[256,256]{0,1:T(8,128)}, f32[256,256]{0,1:T(8,128)}, f32[256,256]{0,1:T(8,128)}, f32[256,256]{1,0:T(8,128)}) async-done(((f32[256,256]{0,1:T(8,128)}, f32[256,256]{0,1:T(8,128)}, f32[256,256]{0,1:T(8,128)}, f32[256,256]{1,0:T(8,128)}), (f32[256,256]{0,1:T(8,128)}, f32[256,256]{0,1:T(8,128)}, f32[256,256]{0,1:T(8,128)}, ...) | async-done | bytes 1048592 | tf_op jit(solution)/shard_map/psum | solution.py:248
  257.8 1.8 copy.531
  259.6 1.8 copy.532
  261.4 1.8 copy.533
  263.2 1.7 copy.1109
  (278 shorter events, 25.6 us)
Async XLA Ops:
  7.2 17.4 %copy-start.59 = (s32[1,1,4,2]{2,3,1,0:T(2,128)S(1)}, s32[1,1,4,2]{2,3,1,0:T(2,128)}, u32[]{:S(2)}) copy-start(s32[1,1,4,2]{2,3,1,0:T(2,128)} %param.16) | copy-start | bytes 100
  7.2 17.4 %copy-start.60 = (s32[1,1,4,2]{2,3,1,0:T(2,128)S(1)}, s32[1,1,4,2]{2,3,1,0:T(2,128)}, u32[]{:S(2)}) copy-start(s32[1,1,4,2]{2,3,1,0:T(2,128)} %param.15) | copy-start | bytes 100
  7.2 58.2 %all-gather.3.cloned.1.call-start = ((), (), s32[]{:S(2)}) async-start(), calls=%async_computation | async-start | bytes 2359296 | tf_op jit(solution)/shard_map/all_gather | solution.py:198
  7.9 249.9 %all-reduce.3.cloned.1.call-start = ((), (), s32[]{:S(2)}) async-start(), calls=%async_computation.1 | async-start | bytes 2097152 | tf_op jit(solution)/shard_map/psum | solution.py:248
  9.3 23.5 %collective-permute-start.1 = (bf16[8,16,512]{2,1,0:T(8,128)(2,1)S(1)}, bf16[8,16,512]{2,1,0:T(8,128)(2,1)S(1)}, u32[]{:S(2)}, u32[]{:S(2)}) collective-permute-start(bf16[8,16,512]{2,1,0:T(8,128)(2,1)S(1)} %bitcast.504), channel_id=1, source_target_pairs={{4,0},{8,4},{12,8},{16,12},{20,16},{24,20},{28,24},{5,1},{9,5},{13... | collective-permute-start | bytes 393224 | tf_op jit(solution)/shard_map/ppermute | solution.py:26
  10.6 22.2 %collective-permute-start = (bf16[8,16,512]{2,1,0:T(8,128)(2,1)S(1)}, bf16[8,16,512]{2,1,0:T(8,128)(2,1)S(1)}, u32[]{:S(2)}, u32[]{:S(2)}) collective-permute-start(bf16[8,16,512]{2,1,0:T(8,128)(2,1)S(1)} %bitcast.503), channel_id=1, source_target_pairs={{0,4},{4,8},{8,12},{12,16},{16,20},{20,24},{24,28},{1,5},{5,9},{9,... | collective-permute-start | bytes 393224 | tf_op jit(solution)/shard_map/ppermute | solution.py:23
  18.4 10.2 %collective-permute-start.4 = (bf16[8,16,512]{2,1,0:T(8,128)(2,1)S(1)}, bf16[8,16,512]{2,1,0:T(8,128)(2,1)S(1)}, u32[]{:S(2)}, u32[]{:S(2)}) collective-permute-start(bf16[8,16,512]{2,1,0:T(8,128)(2,1)S(1)} %get-tuple-element.85), channel_id=1, source_target_pairs={{0,4},{4,8},{8,12},{12,16},{16,20},{20,24},{24,28},{1,5},{5,9},{9,... | collective-permute-start | bytes 393224 | tf_op jit(solution)/shard_map/ppermute | solution.py:23
  23.2 6.9 %collective-permute-start.5 = (bf16[8,16,512]{2,1,0:T(8,128)(2,1)S(1)}, bf16[8,16,512]{2,1,0:T(8,128)(2,1)S(1)}, u32[]{:S(2)}, u32[]{:S(2)}) collective-permute-start(bf16[8,16,512]{2,1,0:T(8,128)(2,1)S(1)} %get-tuple-element.86), channel_id=1, source_target_pairs={{4,0},{8,4},{12,8},{16,12},{20,16},{24,20},{28,24},{5,1},{9,5},{13... | collective-permute-start | bytes 393224 | tf_op jit(solution)/shard_map/ppermute | solution.py:26
  25.0 20.0 %copy-start.75 = (pred[2,2]{1,0:T(4,128)(4,1)}, pred[2,2]{1,0:T(4,128)(4,1)S(1)}, u32[]{:S(2)}) copy-start(pred[2,2]{1,0:T(4,128)(4,1)S(1)} %get-tuple-element.112) | copy-start | bytes 16
  25.0 20.3 %copy-start.73 = (pred[2,2]{1,0:T(4,128)(4,1)}, pred[2,2]{1,0:T(4,128)(4,1)S(1)}, u32[]{:S(2)}) copy-start(pred[2,2]{1,0:T(4,128)(4,1)S(1)} %get-tuple-element.113) | copy-start | bytes 16
  25.0 20.5 %copy-start.71 = (pred[2,2]{1,0:T(4,128)(4,1)}, pred[2,2]{1,0:T(4,128)(4,1)S(1)}, u32[]{:S(2)}) copy-start(pred[2,2]{1,0:T(4,128)(4,1)S(1)} %get-tuple-element.114) | copy-start | bytes 16
  25.0 20.7 %copy-start.69 = (pred[2,2]{1,0:T(4,128)(4,1)}, pred[2,2]{1,0:T(4,128)(4,1)S(1)}, u32[]{:S(2)}) copy-start(pred[2,2]{1,0:T(4,128)(4,1)S(1)} %get-tuple-element.115) | copy-start | bytes 16
  25.0 20.9 %copy-start.65 = (pred[2,2]{1,0:T(4,128)(4,1)}, pred[2,2]{1,0:T(4,128)(4,1)S(1)}, u32[]{:S(2)}) copy-start(pred[2,2]{1,0:T(4,128)(4,1)S(1)} %get-tuple-element.117) | copy-start | bytes 16
  25.0 21.8 %copy-start.63 = (pred[2,2]{1,0:T(4,128)(4,1)}, pred[2,2]{1,0:T(4,128)(4,1)S(1)}, u32[]{:S(2)}) copy-start(pred[2,2]{1,0:T(4,128)(4,1)S(1)} %get-tuple-element.118) | copy-start | bytes 16
  25.1 22.6 %copy-start.61 = (pred[2,2]{1,0:T(4,128)(4,1)}, pred[2,2]{1,0:T(4,128)(4,1)S(1)}, u32[]{:S(2)}) copy-start(pred[2,2]{1,0:T(4,128)(4,1)S(1)} %get-tuple-element.111) | copy-start | bytes 16
  25.1 23.4 %copy-start.77 = (pred[2,2]{1,0:T(4,128)(4,1)}, pred[2,2]{1,0:T(4,128)(4,1)S(1)}, u32[]{:S(2)}) copy-start(pred[2,2]{1,0:T(4,128)(4,1)S(1)} %get-tuple-element.119) | copy-start | bytes 16
  25.1 24.3 %copy-start.67 = (pred[2,2]{1,0:T(4,128)(4,1)}, pred[2,2]{1,0:T(4,128)(4,1)S(1)}, u32[]{:S(2)}) copy-start(pred[2,2]{1,0:T(4,128)(4,1)S(1)} %get-tuple-element.116) | copy-start | bytes 16
  30.2 9.3 %collective-permute-start.6 = (bf16[32,8,512]{2,1,0:T(8,128)(2,1)S(1)}, bf16[32,8,512]{2,1,0:T(8,128)(2,1)S(1)}, u32[]{:S(2)}, u32[]{:S(2)}) collective-permute-start(bf16[32,8,512]{2,1,0:T(8,128)(2,1)S(1)} %get-tuple-element.79), channel_id=1, source_target_pairs={{0,1},{1,2},{2,3},{4,5},{5,6},{6,7},{8,9},{9,10},{10,11},{12,13},{... | collective-permute-start | bytes 786440 | tf_op jit(solution)/shard_map/ppermute | solution.py:23
  31.5 8.0 %collective-permute-start.7 = (bf16[32,8,512]{2,1,0:T(8,128)(2,1)S(1)}, bf16[32,8,512]{2,1,0:T(8,128)(2,1)S(1)}, u32[]{:S(2)}, u32[]{:S(2)}) collective-permute-start(bf16[32,8,512]{2,1,0:T(8,128)(2,1)S(1)} %get-tuple-element.80), channel_id=1, source_target_pairs={{1,0},{2,1},{3,2},{5,4},{6,5},{7,6},{9,8},{10,9},{11,10},{13,12},{... | collective-permute-start | bytes 786440 | tf_op jit(solution)/shard_map/ppermute | solution.py:26
  33.0 6.8 %collective-permute-start.2 = (bf16[32,8,512]{2,1,0:T(8,128)(2,1)S(1)}, bf16[32,8,512]{2,1,0:T(8,128)(2,1)S(1)}, u32[]{:S(2)}, u32[]{:S(2)}) collective-permute-start(bf16[32,8,512]{2,1,0:T(8,128)(2,1)S(1)} %get-tuple-element.83), channel_id=1, source_target_pairs={{0,1},{1,2},{2,3},{4,5},{5,6},{6,7},{8,9},{9,10},{10,11},{12,13},{... | collective-permute-start | bytes 786440 | tf_op jit(solution)/shard_map/ppermute | solution.py:23
  37.7 4.8 %collective-permute-start.3 = (bf16[32,8,512]{2,1,0:T(8,128)(2,1)S(1)}, bf16[32,8,512]{2,1,0:T(8,128)(2,1)}, u32[]{:S(2)}, u32[]{:S(2)}) collective-permute-start(bf16[32,8,512]{2,1,0:T(8,128)(2,1)S(1)} %get-tuple-element.84), channel_id=1, source_target_pairs={{1,0},{2,1},{3,2},{5,4},{6,5},{7,6},{9,8},{10,9},{11,10},{13,12},{... | collective-permute-start | bytes 786440 | tf_op jit(solution)/shard_map/ppermute | solution.py:26
  39.4 9.9 %copy-start.48 = (bf16[2,2,64,2,128]{4,3,2,1,0:T(2,128)(2,1)}, bf16[2,2,64,2,128]{4,3,2,1,0:T(2,128)(2,1)S(1)}, u32[]{:S(2)}) copy-start(bf16[2,2,64,2,128]{4,3,2,1,0:T(2,128)(2,1)S(1)} %reshape_reshape.29) | copy-start | bytes 393220
  44.9 4.3 %copy-start.38 = (bf16[2,2,8,2,8,128]{5,4,3,2,1,0:T(8,128)(2,1)}, bf16[2,2,8,2,8,128]{5,4,3,2,1,0:T(8,128)(2,1)S(1)}, u32[]{:S(2)}) copy-start(bf16[2,2,8,2,8,128]{5,4,3,2,1,0:T(8,128)(2,1)S(1)} %get-tuple-element.69) | copy-start | bytes 393220
  45.0 4.3 %copy-start.40 = (bf16[2,2,8,2,8,128]{5,4,3,2,1,0:T(8,128)(2,1)}, bf16[2,2,8,2,8,128]{5,4,3,2,1,0:T(8,128)(2,1)S(1)}, u32[]{:S(2)}) copy-start(bf16[2,2,8,2,8,128]{5,4,3,2,1,0:T(8,128)(2,1)S(1)} %get-tuple-element.70) | copy-start | bytes 393220
  45.0 4.3 %copy-start.42 = (bf16[2,2,8,2,8,128]{5,4,3,2,1,0:T(8,128)(2,1)}, bf16[2,2,8,2,8,128]{5,4,3,2,1,0:T(8,128)(2,1)S(1)}, u32[]{:S(2)}) copy-start(bf16[2,2,8,2,8,128]{5,4,3,2,1,0:T(8,128)(2,1)S(1)} %get-tuple-element.71) | copy-start | bytes 393220
  45.0 4.3 %copy-start.43 = (bf16[2,2,8,2,8,128]{5,4,3,2,1,0:T(8,128)(2,1)}, bf16[2,2,8,2,8,128]{5,4,3,2,1,0:T(8,128)(2,1)S(1)}, u32[]{:S(2)}) copy-start(bf16[2,2,8,2,8,128]{5,4,3,2,1,0:T(8,128)(2,1)S(1)} %get-tuple-element.72) | copy-start | bytes 393220
  45.0 4.3 %copy-start.44 = (bf16[2,2,8,2,8,128]{5,4,3,2,1,0:T(8,128)(2,1)}, bf16[2,2,8,2,8,128]{5,4,3,2,1,0:T(8,128)(2,1)S(1)}, u32[]{:S(2)}) copy-start(bf16[2,2,8,2,8,128]{5,4,3,2,1,0:T(8,128)(2,1)S(1)} %get-tuple-element.74) | copy-start | bytes 393220
  45.0 4.3 %copy-start.45 = (bf16[2,2,8,2,8,128]{5,4,3,2,1,0:T(8,128)(2,1)}, bf16[2,2,8,2,8,128]{5,4,3,2,1,0:T(8,128)(2,1)S(1)}, u32[]{:S(2)}) copy-start(bf16[2,2,8,2,8,128]{5,4,3,2,1,0:T(8,128)(2,1)S(1)} %get-tuple-element.75) | copy-start | bytes 393220
  45.0 4.3 %copy-start.46 = (bf16[2,2,8,2,8,128]{5,4,3,2,1,0:T(8,128)(2,1)}, bf16[2,2,8,2,8,128]{5,4,3,2,1,0:T(8,128)(2,1)S(1)}, u32[]{:S(2)}) copy-start(bf16[2,2,8,2,8,128]{5,4,3,2,1,0:T(8,128)(2,1)S(1)} %get-tuple-element.76) | copy-start | bytes 393220
  45.0 4.3 %copy-start.47 = (bf16[2,2,8,2,8,128]{5,4,3,2,1,0:T(8,128)(2,1)}, bf16[2,2,8,2,8,128]{5,4,3,2,1,0:T(8,128)(2,1)S(1)}, u32[]{:S(2)}) copy-start(bf16[2,2,8,2,8,128]{5,4,3,2,1,0:T(8,128)(2,1)S(1)} %get-tuple-element.77) | copy-start | bytes 393220
  45.0 4.3 %copy-start.32 = (bf16[2,2,8,2,8,128]{5,4,3,2,1,0:T(8,128)(2,1)}, bf16[2,2,8,2,8,128]{5,4,3,2,1,0:T(8,128)(2,1)S(1)}, u32[]{:S(2)}) copy-start(bf16[2,2,8,2,8,128]{5,4,3,2,1,0:T(8,128)(2,1)S(1)} %get-tuple-element.73) | copy-start | bytes 393220
  77.3 4.5 %copy-start.18 = (bf16[2,2,8,2,8,128]{5,4,3,2,1,0:T(8,128)(2,1)S(1)}, bf16[2,2,8,2,8,128]{5,4,3,2,1,0:T(8,128)(2,1)}, u32[]{:S(2)}) copy-start(bf16[2,2,8,2,8,128]{5,4,3,2,1,0:T(8,128)(2,1)} %get-tuple-element.66) | copy-start | bytes 393220
  79.5 5.0 %copy-start.16 = (bf16[2,2,8,2,8,128]{5,4,3,2,1,0:T(8,128)(2,1)S(1)}, bf16[2,2,8,2,8,128]{5,4,3,2,1,0:T(8,128)(2,1)}, u32[]{:S(2)}) copy-start(bf16[2,2,8,2,8,128]{5,4,3,2,1,0:T(8,128)(2,1)} %get-tuple-element.64) | copy-start | bytes 393220
  79.5 6.4 %copy-start.14 = (bf16[2,2,8,2,8,128]{5,4,3,2,1,0:T(8,128)(2,1)S(1)}, bf16[2,2,8,2,8,128]{5,4,3,2,1,0:T(8,128)(2,1)}, u32[]{:S(2)}) copy-start(bf16[2,2,8,2,8,128]{5,4,3,2,1,0:T(8,128)(2,1)} %get-tuple-element.63) | copy-start | bytes 393220
  81.7 5.5 %copy-start.12 = (bf16[2,2,8,2,8,128]{5,4,3,2,1,0:T(8,128)(2,1)S(1)}, bf16[2,2,8,2,8,128]{5,4,3,2,1,0:T(8,128)(2,1)}, u32[]{:S(2)}) copy-start(bf16[2,2,8,2,8,128]{5,4,3,2,1,0:T(8,128)(2,1)} %get-tuple-element.62) | copy-start | bytes 393220
  83.2 4.5 %copy-start.10 = (bf16[2,2,8,2,8,128]{5,4,3,2,1,0:T(8,128)(2,1)S(1)}, bf16[2,2,8,2,8,128]{5,4,3,2,1,0:T(8,128)(2,1)}, u32[]{:S(2)}) copy-start(bf16[2,2,8,2,8,128]{5,4,3,2,1,0:T(8,128)(2,1)} %get-tuple-element.61) | copy-start | bytes 393220
  88.7 5.5 %collective-permute-start.8 = (f32[8,16,4]{1,0,2:T(8,128)S(1)}, f32[8,16,4]{1,0,2:T(8,128)S(1)}, u32[]{:S(2)}, u32[]{:S(2)}) collective-permute-start(f32[8,16,4]{1,0,2:T(8,128)S(1)} %slice.401), channel_id=1, source_target_pairs={{0,4},{4,8},{8,12},{12,16},{16,20},{20,24},{24,28},{1,5},{5,9},{9,... | collective-permute-start | bytes 6152 | tf_op jit(solution)/shard_map/ppermute | solution.py:23
  91.4 14.9 %copy-start.33 = (bf16[2,2,8,2,8,128]{5,4,3,2,1,0:T(8,128)(2,1)S(1)}, bf16[2,2,8,2,8,128]{5,4,3,2,1,0:T(8,128)(2,1)}, u32[]{:S(2)}) copy-start(bf16[2,2,8,2,8,128]{5,4,3,2,1,0:T(8,128)(2,1)} %copy-done.32) | copy-start | bytes 393220
  91.5 14.9 %copy-start.37 = (bf16[2,2,8,2,8,128]{5,4,3,2,1,0:T(8,128)(2,1)S(1)}, bf16[2,2,8,2,8,128]{5,4,3,2,1,0:T(8,128)(2,1)}, u32[]{:S(2)}) copy-start(bf16[2,2,8,2,8,128]{5,4,3,2,1,0:T(8,128)(2,1)} %get-tuple-element.60) | copy-start | bytes 393220
  91.5 14.9 %copy-start.78 = (pred[2,2]{1,0:T(4,128)(4,1)S(1)}, pred[2,2]{1,0:T(4,128)(4,1)}, u32[]{:S(2)}) copy-start(pred[2,2]{1,0:T(4,128)(4,1)} %copy-done.77) | copy-start | bytes 16
  92.5 14.1 %copy-start.8 = (bf16[2,2,8,2,8,128]{5,4,3,2,1,0:T(8,128)(2,1)S(1)}, bf16[2,2,8,2,8,128]{5,4,3,2,1,0:T(8,128)(2,1)}, u32[]{:S(2)}) copy-start(bf16[2,2,8,2,8,128]{5,4,3,2,1,0:T(8,128)(2,1)} %get-tuple-element.59) | copy-start | bytes 393220
  92.7 13.8 %copy-start.50 = (bf16[2,8,2,8,256]{4,3,2,1,0:T(8,128)(2,1)}, bf16[2,8,2,8,256]{4,3,2,1,0:T(8,128)(2,1)S(1)}, u32[]{:S(2)}) copy-start(bf16[2,8,2,8,256]{4,3,2,1,0:T(8,128)(2,1)S(1)} %copy.449) | copy-start | bytes 393220
  93.0 6.0 %collective-permute-start.9 = (f32[8,16,4]{1,0,2:T(8,128)S(1)}, f32[8,16,4]{1,0,2:T(8,128)S(1)}, u32[]{:S(2)}, u32[]{:S(2)}) collective-permute-start(f32[8,16,4]{1,0,2:T(8,128)S(1)} %slice.403), channel_id=1, source_target_pairs={{4,0},{8,4},{12,8},{16,12},{20,16},{24,20},{28,24},{5,1},{9,5},{13... | collective-permute-start | bytes 6152 | tf_op jit(solution)/shard_map/ppermute | solution.py:26
  99.0 3.7 %collective-permute-start.10 = (f32[32,8,4]{1,0,2:T(8,128)S(1)}, f32[32,8,4]{1,0,2:T(8,128)S(1)}, u32[]{:S(2)}, u32[]{:S(2)}) collective-permute-start(f32[32,8,4]{1,0,2:T(8,128)S(1)} %get-tuple-element.89), channel_id=1, source_target_pairs={{0,1},{1,2},{2,3},{4,5},{5,6},{6,7},{8,9},{9,10},{10,11},{12,13},{... | collective-permute-start | bytes 12296 | tf_op jit(solution)/shard_map/ppermute | solution.py:23
  100.3 4.8 %collective-permute-start.11 = (f32[32,8,4]{1,0,2:T(8,128)S(1)}, f32[32,8,4]{1,0,2:T(8,128)S(1)}, u32[]{:S(2)}, u32[]{:S(2)}) collective-permute-start(f32[32,8,4]{1,0,2:T(8,128)S(1)} %get-tuple-element.90), channel_id=1, source_target_pairs={{1,0},{2,1},{3,2},{5,4},{6,5},{7,6},{9,8},{10,9},{11,10},{13,12},{... | collective-permute-start | bytes 12296 | tf_op jit(solution)/shard_map/ppermute | solution.py:26
  101.8 5.3 %copy-start.53 = (bf16[2,2,8,2,8,128]{5,4,3,2,1,0:T(8,128)(2,1)S(1)}, bf16[2,2,8,2,8,128]{5,4,3,2,1,0:T(8,128)(2,1)}, u32[]{:S(2)}) copy-start(bf16[2,2,8,2,8,128]{5,4,3,2,1,0:T(8,128)(2,1)} %get-tuple-element.44) | copy-start | bytes 393220
  101.8 5.3 %copy-start.76 = (pred[2,2]{1,0:T(4,128)(4,1)S(1)}, pred[2,2]{1,0:T(4,128)(4,1)}, u32[]{:S(2)}) copy-start(pred[2,2]{1,0:T(4,128)(4,1)} %copy-done.75) | copy-start | bytes 16
  110.5 6.6 %copy-start.23 = (f32[2,2,2,64,64]{3,4,2,1,0:T(8,128)S(1)}, f32[2,2,2,64,64]{3,4,2,1,0:T(8,128)}, u32[]{:S(2)}) copy-start(f32[2,2,2,64,64]{3,4,2,1,0:T(8,128)} %copy-done.22) | copy-start | bytes 393220
  (45 other events, 95.9 us)
Sparse Core Ops, SparseCore 0:
  10.2 55.1 all-gather.2
  125.6 132.2 all-reduce.2
where the time goes:
time: 273 us; the launch traced here: 272 us
  waiting for transfers between devices  160 us (59%)
  matrix products  44.2 us (16%)
  starting transfers between devices  28.1 us (10%)
  local copies, waits for them, and re-layouts  20.5 us (8%)
  between operations  15.9 us (6%)
  other arithmetic  3.19 us (1%)
    psum x1, waiting for transfers between devices, on_device(): lax.psum((inner_rows(flat_in, dq_flat), inner_rows(flat_in, dk_flat), inn...  131 us
    ppermute x6, starting transfers between devices, padded(): lax.ppermute(lax.slice_in_dim(block, block.shape[dim] - width, None, axis...  20.1 us
    all_gather x1, waiting for transfers between devices, on_device(): row_tables = lax.all_gather(memory_local, 'gx', axis=0, tiled=True)  13.7 us
    dot_general x10, matrix products, query_grads(): jnp.einsum('abhqk,abkhe->abqhe', grad_score, split_heads(key_part), prefe...  13.1 us
    ppermute x6, waiting for transfers between devices, padded(): lax.ppermute(lax.slice_in_dim(block, 0, width, axis=dim), axis, backward)  11.4 us
    unnamed x166, local copies, waits for them, and re-layouts  10.8 us
    dot_general x9, matrix products, key_grads(): jnp.einsum('abhqk,abqhe->abkhe', grad_score, query_heads, preferred_eleme...  8.38 us
    ppermute x6, starting transfers between devices, padded(): lax.ppermute(lax.slice_in_dim(block, 0, width, axis=dim), axis, backward)  7.92 us
  transfers between devices with their start and end apart: 14, of which 7 were waited for; matrix products, arithmetic and copies ran while one was open for 7% of the time, Pallas kernels for 0%

commit v1 on v0

--- a/solution.py
+++ b/solution.py
@@ -169,6 +169,47 @@
     )
 
 
+def halving_steps(axes):
+    steps = []
+    for axis in axes:
+        count = lax.axis_size(axis)
+        stride = 1
+        while stride < count:
+            steps.append((axis, stride))
+            stride *= 2
+    return steps
+
+
+def tree_sum(parts, axes):
+    sizes = [lax.axis_size(axis) for axis in axes]
+    rows = sum(part.shape[0] for part in parts)
+    total = math.prod(sizes)
+    if any(size & (size - 1) for size in sizes) or rows % total:
+        return lax.psum(parts, axes)
+    steps = halving_steps(axes)
+    joined = jnp.concatenate(parts, 0)
+    for axis, stride in steps:
+        pairs = [(i, i ^ stride) for i in range(lax.axis_size(axis))]
+        bit = (lax.axis_index(axis) // stride) % 2
+        half = joined.shape[0] // 2
+        keep = lax.dynamic_slice_in_dim(joined, bit * half, half, 0)
+        send = lax.dynamic_slice_in_dim(joined, (1 - bit) * half, half, 0)
+        joined = keep + lax.ppermute(send, axis, pairs)
+    for axis, stride in reversed(steps):
+        pairs = [(i, i ^ stride) for i in range(lax.axis_size(axis))]
+        bit = (lax.axis_index(axis) // stride) % 2
+        got = lax.ppermute(joined, axis, pairs)
+        low = jnp.where(bit == 0, joined, got)
+        high = jnp.where(bit == 0, got, joined)
+        joined = jnp.concatenate([low, high], 0)
+    out = []
+    start = 0
+    for part in parts:
+        out.append(joined[start : start + part.shape[0]])
+        start += part.shape[0]
+    return tuple(out)
+
+
 def on_device(
     patches, w_query, w_key, w_value, w_out, region_memory, region_owner, region_local, grad_out
 ):
@@ -245,15 +286,13 @@
     grad_patches = jnp.dot(grads_joined, w_stacked, preferred_element_type=jnp.float32).astype(
         jnp.bfloat16
     )
-    summed = lax.psum(
-        (
-            inner_rows(flat_in, dq_flat),
-            inner_rows(flat_in, dk_flat),
-            inner_rows(flat_in, dv_flat),
-            grad_out_local,
-        ),
-        ("gx", "gy"),
-    )
+    partials = (
+        inner_rows(flat_in, dq_flat),
+        inner_rows(flat_in, dk_flat),
+        inner_rows(flat_in, dv_flat),
+        grad_out_local,
+    )
+    summed = tree_sum(partials, ("gy", "gx"))
     return (
         layer_out.reshape(tile_rows, tile_cols, model_width),
         grad_patches.reshape(tile_rows, tile_cols, model_width),

time: 273 us -> 188 us (0.69)
  waiting for transfers between devices: 160 us -> 66.3 us
  starting transfers between devices: 28.1 us -> 41.2 us
  local copies, waits for them, and re-layouts: 20.5 us -> 15.3 us
    psum x1 -> x0, waiting for transfers between devices: 131 us -> none  [on_device(): lax.psum((inner_rows(flat_in, dq_flat), inner_rows(flat_in, dk_flat), inn...]
    ppermute x0 -> x10, waiting for transfers between devices: none -> 37 us  [the longest x5 20.4 us: tree_sum(): joined = keep + lax.ppermute(send, axis, pairs)]
    ppermute x0 -> x10, starting transfers between devices: none -> 13.1 us  [the longest x5 8.19 us: tree_sum(): joined = keep + lax.ppermute(send, axis, pairs)]
    unnamed x166 -> x164, local copies, waits for them, and re-layouts: 10.8 us -> 3.76 us
  transfers between devices with their start and end apart: 14 -> 23, of which waited for: 7 -> 16; matrix products, arithmetic and copies ran while one was open for 7% -> 10% of each run, Pallas kernels for 0% -> 0%
where the time goes in v1:
time: 188 us; the launch traced here: 187 us
  waiting for transfers between devices  66.3 us (35%)
  matrix products  44.2 us (24%)
  starting transfers between devices  41.2 us (22%)
  between operations  16 us (9%)
  local copies, waits for them, and re-layouts  15.3 us (8%)
  other arithmetic  3.63 us (2%)
    ppermute x5, waiting for transfers between devices, tree_sum(): joined = keep + lax.ppermute(send, axis, pairs)  20.4 us
    ppermute x6, starting transfers between devices, padded(): lax.ppermute(lax.slice_in_dim(block, block.shape[dim] - width, None, axis...  20.1 us
    ppermute x5, waiting for transfers between devices, tree_sum(): got = lax.ppermute(joined, axis, pairs)  16.6 us
    all_gather x1, waiting for transfers between devices, on_device(): row_tables = lax.all_gather(memory_local, 'gx', axis=0, tiled=True)  13.7 us
    dot_general x10, matrix products, query_grads(): jnp.einsum('abhqk,abkhe->abqhe', grad_score, split_heads(key_part), prefe...  13.1 us
    ppermute x6, waiting for transfers between devices, padded(): lax.ppermute(lax.slice_in_dim(block, 0, width, axis=dim), axis, backward)  11.4 us
    dot_general x9, matrix products, key_grads(): jnp.einsum('abhqk,abqhe->abkhe', grad_score, query_heads, preferred_eleme...  8.41 us
    ppermute x5, starting transfers between devices, tree_sum(): joined = keep + lax.ppermute(send, axis, pairs)  8.19 us
  transfers between devices with their start and end apart: 23, of which 16 were waited for; matrix products, arithmetic and copies ran while one was open for 10% of the time, Pallas kernels for 0%

profile of v1, /device:TPU:0, one launch (start us, length us, event | category | flops | bytes accessed | tf_op | source)
XLA Modules:
  0.0 186.7 jit_solution(12539267891162405067)
XLA Ops:
  9.3 1.3 collective-permute-start.1
  10.6 5.5 %collective-permute-start = (bf16[8,16,512]{2,1,0:T(8,128)(2,1)S(1)}, bf16[8,16,512]{2,1,0:T(8,128)(2,1)S(1)}, u32[]{:S(2)}, u32[]{:S(2)}) collective-permute-start(bf16[8,16,512]{2,1,0:T(8,128)(2,1)S(1)} %bitcast.503), channel_id=1, source_target_pairs={{0,4},{4,8},{8,12},{12,16},{16,20},{20,24},{24,28},{1,5},{5,9},{9,... | collective-permute-start | bytes 393224 | tf_op jit(solution)/shard_map/ppermute | solution.py:23
  18.4 4.8 %collective-permute-start.4 = (bf16[8,16,512]{2,1,0:T(8,128)(2,1)S(1)}, bf16[8,16,512]{2,1,0:T(8,128)(2,1)S(1)}, u32[]{:S(2)}, u32[]{:S(2)}) collective-permute-start(bf16[8,16,512]{2,1,0:T(8,128)(2,1)S(1)} %get-tuple-element.67), channel_id=1, source_target_pairs={{0,4},{4,8},{8,12},{12,16},{16,20},{20,24},{24,28},{1,5},{5,9},{9,... | collective-permute-start | bytes 393224 | tf_op jit(solution)/shard_map/ppermute | solution.py:23
  23.2 1.3 collective-permute-start.5
  25.1 3.5 %collective-permute-done.4 = bf16[8,16,512]{2,1,0:T(8,128)(2,1)S(1)} collective-permute-done((bf16[8,16,512]{2,1,0:T(8,128)(2,1)S(1)}, bf16[8,16,512]{2,1,0:T(8,128)(2,1)S(1)}, u32[]{:S(2)}, u32[]{:S(2)}) %collective-permute-start.4) | collective-permute-done | bytes 131104 | tf_op jit(solution)/shard_map/ppermute | solution.py:23
  28.6 1.5 collective-permute-done.5
  30.2 1.3 collective-permute-start.6
  31.5 1.3 collective-permute-start.7
  33.0 4.8 %collective-permute-start.2 = (bf16[32,8,512]{2,1,0:T(8,128)(2,1)S(1)}, bf16[32,8,512]{2,1,0:T(8,128)(2,1)S(1)}, u32[]{:S(2)}, u32[]{:S(2)}) collective-permute-start(bf16[32,8,512]{2,1,0:T(8,128)(2,1)S(1)} %get-tuple-element.63), channel_id=1, source_target_pairs={{0,1},{1,2},{2,3},{4,5},{5,6},{6,7},{8,9},{9,10},{10,11},{12,13},{... | collective-permute-start | bytes 786440 | tf_op jit(solution)/shard_map/ppermute | solution.py:23
  37.7 1.3 collective-permute-start.3
  39.7 2.8 %collective-permute-done.3 = bf16[32,8,512]{2,1,0:T(8,128)(2,1)} collective-permute-done((bf16[32,8,512]{2,1,0:T(8,128)(2,1)S(1)}, bf16[32,8,512]{2,1,0:T(8,128)(2,1)}, u32[]{:S(2)}, u32[]{:S(2)}) %collective-permute-start.3) | collective-permute-done | bytes 262176 | tf_op jit(solution)/shard_map/ppermute | solution.py:26
  43.7 1.2 slice_bitcast_fusion.18
  50.1 1.5 slice_bitcast_fusion
  51.6 13.7 %all-gather.3.cloned.1.call-done = bf16[1,1,32,64,512]{4,3,1,0,2:T(8,128)(2,1)} async-done(((bf16[1,1,4,64,512]{4,3,1,0,2:T(8,128)(2,1)}), bf16[1,1,32,64,512]{4,3,1,0,2:T(8,128)(2,1)}) %all-gather.3.cloned.1.call-update) | async-done | bytes 2097168 | tf_op jit(solution)/shard_map/all_gather | solution.py:239
  65.4 2.2 %gather_fusion = bf16[8,64,512]{2,1,0:T(8,128)(2,1)S(1)} fusion(bf16[32,64,512]{2,1,0:T(8,128)(2,1)} %bitcast.502, s32[1024]{0:T(1024)S(1)} %pad_clamp_fusion), kind=kCustom, calls=%fused_computation | custom fusion | bytes 1048608 | tf_op jit(solution)/shard_map/jit(_take)/gather | solution.py:240
  68.1 1.2 fusion.447
  75.2 2.1 %fusion.84 = f32[2,2,2,128,64]{3,4,2,1,0:T(8,128)} fusion(f32[2,2,2,64,64]{3,4,2,1,0:T(8,128)S(1)} %get-tuple-element.123, f32[2,2,2,64]{3,2,1,0:T(2,128)S(1)} %bitcast.469, f32[2,2,2,64]{3,2,1,0:T(2,128)S(1)} %log_add_fusion, bf16[2,2,8,2,8,128]{5,4,3,2,1,0:T(8,128)(2,1)} %copy-done.48, bf16[2,2,8,2,8,128]{5,4,3,2,1,0:T(8,128)(2,1)} %get-tuple-element.52, ...), kind=kOutput, calls=%fused_computation.165 | convolution fusion | flops 16908288 | bytes 790528 | tf_op jit(solution)/shard_map/abhqk,abkhe->abqhe/dot_general | solution.py:115
  77.3 2.2 %convolution_add_fusion.24 = f32[2,2,2,128,64]{3,4,2,1,0:T(8,128)} fusion(f32[2,2,2,128,64]{3,4,2,1,0:T(8,128)} %fusion.84, f32[2,2,2,64,64]{3,4,2,1,0:T(8,128)S(1)} %get-tuple-element.125, f32[2,2,2,64]{3,2,1,0:T(2,128)S(1)} %bitcast.471, f32[2,2,2,64]{3,2,1,0:T(2,128)S(1)} %log_add_fusion, bf16[2,2,8,2,8,128]{5,4,3,2,1,0:T(8,128)(2,1)} %get-tuple-element.42, ...), kind=kOutput, calls=%fused_computation.98 | convolution fusion | flops 16973824 | bytes 1052672 | tf_op jit(solution)/shard_map/abhqk,abkhe->abqhe/dot_general | solution.py:115
  79.5 2.2 %convolution_add_fusion.23 = f32[2,2,2,128,64]{3,4,2,1,0:T(8,128)} fusion(f32[2,2,2,128,64]{3,4,2,1,0:T(8,128)} %convolution_add_fusion.24, f32[2,2,2,64,64]{3,4,2,1,0:T(8,128)S(1)} %get-tuple-element.121, f32[2,2,2,64]{3,2,1,0:T(2,128)S(1)} %bitcast.472, f32[2,2,2,64]{3,2,1,0:T(2,128)S(1)} %log_add_fusion, ...), kind=kOutput, calls=%fused_computation.95 | convolution fusion | flops 16973824 | bytes 1052672 | tf_op jit(solution)/shard_map/abhqk,abkhe->abqhe/dot_general | solution.py:115
  81.7 1.4 convolution_add_fusion.22
  83.2 1.3 convolution_add_fusion.21
  84.6 1.3 convolution_add_fusion.20
  85.9 1.3 convolution_add_fusion.19
  88.7 2.4 %collective-permute-start.8 = (f32[8,16,4]{1,0,2:T(8,128)S(1)}, f32[8,16,4]{1,0,2:T(8,128)S(1)}, u32[]{:S(2)}, u32[]{:S(2)}) collective-permute-start(f32[8,16,4]{1,0,2:T(8,128)S(1)} %slice.413), channel_id=1, source_target_pairs={{0,4},{4,8},{8,12},{12,16},{16,20},{20,24},{24,28},{1,5},{5,9},{9,... | collective-permute-start | bytes 6152 | tf_op jit(solution)/shard_map/ppermute | solution.py:23
  93.0 1.3 collective-permute-start.9
  94.3 4.7 %collective-permute-done.9 = f32[8,16,4]{1,0,2:T(8,128)S(1)} collective-permute-done((f32[8,16,4]{1,0,2:T(8,128)S(1)}, f32[8,16,4]{1,0,2:T(8,128)S(1)}, u32[]{:S(2)}, u32[]{:S(2)}) %collective-permute-start.9) | collective-permute-done | bytes 2080 | tf_op jit(solution)/shard_map/ppermute | solution.py:26
  99.1 1.3 collective-permute-start.10
  100.4 1.5 collective-permute-start.11
  102.8 2.4 %collective-permute-done.11 = f32[32,8,4]{1,0,2:T(8,128)S(1)} collective-permute-done((f32[32,8,4]{1,0,2:T(8,128)S(1)}, f32[32,8,4]{1,0,2:T(8,128)S(1)}, u32[]{:S(2)}, u32[]{:S(2)}) %collective-permute-start.11) | collective-permute-done | bytes 4128 | tf_op jit(solution)/shard_map/ppermute | solution.py:26
  113.3 1.6 convert_element_type.219
  115.0 1.6 copy.521
  116.5 2.0 %convolution_add_fusion.15 = f32[2,2,2,128,64]{3,4,2,1,0:T(8,128)} fusion(f32[2,2,2,128,64]{3,4,2,1,0:T(8,128)S(1)} %fusion.82, f32[2,2,2,64,64]{3,4,2,1,0:T(8,128)} %copy-done.23, f32[2,2,2,64]{3,2,1,0:T(2,128)} %get-tuple-element.93, bf16[2,2,8,2,8,128]{5,4,3,2,1,0:T(8,128)(2,1)S(1)} %copy-done.7, bf16[2,2,8,2,8,128]{5,4,3,2,1,0:T(8,128)(2,1)S(1)} %copy-done.37, ...), kind=kOutput, calls=%fused_computation.18 | convolution fusion | flops 16941056 | bytes 1050624 | tf_op jit(solution)/shard_map/abhqk,abqhe->abkhe/dot_general | solution.py:154
  118.5 1.4 convolution_add_fusion.14
  120.0 1.2 convolution_add_fusion.13
  121.2 1.3 convolution_add_fusion.12
  122.5 1.2 convolution_add_fusion.11
  125.6 3.0 %collective-permute-start.12 = (f32[512,256]{1,0:T(8,128)S(1)}, f32[512,256]{1,0:T(8,128)S(1)}, u32[]{:S(2)}, u32[]{:S(2)}) collective-permute-start(f32[512,256]{1,0:T(8,128)S(1)} %constant_dynamic-slice_fusion.4), channel_id=1, source_target_pairs={{0,1},{1,0},{2,3},{3,2},{4,5},{5,4},{6,7},{7,6},{8,9},{9,8},{10,11... | collective-permute-start | bytes 1572872 | tf_op jit(solution)/shard_map/ppermute | solution.py:197
  128.6 1.5 collective-permute-done.12
  130.5 8.4 %collective-permute-done.13 = f32[256,256]{1,0:T(8,128)S(1)} collective-permute-done((f32[256,256]{1,0:T(8,128)S(1)}, f32[256,256]{1,0:T(8,128)S(1)}, u32[]{:S(2)}, u32[]{:S(2)}) %collective-permute-start.13) | collective-permute-done | bytes 262176 | tf_op jit(solution)/shard_map/ppermute | solution.py:197
  139.0 3.0 %collective-permute-start.14 = (f32[128,256]{1,0:T(8,128)S(1)}, f32[128,256]{1,0:T(8,128)S(1)}, u32[]{:S(2)}, u32[]{:S(2)}) collective-permute-start(f32[128,256]{1,0:T(8,128)S(1)} %constant_dynamic-slice_fusion.2), channel_id=1, source_target_pairs={{0,4},{4,0},{8,12},{12,8},{16,20},{20,16},{24,28},{28,24},{1,5},{5... | collective-permute-start | bytes 393224 | tf_op jit(solution)/shard_map/ppermute | solution.py:197
  141.9 3.2 %collective-permute-done.14 = f32[128,256]{1,0:T(8,128)S(1)} collective-permute-done((f32[128,256]{1,0:T(8,128)S(1)}, f32[128,256]{1,0:T(8,128)S(1)}, u32[]{:S(2)}, u32[]{:S(2)}) %collective-permute-start.14) | collective-permute-done | bytes 131104 | tf_op jit(solution)/shard_map/ppermute | solution.py:197
  146.2 3.4 %collective-permute-done.15 = f32[64,256]{1,0:T(8,128)S(1)} collective-permute-done((f32[64,256]{1,0:T(8,128)S(1)}, f32[64,256]{1,0:T(8,128)S(1)}, u32[]{:S(2)}, u32[]{:S(2)}) %collective-permute-start.15) | collective-permute-done | bytes 65568 | tf_op jit(solution)/shard_map/ppermute | solution.py:197
  150.5 3.9 %collective-permute-done.16 = f32[32,256]{1,0:T(8,128)S(1)} collective-permute-done((f32[32,256]{1,0:T(8,128)S(1)}, f32[32,256]{1,0:T(8,128)S(1)}, u32[]{:S(2)}, u32[]{:S(2)}) %collective-permute-start.16) | collective-permute-done | bytes 32800 | tf_op jit(solution)/shard_map/ppermute | solution.py:197
  155.4 3.9 %collective-permute-done.17 = f32[32,256]{1,0:T(8,128)S(1)} collective-permute-done((f32[32,256]{1,0:T(8,128)S(1)}, f32[32,256]{1,0:T(8,128)S(1)}, u32[]{:S(2)}, u32[]{:S(2)}) %collective-permute-start.17) | collective-permute-done | bytes 32800 | tf_op jit(solution)/shard_map/ppermute | solution.py:201
  160.4 3.3 %collective-permute-done.18 = f32[64,256]{1,0:T(8,128)S(1)} collective-permute-done((f32[64,256]{1,0:T(8,128)S(1)}, f32[64,256]{1,0:T(8,128)S(1)}, u32[]{:S(2)}, u32[]{:S(2)}) %collective-permute-start.18) | collective-permute-done | bytes 65568 | tf_op jit(solution)/shard_map/ppermute | solution.py:201
  163.7 2.9 %collective-permute-start.19 = (f32[128,256]{1,0:T(8,128)S(1)}, f32[128,256]{1,0:T(8,128)S(1)}, u32[]{:S(2)}, u32[]{:S(2)}) collective-permute-start(f32[128,256]{1,0:T(8,128)S(1)} %pad_maximum_fusion.8), channel_id=1, source_target_pairs={{0,4},{4,0},{8,12},{12,8},{16,20},{20,16},{24,28},{28,24},{1,5},{5... | collective-permute-start | bytes 393224 | tf_op jit(solution)/shard_map/ppermute | solution.py:201
  166.7 2.9 %collective-permute-done.19 = f32[128,256]{1,0:T(8,128)S(1)} collective-permute-done((f32[128,256]{1,0:T(8,128)S(1)}, f32[128,256]{1,0:T(8,128)S(1)}, u32[]{:S(2)}, u32[]{:S(2)}) %collective-permute-start.19) | collective-permute-done | bytes 131104 | tf_op jit(solution)/shard_map/ppermute | solution.py:201
  169.7 6.4 %collective-permute-done.20 = f32[256,256]{1,0:T(8,128)S(1)} collective-permute-done((f32[256,256]{1,0:T(8,128)S(1)}, f32[256,256]{1,0:T(8,128)S(1)}, u32[]{:S(2)}, u32[]{:S(2)}) %collective-permute-start.20) | collective-permute-done | bytes 262176 | tf_op jit(solution)/shard_map/ppermute | solution.py:201
  (315 shorter events, 39.7 us)
Async XLA Ops:
  7.2 17.4 %copy-start.62 = (s32[1,1,4,2]{2,3,1,0:T(2,128)S(1)}, s32[1,1,4,2]{2,3,1,0:T(2,128)}, u32[]{:S(2)}) copy-start(s32[1,1,4,2]{2,3,1,0:T(2,128)} %param.16) | copy-start | bytes 100
  7.2 17.4 %copy-start.63 = (s32[1,1,4,2]{2,3,1,0:T(2,128)S(1)}, s32[1,1,4,2]{2,3,1,0:T(2,128)}, u32[]{:S(2)}) copy-start(s32[1,1,4,2]{2,3,1,0:T(2,128)} %param.15) | copy-start | bytes 100
  7.2 58.2 %all-gather.3.cloned.1.call-start = ((), (), s32[]{:S(2)}) async-start(), calls=%async_computation | async-start | bytes 2359296 | tf_op jit(solution)/shard_map/all_gather | solution.py:239
  9.3 23.5 %collective-permute-start.1 = (bf16[8,16,512]{2,1,0:T(8,128)(2,1)S(1)}, bf16[8,16,512]{2,1,0:T(8,128)(2,1)S(1)}, u32[]{:S(2)}, u32[]{:S(2)}) collective-permute-start(bf16[8,16,512]{2,1,0:T(8,128)(2,1)S(1)} %bitcast.504), channel_id=1, source_target_pairs={{4,0},{8,4},{12,8},{16,12},{20,16},{24,20},{28,24},{5,1},{9,5},{13... | collective-permute-start | bytes 393224 | tf_op jit(solution)/shard_map/ppermute | solution.py:26
  10.6 22.2 %collective-permute-start = (bf16[8,16,512]{2,1,0:T(8,128)(2,1)S(1)}, bf16[8,16,512]{2,1,0:T(8,128)(2,1)S(1)}, u32[]{:S(2)}, u32[]{:S(2)}) collective-permute-start(bf16[8,16,512]{2,1,0:T(8,128)(2,1)S(1)} %bitcast.503), channel_id=1, source_target_pairs={{0,4},{4,8},{8,12},{12,16},{16,20},{20,24},{24,28},{1,5},{5,9},{9,... | collective-permute-start | bytes 393224 | tf_op jit(solution)/shard_map/ppermute | solution.py:23
  18.4 10.2 %collective-permute-start.4 = (bf16[8,16,512]{2,1,0:T(8,128)(2,1)S(1)}, bf16[8,16,512]{2,1,0:T(8,128)(2,1)S(1)}, u32[]{:S(2)}, u32[]{:S(2)}) collective-permute-start(bf16[8,16,512]{2,1,0:T(8,128)(2,1)S(1)} %get-tuple-element.67), channel_id=1, source_target_pairs={{0,4},{4,8},{8,12},{12,16},{16,20},{20,24},{24,28},{1,5},{5,9},{9,... | collective-permute-start | bytes 393224 | tf_op jit(solution)/shard_map/ppermute | solution.py:23
  23.2 6.9 %collective-permute-start.5 = (bf16[8,16,512]{2,1,0:T(8,128)(2,1)S(1)}, bf16[8,16,512]{2,1,0:T(8,128)(2,1)S(1)}, u32[]{:S(2)}, u32[]{:S(2)}) collective-permute-start(bf16[8,16,512]{2,1,0:T(8,128)(2,1)S(1)} %get-tuple-element.68), channel_id=1, source_target_pairs={{4,0},{8,4},{12,8},{16,12},{20,16},{24,20},{28,24},{5,1},{9,5},{13... | collective-permute-start | bytes 393224 | tf_op jit(solution)/shard_map/ppermute | solution.py:26
  25.0 20.0 %copy-start.76 = (pred[2,2]{1,0:T(4,128)(4,1)}, pred[2,2]{1,0:T(4,128)(4,1)S(1)}, u32[]{:S(2)}) copy-start(pred[2,2]{1,0:T(4,128)(4,1)S(1)} %get-tuple-element.98) | copy-start | bytes 16
  25.0 20.2 %copy-start.74 = (pred[2,2]{1,0:T(4,128)(4,1)}, pred[2,2]{1,0:T(4,128)(4,1)S(1)}, u32[]{:S(2)}) copy-start(pred[2,2]{1,0:T(4,128)(4,1)S(1)} %get-tuple-element.99) | copy-start | bytes 16
  25.0 20.5 %copy-start.72 = (pred[2,2]{1,0:T(4,128)(4,1)}, pred[2,2]{1,0:T(4,128)(4,1)S(1)}, u32[]{:S(2)}) copy-start(pred[2,2]{1,0:T(4,128)(4,1)S(1)} %get-tuple-element.100) | copy-start | bytes 16
  25.0 20.7 %copy-start.70 = (pred[2,2]{1,0:T(4,128)(4,1)}, pred[2,2]{1,0:T(4,128)(4,1)S(1)}, u32[]{:S(2)}) copy-start(pred[2,2]{1,0:T(4,128)(4,1)S(1)} %get-tuple-element.101) | copy-start | bytes 16
  25.0 20.9 %copy-start.68 = (pred[2,2]{1,0:T(4,128)(4,1)}, pred[2,2]{1,0:T(4,128)(4,1)S(1)}, u32[]{:S(2)}) copy-start(pred[2,2]{1,0:T(4,128)(4,1)S(1)} %get-tuple-element.103) | copy-start | bytes 16
  25.0 21.8 %copy-start.66 = (pred[2,2]{1,0:T(4,128)(4,1)}, pred[2,2]{1,0:T(4,128)(4,1)S(1)}, u32[]{:S(2)}) copy-start(pred[2,2]{1,0:T(4,128)(4,1)S(1)} %get-tuple-element.104) | copy-start | bytes 16
  25.1 22.6 %copy-start.64 = (pred[2,2]{1,0:T(4,128)(4,1)}, pred[2,2]{1,0:T(4,128)(4,1)S(1)}, u32[]{:S(2)}) copy-start(pred[2,2]{1,0:T(4,128)(4,1)S(1)} %get-tuple-element.97) | copy-start | bytes 16
  25.1 23.4 %copy-start.78 = (pred[2,2]{1,0:T(4,128)(4,1)}, pred[2,2]{1,0:T(4,128)(4,1)S(1)}, u32[]{:S(2)}) copy-start(pred[2,2]{1,0:T(4,128)(4,1)S(1)} %get-tuple-element.105) | copy-start | bytes 16
  25.1 24.2 %copy-start.69 = (pred[2,2]{1,0:T(4,128)(4,1)}, pred[2,2]{1,0:T(4,128)(4,1)S(1)}, u32[]{:S(2)}) copy-start(pred[2,2]{1,0:T(4,128)(4,1)S(1)} %get-tuple-element.102) | copy-start | bytes 16
  30.2 9.3 %collective-permute-start.6 = (bf16[32,8,512]{2,1,0:T(8,128)(2,1)S(1)}, bf16[32,8,512]{2,1,0:T(8,128)(2,1)S(1)}, u32[]{:S(2)}, u32[]{:S(2)}) collective-permute-start(bf16[32,8,512]{2,1,0:T(8,128)(2,1)S(1)} %get-tuple-element.59), channel_id=1, source_target_pairs={{0,1},{1,2},{2,3},{4,5},{5,6},{6,7},{8,9},{9,10},{10,11},{12,13},{... | collective-permute-start | bytes 786440 | tf_op jit(solution)/shard_map/ppermute | solution.py:23
  31.5 8.0 %collective-permute-start.7 = (bf16[32,8,512]{2,1,0:T(8,128)(2,1)S(1)}, bf16[32,8,512]{2,1,0:T(8,128)(2,1)S(1)}, u32[]{:S(2)}, u32[]{:S(2)}) collective-permute-start(bf16[32,8,512]{2,1,0:T(8,128)(2,1)S(1)} %get-tuple-element.60), channel_id=1, source_target_pairs={{1,0},{2,1},{3,2},{5,4},{6,5},{7,6},{9,8},{10,9},{11,10},{13,12},{... | collective-permute-start | bytes 786440 | tf_op jit(solution)/shard_map/ppermute | solution.py:26
  33.0 6.8 %collective-permute-start.2 = (bf16[32,8,512]{2,1,0:T(8,128)(2,1)S(1)}, bf16[32,8,512]{2,1,0:T(8,128)(2,1)S(1)}, u32[]{:S(2)}, u32[]{:S(2)}) collective-permute-start(bf16[32,8,512]{2,1,0:T(8,128)(2,1)S(1)} %get-tuple-element.63), channel_id=1, source_target_pairs={{0,1},{1,2},{2,3},{4,5},{5,6},{6,7},{8,9},{9,10},{10,11},{12,13},{... | collective-permute-start | bytes 786440 | tf_op jit(solution)/shard_map/ppermute | solution.py:23
  37.7 4.8 %collective-permute-start.3 = (bf16[32,8,512]{2,1,0:T(8,128)(2,1)S(1)}, bf16[32,8,512]{2,1,0:T(8,128)(2,1)}, u32[]{:S(2)}, u32[]{:S(2)}) collective-permute-start(bf16[32,8,512]{2,1,0:T(8,128)(2,1)S(1)} %get-tuple-element.64), channel_id=1, source_target_pairs={{1,0},{2,1},{3,2},{5,4},{6,5},{7,6},{9,8},{10,9},{11,10},{13,12},{... | collective-permute-start | bytes 786440 | tf_op jit(solution)/shard_map/ppermute | solution.py:26
  39.5 9.8 %copy-start.49 = (bf16[2,2,64,2,128]{4,3,2,1,0:T(2,128)(2,1)}, bf16[2,2,64,2,128]{4,3,2,1,0:T(2,128)(2,1)S(1)}, u32[]{:S(2)}) copy-start(bf16[2,2,64,2,128]{4,3,2,1,0:T(2,128)(2,1)S(1)} %reshape_reshape.29) | copy-start | bytes 393220
  79.5 6.4 %copy-start.14 = (bf16[2,2,8,2,8,128]{5,4,3,2,1,0:T(8,128)(2,1)S(1)}, bf16[2,2,8,2,8,128]{5,4,3,2,1,0:T(8,128)(2,1)}, u32[]{:S(2)}) copy-start(bf16[2,2,8,2,8,128]{5,4,3,2,1,0:T(8,128)(2,1)} %get-tuple-element.37) | copy-start | bytes 393220
  81.7 5.5 %copy-start.12 = (bf16[2,2,8,2,8,128]{5,4,3,2,1,0:T(8,128)(2,1)S(1)}, bf16[2,2,8,2,8,128]{5,4,3,2,1,0:T(8,128)(2,1)}, u32[]{:S(2)}) copy-start(bf16[2,2,8,2,8,128]{5,4,3,2,1,0:T(8,128)(2,1)} %get-tuple-element.36) | copy-start | bytes 393220
  88.7 5.5 %collective-permute-start.8 = (f32[8,16,4]{1,0,2:T(8,128)S(1)}, f32[8,16,4]{1,0,2:T(8,128)S(1)}, u32[]{:S(2)}, u32[]{:S(2)}) collective-permute-start(f32[8,16,4]{1,0,2:T(8,128)S(1)} %slice.413), channel_id=1, source_target_pairs={{0,4},{4,8},{8,12},{12,16},{16,20},{20,24},{24,28},{1,5},{5,9},{9,... | collective-permute-start | bytes 6152 | tf_op jit(solution)/shard_map/ppermute | solution.py:23
  91.5 14.9 %copy-start.33 = (bf16[2,2,8,2,8,128]{5,4,3,2,1,0:T(8,128)(2,1)S(1)}, bf16[2,2,8,2,8,128]{5,4,3,2,1,0:T(8,128)(2,1)}, u32[]{:S(2)}) copy-start(bf16[2,2,8,2,8,128]{5,4,3,2,1,0:T(8,128)(2,1)} %copy-done.32) | copy-start | bytes 393220
  91.5 14.9 %copy-start.38 = (bf16[2,2,8,2,8,128]{5,4,3,2,1,0:T(8,128)(2,1)S(1)}, bf16[2,2,8,2,8,128]{5,4,3,2,1,0:T(8,128)(2,1)}, u32[]{:S(2)}) copy-start(bf16[2,2,8,2,8,128]{5,4,3,2,1,0:T(8,128)(2,1)} %get-tuple-element.34) | copy-start | bytes 393220
  91.5 14.9 %copy-start.79 = (pred[2,2]{1,0:T(4,128)(4,1)S(1)}, pred[2,2]{1,0:T(4,128)(4,1)}, u32[]{:S(2)}) copy-start(pred[2,2]{1,0:T(4,128)(4,1)} %copy-done.78) | copy-start | bytes 16
  92.5 14.1 %copy-start.8 = (bf16[2,2,8,2,8,128]{5,4,3,2,1,0:T(8,128)(2,1)S(1)}, bf16[2,2,8,2,8,128]{5,4,3,2,1,0:T(8,128)(2,1)}, u32[]{:S(2)}) copy-start(bf16[2,2,8,2,8,128]{5,4,3,2,1,0:T(8,128)(2,1)} %get-tuple-element.33) | copy-start | bytes 393220
  92.8 12.5 %copy-start.51 = (bf16[2,8,2,8,256]{4,3,2,1,0:T(8,128)(2,1)}, bf16[2,8,2,8,256]{4,3,2,1,0:T(8,128)(2,1)S(1)}, u32[]{:S(2)}) copy-start(bf16[2,8,2,8,256]{4,3,2,1,0:T(8,128)(2,1)S(1)} %copy.440) | copy-start | bytes 393220
  93.0 6.0 %collective-permute-start.9 = (f32[8,16,4]{1,0,2:T(8,128)S(1)}, f32[8,16,4]{1,0,2:T(8,128)S(1)}, u32[]{:S(2)}, u32[]{:S(2)}) collective-permute-start(f32[8,16,4]{1,0,2:T(8,128)S(1)} %slice.415), channel_id=1, source_target_pairs={{4,0},{8,4},{12,8},{16,12},{20,16},{24,20},{28,24},{5,1},{9,5},{13... | collective-permute-start | bytes 6152 | tf_op jit(solution)/shard_map/ppermute | solution.py:26
  99.1 3.7 %collective-permute-start.10 = (f32[32,8,4]{1,0,2:T(8,128)S(1)}, f32[32,8,4]{1,0,2:T(8,128)S(1)}, u32[]{:S(2)}, u32[]{:S(2)}) collective-permute-start(f32[32,8,4]{1,0,2:T(8,128)S(1)} %get-tuple-element.75), channel_id=1, source_target_pairs={{0,1},{1,2},{2,3},{4,5},{5,6},{6,7},{8,9},{9,10},{10,11},{12,13},{... | collective-permute-start | bytes 12296 | tf_op jit(solution)/shard_map/ppermute | solution.py:23
  100.4 4.9 %collective-permute-start.11 = (f32[32,8,4]{1,0,2:T(8,128)S(1)}, f32[32,8,4]{1,0,2:T(8,128)S(1)}, u32[]{:S(2)}, u32[]{:S(2)}) collective-permute-start(f32[32,8,4]{1,0,2:T(8,128)S(1)} %get-tuple-element.76), channel_id=1, source_target_pairs={{1,0},{2,1},{3,2},{5,4},{6,5},{7,6},{9,8},{10,9},{11,10},{13,12},{... | collective-permute-start | bytes 12296 | tf_op jit(solution)/shard_map/ppermute | solution.py:26
  101.9 5.3 %copy-start.54 = (bf16[2,2,8,2,8,128]{5,4,3,2,1,0:T(8,128)(2,1)S(1)}, bf16[2,2,8,2,8,128]{5,4,3,2,1,0:T(8,128)(2,1)}, u32[]{:S(2)}) copy-start(bf16[2,2,8,2,8,128]{5,4,3,2,1,0:T(8,128)(2,1)} %get-tuple-element.18) | copy-start | bytes 393220
  125.6 4.5 %collective-permute-start.12 = (f32[512,256]{1,0:T(8,128)S(1)}, f32[512,256]{1,0:T(8,128)S(1)}, u32[]{:S(2)}, u32[]{:S(2)}) collective-permute-start(f32[512,256]{1,0:T(8,128)S(1)} %constant_dynamic-slice_fusion.4), channel_id=1, source_target_pairs={{0,1},{1,0},{2,3},{3,2},{4,5},{5,4},{6,7},{7,6},{8,9},{9,8},{10,11... | collective-permute-start | bytes 1572872 | tf_op jit(solution)/shard_map/ppermute | solution.py:197
  130.3 8.7 %collective-permute-start.13 = (f32[256,256]{1,0:T(8,128)S(1)}, f32[256,256]{1,0:T(8,128)S(1)}, u32[]{:S(2)}, u32[]{:S(2)}) collective-permute-start(f32[256,256]{1,0:T(8,128)S(1)} %constant_dynamic-slice_fusion.3), channel_id=1, source_target_pairs={{0,2},{1,3},{2,0},{3,1},{4,6},{5,7},{6,4},{7,5},{8,10},{9,11},{10,... | collective-permute-start | bytes 786440 | tf_op jit(solution)/shard_map/ppermute | solution.py:197
  139.0 6.2 %collective-permute-start.14 = (f32[128,256]{1,0:T(8,128)S(1)}, f32[128,256]{1,0:T(8,128)S(1)}, u32[]{:S(2)}, u32[]{:S(2)}) collective-permute-start(f32[128,256]{1,0:T(8,128)S(1)} %constant_dynamic-slice_fusion.2), channel_id=1, source_target_pairs={{0,4},{4,0},{8,12},{12,8},{16,20},{20,16},{24,28},{28,24},{1,5},{5... | collective-permute-start | bytes 393224 | tf_op jit(solution)/shard_map/ppermute | solution.py:197
  145.2 4.3 %collective-permute-start.15 = (f32[64,256]{1,0:T(8,128)S(1)}, f32[64,256]{1,0:T(8,128)S(1)}, u32[]{:S(2)}, u32[]{:S(2)}) collective-permute-start(f32[64,256]{1,0:T(8,128)S(1)} %constant_dynamic-slice_fusion.1), channel_id=1, source_target_pairs={{0,8},{4,12},{8,0},{12,4},{16,24},{20,28},{24,16},{28,20},{1,9},{5... | collective-permute-start | bytes 196616 | tf_op jit(solution)/shard_map/ppermute | solution.py:197
  149.6 26.7 %copy-start.26 = (bf16[256,256]{1,0:T(8,128)(2,1)S(1)}, bf16[256,256]{1,0:T(8,128)(2,1)}, u32[]{:S(2)}) copy-start(bf16[256,256]{1,0:T(8,128)(2,1)} %param.13) | copy-start | bytes 393220
  149.6 4.9 %collective-permute-start.16 = (f32[32,256]{1,0:T(8,128)S(1)}, f32[32,256]{1,0:T(8,128)S(1)}, u32[]{:S(2)}, u32[]{:S(2)}) collective-permute-start(f32[32,256]{1,0:T(8,128)S(1)} %constant_dynamic-slice_fusion), channel_id=1, source_target_pairs={{0,16},{4,20},{8,24},{12,28},{16,0},{20,4},{24,8},{28,12},{1,17},{... | collective-permute-start | bytes 98312 | tf_op jit(solution)/shard_map/ppermute | solution.py:197
  154.5 4.8 %collective-permute-start.17 = (f32[32,256]{1,0:T(8,128)S(1)}, f32[32,256]{1,0:T(8,128)S(1)}, u32[]{:S(2)}, u32[]{:S(2)}) collective-permute-start(f32[32,256]{1,0:T(8,128)S(1)} %dynamic-slice_add_fusion.4), channel_id=1, source_target_pairs={{0,16},{4,20},{8,24},{12,28},{16,0},{20,4},{24,8},{28,12},{1,17},{... | collective-permute-start | bytes 98312 | tf_op jit(solution)/shard_map/ppermute | solution.py:201
  159.3 17.8 %copy-start.52 = (bf16[2,8,2,8,256]{4,3,2,1,0:T(8,128)(2,1)S(1)}, bf16[2,8,2,8,256]{4,3,2,1,0:T(8,128)(2,1)}, u32[]{:S(2)}) copy-start(bf16[2,8,2,8,256]{4,3,2,1,0:T(8,128)(2,1)} %copy-done.51) | copy-start | bytes 393220
  159.3 17.8 %copy-start.57 = (bf16[256,256]{1,0:T(8,128)(2,1)S(1)}, bf16[256,256]{1,0:T(8,128)(2,1)}, u32[]{:S(2)}) copy-start(bf16[256,256]{1,0:T(8,128)(2,1)} %param.12) | copy-start | bytes 393220
  159.3 17.8 %copy-start.58 = (bf16[256,256]{1,0:T(8,128)(2,1)S(1)}, bf16[256,256]{1,0:T(8,128)(2,1)}, u32[]{:S(2)}) copy-start(bf16[256,256]{1,0:T(8,128)(2,1)} %param.11) | copy-start | bytes 393220
  159.3 17.8 %copy-start.59 = (bf16[256,256]{1,0:T(8,128)(2,1)S(1)}, bf16[256,256]{1,0:T(8,128)(2,1)}, u32[]{:S(2)}) copy-start(bf16[256,256]{1,0:T(8,128)(2,1)} %param.10) | copy-start | bytes 393220
  159.4 4.3 %collective-permute-start.18 = (f32[64,256]{1,0:T(8,128)S(1)}, f32[64,256]{1,0:T(8,128)S(1)}, u32[]{:S(2)}, u32[]{:S(2)}) collective-permute-start(f32[64,256]{1,0:T(8,128)S(1)} %pad_maximum_fusion.10), channel_id=1, source_target_pairs={{0,8},{4,12},{8,0},{12,4},{16,24},{20,28},{24,16},{28,20},{1,9},{5... | collective-permute-start | bytes 196616 | tf_op jit(solution)/shard_map/ppermute | solution.py:201
  163.7 5.9 %collective-permute-start.19 = (f32[128,256]{1,0:T(8,128)S(1)}, f32[128,256]{1,0:T(8,128)S(1)}, u32[]{:S(2)}, u32[]{:S(2)}) collective-permute-start(f32[128,256]{1,0:T(8,128)S(1)} %pad_maximum_fusion.8), channel_id=1, source_target_pairs={{0,4},{4,0},{8,12},{12,8},{16,20},{20,16},{24,28},{28,24},{1,5},{5... | collective-permute-start | bytes 393224 | tf_op jit(solution)/shard_map/ppermute | solution.py:201
  169.6 6.4 %collective-permute-start.20 = (f32[256,256]{1,0:T(8,128)S(1)}, f32[256,256]{1,0:T(8,128)S(1)}, u32[]{:S(2)}, u32[]{:S(2)}) collective-permute-start(f32[256,256]{1,0:T(8,128)S(1)} %pad_maximum_fusion.6), channel_id=1, source_target_pairs={{0,2},{1,3},{2,0},{3,1},{4,6},{5,7},{6,4},{7,5},{8,10},{9,11},{10,... | collective-permute-start | bytes 786440 | tf_op jit(solution)/shard_map/ppermute | solution.py:201
  176.2 2.0 %collective-permute-start.21 = (f32[512,256]{1,0:T(8,128)S(1)}, f32[512,256]{1,0:T(8,128)S(1)}, u32[]{:S(2)}, u32[]{:S(2)}) collective-permute-start(f32[512,256]{1,0:T(8,128)S(1)} %pad_maximum_fusion.5), channel_id=1, source_target_pairs={{0,1},{1,0},{2,3},{3,2},{4,5},{5,4},{6,7},{7,6},{8,9},{9,8},{10,11... | collective-permute-start | bytes 1572872 | tf_op jit(solution)/shard_map/ppermute | solution.py:201
  (55 other events, 155.3 us)
Sparse Core Ops, SparseCore 0:
  10.2 55.1 all-gather.2

commit v2 on v1

--- a/solution.py
+++ b/solution.py
@@ -180,6 +180,29 @@
     return steps
 
 
+def doubling_gather(joined, steps):
+    for axis, stride in reversed(steps):
+        pairs = [(i, i ^ stride) for i in range(lax.axis_size(axis))]
+        bit = (lax.axis_index(axis) // stride) % 2
+        got = lax.ppermute(joined, axis, pairs)
+        low = jnp.where(bit == 0, joined, got)
+        high = jnp.where(bit == 0, got, joined)
+        joined = jnp.concatenate([low, high], 0)
+    return joined
+
+
+def tree_gather(block, axis):
+    count = lax.axis_size(axis)
+    if count & (count - 1):
+        return lax.all_gather(block, axis, axis=0, tiled=True), lambda index: index
+    width = count.bit_length() - 1
+
+    def slot_of(index):
+        return sum(((index >> bit) & 1) << (width - 1 - bit) for bit in range(width))
+
+    return doubling_gather(block, halving_steps((axis,))), slot_of
+
+
 def tree_sum(parts, axes):
     sizes = [lax.axis_size(axis) for axis in axes]
     rows = sum(part.shape[0] for part in parts)
@@ -195,13 +218,7 @@
         keep = lax.dynamic_slice_in_dim(joined, bit * half, half, 0)
         send = lax.dynamic_slice_in_dim(joined, (1 - bit) * half, half, 0)
         joined = keep + lax.ppermute(send, axis, pairs)
-    for axis, stride in reversed(steps):
-        pairs = [(i, i ^ stride) for i in range(lax.axis_size(axis))]
-        bit = (lax.axis_index(axis) // stride) % 2
-        got = lax.ppermute(joined, axis, pairs)
-        low = jnp.where(bit == 0, joined, got)
-        high = jnp.where(bit == 0, got, joined)
-        joined = jnp.concatenate([low, high], 0)
+    joined = doubling_gather(joined, steps)
     out = []
     start = 0
     for part in parts:
@@ -236,8 +253,8 @@
         region_memory.shape[2], region_memory.shape[3], region_memory.shape[4]
     )
     region_count = memory_local.shape[0]
-    row_tables = lax.all_gather(memory_local, "gx", axis=0, tiled=True)
-    fetched = jnp.take(row_tables, owners * region_count + local_ids, axis=0)
+    row_tables, slot_of = tree_gather(memory_local, "gx")
+    fetched = jnp.take(row_tables, slot_of(owners) * region_count + local_ids, axis=0)
     region_keyval = fetched.reshape(
         block_rows, block_cols, 2, memory_local.shape[1], memory_local.shape[2]
     )

time: 188 us -> 191 us (1.016)
  between operations: 16 us -> 2.68 us
  matrix products: 44.2 us -> 56.6 us
  waiting for transfers between devices: 66.3 us -> 70.9 us
  local copies, waits for them, and re-layouts: 15.3 us -> 11.8 us
  starting transfers between devices: 41.2 us -> 43.6 us
    ppermute x5 -> x8, waiting for transfers between devices: 16.6 us -> 41.5 us  [doubling_gather(): got = lax.ppermute(joined, axis, pairs)]
    all_gather x1 -> x0, waiting for transfers between devices: 13.7 us -> none  [on_device(): row_tables = lax.all_gather(memory_local, 'gx', axis=0, tiled=True)]
    ppermute x5 -> x8, starting transfers between devices: 4.94 us -> 12.6 us  [doubling_gather(): got = lax.ppermute(joined, axis, pairs)]
    dot_general x9, matrix products: 8.41 us -> 15.1 us  [key_grads(): jnp.einsum('abhqk,abqhe->abkhe', grad_score, query_heads, preferred_eleme...]
    dot_general x10, matrix products: 6.21 us -> 10 us  [piece_scores(): jnp.einsum('abqhe,abkhe->abhqk', query_heads, split_heads(key_part), pref...]
    ppermute x6, starting transfers between devices: 20.1 us -> 16.4 us  [padded(): lax.ppermute(lax.slice_in_dim(block, block.shape[dim] - width, None, axis...]
    ppermute x6, waiting for transfers between devices: 11.4 us -> 7.76 us  [padded(): lax.ppermute(lax.slice_in_dim(block, 0, width, axis=dim), axis, backward)]
    ppermute x6, waiting for transfers between devices: 3.5 us -> 0.02 us  [padded(): lax.ppermute(lax.slice_in_dim(block, block.shape[dim] - width, None, axis...]
  transfers between devices with their start and end apart: 23 -> 25, of which waited for: 16 -> 15; matrix products, arithmetic and copies ran while one was open for 10% -> 11% of each run, Pallas kernels for 0% -> 0%
where the time goes in v2:
time: 191 us; the launch traced here: 190 us
  waiting for transfers between devices  70.9 us (37%)
  matrix products  56.6 us (30%)
  starting transfers between devices  43.6 us (23%)
  local copies, waits for them, and re-layouts  11.8 us (6%)
  other arithmetic  4.44 us (2%)
  between operations  2.68 us (1%)
    ppermute x8, waiting for transfers between devices, doubling_gather(): got = lax.ppermute(joined, axis, pairs)  41.5 us
    ppermute x5, waiting for transfers between devices, tree_sum(): joined = keep + lax.ppermute(send, axis, pairs)  21.7 us
    ppermute x6, starting transfers between devices, padded(): lax.ppermute(lax.slice_in_dim(block, block.shape[dim] - width, None, axis...  16.4 us
    dot_general x9, matrix products, key_grads(): jnp.einsum('abhqk,abqhe->abkhe', grad_score, query_heads, preferred_eleme...  15.1 us
    dot_general x10, matrix products, query_grads(): jnp.einsum('abhqk,abkhe->abqhe', grad_score, split_heads(key_part), prefe...  13.1 us
    ppermute x8, starting transfers between devices, doubling_gather(): got = lax.ppermute(joined, axis, pairs)  12.6 us
    dot_general x10, matrix products, piece_scores(): jnp.einsum('abqhe,abkhe->abhqk', query_heads, split_heads(key_part), pref...  10 us
    ppermute x6, starting transfers between devices, padded(): lax.ppermute(lax.slice_in_dim(block, 0, width, axis=dim), axis, backward)  7.92 us
  transfers between devices with their start and end apart: 25, of which 15 were waited for; matrix products, arithmetic and copies ran while one was open for 11% of the time, Pallas kernels for 0%

profile of v2, /device:TPU:0, one launch (start us, length us, event | category | flops | bytes accessed | tf_op | source)
XLA Modules:
  0.0 190.1 jit_solution(12258573576800108807)
XLA Ops:
  0.7 4.1 %collective-permute-start.4 = (bf16[4,64,512]{2,1,0:T(8,128)(2,1)}, bf16[4,64,512]{2,1,0:T(8,128)(2,1)S(1)}, u32[]{:S(2)}, u32[]{:S(2)}) collective-permute-start(bf16[4,64,512]{2,1,0:T(8,128)(2,1)} %bitcast.498), channel_id=1, source_target_pairs={{0,16},{4,20},{8,24},{12,28},{16,0},{20,4},{24,8},{28,12},{1,17},{... | collective-permute-start | bytes 786440 | tf_op jit(solution)/shard_map/ppermute | solution.py:187
  6.0 3.4 %collective-permute-start = (bf16[8,16,512]{2,1,0:T(8,128)(2,1)S(1)}, bf16[8,16,512]{2,1,0:T(8,128)(2,1)S(1)}, u32[]{:S(2)}, u32[]{:S(2)}) collective-permute-start(bf16[8,16,512]{2,1,0:T(8,128)(2,1)S(1)} %bitcast.504), channel_id=1, source_target_pairs={{0,4},{4,8},{8,12},{12,16},{16,20},{20,24},{24,28},{1,5},{5,9},{9,... | collective-permute-start | bytes 393224 | tf_op jit(solution)/shard_map/ppermute | solution.py:23
  9.4 1.3 collective-permute-start.1
  13.0 4.6 %collective-permute-start.7 = (bf16[8,16,512]{2,1,0:T(8,128)(2,1)S(1)}, bf16[8,16,512]{2,1,0:T(8,128)(2,1)S(1)}, u32[]{:S(2)}, u32[]{:S(2)}) collective-permute-start(bf16[8,16,512]{2,1,0:T(8,128)(2,1)S(1)} %get-tuple-element.73), channel_id=1, source_target_pairs={{0,4},{4,8},{8,12},{12,16},{16,20},{20,24},{24,28},{1,5},{5,9},{9,... | collective-permute-start | bytes 393224 | tf_op jit(solution)/shard_map/ppermute | solution.py:23
  17.6 1.3 collective-permute-start.8
  20.1 1.3 collective-permute-start.2
  21.4 1.3 collective-permute-start.3
  22.7 2.1 %collective-permute-done.8 = bf16[8,16,512]{2,1,0:T(8,128)(2,1)S(1)} collective-permute-done((bf16[8,16,512]{2,1,0:T(8,128)(2,1)S(1)}, bf16[8,16,512]{2,1,0:T(8,128)(2,1)S(1)}, u32[]{:S(2)}, u32[]{:S(2)}) %collective-permute-start.8) | collective-permute-done | bytes 131104 | tf_op jit(solution)/shard_map/ppermute | solution.py:26
  25.0 1.3 collective-permute-start.10
  26.3 3.3 %collective-permute-start.9 = (bf16[32,8,512]{2,1,0:T(8,128)(2,1)S(1)}, bf16[32,8,512]{2,1,0:T(8,128)(2,1)S(1)}, u32[]{:S(2)}, u32[]{:S(2)}) collective-permute-start(bf16[32,8,512]{2,1,0:T(8,128)(2,1)S(1)} %get-tuple-element.63), channel_id=1, source_target_pairs={{0,1},{1,2},{2,3},{4,5},{5,6},{6,7},{8,9},{9,10},{10,11},{12,13},{... | collective-permute-start | bytes 786440 | tf_op jit(solution)/shard_map/ppermute | solution.py:23
  29.7 4.6 %collective-permute-start.5 = (bf16[8,64,512]{2,1,0:T(8,128)(2,1)S(1)}, bf16[8,64,512]{2,1,0:T(8,128)(2,1)S(1)}, u32[]{:S(2)}, u32[]{:S(2)}) collective-permute-start(bf16[8,64,512]{2,1,0:T(8,128)(2,1)S(1)} %pad_maximum_fusion.6), channel_id=1, source_target_pairs={{0,8},{4,12},{8,0},{12,4},{16,24},{20,28},{24,16},{28,20},{1,9},{5... | collective-permute-start | bytes 1572872 | tf_op jit(solution)/shard_map/ppermute | solution.py:187
  38.7 1.5 fusion.451
  40.2 1.5 fusion.453
  41.8 4.3 %collective-permute-done.5 = bf16[8,64,512]{2,1,0:T(8,128)(2,1)S(1)} collective-permute-done((bf16[8,64,512]{2,1,0:T(8,128)(2,1)S(1)}, bf16[8,64,512]{2,1,0:T(8,128)(2,1)S(1)}, u32[]{:S(2)}, u32[]{:S(2)}) %collective-permute-start.5) | collective-permute-done | bytes 524320 | tf_op jit(solution)/shard_map/ppermute | solution.py:187
  47.4 1.5 fusion.454
  48.9 1.5 fusion.456
  51.3 1.5 slice_bitcast_fusion
  52.8 19.4 %collective-permute-done.6 = bf16[16,64,512]{2,1,0:T(8,128)(2,1)S(1)} collective-permute-done((bf16[16,64,512]{2,1,0:T(8,128)(2,1)S(1)}, bf16[16,64,512]{2,1,0:T(8,128)(2,1)S(1)}, u32[]{:S(2)}, u32[]{:S(2)}) %collective-permute-start.6) | collective-permute-done | bytes 1048608 | tf_op jit(solution)/shard_map/ppermute | solution.py:187
  72.5 1.4 gather_fusion
  82.7 2.1 %fusion.84 = f32[2,2,2,128,64]{3,4,2,1,0:T(8,128)} fusion(f32[2,2,2,64,64]{3,4,2,1,0:T(8,128)S(1)} %get-tuple-element.129, f32[2,2,2,64]{3,2,1,0:T(2,128)S(1)} %bitcast.470, f32[2,2,2,64]{3,2,1,0:T(2,128)S(1)} %log_add_fusion, bf16[2,2,8,2,8,128]{5,4,3,2,1,0:T(8,128)(2,1)} %copy-done.53, bf16[2,2,8,2,8,128]{5,4,3,2,1,0:T(8,128)(2,1)} %get-tuple-element.54, ...), kind=kOutput, calls=%fused_computation.166 | convolution fusion | flops 16908288 | bytes 790528 | tf_op jit(solution)/shard_map/abhqk,abkhe->abqhe/dot_general | solution.py:115
  84.7 2.2 %convolution_add_fusion.24 = f32[2,2,2,128,64]{3,4,2,1,0:T(8,128)} fusion(f32[2,2,2,128,64]{3,4,2,1,0:T(8,128)} %fusion.84, f32[2,2,2,64,64]{3,4,2,1,0:T(8,128)S(1)} %copy-done.5, f32[2,2,2,64]{3,2,1,0:T(2,128)S(1)} %bitcast.472, f32[2,2,2,64]{3,2,1,0:T(2,128)S(1)} %log_add_fusion, bf16[2,2,8,2,8,128]{5,4,3,2,1,0:T(8,128)(2,1)} %get-tuple-element.44, ...), kind=kOutput, calls=%fused_computation.99 | convolution fusion | flops 16973824 | bytes 1052672 | tf_op jit(solution)/shard_map/abhqk,abkhe->abqhe/dot_general | solution.py:115
  87.0 2.2 %convolution_add_fusion.23 = f32[2,2,2,128,64]{3,4,2,1,0:T(8,128)} fusion(f32[2,2,2,128,64]{3,4,2,1,0:T(8,128)} %convolution_add_fusion.24, f32[2,2,2,64,64]{3,4,2,1,0:T(8,128)S(1)} %copy-done.4, f32[2,2,2,64]{3,2,1,0:T(2,128)S(1)} %bitcast.473, f32[2,2,2,64]{3,2,1,0:T(2,128)S(1)} %log_add_fusion, bf16[2,2,8,2,8,128]{5,4,3,2,1,0:T(8,128)(2,1)} %get-tuple-element.43, ...), kind=kOutput, calls=%fused_computation.96 | convolution fusion | flops 16973824 | bytes 1052672 | tf_op jit(solution)/shard_map/abhqk,abkhe->abqhe/dot_general | solution.py:115
  89.2 1.4 convolution_add_fusion.22
  90.7 1.3 convolution_add_fusion.21
  92.0 1.3 convolution_add_fusion.20
  93.4 1.3 convolution_add_fusion.19
  96.5 2.6 %collective-permute-start.11 = (f32[8,16,4]{1,0,2:T(8,128)S(1)}, f32[8,16,4]{1,0,2:T(8,128)S(1)}, u32[]{:S(2)}, u32[]{:S(2)}) collective-permute-start(f32[8,16,4]{1,0,2:T(8,128)S(1)} %slice.413), channel_id=1, source_target_pairs={{0,4},{4,8},{8,12},{12,16},{16,20},{20,24},{24,28},{1,5},{5,9},{9,... | collective-permute-start | bytes 6152 | tf_op jit(solution)/shard_map/ppermute | solution.py:23
  101.9 4.9 %collective-permute-done.12 = f32[8,16,4]{1,0,2:T(8,128)S(1)} collective-permute-done((f32[8,16,4]{1,0,2:T(8,128)S(1)}, f32[8,16,4]{1,0,2:T(8,128)S(1)}, u32[]{:S(2)}, u32[]{:S(2)}) %collective-permute-start.12) | collective-permute-done | bytes 2080 | tf_op jit(solution)/shard_map/ppermute | solution.py:26
  106.9 1.3 collective-permute-start.13
  108.2 1.5 collective-permute-start.14
  116.7 2.1 %convolution_add_fusion.15 = f32[2,2,2,128,64]{3,4,2,1,0:T(8,128)} fusion(f32[2,2,2,128,64]{3,4,2,1,0:T(8,128)} %fusion.82, f32[2,2,2,64,64]{3,4,2,1,0:T(8,128)S(1)} %fusion.32, f32[2,2,2,64]{3,2,1,0:T(2,128)} %get-tuple-element.99, bf16[2,2,8,2,8,128]{5,4,3,2,1,0:T(8,128)(2,1)S(1)} %copy-done.12, bf16[2,2,8,2,8,128]{5,4,3,2,1,0:T(8,128)(2,1)} %get-tuple-element.34, ...), kind=kOutput, calls=%fused_computation.19 | convolution fusion | flops 16941056 | bytes 1050624 | tf_op jit(solution)/shard_map/abhqk,abqhe->abkhe/dot_general | solution.py:154
  118.7 2.2 %convolution_add_fusion.14 = f32[2,2,2,128,64]{3,4,2,1,0:T(8,128)} fusion(f32[2,2,2,128,64]{3,4,2,1,0:T(8,128)} %convolution_add_fusion.15, f32[2,2,2,64,64]{3,4,2,1,0:T(8,128)} %fusion.28, f32[2,2,2,64]{3,2,1,0:T(2,128)} %get-tuple-element.97, bf16[2,2,8,2,8,128]{5,4,3,2,1,0:T(8,128)(2,1)S(1)} %copy-done.11, ...), kind=kOutput, calls=%fused_computation.18 | convolution fusion | flops 16941056 | bytes 1050624 | tf_op jit(solution)/shard_map/abhqk,abqhe->abkhe/dot_general | solution.py:154
  120.9 2.1 %convolution_add_fusion.13 = f32[2,2,2,128,64]{3,4,2,1,0:T(8,128)} fusion(f32[2,2,2,128,64]{3,4,2,1,0:T(8,128)} %convolution_add_fusion.14, f32[2,2,2,64,64]{3,4,2,1,0:T(8,128)S(1)} %fusion.24, f32[2,2,2,64]{3,2,1,0:T(2,128)} %get-tuple-element.95, bf16[2,2,8,2,8,128]{5,4,3,2,1,0:T(8,128)(2,1)S(1)} %copy-done.10, ...), kind=kOutput, calls=%fused_computation.17 | convolution fusion | flops 16941056 | bytes 1050624 | tf_op jit(solution)/shard_map/abhqk,abqhe->abkhe/dot_general | solution.py:154
  123.0 1.4 convolution_add_fusion.12
  124.4 1.9 %convolution_add_fusion.11 = f32[2,2,2,128,64]{3,4,2,1,0:T(8,128)} fusion(f32[2,2,2,128,64]{3,4,2,1,0:T(8,128)S(1)} %convolution_add_fusion.12, f32[2,2,2,64,64]{3,4,2,1,0:T(8,128)S(1)} %fusion.16, f32[2,2,2,64]{3,2,1,0:T(2,128)S(1)} %get-tuple-element.91, bf16[2,2,8,2,8,128]{5,4,3,2,1,0:T(8,128)(2,1)S(1)} %copy-done.8, ...), kind=kOutput, calls=%fused_computation.15 | convolution fusion | flops 16941056 | bytes 1050624 | tf_op jit(solution)/shard_map/abhqk,abqhe->abkhe/dot_general | solution.py:154
  126.3 2.0 %convolution_add_fusion.10 = f32[2,2,2,128,64]{3,4,2,1,0:T(8,128)} fusion(f32[2,2,2,128,64]{3,4,2,1,0:T(8,128)} %convolution_add_fusion.11, f32[2,2,2,64,64]{3,4,2,1,0:T(8,128)S(1)} %fusion.12, f32[2,2,2,64]{3,2,1,0:T(2,128)S(1)} %get-tuple-element.89, bf16[2,2,8,2,8,128]{5,4,3,2,1,0:T(8,128)(2,1)S(1)} %copy-done.7, ...), kind=kOutput, calls=%fused_computation.14 | convolution fusion | flops 16941056 | bytes 1050624 | tf_op jit(solution)/shard_map/abhqk,abqhe->abkhe/dot_general | solution.py:154
  136.9 2.4 %collective-permute-start.15 = (f32[512,256]{1,0:T(8,128)S(1)}, f32[512,256]{1,0:T(8,128)S(1)}, u32[]{:S(2)}, u32[]{:S(2)}) collective-permute-start(f32[512,256]{1,0:T(8,128)S(1)} %constant_dynamic-slice_fusion.4), channel_id=1, source_target_pairs={{0,1},{1,0},{2,3},{3,2},{4,5},{5,4},{6,7},{7,6},{8,9},{9,8},{10,11... | collective-permute-start | bytes 1572872 | tf_op jit(solution)/shard_map/ppermute | solution.py:220
  139.3 1.5 collective-permute-done.15
  141.3 8.4 %collective-permute-done.16 = f32[256,256]{1,0:T(8,128)S(1)} collective-permute-done((f32[256,256]{1,0:T(8,128)S(1)}, f32[256,256]{1,0:T(8,128)S(1)}, u32[]{:S(2)}, u32[]{:S(2)}) %collective-permute-start.16) | collective-permute-done | bytes 262176 | tf_op jit(solution)/shard_map/ppermute | solution.py:220
  149.7 3.0 %collective-permute-start.17 = (f32[128,256]{1,0:T(8,128)S(1)}, f32[128,256]{1,0:T(8,128)S(1)}, u32[]{:S(2)}, u32[]{:S(2)}) collective-permute-start(f32[128,256]{1,0:T(8,128)S(1)} %constant_dynamic-slice_fusion.2), channel_id=1, source_target_pairs={{0,4},{4,0},{8,12},{12,8},{16,20},{20,16},{24,28},{28,24},{1,5},{5... | collective-permute-start | bytes 393224 | tf_op jit(solution)/shard_map/ppermute | solution.py:220
  152.7 3.2 %collective-permute-done.17 = f32[128,256]{1,0:T(8,128)S(1)} collective-permute-done((f32[128,256]{1,0:T(8,128)S(1)}, f32[128,256]{1,0:T(8,128)S(1)}, u32[]{:S(2)}, u32[]{:S(2)}) %collective-permute-start.17) | collective-permute-done | bytes 131104 | tf_op jit(solution)/shard_map/ppermute | solution.py:220
  156.0 4.2 %collective-permute-done.18 = f32[64,256]{1,0:T(8,128)S(1)} collective-permute-done((f32[64,256]{1,0:T(8,128)S(1)}, f32[64,256]{1,0:T(8,128)S(1)}, u32[]{:S(2)}, u32[]{:S(2)}) %collective-permute-start.18) | collective-permute-done | bytes 65568 | tf_op jit(solution)/shard_map/ppermute | solution.py:220
  161.2 4.4 %collective-permute-done.19 = f32[32,256]{1,0:T(8,128)S(1)} collective-permute-done((f32[32,256]{1,0:T(8,128)S(1)}, f32[32,256]{1,0:T(8,128)S(1)}, u32[]{:S(2)}, u32[]{:S(2)}) %collective-permute-start.19) | collective-permute-done | bytes 32800 | tf_op jit(solution)/shard_map/ppermute | solution.py:220
  166.0 4.4 %collective-permute-done.20 = f32[32,256]{1,0:T(8,128)S(1)} collective-permute-done((f32[32,256]{1,0:T(8,128)S(1)}, f32[32,256]{1,0:T(8,128)S(1)}, u32[]{:S(2)}, u32[]{:S(2)}) %collective-permute-start.20) | collective-permute-done | bytes 32800 | tf_op jit(solution)/shard_map/ppermute | solution.py:187
  170.5 4.3 %collective-permute-done.21 = f32[64,256]{1,0:T(8,128)S(1)} collective-permute-done((f32[64,256]{1,0:T(8,128)S(1)}, f32[64,256]{1,0:T(8,128)S(1)}, u32[]{:S(2)}, u32[]{:S(2)}) %collective-permute-start.21) | collective-permute-done | bytes 65568 | tf_op jit(solution)/shard_map/ppermute | solution.py:187
  174.8 2.0 %collective-permute-start.22 = (f32[128,256]{1,0:T(8,128)S(1)}, f32[128,256]{1,0:T(8,128)S(1)}, u32[]{:S(2)}, u32[]{:S(2)}) collective-permute-start(f32[128,256]{1,0:T(8,128)S(1)} %pad_maximum_fusion.11), channel_id=1, source_target_pairs={{0,4},{4,0},{8,12},{12,8},{16,20},{20,16},{24,28},{28,24},{1,5},{5... | collective-permute-start | bytes 393224 | tf_op jit(solution)/shard_map/ppermute | solution.py:187
  176.8 3.0 %collective-permute-done.22 = f32[128,256]{1,0:T(8,128)S(1)} collective-permute-done((f32[128,256]{1,0:T(8,128)S(1)}, f32[128,256]{1,0:T(8,128)S(1)}, u32[]{:S(2)}, u32[]{:S(2)}) %collective-permute-start.22) | collective-permute-done | bytes 131104 | tf_op jit(solution)/shard_map/ppermute | solution.py:187
  180.3 6.1 %collective-permute-done.23 = f32[256,256]{1,0:T(8,128)S(1)} collective-permute-done((f32[256,256]{1,0:T(8,128)S(1)}, f32[256,256]{1,0:T(8,128)S(1)}, u32[]{:S(2)}, u32[]{:S(2)}) %collective-permute-start.23) | collective-permute-done | bytes 262176 | tf_op jit(solution)/shard_map/ppermute | solution.py:187
  (338 shorter events, 45.7 us)
Async XLA Ops:
  0.6 18.3 %copy-start.68 = (s32[1,1,4,2]{2,3,1,0:T(2,128)S(1)}, s32[1,1,4,2]{2,3,1,0:T(2,128)}, u32[]{:S(2)}) copy-start(s32[1,1,4,2]{2,3,1,0:T(2,128)} %param.15) | copy-start | bytes 100
  0.7 18.3 %copy-start.67 = (s32[1,1,4,2]{2,3,1,0:T(2,128)S(1)}, s32[1,1,4,2]{2,3,1,0:T(2,128)}, u32[]{:S(2)}) copy-start(s32[1,1,4,2]{2,3,1,0:T(2,128)} %param.16) | copy-start | bytes 100
  0.7 28.9 %collective-permute-start.4 = (bf16[4,64,512]{2,1,0:T(8,128)(2,1)}, bf16[4,64,512]{2,1,0:T(8,128)(2,1)S(1)}, u32[]{:S(2)}, u32[]{:S(2)}) collective-permute-start(bf16[4,64,512]{2,1,0:T(8,128)(2,1)} %bitcast.498), channel_id=1, source_target_pairs={{0,16},{4,20},{8,24},{12,28},{16,0},{20,4},{24,8},{28,12},{1,17},{... | collective-permute-start | bytes 786440 | tf_op jit(solution)/shard_map/ppermute | solution.py:187
  6.0 14.0 %collective-permute-start = (bf16[8,16,512]{2,1,0:T(8,128)(2,1)S(1)}, bf16[8,16,512]{2,1,0:T(8,128)(2,1)S(1)}, u32[]{:S(2)}, u32[]{:S(2)}) collective-permute-start(bf16[8,16,512]{2,1,0:T(8,128)(2,1)S(1)} %bitcast.504), channel_id=1, source_target_pairs={{0,4},{4,8},{8,12},{12,16},{16,20},{20,24},{24,28},{1,5},{5,9},{9,... | collective-permute-start | bytes 393224 | tf_op jit(solution)/shard_map/ppermute | solution.py:23
  9.4 10.6 %collective-permute-start.1 = (bf16[8,16,512]{2,1,0:T(8,128)(2,1)S(1)}, bf16[8,16,512]{2,1,0:T(8,128)(2,1)S(1)}, u32[]{:S(2)}, u32[]{:S(2)}) collective-permute-start(bf16[8,16,512]{2,1,0:T(8,128)(2,1)S(1)} %bitcast.503), channel_id=1, source_target_pairs={{4,0},{8,4},{12,8},{16,12},{20,16},{24,20},{28,24},{5,1},{9,5},{13... | collective-permute-start | bytes 393224 | tf_op jit(solution)/shard_map/ppermute | solution.py:26
  13.0 9.7 %collective-permute-start.7 = (bf16[8,16,512]{2,1,0:T(8,128)(2,1)S(1)}, bf16[8,16,512]{2,1,0:T(8,128)(2,1)S(1)}, u32[]{:S(2)}, u32[]{:S(2)}) collective-permute-start(bf16[8,16,512]{2,1,0:T(8,128)(2,1)S(1)} %get-tuple-element.73), channel_id=1, source_target_pairs={{0,4},{4,8},{8,12},{12,16},{16,20},{20,24},{24,28},{1,5},{5,9},{9,... | collective-permute-start | bytes 393224 | tf_op jit(solution)/shard_map/ppermute | solution.py:23
  17.6 7.3 %collective-permute-start.8 = (bf16[8,16,512]{2,1,0:T(8,128)(2,1)S(1)}, bf16[8,16,512]{2,1,0:T(8,128)(2,1)S(1)}, u32[]{:S(2)}, u32[]{:S(2)}) collective-permute-start(bf16[8,16,512]{2,1,0:T(8,128)(2,1)S(1)} %get-tuple-element.74), channel_id=1, source_target_pairs={{4,0},{8,4},{12,8},{16,12},{20,16},{24,20},{28,24},{5,1},{9,5},{13... | collective-permute-start | bytes 393224 | tf_op jit(solution)/shard_map/ppermute | solution.py:26
  19.4 16.4 %copy-start.77 = (pred[2,2]{1,0:T(4,128)(4,1)}, pred[2,2]{1,0:T(4,128)(4,1)S(1)}, u32[]{:S(2)}) copy-start(pred[2,2]{1,0:T(4,128)(4,1)S(1)} %get-tuple-element.108) | copy-start | bytes 16
  19.4 17.5 %copy-start.69 = (pred[2,2]{1,0:T(4,128)(4,1)}, pred[2,2]{1,0:T(4,128)(4,1)S(1)}, u32[]{:S(2)}) copy-start(pred[2,2]{1,0:T(4,128)(4,1)S(1)} %get-tuple-element.104) | copy-start | bytes 16
  19.4 17.7 %copy-start.71 = (pred[2,2]{1,0:T(4,128)(4,1)}, pred[2,2]{1,0:T(4,128)(4,1)S(1)}, u32[]{:S(2)}) copy-start(pred[2,2]{1,0:T(4,128)(4,1)S(1)} %get-tuple-element.105) | copy-start | bytes 16
  19.4 18.5 %copy-start.73 = (pred[2,2]{1,0:T(4,128)(4,1)}, pred[2,2]{1,0:T(4,128)(4,1)S(1)}, u32[]{:S(2)}) copy-start(pred[2,2]{1,0:T(4,128)(4,1)S(1)} %get-tuple-element.106) | copy-start | bytes 16
  19.4 19.3 %copy-start.75 = (pred[2,2]{1,0:T(4,128)(4,1)}, pred[2,2]{1,0:T(4,128)(4,1)S(1)}, u32[]{:S(2)}) copy-start(pred[2,2]{1,0:T(4,128)(4,1)S(1)} %get-tuple-element.107) | copy-start | bytes 16
  19.4 20.8 %copy-start.79 = (pred[2,2]{1,0:T(4,128)(4,1)}, pred[2,2]{1,0:T(4,128)(4,1)S(1)}, u32[]{:S(2)}) copy-start(pred[2,2]{1,0:T(4,128)(4,1)S(1)} %get-tuple-element.109) | copy-start | bytes 16
  19.4 28.0 %copy-start.81 = (pred[2,2]{1,0:T(4,128)(4,1)}, pred[2,2]{1,0:T(4,128)(4,1)S(1)}, u32[]{:S(2)}) copy-start(pred[2,2]{1,0:T(4,128)(4,1)S(1)} %get-tuple-element.110) | copy-start | bytes 16
  19.4 29.5 %copy-start.83 = (pred[2,2]{1,0:T(4,128)(4,1)}, pred[2,2]{1,0:T(4,128)(4,1)S(1)}, u32[]{:S(2)}) copy-start(pred[2,2]{1,0:T(4,128)(4,1)S(1)} %get-tuple-element.103) | copy-start | bytes 16
  19.4 31.0 %copy-start.85 = (pred[2,2]{1,0:T(4,128)(4,1)}, pred[2,2]{1,0:T(4,128)(4,1)S(1)}, u32[]{:S(2)}) copy-start(pred[2,2]{1,0:T(4,128)(4,1)S(1)} %get-tuple-element.111) | copy-start | bytes 16
  19.9 30.6 %copy-start.54 = (bf16[2,2,64,2,128]{4,3,2,1,0:T(2,128)(2,1)}, bf16[2,2,64,2,128]{4,3,2,1,0:T(2,128)(2,1)S(1)}, u32[]{:S(2)}) copy-start(bf16[2,2,64,2,128]{4,3,2,1,0:T(2,128)(2,1)S(1)} %reshape_reshape.29) | copy-start | bytes 393220
  20.1 14.2 %collective-permute-start.2 = (bf16[32,8,512]{2,1,0:T(8,128)(2,1)S(1)}, bf16[32,8,512]{2,1,0:T(8,128)(2,1)S(1)}, u32[]{:S(2)}, u32[]{:S(2)}) collective-permute-start(bf16[32,8,512]{2,1,0:T(8,128)(2,1)S(1)} %get-tuple-element.69), channel_id=1, source_target_pairs={{0,1},{1,2},{2,3},{4,5},{5,6},{6,7},{8,9},{9,10},{10,11},{12,13},{... | collective-permute-start | bytes 786440 | tf_op jit(solution)/shard_map/ppermute | solution.py:23
  21.4 12.9 %collective-permute-start.3 = (bf16[32,8,512]{2,1,0:T(8,128)(2,1)S(1)}, bf16[32,8,512]{2,1,0:T(8,128)(2,1)S(1)}, u32[]{:S(2)}, u32[]{:S(2)}) collective-permute-start(bf16[32,8,512]{2,1,0:T(8,128)(2,1)S(1)} %get-tuple-element.70), channel_id=1, source_target_pairs={{1,0},{2,1},{3,2},{5,4},{6,5},{7,6},{9,8},{10,9},{11,10},{13,12},{... | collective-permute-start | bytes 786440 | tf_op jit(solution)/shard_map/ppermute | solution.py:26
  25.0 22.2 %collective-permute-start.10 = (bf16[32,8,512]{2,1,0:T(8,128)(2,1)S(1)}, bf16[32,8,512]{2,1,0:T(8,128)(2,1)S(1)}, u32[]{:S(2)}, u32[]{:S(2)}) collective-permute-start(bf16[32,8,512]{2,1,0:T(8,128)(2,1)S(1)} %get-tuple-element.64), channel_id=1, source_target_pairs={{1,0},{2,1},{3,2},{5,4},{6,5},{7,6},{9,8},{10,9},{11,10},{13,12},{... | collective-permute-start | bytes 786440 | tf_op jit(solution)/shard_map/ppermute | solution.py:26
  26.3 20.9 %collective-permute-start.9 = (bf16[32,8,512]{2,1,0:T(8,128)(2,1)S(1)}, bf16[32,8,512]{2,1,0:T(8,128)(2,1)S(1)}, u32[]{:S(2)}, u32[]{:S(2)}) collective-permute-start(bf16[32,8,512]{2,1,0:T(8,128)(2,1)S(1)} %get-tuple-element.63), channel_id=1, source_target_pairs={{0,1},{1,2},{2,3},{4,5},{5,6},{6,7},{8,9},{9,10},{10,11},{12,13},{... | collective-permute-start | bytes 786440 | tf_op jit(solution)/shard_map/ppermute | solution.py:23
  29.7 16.3 %collective-permute-start.5 = (bf16[8,64,512]{2,1,0:T(8,128)(2,1)S(1)}, bf16[8,64,512]{2,1,0:T(8,128)(2,1)S(1)}, u32[]{:S(2)}, u32[]{:S(2)}) collective-permute-start(bf16[8,64,512]{2,1,0:T(8,128)(2,1)S(1)} %pad_maximum_fusion.6), channel_id=1, source_target_pairs={{0,8},{4,12},{8,0},{12,4},{16,24},{20,28},{24,16},{28,20},{1,9},{5... | collective-permute-start | bytes 1572872 | tf_op jit(solution)/shard_map/ppermute | solution.py:187
  35.8 13.1 %copy-start.52 = (bf16[2,2,8,2,8,128]{5,4,3,2,1,0:T(8,128)(2,1)}, bf16[2,2,8,2,8,128]{5,4,3,2,1,0:T(8,128)(2,1)S(1)}, u32[]{:S(2)}) copy-start(bf16[2,2,8,2,8,128]{5,4,3,2,1,0:T(8,128)(2,1)S(1)} %get-tuple-element.52) | copy-start | bytes 393220
  35.8 14.7 %copy-start.53 = (bf16[2,2,8,2,8,128]{5,4,3,2,1,0:T(8,128)(2,1)}, bf16[2,2,8,2,8,128]{5,4,3,2,1,0:T(8,128)(2,1)S(1)}, u32[]{:S(2)}) copy-start(bf16[2,2,8,2,8,128]{5,4,3,2,1,0:T(8,128)(2,1)S(1)} %get-tuple-element.53) | copy-start | bytes 393220
  46.2 26.0 %collective-permute-start.6 = (bf16[16,64,512]{2,1,0:T(8,128)(2,1)S(1)}, bf16[16,64,512]{2,1,0:T(8,128)(2,1)S(1)}, u32[]{:S(2)}, u32[]{:S(2)}) collective-permute-start(bf16[16,64,512]{2,1,0:T(8,128)(2,1)S(1)} %pad_maximum_fusion.2), channel_id=1, source_target_pairs={{0,4},{4,0},{8,12},{12,8},{16,20},{20,16},{24,28},{28,24},{1,5},{5... | collective-permute-start | bytes 3145736 | tf_op jit(solution)/shard_map/ppermute | solution.py:187
  95.5 14.2 %copy-start.56 = (bf16[16,16,256]{2,1,0:T(8,128)(2,1)S(1)}, bf16[16,16,256]{2,1,0:T(8,128)(2,1)}, u32[]{:S(2)}) copy-start(bf16[16,16,256]{2,1,0:T(8,128)(2,1)} %param.17) | copy-start | bytes 393220
  96.4 16.1 %copy-start.35 = (bf16[2,2,8,2,8,128]{5,4,3,2,1,0:T(8,128)(2,1)S(1)}, bf16[2,2,8,2,8,128]{5,4,3,2,1,0:T(8,128)(2,1)}, u32[]{:S(2)}) copy-start(bf16[2,2,8,2,8,128]{5,4,3,2,1,0:T(8,128)(2,1)} %copy-done.34) | copy-start | bytes 393220
  96.4 16.1 %copy-start.43 = (bf16[2,2,8,2,8,128]{5,4,3,2,1,0:T(8,128)(2,1)S(1)}, bf16[2,2,8,2,8,128]{5,4,3,2,1,0:T(8,128)(2,1)}, u32[]{:S(2)}) copy-start(bf16[2,2,8,2,8,128]{5,4,3,2,1,0:T(8,128)(2,1)} %get-tuple-element.36) | copy-start | bytes 393220
  96.4 16.1 %copy-start.86 = (pred[2,2]{1,0:T(4,128)(4,1)S(1)}, pred[2,2]{1,0:T(4,128)(4,1)}, u32[]{:S(2)}) copy-start(pred[2,2]{1,0:T(4,128)(4,1)} %copy-done.85) | copy-start | bytes 16
  96.5 5.4 %collective-permute-start.11 = (f32[8,16,4]{1,0,2:T(8,128)S(1)}, f32[8,16,4]{1,0,2:T(8,128)S(1)}, u32[]{:S(2)}, u32[]{:S(2)}) collective-permute-start(f32[8,16,4]{1,0,2:T(8,128)S(1)} %slice.413), channel_id=1, source_target_pairs={{0,4},{4,8},{8,12},{12,16},{16,20},{20,24},{24,28},{1,5},{5,9},{9,... | collective-permute-start | bytes 6152 | tf_op jit(solution)/shard_map/ppermute | solution.py:23
  100.3 6.5 %collective-permute-start.12 = (f32[8,16,4]{1,0,2:T(8,128)S(1)}, f32[8,16,4]{1,0,2:T(8,128)S(1)}, u32[]{:S(2)}, u32[]{:S(2)}) collective-permute-start(f32[8,16,4]{1,0,2:T(8,128)S(1)} %slice.415), channel_id=1, source_target_pairs={{4,0},{8,4},{12,8},{16,12},{20,16},{24,20},{28,24},{5,1},{9,5},{13... | collective-permute-start | bytes 6152 | tf_op jit(solution)/shard_map/ppermute | solution.py:26
  106.9 3.8 %collective-permute-start.13 = (f32[32,8,4]{1,0,2:T(8,128)S(1)}, f32[32,8,4]{1,0,2:T(8,128)S(1)}, u32[]{:S(2)}, u32[]{:S(2)}) collective-permute-start(f32[32,8,4]{1,0,2:T(8,128)S(1)} %get-tuple-element.81), channel_id=1, source_target_pairs={{0,1},{1,2},{2,3},{4,5},{5,6},{6,7},{8,9},{9,10},{10,11},{12,13},{... | collective-permute-start | bytes 12296 | tf_op jit(solution)/shard_map/ppermute | solution.py:23
  108.2 3.1 %collective-permute-start.14 = (f32[32,8,4]{1,0,2:T(8,128)S(1)}, f32[32,8,4]{1,0,2:T(8,128)S(1)}, u32[]{:S(2)}, u32[]{:S(2)}) collective-permute-start(f32[32,8,4]{1,0,2:T(8,128)S(1)} %get-tuple-element.82), channel_id=1, source_target_pairs={{1,0},{2,1},{3,2},{5,4},{6,5},{7,6},{9,8},{10,9},{11,10},{13,12},{... | collective-permute-start | bytes 12296 | tf_op jit(solution)/shard_map/ppermute | solution.py:26
  136.9 3.9 %collective-permute-start.15 = (f32[512,256]{1,0:T(8,128)S(1)}, f32[512,256]{1,0:T(8,128)S(1)}, u32[]{:S(2)}, u32[]{:S(2)}) collective-permute-start(f32[512,256]{1,0:T(8,128)S(1)} %constant_dynamic-slice_fusion.4), channel_id=1, source_target_pairs={{0,1},{1,0},{2,3},{3,2},{4,5},{5,4},{6,7},{7,6},{8,9},{9,8},{10,11... | collective-permute-start | bytes 1572872 | tf_op jit(solution)/shard_map/ppermute | solution.py:220
  141.0 8.7 %collective-permute-start.16 = (f32[256,256]{1,0:T(8,128)S(1)}, f32[256,256]{1,0:T(8,128)S(1)}, u32[]{:S(2)}, u32[]{:S(2)}) collective-permute-start(f32[256,256]{1,0:T(8,128)S(1)} %constant_dynamic-slice_fusion.3), channel_id=1, source_target_pairs={{0,2},{1,3},{2,0},{3,1},{4,6},{5,7},{6,4},{7,5},{8,10},{9,11},{10,... | collective-permute-start | bytes 786440 | tf_op jit(solution)/shard_map/ppermute | solution.py:220
  149.7 6.2 %collective-permute-start.17 = (f32[128,256]{1,0:T(8,128)S(1)}, f32[128,256]{1,0:T(8,128)S(1)}, u32[]{:S(2)}, u32[]{:S(2)}) collective-permute-start(f32[128,256]{1,0:T(8,128)S(1)} %constant_dynamic-slice_fusion.2), channel_id=1, source_target_pairs={{0,4},{4,0},{8,12},{12,8},{16,20},{20,16},{24,28},{28,24},{1,5},{5... | collective-permute-start | bytes 393224 | tf_op jit(solution)/shard_map/ppermute | solution.py:220
  155.9 4.3 %collective-permute-start.18 = (f32[64,256]{1,0:T(8,128)S(1)}, f32[64,256]{1,0:T(8,128)S(1)}, u32[]{:S(2)}, u32[]{:S(2)}) collective-permute-start(f32[64,256]{1,0:T(8,128)S(1)} %constant_dynamic-slice_fusion.1), channel_id=1, source_target_pairs={{0,8},{4,12},{8,0},{12,4},{16,24},{20,28},{24,16},{28,20},{1,9},{5... | collective-permute-start | bytes 196616 | tf_op jit(solution)/shard_map/ppermute | solution.py:220
  160.3 26.2 %copy-start.33 = (bf16[256,256]{1,0:T(8,128)(2,1)S(1)}, bf16[256,256]{1,0:T(8,128)(2,1)}, u32[]{:S(2)}) copy-start(bf16[256,256]{1,0:T(8,128)(2,1)} %param.13) | copy-start | bytes 393220
  160.3 5.2 %collective-permute-start.19 = (f32[32,256]{1,0:T(8,128)S(1)}, f32[32,256]{1,0:T(8,128)S(1)}, u32[]{:S(2)}, u32[]{:S(2)}) collective-permute-start(f32[32,256]{1,0:T(8,128)S(1)} %constant_dynamic-slice_fusion), channel_id=1, source_target_pairs={{0,16},{4,20},{8,24},{12,28},{16,0},{20,4},{24,8},{28,12},{1,17},{... | collective-permute-start | bytes 98312 | tf_op jit(solution)/shard_map/ppermute | solution.py:220
  165.5 4.8 %collective-permute-start.20 = (f32[32,256]{1,0:T(8,128)S(1)}, f32[32,256]{1,0:T(8,128)S(1)}, u32[]{:S(2)}, u32[]{:S(2)}) collective-permute-start(f32[32,256]{1,0:T(8,128)S(1)} %dynamic-slice_add_fusion.4), channel_id=1, source_target_pairs={{0,16},{4,20},{8,24},{12,28},{16,0},{20,4},{24,8},{28,12},{1,17},{... | collective-permute-start | bytes 98312 | tf_op jit(solution)/shard_map/ppermute | solution.py:187
  170.4 17.0 %copy-start.58 = (bf16[2,8,2,8,256]{4,3,2,1,0:T(8,128)(2,1)S(1)}, bf16[2,8,2,8,256]{4,3,2,1,0:T(8,128)(2,1)}, u32[]{:S(2)}) copy-start(bf16[2,8,2,8,256]{4,3,2,1,0:T(8,128)(2,1)} %copy-done.57) | copy-start | bytes 393220
  170.4 17.0 %copy-start.62 = (bf16[256,256]{1,0:T(8,128)(2,1)S(1)}, bf16[256,256]{1,0:T(8,128)(2,1)}, u32[]{:S(2)}) copy-start(bf16[256,256]{1,0:T(8,128)(2,1)} %param.12) | copy-start | bytes 393220
  170.4 17.0 %copy-start.63 = (bf16[256,256]{1,0:T(8,128)(2,1)S(1)}, bf16[256,256]{1,0:T(8,128)(2,1)}, u32[]{:S(2)}) copy-start(bf16[256,256]{1,0:T(8,128)(2,1)} %param.11) | copy-start | bytes 393220
  170.4 16.9 %copy-start.64 = (bf16[256,256]{1,0:T(8,128)(2,1)S(1)}, bf16[256,256]{1,0:T(8,128)(2,1)}, u32[]{:S(2)}) copy-start(bf16[256,256]{1,0:T(8,128)(2,1)} %param.10) | copy-start | bytes 393220
  170.4 4.3 %collective-permute-start.21 = (f32[64,256]{1,0:T(8,128)S(1)}, f32[64,256]{1,0:T(8,128)S(1)}, u32[]{:S(2)}, u32[]{:S(2)}) collective-permute-start(f32[64,256]{1,0:T(8,128)S(1)} %pad_maximum_fusion.13), channel_id=1, source_target_pairs={{0,8},{4,12},{8,0},{12,4},{16,24},{20,28},{24,16},{28,20},{1,9},{5... | collective-permute-start | bytes 196616 | tf_op jit(solution)/shard_map/ppermute | solution.py:187
  174.8 5.0 %collective-permute-start.22 = (f32[128,256]{1,0:T(8,128)S(1)}, f32[128,256]{1,0:T(8,128)S(1)}, u32[]{:S(2)}, u32[]{:S(2)}) collective-permute-start(f32[128,256]{1,0:T(8,128)S(1)} %pad_maximum_fusion.11), channel_id=1, source_target_pairs={{0,4},{4,0},{8,12},{12,8},{16,20},{20,16},{24,28},{28,24},{1,5},{5... | collective-permute-start | bytes 393224 | tf_op jit(solution)/shard_map/ppermute | solution.py:187
  179.9 6.4 %collective-permute-start.23 = (f32[256,256]{1,0:T(8,128)S(1)}, f32[256,256]{1,0:T(8,128)S(1)}, u32[]{:S(2)}, u32[]{:S(2)}) collective-permute-start(f32[256,256]{1,0:T(8,128)S(1)} %pad_maximum_fusion.9), channel_id=1, source_target_pairs={{0,2},{1,3},{2,0},{3,1},{4,6},{5,7},{6,4},{7,5},{8,10},{9,11},{10,... | collective-permute-start | bytes 786440 | tf_op jit(solution)/shard_map/ppermute | solution.py:187
  186.4 2.0 %collective-permute-start.24 = (f32[512,256]{1,0:T(8,128)S(1)}, f32[512,256]{1,0:T(8,128)S(1)}, u32[]{:S(2)}, u32[]{:S(2)}) collective-permute-start(f32[512,256]{1,0:T(8,128)S(1)} %pad_maximum_fusion.8), channel_id=1, source_target_pairs={{0,1},{1,0},{2,3},{3,2},{4,5},{5,4},{6,7},{7,6},{8,9},{9,8},{10,11... | collective-permute-start | bytes 1572872 | tf_op jit(solution)/shard_map/ppermute | solution.py:187
  (64 other events, 258.7 us)

commit v3 on v2

--- a/solution.py
+++ b/solution.py
@@ -206,19 +206,24 @@
 def tree_sum(parts, axes):
     sizes = [lax.axis_size(axis) for axis in axes]
     rows = sum(part.shape[0] for part in parts)
-    total = math.prod(sizes)
-    if any(size & (size - 1) for size in sizes) or rows % total:
+    if any(size & (size - 1) for size in sizes) or rows % math.prod(sizes):
         return lax.psum(parts, axes)
     steps = halving_steps(axes)
+    last = [step for step in steps if step[0] == axes[-1]]
+    halving = steps[: len(steps) - len(last) + 1]
+    doubling = steps[len(halving) :]
     joined = jnp.concatenate(parts, 0)
-    for axis, stride in steps:
+    for axis, stride in halving:
         pairs = [(i, i ^ stride) for i in range(lax.axis_size(axis))]
         bit = (lax.axis_index(axis) // stride) % 2
         half = joined.shape[0] // 2
         keep = lax.dynamic_slice_in_dim(joined, bit * half, half, 0)
         send = lax.dynamic_slice_in_dim(joined, (1 - bit) * half, half, 0)
         joined = keep + lax.ppermute(send, axis, pairs)
-    joined = doubling_gather(joined, steps)
+    for axis, stride in doubling:
+        pairs = [(i, i ^ stride) for i in range(lax.axis_size(axis))]
+        joined = joined + lax.ppermute(joined, axis, pairs)
+    joined = doubling_gather(joined, halving)
     out = []
     start = 0
     for part in parts:

time: 191 us -> 182 us (0.953)
  waiting for transfers between devices: 70.9 us -> 64.6 us
  matrix products: 56.6 us -> 54.2 us
    ppermute x0 -> x2, waiting for transfers between devices: none -> 10.9 us  [tree_sum(): joined = joined + lax.ppermute(joined, axis, pairs)]
    ppermute x5 -> x3, waiting for transfers between devices: 21.7 us -> 13.1 us  [tree_sum(): joined = keep + lax.ppermute(send, axis, pairs)]
    ppermute x8 -> x6, waiting for transfers between devices: 41.5 us -> 32.9 us  [doubling_gather(): got = lax.ppermute(joined, axis, pairs)]
    ppermute x5 -> x3, starting transfers between devices: 6.64 us -> 5.67 us  [tree_sum(): joined = keep + lax.ppermute(send, axis, pairs)]
    ppermute x8 -> x6, starting transfers between devices: 12.6 us -> 12 us  [doubling_gather(): got = lax.ppermute(joined, axis, pairs)]
  transfers between devices with their start and end apart: 25 -> 23, of which waited for: 15 -> 13; matrix products, arithmetic and copies ran while one was open for 11% -> 12% of each run, Pallas kernels for 0% -> 0%
where the time goes in v3:
time: 182 us; the launch traced here: 181 us
  waiting for transfers between devices  64.6 us (35%)
  matrix products  54.2 us (30%)
  starting transfers between devices  43 us (24%)
  local copies, waits for them, and re-layouts  11.9 us (7%)
  other arithmetic  4.42 us (2%)
  between operations  2.73 us (2%)
    ppermute x6, waiting for transfers between devices, doubling_gather(): got = lax.ppermute(joined, axis, pairs)  32.9 us
    ppermute x6, starting transfers between devices, padded(): lax.ppermute(lax.slice_in_dim(block, block.shape[dim] - width, None, axis...  16.4 us
    dot_general x9, matrix products, key_grads(): jnp.einsum('abhqk,abqhe->abkhe', grad_score, query_heads, preferred_eleme...  13.4 us
    dot_general x10, matrix products, query_grads(): jnp.einsum('abhqk,abkhe->abqhe', grad_score, split_heads(key_part), prefe...  13.1 us
    ppermute x3, waiting for transfers between devices, tree_sum(): joined = keep + lax.ppermute(send, axis, pairs)  13.1 us
    ppermute x6, starting transfers between devices, doubling_gather(): got = lax.ppermute(joined, axis, pairs)  12 us
    ppermute x2, waiting for transfers between devices, tree_sum(): joined = joined + lax.ppermute(joined, axis, pairs)  10.9 us
    dot_general x10, matrix products, piece_scores(): jnp.einsum('abqhe,abkhe->abhqk', query_heads, split_heads(key_part), pref...  10 us
  transfers between devices with their start and end apart: 23, of which 13 were waited for; matrix products, arithmetic and copies ran while one was open for 12% of the time, Pallas kernels for 0%

profile of v3, /device:TPU:0, one launch (start us, length us, event | category | flops | bytes accessed | tf_op | source)
XLA Modules:
  0.0 180.9 jit_solution(15531922341996057443)
XLA Ops:
  0.7 4.1 %collective-permute-start.4 = (bf16[4,64,512]{2,1,0:T(8,128)(2,1)}, bf16[4,64,512]{2,1,0:T(8,128)(2,1)S(1)}, u32[]{:S(2)}, u32[]{:S(2)}) collective-permute-start(bf16[4,64,512]{2,1,0:T(8,128)(2,1)} %bitcast.498), channel_id=1, source_target_pairs={{0,16},{4,20},{8,24},{12,28},{16,0},{20,4},{24,8},{28,12},{1,17},{... | collective-permute-start | bytes 786440 | tf_op jit(solution)/shard_map/ppermute | solution.py:187
  6.0 3.4 %collective-permute-start = (bf16[8,16,512]{2,1,0:T(8,128)(2,1)S(1)}, bf16[8,16,512]{2,1,0:T(8,128)(2,1)S(1)}, u32[]{:S(2)}, u32[]{:S(2)}) collective-permute-start(bf16[8,16,512]{2,1,0:T(8,128)(2,1)S(1)} %bitcast.504), channel_id=1, source_target_pairs={{0,4},{4,8},{8,12},{12,16},{16,20},{20,24},{24,28},{1,5},{5,9},{9,... | collective-permute-start | bytes 393224 | tf_op jit(solution)/shard_map/ppermute | solution.py:23
  9.4 1.3 collective-permute-start.1
  13.0 4.6 %collective-permute-start.7 = (bf16[8,16,512]{2,1,0:T(8,128)(2,1)S(1)}, bf16[8,16,512]{2,1,0:T(8,128)(2,1)S(1)}, u32[]{:S(2)}, u32[]{:S(2)}) collective-permute-start(bf16[8,16,512]{2,1,0:T(8,128)(2,1)S(1)} %get-tuple-element.73), channel_id=1, source_target_pairs={{0,4},{4,8},{8,12},{12,16},{16,20},{20,24},{24,28},{1,5},{5,9},{9,... | collective-permute-start | bytes 393224 | tf_op jit(solution)/shard_map/ppermute | solution.py:23
  17.6 1.3 collective-permute-start.8
  20.1 1.3 collective-permute-start.2
  21.4 1.3 collective-permute-start.3
  22.7 2.1 %collective-permute-done.8 = bf16[8,16,512]{2,1,0:T(8,128)(2,1)S(1)} collective-permute-done((bf16[8,16,512]{2,1,0:T(8,128)(2,1)S(1)}, bf16[8,16,512]{2,1,0:T(8,128)(2,1)S(1)}, u32[]{:S(2)}, u32[]{:S(2)}) %collective-permute-start.8) | collective-permute-done | bytes 131104 | tf_op jit(solution)/shard_map/ppermute | solution.py:26
  25.0 1.3 collective-permute-start.10
  26.3 3.3 %collective-permute-start.9 = (bf16[32,8,512]{2,1,0:T(8,128)(2,1)S(1)}, bf16[32,8,512]{2,1,0:T(8,128)(2,1)S(1)}, u32[]{:S(2)}, u32[]{:S(2)}) collective-permute-start(bf16[32,8,512]{2,1,0:T(8,128)(2,1)S(1)} %get-tuple-element.63), channel_id=1, source_target_pairs={{0,1},{1,2},{2,3},{4,5},{5,6},{6,7},{8,9},{9,10},{10,11},{12,13},{... | collective-permute-start | bytes 786440 | tf_op jit(solution)/shard_map/ppermute | solution.py:23
  29.7 4.6 %collective-permute-start.5 = (bf16[8,64,512]{2,1,0:T(8,128)(2,1)S(1)}, bf16[8,64,512]{2,1,0:T(8,128)(2,1)S(1)}, u32[]{:S(2)}, u32[]{:S(2)}) collective-permute-start(bf16[8,64,512]{2,1,0:T(8,128)(2,1)S(1)} %pad_maximum_fusion.6), channel_id=1, source_target_pairs={{0,8},{4,12},{8,0},{12,4},{16,24},{20,28},{24,16},{28,20},{1,9},{5... | collective-permute-start | bytes 1572872 | tf_op jit(solution)/shard_map/ppermute | solution.py:187
  38.7 1.5 fusion.451
  40.2 1.5 fusion.453
  41.8 4.2 %collective-permute-done.5 = bf16[8,64,512]{2,1,0:T(8,128)(2,1)S(1)} collective-permute-done((bf16[8,64,512]{2,1,0:T(8,128)(2,1)S(1)}, bf16[8,64,512]{2,1,0:T(8,128)(2,1)S(1)}, u32[]{:S(2)}, u32[]{:S(2)}) %collective-permute-start.5) | collective-permute-done | bytes 524320 | tf_op jit(solution)/shard_map/ppermute | solution.py:187
  47.4 1.5 fusion.454
  48.9 1.5 fusion.456
  51.3 1.5 slice_bitcast_fusion
  52.8 19.4 %collective-permute-done.6 = bf16[16,64,512]{2,1,0:T(8,128)(2,1)S(1)} collective-permute-done((bf16[16,64,512]{2,1,0:T(8,128)(2,1)S(1)}, bf16[16,64,512]{2,1,0:T(8,128)(2,1)S(1)}, u32[]{:S(2)}, u32[]{:S(2)}) %collective-permute-start.6) | collective-permute-done | bytes 1048608 | tf_op jit(solution)/shard_map/ppermute | solution.py:187
  72.5 1.4 gather_fusion
  73.9 1.3 broadcast_select_fusion.4
  82.7 2.1 %fusion.84 = f32[2,2,2,128,64]{3,4,2,1,0:T(8,128)} fusion(f32[2,2,2,64,64]{3,4,2,1,0:T(8,128)S(1)} %get-tuple-element.125, f32[2,2,2,64]{3,2,1,0:T(2,128)S(1)} %bitcast.470, f32[2,2,2,64]{3,2,1,0:T(2,128)S(1)} %log_add_fusion, bf16[2,2,8,2,8,128]{5,4,3,2,1,0:T(8,128)(2,1)} %copy-done.55, bf16[2,2,8,2,8,128]{5,4,3,2,1,0:T(8,128)(2,1)} %get-tuple-element.54, ...), kind=kOutput, calls=%fused_computation.166 | convolution fusion | flops 16908288 | bytes 790528 | tf_op jit(solution)/shard_map/abhqk,abkhe->abqhe/dot_general | solution.py:115
  84.7 2.2 %convolution_add_fusion.24 = f32[2,2,2,128,64]{3,4,2,1,0:T(8,128)} fusion(f32[2,2,2,128,64]{3,4,2,1,0:T(8,128)} %fusion.84, f32[2,2,2,64,64]{3,4,2,1,0:T(8,128)S(1)} %copy-done.5, f32[2,2,2,64]{3,2,1,0:T(2,128)S(1)} %bitcast.472, f32[2,2,2,64]{3,2,1,0:T(2,128)S(1)} %log_add_fusion, bf16[2,2,8,2,8,128]{5,4,3,2,1,0:T(8,128)(2,1)} %get-tuple-element.44, ...), kind=kOutput, calls=%fused_computation.99 | convolution fusion | flops 16973824 | bytes 1052672 | tf_op jit(solution)/shard_map/abhqk,abkhe->abqhe/dot_general | solution.py:115
  87.0 2.2 %convolution_add_fusion.23 = f32[2,2,2,128,64]{3,4,2,1,0:T(8,128)} fusion(f32[2,2,2,128,64]{3,4,2,1,0:T(8,128)} %convolution_add_fusion.24, f32[2,2,2,64,64]{3,4,2,1,0:T(8,128)S(1)} %copy-done.4, f32[2,2,2,64]{3,2,1,0:T(2,128)S(1)} %bitcast.473, f32[2,2,2,64]{3,2,1,0:T(2,128)S(1)} %log_add_fusion, bf16[2,2,8,2,8,128]{5,4,3,2,1,0:T(8,128)(2,1)} %get-tuple-element.43, ...), kind=kOutput, calls=%fused_computation.96 | convolution fusion | flops 16973824 | bytes 1052672 | tf_op jit(solution)/shard_map/abhqk,abkhe->abqhe/dot_general | solution.py:115
  89.2 1.4 convolution_add_fusion.22
  90.6 1.3 convolution_add_fusion.21
  92.0 1.3 convolution_add_fusion.20
  93.4 1.3 convolution_add_fusion.19
  96.5 2.6 %collective-permute-start.11 = (f32[8,16,4]{1,0,2:T(8,128)S(1)}, f32[8,16,4]{1,0,2:T(8,128)S(1)}, u32[]{:S(2)}, u32[]{:S(2)}) collective-permute-start(f32[8,16,4]{1,0,2:T(8,128)S(1)} %slice.413), channel_id=1, source_target_pairs={{0,4},{4,8},{8,12},{12,16},{16,20},{20,24},{24,28},{1,5},{5,9},{9,... | collective-permute-start | bytes 6152 | tf_op jit(solution)/shard_map/ppermute | solution.py:23
  100.3 1.3 collective-permute-start.12
  101.9 4.9 %collective-permute-done.12 = f32[8,16,4]{1,0,2:T(8,128)S(1)} collective-permute-done((f32[8,16,4]{1,0,2:T(8,128)S(1)}, f32[8,16,4]{1,0,2:T(8,128)S(1)}, u32[]{:S(2)}, u32[]{:S(2)}) %collective-permute-start.12) | collective-permute-done | bytes 2080 | tf_op jit(solution)/shard_map/ppermute | solution.py:26
  106.9 1.3 collective-permute-start.13
  108.2 1.5 collective-permute-start.14
  116.0 2.1 %convolution_add_fusion.15 = f32[2,2,2,128,64]{3,4,2,1,0:T(8,128)} fusion(f32[2,2,2,128,64]{3,4,2,1,0:T(8,128)} %fusion.82, f32[2,2,2,64,64]{3,4,2,1,0:T(8,128)S(1)} %fusion.32, f32[2,2,2,64]{3,2,1,0:T(2,128)} %get-tuple-element.95, bf16[2,2,8,2,8,128]{5,4,3,2,1,0:T(8,128)(2,1)S(1)} %copy-done.12, bf16[2,2,8,2,8,128]{5,4,3,2,1,0:T(8,128)(2,1)} %get-tuple-element.34, ...), kind=kOutput, calls=%fused_computation.19 | convolution fusion | flops 16941056 | bytes 1050624 | tf_op jit(solution)/shard_map/abhqk,abqhe->abkhe/dot_general | solution.py:154
  118.1 2.1 %convolution_add_fusion.14 = f32[2,2,2,128,64]{3,4,2,1,0:T(8,128)} fusion(f32[2,2,2,128,64]{3,4,2,1,0:T(8,128)} %convolution_add_fusion.15, f32[2,2,2,64,64]{3,4,2,1,0:T(8,128)S(1)} %fusion.28, f32[2,2,2,64]{3,2,1,0:T(2,128)} %get-tuple-element.93, bf16[2,2,8,2,8,128]{5,4,3,2,1,0:T(8,128)(2,1)S(1)} %copy-done.11, ...), kind=kOutput, calls=%fused_computation.18 | convolution fusion | flops 16941056 | bytes 1050624 | tf_op jit(solution)/shard_map/abhqk,abqhe->abkhe/dot_general | solution.py:154
  120.2 1.4 convolution_add_fusion.13
  121.6 2.0 %convolution_add_fusion.12 = f32[2,2,2,128,64]{3,4,2,1,0:T(8,128)} fusion(f32[2,2,2,128,64]{3,4,2,1,0:T(8,128)S(1)} %convolution_add_fusion.13, f32[2,2,2,64,64]{3,4,2,1,0:T(8,128)S(1)} %fusion.20, f32[2,2,2,64]{3,2,1,0:T(2,128)} %get-tuple-element.89, bf16[2,2,8,2,8,128]{5,4,3,2,1,0:T(8,128)(2,1)S(1)} %copy-done.9, ...), kind=kOutput, calls=%fused_computation.16 | convolution fusion | flops 16941056 | bytes 1050624 | tf_op jit(solution)/shard_map/abhqk,abqhe->abkhe/dot_general | solution.py:154
  123.6 1.4 convolution_add_fusion.11
  125.0 1.9 %convolution_add_fusion.10 = f32[2,2,2,128,64]{3,4,2,1,0:T(8,128)} fusion(f32[2,2,2,128,64]{3,4,2,1,0:T(8,128)S(1)} %convolution_add_fusion.11, f32[2,2,2,64,64]{3,4,2,1,0:T(8,128)S(1)} %fusion.12, f32[2,2,2,64]{3,2,1,0:T(2,128)S(1)} %get-tuple-element.85, bf16[2,2,8,2,8,128]{5,4,3,2,1,0:T(8,128)(2,1)S(1)} %copy-done.7, ...), kind=kOutput, calls=%fused_computation.14 | convolution fusion | flops 16941056 | bytes 1050624 | tf_op jit(solution)/shard_map/abhqk,abqhe->abkhe/dot_general | solution.py:154
  134.6 2.4 %collective-permute-start.15 = (f32[512,256]{1,0:T(8,128)S(1)}, f32[512,256]{1,0:T(8,128)S(1)}, u32[]{:S(2)}, u32[]{:S(2)}) collective-permute-start(f32[512,256]{1,0:T(8,128)S(1)} %constant_dynamic-slice_fusion.2), channel_id=1, source_target_pairs={{0,1},{1,0},{2,3},{3,2},{4,5},{5,4},{6,7},{7,6},{8,9},{9,8},{10,11... | collective-permute-start | bytes 1572872 | tf_op jit(solution)/shard_map/ppermute | solution.py:222
  137.0 1.5 collective-permute-done.15
  139.0 8.4 %collective-permute-done.16 = f32[256,256]{1,0:T(8,128)S(1)} collective-permute-done((f32[256,256]{1,0:T(8,128)S(1)}, f32[256,256]{1,0:T(8,128)S(1)}, u32[]{:S(2)}, u32[]{:S(2)}) %collective-permute-start.16) | collective-permute-done | bytes 262176 | tf_op jit(solution)/shard_map/ppermute | solution.py:222
  147.4 3.0 %collective-permute-start.17 = (f32[128,256]{1,0:T(8,128)S(1)}, f32[128,256]{1,0:T(8,128)S(1)}, u32[]{:S(2)}, u32[]{:S(2)}) collective-permute-start(f32[128,256]{1,0:T(8,128)S(1)} %constant_dynamic-slice_fusion), channel_id=1, source_target_pairs={{0,4},{4,0},{8,12},{12,8},{16,20},{20,16},{24,28},{28,24},{1,5},{5... | collective-permute-start | bytes 393224 | tf_op jit(solution)/shard_map/ppermute | solution.py:222
  150.4 3.2 %collective-permute-done.17 = f32[128,256]{1,0:T(8,128)S(1)} collective-permute-done((f32[128,256]{1,0:T(8,128)S(1)}, f32[128,256]{1,0:T(8,128)S(1)}, u32[]{:S(2)}, u32[]{:S(2)}) %collective-permute-start.17) | collective-permute-done | bytes 131104 | tf_op jit(solution)/shard_map/ppermute | solution.py:222
  153.8 4.9 %collective-permute-done.18 = f32[128,256]{1,0:T(8,128)S(1)} collective-permute-done((f32[128,256]{1,0:T(8,128)S(1)}, f32[128,256]{1,0:T(8,128)S(1)}, u32[]{:S(2)}, u32[]{:S(2)}) %collective-permute-start.18) | collective-permute-done | bytes 131104 | tf_op jit(solution)/shard_map/ppermute | solution.py:225
  159.6 5.9 %collective-permute-done.19 = f32[128,256]{1,0:T(8,128)S(1)} collective-permute-done((f32[128,256]{1,0:T(8,128)S(1)}, f32[128,256]{1,0:T(8,128)S(1)}, u32[]{:S(2)}, u32[]{:S(2)}) %collective-permute-start.19) | collective-permute-done | bytes 131104 | tf_op jit(solution)/shard_map/ppermute | solution.py:225
  165.6 1.8 %collective-permute-start.20 = (f32[128,256]{1,0:T(8,128)S(1)}, f32[128,256]{1,0:T(8,128)S(1)}, u32[]{:S(2)}, u32[]{:S(2)}) collective-permute-start(f32[128,256]{1,0:T(8,128)S(1)} %add.437), channel_id=1, source_target_pairs={{0,4},{4,0},{8,12},{12,8},{16,20},{20,16},{24,28},{28,24},{1,5},{5... | collective-permute-start | bytes 393224 | tf_op jit(solution)/shard_map/ppermute | solution.py:187
  167.4 3.2 %collective-permute-done.20 = f32[128,256]{1,0:T(8,128)S(1)} collective-permute-done((f32[128,256]{1,0:T(8,128)S(1)}, f32[128,256]{1,0:T(8,128)S(1)}, u32[]{:S(2)}, u32[]{:S(2)}) %collective-permute-start.20) | collective-permute-done | bytes 131104 | tf_op jit(solution)/shard_map/ppermute | solution.py:187
  171.1 6.0 %collective-permute-done.21 = f32[256,256]{1,0:T(8,128)S(1)} collective-permute-done((f32[256,256]{1,0:T(8,128)S(1)}, f32[256,256]{1,0:T(8,128)S(1)}, u32[]{:S(2)}, u32[]{:S(2)}) %collective-permute-start.21) | collective-permute-done | bytes 262176 | tf_op jit(solution)/shard_map/ppermute | solution.py:187
  (336 shorter events, 41.1 us)
Async XLA Ops:
  0.6 18.3 %copy-start.72 = (s32[1,1,4,2]{2,3,1,0:T(2,128)S(1)}, s32[1,1,4,2]{2,3,1,0:T(2,128)}, u32[]{:S(2)}) copy-start(s32[1,1,4,2]{2,3,1,0:T(2,128)} %param.15) | copy-start | bytes 100
  0.7 18.3 %copy-start.71 = (s32[1,1,4,2]{2,3,1,0:T(2,128)S(1)}, s32[1,1,4,2]{2,3,1,0:T(2,128)}, u32[]{:S(2)}) copy-start(s32[1,1,4,2]{2,3,1,0:T(2,128)} %param.16) | copy-start | bytes 100
  0.7 28.9 %collective-permute-start.4 = (bf16[4,64,512]{2,1,0:T(8,128)(2,1)}, bf16[4,64,512]{2,1,0:T(8,128)(2,1)S(1)}, u32[]{:S(2)}, u32[]{:S(2)}) collective-permute-start(bf16[4,64,512]{2,1,0:T(8,128)(2,1)} %bitcast.498), channel_id=1, source_target_pairs={{0,16},{4,20},{8,24},{12,28},{16,0},{20,4},{24,8},{28,12},{1,17},{... | collective-permute-start | bytes 786440 | tf_op jit(solution)/shard_map/ppermute | solution.py:187
  6.0 14.0 %collective-permute-start = (bf16[8,16,512]{2,1,0:T(8,128)(2,1)S(1)}, bf16[8,16,512]{2,1,0:T(8,128)(2,1)S(1)}, u32[]{:S(2)}, u32[]{:S(2)}) collective-permute-start(bf16[8,16,512]{2,1,0:T(8,128)(2,1)S(1)} %bitcast.504), channel_id=1, source_target_pairs={{0,4},{4,8},{8,12},{12,16},{16,20},{20,24},{24,28},{1,5},{5,9},{9,... | collective-permute-start | bytes 393224 | tf_op jit(solution)/shard_map/ppermute | solution.py:23
  9.4 10.6 %collective-permute-start.1 = (bf16[8,16,512]{2,1,0:T(8,128)(2,1)S(1)}, bf16[8,16,512]{2,1,0:T(8,128)(2,1)S(1)}, u32[]{:S(2)}, u32[]{:S(2)}) collective-permute-start(bf16[8,16,512]{2,1,0:T(8,128)(2,1)S(1)} %bitcast.503), channel_id=1, source_target_pairs={{4,0},{8,4},{12,8},{16,12},{20,16},{24,20},{28,24},{5,1},{9,5},{13... | collective-permute-start | bytes 393224 | tf_op jit(solution)/shard_map/ppermute | solution.py:26
  13.0 9.7 %collective-permute-start.7 = (bf16[8,16,512]{2,1,0:T(8,128)(2,1)S(1)}, bf16[8,16,512]{2,1,0:T(8,128)(2,1)S(1)}, u32[]{:S(2)}, u32[]{:S(2)}) collective-permute-start(bf16[8,16,512]{2,1,0:T(8,128)(2,1)S(1)} %get-tuple-element.73), channel_id=1, source_target_pairs={{0,4},{4,8},{8,12},{12,16},{16,20},{20,24},{24,28},{1,5},{5,9},{9,... | collective-permute-start | bytes 393224 | tf_op jit(solution)/shard_map/ppermute | solution.py:23
  17.6 7.3 %collective-permute-start.8 = (bf16[8,16,512]{2,1,0:T(8,128)(2,1)S(1)}, bf16[8,16,512]{2,1,0:T(8,128)(2,1)S(1)}, u32[]{:S(2)}, u32[]{:S(2)}) collective-permute-start(bf16[8,16,512]{2,1,0:T(8,128)(2,1)S(1)} %get-tuple-element.74), channel_id=1, source_target_pairs={{4,0},{8,4},{12,8},{16,12},{20,16},{24,20},{28,24},{5,1},{9,5},{13... | collective-permute-start | bytes 393224 | tf_op jit(solution)/shard_map/ppermute | solution.py:26
  19.4 16.5 %copy-start.81 = (pred[2,2]{1,0:T(4,128)(4,1)}, pred[2,2]{1,0:T(4,128)(4,1)S(1)}, u32[]{:S(2)}) copy-start(pred[2,2]{1,0:T(4,128)(4,1)S(1)} %get-tuple-element.104) | copy-start | bytes 16
  19.4 17.5 %copy-start.73 = (pred[2,2]{1,0:T(4,128)(4,1)}, pred[2,2]{1,0:T(4,128)(4,1)S(1)}, u32[]{:S(2)}) copy-start(pred[2,2]{1,0:T(4,128)(4,1)S(1)} %get-tuple-element.100) | copy-start | bytes 16
  19.4 17.7 %copy-start.75 = (pred[2,2]{1,0:T(4,128)(4,1)}, pred[2,2]{1,0:T(4,128)(4,1)S(1)}, u32[]{:S(2)}) copy-start(pred[2,2]{1,0:T(4,128)(4,1)S(1)} %get-tuple-element.101) | copy-start | bytes 16
  19.4 18.5 %copy-start.77 = (pred[2,2]{1,0:T(4,128)(4,1)}, pred[2,2]{1,0:T(4,128)(4,1)S(1)}, u32[]{:S(2)}) copy-start(pred[2,2]{1,0:T(4,128)(4,1)S(1)} %get-tuple-element.102) | copy-start | bytes 16
  19.4 19.3 %copy-start.79 = (pred[2,2]{1,0:T(4,128)(4,1)}, pred[2,2]{1,0:T(4,128)(4,1)S(1)}, u32[]{:S(2)}) copy-start(pred[2,2]{1,0:T(4,128)(4,1)S(1)} %get-tuple-element.103) | copy-start | bytes 16
  19.4 20.8 %copy-start.83 = (pred[2,2]{1,0:T(4,128)(4,1)}, pred[2,2]{1,0:T(4,128)(4,1)S(1)}, u32[]{:S(2)}) copy-start(pred[2,2]{1,0:T(4,128)(4,1)S(1)} %get-tuple-element.105) | copy-start | bytes 16
  19.4 28.0 %copy-start.85 = (pred[2,2]{1,0:T(4,128)(4,1)}, pred[2,2]{1,0:T(4,128)(4,1)S(1)}, u32[]{:S(2)}) copy-start(pred[2,2]{1,0:T(4,128)(4,1)S(1)} %get-tuple-element.106) | copy-start | bytes 16
  19.4 29.5 %copy-start.87 = (pred[2,2]{1,0:T(4,128)(4,1)}, pred[2,2]{1,0:T(4,128)(4,1)S(1)}, u32[]{:S(2)}) copy-start(pred[2,2]{1,0:T(4,128)(4,1)S(1)} %get-tuple-element.99) | copy-start | bytes 16
  19.4 31.0 %copy-start.89 = (pred[2,2]{1,0:T(4,128)(4,1)}, pred[2,2]{1,0:T(4,128)(4,1)S(1)}, u32[]{:S(2)}) copy-start(pred[2,2]{1,0:T(4,128)(4,1)S(1)} %get-tuple-element.107) | copy-start | bytes 16
  19.9 30.6 %copy-start.56 = (bf16[2,2,64,2,128]{4,3,2,1,0:T(2,128)(2,1)}, bf16[2,2,64,2,128]{4,3,2,1,0:T(2,128)(2,1)S(1)}, u32[]{:S(2)}) copy-start(bf16[2,2,64,2,128]{4,3,2,1,0:T(2,128)(2,1)S(1)} %reshape_reshape.29) | copy-start | bytes 393220
  20.1 14.2 %collective-permute-start.2 = (bf16[32,8,512]{2,1,0:T(8,128)(2,1)S(1)}, bf16[32,8,512]{2,1,0:T(8,128)(2,1)S(1)}, u32[]{:S(2)}, u32[]{:S(2)}) collective-permute-start(bf16[32,8,512]{2,1,0:T(8,128)(2,1)S(1)} %get-tuple-element.69), channel_id=1, source_target_pairs={{0,1},{1,2},{2,3},{4,5},{5,6},{6,7},{8,9},{9,10},{10,11},{12,13},{... | collective-permute-start | bytes 786440 | tf_op jit(solution)/shard_map/ppermute | solution.py:23
  21.4 12.9 %collective-permute-start.3 = (bf16[32,8,512]{2,1,0:T(8,128)(2,1)S(1)}, bf16[32,8,512]{2,1,0:T(8,128)(2,1)S(1)}, u32[]{:S(2)}, u32[]{:S(2)}) collective-permute-start(bf16[32,8,512]{2,1,0:T(8,128)(2,1)S(1)} %get-tuple-element.70), channel_id=1, source_target_pairs={{1,0},{2,1},{3,2},{5,4},{6,5},{7,6},{9,8},{10,9},{11,10},{13,12},{... | collective-permute-start | bytes 786440 | tf_op jit(solution)/shard_map/ppermute | solution.py:26
  25.0 22.2 %collective-permute-start.10 = (bf16[32,8,512]{2,1,0:T(8,128)(2,1)S(1)}, bf16[32,8,512]{2,1,0:T(8,128)(2,1)S(1)}, u32[]{:S(2)}, u32[]{:S(2)}) collective-permute-start(bf16[32,8,512]{2,1,0:T(8,128)(2,1)S(1)} %get-tuple-element.64), channel_id=1, source_target_pairs={{1,0},{2,1},{3,2},{5,4},{6,5},{7,6},{9,8},{10,9},{11,10},{13,12},{... | collective-permute-start | bytes 786440 | tf_op jit(solution)/shard_map/ppermute | solution.py:26
  26.3 20.9 %collective-permute-start.9 = (bf16[32,8,512]{2,1,0:T(8,128)(2,1)S(1)}, bf16[32,8,512]{2,1,0:T(8,128)(2,1)S(1)}, u32[]{:S(2)}, u32[]{:S(2)}) collective-permute-start(bf16[32,8,512]{2,1,0:T(8,128)(2,1)S(1)} %get-tuple-element.63), channel_id=1, source_target_pairs={{0,1},{1,2},{2,3},{4,5},{5,6},{6,7},{8,9},{9,10},{10,11},{12,13},{... | collective-permute-start | bytes 786440 | tf_op jit(solution)/shard_map/ppermute | solution.py:23
  29.7 16.3 %collective-permute-start.5 = (bf16[8,64,512]{2,1,0:T(8,128)(2,1)S(1)}, bf16[8,64,512]{2,1,0:T(8,128)(2,1)S(1)}, u32[]{:S(2)}, u32[]{:S(2)}) collective-permute-start(bf16[8,64,512]{2,1,0:T(8,128)(2,1)S(1)} %pad_maximum_fusion.6), channel_id=1, source_target_pairs={{0,8},{4,12},{8,0},{12,4},{16,24},{20,28},{24,16},{28,20},{1,9},{5... | collective-permute-start | bytes 1572872 | tf_op jit(solution)/shard_map/ppermute | solution.py:187
  35.8 11.6 %copy-start.53 = (bf16[2,2,8,2,8,128]{5,4,3,2,1,0:T(8,128)(2,1)}, bf16[2,2,8,2,8,128]{5,4,3,2,1,0:T(8,128)(2,1)S(1)}, u32[]{:S(2)}) copy-start(bf16[2,2,8,2,8,128]{5,4,3,2,1,0:T(8,128)(2,1)S(1)} %get-tuple-element.51) | copy-start | bytes 393220
  35.8 13.1 %copy-start.54 = (bf16[2,2,8,2,8,128]{5,4,3,2,1,0:T(8,128)(2,1)}, bf16[2,2,8,2,8,128]{5,4,3,2,1,0:T(8,128)(2,1)S(1)}, u32[]{:S(2)}) copy-start(bf16[2,2,8,2,8,128]{5,4,3,2,1,0:T(8,128)(2,1)S(1)} %get-tuple-element.52) | copy-start | bytes 393220
  35.8 14.6 %copy-start.55 = (bf16[2,2,8,2,8,128]{5,4,3,2,1,0:T(8,128)(2,1)}, bf16[2,2,8,2,8,128]{5,4,3,2,1,0:T(8,128)(2,1)S(1)}, u32[]{:S(2)}) copy-start(bf16[2,2,8,2,8,128]{5,4,3,2,1,0:T(8,128)(2,1)S(1)} %get-tuple-element.53) | copy-start | bytes 393220
  46.2 26.0 %collective-permute-start.6 = (bf16[16,64,512]{2,1,0:T(8,128)(2,1)S(1)}, bf16[16,64,512]{2,1,0:T(8,128)(2,1)S(1)}, u32[]{:S(2)}, u32[]{:S(2)}) collective-permute-start(bf16[16,64,512]{2,1,0:T(8,128)(2,1)S(1)} %pad_maximum_fusion.2), channel_id=1, source_target_pairs={{0,4},{4,0},{8,12},{12,8},{16,20},{20,16},{24,28},{28,24},{1,5},{5... | collective-permute-start | bytes 3145736 | tf_op jit(solution)/shard_map/ppermute | solution.py:187
  95.5 14.2 %copy-start.58 = (bf16[16,16,256]{2,1,0:T(8,128)(2,1)S(1)}, bf16[16,16,256]{2,1,0:T(8,128)(2,1)}, u32[]{:S(2)}) copy-start(bf16[16,16,256]{2,1,0:T(8,128)(2,1)} %param.17) | copy-start | bytes 393220
  96.4 16.1 %copy-start.36 = (bf16[2,2,8,2,8,128]{5,4,3,2,1,0:T(8,128)(2,1)S(1)}, bf16[2,2,8,2,8,128]{5,4,3,2,1,0:T(8,128)(2,1)}, u32[]{:S(2)}) copy-start(bf16[2,2,8,2,8,128]{5,4,3,2,1,0:T(8,128)(2,1)} %copy-done.35) | copy-start | bytes 393220
  96.4 16.1 %copy-start.45 = (bf16[2,2,8,2,8,128]{5,4,3,2,1,0:T(8,128)(2,1)S(1)}, bf16[2,2,8,2,8,128]{5,4,3,2,1,0:T(8,128)(2,1)}, u32[]{:S(2)}) copy-start(bf16[2,2,8,2,8,128]{5,4,3,2,1,0:T(8,128)(2,1)} %get-tuple-element.36) | copy-start | bytes 393220
  96.4 16.1 %copy-start.90 = (pred[2,2]{1,0:T(4,128)(4,1)S(1)}, pred[2,2]{1,0:T(4,128)(4,1)}, u32[]{:S(2)}) copy-start(pred[2,2]{1,0:T(4,128)(4,1)} %copy-done.89) | copy-start | bytes 16
  96.5 5.4 %collective-permute-start.11 = (f32[8,16,4]{1,0,2:T(8,128)S(1)}, f32[8,16,4]{1,0,2:T(8,128)S(1)}, u32[]{:S(2)}, u32[]{:S(2)}) collective-permute-start(f32[8,16,4]{1,0,2:T(8,128)S(1)} %slice.413), channel_id=1, source_target_pairs={{0,4},{4,8},{8,12},{12,16},{16,20},{20,24},{24,28},{1,5},{5,9},{9,... | collective-permute-start | bytes 6152 | tf_op jit(solution)/shard_map/ppermute | solution.py:23
  100.1 12.7 %copy-start.13 = (bf16[2,2,8,2,8,128]{5,4,3,2,1,0:T(8,128)(2,1)S(1)}, bf16[2,2,8,2,8,128]{5,4,3,2,1,0:T(8,128)(2,1)}, u32[]{:S(2)}) copy-start(bf16[2,2,8,2,8,128]{5,4,3,2,1,0:T(8,128)(2,1)} %get-tuple-element.35) | copy-start | bytes 393220
  100.3 6.5 %collective-permute-start.12 = (f32[8,16,4]{1,0,2:T(8,128)S(1)}, f32[8,16,4]{1,0,2:T(8,128)S(1)}, u32[]{:S(2)}, u32[]{:S(2)}) collective-permute-start(f32[8,16,4]{1,0,2:T(8,128)S(1)} %slice.415), channel_id=1, source_target_pairs={{4,0},{8,4},{12,8},{16,12},{20,16},{24,20},{28,24},{5,1},{9,5},{13... | collective-permute-start | bytes 6152 | tf_op jit(solution)/shard_map/ppermute | solution.py:26
  106.9 3.8 %collective-permute-start.13 = (f32[32,8,4]{1,0,2:T(8,128)S(1)}, f32[32,8,4]{1,0,2:T(8,128)S(1)}, u32[]{:S(2)}, u32[]{:S(2)}) collective-permute-start(f32[32,8,4]{1,0,2:T(8,128)S(1)} %get-tuple-element.77), channel_id=1, source_target_pairs={{0,1},{1,2},{2,3},{4,5},{5,6},{6,7},{8,9},{9,10},{10,11},{12,13},{... | collective-permute-start | bytes 12296 | tf_op jit(solution)/shard_map/ppermute | solution.py:23
  108.2 3.1 %collective-permute-start.14 = (f32[32,8,4]{1,0,2:T(8,128)S(1)}, f32[32,8,4]{1,0,2:T(8,128)S(1)}, u32[]{:S(2)}, u32[]{:S(2)}) collective-permute-start(f32[32,8,4]{1,0,2:T(8,128)S(1)} %get-tuple-element.78), channel_id=1, source_target_pairs={{1,0},{2,1},{3,2},{5,4},{6,5},{7,6},{9,8},{10,9},{11,10},{13,12},{... | collective-permute-start | bytes 12296 | tf_op jit(solution)/shard_map/ppermute | solution.py:26
  134.6 3.9 %collective-permute-start.15 = (f32[512,256]{1,0:T(8,128)S(1)}, f32[512,256]{1,0:T(8,128)S(1)}, u32[]{:S(2)}, u32[]{:S(2)}) collective-permute-start(f32[512,256]{1,0:T(8,128)S(1)} %constant_dynamic-slice_fusion.2), channel_id=1, source_target_pairs={{0,1},{1,0},{2,3},{3,2},{4,5},{5,4},{6,7},{7,6},{8,9},{9,8},{10,11... | collective-permute-start | bytes 1572872 | tf_op jit(solution)/shard_map/ppermute | solution.py:222
  138.7 8.7 %collective-permute-start.16 = (f32[256,256]{1,0:T(8,128)S(1)}, f32[256,256]{1,0:T(8,128)S(1)}, u32[]{:S(2)}, u32[]{:S(2)}) collective-permute-start(f32[256,256]{1,0:T(8,128)S(1)} %constant_dynamic-slice_fusion.1), channel_id=1, source_target_pairs={{0,2},{1,3},{2,0},{3,1},{4,6},{5,7},{6,4},{7,5},{8,10},{9,11},{10,... | collective-permute-start | bytes 786440 | tf_op jit(solution)/shard_map/ppermute | solution.py:222
  147.4 6.2 %collective-permute-start.17 = (f32[128,256]{1,0:T(8,128)S(1)}, f32[128,256]{1,0:T(8,128)S(1)}, u32[]{:S(2)}, u32[]{:S(2)}) collective-permute-start(f32[128,256]{1,0:T(8,128)S(1)} %constant_dynamic-slice_fusion), channel_id=1, source_target_pairs={{0,4},{4,0},{8,12},{12,8},{16,20},{20,16},{24,28},{28,24},{1,5},{5... | collective-permute-start | bytes 393224 | tf_op jit(solution)/shard_map/ppermute | solution.py:222
  150.4 26.9 %copy-start.34 = (bf16[256,256]{1,0:T(8,128)(2,1)S(1)}, bf16[256,256]{1,0:T(8,128)(2,1)}, u32[]{:S(2)}) copy-start(bf16[256,256]{1,0:T(8,128)(2,1)} %param.13) | copy-start | bytes 393220
  153.6 24.5 %copy-start.60 = (bf16[2,8,2,8,256]{4,3,2,1,0:T(8,128)(2,1)S(1)}, bf16[2,8,2,8,256]{4,3,2,1,0:T(8,128)(2,1)}, u32[]{:S(2)}) copy-start(bf16[2,8,2,8,256]{4,3,2,1,0:T(8,128)(2,1)} %copy-done.59) | copy-start | bytes 393220
  153.6 24.5 %copy-start.65 = (bf16[256,256]{1,0:T(8,128)(2,1)S(1)}, bf16[256,256]{1,0:T(8,128)(2,1)}, u32[]{:S(2)}) copy-start(bf16[256,256]{1,0:T(8,128)(2,1)} %param.12) | copy-start | bytes 393220
  153.6 24.5 %copy-start.66 = (bf16[256,256]{1,0:T(8,128)(2,1)S(1)}, bf16[256,256]{1,0:T(8,128)(2,1)}, u32[]{:S(2)}) copy-start(bf16[256,256]{1,0:T(8,128)(2,1)} %param.11) | copy-start | bytes 393220
  153.7 24.5 %copy-start.67 = (bf16[256,256]{1,0:T(8,128)(2,1)S(1)}, bf16[256,256]{1,0:T(8,128)(2,1)}, u32[]{:S(2)}) copy-start(bf16[256,256]{1,0:T(8,128)(2,1)} %param.10) | copy-start | bytes 393220
  153.7 5.0 %collective-permute-start.18 = (f32[128,256]{1,0:T(8,128)S(1)}, f32[128,256]{1,0:T(8,128)S(1)}, u32[]{:S(2)}, u32[]{:S(2)}) collective-permute-start(f32[128,256]{1,0:T(8,128)S(1)} %dynamic-slice_add_fusion.2), channel_id=1, source_target_pairs={{0,8},{4,12},{8,0},{12,4},{16,24},{20,28},{24,16},{28,20},{1,9},{5... | collective-permute-start | bytes 393224 | tf_op jit(solution)/shard_map/ppermute | solution.py:225
  158.7 6.8 %collective-permute-start.19 = (f32[128,256]{1,0:T(8,128)S(1)}, f32[128,256]{1,0:T(8,128)S(1)}, u32[]{:S(2)}, u32[]{:S(2)}) collective-permute-start(f32[128,256]{1,0:T(8,128)S(1)} %add.436), channel_id=1, source_target_pairs={{0,16},{4,20},{8,24},{12,28},{16,0},{20,4},{24,8},{28,12},{1,17},{... | collective-permute-start | bytes 393224 | tf_op jit(solution)/shard_map/ppermute | solution.py:225
  165.6 5.0 %collective-permute-start.20 = (f32[128,256]{1,0:T(8,128)S(1)}, f32[128,256]{1,0:T(8,128)S(1)}, u32[]{:S(2)}, u32[]{:S(2)}) collective-permute-start(f32[128,256]{1,0:T(8,128)S(1)} %add.437), channel_id=1, source_target_pairs={{0,4},{4,0},{8,12},{12,8},{16,20},{20,16},{24,28},{28,24},{1,5},{5... | collective-permute-start | bytes 393224 | tf_op jit(solution)/shard_map/ppermute | solution.py:187
  170.6 6.4 %collective-permute-start.21 = (f32[256,256]{1,0:T(8,128)S(1)}, f32[256,256]{1,0:T(8,128)S(1)}, u32[]{:S(2)}, u32[]{:S(2)}) collective-permute-start(f32[256,256]{1,0:T(8,128)S(1)} %pad_maximum_fusion.9), channel_id=1, source_target_pairs={{0,2},{1,3},{2,0},{3,1},{4,6},{5,7},{6,4},{7,5},{8,10},{9,11},{10,... | collective-permute-start | bytes 786440 | tf_op jit(solution)/shard_map/ppermute | solution.py:187
  177.2 2.0 %collective-permute-start.22 = (f32[512,256]{1,0:T(8,128)S(1)}, f32[512,256]{1,0:T(8,128)S(1)}, u32[]{:S(2)}, u32[]{:S(2)}) collective-permute-start(f32[512,256]{1,0:T(8,128)S(1)} %pad_maximum_fusion.8), channel_id=1, source_target_pairs={{0,1},{1,0},{2,3},{3,2},{4,5},{5,4},{6,7},{7,6},{8,9},{9,8},{10,11... | collective-permute-start | bytes 1572872 | tf_op jit(solution)/shard_map/ppermute | solution.py:187
  (66 other events, 244.2 us)

commit v4 on v3

--- a/solution.py
+++ b/solution.py
@@ -258,8 +258,8 @@
         region_memory.shape[2], region_memory.shape[3], region_memory.shape[4]
     )
     region_count = memory_local.shape[0]
-    row_tables, slot_of = tree_gather(memory_local, "gx")
-    fetched = jnp.take(row_tables, slot_of(owners) * region_count + local_ids, axis=0)
+    row_tables = lax.all_gather(memory_local, "gx", axis=0, tiled=True)
+    fetched = jnp.take(row_tables, owners * region_count + local_ids, axis=0)
     region_keyval = fetched.reshape(
         block_rows, block_cols, 2, memory_local.shape[1], memory_local.shape[2]
     )

time: 182 us -> 181 us (level)
  between operations: 2.73 us -> 16 us
  matrix products: 54.2 us -> 44.2 us
  starting transfers between devices: 43 us -> 38.5 us
  local copies, waits for them, and re-layouts: 11.9 us -> 15.3 us
  waiting for transfers between devices: 64.6 us -> 62.2 us
    ppermute x6 -> x3, waiting for transfers between devices: 32.9 us -> 9.27 us  [doubling_gather(): got = lax.ppermute(joined, axis, pairs)]
    all_gather x0 -> x1, waiting for transfers between devices: none -> 13.8 us  [on_device(): row_tables = lax.all_gather(memory_local, 'gx', axis=0, tiled=True)]
    ppermute x6 -> x3, starting transfers between devices: 12 us -> 2.33 us  [doubling_gather(): got = lax.ppermute(joined, axis, pairs)]
    dot_general x9, matrix products: 13.4 us -> 8.41 us  [key_grads(): jnp.einsum('abhqk,abqhe->abkhe', grad_score, query_heads, preferred_eleme...]
    dot_general x10, matrix products: 10 us -> 6.21 us  [piece_scores(): jnp.einsum('abqhe,abkhe->abhqk', query_heads, split_heads(key_part), pref...]
    ppermute x6, waiting for transfers between devices: 7.76 us -> 11.4 us  [padded(): lax.ppermute(lax.slice_in_dim(block, 0, width, axis=dim), axis, backward)]
    ppermute x6, starting transfers between devices: 16.4 us -> 20.1 us  [padded(): lax.ppermute(lax.slice_in_dim(block, block.shape[dim] - width, None, axis...]
    ppermute x6, waiting for transfers between devices: 0.02 us -> 3.5 us  [padded(): lax.ppermute(lax.slice_in_dim(block, block.shape[dim] - width, None, axis...]
  transfers between devices with their start and end apart: 23 -> 21, of which waited for: 13 -> 14; matrix products, arithmetic and copies ran while one was open for 12% -> 10% of each run, Pallas kernels for 0% -> 0%
where the time goes in v4:
time: 181 us; the launch traced here: 180 us
  waiting for transfers between devices  62.2 us (34%)
  matrix products  44.2 us (24%)
  starting transfers between devices  38.5 us (21%)
  between operations  16 us (9%)
  local copies, waits for them, and re-layouts  15.3 us (8%)
  other arithmetic  3.61 us (2%)
    ppermute x6, starting transfers between devices, padded(): lax.ppermute(lax.slice_in_dim(block, block.shape[dim] - width, None, axis...  20.1 us
    all_gather x1, waiting for transfers between devices, on_device(): row_tables = lax.all_gather(memory_local, 'gx', axis=0, tiled=True)  13.8 us
    dot_general x10, matrix products, query_grads(): jnp.einsum('abhqk,abkhe->abqhe', grad_score, split_heads(key_part), prefe...  13.1 us
    ppermute x3, waiting for transfers between devices, tree_sum(): joined = keep + lax.ppermute(send, axis, pairs)  13.1 us
    ppermute x6, waiting for transfers between devices, padded(): lax.ppermute(lax.slice_in_dim(block, 0, width, axis=dim), axis, backward)  11.4 us
    ppermute x2, waiting for transfers between devices, tree_sum(): joined = joined + lax.ppermute(joined, axis, pairs)  10.4 us
    ppermute x3, waiting for transfers between devices, doubling_gather(): got = lax.ppermute(joined, axis, pairs)  9.27 us
    dot_general x9, matrix products, key_grads(): jnp.einsum('abhqk,abqhe->abkhe', grad_score, query_heads, preferred_eleme...  8.41 us
  transfers between devices with their start and end apart: 21, of which 14 were waited for; matrix products, arithmetic and copies ran while one was open for 10% of the time, Pallas kernels for 0%

profile of v4, /device:TPU:0, one launch (start us, length us, event | category | flops | bytes accessed | tf_op | source)
XLA Modules:
  0.0 179.8 jit_solution(6097018177920755846)
XLA Ops:
  8.1 1.2 convolution_convert_fusion
  9.3 1.3 collective-permute-start.1
  10.6 5.5 %collective-permute-start = (bf16[8,16,512]{2,1,0:T(8,128)(2,1)S(1)}, bf16[8,16,512]{2,1,0:T(8,128)(2,1)S(1)}, u32[]{:S(2)}, u32[]{:S(2)}) collective-permute-start(bf16[8,16,512]{2,1,0:T(8,128)(2,1)S(1)} %bitcast.503), channel_id=1, source_target_pairs={{0,4},{4,8},{8,12},{12,16},{16,20},{20,24},{24,28},{1,5},{5,9},{9,... | collective-permute-start | bytes 393224 | tf_op jit(solution)/shard_map/ppermute | solution.py:23
  17.2 1.2 convolution_convert_fusion.2
  18.4 4.8 %collective-permute-start.4 = (bf16[8,16,512]{2,1,0:T(8,128)(2,1)S(1)}, bf16[8,16,512]{2,1,0:T(8,128)(2,1)S(1)}, u32[]{:S(2)}, u32[]{:S(2)}) collective-permute-start(bf16[8,16,512]{2,1,0:T(8,128)(2,1)S(1)} %get-tuple-element.67), channel_id=1, source_target_pairs={{0,4},{4,8},{8,12},{12,16},{16,20},{20,24},{24,28},{1,5},{5,9},{9,... | collective-permute-start | bytes 393224 | tf_op jit(solution)/shard_map/ppermute | solution.py:23
  23.2 1.3 collective-permute-start.5
  25.1 3.5 %collective-permute-done.4 = bf16[8,16,512]{2,1,0:T(8,128)(2,1)S(1)} collective-permute-done((bf16[8,16,512]{2,1,0:T(8,128)(2,1)S(1)}, bf16[8,16,512]{2,1,0:T(8,128)(2,1)S(1)}, u32[]{:S(2)}, u32[]{:S(2)}) %collective-permute-start.4) | collective-permute-done | bytes 131104 | tf_op jit(solution)/shard_map/ppermute | solution.py:23
  28.6 1.5 collective-permute-done.5
  30.2 1.3 collective-permute-start.6
  31.5 1.3 collective-permute-start.7
  33.0 4.8 %collective-permute-start.2 = (bf16[32,8,512]{2,1,0:T(8,128)(2,1)S(1)}, bf16[32,8,512]{2,1,0:T(8,128)(2,1)S(1)}, u32[]{:S(2)}, u32[]{:S(2)}) collective-permute-start(bf16[32,8,512]{2,1,0:T(8,128)(2,1)S(1)} %get-tuple-element.63), channel_id=1, source_target_pairs={{0,1},{1,2},{2,3},{4,5},{5,6},{6,7},{8,9},{9,10},{10,11},{12,13},{... | collective-permute-start | bytes 786440 | tf_op jit(solution)/shard_map/ppermute | solution.py:23
  37.7 1.3 collective-permute-start.3
  39.7 2.8 %collective-permute-done.3 = bf16[32,8,512]{2,1,0:T(8,128)(2,1)} collective-permute-done((bf16[32,8,512]{2,1,0:T(8,128)(2,1)S(1)}, bf16[32,8,512]{2,1,0:T(8,128)(2,1)}, u32[]{:S(2)}, u32[]{:S(2)}) %collective-permute-start.3) | collective-permute-done | bytes 262176 | tf_op jit(solution)/shard_map/ppermute | solution.py:26
  43.7 1.2 slice_bitcast_fusion.18
  50.1 1.5 slice_bitcast_fusion
  51.6 13.8 %all-gather.3.cloned.1.call-done = bf16[1,1,32,64,512]{4,3,1,0,2:T(8,128)(2,1)} async-done(((bf16[1,1,4,64,512]{4,3,1,0,2:T(8,128)(2,1)}), bf16[1,1,32,64,512]{4,3,1,0,2:T(8,128)(2,1)}) %all-gather.3.cloned.1.call-update) | async-done | bytes 2097168 | tf_op jit(solution)/shard_map/all_gather | solution.py:261
  65.4 2.2 %gather_fusion = bf16[8,64,512]{2,1,0:T(8,128)(2,1)S(1)} fusion(bf16[32,64,512]{2,1,0:T(8,128)(2,1)} %bitcast.502, s32[1024]{0:T(1024)S(1)} %pad_clamp_fusion), kind=kCustom, calls=%fused_computation | custom fusion | bytes 1048608 | tf_op jit(solution)/shard_map/jit(_take)/gather | solution.py:262
  68.1 1.2 fusion.447
  75.2 2.1 %fusion.84 = f32[2,2,2,128,64]{3,4,2,1,0:T(8,128)} fusion(f32[2,2,2,64,64]{3,4,2,1,0:T(8,128)S(1)} %get-tuple-element.119, f32[2,2,2,64]{3,2,1,0:T(2,128)S(1)} %bitcast.469, f32[2,2,2,64]{3,2,1,0:T(2,128)S(1)} %log_add_fusion, bf16[2,2,8,2,8,128]{5,4,3,2,1,0:T(8,128)(2,1)} %copy-done.48, bf16[2,2,8,2,8,128]{5,4,3,2,1,0:T(8,128)(2,1)} %get-tuple-element.52, ...), kind=kOutput, calls=%fused_computation.165 | convolution fusion | flops 16908288 | bytes 790528 | tf_op jit(solution)/shard_map/abhqk,abkhe->abqhe/dot_general | solution.py:115
  77.3 2.2 %convolution_add_fusion.24 = f32[2,2,2,128,64]{3,4,2,1,0:T(8,128)} fusion(f32[2,2,2,128,64]{3,4,2,1,0:T(8,128)} %fusion.84, f32[2,2,2,64,64]{3,4,2,1,0:T(8,128)S(1)} %get-tuple-element.121, f32[2,2,2,64]{3,2,1,0:T(2,128)S(1)} %bitcast.471, f32[2,2,2,64]{3,2,1,0:T(2,128)S(1)} %log_add_fusion, bf16[2,2,8,2,8,128]{5,4,3,2,1,0:T(8,128)(2,1)} %get-tuple-element.42, ...), kind=kOutput, calls=%fused_computation.98 | convolution fusion | flops 16973824 | bytes 1052672 | tf_op jit(solution)/shard_map/abhqk,abkhe->abqhe/dot_general | solution.py:115
  79.6 2.2 %convolution_add_fusion.23 = f32[2,2,2,128,64]{3,4,2,1,0:T(8,128)} fusion(f32[2,2,2,128,64]{3,4,2,1,0:T(8,128)} %convolution_add_fusion.24, f32[2,2,2,64,64]{3,4,2,1,0:T(8,128)S(1)} %get-tuple-element.117, f32[2,2,2,64]{3,2,1,0:T(2,128)S(1)} %bitcast.472, f32[2,2,2,64]{3,2,1,0:T(2,128)S(1)} %log_add_fusion, ...), kind=kOutput, calls=%fused_computation.95 | convolution fusion | flops 16973824 | bytes 1052672 | tf_op jit(solution)/shard_map/abhqk,abkhe->abqhe/dot_general | solution.py:115
  81.8 1.4 convolution_add_fusion.22
  83.2 1.3 convolution_add_fusion.21
  84.6 1.3 convolution_add_fusion.20
  86.0 1.3 convolution_add_fusion.19
  88.8 2.4 %collective-permute-start.8 = (f32[8,16,4]{1,0,2:T(8,128)S(1)}, f32[8,16,4]{1,0,2:T(8,128)S(1)}, u32[]{:S(2)}, u32[]{:S(2)}) collective-permute-start(f32[8,16,4]{1,0,2:T(8,128)S(1)} %slice.413), channel_id=1, source_target_pairs={{0,4},{4,8},{8,12},{12,16},{16,20},{20,24},{24,28},{1,5},{5,9},{9,... | collective-permute-start | bytes 6152 | tf_op jit(solution)/shard_map/ppermute | solution.py:23
  93.0 1.3 collective-permute-start.9
  94.3 4.7 %collective-permute-done.9 = f32[8,16,4]{1,0,2:T(8,128)S(1)} collective-permute-done((f32[8,16,4]{1,0,2:T(8,128)S(1)}, f32[8,16,4]{1,0,2:T(8,128)S(1)}, u32[]{:S(2)}, u32[]{:S(2)}) %collective-permute-start.9) | collective-permute-done | bytes 2080 | tf_op jit(solution)/shard_map/ppermute | solution.py:26
  99.1 1.3 collective-permute-start.10
  100.4 1.5 collective-permute-start.11
  102.8 2.4 %collective-permute-done.11 = f32[32,8,4]{1,0,2:T(8,128)S(1)} collective-permute-done((f32[32,8,4]{1,0,2:T(8,128)S(1)}, f32[32,8,4]{1,0,2:T(8,128)S(1)}, u32[]{:S(2)}, u32[]{:S(2)}) %collective-permute-start.11) | collective-permute-done | bytes 4128 | tf_op jit(solution)/shard_map/ppermute | solution.py:26
  113.3 1.6 convert_element_type.219
  115.0 1.6 copy.521
  116.5 2.0 %convolution_add_fusion.15 = f32[2,2,2,128,64]{3,4,2,1,0:T(8,128)} fusion(f32[2,2,2,128,64]{3,4,2,1,0:T(8,128)S(1)} %fusion.82, f32[2,2,2,64,64]{3,4,2,1,0:T(8,128)} %copy-done.23, f32[2,2,2,64]{3,2,1,0:T(2,128)} %get-tuple-element.89, bf16[2,2,8,2,8,128]{5,4,3,2,1,0:T(8,128)(2,1)S(1)} %copy-done.7, bf16[2,2,8,2,8,128]{5,4,3,2,1,0:T(8,128)(2,1)S(1)} %copy-done.37, ...), kind=kOutput, calls=%fused_computation.18 | convolution fusion | flops 16941056 | bytes 1050624 | tf_op jit(solution)/shard_map/abhqk,abqhe->abkhe/dot_general | solution.py:154
  118.5 1.4 convolution_add_fusion.14
  120.0 1.2 convolution_add_fusion.13
  121.2 1.3 convolution_add_fusion.12
  122.5 1.2 convolution_add_fusion.11
  125.6 3.0 %collective-permute-start.12 = (f32[512,256]{1,0:T(8,128)S(1)}, f32[512,256]{1,0:T(8,128)S(1)}, u32[]{:S(2)}, u32[]{:S(2)}) collective-permute-start(f32[512,256]{1,0:T(8,128)S(1)} %constant_dynamic-slice_fusion.2), channel_id=1, source_target_pairs={{0,1},{1,0},{2,3},{3,2},{4,5},{5,4},{6,7},{7,6},{8,9},{9,8},{10,11... | collective-permute-start | bytes 1572872 | tf_op jit(solution)/shard_map/ppermute | solution.py:222
  128.6 1.5 collective-permute-done.12
  130.5 8.4 %collective-permute-done.13 = f32[256,256]{1,0:T(8,128)S(1)} collective-permute-done((f32[256,256]{1,0:T(8,128)S(1)}, f32[256,256]{1,0:T(8,128)S(1)}, u32[]{:S(2)}, u32[]{:S(2)}) %collective-permute-start.13) | collective-permute-done | bytes 262176 | tf_op jit(solution)/shard_map/ppermute | solution.py:222
  139.0 3.0 %collective-permute-start.14 = (f32[128,256]{1,0:T(8,128)S(1)}, f32[128,256]{1,0:T(8,128)S(1)}, u32[]{:S(2)}, u32[]{:S(2)}) collective-permute-start(f32[128,256]{1,0:T(8,128)S(1)} %constant_dynamic-slice_fusion), channel_id=1, source_target_pairs={{0,4},{4,0},{8,12},{12,8},{16,20},{20,16},{24,28},{28,24},{1,5},{5... | collective-permute-start | bytes 393224 | tf_op jit(solution)/shard_map/ppermute | solution.py:222
  141.9 3.2 %collective-permute-done.14 = f32[128,256]{1,0:T(8,128)S(1)} collective-permute-done((f32[128,256]{1,0:T(8,128)S(1)}, f32[128,256]{1,0:T(8,128)S(1)}, u32[]{:S(2)}, u32[]{:S(2)}) %collective-permute-start.14) | collective-permute-done | bytes 131104 | tf_op jit(solution)/shard_map/ppermute | solution.py:222
  146.2 4.1 %collective-permute-done.15 = f32[128,256]{1,0:T(8,128)S(1)} collective-permute-done((f32[128,256]{1,0:T(8,128)S(1)}, f32[128,256]{1,0:T(8,128)S(1)}, u32[]{:S(2)}, u32[]{:S(2)}) %collective-permute-start.15) | collective-permute-done | bytes 131104 | tf_op jit(solution)/shard_map/ppermute | solution.py:225
  151.2 6.4 %collective-permute-done.16 = f32[128,256]{1,0:T(8,128)S(1)} collective-permute-done((f32[128,256]{1,0:T(8,128)S(1)}, f32[128,256]{1,0:T(8,128)S(1)}, u32[]{:S(2)}, u32[]{:S(2)}) %collective-permute-start.16) | collective-permute-done | bytes 131104 | tf_op jit(solution)/shard_map/ppermute | solution.py:225
  157.6 1.8 %collective-permute-start.17 = (f32[128,256]{1,0:T(8,128)S(1)}, f32[128,256]{1,0:T(8,128)S(1)}, u32[]{:S(2)}, u32[]{:S(2)}) collective-permute-start(f32[128,256]{1,0:T(8,128)S(1)} %add.392), channel_id=1, source_target_pairs={{0,4},{4,0},{8,12},{12,8},{16,20},{20,16},{24,28},{28,24},{1,5},{5... | collective-permute-start | bytes 393224 | tf_op jit(solution)/shard_map/ppermute | solution.py:187
  159.4 3.2 %collective-permute-done.17 = f32[128,256]{1,0:T(8,128)S(1)} collective-permute-done((f32[128,256]{1,0:T(8,128)S(1)}, f32[128,256]{1,0:T(8,128)S(1)}, u32[]{:S(2)}, u32[]{:S(2)}) %collective-permute-start.17) | collective-permute-done | bytes 131104 | tf_op jit(solution)/shard_map/ppermute | solution.py:187
  163.2 6.0 %collective-permute-done.18 = f32[256,256]{1,0:T(8,128)S(1)} collective-permute-done((f32[256,256]{1,0:T(8,128)S(1)}, f32[256,256]{1,0:T(8,128)S(1)}, u32[]{:S(2)}, u32[]{:S(2)}) %collective-permute-start.18) | collective-permute-done | bytes 262176 | tf_op jit(solution)/shard_map/ppermute | solution.py:187
  (305 shorter events, 35.8 us)
Async XLA Ops:
  7.2 17.4 %copy-start.62 = (s32[1,1,4,2]{2,3,1,0:T(2,128)S(1)}, s32[1,1,4,2]{2,3,1,0:T(2,128)}, u32[]{:S(2)}) copy-start(s32[1,1,4,2]{2,3,1,0:T(2,128)} %param.16) | copy-start | bytes 100
  7.2 17.4 %copy-start.63 = (s32[1,1,4,2]{2,3,1,0:T(2,128)S(1)}, s32[1,1,4,2]{2,3,1,0:T(2,128)}, u32[]{:S(2)}) copy-start(s32[1,1,4,2]{2,3,1,0:T(2,128)} %param.15) | copy-start | bytes 100
  7.2 58.2 %all-gather.3.cloned.1.call-start = ((), (), s32[]{:S(2)}) async-start(), calls=%async_computation | async-start | bytes 2359296 | tf_op jit(solution)/shard_map/all_gather | solution.py:261
  9.3 23.5 %collective-permute-start.1 = (bf16[8,16,512]{2,1,0:T(8,128)(2,1)S(1)}, bf16[8,16,512]{2,1,0:T(8,128)(2,1)S(1)}, u32[]{:S(2)}, u32[]{:S(2)}) collective-permute-start(bf16[8,16,512]{2,1,0:T(8,128)(2,1)S(1)} %bitcast.504), channel_id=1, source_target_pairs={{4,0},{8,4},{12,8},{16,12},{20,16},{24,20},{28,24},{5,1},{9,5},{13... | collective-permute-start | bytes 393224 | tf_op jit(solution)/shard_map/ppermute | solution.py:26
  10.6 22.2 %collective-permute-start = (bf16[8,16,512]{2,1,0:T(8,128)(2,1)S(1)}, bf16[8,16,512]{2,1,0:T(8,128)(2,1)S(1)}, u32[]{:S(2)}, u32[]{:S(2)}) collective-permute-start(bf16[8,16,512]{2,1,0:T(8,128)(2,1)S(1)} %bitcast.503), channel_id=1, source_target_pairs={{0,4},{4,8},{8,12},{12,16},{16,20},{20,24},{24,28},{1,5},{5,9},{9,... | collective-permute-start | bytes 393224 | tf_op jit(solution)/shard_map/ppermute | solution.py:23
  18.4 10.2 %collective-permute-start.4 = (bf16[8,16,512]{2,1,0:T(8,128)(2,1)S(1)}, bf16[8,16,512]{2,1,0:T(8,128)(2,1)S(1)}, u32[]{:S(2)}, u32[]{:S(2)}) collective-permute-start(bf16[8,16,512]{2,1,0:T(8,128)(2,1)S(1)} %get-tuple-element.67), channel_id=1, source_target_pairs={{0,4},{4,8},{8,12},{12,16},{16,20},{20,24},{24,28},{1,5},{5,9},{9,... | collective-permute-start | bytes 393224 | tf_op jit(solution)/shard_map/ppermute | solution.py:23
  23.2 6.9 %collective-permute-start.5 = (bf16[8,16,512]{2,1,0:T(8,128)(2,1)S(1)}, bf16[8,16,512]{2,1,0:T(8,128)(2,1)S(1)}, u32[]{:S(2)}, u32[]{:S(2)}) collective-permute-start(bf16[8,16,512]{2,1,0:T(8,128)(2,1)S(1)} %get-tuple-element.68), channel_id=1, source_target_pairs={{4,0},{8,4},{12,8},{16,12},{20,16},{24,20},{28,24},{5,1},{9,5},{13... | collective-permute-start | bytes 393224 | tf_op jit(solution)/shard_map/ppermute | solution.py:26
  25.0 20.0 %copy-start.76 = (pred[2,2]{1,0:T(4,128)(4,1)}, pred[2,2]{1,0:T(4,128)(4,1)S(1)}, u32[]{:S(2)}) copy-start(pred[2,2]{1,0:T(4,128)(4,1)S(1)} %get-tuple-element.94) | copy-start | bytes 16
  25.0 20.2 %copy-start.74 = (pred[2,2]{1,0:T(4,128)(4,1)}, pred[2,2]{1,0:T(4,128)(4,1)S(1)}, u32[]{:S(2)}) copy-start(pred[2,2]{1,0:T(4,128)(4,1)S(1)} %get-tuple-element.95) | copy-start | bytes 16
  25.0 20.5 %copy-start.72 = (pred[2,2]{1,0:T(4,128)(4,1)}, pred[2,2]{1,0:T(4,128)(4,1)S(1)}, u32[]{:S(2)}) copy-start(pred[2,2]{1,0:T(4,128)(4,1)S(1)} %get-tuple-element.96) | copy-start | bytes 16
  25.0 20.7 %copy-start.70 = (pred[2,2]{1,0:T(4,128)(4,1)}, pred[2,2]{1,0:T(4,128)(4,1)S(1)}, u32[]{:S(2)}) copy-start(pred[2,2]{1,0:T(4,128)(4,1)S(1)} %get-tuple-element.97) | copy-start | bytes 16
  25.0 20.9 %copy-start.68 = (pred[2,2]{1,0:T(4,128)(4,1)}, pred[2,2]{1,0:T(4,128)(4,1)S(1)}, u32[]{:S(2)}) copy-start(pred[2,2]{1,0:T(4,128)(4,1)S(1)} %get-tuple-element.99) | copy-start | bytes 16
  25.0 21.7 %copy-start.66 = (pred[2,2]{1,0:T(4,128)(4,1)}, pred[2,2]{1,0:T(4,128)(4,1)S(1)}, u32[]{:S(2)}) copy-start(pred[2,2]{1,0:T(4,128)(4,1)S(1)} %get-tuple-element.100) | copy-start | bytes 16
  25.1 22.6 %copy-start.64 = (pred[2,2]{1,0:T(4,128)(4,1)}, pred[2,2]{1,0:T(4,128)(4,1)S(1)}, u32[]{:S(2)}) copy-start(pred[2,2]{1,0:T(4,128)(4,1)S(1)} %get-tuple-element.93) | copy-start | bytes 16
  25.1 23.4 %copy-start.78 = (pred[2,2]{1,0:T(4,128)(4,1)}, pred[2,2]{1,0:T(4,128)(4,1)S(1)}, u32[]{:S(2)}) copy-start(pred[2,2]{1,0:T(4,128)(4,1)S(1)} %get-tuple-element.101) | copy-start | bytes 16
  25.1 24.2 %copy-start.69 = (pred[2,2]{1,0:T(4,128)(4,1)}, pred[2,2]{1,0:T(4,128)(4,1)S(1)}, u32[]{:S(2)}) copy-start(pred[2,2]{1,0:T(4,128)(4,1)S(1)} %get-tuple-element.98) | copy-start | bytes 16
  30.2 9.3 %collective-permute-start.6 = (bf16[32,8,512]{2,1,0:T(8,128)(2,1)S(1)}, bf16[32,8,512]{2,1,0:T(8,128)(2,1)S(1)}, u32[]{:S(2)}, u32[]{:S(2)}) collective-permute-start(bf16[32,8,512]{2,1,0:T(8,128)(2,1)S(1)} %get-tuple-element.59), channel_id=1, source_target_pairs={{0,1},{1,2},{2,3},{4,5},{5,6},{6,7},{8,9},{9,10},{10,11},{12,13},{... | collective-permute-start | bytes 786440 | tf_op jit(solution)/shard_map/ppermute | solution.py:23
  31.5 8.0 %collective-permute-start.7 = (bf16[32,8,512]{2,1,0:T(8,128)(2,1)S(1)}, bf16[32,8,512]{2,1,0:T(8,128)(2,1)S(1)}, u32[]{:S(2)}, u32[]{:S(2)}) collective-permute-start(bf16[32,8,512]{2,1,0:T(8,128)(2,1)S(1)} %get-tuple-element.60), channel_id=1, source_target_pairs={{1,0},{2,1},{3,2},{5,4},{6,5},{7,6},{9,8},{10,9},{11,10},{13,12},{... | collective-permute-start | bytes 786440 | tf_op jit(solution)/shard_map/ppermute | solution.py:26
  33.0 6.8 %collective-permute-start.2 = (bf16[32,8,512]{2,1,0:T(8,128)(2,1)S(1)}, bf16[32,8,512]{2,1,0:T(8,128)(2,1)S(1)}, u32[]{:S(2)}, u32[]{:S(2)}) collective-permute-start(bf16[32,8,512]{2,1,0:T(8,128)(2,1)S(1)} %get-tuple-element.63), channel_id=1, source_target_pairs={{0,1},{1,2},{2,3},{4,5},{5,6},{6,7},{8,9},{9,10},{10,11},{12,13},{... | collective-permute-start | bytes 786440 | tf_op jit(solution)/shard_map/ppermute | solution.py:23
  37.7 4.8 %collective-permute-start.3 = (bf16[32,8,512]{2,1,0:T(8,128)(2,1)S(1)}, bf16[32,8,512]{2,1,0:T(8,128)(2,1)}, u32[]{:S(2)}, u32[]{:S(2)}) collective-permute-start(bf16[32,8,512]{2,1,0:T(8,128)(2,1)S(1)} %get-tuple-element.64), channel_id=1, source_target_pairs={{1,0},{2,1},{3,2},{5,4},{6,5},{7,6},{9,8},{10,9},{11,10},{13,12},{... | collective-permute-start | bytes 786440 | tf_op jit(solution)/shard_map/ppermute | solution.py:26
  39.5 9.8 %copy-start.49 = (bf16[2,2,64,2,128]{4,3,2,1,0:T(2,128)(2,1)}, bf16[2,2,64,2,128]{4,3,2,1,0:T(2,128)(2,1)S(1)}, u32[]{:S(2)}) copy-start(bf16[2,2,64,2,128]{4,3,2,1,0:T(2,128)(2,1)S(1)} %reshape_reshape.29) | copy-start | bytes 393220
  79.5 6.4 %copy-start.14 = (bf16[2,2,8,2,8,128]{5,4,3,2,1,0:T(8,128)(2,1)S(1)}, bf16[2,2,8,2,8,128]{5,4,3,2,1,0:T(8,128)(2,1)}, u32[]{:S(2)}) copy-start(bf16[2,2,8,2,8,128]{5,4,3,2,1,0:T(8,128)(2,1)} %get-tuple-element.37) | copy-start | bytes 393220
  81.8 5.5 %copy-start.12 = (bf16[2,2,8,2,8,128]{5,4,3,2,1,0:T(8,128)(2,1)S(1)}, bf16[2,2,8,2,8,128]{5,4,3,2,1,0:T(8,128)(2,1)}, u32[]{:S(2)}) copy-start(bf16[2,2,8,2,8,128]{5,4,3,2,1,0:T(8,128)(2,1)} %get-tuple-element.36) | copy-start | bytes 393220
  88.8 5.5 %collective-permute-start.8 = (f32[8,16,4]{1,0,2:T(8,128)S(1)}, f32[8,16,4]{1,0,2:T(8,128)S(1)}, u32[]{:S(2)}, u32[]{:S(2)}) collective-permute-start(f32[8,16,4]{1,0,2:T(8,128)S(1)} %slice.413), channel_id=1, source_target_pairs={{0,4},{4,8},{8,12},{12,16},{16,20},{20,24},{24,28},{1,5},{5,9},{9,... | collective-permute-start | bytes 6152 | tf_op jit(solution)/shard_map/ppermute | solution.py:23
  91.5 14.9 %copy-start.33 = (bf16[2,2,8,2,8,128]{5,4,3,2,1,0:T(8,128)(2,1)S(1)}, bf16[2,2,8,2,8,128]{5,4,3,2,1,0:T(8,128)(2,1)}, u32[]{:S(2)}) copy-start(bf16[2,2,8,2,8,128]{5,4,3,2,1,0:T(8,128)(2,1)} %copy-done.32) | copy-start | bytes 393220
  91.5 14.9 %copy-start.38 = (bf16[2,2,8,2,8,128]{5,4,3,2,1,0:T(8,128)(2,1)S(1)}, bf16[2,2,8,2,8,128]{5,4,3,2,1,0:T(8,128)(2,1)}, u32[]{:S(2)}) copy-start(bf16[2,2,8,2,8,128]{5,4,3,2,1,0:T(8,128)(2,1)} %get-tuple-element.34) | copy-start | bytes 393220
  91.5 14.9 %copy-start.79 = (pred[2,2]{1,0:T(4,128)(4,1)S(1)}, pred[2,2]{1,0:T(4,128)(4,1)}, u32[]{:S(2)}) copy-start(pred[2,2]{1,0:T(4,128)(4,1)} %copy-done.78) | copy-start | bytes 16
  92.5 14.1 %copy-start.8 = (bf16[2,2,8,2,8,128]{5,4,3,2,1,0:T(8,128)(2,1)S(1)}, bf16[2,2,8,2,8,128]{5,4,3,2,1,0:T(8,128)(2,1)}, u32[]{:S(2)}) copy-start(bf16[2,2,8,2,8,128]{5,4,3,2,1,0:T(8,128)(2,1)} %get-tuple-element.33) | copy-start | bytes 393220
  92.7 12.5 %copy-start.51 = (bf16[2,8,2,8,256]{4,3,2,1,0:T(8,128)(2,1)}, bf16[2,8,2,8,256]{4,3,2,1,0:T(8,128)(2,1)S(1)}, u32[]{:S(2)}) copy-start(bf16[2,8,2,8,256]{4,3,2,1,0:T(8,128)(2,1)S(1)} %copy.440) | copy-start | bytes 393220
  93.0 6.0 %collective-permute-start.9 = (f32[8,16,4]{1,0,2:T(8,128)S(1)}, f32[8,16,4]{1,0,2:T(8,128)S(1)}, u32[]{:S(2)}, u32[]{:S(2)}) collective-permute-start(f32[8,16,4]{1,0,2:T(8,128)S(1)} %slice.415), channel_id=1, source_target_pairs={{4,0},{8,4},{12,8},{16,12},{20,16},{24,20},{28,24},{5,1},{9,5},{13... | collective-permute-start | bytes 6152 | tf_op jit(solution)/shard_map/ppermute | solution.py:26
  99.1 3.7 %collective-permute-start.10 = (f32[32,8,4]{1,0,2:T(8,128)S(1)}, f32[32,8,4]{1,0,2:T(8,128)S(1)}, u32[]{:S(2)}, u32[]{:S(2)}) collective-permute-start(f32[32,8,4]{1,0,2:T(8,128)S(1)} %get-tuple-element.71), channel_id=1, source_target_pairs={{0,1},{1,2},{2,3},{4,5},{5,6},{6,7},{8,9},{9,10},{10,11},{12,13},{... | collective-permute-start | bytes 12296 | tf_op jit(solution)/shard_map/ppermute | solution.py:23
  100.4 4.9 %collective-permute-start.11 = (f32[32,8,4]{1,0,2:T(8,128)S(1)}, f32[32,8,4]{1,0,2:T(8,128)S(1)}, u32[]{:S(2)}, u32[]{:S(2)}) collective-permute-start(f32[32,8,4]{1,0,2:T(8,128)S(1)} %get-tuple-element.72), channel_id=1, source_target_pairs={{1,0},{2,1},{3,2},{5,4},{6,5},{7,6},{9,8},{10,9},{11,10},{13,12},{... | collective-permute-start | bytes 12296 | tf_op jit(solution)/shard_map/ppermute | solution.py:26
  101.8 5.3 %copy-start.54 = (bf16[2,2,8,2,8,128]{5,4,3,2,1,0:T(8,128)(2,1)S(1)}, bf16[2,2,8,2,8,128]{5,4,3,2,1,0:T(8,128)(2,1)}, u32[]{:S(2)}) copy-start(bf16[2,2,8,2,8,128]{5,4,3,2,1,0:T(8,128)(2,1)} %get-tuple-element.18) | copy-start | bytes 393220
  101.8 5.3 %copy-start.77 = (pred[2,2]{1,0:T(4,128)(4,1)S(1)}, pred[2,2]{1,0:T(4,128)(4,1)}, u32[]{:S(2)}) copy-start(pred[2,2]{1,0:T(4,128)(4,1)} %copy-done.76) | copy-start | bytes 16
  118.5 5.2 %copy-start.29 = (bf16[2,2,8,2,8,128]{5,4,3,2,1,0:T(8,128)(2,1)S(1)}, bf16[2,2,8,2,8,128]{5,4,3,2,1,0:T(8,128)(2,1)}, u32[]{:S(2)}) copy-start(bf16[2,2,8,2,8,128]{5,4,3,2,1,0:T(8,128)(2,1)} %get-tuple-element.22) | copy-start | bytes 393220
  125.6 4.5 %collective-permute-start.12 = (f32[512,256]{1,0:T(8,128)S(1)}, f32[512,256]{1,0:T(8,128)S(1)}, u32[]{:S(2)}, u32[]{:S(2)}) collective-permute-start(f32[512,256]{1,0:T(8,128)S(1)} %constant_dynamic-slice_fusion.2), channel_id=1, source_target_pairs={{0,1},{1,0},{2,3},{3,2},{4,5},{5,4},{6,7},{7,6},{8,9},{9,8},{10,11... | collective-permute-start | bytes 1572872 | tf_op jit(solution)/shard_map/ppermute | solution.py:222
  130.2 8.7 %collective-permute-start.13 = (f32[256,256]{1,0:T(8,128)S(1)}, f32[256,256]{1,0:T(8,128)S(1)}, u32[]{:S(2)}, u32[]{:S(2)}) collective-permute-start(f32[256,256]{1,0:T(8,128)S(1)} %constant_dynamic-slice_fusion.1), channel_id=1, source_target_pairs={{0,2},{1,3},{2,0},{3,1},{4,6},{5,7},{6,4},{7,5},{8,10},{9,11},{10,... | collective-permute-start | bytes 786440 | tf_op jit(solution)/shard_map/ppermute | solution.py:222
  139.0 6.2 %collective-permute-start.14 = (f32[128,256]{1,0:T(8,128)S(1)}, f32[128,256]{1,0:T(8,128)S(1)}, u32[]{:S(2)}, u32[]{:S(2)}) collective-permute-start(f32[128,256]{1,0:T(8,128)S(1)} %constant_dynamic-slice_fusion), channel_id=1, source_target_pairs={{0,4},{4,0},{8,12},{12,8},{16,20},{20,16},{24,28},{28,24},{1,5},{5... | collective-permute-start | bytes 393224 | tf_op jit(solution)/shard_map/ppermute | solution.py:222
  141.9 27.4 %copy-start.26 = (bf16[256,256]{1,0:T(8,128)(2,1)S(1)}, bf16[256,256]{1,0:T(8,128)(2,1)}, u32[]{:S(2)}) copy-start(bf16[256,256]{1,0:T(8,128)(2,1)} %param.13) | copy-start | bytes 393220
  145.2 25.0 %copy-start.52 = (bf16[2,8,2,8,256]{4,3,2,1,0:T(8,128)(2,1)S(1)}, bf16[2,8,2,8,256]{4,3,2,1,0:T(8,128)(2,1)}, u32[]{:S(2)}) copy-start(bf16[2,8,2,8,256]{4,3,2,1,0:T(8,128)(2,1)} %copy-done.51) | copy-start | bytes 393220
  145.2 25.0 %copy-start.57 = (bf16[256,256]{1,0:T(8,128)(2,1)S(1)}, bf16[256,256]{1,0:T(8,128)(2,1)}, u32[]{:S(2)}) copy-start(bf16[256,256]{1,0:T(8,128)(2,1)} %param.12) | copy-start | bytes 393220
  145.2 25.0 %copy-start.58 = (bf16[256,256]{1,0:T(8,128)(2,1)S(1)}, bf16[256,256]{1,0:T(8,128)(2,1)}, u32[]{:S(2)}) copy-start(bf16[256,256]{1,0:T(8,128)(2,1)} %param.11) | copy-start | bytes 393220
  145.2 25.0 %copy-start.59 = (bf16[256,256]{1,0:T(8,128)(2,1)S(1)}, bf16[256,256]{1,0:T(8,128)(2,1)}, u32[]{:S(2)}) copy-start(bf16[256,256]{1,0:T(8,128)(2,1)} %param.10) | copy-start | bytes 393220
  145.2 5.0 %collective-permute-start.15 = (f32[128,256]{1,0:T(8,128)S(1)}, f32[128,256]{1,0:T(8,128)S(1)}, u32[]{:S(2)}, u32[]{:S(2)}) collective-permute-start(f32[128,256]{1,0:T(8,128)S(1)} %dynamic-slice_add_fusion.2), channel_id=1, source_target_pairs={{0,8},{4,12},{8,0},{12,4},{16,24},{20,28},{24,16},{28,20},{1,9},{5... | collective-permute-start | bytes 393224 | tf_op jit(solution)/shard_map/ppermute | solution.py:225
  150.3 7.3 %collective-permute-start.16 = (f32[128,256]{1,0:T(8,128)S(1)}, f32[128,256]{1,0:T(8,128)S(1)}, u32[]{:S(2)}, u32[]{:S(2)}) collective-permute-start(f32[128,256]{1,0:T(8,128)S(1)} %add.391), channel_id=1, source_target_pairs={{0,16},{4,20},{8,24},{12,28},{16,0},{20,4},{24,8},{28,12},{1,17},{... | collective-permute-start | bytes 393224 | tf_op jit(solution)/shard_map/ppermute | solution.py:225
  157.6 5.0 %collective-permute-start.17 = (f32[128,256]{1,0:T(8,128)S(1)}, f32[128,256]{1,0:T(8,128)S(1)}, u32[]{:S(2)}, u32[]{:S(2)}) collective-permute-start(f32[128,256]{1,0:T(8,128)S(1)} %add.392), channel_id=1, source_target_pairs={{0,4},{4,0},{8,12},{12,8},{16,20},{20,16},{24,28},{28,24},{1,5},{5... | collective-permute-start | bytes 393224 | tf_op jit(solution)/shard_map/ppermute | solution.py:187
  162.7 6.4 %collective-permute-start.18 = (f32[256,256]{1,0:T(8,128)S(1)}, f32[256,256]{1,0:T(8,128)S(1)}, u32[]{:S(2)}, u32[]{:S(2)}) collective-permute-start(f32[256,256]{1,0:T(8,128)S(1)} %pad_maximum_fusion.6), channel_id=1, source_target_pairs={{0,2},{1,3},{2,0},{3,1},{4,6},{5,7},{6,4},{7,5},{8,10},{9,11},{10,... | collective-permute-start | bytes 786440 | tf_op jit(solution)/shard_map/ppermute | solution.py:187
  169.2 2.0 %collective-permute-start.19 = (f32[512,256]{1,0:T(8,128)S(1)}, f32[512,256]{1,0:T(8,128)S(1)}, u32[]{:S(2)}, u32[]{:S(2)}) collective-permute-start(f32[512,256]{1,0:T(8,128)S(1)} %pad_maximum_fusion.5), channel_id=1, source_target_pairs={{0,1},{1,0},{2,3},{3,2},{4,5},{5,4},{6,7},{7,6},{8,9},{9,8},{10,11... | collective-permute-start | bytes 1572872 | tf_op jit(solution)/shard_map/ppermute | solution.py:187
  (53 other events, 144.7 us)
Sparse Core Ops, SparseCore 0:
  10.2 55.2 all-gather.2

commit v5 on v4

--- a/solution.py
+++ b/solution.py
@@ -26,6 +26,30 @@
         high = lax.ppermute(lax.slice_in_dim(block, 0, width, axis=dim), axis, backward)
         block = jnp.concatenate([low, block, high], axis=dim)
     return block
+
+
+def halo(block, width):
+    axes = ("gx", "gy")
+    rows_n, cols_n = lax.axis_size("gx"), lax.axis_size("gy")
+    rows, cols = block.shape[0], block.shape[1]
+    row_parts = {-1: slice(rows - width, rows), 0: slice(0, rows), 1: slice(0, width)}
+    col_parts = {-1: slice(cols - width, cols), 0: slice(0, cols), 1: slice(0, width)}
+    grid = []
+    for row_off in (-1, 0, 1):
+        line = []
+        for col_off in (-1, 0, 1):
+            piece = block[row_parts[row_off], col_parts[col_off]]
+            if row_off or col_off:
+                pairs = [
+                    ((i + row_off) * cols_n + j + col_off, i * cols_n + j)
+                    for i in range(rows_n)
+                    for j in range(cols_n)
+                    if 0 <= i + row_off < rows_n and 0 <= j + col_off < cols_n
+                ]
+                piece = lax.ppermute(piece, axes, pairs)
+            line.append(piece)
+        grid.append(jnp.concatenate(line, axis=1))
+    return jnp.concatenate(grid, axis=0)
 
 
 def to_blocks(grid_array):
@@ -243,7 +267,7 @@
     queries = jnp.dot(flat_in, w_query, preferred_element_type=jnp.float32).astype(jnp.bfloat16)
     keyvals = jnp.dot(flat_in, w_pair, preferred_element_type=jnp.float32).astype(jnp.bfloat16)
     keyvals = keyvals.reshape(tile_rows, tile_cols, 2 * model_width)
-    keyval_grid = padded(keyvals, (("gx", 0), ("gy", 1)), BSIDE)
+    keyval_grid = halo(keyvals, BSIDE)
     keyval_pad = to_blocks(keyval_grid)
     gx_count = lax.axis_size("gx")
     gy_count = lax.axis_size("gy")
@@ -287,9 +311,9 @@
         ],
         -1,
     )
-    query_halo = padded(query_grid, (("gx", 0), ("gy", 1)), BSIDE)
+    query_halo = halo(query_grid, BSIDE)
     stat_grid = from_blocks(jnp.concatenate([log_totals, delta_rows], 2).transpose(0, 1, 3, 2))
-    stat_halo = padded(stat_grid, (("gx", 0), ("gy", 1)), BSIDE)
+    stat_halo = halo(stat_grid, BSIDE)
     query_all = to_blocks(query_halo)
     stat_pad = to_blocks(stat_halo).transpose(0, 1, 3, 2)
     d_keys, d_values = key_grads(

time: 181 us -> 224 us (1.24)
  starting transfers between devices: 38.5 us -> 79.5 us
  waiting for transfers between devices: 62.2 us -> 53.5 us
  matrix products: 44.2 us -> 52.1 us
  local copies, waits for them, and re-layouts: 15.3 us -> 18.8 us
    ppermute x12 -> x24, starting transfers between devices: 28 us -> 65.4 us  [halo(): piece = lax.ppermute(piece, axes, pairs)]
    all_gather x1, waiting for transfers between devices: 13.8 us -> 0.01 us  [on_device(): row_tables = lax.all_gather(memory_local, 'gx', axis=0, tiled=True)]
    ppermute x12 -> x24, waiting for transfers between devices: 14.9 us -> 25.3 us  [halo(): piece = lax.ppermute(piece, axes, pairs)]
    dot_general x9, matrix products: 8.41 us -> 17.5 us  [key_grads(): jnp.einsum('abhqk,abqhe->abkhe', grad_score, query_heads, preferred_eleme...]
    unnamed x164 -> x180, local copies, waits for them, and re-layouts: 3.75 us -> 5.69 us
  transfers between devices with their start and end apart: 21 -> 33, of which waited for: 14 -> 12; matrix products, arithmetic and copies ran while one was open for 10% -> 7% of each run, Pallas kernels for 0% -> 0%
where the time goes in v5:
time: 224 us; the launch traced here: 223 us
  starting transfers between devices  79.5 us (35%)
  waiting for transfers between devices  53.5 us (24%)
  matrix products  52.1 us (23%)
  local copies, waits for them, and re-layouts  18.8 us (8%)
  between operations  16.1 us (7%)
  other arithmetic  2.6 us (1%)
    ppermute x24, starting transfers between devices, halo(): piece = lax.ppermute(piece, axes, pairs)  65.4 us
    ppermute x24, waiting for transfers between devices, halo(): piece = lax.ppermute(piece, axes, pairs)  25.3 us
    dot_general x9, matrix products, key_grads(): jnp.einsum('abhqk,abqhe->abkhe', grad_score, query_heads, preferred_eleme...  17.5 us
    dot_general x10, matrix products, query_grads(): jnp.einsum('abhqk,abkhe->abqhe', grad_score, split_heads(key_part), prefe...  13.1 us
    ppermute x3, waiting for transfers between devices, tree_sum(): joined = keep + lax.ppermute(send, axis, pairs)  11.4 us
    ppermute x2, waiting for transfers between devices, tree_sum(): joined = joined + lax.ppermute(joined, axis, pairs)  8.49 us
    ppermute x3, waiting for transfers between devices, doubling_gather(): got = lax.ppermute(joined, axis, pairs)  8.23 us
    ppermute x3, starting transfers between devices, tree_sum(): joined = keep + lax.ppermute(send, axis, pairs)  6.85 us
  transfers between devices with their start and end apart: 33, of which 12 were waited for; matrix products, arithmetic and copies ran while one was open for 7% of the time, Pallas kernels for 0%

profile of v5, /device:TPU:0, one launch (start us, length us, event | category | flops | bytes accessed | tf_op | source)
XLA Modules:
  0.0 222.7 jit_solution(2568769092520231509)
XLA Ops:
  9.3 4.3 %collective-permute-start = (bf16[8,8,512]{2,1,0:T(8,128)(2,1)S(1)}, bf16[8,8,512]{2,1,0:T(8,128)(2,1)S(1)}, u32[]{:S(2)}, u32[]{:S(2)}) collective-permute-start(bf16[8,8,512]{2,1,0:T(8,128)(2,1)S(1)} %get-tuple-element.71), channel_id=1, source_target_pairs={{0,5},{1,6},{2,7},{4,9},{5,10},{6,11},{8,13},{9,14},{10,15},{12,17... | collective-permute-start | bytes 196616 | tf_op jit(solution)/shard_map/ppermute | solution.py:49
  14.9 1.3 collective-permute-start.7
  19.9 9.0 %collective-permute-start.3 = (bf16[16,8,512]{2,1,0:T(8,128)(2,1)S(1)}, bf16[16,8,512]{2,1,0:T(8,128)(2,1)S(1)}, u32[]{:S(2)}, u32[]{:S(2)}) collective-permute-start(bf16[16,8,512]{2,1,0:T(8,128)(2,1)S(1)} %get-tuple-element.77), channel_id=1, source_target_pairs={{0,1},{1,2},{2,3},{4,5},{5,6},{6,7},{8,9},{9,10},{10,11},{12,13},{... | collective-permute-start | bytes 393224 | tf_op jit(solution)/shard_map/ppermute | solution.py:49
  29.0 1.3 collective-permute-start.4
  30.3 5.0 %collective-permute-start.1 = (bf16[8,16,512]{2,1,0:T(8,128)(2,1)S(1)}, bf16[8,16,512]{2,1,0:T(8,128)(2,1)S(1)}, u32[]{:S(2)}, u32[]{:S(2)}) collective-permute-start(bf16[8,16,512]{2,1,0:T(8,128)(2,1)S(1)} %bitcast.507), channel_id=1, source_target_pairs={{0,4},{1,5},{2,6},{3,7},{4,8},{5,9},{6,10},{7,11},{8,12},{9,13},{1... | collective-permute-start | bytes 393224 | tf_op jit(solution)/shard_map/ppermute | solution.py:49
  35.3 1.3 collective-permute-start.6
  37.7 1.3 collective-permute-start.15
  39.0 16.4 %collective-permute-done.15 = bf16[8,8,512]{2,1,0:T(8,128)(2,1)S(1)} collective-permute-done((bf16[8,8,512]{2,1,0:T(8,128)(2,1)S(1)}, bf16[8,8,512]{2,1,0:T(8,128)(2,1)S(1)}, u32[]{:S(2)}, u32[]{:S(2)}) %collective-permute-start.15) | collective-permute-done | bytes 65568 | tf_op jit(solution)/shard_map/ppermute | solution.py:49
  55.4 7.3 %collective-permute-start.8 = (bf16[8,8,512]{2,1,0:T(8,128)(2,1)S(1)}, bf16[8,8,512]{2,1,0:T(8,128)(2,1)S(1)}, u32[]{:S(2)}, u32[]{:S(2)}) collective-permute-start(bf16[8,8,512]{2,1,0:T(8,128)(2,1)S(1)} %get-tuple-element.63), channel_id=1, source_target_pairs={{0,5},{1,6},{2,7},{4,9},{5,10},{6,11},{8,13},{9,14},{10,15},{12,17... | collective-permute-start | bytes 196616 | tf_op jit(solution)/shard_map/ppermute | solution.py:49
  62.7 3.9 %collective-permute-start.11 = (bf16[16,8,512]{2,1,0:T(8,128)(2,1)S(1)}, bf16[16,8,512]{2,1,0:T(8,128)(2,1)S(1)}, u32[]{:S(2)}, u32[]{:S(2)}) collective-permute-start(bf16[16,8,512]{2,1,0:T(8,128)(2,1)S(1)} %get-tuple-element.69), channel_id=1, source_target_pairs={{0,1},{1,2},{2,3},{4,5},{5,6},{6,7},{8,9},{9,10},{10,11},{12,13},{... | collective-permute-start | bytes 393224 | tf_op jit(solution)/shard_map/ppermute | solution.py:49
  69.3 4.6 %collective-permute-start.9 = (bf16[8,16,512]{2,1,0:T(8,128)(2,1)S(1)}, bf16[8,16,512]{2,1,0:T(8,128)(2,1)S(1)}, u32[]{:S(2)}, u32[]{:S(2)}) collective-permute-start(bf16[8,16,512]{2,1,0:T(8,128)(2,1)S(1)} %get-tuple-element.67), channel_id=1, source_target_pairs={{0,4},{1,5},{2,6},{3,7},{4,8},{5,9},{6,10},{7,11},{8,12},{9,13},{1... | collective-permute-start | bytes 393224 | tf_op jit(solution)/shard_map/ppermute | solution.py:49
  74.1 2.0 collective-permute-done.14
  76.1 3.4 %collective-permute-done.9 = bf16[8,16,512]{2,1,0:T(8,128)(2,1)S(1)} collective-permute-done((bf16[8,16,512]{2,1,0:T(8,128)(2,1)S(1)}, bf16[8,16,512]{2,1,0:T(8,128)(2,1)S(1)}, u32[]{:S(2)}, u32[]{:S(2)}) %collective-permute-start.9) | collective-permute-done | bytes 131104 | tf_op jit(solution)/shard_map/ppermute | solution.py:49
  87.0 1.5 slice_bitcast_fusion
  88.5 2.2 gather_fusion
  98.2 2.1 fusion.84
  102.5 2.2 convolution_add_fusion.24
  104.7 2.2 convolution_add_fusion.23
  106.9 1.4 convolution_add_fusion.22
  108.4 1.3 convolution_add_fusion.21
  109.7 1.3 convolution_add_fusion.20
  111.1 1.3 convolution_add_fusion.19
  115.0 4.1 %collective-permute-start.16 = (f32[8,8,4]{1,0,2:T(8,128)S(1)}, f32[8,8,4]{1,0,2:T(8,128)S(1)}, u32[]{:S(2)}, u32[]{:S(2)}) collective-permute-start(f32[8,8,4]{1,0,2:T(8,128)S(1)} %copy-done.67), channel_id=1, source_target_pairs={{0,5},{1,6},{2,7},{4,9},{5,10},{6,11},{8,13},{9,14},{10,15},{12,17... | collective-permute-start | bytes 3080 | tf_op jit(solution)/shard_map/ppermute | solution.py:49
  120.5 4.1 %collective-permute-start.19 = (f32[16,8,4]{1,0,2:T(8,128)S(1)}, f32[16,8,4]{1,0,2:T(8,128)S(1)}, u32[]{:S(2)}, u32[]{:S(2)}) collective-permute-start(f32[16,8,4]{1,0,2:T(8,128)S(1)} %copy-done.63), channel_id=1, source_target_pairs={{0,1},{1,2},{2,3},{4,5},{5,6},{6,7},{8,9},{9,10},{10,11},{12,13},{... | collective-permute-start | bytes 6152 | tf_op jit(solution)/shard_map/ppermute | solution.py:49
  127.7 7.4 %collective-permute-start.17 = (f32[8,16,4]{1,0,2:T(8,128)S(1)}, f32[8,16,4]{1,0,2:T(8,128)S(1)}, u32[]{:S(2)}, u32[]{:S(2)}) collective-permute-start(f32[8,16,4]{1,0,2:T(8,128)S(1)} %slice.458), channel_id=1, source_target_pairs={{0,4},{1,5},{2,6},{3,7},{4,8},{5,9},{6,10},{7,11},{8,12},{9,13},{1... | collective-permute-start | bytes 6152 | tf_op jit(solution)/shard_map/ppermute | solution.py:49
  135.1 1.5 collective-permute-start.22
  137.6 3.5 %collective-permute-done.22 = f32[8,16,4]{1,0,2:T(8,128)S(1)} collective-permute-done((f32[8,16,4]{1,0,2:T(8,128)S(1)}, f32[8,16,4]{1,0,2:T(8,128)S(1)}, u32[]{:S(2)}, u32[]{:S(2)}) %collective-permute-start.22) | collective-permute-done | bytes 2080 | tf_op jit(solution)/shard_map/ppermute | solution.py:49
  145.7 2.1 convolution_add_fusion.15
  147.8 2.1 convolution_add_fusion.14
  149.9 2.1 convolution_add_fusion.13
  151.9 2.1 convolution_add_fusion.12
  154.0 2.0 convolution_add_fusion.11
  156.1 2.0 convolution_add_fusion.10
  158.1 2.0 convolution_add_fusion.9
  160.2 2.0 fusion.81
  170.3 1.5 collective-permute-done.24
  171.9 3.2 %collective-permute-start.25 = (f32[256,256]{1,0:T(8,128)S(1)}, f32[256,256]{1,0:T(8,128)S(1)}, u32[]{:S(2)}, u32[]{:S(2)}) collective-permute-start(f32[256,256]{1,0:T(8,128)S(1)} %constant_dynamic-slice_fusion.1), channel_id=1, source_target_pairs={{0,2},{1,3},{2,0},{3,1},{4,6},{5,7},{6,4},{7,5},{8,10},{9,11},{10,... | collective-permute-start | bytes 786440 | tf_op jit(solution)/shard_map/ppermute | solution.py:246
  175.1 6.6 %collective-permute-done.25 = f32[256,256]{1,0:T(8,128)S(1)} collective-permute-done((f32[256,256]{1,0:T(8,128)S(1)}, f32[256,256]{1,0:T(8,128)S(1)}, u32[]{:S(2)}, u32[]{:S(2)}) %collective-permute-start.25) | collective-permute-done | bytes 262176 | tf_op jit(solution)/shard_map/ppermute | solution.py:246
  181.8 3.0 %collective-permute-start.26 = (f32[128,256]{1,0:T(8,128)S(1)}, f32[128,256]{1,0:T(8,128)S(1)}, u32[]{:S(2)}, u32[]{:S(2)}) collective-permute-start(f32[128,256]{1,0:T(8,128)S(1)} %constant_dynamic-slice_fusion), channel_id=1, source_target_pairs={{0,4},{4,0},{8,12},{12,8},{16,20},{20,16},{24,28},{28,24},{1,5},{5... | collective-permute-start | bytes 393224 | tf_op jit(solution)/shard_map/ppermute | solution.py:246
  184.8 3.3 %collective-permute-done.26 = f32[128,256]{1,0:T(8,128)S(1)} collective-permute-done((f32[128,256]{1,0:T(8,128)S(1)}, f32[128,256]{1,0:T(8,128)S(1)}, u32[]{:S(2)}, u32[]{:S(2)}) %collective-permute-start.26) | collective-permute-done | bytes 131104 | tf_op jit(solution)/shard_map/ppermute | solution.py:246
  188.1 1.5 collective-permute-start.27
  189.6 3.5 %collective-permute-done.27 = f32[128,256]{1,0:T(8,128)S(1)} collective-permute-done((f32[128,256]{1,0:T(8,128)S(1)}, f32[128,256]{1,0:T(8,128)S(1)}, u32[]{:S(2)}, u32[]{:S(2)}) %collective-permute-start.27) | collective-permute-done | bytes 131104 | tf_op jit(solution)/shard_map/ppermute | solution.py:249
  193.2 2.4 %collective-permute-start.28 = (f32[128,256]{1,0:T(8,128)S(1)}, f32[128,256]{1,0:T(8,128)S(1)}, u32[]{:S(2)}, u32[]{:S(2)}) collective-permute-start(f32[128,256]{1,0:T(8,128)S(1)} %add.391), channel_id=1, source_target_pairs={{0,16},{4,20},{8,24},{12,28},{16,0},{20,4},{24,8},{28,12},{1,17},{... | collective-permute-start | bytes 393224 | tf_op jit(solution)/shard_map/ppermute | solution.py:249
  195.5 5.0 %collective-permute-done.28 = f32[128,256]{1,0:T(8,128)S(1)} collective-permute-done((f32[128,256]{1,0:T(8,128)S(1)}, f32[128,256]{1,0:T(8,128)S(1)}, u32[]{:S(2)}, u32[]{:S(2)}) %collective-permute-start.28) | collective-permute-done | bytes 131104 | tf_op jit(solution)/shard_map/ppermute | solution.py:249
  200.5 1.8 collective-permute-start.29
  202.3 3.2 %collective-permute-done.29 = f32[128,256]{1,0:T(8,128)S(1)} collective-permute-done((f32[128,256]{1,0:T(8,128)S(1)}, f32[128,256]{1,0:T(8,128)S(1)}, u32[]{:S(2)}, u32[]{:S(2)}) %collective-permute-start.29) | collective-permute-done | bytes 131104 | tf_op jit(solution)/shard_map/ppermute | solution.py:211
  205.6 1.5 collective-permute-start.30
  207.1 4.9 %collective-permute-done.30 = f32[256,256]{1,0:T(8,128)S(1)} collective-permute-done((f32[256,256]{1,0:T(8,128)S(1)}, f32[256,256]{1,0:T(8,128)S(1)}, u32[]{:S(2)}, u32[]{:S(2)}) %collective-permute-start.30) | collective-permute-done | bytes 262176 | tf_op jit(solution)/shard_map/ppermute | solution.py:211
  (345 shorter events, 51.6 us)
Async XLA Ops:
  7.2 81.3 %all-gather.3.cloned.1.call-start = ((), (), s32[]{:S(2)}) async-start(), calls=%async_computation | async-start | bytes 2359296 | tf_op jit(solution)/shard_map/all_gather | solution.py:285
  9.3 10.6 %collective-permute-start = (bf16[8,8,512]{2,1,0:T(8,128)(2,1)S(1)}, bf16[8,8,512]{2,1,0:T(8,128)(2,1)S(1)}, u32[]{:S(2)}, u32[]{:S(2)}) collective-permute-start(bf16[8,8,512]{2,1,0:T(8,128)(2,1)S(1)} %get-tuple-element.71), channel_id=1, source_target_pairs={{0,5},{1,6},{2,7},{4,9},{5,10},{6,11},{8,13},{9,14},{10,15},{12,17... | collective-permute-start | bytes 196616 | tf_op jit(solution)/shard_map/ppermute | solution.py:49
  13.6 15.4 %collective-permute-start.2 = (bf16[8,8,512]{2,1,0:T(8,128)(2,1)S(1)}, bf16[8,8,512]{2,1,0:T(8,128)(2,1)S(1)}, u32[]{:S(2)}, u32[]{:S(2)}) collective-permute-start(bf16[8,8,512]{2,1,0:T(8,128)(2,1)S(1)} %get-tuple-element.74), channel_id=1, source_target_pairs={{1,4},{2,5},{3,6},{5,8},{6,9},{7,10},{9,12},{10,13},{11,14},{13,16... | collective-permute-start | bytes 196616 | tf_op jit(solution)/shard_map/ppermute | solution.py:49
  14.3 16.0 %collective-permute-start.5 = (bf16[8,8,512]{2,1,0:T(8,128)(2,1)S(1)}, bf16[8,8,512]{2,1,0:T(8,128)(2,1)S(1)}, u32[]{:S(2)}, u32[]{:S(2)}) collective-permute-start(bf16[8,8,512]{2,1,0:T(8,128)(2,1)S(1)} %get-tuple-element.73), channel_id=1, source_target_pairs={{4,1},{5,2},{6,3},{8,5},{9,6},{10,7},{12,9},{13,10},{14,11},{16,13... | collective-permute-start | bytes 196616 | tf_op jit(solution)/shard_map/ppermute | solution.py:49
  14.9 20.3 %collective-permute-start.7 = (bf16[8,8,512]{2,1,0:T(8,128)(2,1)S(1)}, bf16[8,8,512]{2,1,0:T(8,128)(2,1)S(1)}, u32[]{:S(2)}, u32[]{:S(2)}) collective-permute-start(bf16[8,8,512]{2,1,0:T(8,128)(2,1)S(1)} %get-tuple-element.72), channel_id=1, source_target_pairs={{5,0},{6,1},{7,2},{9,4},{10,5},{11,6},{13,8},{14,9},{15,10},{17,12... | collective-permute-start | bytes 196616 | tf_op jit(solution)/shard_map/ppermute | solution.py:49
  18.6 18.0 %collective-permute-start.10 = (bf16[8,8,512]{2,1,0:T(8,128)(2,1)S(1)}, bf16[8,8,512]{2,1,0:T(8,128)(2,1)S(1)}, u32[]{:S(2)}, u32[]{:S(2)}) collective-permute-start(bf16[8,8,512]{2,1,0:T(8,128)(2,1)S(1)} %get-tuple-element.64), channel_id=1, source_target_pairs={{1,4},{2,5},{3,6},{5,8},{6,9},{7,10},{9,12},{10,13},{11,14},{13,16... | collective-permute-start | bytes 196616 | tf_op jit(solution)/shard_map/ppermute | solution.py:49
  19.7 61.3 %copy-start.79 = (pred[2,2]{1,0:T(4,128)(4,1)}, pred[2,2]{1,0:T(4,128)(4,1)S(1)}, u32[]{:S(2)}) copy-start(pred[2,2]{1,0:T(4,128)(4,1)S(1)} %get-tuple-element.110) | copy-start | bytes 16
  19.7 61.8 %copy-start.71 = (pred[2,2]{1,0:T(4,128)(4,1)}, pred[2,2]{1,0:T(4,128)(4,1)S(1)}, u32[]{:S(2)}) copy-start(pred[2,2]{1,0:T(4,128)(4,1)S(1)} %get-tuple-element.106) | copy-start | bytes 16
  19.7 62.1 %copy-start.73 = (pred[2,2]{1,0:T(4,128)(4,1)}, pred[2,2]{1,0:T(4,128)(4,1)S(1)}, u32[]{:S(2)}) copy-start(pred[2,2]{1,0:T(4,128)(4,1)S(1)} %get-tuple-element.107) | copy-start | bytes 16
  19.7 62.3 %copy-start.75 = (pred[2,2]{1,0:T(4,128)(4,1)}, pred[2,2]{1,0:T(4,128)(4,1)S(1)}, u32[]{:S(2)}) copy-start(pred[2,2]{1,0:T(4,128)(4,1)S(1)} %get-tuple-element.108) | copy-start | bytes 16
  19.7 63.1 %copy-start.77 = (pred[2,2]{1,0:T(4,128)(4,1)}, pred[2,2]{1,0:T(4,128)(4,1)S(1)}, u32[]{:S(2)}) copy-start(pred[2,2]{1,0:T(4,128)(4,1)S(1)} %get-tuple-element.109) | copy-start | bytes 16
  19.7 63.9 %copy-start.81 = (pred[2,2]{1,0:T(4,128)(4,1)}, pred[2,2]{1,0:T(4,128)(4,1)S(1)}, u32[]{:S(2)}) copy-start(pred[2,2]{1,0:T(4,128)(4,1)S(1)} %get-tuple-element.111) | copy-start | bytes 16
  19.7 64.7 %copy-start.83 = (pred[2,2]{1,0:T(4,128)(4,1)}, pred[2,2]{1,0:T(4,128)(4,1)S(1)}, u32[]{:S(2)}) copy-start(pred[2,2]{1,0:T(4,128)(4,1)S(1)} %get-tuple-element.112) | copy-start | bytes 16
  19.8 65.5 %copy-start.85 = (pred[2,2]{1,0:T(4,128)(4,1)}, pred[2,2]{1,0:T(4,128)(4,1)S(1)}, u32[]{:S(2)}) copy-start(pred[2,2]{1,0:T(4,128)(4,1)S(1)} %get-tuple-element.105) | copy-start | bytes 16
  19.8 66.4 %copy-start.87 = (pred[2,2]{1,0:T(4,128)(4,1)}, pred[2,2]{1,0:T(4,128)(4,1)S(1)}, u32[]{:S(2)}) copy-start(pred[2,2]{1,0:T(4,128)(4,1)S(1)} %get-tuple-element.113) | copy-start | bytes 16
  19.9 42.8 %collective-permute-start.3 = (bf16[16,8,512]{2,1,0:T(8,128)(2,1)S(1)}, bf16[16,8,512]{2,1,0:T(8,128)(2,1)S(1)}, u32[]{:S(2)}, u32[]{:S(2)}) collective-permute-start(bf16[16,8,512]{2,1,0:T(8,128)(2,1)S(1)} %get-tuple-element.77), channel_id=1, source_target_pairs={{0,1},{1,2},{2,3},{4,5},{5,6},{6,7},{8,9},{9,10},{10,11},{12,13},{... | collective-permute-start | bytes 393224 | tf_op jit(solution)/shard_map/ppermute | solution.py:49
  29.0 37.7 %collective-permute-start.4 = (bf16[16,8,512]{2,1,0:T(8,128)(2,1)S(1)}, bf16[16,8,512]{2,1,0:T(8,128)(2,1)S(1)}, u32[]{:S(2)}, u32[]{:S(2)}) collective-permute-start(bf16[16,8,512]{2,1,0:T(8,128)(2,1)S(1)} %get-tuple-element.78), channel_id=1, source_target_pairs={{1,0},{2,1},{3,2},{5,4},{6,5},{7,6},{9,8},{10,9},{11,10},{13,12},{... | collective-permute-start | bytes 393224 | tf_op jit(solution)/shard_map/ppermute | solution.py:49
  30.3 37.7 %collective-permute-start.1 = (bf16[8,16,512]{2,1,0:T(8,128)(2,1)S(1)}, bf16[8,16,512]{2,1,0:T(8,128)(2,1)S(1)}, u32[]{:S(2)}, u32[]{:S(2)}) collective-permute-start(bf16[8,16,512]{2,1,0:T(8,128)(2,1)S(1)} %bitcast.507), channel_id=1, source_target_pairs={{0,4},{1,5},{2,6},{3,7},{4,8},{5,9},{6,10},{7,11},{8,12},{9,13},{1... | collective-permute-start | bytes 393224 | tf_op jit(solution)/shard_map/ppermute | solution.py:49
  35.3 34.0 %collective-permute-start.6 = (bf16[8,16,512]{2,1,0:T(8,128)(2,1)S(1)}, bf16[8,16,512]{2,1,0:T(8,128)(2,1)S(1)}, u32[]{:S(2)}, u32[]{:S(2)}) collective-permute-start(bf16[8,16,512]{2,1,0:T(8,128)(2,1)S(1)} %bitcast.506), channel_id=1, source_target_pairs={{4,0},{5,1},{6,2},{7,3},{8,4},{9,5},{10,6},{11,7},{12,8},{13,9},{1... | collective-permute-start | bytes 393224 | tf_op jit(solution)/shard_map/ppermute | solution.py:49
  36.6 1.1 collective-permute-start.13
  37.7 17.7 %collective-permute-start.15 = (bf16[8,8,512]{2,1,0:T(8,128)(2,1)S(1)}, bf16[8,8,512]{2,1,0:T(8,128)(2,1)S(1)}, u32[]{:S(2)}, u32[]{:S(2)}) collective-permute-start(bf16[8,8,512]{2,1,0:T(8,128)(2,1)S(1)} %get-tuple-element.66), channel_id=1, source_target_pairs={{5,0},{6,1},{7,2},{9,4},{10,5},{11,6},{13,8},{14,9},{15,10},{17,12... | collective-permute-start | bytes 196616 | tf_op jit(solution)/shard_map/ppermute | solution.py:49
  55.4 18.7 %collective-permute-start.8 = (bf16[8,8,512]{2,1,0:T(8,128)(2,1)S(1)}, bf16[8,8,512]{2,1,0:T(8,128)(2,1)S(1)}, u32[]{:S(2)}, u32[]{:S(2)}) collective-permute-start(bf16[8,8,512]{2,1,0:T(8,128)(2,1)S(1)} %get-tuple-element.63), channel_id=1, source_target_pairs={{0,5},{1,6},{2,7},{4,9},{5,10},{6,11},{8,13},{9,14},{10,15},{12,17... | collective-permute-start | bytes 196616 | tf_op jit(solution)/shard_map/ppermute | solution.py:49
  62.7 11.3 %collective-permute-start.11 = (bf16[16,8,512]{2,1,0:T(8,128)(2,1)S(1)}, bf16[16,8,512]{2,1,0:T(8,128)(2,1)S(1)}, u32[]{:S(2)}, u32[]{:S(2)}) collective-permute-start(bf16[16,8,512]{2,1,0:T(8,128)(2,1)S(1)} %get-tuple-element.69), channel_id=1, source_target_pairs={{0,1},{1,2},{2,3},{4,5},{5,6},{6,7},{8,9},{9,10},{10,11},{12,13},{... | collective-permute-start | bytes 393224 | tf_op jit(solution)/shard_map/ppermute | solution.py:49
  66.7 7.4 %collective-permute-start.12 = (bf16[16,8,512]{2,1,0:T(8,128)(2,1)S(1)}, bf16[16,8,512]{2,1,0:T(8,128)(2,1)S(1)}, u32[]{:S(2)}, u32[]{:S(2)}) collective-permute-start(bf16[16,8,512]{2,1,0:T(8,128)(2,1)S(1)} %get-tuple-element.70), channel_id=1, source_target_pairs={{1,0},{2,1},{3,2},{5,4},{6,5},{7,6},{9,8},{10,9},{11,10},{13,12},{... | collective-permute-start | bytes 393224 | tf_op jit(solution)/shard_map/ppermute | solution.py:49
  68.0 8.1 %collective-permute-start.14 = (bf16[8,16,512]{2,1,0:T(8,128)(2,1)S(1)}, bf16[8,16,512]{2,1,0:T(8,128)(2,1)S(1)}, u32[]{:S(2)}, u32[]{:S(2)}) collective-permute-start(bf16[8,16,512]{2,1,0:T(8,128)(2,1)S(1)} %get-tuple-element.68), channel_id=1, source_target_pairs={{4,0},{5,1},{6,2},{7,3},{8,4},{9,5},{10,6},{11,7},{12,8},{13,9},{1... | collective-permute-start | bytes 393224 | tf_op jit(solution)/shard_map/ppermute | solution.py:49
  69.3 10.2 %collective-permute-start.9 = (bf16[8,16,512]{2,1,0:T(8,128)(2,1)S(1)}, bf16[8,16,512]{2,1,0:T(8,128)(2,1)S(1)}, u32[]{:S(2)}, u32[]{:S(2)}) collective-permute-start(bf16[8,16,512]{2,1,0:T(8,128)(2,1)S(1)} %get-tuple-element.67), channel_id=1, source_target_pairs={{0,4},{1,5},{2,6},{3,7},{4,8},{5,9},{6,10},{7,11},{8,12},{9,13},{1... | collective-permute-start | bytes 393224 | tf_op jit(solution)/shard_map/ppermute | solution.py:49
  113.3 27.8 %copy-start.23 = (f32[16,16,4]{1,0,2:T(8,128)S(1)}, f32[16,16,4]{1,0,2:T(8,128)}, u32[]{:S(2)}) copy-start(f32[16,16,4]{1,0,2:T(8,128)} %copy-done.22) | copy-start | bytes 12292
  113.9 28.3 %copy-start.33 = (bf16[2,2,8,2,8,128]{5,4,3,2,1,0:T(8,128)(2,1)S(1)}, bf16[2,2,8,2,8,128]{5,4,3,2,1,0:T(8,128)(2,1)}, u32[]{:S(2)}) copy-start(bf16[2,2,8,2,8,128]{5,4,3,2,1,0:T(8,128)(2,1)} %copy-done.32) | copy-start | bytes 393220
  113.9 28.3 %copy-start.41 = (bf16[2,2,8,2,8,128]{5,4,3,2,1,0:T(8,128)(2,1)S(1)}, bf16[2,2,8,2,8,128]{5,4,3,2,1,0:T(8,128)(2,1)}, u32[]{:S(2)}) copy-start(bf16[2,2,8,2,8,128]{5,4,3,2,1,0:T(8,128)(2,1)} %get-tuple-element.34) | copy-start | bytes 393220
  113.9 28.3 %copy-start.88 = (pred[2,2]{1,0:T(4,128)(4,1)S(1)}, pred[2,2]{1,0:T(4,128)(4,1)}, u32[]{:S(2)}) copy-start(pred[2,2]{1,0:T(4,128)(4,1)} %copy-done.87) | copy-start | bytes 16
  114.1 28.4 %copy-start.8 = (bf16[2,2,8,2,8,128]{5,4,3,2,1,0:T(8,128)(2,1)S(1)}, bf16[2,2,8,2,8,128]{5,4,3,2,1,0:T(8,128)(2,1)}, u32[]{:S(2)}) copy-start(bf16[2,2,8,2,8,128]{5,4,3,2,1,0:T(8,128)(2,1)} %get-tuple-element.33) | copy-start | bytes 393220
  115.0 11.4 %collective-permute-start.16 = (f32[8,8,4]{1,0,2:T(8,128)S(1)}, f32[8,8,4]{1,0,2:T(8,128)S(1)}, u32[]{:S(2)}, u32[]{:S(2)}) collective-permute-start(f32[8,8,4]{1,0,2:T(8,128)S(1)} %copy-done.67), channel_id=1, source_target_pairs={{0,5},{1,6},{2,7},{4,9},{5,10},{6,11},{8,13},{9,14},{10,15},{12,17... | collective-permute-start | bytes 3080 | tf_op jit(solution)/shard_map/ppermute | solution.py:49
  119.1 8.6 %collective-permute-start.18 = (f32[8,8,4]{1,0,2:T(8,128)S(1)}, f32[8,8,4]{1,0,2:T(8,128)S(1)}, u32[]{:S(2)}, u32[]{:S(2)}) collective-permute-start(f32[8,8,4]{1,0,2:T(8,128)S(1)} %copy-done.66), channel_id=1, source_target_pairs={{1,4},{2,5},{3,6},{5,8},{6,9},{7,10},{9,12},{10,13},{11,14},{13,16... | collective-permute-start | bytes 3080 | tf_op jit(solution)/shard_map/ppermute | solution.py:49
  119.8 15.3 %collective-permute-start.21 = (f32[8,8,4]{1,0,2:T(8,128)S(1)}, f32[8,8,4]{1,0,2:T(8,128)S(1)}, u32[]{:S(2)}, u32[]{:S(2)}) collective-permute-start(f32[8,8,4]{1,0,2:T(8,128)S(1)} %copy-done.65), channel_id=1, source_target_pairs={{4,1},{5,2},{6,3},{8,5},{9,6},{10,7},{12,9},{13,10},{14,11},{16,13... | collective-permute-start | bytes 3080 | tf_op jit(solution)/shard_map/ppermute | solution.py:49
  120.5 17.1 %collective-permute-start.19 = (f32[16,8,4]{1,0,2:T(8,128)S(1)}, f32[16,8,4]{1,0,2:T(8,128)S(1)}, u32[]{:S(2)}, u32[]{:S(2)}) collective-permute-start(f32[16,8,4]{1,0,2:T(8,128)S(1)} %copy-done.63), channel_id=1, source_target_pairs={{0,1},{1,2},{2,3},{4,5},{5,6},{6,7},{8,9},{9,10},{10,11},{12,13},{... | collective-permute-start | bytes 6152 | tf_op jit(solution)/shard_map/ppermute | solution.py:49
  124.6 13.0 %collective-permute-start.20 = (f32[16,8,4]{1,0,2:T(8,128)S(1)}, f32[16,8,4]{1,0,2:T(8,128)S(1)}, u32[]{:S(2)}, u32[]{:S(2)}) collective-permute-start(f32[16,8,4]{1,0,2:T(8,128)S(1)} %copy-done.62), channel_id=1, source_target_pairs={{1,0},{2,1},{3,2},{5,4},{6,5},{7,6},{9,8},{10,9},{11,10},{13,12},{... | collective-permute-start | bytes 6152 | tf_op jit(solution)/shard_map/ppermute | solution.py:49
  126.4 11.2 %collective-permute-start.23 = (f32[8,8,4]{1,0,2:T(8,128)S(1)}, f32[8,8,4]{1,0,2:T(8,128)S(1)}, u32[]{:S(2)}, u32[]{:S(2)}) collective-permute-start(f32[8,8,4]{1,0,2:T(8,128)S(1)} %copy-done.64), channel_id=1, source_target_pairs={{5,0},{6,1},{7,2},{9,4},{10,5},{11,6},{13,8},{14,9},{15,10},{17,12... | collective-permute-start | bytes 3080 | tf_op jit(solution)/shard_map/ppermute | solution.py:49
  127.7 9.9 %collective-permute-start.17 = (f32[8,16,4]{1,0,2:T(8,128)S(1)}, f32[8,16,4]{1,0,2:T(8,128)S(1)}, u32[]{:S(2)}, u32[]{:S(2)}) collective-permute-start(f32[8,16,4]{1,0,2:T(8,128)S(1)} %slice.458), channel_id=1, source_target_pairs={{0,4},{1,5},{2,6},{3,7},{4,8},{5,9},{6,10},{7,11},{8,12},{9,13},{1... | collective-permute-start | bytes 6152 | tf_op jit(solution)/shard_map/ppermute | solution.py:49
  135.1 6.0 %collective-permute-start.22 = (f32[8,16,4]{1,0,2:T(8,128)S(1)}, f32[8,16,4]{1,0,2:T(8,128)S(1)}, u32[]{:S(2)}, u32[]{:S(2)}) collective-permute-start(f32[8,16,4]{1,0,2:T(8,128)S(1)} %slice.464), channel_id=1, source_target_pairs={{4,0},{5,1},{6,2},{7,3},{8,4},{9,5},{10,6},{11,7},{12,8},{13,9},{1... | collective-permute-start | bytes 6152 | tf_op jit(solution)/shard_map/ppermute | solution.py:49
  169.6 2.2 collective-permute-start.24
  171.9 9.8 %collective-permute-start.25 = (f32[256,256]{1,0:T(8,128)S(1)}, f32[256,256]{1,0:T(8,128)S(1)}, u32[]{:S(2)}, u32[]{:S(2)}) collective-permute-start(f32[256,256]{1,0:T(8,128)S(1)} %constant_dynamic-slice_fusion.1), channel_id=1, source_target_pairs={{0,2},{1,3},{2,0},{3,1},{4,6},{5,7},{6,4},{7,5},{8,10},{9,11},{10,... | collective-permute-start | bytes 786440 | tf_op jit(solution)/shard_map/ppermute | solution.py:246
  181.8 6.3 %collective-permute-start.26 = (f32[128,256]{1,0:T(8,128)S(1)}, f32[128,256]{1,0:T(8,128)S(1)}, u32[]{:S(2)}, u32[]{:S(2)}) collective-permute-start(f32[128,256]{1,0:T(8,128)S(1)} %constant_dynamic-slice_fusion), channel_id=1, source_target_pairs={{0,4},{4,0},{8,12},{12,8},{16,20},{20,16},{24,28},{28,24},{1,5},{5... | collective-permute-start | bytes 393224 | tf_op jit(solution)/shard_map/ppermute | solution.py:246
  184.7 27.5 %copy-start.31 = (bf16[256,256]{1,0:T(8,128)(2,1)S(1)}, bf16[256,256]{1,0:T(8,128)(2,1)}, u32[]{:S(2)}) copy-start(bf16[256,256]{1,0:T(8,128)(2,1)} %param.13) | copy-start | bytes 393220
  188.1 5.0 %collective-permute-start.27 = (f32[128,256]{1,0:T(8,128)S(1)}, f32[128,256]{1,0:T(8,128)S(1)}, u32[]{:S(2)}, u32[]{:S(2)}) collective-permute-start(f32[128,256]{1,0:T(8,128)S(1)} %dynamic-slice_add_fusion.2), channel_id=1, source_target_pairs={{0,8},{4,12},{8,0},{12,4},{16,24},{20,28},{24,16},{28,20},{1,9},{5... | collective-permute-start | bytes 393224 | tf_op jit(solution)/shard_map/ppermute | solution.py:249
  193.2 7.3 %collective-permute-start.28 = (f32[128,256]{1,0:T(8,128)S(1)}, f32[128,256]{1,0:T(8,128)S(1)}, u32[]{:S(2)}, u32[]{:S(2)}) collective-permute-start(f32[128,256]{1,0:T(8,128)S(1)} %add.391), channel_id=1, source_target_pairs={{0,16},{4,20},{8,24},{12,28},{16,0},{20,4},{24,8},{28,12},{1,17},{... | collective-permute-start | bytes 393224 | tf_op jit(solution)/shard_map/ppermute | solution.py:249
  200.5 5.0 %collective-permute-start.29 = (f32[128,256]{1,0:T(8,128)S(1)}, f32[128,256]{1,0:T(8,128)S(1)}, u32[]{:S(2)}, u32[]{:S(2)}) collective-permute-start(f32[128,256]{1,0:T(8,128)S(1)} %add.392), channel_id=1, source_target_pairs={{0,4},{4,0},{8,12},{12,8},{16,20},{20,16},{24,28},{28,24},{1,5},{5... | collective-permute-start | bytes 393224 | tf_op jit(solution)/shard_map/ppermute | solution.py:211
  205.6 6.4 %collective-permute-start.30 = (f32[256,256]{1,0:T(8,128)S(1)}, f32[256,256]{1,0:T(8,128)S(1)}, u32[]{:S(2)}, u32[]{:S(2)}) collective-permute-start(f32[256,256]{1,0:T(8,128)S(1)} %pad_maximum_fusion.2), channel_id=1, source_target_pairs={{0,2},{1,3},{2,0},{3,1},{4,6},{5,7},{6,4},{7,5},{8,10},{9,11},{10,... | collective-permute-start | bytes 786440 | tf_op jit(solution)/shard_map/ppermute | solution.py:211
  212.1 2.0 collective-permute-start.31
  (74 other events, 447.0 us)
Sparse Core Ops, SparseCore 0:
  16.4 64.4 all-gather.2

commit v6 on v4

--- a/solution.py
+++ b/solution.py
@@ -259,26 +259,9 @@
     )
     region_count = memory_local.shape[0]
     row_tables = lax.all_gather(memory_local, "gx", axis=0, tiled=True)
-    fetched = jnp.take(row_tables, owners * region_count + local_ids, axis=0)
-    region_keyval = fetched.reshape(
-        block_rows, block_cols, 2, memory_local.shape[1], memory_local.shape[2]
-    )
-    query_blocks = to_blocks(queries.reshape(tile_rows, tile_cols, model_width))
-    outputs, log_totals = attend_forward(query_blocks, keyval_pad, key_valid, region_keyval)
-    attended = from_blocks(outputs).reshape(-1, model_width)
-    layer_out = jnp.dot(attended, w_out, preferred_element_type=jnp.float32).astype(jnp.bfloat16)
     grad_flat = grad_out.reshape(-1, model_width)
     d_attended = jnp.dot(grad_flat, w_out.T, preferred_element_type=jnp.float32).astype(
         jnp.bfloat16
-    )
-    grad_out_local = inner_rows(attended, grad_flat)
-    dout_blocks = to_blocks(d_attended.reshape(tile_rows, tile_cols, model_width))
-    delta_rows = jnp.sum(
-        split_heads(dout_blocks).astype(jnp.float32) * split_heads(outputs).astype(jnp.float32), -1
-    )
-    delta_rows = delta_rows.transpose(0, 1, 3, 2)
-    d_queries = query_grads(
-        query_blocks, keyval_pad, key_valid, region_keyval, log_totals, dout_blocks, delta_rows
     )
     query_grid = jnp.concatenate(
         [
@@ -288,6 +271,24 @@
         -1,
     )
     query_halo = padded(query_grid, (("gx", 0), ("gy", 1)), BSIDE)
+    row_tables, query_halo = lax.optimization_barrier((row_tables, query_halo))
+    fetched = jnp.take(row_tables, owners * region_count + local_ids, axis=0)
+    region_keyval = fetched.reshape(
+        block_rows, block_cols, 2, memory_local.shape[1], memory_local.shape[2]
+    )
+    query_blocks = to_blocks(queries.reshape(tile_rows, tile_cols, model_width))
+    outputs, log_totals = attend_forward(query_blocks, keyval_pad, key_valid, region_keyval)
+    attended = from_blocks(outputs).reshape(-1, model_width)
+    layer_out = jnp.dot(attended, w_out, preferred_element_type=jnp.float32).astype(jnp.bfloat16)
+    grad_out_local = inner_rows(attended, grad_flat)
+    dout_blocks = to_blocks(d_attended.reshape(tile_rows, tile_cols, model_width))
+    delta_rows = jnp.sum(
+        split_heads(dout_blocks).astype(jnp.float32) * split_heads(outputs).astype(jnp.float32), -1
+    )
+    delta_rows = delta_rows.transpose(0, 1, 3, 2)
+    d_queries = query_grads(
+        query_blocks, keyval_pad, key_valid, region_keyval, log_totals, dout_blocks, delta_rows
+    )
     stat_grid = from_blocks(jnp.concatenate([log_totals, delta_rows], 2).transpose(0, 1, 3, 2))
     stat_halo = padded(stat_grid, (("gx", 0), ("gy", 1)), BSIDE)
     query_all = to_blocks(query_halo)

time: 181 us -> 189 us (1.044)
  matrix products: 44.2 us -> 56.7 us
  waiting for transfers between devices: 62.2 us -> 55.1 us
  other arithmetic: 3.61 us -> 5.82 us
    dot_general x10, matrix products: 6.21 us -> 13.3 us  [piece_scores(): jnp.einsum('abqhe,abkhe->abhqk', query_heads, split_heads(key_part), pref...]
    all_gather x1, waiting for transfers between devices: 13.8 us -> 7.96 us  [on_device(): row_tables = lax.all_gather(memory_local, 'gx', axis=0, tiled=True)]
    dot_general x10, matrix products: 13.1 us -> 16.7 us  [query_grads(): jnp.einsum('abhqk,abkhe->abqhe', grad_score, split_heads(key_part), prefe...]
    convert_element_type x2, local copies, waits for them, and re-layouts: 2.44 us -> 0.23 us  [key_grads(): return (grad_key, grad_value.reshape(out_shape).astype(jnp.bfloat16))]
    unnamed x164 -> x168, local copies, waits for them, and re-layouts: 3.75 us -> 3.84 us
  transfers between devices with their start and end apart: 21 -> 21, of which waited for: 14 -> 14; matrix products, arithmetic and copies ran while one was open for 10% -> 14% of each run, Pallas kernels for 0% -> 0%
where the time goes in v6:
time: 189 us; the launch traced here: 188 us
  matrix products  56.7 us (30%)
  waiting for transfers between devices  55.1 us (29%)
  starting transfers between devices  39 us (21%)
  between operations  15.8 us (8%)
  local copies, waits for them, and re-layouts  15.6 us (8%)
  other arithmetic  5.82 us (3%)
    ppermute x6, starting transfers between devices, padded(): lax.ppermute(lax.slice_in_dim(block, block.shape[dim] - width, None, axis...  20.7 us
    dot_general x10, matrix products, query_grads(): jnp.einsum('abhqk,abkhe->abqhe', grad_score, split_heads(key_part), prefe...  16.7 us
    dot_general x10, matrix products, piece_scores(): jnp.einsum('abqhe,abkhe->abhqk', query_heads, split_heads(key_part), pref...  13.3 us
    ppermute x3, waiting for transfers between devices, tree_sum(): joined = keep + lax.ppermute(send, axis, pairs)  13.1 us
    ppermute x6, waiting for transfers between devices, padded(): lax.ppermute(lax.slice_in_dim(block, 0, width, axis=dim), axis, backward)  10.6 us
    ppermute x2, waiting for transfers between devices, tree_sum(): joined = joined + lax.ppermute(joined, axis, pairs)  10.4 us
    ppermute x3, waiting for transfers between devices, doubling_gather(): got = lax.ppermute(joined, axis, pairs)  9.27 us
    dot_general x9, matrix products, key_grads(): jnp.einsum('abhqk,abqhe->abkhe', grad_score, query_heads, preferred_eleme...  8.42 us
  transfers between devices with their start and end apart: 21, of which 14 were waited for; matrix products, arithmetic and copies ran while one was open for 14% of the time, Pallas kernels for 0%

profile of v6, /device:TPU:0, one launch (start us, length us, event | category | flops | bytes accessed | tf_op | source)
XLA Modules:
  0.0 188.0 jit_solution(17394024245961080482)
XLA Ops:
  9.3 1.3 collective-permute-start.1
  10.6 5.5 %collective-permute-start = (bf16[8,16,512]{2,1,0:T(8,128)(2,1)S(1)}, bf16[8,16,512]{2,1,0:T(8,128)(2,1)S(1)}, u32[]{:S(2)}, u32[]{:S(2)}) collective-permute-start(bf16[8,16,512]{2,1,0:T(8,128)(2,1)S(1)} %bitcast.503), channel_id=1, source_target_pairs={{0,4},{4,8},{8,12},{12,16},{16,20},{20,24},{24,28},{1,5},{5,9},{9,... | collective-permute-start | bytes 393224 | tf_op jit(solution)/shard_map/ppermute | solution.py:23
  18.4 4.8 %collective-permute-start.4 = (bf16[8,16,512]{2,1,0:T(8,128)(2,1)S(1)}, bf16[8,16,512]{2,1,0:T(8,128)(2,1)S(1)}, u32[]{:S(2)}, u32[]{:S(2)}) collective-permute-start(bf16[8,16,512]{2,1,0:T(8,128)(2,1)S(1)} %get-tuple-element.71), channel_id=1, source_target_pairs={{0,4},{4,8},{8,12},{12,16},{16,20},{20,24},{24,28},{1,5},{5,9},{9,... | collective-permute-start | bytes 393224 | tf_op jit(solution)/shard_map/ppermute | solution.py:23
  23.2 1.3 collective-permute-start.5
  25.6 3.0 %collective-permute-done.4 = bf16[8,16,512]{2,1,0:T(8,128)(2,1)S(1)} collective-permute-done((bf16[8,16,512]{2,1,0:T(8,128)(2,1)S(1)}, bf16[8,16,512]{2,1,0:T(8,128)(2,1)S(1)}, u32[]{:S(2)}, u32[]{:S(2)}) %collective-permute-start.4) | collective-permute-done | bytes 131104 | tf_op jit(solution)/shard_map/ppermute | solution.py:23
  28.6 1.5 collective-permute-done.5
  30.2 1.3 collective-permute-start.6
  31.5 1.3 collective-permute-start.7
  33.0 4.8 %collective-permute-start.2 = (bf16[32,8,512]{2,1,0:T(8,128)(2,1)S(1)}, bf16[32,8,512]{2,1,0:T(8,128)(2,1)S(1)}, u32[]{:S(2)}, u32[]{:S(2)}) collective-permute-start(bf16[32,8,512]{2,1,0:T(8,128)(2,1)S(1)} %get-tuple-element.67), channel_id=1, source_target_pairs={{0,1},{1,2},{2,3},{4,5},{5,6},{6,7},{8,9},{9,10},{10,11},{12,13},{... | collective-permute-start | bytes 786440 | tf_op jit(solution)/shard_map/ppermute | solution.py:23
  37.7 1.3 collective-permute-start.3
  39.5 3.0 %collective-permute-done.3 = bf16[32,8,512]{2,1,0:T(8,128)(2,1)} collective-permute-done((bf16[32,8,512]{2,1,0:T(8,128)(2,1)S(1)}, bf16[32,8,512]{2,1,0:T(8,128)(2,1)}, u32[]{:S(2)}, u32[]{:S(2)}) %collective-permute-start.3) | collective-permute-done | bytes 262176 | tf_op jit(solution)/shard_map/ppermute | solution.py:26
  43.9 1.3 slice_bitcast_fusion.18
  47.4 1.8 fusion.453
  49.2 2.5 %fusion.454 = (f32[2,2,2,64]{3,2,1,0:T(2,128)}, f32[2,2,2,64,64]{3,4,2,1,0:T(8,128)}) fusion(bf16[2,2,8,2,8,128]{5,4,3,2,1,0:T(8,128)(2,1)S(1)} %get-tuple-element.53, bf16[2,2,64,2,128]{4,3,2,1,0:T(2,128)(2,1)} %copy-done.50, pred[2,2]{1,0:T(4,128)(4,1)S(1)} %copy-done.70), kind=kOutput, calls=%fused_computation.560 | convolution fusion | flops 8486400 | bytes 395268 | tf_op jit(solution)/shard_map/abqhe,abkhe->abhqk/dot_general | solution.py:67
  51.7 2.4 %fusion.456 = (f32[2,2,2,64]{3,2,1,0:T(2,128)}, f32[2,2,2,64,64]{3,4,2,1,0:T(8,128)}) fusion(bf16[2,2,8,2,8,128]{5,4,3,2,1,0:T(8,128)(2,1)S(1)} %get-tuple-element.54, bf16[2,2,64,2,128]{4,3,2,1,0:T(2,128)(2,1)} %copy-done.50, pred[2,2]{1,0:T(4,128)(4,1)S(1)} %copy-done.68), kind=kOutput, calls=%fused_computation.562 | convolution fusion | flops 8486400 | bytes 395268 | tf_op jit(solution)/shard_map/abqhe,abkhe->abhqk/dot_general | solution.py:67
  54.1 1.7 fusion.455
  55.9 1.5 fusion.452
  57.4 8.0 %all-gather.3.cloned.1.call-done = bf16[1,1,32,64,512]{4,3,1,0,2:T(8,128)(2,1)} async-done(((bf16[1,1,4,64,512]{4,3,1,0,2:T(8,128)(2,1)}), bf16[1,1,32,64,512]{4,3,1,0,2:T(8,128)(2,1)}) %all-gather.3.cloned.1.call-update) | async-done | bytes 2097168 | tf_op jit(solution)/shard_map/all_gather | solution.py:261
  65.4 3.0 %gather_fusion = bf16[8,64,512]{2,1,0:T(8,128)(2,1)} fusion(bf16[32,64,512]{2,1,0:T(8,128)(2,1)} %bitcast.502, s32[1024]{0:T(1024)S(1)} %pad_clamp_fusion), kind=kCustom, calls=%fused_computation | custom fusion | bytes 1048608 | tf_op jit(solution)/shard_map/jit(_take)/gather | solution.py:275
  70.6 1.3 fusion.447
  73.0 1.7 exponential_reduce_fusion.8
  80.4 2.3 %convolution_add_fusion.24 = f32[2,2,2,128,64]{3,4,2,1,0:T(8,128)} fusion(f32[2,2,2,128,64]{3,4,2,1,0:T(8,128)} %fusion.84, f32[2,2,2,64,64]{3,4,2,1,0:T(8,128)} %get-tuple-element.125, f32[2,2,2,64]{3,2,1,0:T(2,128)S(1)} %bitcast.471, f32[2,2,2,64]{3,2,1,0:T(2,128)S(1)} %log_add_fusion, bf16[2,2,8,2,8,128]{5,4,3,2,1,0:T(8,128)(2,1)} %get-tuple-element.46, ...), kind=kOutput, calls=%fused_computation.98 | convolution fusion | flops 16973824 | bytes 1052672 | tf_op jit(solution)/shard_map/abhqk,abkhe->abqhe/dot_general | solution.py:115
  82.7 2.3 %convolution_add_fusion.23 = f32[2,2,2,128,64]{3,4,2,1,0:T(8,128)} fusion(f32[2,2,2,128,64]{3,4,2,1,0:T(8,128)} %convolution_add_fusion.24, f32[2,2,2,64,64]{3,4,2,1,0:T(8,128)} %get-tuple-element.121, f32[2,2,2,64]{3,2,1,0:T(2,128)S(1)} %bitcast.472, f32[2,2,2,64]{3,2,1,0:T(2,128)S(1)} %log_add_fusion, ...), kind=kOutput, calls=%fused_computation.95 | convolution fusion | flops 16973824 | bytes 1052672 | tf_op jit(solution)/shard_map/abhqk,abkhe->abqhe/dot_general | solution.py:115
  85.0 2.2 %convolution_add_fusion.22 = f32[2,2,2,128,64]{3,4,2,1,0:T(8,128)} fusion(f32[2,2,2,128,64]{3,4,2,1,0:T(8,128)} %convolution_add_fusion.23, f32[2,2,2,64,64]{3,4,2,1,0:T(8,128)S(1)} %copy-done.4, f32[2,2,2,64]{3,2,1,0:T(2,128)S(1)} %bitcast.473, f32[2,2,2,64]{3,2,1,0:T(2,128)S(1)} %log_add_fusion, bf16[2,2,8,2,8,128]{5,4,3,2,1,0:T(8,128)(2,1)S(1)} %copy-done.20, ...), kind=kOutput, calls=%fused_computation.92 | convolution fusion | flops 16973824 | bytes 1052672 | tf_op jit(solution)/shard_map/abhqk,abkhe->abqhe/dot_general | solution.py:115
  87.2 2.2 %convolution_add_fusion.21 = f32[2,2,2,128,64]{3,4,2,1,0:T(8,128)} fusion(f32[2,2,2,128,64]{3,4,2,1,0:T(8,128)} %convolution_add_fusion.22, f32[2,2,2,64,64]{3,4,2,1,0:T(8,128)S(1)} %copy-done.9, f32[2,2,2,64]{3,2,1,0:T(2,128)S(1)} %bitcast.474, f32[2,2,2,64]{3,2,1,0:T(2,128)S(1)} %log_add_fusion, bf16[2,2,8,2,8,128]{5,4,3,2,1,0:T(8,128)(2,1)S(1)} %get-tuple-element.43, ...), kind=kOutput, calls=%fused_computation.89 | convolution fusion | flops 16973824 | bytes 1052672 | tf_op jit(solution)/shard_map/abhqk,abkhe->abqhe/dot_general | solution.py:115
  89.3 2.2 %convolution_add_fusion.20 = f32[2,2,2,128,64]{3,4,2,1,0:T(8,128)} fusion(f32[2,2,2,128,64]{3,4,2,1,0:T(8,128)} %convolution_add_fusion.21, f32[2,2,2,64,64]{3,4,2,1,0:T(8,128)S(1)} %copy-done.2, f32[2,2,2,64]{3,2,1,0:T(2,128)S(1)} %bitcast.475, f32[2,2,2,64]{3,2,1,0:T(2,128)S(1)} %log_add_fusion, bf16[2,2,8,2,8,128]{5,4,3,2,1,0:T(8,128)(2,1)} %get-tuple-element.42, ...), kind=kOutput, calls=%fused_computation.86 | convolution fusion | flops 16973824 | bytes 1052672 | tf_op jit(solution)/shard_map/abhqk,abkhe->abqhe/dot_general | solution.py:115
  91.5 1.5 convolution_add_fusion.19
  93.0 1.3 convolution_add_fusion.18
  94.4 1.3 convolution_add_fusion.17
  97.0 3.0 %collective-permute-start.8 = (f32[8,16,4]{1,0,2:T(8,128)S(1)}, f32[8,16,4]{1,0,2:T(8,128)}, u32[]{:S(2)}, u32[]{:S(2)}) collective-permute-start(f32[8,16,4]{1,0,2:T(8,128)S(1)} %slice.413), channel_id=1, source_target_pairs={{0,4},{4,8},{8,12},{12,16},{16,20},{20,24},{24,28},{1,5},{5,9},{9,... | collective-permute-start | bytes 6152 | tf_op jit(solution)/shard_map/ppermute | solution.py:23
  100.2 1.3 slice_bitcast_fusion
  103.8 1.3 collective-permute-start.9
  105.8 3.6 %collective-permute-done.9 = f32[8,16,4]{1,0,2:T(8,128)S(1)} collective-permute-done((f32[8,16,4]{1,0,2:T(8,128)S(1)}, f32[8,16,4]{1,0,2:T(8,128)S(1)}, u32[]{:S(2)}, u32[]{:S(2)}) %collective-permute-start.9) | collective-permute-done | bytes 2080 | tf_op jit(solution)/shard_map/ppermute | solution.py:26
  109.5 1.3 collective-permute-start.10
  110.8 1.5 collective-permute-start.11
  113.2 2.4 %collective-permute-done.11 = f32[32,8,4]{1,0,2:T(8,128)S(1)} collective-permute-done((f32[32,8,4]{1,0,2:T(8,128)S(1)}, f32[32,8,4]{1,0,2:T(8,128)S(1)}, u32[]{:S(2)}, u32[]{:S(2)}) %collective-permute-start.11) | collective-permute-done | bytes 4128 | tf_op jit(solution)/shard_map/ppermute | solution.py:26
  125.6 1.3 convolution_add_fusion.15
  127.0 1.3 convolution_add_fusion.14
  134.0 3.0 %collective-permute-start.12 = (f32[512,256]{1,0:T(8,128)S(1)}, f32[512,256]{1,0:T(8,128)S(1)}, u32[]{:S(2)}, u32[]{:S(2)}) collective-permute-start(f32[512,256]{1,0:T(8,128)S(1)} %constant_dynamic-slice_fusion.2), channel_id=1, source_target_pairs={{0,1},{1,0},{2,3},{3,2},{4,5},{5,4},{6,7},{7,6},{8,9},{9,8},{10,11... | collective-permute-start | bytes 1572872 | tf_op jit(solution)/shard_map/ppermute | solution.py:222
  137.0 1.5 collective-permute-done.12
  139.0 8.4 %collective-permute-done.13 = f32[256,256]{1,0:T(8,128)S(1)} collective-permute-done((f32[256,256]{1,0:T(8,128)S(1)}, f32[256,256]{1,0:T(8,128)S(1)}, u32[]{:S(2)}, u32[]{:S(2)}) %collective-permute-start.13) | collective-permute-done | bytes 262176 | tf_op jit(solution)/shard_map/ppermute | solution.py:222
  147.4 2.8 %collective-permute-start.14 = (f32[128,256]{1,0:T(8,128)S(1)}, f32[128,256]{1,0:T(8,128)S(1)}, u32[]{:S(2)}, u32[]{:S(2)}) collective-permute-start(f32[128,256]{1,0:T(8,128)S(1)} %constant_dynamic-slice_fusion), channel_id=1, source_target_pairs={{0,4},{4,0},{8,12},{12,8},{16,20},{20,16},{24,28},{28,24},{1,5},{5... | collective-permute-start | bytes 393224 | tf_op jit(solution)/shard_map/ppermute | solution.py:222
  150.2 3.2 %collective-permute-done.14 = f32[128,256]{1,0:T(8,128)S(1)} collective-permute-done((f32[128,256]{1,0:T(8,128)S(1)}, f32[128,256]{1,0:T(8,128)S(1)}, u32[]{:S(2)}, u32[]{:S(2)}) %collective-permute-start.14) | collective-permute-done | bytes 131104 | tf_op jit(solution)/shard_map/ppermute | solution.py:222
  154.4 4.1 %collective-permute-done.15 = f32[128,256]{1,0:T(8,128)S(1)} collective-permute-done((f32[128,256]{1,0:T(8,128)S(1)}, f32[128,256]{1,0:T(8,128)S(1)}, u32[]{:S(2)}, u32[]{:S(2)}) %collective-permute-start.15) | collective-permute-done | bytes 131104 | tf_op jit(solution)/shard_map/ppermute | solution.py:225
  159.5 6.4 %collective-permute-done.16 = f32[128,256]{1,0:T(8,128)S(1)} collective-permute-done((f32[128,256]{1,0:T(8,128)S(1)}, f32[128,256]{1,0:T(8,128)S(1)}, u32[]{:S(2)}, u32[]{:S(2)}) %collective-permute-start.16) | collective-permute-done | bytes 131104 | tf_op jit(solution)/shard_map/ppermute | solution.py:225
  165.9 1.8 collective-permute-start.17
  167.7 3.2 %collective-permute-done.17 = f32[128,256]{1,0:T(8,128)S(1)} collective-permute-done((f32[128,256]{1,0:T(8,128)S(1)}, f32[128,256]{1,0:T(8,128)S(1)}, u32[]{:S(2)}, u32[]{:S(2)}) %collective-permute-start.17) | collective-permute-done | bytes 131104 | tf_op jit(solution)/shard_map/ppermute | solution.py:187
  171.4 6.0 %collective-permute-done.18 = f32[256,256]{1,0:T(8,128)S(1)} collective-permute-done((f32[256,256]{1,0:T(8,128)S(1)}, f32[256,256]{1,0:T(8,128)S(1)}, u32[]{:S(2)}, u32[]{:S(2)}) %collective-permute-start.18) | collective-permute-done | bytes 262176 | tf_op jit(solution)/shard_map/ppermute | solution.py:187
  (309 shorter events, 45.2 us)
Async XLA Ops:
  7.2 17.4 %copy-start.66 = (s32[1,1,4,2]{2,3,1,0:T(2,128)S(1)}, s32[1,1,4,2]{2,3,1,0:T(2,128)}, u32[]{:S(2)}) copy-start(s32[1,1,4,2]{2,3,1,0:T(2,128)} %param.16) | copy-start | bytes 100
  7.2 17.4 %copy-start.67 = (s32[1,1,4,2]{2,3,1,0:T(2,128)S(1)}, s32[1,1,4,2]{2,3,1,0:T(2,128)}, u32[]{:S(2)}) copy-start(s32[1,1,4,2]{2,3,1,0:T(2,128)} %param.15) | copy-start | bytes 100
  7.2 58.2 %all-gather.3.cloned.1.call-start = ((), (), s32[]{:S(2)}) async-start(), calls=%async_computation | async-start | bytes 2359296 | tf_op jit(solution)/shard_map/all_gather | solution.py:261
  9.3 23.5 %collective-permute-start.1 = (bf16[8,16,512]{2,1,0:T(8,128)(2,1)S(1)}, bf16[8,16,512]{2,1,0:T(8,128)(2,1)S(1)}, u32[]{:S(2)}, u32[]{:S(2)}) collective-permute-start(bf16[8,16,512]{2,1,0:T(8,128)(2,1)S(1)} %bitcast.504), channel_id=1, source_target_pairs={{4,0},{8,4},{12,8},{16,12},{20,16},{24,20},{28,24},{5,1},{9,5},{13... | collective-permute-start | bytes 393224 | tf_op jit(solution)/shard_map/ppermute | solution.py:26
  10.6 22.2 %collective-permute-start = (bf16[8,16,512]{2,1,0:T(8,128)(2,1)S(1)}, bf16[8,16,512]{2,1,0:T(8,128)(2,1)S(1)}, u32[]{:S(2)}, u32[]{:S(2)}) collective-permute-start(bf16[8,16,512]{2,1,0:T(8,128)(2,1)S(1)} %bitcast.503), channel_id=1, source_target_pairs={{0,4},{4,8},{8,12},{12,16},{16,20},{20,24},{24,28},{1,5},{5,9},{9,... | collective-permute-start | bytes 393224 | tf_op jit(solution)/shard_map/ppermute | solution.py:23
  18.4 10.2 %collective-permute-start.4 = (bf16[8,16,512]{2,1,0:T(8,128)(2,1)S(1)}, bf16[8,16,512]{2,1,0:T(8,128)(2,1)S(1)}, u32[]{:S(2)}, u32[]{:S(2)}) collective-permute-start(bf16[8,16,512]{2,1,0:T(8,128)(2,1)S(1)} %get-tuple-element.71), channel_id=1, source_target_pairs={{0,4},{4,8},{8,12},{12,16},{16,20},{20,24},{24,28},{1,5},{5,9},{9,... | collective-permute-start | bytes 393224 | tf_op jit(solution)/shard_map/ppermute | solution.py:23
  23.2 6.9 %collective-permute-start.5 = (bf16[8,16,512]{2,1,0:T(8,128)(2,1)S(1)}, bf16[8,16,512]{2,1,0:T(8,128)(2,1)S(1)}, u32[]{:S(2)}, u32[]{:S(2)}) collective-permute-start(bf16[8,16,512]{2,1,0:T(8,128)(2,1)S(1)} %get-tuple-element.72), channel_id=1, source_target_pairs={{4,0},{8,4},{12,8},{16,12},{20,16},{24,20},{28,24},{5,1},{9,5},{13... | collective-permute-start | bytes 393224 | tf_op jit(solution)/shard_map/ppermute | solution.py:26
  25.6 19.7 %copy-start.78 = (pred[2,2]{1,0:T(4,128)(4,1)}, pred[2,2]{1,0:T(4,128)(4,1)S(1)}, u32[]{:S(2)}) copy-start(pred[2,2]{1,0:T(4,128)(4,1)S(1)} %get-tuple-element.98) | copy-start | bytes 16
  25.6 20.0 %copy-start.76 = (pred[2,2]{1,0:T(4,128)(4,1)}, pred[2,2]{1,0:T(4,128)(4,1)S(1)}, u32[]{:S(2)}) copy-start(pred[2,2]{1,0:T(4,128)(4,1)S(1)} %get-tuple-element.99) | copy-start | bytes 16
  30.2 13.5 %collective-permute-start.6 = (bf16[32,8,512]{2,1,0:T(8,128)(2,1)S(1)}, bf16[32,8,512]{2,1,0:T(8,128)(2,1)S(1)}, u32[]{:S(2)}, u32[]{:S(2)}) collective-permute-start(bf16[32,8,512]{2,1,0:T(8,128)(2,1)S(1)} %get-tuple-element.65), channel_id=1, source_target_pairs={{0,1},{1,2},{2,3},{4,5},{5,6},{6,7},{8,9},{9,10},{10,11},{12,13},{... | collective-permute-start | bytes 786440 | tf_op jit(solution)/shard_map/ppermute | solution.py:23
  31.5 12.2 %collective-permute-start.7 = (bf16[32,8,512]{2,1,0:T(8,128)(2,1)S(1)}, bf16[32,8,512]{2,1,0:T(8,128)(2,1)S(1)}, u32[]{:S(2)}, u32[]{:S(2)}) collective-permute-start(bf16[32,8,512]{2,1,0:T(8,128)(2,1)S(1)} %get-tuple-element.66), channel_id=1, source_target_pairs={{1,0},{2,1},{3,2},{5,4},{6,5},{7,6},{9,8},{10,9},{11,10},{13,12},{... | collective-permute-start | bytes 786440 | tf_op jit(solution)/shard_map/ppermute | solution.py:26
  33.0 6.5 %collective-permute-start.2 = (bf16[32,8,512]{2,1,0:T(8,128)(2,1)S(1)}, bf16[32,8,512]{2,1,0:T(8,128)(2,1)S(1)}, u32[]{:S(2)}, u32[]{:S(2)}) collective-permute-start(bf16[32,8,512]{2,1,0:T(8,128)(2,1)S(1)} %get-tuple-element.67), channel_id=1, source_target_pairs={{0,1},{1,2},{2,3},{4,5},{5,6},{6,7},{8,9},{9,10},{10,11},{12,13},{... | collective-permute-start | bytes 786440 | tf_op jit(solution)/shard_map/ppermute | solution.py:23
  37.7 4.8 %collective-permute-start.3 = (bf16[32,8,512]{2,1,0:T(8,128)(2,1)S(1)}, bf16[32,8,512]{2,1,0:T(8,128)(2,1)}, u32[]{:S(2)}, u32[]{:S(2)}) collective-permute-start(bf16[32,8,512]{2,1,0:T(8,128)(2,1)S(1)} %get-tuple-element.68), channel_id=1, source_target_pairs={{1,0},{2,1},{3,2},{5,4},{6,5},{7,6},{9,8},{10,9},{11,10},{13,12},{... | collective-permute-start | bytes 786440 | tf_op jit(solution)/shard_map/ppermute | solution.py:26
  45.2 9.0 %copy-start.44 = (bf16[2,2,8,2,8,128]{5,4,3,2,1,0:T(8,128)(2,1)}, bf16[2,2,8,2,8,128]{5,4,3,2,1,0:T(8,128)(2,1)S(1)}, u32[]{:S(2)}) copy-start(bf16[2,2,8,2,8,128]{5,4,3,2,1,0:T(8,128)(2,1)S(1)} %get-tuple-element.50) | copy-start | bytes 393220
  45.2 9.0 %copy-start.45 = (bf16[2,2,8,2,8,128]{5,4,3,2,1,0:T(8,128)(2,1)}, bf16[2,2,8,2,8,128]{5,4,3,2,1,0:T(8,128)(2,1)S(1)}, u32[]{:S(2)}) copy-start(bf16[2,2,8,2,8,128]{5,4,3,2,1,0:T(8,128)(2,1)S(1)} %get-tuple-element.52) | copy-start | bytes 393220
  45.2 10.7 %copy-start.39 = (bf16[2,2,8,2,8,128]{5,4,3,2,1,0:T(8,128)(2,1)}, bf16[2,2,8,2,8,128]{5,4,3,2,1,0:T(8,128)(2,1)S(1)}, u32[]{:S(2)}) copy-start(bf16[2,2,8,2,8,128]{5,4,3,2,1,0:T(8,128)(2,1)S(1)} %get-tuple-element.47) | copy-start | bytes 393220
  45.2 10.7 %copy-start.42 = (bf16[2,2,8,2,8,128]{5,4,3,2,1,0:T(8,128)(2,1)}, bf16[2,2,8,2,8,128]{5,4,3,2,1,0:T(8,128)(2,1)S(1)}, u32[]{:S(2)}) copy-start(bf16[2,2,8,2,8,128]{5,4,3,2,1,0:T(8,128)(2,1)S(1)} %get-tuple-element.48) | copy-start | bytes 393220
  45.2 10.7 %copy-start.43 = (bf16[2,2,8,2,8,128]{5,4,3,2,1,0:T(8,128)(2,1)}, bf16[2,2,8,2,8,128]{5,4,3,2,1,0:T(8,128)(2,1)S(1)}, u32[]{:S(2)}) copy-start(bf16[2,2,8,2,8,128]{5,4,3,2,1,0:T(8,128)(2,1)S(1)} %get-tuple-element.49) | copy-start | bytes 393220
  45.2 10.7 %copy-start.46 = (bf16[2,2,8,2,8,128]{5,4,3,2,1,0:T(8,128)(2,1)}, bf16[2,2,8,2,8,128]{5,4,3,2,1,0:T(8,128)(2,1)S(1)}, u32[]{:S(2)}) copy-start(bf16[2,2,8,2,8,128]{5,4,3,2,1,0:T(8,128)(2,1)S(1)} %get-tuple-element.53) | copy-start | bytes 393220
  45.2 10.7 %copy-start.47 = (bf16[2,2,8,2,8,128]{5,4,3,2,1,0:T(8,128)(2,1)}, bf16[2,2,8,2,8,128]{5,4,3,2,1,0:T(8,128)(2,1)S(1)}, u32[]{:S(2)}) copy-start(bf16[2,2,8,2,8,128]{5,4,3,2,1,0:T(8,128)(2,1)S(1)} %get-tuple-element.54) | copy-start | bytes 393220
  45.2 10.7 %copy-start.48 = (bf16[2,2,8,2,8,128]{5,4,3,2,1,0:T(8,128)(2,1)}, bf16[2,2,8,2,8,128]{5,4,3,2,1,0:T(8,128)(2,1)S(1)}, u32[]{:S(2)}) copy-start(bf16[2,2,8,2,8,128]{5,4,3,2,1,0:T(8,128)(2,1)S(1)} %get-tuple-element.55) | copy-start | bytes 393220
  45.2 10.7 %copy-start.31 = (bf16[2,2,8,2,8,128]{5,4,3,2,1,0:T(8,128)(2,1)}, bf16[2,2,8,2,8,128]{5,4,3,2,1,0:T(8,128)(2,1)S(1)}, u32[]{:S(2)}) copy-start(bf16[2,2,8,2,8,128]{5,4,3,2,1,0:T(8,128)(2,1)S(1)} %get-tuple-element.51) | copy-start | bytes 393220
  45.5 10.4 %copy-start.73 = (pred[2,2]{1,0:T(4,128)(4,1)S(1)}, pred[2,2]{1,0:T(4,128)(4,1)}, u32[]{:S(2)}) copy-start(pred[2,2]{1,0:T(4,128)(4,1)} %get-tuple-element.102) | copy-start | bytes 16
  47.4 29.7 %copy-start.1 = (f32[2,2,2,64,64]{3,4,2,1,0:T(8,128)}, f32[2,2,2,64,64]{3,4,2,1,0:T(8,128)S(1)}, u32[]{:S(2)}) copy-start(f32[2,2,2,64,64]{3,4,2,1,0:T(8,128)S(1)} %get-tuple-element.115) | copy-start | bytes 393220
  49.2 27.3 %copy-start.3 = (f32[2,2,2,64,64]{3,4,2,1,0:T(8,128)}, f32[2,2,2,64,64]{3,4,2,1,0:T(8,128)S(1)}, u32[]{:S(2)}) copy-start(f32[2,2,2,64,64]{3,4,2,1,0:T(8,128)S(1)} %get-tuple-element.119) | copy-start | bytes 393220
  97.0 8.1 %collective-permute-start.8 = (f32[8,16,4]{1,0,2:T(8,128)S(1)}, f32[8,16,4]{1,0,2:T(8,128)}, u32[]{:S(2)}, u32[]{:S(2)}) collective-permute-start(f32[8,16,4]{1,0,2:T(8,128)S(1)} %slice.413), channel_id=1, source_target_pairs={{0,4},{4,8},{8,12},{12,16},{16,20},{20,24},{24,28},{1,5},{5,9},{9,... | collective-permute-start | bytes 6152 | tf_op jit(solution)/shard_map/ppermute | solution.py:23
  101.6 16.9 %copy-start.33 = (bf16[2,2,8,2,8,128]{5,4,3,2,1,0:T(8,128)(2,1)}, bf16[2,2,8,2,8,128]{5,4,3,2,1,0:T(8,128)(2,1)S(1)}, u32[]{:S(2)}) copy-start(bf16[2,2,8,2,8,128]{5,4,3,2,1,0:T(8,128)(2,1)S(1)} %get-tuple-element.24) | copy-start | bytes 393220
  101.6 17.1 %copy-start.35 = (bf16[2,2,8,2,8,128]{5,4,3,2,1,0:T(8,128)(2,1)}, bf16[2,2,8,2,8,128]{5,4,3,2,1,0:T(8,128)(2,1)S(1)}, u32[]{:S(2)}) copy-start(bf16[2,2,8,2,8,128]{5,4,3,2,1,0:T(8,128)(2,1)S(1)} %get-tuple-element.26) | copy-start | bytes 393220
  101.6 18.0 %copy-start.37 = (bf16[2,2,8,2,8,128]{5,4,3,2,1,0:T(8,128)(2,1)}, bf16[2,2,8,2,8,128]{5,4,3,2,1,0:T(8,128)(2,1)S(1)}, u32[]{:S(2)}) copy-start(bf16[2,2,8,2,8,128]{5,4,3,2,1,0:T(8,128)(2,1)S(1)} %get-tuple-element.28) | copy-start | bytes 393220
  101.6 15.2 %copy-start.32 = (bf16[2,2,8,2,8,128]{5,4,3,2,1,0:T(8,128)(2,1)S(1)}, bf16[2,2,8,2,8,128]{5,4,3,2,1,0:T(8,128)(2,1)}, u32[]{:S(2)}) copy-start(bf16[2,2,8,2,8,128]{5,4,3,2,1,0:T(8,128)(2,1)} %copy-done.31) | copy-start | bytes 393220
  101.6 15.2 %copy-start.81 = (pred[2,2]{1,0:T(4,128)(4,1)S(1)}, pred[2,2]{1,0:T(4,128)(4,1)}, u32[]{:S(2)}) copy-start(pred[2,2]{1,0:T(4,128)(4,1)} %get-tuple-element.105) | copy-start | bytes 16
  102.8 12.8 %copy-start.53 = (bf16[2,8,2,8,256]{4,3,2,1,0:T(8,128)(2,1)}, bf16[2,8,2,8,256]{4,3,2,1,0:T(8,128)(2,1)S(1)}, u32[]{:S(2)}) copy-start(bf16[2,8,2,8,256]{4,3,2,1,0:T(8,128)(2,1)S(1)} %copy.440) | copy-start | bytes 393220
  103.8 5.6 %collective-permute-start.9 = (f32[8,16,4]{1,0,2:T(8,128)S(1)}, f32[8,16,4]{1,0,2:T(8,128)S(1)}, u32[]{:S(2)}, u32[]{:S(2)}) collective-permute-start(f32[8,16,4]{1,0,2:T(8,128)S(1)} %slice.415), channel_id=1, source_target_pairs={{4,0},{8,4},{12,8},{16,12},{20,16},{24,20},{28,24},{5,1},{9,5},{13... | collective-permute-start | bytes 6152 | tf_op jit(solution)/shard_map/ppermute | solution.py:26
  109.5 3.7 %collective-permute-start.10 = (f32[32,8,4]{1,0,2:T(8,128)S(1)}, f32[32,8,4]{1,0,2:T(8,128)S(1)}, u32[]{:S(2)}, u32[]{:S(2)}) collective-permute-start(f32[32,8,4]{1,0,2:T(8,128)S(1)} %get-tuple-element.75), channel_id=1, source_target_pairs={{0,1},{1,2},{2,3},{4,5},{5,6},{6,7},{8,9},{9,10},{10,11},{12,13},{... | collective-permute-start | bytes 12296 | tf_op jit(solution)/shard_map/ppermute | solution.py:23
  110.8 4.8 %collective-permute-start.11 = (f32[32,8,4]{1,0,2:T(8,128)S(1)}, f32[32,8,4]{1,0,2:T(8,128)S(1)}, u32[]{:S(2)}, u32[]{:S(2)}) collective-permute-start(f32[32,8,4]{1,0,2:T(8,128)S(1)} %get-tuple-element.76), channel_id=1, source_target_pairs={{1,0},{2,1},{3,2},{5,4},{6,5},{7,6},{9,8},{10,9},{11,10},{13,12},{... | collective-permute-start | bytes 12296 | tf_op jit(solution)/shard_map/ppermute | solution.py:26
  134.0 4.5 %collective-permute-start.12 = (f32[512,256]{1,0:T(8,128)S(1)}, f32[512,256]{1,0:T(8,128)S(1)}, u32[]{:S(2)}, u32[]{:S(2)}) collective-permute-start(f32[512,256]{1,0:T(8,128)S(1)} %constant_dynamic-slice_fusion.2), channel_id=1, source_target_pairs={{0,1},{1,0},{2,3},{3,2},{4,5},{5,4},{6,7},{7,6},{8,9},{9,8},{10,11... | collective-permute-start | bytes 1572872 | tf_op jit(solution)/shard_map/ppermute | solution.py:222
  138.7 8.7 %collective-permute-start.13 = (f32[256,256]{1,0:T(8,128)S(1)}, f32[256,256]{1,0:T(8,128)S(1)}, u32[]{:S(2)}, u32[]{:S(2)}) collective-permute-start(f32[256,256]{1,0:T(8,128)S(1)} %constant_dynamic-slice_fusion.1), channel_id=1, source_target_pairs={{0,2},{1,3},{2,0},{3,1},{4,6},{5,7},{6,4},{7,5},{8,10},{9,11},{10,... | collective-permute-start | bytes 786440 | tf_op jit(solution)/shard_map/ppermute | solution.py:222
  147.4 6.0 %collective-permute-start.14 = (f32[128,256]{1,0:T(8,128)S(1)}, f32[128,256]{1,0:T(8,128)S(1)}, u32[]{:S(2)}, u32[]{:S(2)}) collective-permute-start(f32[128,256]{1,0:T(8,128)S(1)} %constant_dynamic-slice_fusion), channel_id=1, source_target_pairs={{0,4},{4,0},{8,12},{12,8},{16,20},{20,16},{24,28},{28,24},{1,5},{5... | collective-permute-start | bytes 393224 | tf_op jit(solution)/shard_map/ppermute | solution.py:222
  150.2 27.4 %copy-start.30 = (bf16[256,256]{1,0:T(8,128)(2,1)S(1)}, bf16[256,256]{1,0:T(8,128)(2,1)}, u32[]{:S(2)}) copy-start(bf16[256,256]{1,0:T(8,128)(2,1)} %param.13) | copy-start | bytes 393220
  153.4 25.0 %copy-start.54 = (bf16[2,8,2,8,256]{4,3,2,1,0:T(8,128)(2,1)S(1)}, bf16[2,8,2,8,256]{4,3,2,1,0:T(8,128)(2,1)}, u32[]{:S(2)}) copy-start(bf16[2,8,2,8,256]{4,3,2,1,0:T(8,128)(2,1)} %copy-done.53) | copy-start | bytes 393220
  153.4 25.0 %copy-start.59 = (bf16[256,256]{1,0:T(8,128)(2,1)S(1)}, bf16[256,256]{1,0:T(8,128)(2,1)}, u32[]{:S(2)}) copy-start(bf16[256,256]{1,0:T(8,128)(2,1)} %param.12) | copy-start | bytes 393220
  153.4 25.0 %copy-start.60 = (bf16[256,256]{1,0:T(8,128)(2,1)S(1)}, bf16[256,256]{1,0:T(8,128)(2,1)}, u32[]{:S(2)}) copy-start(bf16[256,256]{1,0:T(8,128)(2,1)} %param.11) | copy-start | bytes 393220
  153.4 25.0 %copy-start.61 = (bf16[256,256]{1,0:T(8,128)(2,1)S(1)}, bf16[256,256]{1,0:T(8,128)(2,1)}, u32[]{:S(2)}) copy-start(bf16[256,256]{1,0:T(8,128)(2,1)} %param.10) | copy-start | bytes 393220
  153.5 5.0 %collective-permute-start.15 = (f32[128,256]{1,0:T(8,128)S(1)}, f32[128,256]{1,0:T(8,128)S(1)}, u32[]{:S(2)}, u32[]{:S(2)}) collective-permute-start(f32[128,256]{1,0:T(8,128)S(1)} %dynamic-slice_add_fusion.2), channel_id=1, source_target_pairs={{0,8},{4,12},{8,0},{12,4},{16,24},{20,28},{24,16},{28,20},{1,9},{5... | collective-permute-start | bytes 393224 | tf_op jit(solution)/shard_map/ppermute | solution.py:225
  158.5 7.3 %collective-permute-start.16 = (f32[128,256]{1,0:T(8,128)S(1)}, f32[128,256]{1,0:T(8,128)S(1)}, u32[]{:S(2)}, u32[]{:S(2)}) collective-permute-start(f32[128,256]{1,0:T(8,128)S(1)} %add.391), channel_id=1, source_target_pairs={{0,16},{4,20},{8,24},{12,28},{16,0},{20,4},{24,8},{28,12},{1,17},{... | collective-permute-start | bytes 393224 | tf_op jit(solution)/shard_map/ppermute | solution.py:225
  165.9 5.0 %collective-permute-start.17 = (f32[128,256]{1,0:T(8,128)S(1)}, f32[128,256]{1,0:T(8,128)S(1)}, u32[]{:S(2)}, u32[]{:S(2)}) collective-permute-start(f32[128,256]{1,0:T(8,128)S(1)} %add.392), channel_id=1, source_target_pairs={{0,4},{4,0},{8,12},{12,8},{16,20},{20,16},{24,28},{28,24},{1,5},{5... | collective-permute-start | bytes 393224 | tf_op jit(solution)/shard_map/ppermute | solution.py:187
  171.0 6.4 %collective-permute-start.18 = (f32[256,256]{1,0:T(8,128)S(1)}, f32[256,256]{1,0:T(8,128)S(1)}, u32[]{:S(2)}, u32[]{:S(2)}) collective-permute-start(f32[256,256]{1,0:T(8,128)S(1)} %pad_maximum_fusion.6), channel_id=1, source_target_pairs={{0,2},{1,3},{2,0},{3,1},{4,6},{5,7},{6,4},{7,5},{8,10},{9,11},{10,... | collective-permute-start | bytes 786440 | tf_op jit(solution)/shard_map/ppermute | solution.py:187
  177.5 2.0 %collective-permute-start.19 = (f32[512,256]{1,0:T(8,128)S(1)}, f32[512,256]{1,0:T(8,128)S(1)}, u32[]{:S(2)}, u32[]{:S(2)}) collective-permute-start(f32[512,256]{1,0:T(8,128)S(1)} %pad_maximum_fusion.5), channel_id=1, source_target_pairs={{0,1},{1,0},{2,3},{3,2},{4,5},{5,4},{6,7},{7,6},{8,9},{9,8},{10,11... | collective-permute-start | bytes 1572872 | tf_op jit(solution)/shard_map/ppermute | solution.py:187
  (55 other events, 215.1 us)
Sparse Core Ops, SparseCore 0:
  10.2 55.1 all-gather.2

commit v7 on v4

--- a/solution.py
+++ b/solution.py
@@ -10,6 +10,7 @@
 HEAD_DIM = 128
 BSIDE = 8
 BT = 64
+CAP = 2
 
 
 masked_score = -1000000000.0
@@ -232,6 +233,24 @@
     return tuple(out)
 
 
+def fetch_regions(memory_local, owners, local_ids, axis):
+    count = lax.axis_size(axis)
+    entries = owners.shape[0]
+    order = jnp.arange(entries)
+    same = owners[:, None] == owners[None, :]
+    rank = jnp.sum(same & (order[None, :] < order[:, None]), axis=1)
+    wanted = (owners[:, None, None] == jnp.arange(count)[None, :, None]) & (
+        rank[:, None, None] == jnp.arange(CAP)[None, None, :]
+    )
+    requests = jnp.sum(jnp.where(wanted, local_ids[:, None, None], 0), axis=0)
+    asked = lax.all_to_all(requests, axis, 0, 0, tiled=True)
+    sent = jnp.take(memory_local, asked.reshape(-1), axis=0)
+    sent = sent.reshape((count, CAP) + memory_local.shape[1:])
+    received = lax.all_to_all(sent, axis, 0, 0, tiled=True)
+    received = received.reshape((count * CAP,) + memory_local.shape[1:])
+    return jnp.take(received, owners * CAP + rank, axis=0)
+
+
 def on_device(
     patches, w_query, w_key, w_value, w_out, region_memory, region_owner, region_local, grad_out
 ):
@@ -257,9 +276,7 @@
     memory_local = region_memory.reshape(
         region_memory.shape[2], region_memory.shape[3], region_memory.shape[4]
     )
-    region_count = memory_local.shape[0]
-    row_tables = lax.all_gather(memory_local, "gx", axis=0, tiled=True)
-    fetched = jnp.take(row_tables, owners * region_count + local_ids, axis=0)
+    fetched = fetch_regions(memory_local, owners, local_ids, "gx")
     region_keyval = fetched.reshape(
         block_rows, block_cols, 2, memory_local.shape[1], memory_local.shape[2]
     )

time: 181 us -> 181 us (level)
  between operations: 16 us -> 2.45 us
  local copies, waits for them, and re-layouts: 15.3 us -> 25 us
  starting transfers between devices: 38.5 us -> 47.3 us
  matrix products: 44.2 us -> 39.1 us
  waiting for transfers between devices: 62.2 us -> 58.9 us
  other arithmetic: 3.61 us -> 6.87 us
    all_to_all x0 -> x2, waiting for transfers between devices: none -> 15.6 us  [the longest x1 15.6 us: fetch_regions(): received = lax.all_to_all(sent, axis, 0, 0, tiled=True)]
    all_gather x1 -> x0, waiting for transfers between devices: 13.8 us -> none  [on_device(): row_tables = lax.all_gather(memory_local, 'gx', axis=0, tiled=True)]
    all_to_all x0 -> x2, starting transfers between devices: none -> 11.8 us  [the longest x1 7.25 us: fetch_regions(): asked = lax.all_to_all(requests, axis, 0, 0, tiled=True)]
    unnamed x164 -> x196, local copies, waits for them, and re-layouts: 3.75 us -> 9.39 us
    ppermute x6, waiting for transfers between devices: 3.5 us -> 0.02 us  [padded(): lax.ppermute(lax.slice_in_dim(block, block.shape[dim] - width, None, axis...]
    ppermute x6, waiting for transfers between devices: 11.4 us -> 8.84 us  [padded(): lax.ppermute(lax.slice_in_dim(block, 0, width, axis=dim), axis, backward)]
    ppermute x3, starting transfers between devices: 6.26 us -> 4.27 us  [tree_sum(): joined = keep + lax.ppermute(send, axis, pairs)]
    dot_general x10, matrix products: 13.1 us -> 11.3 us  [query_grads(): jnp.einsum('abhqk,abkhe->abqhe', grad_score, split_heads(key_part), prefe...]
  transfers between devices with their start and end apart: 21 -> 22, of which waited for: 14 -> 12; matrix products, arithmetic and copies ran while one was open for 10% -> 13% of each run, Pallas kernels for 0% -> 0%
where the time goes in v7:
time: 181 us; the launch traced here: 180 us
  waiting for transfers between devices  58.9 us (33%)
  starting transfers between devices  47.3 us (26%)
  matrix products  39.1 us (22%)
  local copies, waits for them, and re-layouts  25 us (14%)
  other arithmetic  6.87 us (4%)
  between operations  2.45 us (1%)
    ppermute x6, starting transfers between devices, padded(): lax.ppermute(lax.slice_in_dim(block, block.shape[dim] - width, None, axis...  20.5 us
    all_to_all x1, waiting for transfers between devices, fetch_regions(): received = lax.all_to_all(sent, axis, 0, 0, tiled=True)  15.6 us
    ppermute x3, waiting for transfers between devices, tree_sum(): joined = keep + lax.ppermute(send, axis, pairs)  14 us
    dot_general x10, matrix products, query_grads(): jnp.einsum('abhqk,abkhe->abqhe', grad_score, split_heads(key_part), prefe...  11.3 us
    ppermute x2, waiting for transfers between devices, tree_sum(): joined = joined + lax.ppermute(joined, axis, pairs)  10.8 us
    ppermute x3, waiting for transfers between devices, doubling_gather(): got = lax.ppermute(joined, axis, pairs)  9.77 us
    unnamed x196, local copies, waits for them, and re-layouts  9.39 us
    ppermute x6, waiting for transfers between devices, padded(): lax.ppermute(lax.slice_in_dim(block, 0, width, axis=dim), axis, backward)  8.84 us
  transfers between devices with their start and end apart: 22, of which 12 were waited for; matrix products, arithmetic and copies ran while one was open for 13% of the time, Pallas kernels for 0%

profile of v7, /device:TPU:0, one launch (start us, length us, event | category | flops | bytes accessed | tf_op | source)
XLA Modules:
  0.0 179.7 jit_solution(9401210925703053083)
XLA Ops:
  3.5 7.3 %all-to-all-start = ((s32[8,1,2]{2,1,0:T(1,128)}), s32[8,1,2]{2,1,0:T(1,128)S(1)}, u32[]{:S(2)}, u32[]{:S(2)}) async-start(s32[8,1,2]{2,1,0:T(1,128)} %copy.566), calls=%async_computation | async-start | bytes 8192 | tf_op jit(solution)/shard_map/all_to_all | solution.py:246
  10.8 1.3 convolution_convert_fusion
  12.1 1.3 collective-permute-start.1
  13.4 4.6 %collective-permute-start = (bf16[8,16,512]{2,1,0:T(8,128)(2,1)S(1)}, bf16[8,16,512]{2,1,0:T(8,128)(2,1)S(1)}, u32[]{:S(2)}, u32[]{:S(2)}) collective-permute-start(bf16[8,16,512]{2,1,0:T(8,128)(2,1)S(1)} %bitcast.513), channel_id=1, source_target_pairs={{0,4},{4,8},{8,12},{12,16},{16,20},{20,24},{24,28},{1,5},{5,9},{9,... | collective-permute-start | bytes 393224 | tf_op jit(solution)/shard_map/ppermute | solution.py:24
  18.4 4.8 %collective-permute-start.4 = (bf16[8,16,512]{2,1,0:T(8,128)(2,1)S(1)}, bf16[8,16,512]{2,1,0:T(8,128)(2,1)S(1)}, u32[]{:S(2)}, u32[]{:S(2)}) collective-permute-start(bf16[8,16,512]{2,1,0:T(8,128)(2,1)S(1)} %get-tuple-element.67), channel_id=1, source_target_pairs={{0,4},{4,8},{8,12},{12,16},{16,20},{20,24},{24,28},{1,5},{5,9},{9,... | collective-permute-start | bytes 393224 | tf_op jit(solution)/shard_map/ppermute | solution.py:24
  23.2 1.3 collective-permute-start.5
  28.3 1.8 collective-permute-done.5
  30.2 2.0 %collective-permute-start.6 = (bf16[32,8,512]{2,1,0:T(8,128)(2,1)S(1)}, bf16[32,8,512]{2,1,0:T(8,128)(2,1)}, u32[]{:S(2)}, u32[]{:S(2)}) collective-permute-start(bf16[32,8,512]{2,1,0:T(8,128)(2,1)S(1)} %get-tuple-element.59), channel_id=1, source_target_pairs={{0,1},{1,2},{2,3},{4,5},{5,6},{6,7},{8,9},{9,10},{10,11},{12,13},{... | collective-permute-start | bytes 786440 | tf_op jit(solution)/shard_map/ppermute | solution.py:24
  32.2 1.3 collective-permute-start.7
  34.4 4.8 %collective-permute-start.2 = (bf16[32,8,512]{2,1,0:T(8,128)(2,1)}, bf16[32,8,512]{2,1,0:T(8,128)(2,1)}, u32[]{:S(2)}, u32[]{:S(2)}) collective-permute-start(bf16[32,8,512]{2,1,0:T(8,128)(2,1)} %get-tuple-element.63), channel_id=1, source_target_pairs={{0,1},{1,2},{2,3},{4,5},{5,6},{6,7},{8,9},{9,10},{10,11},{12,13},{... | collective-permute-start | bytes 786440 | tf_op jit(solution)/shard_map/ppermute | solution.py:24
  39.2 1.3 collective-permute-start.3
  40.5 1.1 broadcast_select_fusion
  41.6 4.5 %all-to-all-start.1 = ((bf16[8,2,64,512]{3,2,1,0:T(8,128)(2,1)}), bf16[8,2,64,512]{3,2,1,0:T(8,128)(2,1)}, u32[]{:S(2)}, u32[]{:S(2)}) async-start(bf16[8,2,64,512]{3,2,1,0:T(8,128)(2,1)} %broadcast_select_fusion), calls=%async_computation.1 | async-start | bytes 2097152 | tf_op jit(solution)/shard_map/all_to_all | solution.py:249
  46.2 1.1 pad_maximum_fusion.1
  47.5 1.1 pad_maximum_fusion
  48.7 1.2 slice_bitcast_fusion.18
  56.4 1.5 slice_bitcast_fusion
  57.9 15.6 %all-to-all-done.1 = bf16[8,2,64,512]{3,2,1,0:T(8,128)(2,1)} async-done(((bf16[8,2,64,512]{3,2,1,0:T(8,128)(2,1)}), bf16[8,2,64,512]{3,2,1,0:T(8,128)(2,1)}, u32[]{:S(2)}, u32[]{:S(2)}) %all-to-all-start.1) | async-done | bytes 1048608 | tf_op jit(solution)/shard_map/all_to_all | solution.py:249
  73.6 1.8 %gather_fusion.1 = bf16[8,64,512]{2,1,0:T(8,128)(2,1)S(1)} fusion(bf16[16,64,512]{2,1,0:T(8,128)(2,1)} %bitcast.15, s32[1024]{0:T(1024)S(1)} %pad_clamp_fusion), kind=kCustom, calls=%fused_computation.1 | custom fusion | bytes 1048608 | tf_op jit(solution)/shard_map/jit(_take)/gather | solution.py:251
  76.6 1.2 fusion.449
  83.3 1.0 multiply_reduce_fusion
  84.3 2.1 %fusion.84 = f32[2,2,2,128,64]{3,4,2,1,0:T(8,128)} fusion(f32[2,2,2,64,64]{3,4,2,1,0:T(8,128)S(1)} %get-tuple-element.119, f32[2,2,2,64]{3,2,1,0:T(2,128)S(1)} %bitcast.481, f32[2,2,2,64]{3,2,1,0:T(2,128)S(1)} %log_add_fusion, bf16[2,2,8,2,8,128]{5,4,3,2,1,0:T(8,128)(2,1)} %copy-done.57, bf16[2,2,8,2,8,128]{5,4,3,2,1,0:T(8,128)(2,1)} %get-tuple-element.52, ...), kind=kOutput, calls=%fused_computation.166 | convolution fusion | flops 16908288 | bytes 790528 | tf_op jit(solution)/shard_map/abhqk,abkhe->abqhe/dot_general | solution.py:116
  86.4 2.2 %convolution_add_fusion.24 = f32[2,2,2,128,64]{3,4,2,1,0:T(8,128)} fusion(f32[2,2,2,128,64]{3,4,2,1,0:T(8,128)} %fusion.84, f32[2,2,2,64,64]{3,4,2,1,0:T(8,128)S(1)} %get-tuple-element.121, f32[2,2,2,64]{3,2,1,0:T(2,128)S(1)} %bitcast.483, f32[2,2,2,64]{3,2,1,0:T(2,128)S(1)} %log_add_fusion, bf16[2,2,8,2,8,128]{5,4,3,2,1,0:T(8,128)(2,1)} %get-tuple-element.42, ...), kind=kOutput, calls=%fused_computation.99 | convolution fusion | flops 16973824 | bytes 1052672 | tf_op jit(solution)/shard_map/abhqk,abkhe->abqhe/dot_general | solution.py:116
  88.6 1.4 convolution_add_fusion.23
  90.0 1.3 convolution_add_fusion.22
  91.4 1.3 convolution_add_fusion.21
  92.8 1.3 convolution_add_fusion.20
  96.2 2.9 %collective-permute-start.8 = (f32[8,16,4]{1,0,2:T(8,128)S(1)}, f32[8,16,4]{1,0,2:T(8,128)S(1)}, u32[]{:S(2)}, u32[]{:S(2)}) collective-permute-start(f32[8,16,4]{1,0,2:T(8,128)S(1)} %slice.413), channel_id=1, source_target_pairs={{0,4},{4,8},{8,12},{12,16},{16,20},{20,24},{24,28},{1,5},{5,9},{9,... | collective-permute-start | bytes 6152 | tf_op jit(solution)/shard_map/ppermute | solution.py:24
  100.9 1.3 collective-permute-start.9
  102.2 4.3 %collective-permute-done.9 = f32[8,16,4]{1,0,2:T(8,128)S(1)} collective-permute-done((f32[8,16,4]{1,0,2:T(8,128)S(1)}, f32[8,16,4]{1,0,2:T(8,128)S(1)}, u32[]{:S(2)}, u32[]{:S(2)}) %collective-permute-start.9) | collective-permute-done | bytes 2080 | tf_op jit(solution)/shard_map/ppermute | solution.py:27
  106.6 1.4 collective-permute-start.10
  108.1 1.5 collective-permute-start.11
  110.5 2.8 %collective-permute-done.11 = f32[32,8,4]{1,0,2:T(8,128)S(1)} collective-permute-done((f32[32,8,4]{1,0,2:T(8,128)S(1)}, f32[32,8,4]{1,0,2:T(8,128)S(1)}, u32[]{:S(2)}, u32[]{:S(2)}) %collective-permute-start.11) | collective-permute-done | bytes 4128 | tf_op jit(solution)/shard_map/ppermute | solution.py:27
  121.6 1.6 convert_element_type.223
  123.2 1.6 copy.727
  124.8 2.0 %convolution_add_fusion.15 = f32[2,2,2,128,64]{3,4,2,1,0:T(8,128)} fusion(f32[2,2,2,128,64]{3,4,2,1,0:T(8,128)S(1)} %fusion.82, f32[2,2,2,64,64]{3,4,2,1,0:T(8,128)} %copy-done.28, f32[2,2,2,64]{3,2,1,0:T(2,128)} %get-tuple-element.89, bf16[2,2,8,2,8,128]{5,4,3,2,1,0:T(8,128)(2,1)S(1)} %copy-done.10, bf16[2,2,8,2,8,128]{5,4,3,2,1,0:T(8,128)(2,1)} %get-tuple-element.32, ...), kind=kOutput, calls=%fused_computation.19 | convolution fusion | flops 16941056 | bytes 1050624 | tf_op jit(solution)/shard_map/abhqk,abqhe->abkhe/dot_general | solution.py:155
  126.8 1.4 convolution_add_fusion.14
  128.3 1.7 convolution_add_fusion.13
  130.0 1.4 convolution_add_fusion.12
  134.1 3.0 %collective-permute-start.12 = (f32[512,256]{1,0:T(8,128)S(1)}, f32[512,256]{1,0:T(8,128)S(1)}, u32[]{:S(2)}, u32[]{:S(2)}) collective-permute-start(f32[512,256]{1,0:T(8,128)S(1)} %constant_dynamic-slice_fusion.2), channel_id=1, source_target_pairs={{0,1},{1,0},{2,3},{3,2},{4,5},{5,4},{6,7},{7,6},{8,9},{9,8},{10,11... | collective-permute-start | bytes 1572872 | tf_op jit(solution)/shard_map/ppermute | solution.py:223
  137.1 1.5 collective-permute-done.12
  139.1 8.4 %collective-permute-done.13 = f32[256,256]{1,0:T(8,128)S(1)} collective-permute-done((f32[256,256]{1,0:T(8,128)S(1)}, f32[256,256]{1,0:T(8,128)S(1)}, u32[]{:S(2)}, u32[]{:S(2)}) %collective-permute-start.13) | collective-permute-done | bytes 262176 | tf_op jit(solution)/shard_map/ppermute | solution.py:223
  148.5 4.1 %collective-permute-done.14 = f32[128,256]{1,0:T(8,128)S(1)} collective-permute-done((f32[128,256]{1,0:T(8,128)S(1)}, f32[128,256]{1,0:T(8,128)S(1)}, u32[]{:S(2)}, u32[]{:S(2)}) %collective-permute-start.14) | collective-permute-done | bytes 131104 | tf_op jit(solution)/shard_map/ppermute | solution.py:223
  152.6 5.0 %collective-permute-done.15 = f32[128,256]{1,0:T(8,128)S(1)} collective-permute-done((f32[128,256]{1,0:T(8,128)S(1)}, f32[128,256]{1,0:T(8,128)S(1)}, u32[]{:S(2)}, u32[]{:S(2)}) %collective-permute-start.15) | collective-permute-done | bytes 131104 | tf_op jit(solution)/shard_map/ppermute | solution.py:226
  158.6 5.8 %collective-permute-done.16 = f32[128,256]{1,0:T(8,128)S(1)} collective-permute-done((f32[128,256]{1,0:T(8,128)S(1)}, f32[128,256]{1,0:T(8,128)S(1)}, u32[]{:S(2)}, u32[]{:S(2)}) %collective-permute-start.16) | collective-permute-done | bytes 131104 | tf_op jit(solution)/shard_map/ppermute | solution.py:226
  164.4 1.3 collective-permute-start.17
  165.7 3.7 %collective-permute-done.17 = f32[128,256]{1,0:T(8,128)S(1)} collective-permute-done((f32[128,256]{1,0:T(8,128)S(1)}, f32[128,256]{1,0:T(8,128)S(1)}, u32[]{:S(2)}, u32[]{:S(2)}) %collective-permute-start.17) | collective-permute-done | bytes 131104 | tf_op jit(solution)/shard_map/ppermute | solution.py:188
  170.0 6.0 %collective-permute-done.18 = f32[256,256]{1,0:T(8,128)S(1)} collective-permute-done((f32[256,256]{1,0:T(8,128)S(1)}, f32[256,256]{1,0:T(8,128)S(1)}, u32[]{:S(2)}, u32[]{:S(2)}) %collective-permute-start.18) | collective-permute-done | bytes 262176 | tf_op jit(solution)/shard_map/ppermute | solution.py:188
  (357 shorter events, 43.0 us)
Async XLA Ops:
  0.6 27.1 %copy-start = (bf16[1,1,4,64,512]{4,3,2,1,0:T(8,128)(2,1)S(1)}, bf16[1,1,4,64,512]{4,3,2,1,0:T(8,128)(2,1)}, u32[]{:S(2)}) copy-start(bf16[1,1,4,64,512]{4,3,2,1,0:T(8,128)(2,1)} %param.14) | copy-start | bytes 786436
  0.6 17.3 %copy-start.1 = (bf16[16,16,256]{2,1,0:T(8,128)(2,1)S(1)}, bf16[16,16,256]{2,1,0:T(8,128)(2,1)}, u32[]{:S(2)}) copy-start(bf16[16,16,256]{2,1,0:T(8,128)(2,1)} %param.9) | copy-start | bytes 393220
  0.7 17.3 %copy-start.69 = (bf16[256,256]{1,0:T(8,128)(2,1)S(1)}, bf16[256,256]{1,0:T(8,128)(2,1)}, u32[]{:S(2)}) copy-start(bf16[256,256]{1,0:T(8,128)(2,1)} %param.10) | copy-start | bytes 393220
  0.7 17.5 %copy-start.31 = (bf16[256,256]{1,0:T(8,128)(2,1)S(1)}, bf16[256,256]{1,0:T(8,128)(2,1)}, u32[]{:S(2)}) copy-start(bf16[256,256]{1,0:T(8,128)(2,1)} %param.13) | copy-start | bytes 393220
  0.7 17.5 %copy-start.59 = (bf16[16,16,256]{2,1,0:T(8,128)(2,1)S(1)}, bf16[16,16,256]{2,1,0:T(8,128)(2,1)}, u32[]{:S(2)}) copy-start(bf16[16,16,256]{2,1,0:T(8,128)(2,1)} %param.17) | copy-start | bytes 393220
  3.5 22.7 %all-to-all-start = ((s32[8,1,2]{2,1,0:T(1,128)}), s32[8,1,2]{2,1,0:T(1,128)S(1)}, u32[]{:S(2)}, u32[]{:S(2)}) async-start(s32[8,1,2]{2,1,0:T(1,128)} %copy.566), calls=%async_computation | async-start | bytes 8192 | tf_op jit(solution)/shard_map/all_to_all | solution.py:246
  12.0 12.5 %copy-start.74 = (s32[1,1,4,2]{2,3,1,0:T(2,128)S(1)}, s32[1,1,4,2]{2,3,1,0:T(2,128)}, u32[]{:S(2)}) copy-start(s32[1,1,4,2]{2,3,1,0:T(2,128)} %param.15) | copy-start | bytes 100
  12.1 21.4 %collective-permute-start.1 = (bf16[8,16,512]{2,1,0:T(8,128)(2,1)S(1)}, bf16[8,16,512]{2,1,0:T(8,128)(2,1)S(1)}, u32[]{:S(2)}, u32[]{:S(2)}) collective-permute-start(bf16[8,16,512]{2,1,0:T(8,128)(2,1)S(1)} %bitcast.514), channel_id=1, source_target_pairs={{4,0},{8,4},{12,8},{16,12},{20,16},{24,20},{28,24},{5,1},{9,5},{13... | collective-permute-start | bytes 393224 | tf_op jit(solution)/shard_map/ppermute | solution.py:27
  13.4 20.1 %collective-permute-start = (bf16[8,16,512]{2,1,0:T(8,128)(2,1)S(1)}, bf16[8,16,512]{2,1,0:T(8,128)(2,1)S(1)}, u32[]{:S(2)}, u32[]{:S(2)}) collective-permute-start(bf16[8,16,512]{2,1,0:T(8,128)(2,1)S(1)} %bitcast.513), channel_id=1, source_target_pairs={{0,4},{4,8},{8,12},{12,16},{16,20},{20,24},{24,28},{1,5},{5,9},{9,... | collective-permute-start | bytes 393224 | tf_op jit(solution)/shard_map/ppermute | solution.py:24
  18.4 9.9 %collective-permute-start.4 = (bf16[8,16,512]{2,1,0:T(8,128)(2,1)S(1)}, bf16[8,16,512]{2,1,0:T(8,128)(2,1)S(1)}, u32[]{:S(2)}, u32[]{:S(2)}) collective-permute-start(bf16[8,16,512]{2,1,0:T(8,128)(2,1)S(1)} %get-tuple-element.67), channel_id=1, source_target_pairs={{0,4},{4,8},{8,12},{12,16},{16,20},{20,24},{24,28},{1,5},{5,9},{9,... | collective-permute-start | bytes 393224 | tf_op jit(solution)/shard_map/ppermute | solution.py:24
  23.2 6.9 %collective-permute-start.5 = (bf16[8,16,512]{2,1,0:T(8,128)(2,1)S(1)}, bf16[8,16,512]{2,1,0:T(8,128)(2,1)S(1)}, u32[]{:S(2)}, u32[]{:S(2)}) collective-permute-start(bf16[8,16,512]{2,1,0:T(8,128)(2,1)S(1)} %get-tuple-element.68), channel_id=1, source_target_pairs={{4,0},{8,4},{12,8},{16,12},{20,16},{24,20},{28,24},{5,1},{9,5},{13... | collective-permute-start | bytes 393224 | tf_op jit(solution)/shard_map/ppermute | solution.py:27
  26.1 24.0 %copy-start.91 = (pred[2,2]{1,0:T(4,128)(4,1)}, pred[2,2]{1,0:T(4,128)(4,1)S(1)}, u32[]{:S(2)}) copy-start(pred[2,2]{1,0:T(4,128)(4,1)S(1)} %get-tuple-element.94) | copy-start | bytes 16
  26.2 29.4 %copy-start.58 = (bf16[2,2,64,2,128]{4,3,2,1,0:T(2,128)(2,1)}, bf16[2,2,64,2,128]{4,3,2,1,0:T(2,128)(2,1)S(1)}, u32[]{:S(2)}) copy-start(bf16[2,2,64,2,128]{4,3,2,1,0:T(2,128)(2,1)S(1)} %reshape_reshape.29) | copy-start | bytes 393220
  30.2 16.0 %collective-permute-start.6 = (bf16[32,8,512]{2,1,0:T(8,128)(2,1)S(1)}, bf16[32,8,512]{2,1,0:T(8,128)(2,1)}, u32[]{:S(2)}, u32[]{:S(2)}) collective-permute-start(bf16[32,8,512]{2,1,0:T(8,128)(2,1)S(1)} %get-tuple-element.59), channel_id=1, source_target_pairs={{0,1},{1,2},{2,3},{4,5},{5,6},{6,7},{8,9},{9,10},{10,11},{12,13},{... | collective-permute-start | bytes 786440 | tf_op jit(solution)/shard_map/ppermute | solution.py:24
  32.2 14.0 %collective-permute-start.7 = (bf16[32,8,512]{2,1,0:T(8,128)(2,1)S(1)}, bf16[32,8,512]{2,1,0:T(8,128)(2,1)}, u32[]{:S(2)}, u32[]{:S(2)}) collective-permute-start(bf16[32,8,512]{2,1,0:T(8,128)(2,1)S(1)} %get-tuple-element.60), channel_id=1, source_target_pairs={{1,0},{2,1},{3,2},{5,4},{6,5},{7,6},{9,8},{10,9},{11,10},{13,12},{... | collective-permute-start | bytes 786440 | tf_op jit(solution)/shard_map/ppermute | solution.py:27
  34.4 13.1 %collective-permute-start.2 = (bf16[32,8,512]{2,1,0:T(8,128)(2,1)}, bf16[32,8,512]{2,1,0:T(8,128)(2,1)}, u32[]{:S(2)}, u32[]{:S(2)}) collective-permute-start(bf16[32,8,512]{2,1,0:T(8,128)(2,1)} %get-tuple-element.63), channel_id=1, source_target_pairs={{0,1},{1,2},{2,3},{4,5},{5,6},{6,7},{8,9},{9,10},{10,11},{12,13},{... | collective-permute-start | bytes 786440 | tf_op jit(solution)/shard_map/ppermute | solution.py:24
  39.2 8.2 %collective-permute-start.3 = (bf16[32,8,512]{2,1,0:T(8,128)(2,1)}, bf16[32,8,512]{2,1,0:T(8,128)(2,1)}, u32[]{:S(2)}, u32[]{:S(2)}) collective-permute-start(bf16[32,8,512]{2,1,0:T(8,128)(2,1)} %get-tuple-element.64), channel_id=1, source_target_pairs={{1,0},{2,1},{3,2},{5,4},{6,5},{7,6},{9,8},{10,9},{11,10},{13,12},{... | collective-permute-start | bytes 786440 | tf_op jit(solution)/shard_map/ppermute | solution.py:27
  41.6 31.9 %all-to-all-start.1 = ((bf16[8,2,64,512]{3,2,1,0:T(8,128)(2,1)}), bf16[8,2,64,512]{3,2,1,0:T(8,128)(2,1)}, u32[]{:S(2)}, u32[]{:S(2)}) async-start(bf16[8,2,64,512]{3,2,1,0:T(8,128)(2,1)} %broadcast_select_fusion), calls=%async_computation.1 | async-start | bytes 2097152 | tf_op jit(solution)/shard_map/all_to_all | solution.py:249
  50.0 4.0 %copy-start.56 = (bf16[2,2,8,2,8,128]{5,4,3,2,1,0:T(8,128)(2,1)}, bf16[2,2,8,2,8,128]{5,4,3,2,1,0:T(8,128)(2,1)S(1)}, u32[]{:S(2)}) copy-start(bf16[2,2,8,2,8,128]{5,4,3,2,1,0:T(8,128)(2,1)S(1)} %get-tuple-element.50) | copy-start | bytes 393220
  50.0 4.8 %copy-start.57 = (bf16[2,2,8,2,8,128]{5,4,3,2,1,0:T(8,128)(2,1)}, bf16[2,2,8,2,8,128]{5,4,3,2,1,0:T(8,128)(2,1)S(1)}, u32[]{:S(2)}) copy-start(bf16[2,2,8,2,8,128]{5,4,3,2,1,0:T(8,128)(2,1)S(1)} %get-tuple-element.51) | copy-start | bytes 393220
  50.0 5.6 %copy-start.40 = (bf16[2,2,8,2,8,128]{5,4,3,2,1,0:T(8,128)(2,1)}, bf16[2,2,8,2,8,128]{5,4,3,2,1,0:T(8,128)(2,1)S(1)}, u32[]{:S(2)}) copy-start(bf16[2,2,8,2,8,128]{5,4,3,2,1,0:T(8,128)(2,1)S(1)} %get-tuple-element.47) | copy-start | bytes 393220
  50.7 3.3 %copy-start.77 = (pred[2,2]{1,0:T(4,128)(4,1)S(1)}, pred[2,2]{1,0:T(4,128)(4,1)}, u32[]{:S(2)}) copy-start(pred[2,2]{1,0:T(4,128)(4,1)} %get-tuple-element.93) | copy-start | bytes 16
  51.5 3.3 %copy-start.93 = (pred[2,2]{1,0:T(4,128)(4,1)S(1)}, pred[2,2]{1,0:T(4,128)(4,1)}, u32[]{:S(2)}) copy-start(pred[2,2]{1,0:T(4,128)(4,1)} %get-tuple-element.101) | copy-start | bytes 16
  86.4 3.7 %copy-start.21 = (bf16[2,2,8,2,8,128]{5,4,3,2,1,0:T(8,128)(2,1)S(1)}, bf16[2,2,8,2,8,128]{5,4,3,2,1,0:T(8,128)(2,1)}, u32[]{:S(2)}) copy-start(bf16[2,2,8,2,8,128]{5,4,3,2,1,0:T(8,128)(2,1)} %get-tuple-element.40) | copy-start | bytes 393220
  95.6 3.6 %copy-start.66 = (bf16[2,2,64,2,128]{4,2,3,1,0:T(8,128)(2,1)S(1)}, bf16[2,2,64,2,128]{4,2,3,1,0:T(8,128)(2,1)}, u32[]{:S(2)}) copy-start(bf16[2,2,64,2,128]{4,2,3,1,0:T(8,128)(2,1)} %get-tuple-element.123) | copy-start | bytes 393220
  95.6 3.9 %copy-start.60 = (bf16[16,16,256]{2,1,0:T(8,128)(2,1)S(1)}, bf16[16,16,256]{2,1,0:T(8,128)(2,1)}, u32[]{:S(2)}) copy-start(bf16[16,16,256]{2,1,0:T(8,128)(2,1)} %param.17) | copy-start | bytes 393220
  96.2 6.0 %collective-permute-start.8 = (f32[8,16,4]{1,0,2:T(8,128)S(1)}, f32[8,16,4]{1,0,2:T(8,128)S(1)}, u32[]{:S(2)}, u32[]{:S(2)}) collective-permute-start(f32[8,16,4]{1,0,2:T(8,128)S(1)} %slice.413), channel_id=1, source_target_pairs={{0,4},{4,8},{8,12},{12,16},{16,20},{20,24},{24,28},{1,5},{5,9},{9,... | collective-permute-start | bytes 6152 | tf_op jit(solution)/shard_map/ppermute | solution.py:24
  100.7 12.6 %copy-start.61 = (bf16[2,8,2,8,256]{4,3,2,1,0:T(8,128)(2,1)}, bf16[2,8,2,8,256]{4,3,2,1,0:T(8,128)(2,1)S(1)}, u32[]{:S(2)}) copy-start(bf16[2,8,2,8,256]{4,3,2,1,0:T(8,128)(2,1)S(1)} %copy.646) | copy-start | bytes 393220
  100.9 5.6 %collective-permute-start.9 = (f32[8,16,4]{1,0,2:T(8,128)S(1)}, f32[8,16,4]{1,0,2:T(8,128)S(1)}, u32[]{:S(2)}, u32[]{:S(2)}) collective-permute-start(f32[8,16,4]{1,0,2:T(8,128)S(1)} %slice.415), channel_id=1, source_target_pairs={{4,0},{8,4},{12,8},{16,12},{20,16},{24,20},{28,24},{5,1},{9,5},{13... | collective-permute-start | bytes 6152 | tf_op jit(solution)/shard_map/ppermute | solution.py:27
  106.6 7.7 %copy-start.41 = (bf16[2,2,8,2,8,128]{5,4,3,2,1,0:T(8,128)(2,1)S(1)}, bf16[2,2,8,2,8,128]{5,4,3,2,1,0:T(8,128)(2,1)}, u32[]{:S(2)}) copy-start(bf16[2,2,8,2,8,128]{5,4,3,2,1,0:T(8,128)(2,1)} %copy-done.40) | copy-start | bytes 393220
  106.6 7.7 %copy-start.46 = (bf16[2,2,8,2,8,128]{5,4,3,2,1,0:T(8,128)(2,1)S(1)}, bf16[2,2,8,2,8,128]{5,4,3,2,1,0:T(8,128)(2,1)}, u32[]{:S(2)}) copy-start(bf16[2,2,8,2,8,128]{5,4,3,2,1,0:T(8,128)(2,1)} %get-tuple-element.34) | copy-start | bytes 393220
  106.6 7.7 %copy-start.94 = (pred[2,2]{1,0:T(4,128)(4,1)S(1)}, pred[2,2]{1,0:T(4,128)(4,1)}, u32[]{:S(2)}) copy-start(pred[2,2]{1,0:T(4,128)(4,1)} %get-tuple-element.101) | copy-start | bytes 16
  106.6 3.9 %collective-permute-start.10 = (f32[32,8,4]{1,0,2:T(8,128)S(1)}, f32[32,8,4]{1,0,2:T(8,128)S(1)}, u32[]{:S(2)}, u32[]{:S(2)}) collective-permute-start(f32[32,8,4]{1,0,2:T(8,128)S(1)} %get-tuple-element.71), channel_id=1, source_target_pairs={{0,1},{1,2},{2,3},{4,5},{5,6},{6,7},{8,9},{9,10},{10,11},{12,13},{... | collective-permute-start | bytes 12296 | tf_op jit(solution)/shard_map/ppermute | solution.py:24
  108.1 5.2 %collective-permute-start.11 = (f32[32,8,4]{1,0,2:T(8,128)S(1)}, f32[32,8,4]{1,0,2:T(8,128)S(1)}, u32[]{:S(2)}, u32[]{:S(2)}) collective-permute-start(f32[32,8,4]{1,0,2:T(8,128)S(1)} %get-tuple-element.72), channel_id=1, source_target_pairs={{1,0},{2,1},{3,2},{5,4},{6,5},{7,6},{9,8},{10,9},{11,10},{13,12},{... | collective-permute-start | bytes 12296 | tf_op jit(solution)/shard_map/ppermute | solution.py:27
  110.5 4.1 %copy-start.11 = (bf16[2,2,8,2,8,128]{5,4,3,2,1,0:T(8,128)(2,1)S(1)}, bf16[2,2,8,2,8,128]{5,4,3,2,1,0:T(8,128)(2,1)}, u32[]{:S(2)}) copy-start(bf16[2,2,8,2,8,128]{5,4,3,2,1,0:T(8,128)(2,1)} %get-tuple-element.33) | copy-start | bytes 393220
  134.1 4.5 %collective-permute-start.12 = (f32[512,256]{1,0:T(8,128)S(1)}, f32[512,256]{1,0:T(8,128)S(1)}, u32[]{:S(2)}, u32[]{:S(2)}) collective-permute-start(f32[512,256]{1,0:T(8,128)S(1)} %constant_dynamic-slice_fusion.2), channel_id=1, source_target_pairs={{0,1},{1,0},{2,3},{3,2},{4,5},{5,4},{6,7},{7,6},{8,9},{9,8},{10,11... | collective-permute-start | bytes 1572872 | tf_op jit(solution)/shard_map/ppermute | solution.py:223
  138.8 8.7 %collective-permute-start.13 = (f32[256,256]{1,0:T(8,128)S(1)}, f32[256,256]{1,0:T(8,128)S(1)}, u32[]{:S(2)}, u32[]{:S(2)}) collective-permute-start(f32[256,256]{1,0:T(8,128)S(1)} %constant_dynamic-slice_fusion.1), channel_id=1, source_target_pairs={{0,2},{1,3},{2,0},{3,1},{4,6},{5,7},{6,4},{7,5},{8,10},{9,11},{10,... | collective-permute-start | bytes 786440 | tf_op jit(solution)/shard_map/ppermute | solution.py:223
  147.5 5.0 %collective-permute-start.14 = (f32[128,256]{1,0:T(8,128)S(1)}, f32[128,256]{1,0:T(8,128)S(1)}, u32[]{:S(2)}, u32[]{:S(2)}) collective-permute-start(f32[128,256]{1,0:T(8,128)S(1)} %constant_dynamic-slice_fusion), channel_id=1, source_target_pairs={{0,4},{4,0},{8,12},{12,8},{16,20},{20,16},{24,28},{28,24},{1,5},{5... | collective-permute-start | bytes 393224 | tf_op jit(solution)/shard_map/ppermute | solution.py:223
  152.6 5.0 %collective-permute-start.15 = (f32[128,256]{1,0:T(8,128)S(1)}, f32[128,256]{1,0:T(8,128)S(1)}, u32[]{:S(2)}, u32[]{:S(2)}) collective-permute-start(f32[128,256]{1,0:T(8,128)S(1)} %dynamic-slice_add_fusion.2), channel_id=1, source_target_pairs={{0,8},{4,12},{8,0},{12,4},{16,24},{20,28},{24,16},{28,20},{1,9},{5... | collective-permute-start | bytes 393224 | tf_op jit(solution)/shard_map/ppermute | solution.py:226
  157.6 6.8 %collective-permute-start.16 = (f32[128,256]{1,0:T(8,128)S(1)}, f32[128,256]{1,0:T(8,128)S(1)}, u32[]{:S(2)}, u32[]{:S(2)}) collective-permute-start(f32[128,256]{1,0:T(8,128)S(1)} %add.404), channel_id=1, source_target_pairs={{0,16},{4,20},{8,24},{12,28},{16,0},{20,4},{24,8},{28,12},{1,17},{... | collective-permute-start | bytes 393224 | tf_op jit(solution)/shard_map/ppermute | solution.py:226
  164.4 5.0 %collective-permute-start.17 = (f32[128,256]{1,0:T(8,128)S(1)}, f32[128,256]{1,0:T(8,128)S(1)}, u32[]{:S(2)}, u32[]{:S(2)}) collective-permute-start(f32[128,256]{1,0:T(8,128)S(1)} %add.405), channel_id=1, source_target_pairs={{0,4},{4,0},{8,12},{12,8},{16,20},{20,16},{24,28},{28,24},{1,5},{5... | collective-permute-start | bytes 393224 | tf_op jit(solution)/shard_map/ppermute | solution.py:188
  169.5 6.4 %collective-permute-start.18 = (f32[256,256]{1,0:T(8,128)S(1)}, f32[256,256]{1,0:T(8,128)S(1)}, u32[]{:S(2)}, u32[]{:S(2)}) collective-permute-start(f32[256,256]{1,0:T(8,128)S(1)} %pad_maximum_fusion.6), channel_id=1, source_target_pairs={{0,2},{1,3},{2,0},{3,1},{4,6},{5,7},{6,4},{7,5},{8,10},{9,11},{10,... | collective-permute-start | bytes 786440 | tf_op jit(solution)/shard_map/ppermute | solution.py:188
  169.9 6.2 %copy-start.32 = (bf16[256,256]{1,0:T(8,128)(2,1)S(1)}, bf16[256,256]{1,0:T(8,128)(2,1)}, u32[]{:S(2)}) copy-start(bf16[256,256]{1,0:T(8,128)(2,1)} %param.13) | copy-start | bytes 393220
  169.9 7.0 %copy-start.62 = (bf16[2,8,2,8,256]{4,3,2,1,0:T(8,128)(2,1)S(1)}, bf16[2,8,2,8,256]{4,3,2,1,0:T(8,128)(2,1)}, u32[]{:S(2)}) copy-start(bf16[2,8,2,8,256]{4,3,2,1,0:T(8,128)(2,1)} %copy-done.61) | copy-start | bytes 393220
  169.9 7.0 %copy-start.67 = (bf16[256,256]{1,0:T(8,128)(2,1)S(1)}, bf16[256,256]{1,0:T(8,128)(2,1)}, u32[]{:S(2)}) copy-start(bf16[256,256]{1,0:T(8,128)(2,1)} %param.12) | copy-start | bytes 393220
  169.9 7.0 %copy-start.68 = (bf16[256,256]{1,0:T(8,128)(2,1)S(1)}, bf16[256,256]{1,0:T(8,128)(2,1)}, u32[]{:S(2)}) copy-start(bf16[256,256]{1,0:T(8,128)(2,1)} %param.11) | copy-start | bytes 393220
  169.9 7.0 %copy-start.70 = (bf16[256,256]{1,0:T(8,128)(2,1)S(1)}, bf16[256,256]{1,0:T(8,128)(2,1)}, u32[]{:S(2)}) copy-start(bf16[256,256]{1,0:T(8,128)(2,1)} %param.10) | copy-start | bytes 393220
  176.0 2.0 %collective-permute-start.19 = (f32[512,256]{1,0:T(8,128)S(1)}, f32[512,256]{1,0:T(8,128)S(1)}, u32[]{:S(2)}, u32[]{:S(2)}) collective-permute-start(f32[512,256]{1,0:T(8,128)S(1)} %pad_maximum_fusion.5), channel_id=1, source_target_pairs={{0,1},{1,0},{2,3},{3,2},{4,5},{5,4},{6,7},{7,6},{8,9},{9,8},{10,11... | collective-permute-start | bytes 1572872 | tf_op jit(solution)/shard_map/ppermute | solution.py:188
  (69 other events, 95.4 us)

commit v8 on v7

--- a/solution.py
+++ b/solution.py
@@ -236,18 +236,21 @@
 def fetch_regions(memory_local, owners, local_ids, axis):
     count = lax.axis_size(axis)
     entries = owners.shape[0]
+    me = lax.axis_index(axis)
     order = jnp.arange(entries)
-    same = owners[:, None] == owners[None, :]
-    rank = jnp.sum(same & (order[None, :] < order[:, None]), axis=1)
-    wanted = (owners[:, None, None] == jnp.arange(count)[None, :, None]) & (
-        rank[:, None, None] == jnp.arange(CAP)[None, None, :]
-    )
-    requests = jnp.sum(jnp.where(wanted, local_ids[:, None, None], 0), axis=0)
-    asked = lax.all_to_all(requests, axis, 0, 0, tiled=True)
+    earlier = order[None, :] < order[:, None]
+    tables, slot_of = tree_gather(jnp.stack([owners, local_ids])[None], axis)
+    tables = tables[jnp.array([slot_of(device) for device in range(count)])]
+    mine = tables[:, 0] == me
+    rank_here = jnp.sum(mine[:, None, :] & earlier[None], axis=2)
+    wanted = mine[:, :, None] & (rank_here[:, :, None] == jnp.arange(CAP)[None, None, :])
+    asked = jnp.sum(jnp.where(wanted, tables[:, 1][:, :, None], 0), axis=1)
     sent = jnp.take(memory_local, asked.reshape(-1), axis=0)
     sent = sent.reshape((count, CAP) + memory_local.shape[1:])
     received = lax.all_to_all(sent, axis, 0, 0, tiled=True)
     received = received.reshape((count * CAP,) + memory_local.shape[1:])
+    same = owners[:, None] == owners[None, :]
+    rank = jnp.sum(same & earlier, axis=1)
     return jnp.take(received, owners * CAP + rank, axis=0)
 
 

time: 181 us -> 176 us (0.972)
  waiting for transfers between devices: 58.9 us -> 46.6 us
  matrix products: 39.1 us -> 49.1 us
  starting transfers between devices: 47.3 us -> 52.7 us
  local copies, waits for them, and re-layouts: 25 us -> 19.9 us
  other arithmetic: 6.87 us -> 4.43 us
    all_to_all x1, waiting for transfers between devices: 15.6 us -> 3.64 us  [fetch_regions(): received = lax.all_to_all(sent, axis, 0, 0, tiled=True)]
    ppermute x3 -> x6, starting transfers between devices: 1.81 us -> 11.6 us  [doubling_gather(): got = lax.ppermute(joined, axis, pairs)]
    dot_general x9, matrix products: 8.16 us -> 16 us  [key_grads(): jnp.einsum('abhqk,abqhe->abkhe', grad_score, query_heads, preferred_eleme...]
    all_to_all x1 -> x0, starting transfers between devices: 7.25 us -> none  [fetch_regions(): asked = lax.all_to_all(requests, axis, 0, 0, tiled=True)]
    ppermute x3 -> x6, waiting for transfers between devices: 9.77 us -> 13.8 us  [doubling_gather(): got = lax.ppermute(joined, axis, pairs)]
    ppermute x2, starting transfers between devices: 1.03 us -> 3.83 us  [tree_sum(): joined = joined + lax.ppermute(joined, axis, pairs)]
    ppermute x2, waiting for transfers between devices: 10.8 us -> 8.54 us  [tree_sum(): joined = joined + lax.ppermute(joined, axis, pairs)]
    convert_element_type x2, local copies, waits for them, and re-layouts: 2.44 us -> 0.23 us  [key_grads(): return (grad_key, grad_value.reshape(out_shape).astype(jnp.bfloat16))]
  transfers between devices with their start and end apart: 22 -> 24, of which waited for: 12 -> 13; matrix products, arithmetic and copies ran while one was open for 13% -> 11% of each run, Pallas kernels for 0% -> 0%
where the time goes in v8:
time: 176 us; the launch traced here: 175 us
  starting transfers between devices  52.7 us (30%)
  matrix products  49.1 us (28%)
  waiting for transfers between devices  46.6 us (26%)
  local copies, waits for them, and re-layouts  19.9 us (11%)
  other arithmetic  4.43 us (3%)
  between operations  2.51 us (1%)
    ppermute x6, starting transfers between devices, padded(): lax.ppermute(lax.slice_in_dim(block, block.shape[dim] - width, None, axis...  19.2 us
    dot_general x9, matrix products, key_grads(): jnp.einsum('abhqk,abqhe->abkhe', grad_score, query_heads, preferred_eleme...  16 us
    ppermute x6, waiting for transfers between devices, doubling_gather(): got = lax.ppermute(joined, axis, pairs)  13.8 us
    ppermute x3, waiting for transfers between devices, tree_sum(): joined = keep + lax.ppermute(send, axis, pairs)  13.1 us
    dot_general x10, matrix products, query_grads(): jnp.einsum('abhqk,abkhe->abqhe', grad_score, split_heads(key_part), prefe...  12.1 us
    ppermute x6, starting transfers between devices, doubling_gather(): got = lax.ppermute(joined, axis, pairs)  11.6 us
    ppermute x2, waiting for transfers between devices, tree_sum(): joined = joined + lax.ppermute(joined, axis, pairs)  8.54 us
    unnamed x195, local copies, waits for them, and re-layouts  8.31 us
  transfers between devices with their start and end apart: 24, of which 13 were waited for; matrix products, arithmetic and copies ran while one was open for 11% of the time, Pallas kernels for 0%

profile of v8, /device:TPU:0, one launch (start us, length us, event | category | flops | bytes accessed | tf_op | source)
XLA Modules:
  0.0 175.2 jit_solution(1969298678006648352)
XLA Ops:
  2.5 4.1 %collective-permute-start.4 = (s32[1,2,8]{2,1,0:T(2,128)S(1)}, s32[1,2,8]{2,1,0:T(2,128)S(1)}, u32[]{:S(2)}, u32[]{:S(2)}) collective-permute-start(s32[1,2,8]{2,1,0:T(2,128)S(1)} %add_bitcast_fusion), channel_id=1, source_target_pairs={{0,16},{4,20},{8,24},{12,28},{16,0},{20,4},{24,8},{28,12},{1,17},{... | collective-permute-start | bytes 200 | tf_op jit(solution)/shard_map/ppermute | solution.py:188
  7.9 3.4 %collective-permute-start = (bf16[8,16,512]{2,1,0:T(8,128)(2,1)S(1)}, bf16[8,16,512]{2,1,0:T(8,128)(2,1)S(1)}, u32[]{:S(2)}, u32[]{:S(2)}) collective-permute-start(bf16[8,16,512]{2,1,0:T(8,128)(2,1)S(1)} %bitcast.521), channel_id=1, source_target_pairs={{0,4},{4,8},{8,12},{12,16},{16,20},{20,24},{24,28},{1,5},{5,9},{9,... | collective-permute-start | bytes 393224 | tf_op jit(solution)/shard_map/ppermute | solution.py:24
  11.3 1.3 collective-permute-start.1
  13.1 4.6 %collective-permute-start.7 = (bf16[8,16,512]{2,1,0:T(8,128)(2,1)S(1)}, bf16[8,16,512]{2,1,0:T(8,128)(2,1)S(1)}, u32[]{:S(2)}, u32[]{:S(2)}) collective-permute-start(bf16[8,16,512]{2,1,0:T(8,128)(2,1)S(1)} %get-tuple-element.67), channel_id=1, source_target_pairs={{0,4},{4,8},{8,12},{12,16},{16,20},{20,24},{24,28},{1,5},{5,9},{9,... | collective-permute-start | bytes 393224 | tf_op jit(solution)/shard_map/ppermute | solution.py:24
  17.6 1.3 collective-permute-start.8
  20.5 4.6 %collective-permute-start.5 = (s32[2,2,8]{2,1,0:T(2,128)S(1)}, s32[2,2,8]{2,1,0:T(2,128)S(1)}, u32[]{:S(2)}, u32[]{:S(2)}) collective-permute-start(s32[2,2,8]{2,1,0:T(2,128)S(1)} %pad_add_fusion.2), channel_id=1, source_target_pairs={{0,8},{4,12},{8,0},{12,4},{16,24},{20,28},{24,16},{28,20},{1,9},{5... | collective-permute-start | bytes 392 | tf_op jit(solution)/shard_map/ppermute | solution.py:188
  25.1 1.6 collective-permute-done.5
  27.3 3.0 %collective-permute-done.6 = s32[4,2,8]{2,1,0:T(2,128)S(1)} collective-permute-done((s32[4,2,8]{2,1,0:T(2,128)S(1)}, s32[4,2,8]{2,1,0:T(2,128)S(1)}, u32[]{:S(2)}, u32[]{:S(2)}) %collective-permute-start.6) | collective-permute-done | bytes 288 | tf_op jit(solution)/shard_map/ppermute | solution.py:188
  33.4 4.2 %all-to-all-start = ((bf16[8,2,64,512]{3,2,1,0:T(8,128)(2,1)}), bf16[8,2,64,512]{3,2,1,0:T(8,128)(2,1)}, u32[]{:S(2)}, u32[]{:S(2)}) async-start(bf16[8,2,64,512]{3,2,1,0:T(8,128)(2,1)} %broadcast_select_fusion), calls=%async_computation | async-start | bytes 2097152 | tf_op jit(solution)/shard_map/all_to_all | solution.py:250
  37.7 1.3 collective-permute-start.2
  39.1 1.3 collective-permute-start.3
  40.5 1.3 collective-permute-start.10
  41.8 5.4 %collective-permute-start.9 = (bf16[32,8,512]{2,1,0:T(8,128)(2,1)S(1)}, bf16[32,8,512]{2,1,0:T(8,128)(2,1)S(1)}, u32[]{:S(2)}, u32[]{:S(2)}) collective-permute-start(bf16[32,8,512]{2,1,0:T(8,128)(2,1)S(1)} %get-tuple-element.59), channel_id=1, source_target_pairs={{0,1},{1,2},{2,3},{4,5},{5,6},{6,7},{8,9},{9,10},{10,11},{12,13},{... | collective-permute-start | bytes 786440 | tf_op jit(solution)/shard_map/ppermute | solution.py:24
  55.6 1.5 slice_bitcast_fusion
  57.1 3.6 %all-to-all-done = bf16[8,2,64,512]{3,2,1,0:T(8,128)(2,1)} async-done(((bf16[8,2,64,512]{3,2,1,0:T(8,128)(2,1)}), bf16[8,2,64,512]{3,2,1,0:T(8,128)(2,1)}, u32[]{:S(2)}, u32[]{:S(2)}) %all-to-all-start) | async-done | bytes 1048608 | tf_op jit(solution)/shard_map/all_to_all | solution.py:250
  60.7 1.8 %gather_fusion.2 = bf16[8,64,512]{2,1,0:T(8,128)(2,1)S(1)} fusion(bf16[16,64,512]{2,1,0:T(8,128)(2,1)} %bitcast.15, s32[1024]{0:T(1024)S(1)} %pad_clamp_fusion), kind=kCustom, calls=%fused_computation.2 | custom fusion | bytes 1048608 | tf_op jit(solution)/shard_map/jit(_take)/gather | solution.py:254
  64.8 1.8 %copy.403 = bf16[2,2,128,256]{2,3,1,0:T(8,128)(2,1)} copy(bf16[2,2,128,256]{3,2,1,0:T(8,128)(2,1)} %get-tuple-element.61) | data formatting | bytes 524288 | tf_op jit(solution)/shard_map/slice | solution.py:62
  73.0 2.1 %fusion.84 = f32[2,2,2,128,64]{3,4,2,1,0:T(8,128)} fusion(f32[2,2,2,64,64]{3,4,2,1,0:T(8,128)S(1)} %get-tuple-element.125, f32[2,2,2,64]{3,2,1,0:T(2,128)S(1)} %bitcast.488, f32[2,2,2,64]{3,2,1,0:T(2,128)S(1)} %log_add_fusion, bf16[2,2,8,2,8,128]{5,4,3,2,1,0:T(8,128)(2,1)} %copy-done.59, bf16[2,2,8,2,8,128]{5,4,3,2,1,0:T(8,128)(2,1)} %get-tuple-element.52, ...), kind=kOutput, calls=%fused_computation.167 | convolution fusion | flops 16908288 | bytes 790528 | tf_op jit(solution)/shard_map/abhqk,abkhe->abqhe/dot_general | solution.py:116
  75.1 2.2 %convolution_add_fusion.24 = f32[2,2,2,128,64]{3,4,2,1,0:T(8,128)} fusion(f32[2,2,2,128,64]{3,4,2,1,0:T(8,128)} %fusion.84, f32[2,2,2,64,64]{3,4,2,1,0:T(8,128)S(1)} %get-tuple-element.127, f32[2,2,2,64]{3,2,1,0:T(2,128)S(1)} %bitcast.490, f32[2,2,2,64]{3,2,1,0:T(2,128)S(1)} %log_add_fusion, bf16[2,2,8,2,8,128]{5,4,3,2,1,0:T(8,128)(2,1)} %get-tuple-element.42, ...), kind=kOutput, calls=%fused_computation.100 | convolution fusion | flops 16973824 | bytes 1052672 | tf_op jit(solution)/shard_map/abhqk,abkhe->abqhe/dot_general | solution.py:116
  77.4 1.4 convolution_add_fusion.23
  78.8 2.0 %convolution_add_fusion.22 = f32[2,2,2,128,64]{3,4,2,1,0:T(8,128)} fusion(f32[2,2,2,128,64]{3,4,2,1,0:T(8,128)S(1)} %convolution_add_fusion.23, f32[2,2,2,64,64]{3,4,2,1,0:T(8,128)S(1)} %get-tuple-element.121, f32[2,2,2,64]{3,2,1,0:T(2,128)S(1)} %bitcast.492, f32[2,2,2,64]{3,2,1,0:T(2,128)S(1)} %log_add_fusion, ...), kind=kOutput, calls=%fused_computation.94 | convolution fusion | flops 16973824 | bytes 1052672 | tf_op jit(solution)/shard_map/abhqk,abkhe->abqhe/dot_general | solution.py:116
  80.9 1.4 convolution_add_fusion.21
  82.3 1.3 convolution_add_fusion.20
  86.0 3.1 %collective-permute-start.11 = (f32[8,16,4]{1,0,2:T(8,128)S(1)}, f32[8,16,4]{1,0,2:T(8,128)S(1)}, u32[]{:S(2)}, u32[]{:S(2)}) collective-permute-start(f32[8,16,4]{1,0,2:T(8,128)S(1)} %slice.421), channel_id=1, source_target_pairs={{0,4},{4,8},{8,12},{12,16},{16,20},{20,24},{24,28},{1,5},{5,9},{9,... | collective-permute-start | bytes 6152 | tf_op jit(solution)/shard_map/ppermute | solution.py:24
  90.4 1.3 collective-permute-start.12
  92.0 4.0 %collective-permute-done.12 = f32[8,16,4]{1,0,2:T(8,128)S(1)} collective-permute-done((f32[8,16,4]{1,0,2:T(8,128)S(1)}, f32[8,16,4]{1,0,2:T(8,128)S(1)}, u32[]{:S(2)}, u32[]{:S(2)}) %collective-permute-start.12) | collective-permute-done | bytes 2080 | tf_op jit(solution)/shard_map/ppermute | solution.py:27
  96.1 1.4 collective-permute-start.13
  97.6 1.5 collective-permute-start.14
  100.0 3.5 %collective-permute-done.14 = f32[32,8,4]{1,0,2:T(8,128)S(1)} collective-permute-done((f32[32,8,4]{1,0,2:T(8,128)S(1)}, f32[32,8,4]{1,0,2:T(8,128)S(1)}, u32[]{:S(2)}, u32[]{:S(2)}) %collective-permute-start.14) | collective-permute-done | bytes 4128 | tf_op jit(solution)/shard_map/ppermute | solution.py:27
  108.4 2.0 %convolution_add_fusion.15 = f32[2,2,2,128,64]{3,4,2,1,0:T(8,128)} fusion(f32[2,2,2,128,64]{3,4,2,1,0:T(8,128)S(1)} %fusion.82, f32[2,2,2,64,64]{3,4,2,1,0:T(8,128)S(1)} %fusion.32, f32[2,2,2,64]{3,2,1,0:T(2,128)} %get-tuple-element.89, bf16[2,2,8,2,8,128]{5,4,3,2,1,0:T(8,128)(2,1)S(1)} %copy-done.10, bf16[2,2,8,2,8,128]{5,4,3,2,1,0:T(8,128)(2,1)} %get-tuple-element.32, ...), kind=kOutput, calls=%fused_computation.20 | convolution fusion | flops 16941056 | bytes 1050624 | tf_op jit(solution)/shard_map/abhqk,abqhe->abkhe/dot_general | solution.py:155
  110.4 2.2 %convolution_add_fusion.14 = f32[2,2,2,128,64]{3,4,2,1,0:T(8,128)} fusion(f32[2,2,2,128,64]{3,4,2,1,0:T(8,128)} %convolution_add_fusion.15, f32[2,2,2,64,64]{3,4,2,1,0:T(8,128)} %fusion.28, f32[2,2,2,64]{3,2,1,0:T(2,128)} %get-tuple-element.87, bf16[2,2,8,2,8,128]{5,4,3,2,1,0:T(8,128)(2,1)S(1)} %copy-done.9, ...), kind=kOutput, calls=%fused_computation.19 | convolution fusion | flops 16941056 | bytes 1050624 | tf_op jit(solution)/shard_map/abhqk,abqhe->abkhe/dot_general | solution.py:155
  112.5 2.1 %convolution_add_fusion.13 = f32[2,2,2,128,64]{3,4,2,1,0:T(8,128)} fusion(f32[2,2,2,128,64]{3,4,2,1,0:T(8,128)} %convolution_add_fusion.14, f32[2,2,2,64,64]{3,4,2,1,0:T(8,128)S(1)} %fusion.24, f32[2,2,2,64]{3,2,1,0:T(2,128)} %get-tuple-element.85, bf16[2,2,8,2,8,128]{5,4,3,2,1,0:T(8,128)(2,1)S(1)} %copy-done.8, ...), kind=kOutput, calls=%fused_computation.18 | convolution fusion | flops 16941056 | bytes 1050624 | tf_op jit(solution)/shard_map/abhqk,abqhe->abkhe/dot_general | solution.py:155
  114.6 2.1 %convolution_add_fusion.12 = f32[2,2,2,128,64]{3,4,2,1,0:T(8,128)} fusion(f32[2,2,2,128,64]{3,4,2,1,0:T(8,128)} %convolution_add_fusion.13, f32[2,2,2,64,64]{3,4,2,1,0:T(8,128)S(1)} %fusion.20, f32[2,2,2,64]{3,2,1,0:T(2,128)} %get-tuple-element.83, bf16[2,2,8,2,8,128]{5,4,3,2,1,0:T(8,128)(2,1)S(1)} %copy-done.7, ...), kind=kOutput, calls=%fused_computation.17 | convolution fusion | flops 16941056 | bytes 1050624 | tf_op jit(solution)/shard_map/abhqk,abqhe->abkhe/dot_general | solution.py:155
  116.7 2.1 %convolution_add_fusion.11 = f32[2,2,2,128,64]{3,4,2,1,0:T(8,128)} fusion(f32[2,2,2,128,64]{3,4,2,1,0:T(8,128)} %convolution_add_fusion.12, f32[2,2,2,64,64]{3,4,2,1,0:T(8,128)S(1)} %fusion.16, f32[2,2,2,64]{3,2,1,0:T(2,128)S(1)} %get-tuple-element.81, bf16[2,2,8,2,8,128]{5,4,3,2,1,0:T(8,128)(2,1)S(1)} %copy-done.6, ...), kind=kOutput, calls=%fused_computation.16 | convolution fusion | flops 16941056 | bytes 1050624 | tf_op jit(solution)/shard_map/abhqk,abqhe->abkhe/dot_general | solution.py:155
  118.8 2.0 %convolution_add_fusion.10 = f32[2,2,2,128,64]{3,4,2,1,0:T(8,128)} fusion(f32[2,2,2,128,64]{3,4,2,1,0:T(8,128)} %convolution_add_fusion.11, f32[2,2,2,64,64]{3,4,2,1,0:T(8,128)S(1)} %fusion.12, f32[2,2,2,64]{3,2,1,0:T(2,128)S(1)} %get-tuple-element.79, bf16[2,2,8,2,8,128]{5,4,3,2,1,0:T(8,128)(2,1)S(1)} %copy-done.5, ...), kind=kOutput, calls=%fused_computation.15 | convolution fusion | flops 16941056 | bytes 1050624 | tf_op jit(solution)/shard_map/abhqk,abqhe->abkhe/dot_general | solution.py:155
  120.8 2.0 %convolution_add_fusion.9 = f32[2,2,2,128,64]{3,4,2,1,0:T(8,128)} fusion(f32[2,2,2,128,64]{3,4,2,1,0:T(8,128)} %convolution_add_fusion.10, f32[2,2,2,64,64]{3,4,2,1,0:T(8,128)S(1)} %fusion.8, f32[2,2,2,64]{3,2,1,0:T(2,128)S(1)} %get-tuple-element.77, bf16[2,2,8,2,8,128]{5,4,3,2,1,0:T(8,128)(2,1)S(1)} %copy-done.4, ...), kind=kOutput, calls=%fused_computation.14 | convolution fusion | flops 16941056 | bytes 1050624 | tf_op jit(solution)/shard_map/abhqk,abqhe->abkhe/dot_general | solution.py:155
  128.4 3.0 %collective-permute-start.15 = (f32[512,256]{1,0:T(8,128)S(1)}, f32[512,256]{1,0:T(8,128)S(1)}, u32[]{:S(2)}, u32[]{:S(2)}) collective-permute-start(f32[512,256]{1,0:T(8,128)S(1)} %constant_dynamic-slice_fusion.1), channel_id=1, source_target_pairs={{0,1},{1,0},{2,3},{3,2},{4,5},{5,4},{6,7},{7,6},{8,9},{9,8},{10,11... | collective-permute-start | bytes 1572872 | tf_op jit(solution)/shard_map/ppermute | solution.py:223
  131.4 1.5 collective-permute-done.15
  133.3 8.4 %collective-permute-done.16 = f32[256,256]{1,0:T(8,128)S(1)} collective-permute-done((f32[256,256]{1,0:T(8,128)S(1)}, f32[256,256]{1,0:T(8,128)S(1)}, u32[]{:S(2)}, u32[]{:S(2)}) %collective-permute-start.16) | collective-permute-done | bytes 262176 | tf_op jit(solution)/shard_map/ppermute | solution.py:223
  141.7 2.5 %collective-permute-start.17 = (f32[128,256]{1,0:T(8,128)S(1)}, f32[128,256]{1,0:T(8,128)S(1)}, u32[]{:S(2)}, u32[]{:S(2)}) collective-permute-start(f32[128,256]{1,0:T(8,128)S(1)} %constant_dynamic-slice_fusion.2), channel_id=1, source_target_pairs={{0,4},{4,0},{8,12},{12,8},{16,20},{20,16},{24,28},{28,24},{1,5},{5... | collective-permute-start | bytes 393224 | tf_op jit(solution)/shard_map/ppermute | solution.py:223
  144.2 3.2 %collective-permute-done.17 = f32[128,256]{1,0:T(8,128)S(1)} collective-permute-done((f32[128,256]{1,0:T(8,128)S(1)}, f32[128,256]{1,0:T(8,128)S(1)}, u32[]{:S(2)}, u32[]{:S(2)}) %collective-permute-start.17) | collective-permute-done | bytes 131104 | tf_op jit(solution)/shard_map/ppermute | solution.py:223
  147.5 1.5 collective-permute-start.18
  148.9 3.6 %collective-permute-done.18 = f32[128,256]{1,0:T(8,128)S(1)} collective-permute-done((f32[128,256]{1,0:T(8,128)S(1)}, f32[128,256]{1,0:T(8,128)S(1)}, u32[]{:S(2)}, u32[]{:S(2)}) %collective-permute-start.18) | collective-permute-done | bytes 131104 | tf_op jit(solution)/shard_map/ppermute | solution.py:226
  152.5 2.4 %collective-permute-start.19 = (f32[128,256]{1,0:T(8,128)S(1)}, f32[128,256]{1,0:T(8,128)S(1)}, u32[]{:S(2)}, u32[]{:S(2)}) collective-permute-start(f32[128,256]{1,0:T(8,128)S(1)} %add.419), channel_id=1, source_target_pairs={{0,16},{4,20},{8,24},{12,28},{16,0},{20,4},{24,8},{28,12},{1,17},{... | collective-permute-start | bytes 393224 | tf_op jit(solution)/shard_map/ppermute | solution.py:226
  154.9 5.0 %collective-permute-done.19 = f32[128,256]{1,0:T(8,128)S(1)} collective-permute-done((f32[128,256]{1,0:T(8,128)S(1)}, f32[128,256]{1,0:T(8,128)S(1)}, u32[]{:S(2)}, u32[]{:S(2)}) %collective-permute-start.19) | collective-permute-done | bytes 131104 | tf_op jit(solution)/shard_map/ppermute | solution.py:226
  159.9 1.8 %collective-permute-start.20 = (f32[128,256]{1,0:T(8,128)S(1)}, f32[128,256]{1,0:T(8,128)S(1)}, u32[]{:S(2)}, u32[]{:S(2)}) collective-permute-start(f32[128,256]{1,0:T(8,128)S(1)} %add.420), channel_id=1, source_target_pairs={{0,4},{4,0},{8,12},{12,8},{16,20},{20,16},{24,28},{28,24},{1,5},{5... | collective-permute-start | bytes 393224 | tf_op jit(solution)/shard_map/ppermute | solution.py:188
  161.7 3.2 %collective-permute-done.20 = f32[128,256]{1,0:T(8,128)S(1)} collective-permute-done((f32[128,256]{1,0:T(8,128)S(1)}, f32[128,256]{1,0:T(8,128)S(1)}, u32[]{:S(2)}, u32[]{:S(2)}) %collective-permute-start.20) | collective-permute-done | bytes 131104 | tf_op jit(solution)/shard_map/ppermute | solution.py:188
  165.5 6.0 %collective-permute-done.21 = f32[256,256]{1,0:T(8,128)S(1)} collective-permute-done((f32[256,256]{1,0:T(8,128)S(1)}, f32[256,256]{1,0:T(8,128)S(1)}, u32[]{:S(2)}, u32[]{:S(2)}) %collective-permute-start.21) | collective-permute-done | bytes 262176 | tf_op jit(solution)/shard_map/ppermute | solution.py:188
  (369 shorter events, 44.9 us)
Async XLA Ops:
  0.6 31.0 %copy-start = (bf16[1,1,4,64,512]{4,3,2,1,0:T(8,128)(2,1)S(1)}, bf16[1,1,4,64,512]{4,3,2,1,0:T(8,128)(2,1)}, u32[]{:S(2)}) copy-start(bf16[1,1,4,64,512]{4,3,2,1,0:T(8,128)(2,1)} %param.15) | copy-start | bytes 786436
  0.6 12.0 %copy-start.1 = (bf16[16,16,256]{2,1,0:T(8,128)(2,1)S(1)}, bf16[16,16,256]{2,1,0:T(8,128)(2,1)}, u32[]{:S(2)}) copy-start(bf16[16,16,256]{2,1,0:T(8,128)(2,1)} %param.10) | copy-start | bytes 393220
  0.7 12.0 %copy-start.70 = (bf16[256,256]{1,0:T(8,128)(2,1)S(1)}, bf16[256,256]{1,0:T(8,128)(2,1)}, u32[]{:S(2)}) copy-start(bf16[256,256]{1,0:T(8,128)(2,1)} %param.11) | copy-start | bytes 393220
  0.7 12.1 %copy-start.61 = (bf16[16,16,256]{2,1,0:T(8,128)(2,1)S(1)}, bf16[16,16,256]{2,1,0:T(8,128)(2,1)}, u32[]{:S(2)}) copy-start(bf16[16,16,256]{2,1,0:T(8,128)(2,1)} %param.18) | copy-start | bytes 393220
  0.7 12.1 %copy-start.35 = (bf16[256,256]{1,0:T(8,128)(2,1)S(1)}, bf16[256,256]{1,0:T(8,128)(2,1)}, u32[]{:S(2)}) copy-start(bf16[256,256]{1,0:T(8,128)(2,1)} %param.14) | copy-start | bytes 393220
  2.5 18.0 %collective-permute-start.4 = (s32[1,2,8]{2,1,0:T(2,128)S(1)}, s32[1,2,8]{2,1,0:T(2,128)S(1)}, u32[]{:S(2)}, u32[]{:S(2)}) collective-permute-start(s32[1,2,8]{2,1,0:T(2,128)S(1)} %add_bitcast_fusion), channel_id=1, source_target_pairs={{0,16},{4,20},{8,24},{12,28},{16,0},{20,4},{24,8},{28,12},{1,17},{... | collective-permute-start | bytes 200 | tf_op jit(solution)/shard_map/ppermute | solution.py:188
  7.8 11.3 %copy-start.73 = (s32[1,1,4,2]{2,3,1,0:T(2,128)S(1)}, s32[1,1,4,2]{2,3,1,0:T(2,128)}, u32[]{:S(2)}) copy-start(s32[1,1,4,2]{2,3,1,0:T(2,128)} %param.16) | copy-start | bytes 100
  7.8 11.4 %copy-start.93 = (s32[8]{0:T(128)S(1)}, s32[8]{0:T(128)}, u32[]{:S(2)}) copy-start(s32[8]{0:T(128)} %constant.165) | copy-start | bytes 100
  7.9 29.7 %collective-permute-start = (bf16[8,16,512]{2,1,0:T(8,128)(2,1)S(1)}, bf16[8,16,512]{2,1,0:T(8,128)(2,1)S(1)}, u32[]{:S(2)}, u32[]{:S(2)}) collective-permute-start(bf16[8,16,512]{2,1,0:T(8,128)(2,1)S(1)} %bitcast.521), channel_id=1, source_target_pairs={{0,4},{4,8},{8,12},{12,16},{16,20},{20,24},{24,28},{1,5},{5,9},{9,... | collective-permute-start | bytes 393224 | tf_op jit(solution)/shard_map/ppermute | solution.py:24
  11.3 26.3 %collective-permute-start.1 = (bf16[8,16,512]{2,1,0:T(8,128)(2,1)S(1)}, bf16[8,16,512]{2,1,0:T(8,128)(2,1)S(1)}, u32[]{:S(2)}, u32[]{:S(2)}) collective-permute-start(bf16[8,16,512]{2,1,0:T(8,128)(2,1)S(1)} %bitcast.520), channel_id=1, source_target_pairs={{4,0},{8,4},{12,8},{16,12},{20,16},{24,20},{28,24},{5,1},{9,5},{13... | collective-permute-start | bytes 393224 | tf_op jit(solution)/shard_map/ppermute | solution.py:27
  13.1 27.3 %collective-permute-start.7 = (bf16[8,16,512]{2,1,0:T(8,128)(2,1)S(1)}, bf16[8,16,512]{2,1,0:T(8,128)(2,1)S(1)}, u32[]{:S(2)}, u32[]{:S(2)}) collective-permute-start(bf16[8,16,512]{2,1,0:T(8,128)(2,1)S(1)} %get-tuple-element.67), channel_id=1, source_target_pairs={{0,4},{4,8},{8,12},{12,16},{16,20},{20,24},{24,28},{1,5},{5,9},{9,... | collective-permute-start | bytes 393224 | tf_op jit(solution)/shard_map/ppermute | solution.py:24
  17.6 22.7 %collective-permute-start.8 = (bf16[8,16,512]{2,1,0:T(8,128)(2,1)S(1)}, bf16[8,16,512]{2,1,0:T(8,128)(2,1)S(1)}, u32[]{:S(2)}, u32[]{:S(2)}) collective-permute-start(bf16[8,16,512]{2,1,0:T(8,128)(2,1)S(1)} %get-tuple-element.68), channel_id=1, source_target_pairs={{4,0},{8,4},{12,8},{16,12},{20,16},{24,20},{28,24},{5,1},{9,5},{13... | collective-permute-start | bytes 393224 | tf_op jit(solution)/shard_map/ppermute | solution.py:27
  20.1 34.6 %copy-start.60 = (bf16[2,2,64,2,128]{4,3,2,1,0:T(2,128)(2,1)}, bf16[2,2,64,2,128]{4,3,2,1,0:T(2,128)(2,1)S(1)}, u32[]{:S(2)}) copy-start(bf16[2,2,64,2,128]{4,3,2,1,0:T(2,128)(2,1)S(1)} %reshape_reshape.29) | copy-start | bytes 393220
  20.3 28.7 %copy-start.83 = (pred[2,2]{1,0:T(4,128)(4,1)}, pred[2,2]{1,0:T(4,128)(4,1)S(1)}, u32[]{:S(2)}) copy-start(pred[2,2]{1,0:T(4,128)(4,1)S(1)} %get-tuple-element.104) | copy-start | bytes 16
  20.3 29.3 %copy-start.75 = (pred[2,2]{1,0:T(4,128)(4,1)}, pred[2,2]{1,0:T(4,128)(4,1)S(1)}, u32[]{:S(2)}) copy-start(pred[2,2]{1,0:T(4,128)(4,1)S(1)} %get-tuple-element.100) | copy-start | bytes 16
  20.3 29.5 %copy-start.77 = (pred[2,2]{1,0:T(4,128)(4,1)}, pred[2,2]{1,0:T(4,128)(4,1)S(1)}, u32[]{:S(2)}) copy-start(pred[2,2]{1,0:T(4,128)(4,1)S(1)} %get-tuple-element.101) | copy-start | bytes 16
  20.3 30.3 %copy-start.79 = (pred[2,2]{1,0:T(4,128)(4,1)}, pred[2,2]{1,0:T(4,128)(4,1)S(1)}, u32[]{:S(2)}) copy-start(pred[2,2]{1,0:T(4,128)(4,1)S(1)} %get-tuple-element.102) | copy-start | bytes 16
  20.3 31.1 %copy-start.81 = (pred[2,2]{1,0:T(4,128)(4,1)}, pred[2,2]{1,0:T(4,128)(4,1)S(1)}, u32[]{:S(2)}) copy-start(pred[2,2]{1,0:T(4,128)(4,1)S(1)} %get-tuple-element.103) | copy-start | bytes 16
  20.3 31.9 %copy-start.85 = (pred[2,2]{1,0:T(4,128)(4,1)}, pred[2,2]{1,0:T(4,128)(4,1)S(1)}, u32[]{:S(2)}) copy-start(pred[2,2]{1,0:T(4,128)(4,1)S(1)} %get-tuple-element.105) | copy-start | bytes 16
  20.3 32.7 %copy-start.87 = (pred[2,2]{1,0:T(4,128)(4,1)}, pred[2,2]{1,0:T(4,128)(4,1)S(1)}, u32[]{:S(2)}) copy-start(pred[2,2]{1,0:T(4,128)(4,1)S(1)} %get-tuple-element.106) | copy-start | bytes 16
  20.3 33.6 %copy-start.89 = (pred[2,2]{1,0:T(4,128)(4,1)}, pred[2,2]{1,0:T(4,128)(4,1)S(1)}, u32[]{:S(2)}) copy-start(pred[2,2]{1,0:T(4,128)(4,1)S(1)} %get-tuple-element.99) | copy-start | bytes 16
  20.4 34.4 %copy-start.91 = (pred[2,2]{1,0:T(4,128)(4,1)}, pred[2,2]{1,0:T(4,128)(4,1)S(1)}, u32[]{:S(2)}) copy-start(pred[2,2]{1,0:T(4,128)(4,1)S(1)} %get-tuple-element.107) | copy-start | bytes 16
  20.5 6.2 %collective-permute-start.5 = (s32[2,2,8]{2,1,0:T(2,128)S(1)}, s32[2,2,8]{2,1,0:T(2,128)S(1)}, u32[]{:S(2)}, u32[]{:S(2)}) collective-permute-start(s32[2,2,8]{2,1,0:T(2,128)S(1)} %pad_add_fusion.2), channel_id=1, source_target_pairs={{0,8},{4,12},{8,0},{12,4},{16,24},{20,28},{24,16},{28,20},{1,9},{5... | collective-permute-start | bytes 392 | tf_op jit(solution)/shard_map/ppermute | solution.py:188
  26.6 3.7 %collective-permute-start.6 = (s32[4,2,8]{2,1,0:T(2,128)S(1)}, s32[4,2,8]{2,1,0:T(2,128)S(1)}, u32[]{:S(2)}, u32[]{:S(2)}) collective-permute-start(s32[4,2,8]{2,1,0:T(2,128)S(1)} %pad_add_fusion.1), channel_id=1, source_target_pairs={{0,4},{4,0},{8,12},{12,8},{16,20},{20,16},{24,28},{28,24},{1,5},{5... | collective-permute-start | bytes 776 | tf_op jit(solution)/shard_map/ppermute | solution.py:188
  33.4 27.3 %all-to-all-start = ((bf16[8,2,64,512]{3,2,1,0:T(8,128)(2,1)}), bf16[8,2,64,512]{3,2,1,0:T(8,128)(2,1)}, u32[]{:S(2)}, u32[]{:S(2)}) async-start(bf16[8,2,64,512]{3,2,1,0:T(8,128)(2,1)} %broadcast_select_fusion), calls=%async_computation | async-start | bytes 2097152 | tf_op jit(solution)/shard_map/all_to_all | solution.py:250
  37.7 9.5 %collective-permute-start.2 = (bf16[32,8,512]{2,1,0:T(8,128)(2,1)S(1)}, bf16[32,8,512]{2,1,0:T(8,128)(2,1)S(1)}, u32[]{:S(2)}, u32[]{:S(2)}) collective-permute-start(bf16[32,8,512]{2,1,0:T(8,128)(2,1)S(1)} %get-tuple-element.63), channel_id=1, source_target_pairs={{0,1},{1,2},{2,3},{4,5},{5,6},{6,7},{8,9},{9,10},{10,11},{12,13},{... | collective-permute-start | bytes 786440 | tf_op jit(solution)/shard_map/ppermute | solution.py:24
  39.1 8.2 %collective-permute-start.3 = (bf16[32,8,512]{2,1,0:T(8,128)(2,1)S(1)}, bf16[32,8,512]{2,1,0:T(8,128)(2,1)S(1)}, u32[]{:S(2)}, u32[]{:S(2)}) collective-permute-start(bf16[32,8,512]{2,1,0:T(8,128)(2,1)S(1)} %get-tuple-element.64), channel_id=1, source_target_pairs={{1,0},{2,1},{3,2},{5,4},{6,5},{7,6},{9,8},{10,9},{11,10},{13,12},{... | collective-permute-start | bytes 786440 | tf_op jit(solution)/shard_map/ppermute | solution.py:27
  40.5 8.3 %collective-permute-start.10 = (bf16[32,8,512]{2,1,0:T(8,128)(2,1)S(1)}, bf16[32,8,512]{2,1,0:T(8,128)(2,1)S(1)}, u32[]{:S(2)}, u32[]{:S(2)}) collective-permute-start(bf16[32,8,512]{2,1,0:T(8,128)(2,1)S(1)} %get-tuple-element.60), channel_id=1, source_target_pairs={{1,0},{2,1},{3,2},{5,4},{6,5},{7,6},{9,8},{10,9},{11,10},{13,12},{... | collective-permute-start | bytes 786440 | tf_op jit(solution)/shard_map/ppermute | solution.py:27
  41.8 7.0 %collective-permute-start.9 = (bf16[32,8,512]{2,1,0:T(8,128)(2,1)S(1)}, bf16[32,8,512]{2,1,0:T(8,128)(2,1)S(1)}, u32[]{:S(2)}, u32[]{:S(2)}) collective-permute-start(bf16[32,8,512]{2,1,0:T(8,128)(2,1)S(1)} %get-tuple-element.59), channel_id=1, source_target_pairs={{0,1},{1,2},{2,3},{4,5},{5,6},{6,7},{8,9},{9,10},{10,11},{12,13},{... | collective-permute-start | bytes 786440 | tf_op jit(solution)/shard_map/ppermute | solution.py:24
  85.9 13.1 %copy-start.62 = (bf16[16,16,256]{2,1,0:T(8,128)(2,1)S(1)}, bf16[16,16,256]{2,1,0:T(8,128)(2,1)}, u32[]{:S(2)}) copy-start(bf16[16,16,256]{2,1,0:T(8,128)(2,1)} %param.18) | copy-start | bytes 393220
  86.0 5.9 %collective-permute-start.11 = (f32[8,16,4]{1,0,2:T(8,128)S(1)}, f32[8,16,4]{1,0,2:T(8,128)S(1)}, u32[]{:S(2)}, u32[]{:S(2)}) collective-permute-start(f32[8,16,4]{1,0,2:T(8,128)S(1)} %slice.421), channel_id=1, source_target_pairs={{0,4},{4,8},{8,12},{12,16},{16,20},{20,24},{24,28},{1,5},{5,9},{9,... | collective-permute-start | bytes 6152 | tf_op jit(solution)/shard_map/ppermute | solution.py:24
  90.4 5.6 %collective-permute-start.12 = (f32[8,16,4]{1,0,2:T(8,128)S(1)}, f32[8,16,4]{1,0,2:T(8,128)S(1)}, u32[]{:S(2)}, u32[]{:S(2)}) collective-permute-start(f32[8,16,4]{1,0,2:T(8,128)S(1)} %slice.423), channel_id=1, source_target_pairs={{4,0},{8,4},{12,8},{16,12},{20,16},{24,20},{28,24},{5,1},{9,5},{13... | collective-permute-start | bytes 6152 | tf_op jit(solution)/shard_map/ppermute | solution.py:27
  96.1 8.4 %copy-start.48 = (bf16[2,2,8,2,8,128]{5,4,3,2,1,0:T(8,128)(2,1)S(1)}, bf16[2,2,8,2,8,128]{5,4,3,2,1,0:T(8,128)(2,1)}, u32[]{:S(2)}) copy-start(bf16[2,2,8,2,8,128]{5,4,3,2,1,0:T(8,128)(2,1)} %get-tuple-element.34) | copy-start | bytes 393220
  96.1 8.4 %copy-start.92 = (pred[2,2]{1,0:T(4,128)(4,1)S(1)}, pred[2,2]{1,0:T(4,128)(4,1)}, u32[]{:S(2)}) copy-start(pred[2,2]{1,0:T(4,128)(4,1)} %copy-done.91) | copy-start | bytes 16
  96.1 3.9 %collective-permute-start.13 = (f32[32,8,4]{1,0,2:T(8,128)S(1)}, f32[32,8,4]{1,0,2:T(8,128)S(1)}, u32[]{:S(2)}, u32[]{:S(2)}) collective-permute-start(f32[32,8,4]{1,0,2:T(8,128)S(1)} %get-tuple-element.71), channel_id=1, source_target_pairs={{0,1},{1,2},{2,3},{4,5},{5,6},{6,7},{8,9},{9,10},{10,11},{12,13},{... | collective-permute-start | bytes 12296 | tf_op jit(solution)/shard_map/ppermute | solution.py:24
  97.6 5.9 %collective-permute-start.14 = (f32[32,8,4]{1,0,2:T(8,128)S(1)}, f32[32,8,4]{1,0,2:T(8,128)S(1)}, u32[]{:S(2)}, u32[]{:S(2)}) collective-permute-start(f32[32,8,4]{1,0,2:T(8,128)S(1)} %get-tuple-element.72), channel_id=1, source_target_pairs={{1,0},{2,1},{3,2},{5,4},{6,5},{7,6},{9,8},{10,9},{11,10},{13,12},{... | collective-permute-start | bytes 12296 | tf_op jit(solution)/shard_map/ppermute | solution.py:27
  107.1 7.5 %copy-start.27 = (f32[2,2,2,64,64]{3,4,2,1,0:T(8,128)}, f32[2,2,2,64,64]{3,4,2,1,0:T(8,128)S(1)}, u32[]{:S(2)}) copy-start(f32[2,2,2,64,64]{3,4,2,1,0:T(8,128)S(1)} %fusion.20) | copy-start | bytes 393220
  128.4 4.5 %collective-permute-start.15 = (f32[512,256]{1,0:T(8,128)S(1)}, f32[512,256]{1,0:T(8,128)S(1)}, u32[]{:S(2)}, u32[]{:S(2)}) collective-permute-start(f32[512,256]{1,0:T(8,128)S(1)} %constant_dynamic-slice_fusion.1), channel_id=1, source_target_pairs={{0,1},{1,0},{2,3},{3,2},{4,5},{5,4},{6,7},{7,6},{8,9},{9,8},{10,11... | collective-permute-start | bytes 1572872 | tf_op jit(solution)/shard_map/ppermute | solution.py:223
  133.0 8.7 %collective-permute-start.16 = (f32[256,256]{1,0:T(8,128)S(1)}, f32[256,256]{1,0:T(8,128)S(1)}, u32[]{:S(2)}, u32[]{:S(2)}) collective-permute-start(f32[256,256]{1,0:T(8,128)S(1)} %constant_dynamic-slice_fusion), channel_id=1, source_target_pairs={{0,2},{1,3},{2,0},{3,1},{4,6},{5,7},{6,4},{7,5},{8,10},{9,11},{10,... | collective-permute-start | bytes 786440 | tf_op jit(solution)/shard_map/ppermute | solution.py:223
  141.7 5.7 %collective-permute-start.17 = (f32[128,256]{1,0:T(8,128)S(1)}, f32[128,256]{1,0:T(8,128)S(1)}, u32[]{:S(2)}, u32[]{:S(2)}) collective-permute-start(f32[128,256]{1,0:T(8,128)S(1)} %constant_dynamic-slice_fusion.2), channel_id=1, source_target_pairs={{0,4},{4,0},{8,12},{12,8},{16,20},{20,16},{24,28},{28,24},{1,5},{5... | collective-permute-start | bytes 393224 | tf_op jit(solution)/shard_map/ppermute | solution.py:223
  147.5 5.0 %collective-permute-start.18 = (f32[128,256]{1,0:T(8,128)S(1)}, f32[128,256]{1,0:T(8,128)S(1)}, u32[]{:S(2)}, u32[]{:S(2)}) collective-permute-start(f32[128,256]{1,0:T(8,128)S(1)} %dynamic-slice_add_fusion.2), channel_id=1, source_target_pairs={{0,8},{4,12},{8,0},{12,4},{16,24},{20,28},{24,16},{28,20},{1,9},{5... | collective-permute-start | bytes 393224 | tf_op jit(solution)/shard_map/ppermute | solution.py:226
  152.5 7.3 %collective-permute-start.19 = (f32[128,256]{1,0:T(8,128)S(1)}, f32[128,256]{1,0:T(8,128)S(1)}, u32[]{:S(2)}, u32[]{:S(2)}) collective-permute-start(f32[128,256]{1,0:T(8,128)S(1)} %add.419), channel_id=1, source_target_pairs={{0,16},{4,20},{8,24},{12,28},{16,0},{20,4},{24,8},{28,12},{1,17},{... | collective-permute-start | bytes 393224 | tf_op jit(solution)/shard_map/ppermute | solution.py:226
  159.9 5.0 %collective-permute-start.20 = (f32[128,256]{1,0:T(8,128)S(1)}, f32[128,256]{1,0:T(8,128)S(1)}, u32[]{:S(2)}, u32[]{:S(2)}) collective-permute-start(f32[128,256]{1,0:T(8,128)S(1)} %add.420), channel_id=1, source_target_pairs={{0,4},{4,0},{8,12},{12,8},{16,20},{20,16},{24,28},{28,24},{1,5},{5... | collective-permute-start | bytes 393224 | tf_op jit(solution)/shard_map/ppermute | solution.py:188
  165.0 6.4 %collective-permute-start.21 = (f32[256,256]{1,0:T(8,128)S(1)}, f32[256,256]{1,0:T(8,128)S(1)}, u32[]{:S(2)}, u32[]{:S(2)}) collective-permute-start(f32[256,256]{1,0:T(8,128)S(1)} %pad_maximum_fusion.6), channel_id=1, source_target_pairs={{0,2},{1,3},{2,0},{3,1},{4,6},{5,7},{6,4},{7,5},{8,10},{9,11},{10,... | collective-permute-start | bytes 786440 | tf_op jit(solution)/shard_map/ppermute | solution.py:188
  165.4 7.0 %copy-start.64 = (bf16[2,8,2,8,256]{4,3,2,1,0:T(8,128)(2,1)S(1)}, bf16[2,8,2,8,256]{4,3,2,1,0:T(8,128)(2,1)}, u32[]{:S(2)}) copy-start(bf16[2,8,2,8,256]{4,3,2,1,0:T(8,128)(2,1)} %copy-done.63) | copy-start | bytes 393220
  165.4 7.0 %copy-start.68 = (bf16[256,256]{1,0:T(8,128)(2,1)S(1)}, bf16[256,256]{1,0:T(8,128)(2,1)}, u32[]{:S(2)}) copy-start(bf16[256,256]{1,0:T(8,128)(2,1)} %param.13) | copy-start | bytes 393220
  165.4 7.0 %copy-start.69 = (bf16[256,256]{1,0:T(8,128)(2,1)S(1)}, bf16[256,256]{1,0:T(8,128)(2,1)}, u32[]{:S(2)}) copy-start(bf16[256,256]{1,0:T(8,128)(2,1)} %param.12) | copy-start | bytes 393220
  171.5 2.0 %collective-permute-start.22 = (f32[512,256]{1,0:T(8,128)S(1)}, f32[512,256]{1,0:T(8,128)S(1)}, u32[]{:S(2)}, u32[]{:S(2)}) collective-permute-start(f32[512,256]{1,0:T(8,128)S(1)} %pad_maximum_fusion.5), channel_id=1, source_target_pairs={{0,1},{1,0},{2,3},{3,2},{4,5},{5,4},{6,7},{7,6},{8,9},{9,8},{10,11... | collective-permute-start | bytes 1572872 | tf_op jit(solution)/shard_map/ppermute | solution.py:188
  (70 other events, 159.7 us)

commit v9 on v8

--- a/solution.py
+++ b/solution.py
@@ -233,7 +233,7 @@
     return tuple(out)
 
 
-def fetch_regions(memory_local, owners, local_ids, axis):
+def fetch_regions(memory_local, owners, local_ids, axis, ready):
     count = lax.axis_size(axis)
     entries = owners.shape[0]
     me = lax.axis_index(axis)
@@ -247,11 +247,12 @@
     asked = jnp.sum(jnp.where(wanted, tables[:, 1][:, :, None], 0), axis=1)
     sent = jnp.take(memory_local, asked.reshape(-1), axis=0)
     sent = sent.reshape((count, CAP) + memory_local.shape[1:])
+    sent, ready = lax.optimization_barrier((sent, ready))
     received = lax.all_to_all(sent, axis, 0, 0, tiled=True)
     received = received.reshape((count * CAP,) + memory_local.shape[1:])
     same = owners[:, None] == owners[None, :]
     rank = jnp.sum(same & earlier, axis=1)
-    return jnp.take(received, owners * CAP + rank, axis=0)
+    return jnp.take(received, owners * CAP + rank, axis=0), ready
 
 
 def on_device(
@@ -265,6 +266,12 @@
     queries = jnp.dot(flat_in, w_query, preferred_element_type=jnp.float32).astype(jnp.bfloat16)
     keyvals = jnp.dot(flat_in, w_pair, preferred_element_type=jnp.float32).astype(jnp.bfloat16)
     keyvals = keyvals.reshape(tile_rows, tile_cols, 2 * model_width)
+    owners = region_owner.reshape(2 * block_count)
+    local_ids = region_local.reshape(2 * block_count)
+    memory_local = region_memory.reshape(
+        region_memory.shape[2], region_memory.shape[3], region_memory.shape[4]
+    )
+    fetched, keyvals = fetch_regions(memory_local, owners, local_ids, "gx", keyvals)
     keyval_grid = padded(keyvals, (("gx", 0), ("gy", 1)), BSIDE)
     keyval_pad = to_blocks(keyval_grid)
     gx_count = lax.axis_size("gx")
@@ -274,12 +281,6 @@
     row_valid = (row_ids >= 0) & (row_ids < block_rows * gx_count)
     col_valid = (col_ids >= 0) & (col_ids < block_cols * gy_count)
     key_valid = row_valid[:, None] & col_valid[None, :]
-    owners = region_owner.reshape(2 * block_count)
-    local_ids = region_local.reshape(2 * block_count)
-    memory_local = region_memory.reshape(
-        region_memory.shape[2], region_memory.shape[3], region_memory.shape[4]
-    )
-    fetched = fetch_regions(memory_local, owners, local_ids, "gx")
     region_keyval = fetched.reshape(
         block_rows, block_cols, 2, memory_local.shape[1], memory_local.shape[2]
     )

time: 176 us -> 182 us (1.034)
  starting transfers between devices: 52.7 us -> 61.8 us
  matrix products: 49.1 us -> 40.2 us
  local copies, waits for them, and re-layouts: 19.9 us -> 21.9 us
    dot_general x9, matrix products: 16 us -> 7.56 us  [key_grads(): jnp.einsum('abhqk,abqhe->abkhe', grad_score, query_heads, preferred_eleme...]
    ppermute x6, waiting for transfers between devices: 0.02 us -> 5.33 us  [padded(): lax.ppermute(lax.slice_in_dim(block, block.shape[dim] - width, None, axis...]
    ppermute x3, starting transfers between devices: 5.8 us -> 10.5 us  [tree_sum(): joined = keep + lax.ppermute(send, axis, pairs)]
    ppermute x6, starting transfers between devices: 19.2 us -> 23.2 us  [padded(): lax.ppermute(lax.slice_in_dim(block, block.shape[dim] - width, None, axis...]
    all_to_all x1, waiting for transfers between devices: 3.64 us -> 0.01 us  [fetch_regions(): received = lax.all_to_all(sent, axis, 0, 0, tiled=True)]
    unnamed x195 -> x203, local copies, waits for them, and re-layouts: 8.31 us -> 9.89 us
  transfers between devices with their start and end apart: 24 -> 24, of which waited for: 13 -> 14; matrix products, arithmetic and copies ran while one was open for 11% -> 12% of each run, Pallas kernels for 0% -> 0%
where the time goes in v9:
time: 182 us; the launch traced here: 180 us
  starting transfers between devices  61.8 us (34%)
  waiting for transfers between devices  48.2 us (26%)
  matrix products  40.2 us (22%)
  local copies, waits for them, and re-layouts  21.9 us (12%)
  other arithmetic  5.38 us (3%)
  between operations  2.63 us (1%)
    ppermute x6, starting transfers between devices, padded(): lax.ppermute(lax.slice_in_dim(block, block.shape[dim] - width, None, axis...  23.2 us
    ppermute x6, waiting for transfers between devices, doubling_gather(): got = lax.ppermute(joined, axis, pairs)  13.1 us
    ppermute x3, waiting for transfers between devices, tree_sum(): joined = keep + lax.ppermute(send, axis, pairs)  13.1 us
    ppermute x6, starting transfers between devices, doubling_gather(): got = lax.ppermute(joined, axis, pairs)  11.7 us
    dot_general x10, matrix products, query_grads(): jnp.einsum('abhqk,abkhe->abqhe', grad_score, split_heads(key_part), prefe...  11.3 us
    ppermute x3, starting transfers between devices, tree_sum(): joined = keep + lax.ppermute(send, axis, pairs)  10.5 us
    unnamed x203, local copies, waits for them, and re-layouts  9.89 us
    ppermute x6, waiting for transfers between devices, padded(): lax.ppermute(lax.slice_in_dim(block, 0, width, axis=dim), axis, backward)  8.95 us
  transfers between devices with their start and end apart: 24, of which 14 were waited for; matrix products, arithmetic and copies ran while one was open for 12% of the time, Pallas kernels for 0%

profile of v9, /device:TPU:0, one launch (start us, length us, event | category | flops | bytes accessed | tf_op | source)
XLA Modules:
  0.0 180.2 jit_solution(11412184010641641406)
XLA Ops:
  2.5 4.1 %collective-permute-start = (s32[1,2,8]{2,1,0:T(2,128)S(1)}, s32[1,2,8]{2,1,0:T(2,128)S(1)}, u32[]{:S(2)}, u32[]{:S(2)}) collective-permute-start(s32[1,2,8]{2,1,0:T(2,128)S(1)} %add_bitcast_fusion), channel_id=1, source_target_pairs={{0,16},{4,20},{8,24},{12,28},{16,0},{20,4},{24,8},{28,12},{1,17},{... | collective-permute-start | bytes 200 | tf_op jit(solution)/shard_map/ppermute | solution.py:188
  9.0 3.4 %collective-permute-start.7 = (bf16[8,16,512]{2,1,0:T(8,128)(2,1)S(1)}, bf16[8,16,512]{2,1,0:T(8,128)(2,1)S(1)}, u32[]{:S(2)}, u32[]{:S(2)}) collective-permute-start(bf16[8,16,512]{2,1,0:T(8,128)(2,1)S(1)} %get-tuple-element.71), channel_id=1, source_target_pairs={{0,4},{4,8},{8,12},{12,16},{16,20},{20,24},{24,28},{1,5},{5,9},{9,... | collective-permute-start | bytes 393224 | tf_op jit(solution)/shard_map/ppermute | solution.py:24
  12.4 1.3 collective-permute-start.8
  15.9 3.7 %collective-permute-start.1 = (s32[2,2,8]{2,1,0:T(2,128)S(1)}, s32[2,2,8]{2,1,0:T(2,128)S(1)}, u32[]{:S(2)}, u32[]{:S(2)}) collective-permute-start(s32[2,2,8]{2,1,0:T(2,128)S(1)} %pad_add_fusion.2), channel_id=1, source_target_pairs={{0,8},{4,12},{8,0},{12,4},{16,24},{20,28},{24,16},{28,20},{1,9},{5... | collective-permute-start | bytes 392 | tf_op jit(solution)/shard_map/ppermute | solution.py:188
  19.7 1.5 collective-permute-done.1
  22.4 2.5 %collective-permute-done.2 = s32[4,2,8]{2,1,0:T(2,128)S(1)} collective-permute-done((s32[4,2,8]{2,1,0:T(2,128)S(1)}, s32[4,2,8]{2,1,0:T(2,128)S(1)}, u32[]{:S(2)}, u32[]{:S(2)}) %collective-permute-start.2) | collective-permute-done | bytes 288 | tf_op jit(solution)/shard_map/ppermute | solution.py:188
  27.9 4.3 %all-to-all-start = ((bf16[8,2,64,512]{3,2,1,0:T(8,128)(2,1)}), bf16[8,2,64,512]{3,2,1,0:T(8,128)(2,1)}, u32[]{:S(2)}, u32[]{:S(2)}) async-start(bf16[8,2,64,512]{3,2,1,0:T(8,128)(2,1)} %broadcast_select_fusion), calls=%async_computation | async-start | bytes 2097152 | tf_op jit(solution)/shard_map/all_to_all | solution.py:251
  32.2 1.3 collective-permute-start.4
  33.5 4.6 %collective-permute-start.3 = (bf16[8,16,512]{2,1,0:T(8,128)(2,1)S(1)}, bf16[8,16,512]{2,1,0:T(8,128)(2,1)S(1)}, u32[]{:S(2)}, u32[]{:S(2)}) collective-permute-start(bf16[8,16,512]{2,1,0:T(8,128)(2,1)S(1)} %get-tuple-element.74), channel_id=1, source_target_pairs={{0,4},{4,8},{8,12},{12,16},{16,20},{20,24},{24,28},{1,5},{5,9},{9,... | collective-permute-start | bytes 393224 | tf_op jit(solution)/shard_map/ppermute | solution.py:24
  38.2 1.3 collective-permute-start.9
  39.5 1.3 collective-permute-start.10
  40.8 5.3 %collective-permute-done.3 = bf16[8,16,512]{2,1,0:T(8,128)(2,1)S(1)} collective-permute-done((bf16[8,16,512]{2,1,0:T(8,128)(2,1)S(1)}, bf16[8,16,512]{2,1,0:T(8,128)(2,1)S(1)}, u32[]{:S(2)}, u32[]{:S(2)}) %collective-permute-start.3) | collective-permute-done | bytes 131104 | tf_op jit(solution)/shard_map/ppermute | solution.py:24
  46.3 1.3 collective-permute-start.5
  47.6 1.3 collective-permute-start.6
  49.1 1.6 slice_bitcast_fusion
  50.7 2.0 %collective-permute-done.6 = bf16[32,8,512]{2,1,0:T(8,128)(2,1)S(1)} collective-permute-done((bf16[32,8,512]{2,1,0:T(8,128)(2,1)S(1)}, bf16[32,8,512]{2,1,0:T(8,128)(2,1)S(1)}, u32[]{:S(2)}, u32[]{:S(2)}) %collective-permute-start.6) | collective-permute-done | bytes 262176 | tf_op jit(solution)/shard_map/ppermute | solution.py:27
  52.9 1.4 slice_bitcast_fusion.18
  60.2 1.7 fusion.454
  61.9 2.6 %gather_fusion.2 = bf16[8,64,512]{2,1,0:T(8,128)(2,1)} fusion(bf16[16,64,512]{2,1,0:T(8,128)(2,1)} %bitcast.13, s32[1024]{0:T(1024)S(1)} %pad_clamp_fusion), kind=kCustom, calls=%fused_computation.2 | custom fusion | bytes 1048608 | tf_op jit(solution)/shard_map/jit(_take)/gather | solution.py:255
  66.7 1.2 fusion.449
  74.4 2.1 %fusion.84 = f32[2,2,2,128,64]{3,4,2,1,0:T(8,128)} fusion(f32[2,2,2,64,64]{3,4,2,1,0:T(8,128)S(1)} %get-tuple-element.129, f32[2,2,2,64]{3,2,1,0:T(2,128)S(1)} %bitcast.485, f32[2,2,2,64]{3,2,1,0:T(2,128)S(1)} %log_add_fusion, bf16[2,2,8,2,8,128]{5,4,3,2,1,0:T(8,128)(2,1)} %copy-done.57, bf16[2,2,8,2,8,128]{5,4,3,2,1,0:T(8,128)(2,1)} %get-tuple-element.56, ...), kind=kOutput, calls=%fused_computation.167 | convolution fusion | flops 16908288 | bytes 790528 | tf_op jit(solution)/shard_map/abhqk,abkhe->abqhe/dot_general | solution.py:116
  76.5 2.2 %convolution_add_fusion.24 = f32[2,2,2,128,64]{3,4,2,1,0:T(8,128)} fusion(f32[2,2,2,128,64]{3,4,2,1,0:T(8,128)} %fusion.84, f32[2,2,2,64,64]{3,4,2,1,0:T(8,128)S(1)} %get-tuple-element.131, f32[2,2,2,64]{3,2,1,0:T(2,128)S(1)} %bitcast.487, f32[2,2,2,64]{3,2,1,0:T(2,128)S(1)} %log_add_fusion, bf16[2,2,8,2,8,128]{5,4,3,2,1,0:T(8,128)(2,1)} %get-tuple-element.46, ...), kind=kOutput, calls=%fused_computation.100 | convolution fusion | flops 16973824 | bytes 1052672 | tf_op jit(solution)/shard_map/abhqk,abkhe->abqhe/dot_general | solution.py:116
  78.7 1.4 convolution_add_fusion.23
  80.2 1.3 convolution_add_fusion.22
  81.6 1.3 convolution_add_fusion.21
  82.9 1.3 convolution_add_fusion.20
  86.8 7.0 %collective-permute-start.11 = (f32[8,16,4]{1,0,2:T(8,128)S(1)}, f32[8,16,4]{1,0,2:T(8,128)S(1)}, u32[]{:S(2)}, u32[]{:S(2)}) collective-permute-start(f32[8,16,4]{1,0,2:T(8,128)S(1)} %slice.413), channel_id=1, source_target_pairs={{0,4},{4,8},{8,12},{12,16},{16,20},{20,24},{24,28},{1,5},{5,9},{9,... | collective-permute-start | bytes 6152 | tf_op jit(solution)/shard_map/ppermute | solution.py:24
  95.6 1.3 collective-permute-start.12
  96.9 5.7 %collective-permute-done.12 = f32[8,16,4]{1,0,2:T(8,128)S(1)} collective-permute-done((f32[8,16,4]{1,0,2:T(8,128)S(1)}, f32[8,16,4]{1,0,2:T(8,128)S(1)}, u32[]{:S(2)}, u32[]{:S(2)}) %collective-permute-start.12) | collective-permute-done | bytes 2080 | tf_op jit(solution)/shard_map/ppermute | solution.py:27
  102.7 5.7 %collective-permute-start.13 = (f32[32,8,4]{1,0,2:T(8,128)S(1)}, f32[32,8,4]{1,0,2:T(8,128)S(1)}, u32[]{:S(2)}, u32[]{:S(2)}) collective-permute-start(f32[32,8,4]{1,0,2:T(8,128)S(1)} %get-tuple-element.75), channel_id=1, source_target_pairs={{0,1},{1,2},{2,3},{4,5},{5,6},{6,7},{8,9},{9,10},{10,11},{12,13},{... | collective-permute-start | bytes 12296 | tf_op jit(solution)/shard_map/ppermute | solution.py:24
  108.3 1.5 collective-permute-start.14
  110.8 1.2 collective-permute-done.14
  120.0 2.1 %convolution_add_fusion.15 = f32[2,2,2,128,64]{3,4,2,1,0:T(8,128)} fusion(f32[2,2,2,128,64]{3,4,2,1,0:T(8,128)S(1)} %fusion.82, f32[2,2,2,64,64]{3,4,2,1,0:T(8,128)} %copy-done.30, f32[2,2,2,64]{3,2,1,0:T(2,128)} %get-tuple-element.93, bf16[2,2,8,2,8,128]{5,4,3,2,1,0:T(8,128)(2,1)S(1)} %copy-done.10, bf16[2,2,8,2,8,128]{5,4,3,2,1,0:T(8,128)(2,1)} %get-tuple-element.36, ...), kind=kOutput, calls=%fused_computation.20 | convolution fusion | flops 16941056 | bytes 1050624 | tf_op jit(solution)/shard_map/abhqk,abqhe->abkhe/dot_general | solution.py:155
  122.0 1.4 convolution_add_fusion.14
  123.4 1.2 convolution_add_fusion.13
  124.7 1.3 convolution_add_fusion.12
  128.7 3.0 %collective-permute-start.15 = (f32[512,256]{1,0:T(8,128)S(1)}, f32[512,256]{1,0:T(8,128)S(1)}, u32[]{:S(2)}, u32[]{:S(2)}) collective-permute-start(f32[512,256]{1,0:T(8,128)S(1)} %constant_dynamic-slice_fusion.1), channel_id=1, source_target_pairs={{0,1},{1,0},{2,3},{3,2},{4,5},{5,4},{6,7},{7,6},{8,9},{9,8},{10,11... | collective-permute-start | bytes 1572872 | tf_op jit(solution)/shard_map/ppermute | solution.py:223
  131.7 1.5 collective-permute-done.15
  133.7 8.4 %collective-permute-done.16 = f32[256,256]{1,0:T(8,128)S(1)} collective-permute-done((f32[256,256]{1,0:T(8,128)S(1)}, f32[256,256]{1,0:T(8,128)S(1)}, u32[]{:S(2)}, u32[]{:S(2)}) %collective-permute-start.16) | collective-permute-done | bytes 262176 | tf_op jit(solution)/shard_map/ppermute | solution.py:223
  142.1 7.2 %collective-permute-start.17 = (f32[128,256]{1,0:T(8,128)S(1)}, f32[128,256]{1,0:T(8,128)S(1)}, u32[]{:S(2)}, u32[]{:S(2)}) collective-permute-start(f32[128,256]{1,0:T(8,128)S(1)} %constant_dynamic-slice_fusion.2), channel_id=1, source_target_pairs={{0,4},{4,0},{8,12},{12,8},{16,20},{20,16},{24,28},{28,24},{1,5},{5... | collective-permute-start | bytes 393224 | tf_op jit(solution)/shard_map/ppermute | solution.py:223
  149.3 3.2 %collective-permute-done.17 = f32[128,256]{1,0:T(8,128)S(1)} collective-permute-done((f32[128,256]{1,0:T(8,128)S(1)}, f32[128,256]{1,0:T(8,128)S(1)}, u32[]{:S(2)}, u32[]{:S(2)}) %collective-permute-start.17) | collective-permute-done | bytes 131104 | tf_op jit(solution)/shard_map/ppermute | solution.py:223
  152.5 2.8 %collective-permute-start.18 = (f32[128,256]{1,0:T(8,128)S(1)}, f32[128,256]{1,0:T(8,128)S(1)}, u32[]{:S(2)}, u32[]{:S(2)}) collective-permute-start(f32[128,256]{1,0:T(8,128)S(1)} %dynamic-slice_add_fusion.2), channel_id=1, source_target_pairs={{0,8},{4,12},{8,0},{12,4},{16,24},{20,28},{24,16},{28,20},{1,9},{5... | collective-permute-start | bytes 393224 | tf_op jit(solution)/shard_map/ppermute | solution.py:226
  155.4 3.1 %collective-permute-done.18 = f32[128,256]{1,0:T(8,128)S(1)} collective-permute-done((f32[128,256]{1,0:T(8,128)S(1)}, f32[128,256]{1,0:T(8,128)S(1)}, u32[]{:S(2)}, u32[]{:S(2)}) %collective-permute-start.18) | collective-permute-done | bytes 131104 | tf_op jit(solution)/shard_map/ppermute | solution.py:226
  158.5 1.4 collective-permute-start.19
  159.9 4.6 %collective-permute-done.19 = f32[128,256]{1,0:T(8,128)S(1)} collective-permute-done((f32[128,256]{1,0:T(8,128)S(1)}, f32[128,256]{1,0:T(8,128)S(1)}, u32[]{:S(2)}, u32[]{:S(2)}) %collective-permute-start.19) | collective-permute-done | bytes 131104 | tf_op jit(solution)/shard_map/ppermute | solution.py:226
  164.5 2.5 %collective-permute-start.20 = (f32[128,256]{1,0:T(8,128)S(1)}, f32[128,256]{1,0:T(8,128)S(1)}, u32[]{:S(2)}, u32[]{:S(2)}) collective-permute-start(f32[128,256]{1,0:T(8,128)S(1)} %add.420), channel_id=1, source_target_pairs={{0,4},{4,0},{8,12},{12,8},{16,20},{20,16},{24,28},{28,24},{1,5},{5... | collective-permute-start | bytes 393224 | tf_op jit(solution)/shard_map/ppermute | solution.py:188
  166.9 2.9 %collective-permute-done.20 = f32[128,256]{1,0:T(8,128)S(1)} collective-permute-done((f32[128,256]{1,0:T(8,128)S(1)}, f32[128,256]{1,0:T(8,128)S(1)}, u32[]{:S(2)}, u32[]{:S(2)}) %collective-permute-start.20) | collective-permute-done | bytes 131104 | tf_op jit(solution)/shard_map/ppermute | solution.py:188
  170.3 6.1 %collective-permute-done.21 = f32[256,256]{1,0:T(8,128)S(1)} collective-permute-done((f32[256,256]{1,0:T(8,128)S(1)}, f32[256,256]{1,0:T(8,128)S(1)}, u32[]{:S(2)}, u32[]{:S(2)}) %collective-permute-start.21) | collective-permute-done | bytes 262176 | tf_op jit(solution)/shard_map/ppermute | solution.py:188
  (377 shorter events, 45.2 us)
Async XLA Ops:
  0.6 25.5 %copy-start = (bf16[1,1,4,64,512]{4,3,2,1,0:T(8,128)(2,1)S(1)}, bf16[1,1,4,64,512]{4,3,2,1,0:T(8,128)(2,1)}, u32[]{:S(2)}) copy-start(bf16[1,1,4,64,512]{4,3,2,1,0:T(8,128)(2,1)} %param.15) | copy-start | bytes 786436
  0.6 14.2 %copy-start.96 = (s32[8]{0:T(128)S(1)}, s32[8]{0:T(128)}, u32[]{:S(2)}) copy-start(s32[8]{0:T(128)} %constant.165) | copy-start | bytes 100
  0.7 13.1 %copy-start.75 = (s32[1,1,4,2]{2,3,1,0:T(2,128)S(1)}, s32[1,1,4,2]{2,3,1,0:T(2,128)}, u32[]{:S(2)}) copy-start(s32[1,1,4,2]{2,3,1,0:T(2,128)} %param.16) | copy-start | bytes 100
  0.7 14.9 %copy-start.1 = (bf16[16,16,256]{2,1,0:T(8,128)(2,1)S(1)}, bf16[16,16,256]{2,1,0:T(8,128)(2,1)}, u32[]{:S(2)}) copy-start(bf16[16,16,256]{2,1,0:T(8,128)(2,1)} %param.10) | copy-start | bytes 393220
  0.7 14.9 %copy-start.66 = (bf16[256,256]{1,0:T(8,128)(2,1)S(1)}, bf16[256,256]{1,0:T(8,128)(2,1)}, u32[]{:S(2)}) copy-start(bf16[256,256]{1,0:T(8,128)(2,1)} %param.13) | copy-start | bytes 393220
  0.7 14.9 %copy-start.68 = (bf16[256,256]{1,0:T(8,128)(2,1)S(1)}, bf16[256,256]{1,0:T(8,128)(2,1)}, u32[]{:S(2)}) copy-start(bf16[256,256]{1,0:T(8,128)(2,1)} %param.12) | copy-start | bytes 393220
  2.5 13.4 %collective-permute-start = (s32[1,2,8]{2,1,0:T(2,128)S(1)}, s32[1,2,8]{2,1,0:T(2,128)S(1)}, u32[]{:S(2)}, u32[]{:S(2)}) collective-permute-start(s32[1,2,8]{2,1,0:T(2,128)S(1)} %add_bitcast_fusion), channel_id=1, source_target_pairs={{0,16},{4,20},{8,24},{12,28},{16,0},{20,4},{24,8},{28,12},{1,17},{... | collective-permute-start | bytes 200 | tf_op jit(solution)/shard_map/ppermute | solution.py:188
  9.0 29.1 %collective-permute-start.7 = (bf16[8,16,512]{2,1,0:T(8,128)(2,1)S(1)}, bf16[8,16,512]{2,1,0:T(8,128)(2,1)S(1)}, u32[]{:S(2)}, u32[]{:S(2)}) collective-permute-start(bf16[8,16,512]{2,1,0:T(8,128)(2,1)S(1)} %get-tuple-element.71), channel_id=1, source_target_pairs={{0,4},{4,8},{8,12},{12,16},{16,20},{20,24},{24,28},{1,5},{5,9},{9,... | collective-permute-start | bytes 393224 | tf_op jit(solution)/shard_map/ppermute | solution.py:24
  12.4 25.7 %collective-permute-start.8 = (bf16[8,16,512]{2,1,0:T(8,128)(2,1)S(1)}, bf16[8,16,512]{2,1,0:T(8,128)(2,1)S(1)}, u32[]{:S(2)}, u32[]{:S(2)}) collective-permute-start(bf16[8,16,512]{2,1,0:T(8,128)(2,1)S(1)} %get-tuple-element.72), channel_id=1, source_target_pairs={{4,0},{8,4},{12,8},{16,12},{20,16},{24,20},{28,24},{5,1},{9,5},{13... | collective-permute-start | bytes 393224 | tf_op jit(solution)/shard_map/ppermute | solution.py:27
  15.6 38.8 %copy-start.92 = (pred[2,2]{1,0:T(4,128)(4,1)}, pred[2,2]{1,0:T(4,128)(4,1)S(1)}, u32[]{:S(2)}) copy-start(pred[2,2]{1,0:T(4,128)(4,1)S(1)} %get-tuple-element.104) | copy-start | bytes 16
  15.6 39.4 %copy-start.90 = (pred[2,2]{1,0:T(4,128)(4,1)}, pred[2,2]{1,0:T(4,128)(4,1)S(1)}, u32[]{:S(2)}) copy-start(pred[2,2]{1,0:T(4,128)(4,1)S(1)} %get-tuple-element.105) | copy-start | bytes 16
  15.6 39.6 %copy-start.88 = (pred[2,2]{1,0:T(4,128)(4,1)}, pred[2,2]{1,0:T(4,128)(4,1)S(1)}, u32[]{:S(2)}) copy-start(pred[2,2]{1,0:T(4,128)(4,1)S(1)} %get-tuple-element.106) | copy-start | bytes 16
  15.6 40.4 %copy-start.86 = (pred[2,2]{1,0:T(4,128)(4,1)}, pred[2,2]{1,0:T(4,128)(4,1)S(1)}, u32[]{:S(2)}) copy-start(pred[2,2]{1,0:T(4,128)(4,1)S(1)} %get-tuple-element.107) | copy-start | bytes 16
  15.6 41.2 %copy-start.82 = (pred[2,2]{1,0:T(4,128)(4,1)}, pred[2,2]{1,0:T(4,128)(4,1)S(1)}, u32[]{:S(2)}) copy-start(pred[2,2]{1,0:T(4,128)(4,1)S(1)} %get-tuple-element.109) | copy-start | bytes 16
  15.6 42.1 %copy-start.80 = (pred[2,2]{1,0:T(4,128)(4,1)}, pred[2,2]{1,0:T(4,128)(4,1)S(1)}, u32[]{:S(2)}) copy-start(pred[2,2]{1,0:T(4,128)(4,1)S(1)} %get-tuple-element.110) | copy-start | bytes 16
  15.9 5.3 %collective-permute-start.1 = (s32[2,2,8]{2,1,0:T(2,128)S(1)}, s32[2,2,8]{2,1,0:T(2,128)S(1)}, u32[]{:S(2)}, u32[]{:S(2)}) collective-permute-start(s32[2,2,8]{2,1,0:T(2,128)S(1)} %pad_add_fusion.2), channel_id=1, source_target_pairs={{0,8},{4,12},{8,0},{12,4},{16,24},{20,28},{24,16},{28,20},{1,9},{5... | collective-permute-start | bytes 392 | tf_op jit(solution)/shard_map/ppermute | solution.py:188
  21.2 3.7 %collective-permute-start.2 = (s32[4,2,8]{2,1,0:T(2,128)S(1)}, s32[4,2,8]{2,1,0:T(2,128)S(1)}, u32[]{:S(2)}, u32[]{:S(2)}) collective-permute-start(s32[4,2,8]{2,1,0:T(2,128)S(1)} %pad_add_fusion.1), channel_id=1, source_target_pairs={{0,4},{4,0},{8,12},{12,8},{16,20},{20,16},{24,28},{28,24},{1,5},{5... | collective-permute-start | bytes 776 | tf_op jit(solution)/shard_map/ppermute | solution.py:188
  22.4 37.0 %copy-start.58 = (bf16[2,2,64,2,128]{4,3,2,1,0:T(2,128)(2,1)}, bf16[2,2,64,2,128]{4,3,2,1,0:T(2,128)(2,1)S(1)}, u32[]{:S(2)}) copy-start(bf16[2,2,64,2,128]{4,3,2,1,0:T(2,128)(2,1)S(1)} %reshape_reshape.29) | copy-start | bytes 393220
  27.9 33.9 %all-to-all-start = ((bf16[8,2,64,512]{3,2,1,0:T(8,128)(2,1)}), bf16[8,2,64,512]{3,2,1,0:T(8,128)(2,1)}, u32[]{:S(2)}, u32[]{:S(2)}) async-start(bf16[8,2,64,512]{3,2,1,0:T(8,128)(2,1)} %broadcast_select_fusion), calls=%async_computation | async-start | bytes 2097152 | tf_op jit(solution)/shard_map/all_to_all | solution.py:251
  32.2 14.0 %collective-permute-start.4 = (bf16[8,16,512]{2,1,0:T(8,128)(2,1)S(1)}, bf16[8,16,512]{2,1,0:T(8,128)(2,1)S(1)}, u32[]{:S(2)}, u32[]{:S(2)}) collective-permute-start(bf16[8,16,512]{2,1,0:T(8,128)(2,1)S(1)} %get-tuple-element.73), channel_id=1, source_target_pairs={{4,0},{8,4},{12,8},{16,12},{20,16},{24,20},{28,24},{5,1},{9,5},{13... | collective-permute-start | bytes 393224 | tf_op jit(solution)/shard_map/ppermute | solution.py:27
  33.5 12.6 %collective-permute-start.3 = (bf16[8,16,512]{2,1,0:T(8,128)(2,1)S(1)}, bf16[8,16,512]{2,1,0:T(8,128)(2,1)S(1)}, u32[]{:S(2)}, u32[]{:S(2)}) collective-permute-start(bf16[8,16,512]{2,1,0:T(8,128)(2,1)S(1)} %get-tuple-element.74), channel_id=1, source_target_pairs={{0,4},{4,8},{8,12},{12,16},{16,20},{20,24},{24,28},{1,5},{5,9},{9,... | collective-permute-start | bytes 393224 | tf_op jit(solution)/shard_map/ppermute | solution.py:24
  38.2 10.7 %collective-permute-start.9 = (bf16[32,8,512]{2,1,0:T(8,128)(2,1)S(1)}, bf16[32,8,512]{2,1,0:T(8,128)(2,1)S(1)}, u32[]{:S(2)}, u32[]{:S(2)}) collective-permute-start(bf16[32,8,512]{2,1,0:T(8,128)(2,1)S(1)} %get-tuple-element.63), channel_id=1, source_target_pairs={{0,1},{1,2},{2,3},{4,5},{5,6},{6,7},{8,9},{9,10},{10,11},{12,13},{... | collective-permute-start | bytes 786440 | tf_op jit(solution)/shard_map/ppermute | solution.py:24
  39.5 9.4 %collective-permute-start.10 = (bf16[32,8,512]{2,1,0:T(8,128)(2,1)S(1)}, bf16[32,8,512]{2,1,0:T(8,128)(2,1)S(1)}, u32[]{:S(2)}, u32[]{:S(2)}) collective-permute-start(bf16[32,8,512]{2,1,0:T(8,128)(2,1)S(1)} %get-tuple-element.64), channel_id=1, source_target_pairs={{1,0},{2,1},{3,2},{5,4},{6,5},{7,6},{9,8},{10,9},{11,10},{13,12},{... | collective-permute-start | bytes 786440 | tf_op jit(solution)/shard_map/ppermute | solution.py:27
  46.3 4.4 %collective-permute-start.5 = (bf16[32,8,512]{2,1,0:T(8,128)(2,1)S(1)}, bf16[32,8,512]{2,1,0:T(8,128)(2,1)S(1)}, u32[]{:S(2)}, u32[]{:S(2)}) collective-permute-start(bf16[32,8,512]{2,1,0:T(8,128)(2,1)S(1)} %get-tuple-element.67), channel_id=1, source_target_pairs={{0,1},{1,2},{2,3},{4,5},{5,6},{6,7},{8,9},{9,10},{10,11},{12,13},{... | collective-permute-start | bytes 786440 | tf_op jit(solution)/shard_map/ppermute | solution.py:24
  47.6 5.2 %collective-permute-start.6 = (bf16[32,8,512]{2,1,0:T(8,128)(2,1)S(1)}, bf16[32,8,512]{2,1,0:T(8,128)(2,1)S(1)}, u32[]{:S(2)}, u32[]{:S(2)}) collective-permute-start(bf16[32,8,512]{2,1,0:T(8,128)(2,1)S(1)} %get-tuple-element.68), channel_id=1, source_target_pairs={{1,0},{2,1},{3,2},{5,4},{6,5},{7,6},{9,8},{10,9},{11,10},{13,12},{... | collective-permute-start | bytes 786440 | tf_op jit(solution)/shard_map/ppermute | solution.py:27
  86.2 7.6 %copy-start.65 = (bf16[2,2,64,2,128]{4,2,3,1,0:T(8,128)(2,1)S(1)}, bf16[2,2,64,2,128]{4,2,3,1,0:T(8,128)(2,1)}, u32[]{:S(2)}) copy-start(bf16[2,2,64,2,128]{4,2,3,1,0:T(8,128)(2,1)} %get-tuple-element.133) | copy-start | bytes 393220
  86.2 7.9 %copy-start.59 = (bf16[16,16,256]{2,1,0:T(8,128)(2,1)S(1)}, bf16[16,16,256]{2,1,0:T(8,128)(2,1)}, u32[]{:S(2)}) copy-start(bf16[16,16,256]{2,1,0:T(8,128)(2,1)} %param.18) | copy-start | bytes 393220
  86.8 10.0 %collective-permute-start.11 = (f32[8,16,4]{1,0,2:T(8,128)S(1)}, f32[8,16,4]{1,0,2:T(8,128)S(1)}, u32[]{:S(2)}, u32[]{:S(2)}) collective-permute-start(f32[8,16,4]{1,0,2:T(8,128)S(1)} %slice.413), channel_id=1, source_target_pairs={{0,4},{4,8},{8,12},{12,16},{16,20},{20,24},{24,28},{1,5},{5,9},{9,... | collective-permute-start | bytes 6152 | tf_op jit(solution)/shard_map/ppermute | solution.py:24
  95.3 16.9 %copy-start.60 = (bf16[2,8,2,8,256]{4,3,2,1,0:T(8,128)(2,1)}, bf16[2,8,2,8,256]{4,3,2,1,0:T(8,128)(2,1)S(1)}, u32[]{:S(2)}) copy-start(bf16[2,8,2,8,256]{4,3,2,1,0:T(8,128)(2,1)S(1)} %copy.458) | copy-start | bytes 393220
  95.6 7.0 %collective-permute-start.12 = (f32[8,16,4]{1,0,2:T(8,128)S(1)}, f32[8,16,4]{1,0,2:T(8,128)S(1)}, u32[]{:S(2)}, u32[]{:S(2)}) collective-permute-start(f32[8,16,4]{1,0,2:T(8,128)S(1)} %slice.415), channel_id=1, source_target_pairs={{4,0},{8,4},{12,8},{16,12},{20,16},{24,20},{28,24},{5,1},{9,5},{13... | collective-permute-start | bytes 6152 | tf_op jit(solution)/shard_map/ppermute | solution.py:27
  102.6 10.4 %copy-start.44 = (bf16[2,2,8,2,8,128]{5,4,3,2,1,0:T(8,128)(2,1)S(1)}, bf16[2,2,8,2,8,128]{5,4,3,2,1,0:T(8,128)(2,1)}, u32[]{:S(2)}) copy-start(bf16[2,2,8,2,8,128]{5,4,3,2,1,0:T(8,128)(2,1)} %get-tuple-element.38) | copy-start | bytes 393220
  102.7 10.4 %copy-start.46 = (bf16[2,2,8,2,8,128]{5,4,3,2,1,0:T(8,128)(2,1)S(1)}, bf16[2,2,8,2,8,128]{5,4,3,2,1,0:T(8,128)(2,1)}, u32[]{:S(2)}) copy-start(bf16[2,2,8,2,8,128]{5,4,3,2,1,0:T(8,128)(2,1)} %copy-done.45) | copy-start | bytes 393220
  102.7 10.4 %copy-start.95 = (pred[2,2]{1,0:T(4,128)(4,1)S(1)}, pred[2,2]{1,0:T(4,128)(4,1)}, u32[]{:S(2)}) copy-start(pred[2,2]{1,0:T(4,128)(4,1)} %get-tuple-element.111) | copy-start | bytes 16
  102.7 8.1 %collective-permute-start.13 = (f32[32,8,4]{1,0,2:T(8,128)S(1)}, f32[32,8,4]{1,0,2:T(8,128)S(1)}, u32[]{:S(2)}, u32[]{:S(2)}) collective-permute-start(f32[32,8,4]{1,0,2:T(8,128)S(1)} %get-tuple-element.75), channel_id=1, source_target_pairs={{0,1},{1,2},{2,3},{4,5},{5,6},{6,7},{8,9},{9,10},{10,11},{12,13},{... | collective-permute-start | bytes 12296 | tf_op jit(solution)/shard_map/ppermute | solution.py:24
  108.3 3.6 %collective-permute-start.14 = (f32[32,8,4]{1,0,2:T(8,128)S(1)}, f32[32,8,4]{1,0,2:T(8,128)S(1)}, u32[]{:S(2)}, u32[]{:S(2)}) collective-permute-start(f32[32,8,4]{1,0,2:T(8,128)S(1)} %get-tuple-element.76), channel_id=1, source_target_pairs={{1,0},{2,1},{3,2},{5,4},{6,5},{7,6},{9,8},{10,9},{11,10},{13,12},{... | collective-permute-start | bytes 12296 | tf_op jit(solution)/shard_map/ppermute | solution.py:27
  128.7 4.5 %collective-permute-start.15 = (f32[512,256]{1,0:T(8,128)S(1)}, f32[512,256]{1,0:T(8,128)S(1)}, u32[]{:S(2)}, u32[]{:S(2)}) collective-permute-start(f32[512,256]{1,0:T(8,128)S(1)} %constant_dynamic-slice_fusion.1), channel_id=1, source_target_pairs={{0,1},{1,0},{2,3},{3,2},{4,5},{5,4},{6,7},{7,6},{8,9},{9,8},{10,11... | collective-permute-start | bytes 1572872 | tf_op jit(solution)/shard_map/ppermute | solution.py:223
  133.4 8.7 %collective-permute-start.16 = (f32[256,256]{1,0:T(8,128)S(1)}, f32[256,256]{1,0:T(8,128)S(1)}, u32[]{:S(2)}, u32[]{:S(2)}) collective-permute-start(f32[256,256]{1,0:T(8,128)S(1)} %constant_dynamic-slice_fusion), channel_id=1, source_target_pairs={{0,2},{1,3},{2,0},{3,1},{4,6},{5,7},{6,4},{7,5},{8,10},{9,11},{10,... | collective-permute-start | bytes 786440 | tf_op jit(solution)/shard_map/ppermute | solution.py:223
  142.1 10.4 %collective-permute-start.17 = (f32[128,256]{1,0:T(8,128)S(1)}, f32[128,256]{1,0:T(8,128)S(1)}, u32[]{:S(2)}, u32[]{:S(2)}) collective-permute-start(f32[128,256]{1,0:T(8,128)S(1)} %constant_dynamic-slice_fusion.2), channel_id=1, source_target_pairs={{0,4},{4,0},{8,12},{12,8},{16,20},{20,16},{24,28},{28,24},{1,5},{5... | collective-permute-start | bytes 393224 | tf_op jit(solution)/shard_map/ppermute | solution.py:223
  152.5 6.0 %collective-permute-start.18 = (f32[128,256]{1,0:T(8,128)S(1)}, f32[128,256]{1,0:T(8,128)S(1)}, u32[]{:S(2)}, u32[]{:S(2)}) collective-permute-start(f32[128,256]{1,0:T(8,128)S(1)} %dynamic-slice_add_fusion.2), channel_id=1, source_target_pairs={{0,8},{4,12},{8,0},{12,4},{16,24},{20,28},{24,16},{28,20},{1,9},{5... | collective-permute-start | bytes 393224 | tf_op jit(solution)/shard_map/ppermute | solution.py:226
  158.5 5.9 %collective-permute-start.19 = (f32[128,256]{1,0:T(8,128)S(1)}, f32[128,256]{1,0:T(8,128)S(1)}, u32[]{:S(2)}, u32[]{:S(2)}) collective-permute-start(f32[128,256]{1,0:T(8,128)S(1)} %add.419), channel_id=1, source_target_pairs={{0,16},{4,20},{8,24},{12,28},{16,0},{20,4},{24,8},{28,12},{1,17},{... | collective-permute-start | bytes 393224 | tf_op jit(solution)/shard_map/ppermute | solution.py:226
  164.5 5.4 %collective-permute-start.20 = (f32[128,256]{1,0:T(8,128)S(1)}, f32[128,256]{1,0:T(8,128)S(1)}, u32[]{:S(2)}, u32[]{:S(2)}) collective-permute-start(f32[128,256]{1,0:T(8,128)S(1)} %add.420), channel_id=1, source_target_pairs={{0,4},{4,0},{8,12},{12,8},{16,20},{20,16},{24,28},{28,24},{1,5},{5... | collective-permute-start | bytes 393224 | tf_op jit(solution)/shard_map/ppermute | solution.py:188
  169.9 6.4 %collective-permute-start.21 = (f32[256,256]{1,0:T(8,128)S(1)}, f32[256,256]{1,0:T(8,128)S(1)}, u32[]{:S(2)}, u32[]{:S(2)}) collective-permute-start(f32[256,256]{1,0:T(8,128)S(1)} %pad_maximum_fusion.5), channel_id=1, source_target_pairs={{0,2},{1,3},{2,0},{3,1},{4,6},{5,7},{6,4},{7,5},{8,10},{9,11},{10,... | collective-permute-start | bytes 786440 | tf_op jit(solution)/shard_map/ppermute | solution.py:188
  170.3 6.3 %copy-start.33 = (bf16[256,256]{1,0:T(8,128)(2,1)S(1)}, bf16[256,256]{1,0:T(8,128)(2,1)}, u32[]{:S(2)}) copy-start(bf16[256,256]{1,0:T(8,128)(2,1)} %param.14) | copy-start | bytes 393220
  170.3 7.1 %copy-start.61 = (bf16[2,8,2,8,256]{4,3,2,1,0:T(8,128)(2,1)S(1)}, bf16[2,8,2,8,256]{4,3,2,1,0:T(8,128)(2,1)}, u32[]{:S(2)}) copy-start(bf16[2,8,2,8,256]{4,3,2,1,0:T(8,128)(2,1)} %copy-done.60) | copy-start | bytes 393220
  170.3 7.1 %copy-start.67 = (bf16[256,256]{1,0:T(8,128)(2,1)S(1)}, bf16[256,256]{1,0:T(8,128)(2,1)}, u32[]{:S(2)}) copy-start(bf16[256,256]{1,0:T(8,128)(2,1)} %param.13) | copy-start | bytes 393220
  170.3 7.1 %copy-start.69 = (bf16[256,256]{1,0:T(8,128)(2,1)S(1)}, bf16[256,256]{1,0:T(8,128)(2,1)}, u32[]{:S(2)}) copy-start(bf16[256,256]{1,0:T(8,128)(2,1)} %param.12) | copy-start | bytes 393220
  170.3 7.1 %copy-start.70 = (bf16[256,256]{1,0:T(8,128)(2,1)S(1)}, bf16[256,256]{1,0:T(8,128)(2,1)}, u32[]{:S(2)}) copy-start(bf16[256,256]{1,0:T(8,128)(2,1)} %param.11) | copy-start | bytes 393220
  176.5 2.0 %collective-permute-start.22 = (f32[512,256]{1,0:T(8,128)S(1)}, f32[512,256]{1,0:T(8,128)S(1)}, u32[]{:S(2)}, u32[]{:S(2)}) collective-permute-start(f32[512,256]{1,0:T(8,128)S(1)} %pad_maximum_fusion.4), channel_id=1, source_target_pairs={{0,1},{1,0},{2,3},{3,2},{4,5},{5,4},{6,7},{7,6},{8,9},{9,8},{10,11... | collective-permute-start | bytes 1572872 | tf_op jit(solution)/shard_map/ppermute | solution.py:188
  (73 other events, 118.0 us)

commit v10 on v8

--- a/solution.py
+++ b/solution.py
@@ -328,13 +328,9 @@
     grad_patches = jnp.dot(grads_joined, w_stacked, preferred_element_type=jnp.float32).astype(
         jnp.bfloat16
     )
-    partials = (
-        inner_rows(flat_in, dq_flat),
-        inner_rows(flat_in, dk_flat),
-        inner_rows(flat_in, dv_flat),
-        grad_out_local,
-    )
-    summed = tree_sum(partials, ("gy", "gx"))
+    early = tree_sum((grad_out_local, inner_rows(flat_in, dq_flat)), ("gy", "gx"))
+    late = tree_sum((inner_rows(flat_in, dk_flat), inner_rows(flat_in, dv_flat)), ("gy", "gx"))
+    summed = (early[1], late[0], late[1], early[0])
     return (
         layer_out.reshape(tile_rows, tile_cols, model_width),
         grad_patches.reshape(tile_rows, tile_cols, model_width),

time: 176 us -> 182 us (1.034)
  starting transfers between devices: 52.7 us -> 62.1 us
  matrix products: 49.1 us -> 41.4 us
  other arithmetic: 4.43 us -> 11 us
  waiting for transfers between devices: 46.6 us -> 40.1 us
  local copies, waits for them, and re-layouts: 19.9 us -> 23.2 us
    all_to_all x1, waiting for transfers between devices: 3.64 us -> 15.2 us  [fetch_regions(): received = lax.all_to_all(sent, axis, 0, 0, tiled=True)]
    ppermute x3 -> x6, waiting for transfers between devices: 13.1 us -> 4.94 us  [tree_sum(): joined = keep + lax.ppermute(send, axis, pairs)]
    ppermute x6, waiting for transfers between devices: 7.48 us -> 0.02 us  [padded(): lax.ppermute(lax.slice_in_dim(block, 0, width, axis=dim), axis, backward)]
    ppermute x3 -> x6, starting transfers between devices: 5.8 us -> 12.4 us  [tree_sum(): joined = keep + lax.ppermute(send, axis, pairs)]
    dot_general x9, matrix products: 16 us -> 10.9 us  [key_grads(): jnp.einsum('abhqk,abqhe->abkhe', grad_score, query_heads, preferred_eleme...]
    ppermute x6 -> x9, waiting for transfers between devices: 13.8 us -> 11.6 us  [doubling_gather(): got = lax.ppermute(joined, axis, pairs)]
    ppermute x6, starting transfers between devices: 19.2 us -> 21.5 us  [padded(): lax.ppermute(lax.slice_in_dim(block, block.shape[dim] - width, None, axis...]
    convert_element_type x2, local copies, waits for them, and re-layouts: 0.23 us -> 2.44 us  [key_grads(): return (grad_key, grad_value.reshape(out_shape).astype(jnp.bfloat16))]
  transfers between devices with their start and end apart: 24 -> 32, of which waited for: 13 -> 14; matrix products, arithmetic and copies ran while one was open for 11% -> 25% of each run, Pallas kernels for 0% -> 0%
where the time goes in v10:
time: 182 us; the launch traced here: 181 us
  starting transfers between devices  62.1 us (34%)
  matrix products  41.4 us (23%)
  waiting for transfers between devices  40.1 us (22%)
  local copies, waits for them, and re-layouts  23.2 us (13%)
  other arithmetic  11 us (6%)
  between operations  2.79 us (2%)
    ppermute x6, starting transfers between devices, padded(): lax.ppermute(lax.slice_in_dim(block, block.shape[dim] - width, None, axis...  21.5 us
    all_to_all x1, waiting for transfers between devices, fetch_regions(): received = lax.all_to_all(sent, axis, 0, 0, tiled=True)  15.2 us
    ppermute x6, starting transfers between devices, tree_sum(): joined = keep + lax.ppermute(send, axis, pairs)  12.4 us
    dot_general x10, matrix products, query_grads(): jnp.einsum('abhqk,abkhe->abqhe', grad_score, split_heads(key_part), prefe...  12.3 us
    ppermute x9, waiting for transfers between devices, doubling_gather(): got = lax.ppermute(joined, axis, pairs)  11.6 us
    dot_general x9, matrix products, key_grads(): jnp.einsum('abhqk,abqhe->abkhe', grad_score, query_heads, preferred_eleme...  10.9 us
    ppermute x9, starting transfers between devices, doubling_gather(): got = lax.ppermute(joined, axis, pairs)  9.99 us
    unnamed x195, local copies, waits for them, and re-layouts  8.95 us
  transfers between devices with their start and end apart: 32, of which 14 were waited for; matrix products, arithmetic and copies ran while one was open for 25% of the time, Pallas kernels for 0%

profile of v10, /device:TPU:0, one launch (start us, length us, event | category | flops | bytes accessed | tf_op | source)
XLA Modules:
  0.0 180.5 jit_solution(10817284692246752458)
XLA Ops:
  2.5 4.1 %collective-permute-start.4 = (s32[1,2,8]{2,1,0:T(2,128)S(1)}, s32[1,2,8]{2,1,0:T(2,128)S(1)}, u32[]{:S(2)}, u32[]{:S(2)}) collective-permute-start(s32[1,2,8]{2,1,0:T(2,128)S(1)} %add_bitcast_fusion), channel_id=1, source_target_pairs={{0,16},{4,20},{8,24},{12,28},{16,0},{20,4},{24,8},{28,12},{1,17},{... | collective-permute-start | bytes 200 | tf_op jit(solution)/shard_map/ppermute | solution.py:188
  7.9 1.3 collective-permute-start.1
  9.2 4.6 %collective-permute-start = (bf16[8,16,512]{2,1,0:T(8,128)(2,1)S(1)}, bf16[8,16,512]{2,1,0:T(8,128)(2,1)S(1)}, u32[]{:S(2)}, u32[]{:S(2)}) collective-permute-start(bf16[8,16,512]{2,1,0:T(8,128)(2,1)S(1)} %bitcast.520), channel_id=1, source_target_pairs={{0,4},{4,8},{8,12},{12,16},{16,20},{20,24},{24,28},{1,5},{5,9},{9,... | collective-permute-start | bytes 393224 | tf_op jit(solution)/shard_map/ppermute | solution.py:24
  14.2 4.3 %collective-permute-start.7 = (bf16[8,16,512]{2,1,0:T(8,128)(2,1)S(1)}, bf16[8,16,512]{2,1,0:T(8,128)(2,1)S(1)}, u32[]{:S(2)}, u32[]{:S(2)}) collective-permute-start(bf16[8,16,512]{2,1,0:T(8,128)(2,1)S(1)} %get-tuple-element.65), channel_id=1, source_target_pairs={{0,4},{4,8},{8,12},{12,16},{16,20},{20,24},{24,28},{1,5},{5,9},{9,... | collective-permute-start | bytes 393224 | tf_op jit(solution)/shard_map/ppermute | solution.py:24
  18.5 1.3 collective-permute-start.8
  21.9 2.8 %collective-permute-start.5 = (s32[2,2,8]{2,1,0:T(2,128)S(1)}, s32[2,2,8]{2,1,0:T(2,128)S(1)}, u32[]{:S(2)}, u32[]{:S(2)}) collective-permute-start(s32[2,2,8]{2,1,0:T(2,128)S(1)} %pad_add_fusion.2), channel_id=1, source_target_pairs={{0,8},{4,12},{8,0},{12,4},{16,24},{20,28},{24,16},{28,20},{1,9},{5... | collective-permute-start | bytes 392 | tf_op jit(solution)/shard_map/ppermute | solution.py:188
  24.8 1.5 collective-permute-done.5
  26.3 2.0 %collective-permute-start.6 = (s32[4,2,8]{2,1,0:T(2,128)S(1)}, s32[4,2,8]{2,1,0:T(2,128)S(1)}, u32[]{:S(2)}, u32[]{:S(2)}) collective-permute-start(s32[4,2,8]{2,1,0:T(2,128)S(1)} %pad_add_fusion.1), channel_id=1, source_target_pairs={{0,4},{4,0},{8,12},{12,8},{16,20},{20,16},{24,28},{28,24},{1,5},{5... | collective-permute-start | bytes 776 | tf_op jit(solution)/shard_map/ppermute | solution.py:188
  28.3 1.7 collective-permute-done.6
  32.0 2.0 %collective-permute-start.9 = (bf16[32,8,512]{2,1,0:T(8,128)(2,1)S(1)}, bf16[32,8,512]{2,1,0:T(8,128)(2,1)}, u32[]{:S(2)}, u32[]{:S(2)}) collective-permute-start(bf16[32,8,512]{2,1,0:T(8,128)(2,1)S(1)} %get-tuple-element.55), channel_id=1, source_target_pairs={{0,1},{1,2},{2,3},{4,5},{5,6},{6,7},{8,9},{9,10},{10,11},{12,13},{... | collective-permute-start | bytes 786440 | tf_op jit(solution)/shard_map/ppermute | solution.py:24
  34.0 1.3 collective-permute-start.10
  36.2 4.8 %collective-permute-start.2 = (bf16[32,8,512]{2,1,0:T(8,128)(2,1)}, bf16[32,8,512]{2,1,0:T(8,128)(2,1)}, u32[]{:S(2)}, u32[]{:S(2)}) collective-permute-start(bf16[32,8,512]{2,1,0:T(8,128)(2,1)} %get-tuple-element.59), channel_id=1, source_target_pairs={{0,1},{1,2},{2,3},{4,5},{5,6},{6,7},{8,9},{9,10},{10,11},{12,13},{... | collective-permute-start | bytes 786440 | tf_op jit(solution)/shard_map/ppermute | solution.py:24
  43.4 4.3 %all-to-all-start = ((bf16[8,2,64,512]{3,2,1,0:T(8,128)(2,1)}), bf16[8,2,64,512]{3,2,1,0:T(8,128)(2,1)}, u32[]{:S(2)}, u32[]{:S(2)}) async-start(bf16[8,2,64,512]{3,2,1,0:T(8,128)(2,1)} %broadcast_select_fusion), calls=%async_computation | async-start | bytes 2097152 | tf_op jit(solution)/shard_map/all_to_all | solution.py:250
  50.2 1.3 slice_bitcast_fusion.18
  58.1 1.5 slice_bitcast_fusion
  59.6 15.2 %all-to-all-done = bf16[8,2,64,512]{3,2,1,0:T(8,128)(2,1)} async-done(((bf16[8,2,64,512]{3,2,1,0:T(8,128)(2,1)}), bf16[8,2,64,512]{3,2,1,0:T(8,128)(2,1)}, u32[]{:S(2)}, u32[]{:S(2)}) %all-to-all-start) | async-done | bytes 1048608 | tf_op jit(solution)/shard_map/all_to_all | solution.py:250
  74.8 2.6 %gather_fusion.2 = bf16[8,64,512]{2,1,0:T(8,128)(2,1)} fusion(bf16[16,64,512]{2,1,0:T(8,128)(2,1)} %bitcast.15, s32[1024]{0:T(1024)S(1)} %pad_clamp_fusion), kind=kCustom, calls=%fused_computation.2 | custom fusion | bytes 1048608 | tf_op jit(solution)/shard_map/jit(_take)/gather | solution.py:254
  87.4 2.1 %fusion.84 = f32[2,2,2,128,64]{3,4,2,1,0:T(8,128)} fusion(f32[2,2,2,64,64]{3,4,2,1,0:T(8,128)S(1)} %get-tuple-element.127, f32[2,2,2,64]{3,2,1,0:T(2,128)S(1)} %bitcast.488, f32[2,2,2,64]{3,2,1,0:T(2,128)S(1)} %log_add_fusion, bf16[2,2,8,2,8,128]{5,4,3,2,1,0:T(8,128)(2,1)} %copy-done.54, bf16[2,2,8,2,8,128]{5,4,3,2,1,0:T(8,128)(2,1)} %get-tuple-element.50, ...), kind=kOutput, calls=%fused_computation.167 | convolution fusion | flops 16908288 | bytes 790528 | tf_op jit(solution)/shard_map/abhqk,abkhe->abqhe/dot_general | solution.py:116
  89.5 2.2 %convolution_add_fusion.24 = f32[2,2,2,128,64]{3,4,2,1,0:T(8,128)} fusion(f32[2,2,2,128,64]{3,4,2,1,0:T(8,128)} %fusion.84, f32[2,2,2,64,64]{3,4,2,1,0:T(8,128)S(1)} %get-tuple-element.129, f32[2,2,2,64]{3,2,1,0:T(2,128)S(1)} %bitcast.490, f32[2,2,2,64]{3,2,1,0:T(2,128)S(1)} %log_add_fusion, bf16[2,2,8,2,8,128]{5,4,3,2,1,0:T(8,128)(2,1)} %get-tuple-element.40, ...), kind=kOutput, calls=%fused_computation.100 | convolution fusion | flops 16973824 | bytes 1052672 | tf_op jit(solution)/shard_map/abhqk,abkhe->abqhe/dot_general | solution.py:116
  91.7 1.4 convolution_add_fusion.23
  93.1 1.3 convolution_add_fusion.22
  94.5 1.3 convolution_add_fusion.21
  95.8 1.3 convolution_add_fusion.20
  97.2 1.3 convolution_add_fusion.19
  100.5 1.3 collective-permute-start.12
  101.9 4.5 %collective-permute-start.11 = (f32[8,16,4]{1,0,2:T(8,128)S(1)}, f32[8,16,4]{1,0,2:T(8,128)S(1)}, u32[]{:S(2)}, u32[]{:S(2)}) collective-permute-start(f32[8,16,4]{1,0,2:T(8,128)S(1)} %slice.409), channel_id=1, source_target_pairs={{0,4},{4,8},{8,12},{12,16},{16,20},{20,24},{24,28},{1,5},{5,9},{9,... | collective-permute-start | bytes 6152 | tf_op jit(solution)/shard_map/ppermute | solution.py:24
  108.0 1.3 collective-permute-start.13
  109.3 1.6 collective-permute-start.14
  111.7 3.3 %collective-permute-start.15 = (f32[256,256]{1,0:T(8,128)}, f32[256,256]{1,0:T(8,128)}, u32[]{:S(2)}, u32[]{:S(2)}) collective-permute-start(f32[256,256]{1,0:T(8,128)} %fusion.99), channel_id=1, source_target_pairs={{0,1},{1,0},{2,3},{3,2},{4,5},{5,4},{6,7},{7,6},{8,9},{9,8},{10,11... | collective-permute-start | bytes 786440 | tf_op jit(solution)/shard_map/ppermute | solution.py:223
  123.8 1.6 convert_element_type.227
  125.4 1.6 copy.539
  127.0 2.1 %convolution_add_fusion.15 = f32[2,2,2,128,64]{3,4,2,1,0:T(8,128)} fusion(f32[2,2,2,128,64]{3,4,2,1,0:T(8,128)} %fusion.82, f32[2,2,2,64,64]{3,4,2,1,0:T(8,128)} %copy-done.29, f32[2,2,2,64]{3,2,1,0:T(2,128)} %get-tuple-element.91, bf16[2,2,8,2,8,128]{5,4,3,2,1,0:T(8,128)(2,1)S(1)} %copy-done.10, bf16[2,2,8,2,8,128]{5,4,3,2,1,0:T(8,128)(2,1)} %get-tuple-element.30, ...), kind=kOutput, calls=%fused_computation.20 | convolution fusion | flops 16941056 | bytes 1050624 | tf_op jit(solution)/shard_map/abhqk,abqhe->abkhe/dot_general | solution.py:155
  129.1 2.1 %convolution_add_fusion.14 = f32[2,2,2,128,64]{3,4,2,1,0:T(8,128)} fusion(f32[2,2,2,128,64]{3,4,2,1,0:T(8,128)} %convolution_add_fusion.15, f32[2,2,2,64,64]{3,4,2,1,0:T(8,128)} %copy-done.28, f32[2,2,2,64]{3,2,1,0:T(2,128)} %get-tuple-element.89, bf16[2,2,8,2,8,128]{5,4,3,2,1,0:T(8,128)(2,1)S(1)} %copy-done.9, ...), kind=kOutput, calls=%fused_computation.19 | convolution fusion | flops 16941056 | bytes 1050624 | tf_op jit(solution)/shard_map/abhqk,abqhe->abkhe/dot_general | solution.py:155
  131.2 1.4 convolution_add_fusion.13
  132.6 1.9 %convolution_add_fusion.12 = f32[2,2,2,128,64]{3,4,2,1,0:T(8,128)} fusion(f32[2,2,2,128,64]{3,4,2,1,0:T(8,128)S(1)} %convolution_add_fusion.13, f32[2,2,2,64,64]{3,4,2,1,0:T(8,128)S(1)} %fusion.20, f32[2,2,2,64]{3,2,1,0:T(2,128)} %get-tuple-element.85, bf16[2,2,8,2,8,128]{5,4,3,2,1,0:T(8,128)(2,1)S(1)} %copy-done.7, ...), kind=kOutput, calls=%fused_computation.17 | convolution fusion | flops 16941056 | bytes 1050624 | tf_op jit(solution)/shard_map/abhqk,abqhe->abkhe/dot_general | solution.py:155
  134.6 1.4 convolution_add_fusion.11
  138.1 2.7 %collective-permute-start.23 = (f32[256,256]{1,0:T(8,128)S(1)}, f32[256,256]{1,0:T(8,128)S(1)}, u32[]{:S(2)}, u32[]{:S(2)}) collective-permute-start(f32[256,256]{1,0:T(8,128)S(1)} %fusion.96), channel_id=1, source_target_pairs={{0,1},{1,0},{2,3},{3,2},{4,5},{5,4},{6,7},{7,6},{8,9},{9,8},{10,11... | collective-permute-start | bytes 786440 | tf_op jit(solution)/shard_map/ppermute | solution.py:223
  142.1 2.1 %collective-permute-start.24 = (f32[128,256]{1,0:T(8,128)S(1)}, f32[128,256]{1,0:T(8,128)S(1)}, u32[]{:S(2)}, u32[]{:S(2)}) collective-permute-start(f32[128,256]{1,0:T(8,128)S(1)} %constant_dynamic-slice_fusion), channel_id=1, source_target_pairs={{0,2},{1,3},{2,0},{3,1},{4,6},{5,7},{6,4},{7,5},{8,10},{9,11},{10,... | collective-permute-start | bytes 393224 | tf_op jit(solution)/shard_map/ppermute | solution.py:223
  144.2 4.1 %collective-permute-done.16 = f32[128,256]{1,0:T(8,128)S(1)} collective-permute-done((f32[128,256]{1,0:T(8,128)S(1)}, f32[128,256]{1,0:T(8,128)S(1)}, u32[]{:S(2)}, u32[]{:S(2)}) %collective-permute-start.16) | collective-permute-done | bytes 131104 | tf_op jit(solution)/shard_map/ppermute | solution.py:223
  148.3 2.4 %collective-permute-start.17 = (f32[64,256]{1,0:T(8,128)S(1)}, f32[64,256]{1,0:T(8,128)S(1)}, u32[]{:S(2)}, u32[]{:S(2)}) collective-permute-start(f32[64,256]{1,0:T(8,128)S(1)} %constant_dynamic-slice_fusion.1), channel_id=1, source_target_pairs={{0,4},{4,0},{8,12},{12,8},{16,20},{20,16},{24,28},{28,24},{1,5},{5... | collective-permute-start | bytes 196616 | tf_op jit(solution)/shard_map/ppermute | solution.py:223
  150.8 1.8 %collective-permute-start.25 = (f32[64,256]{1,0:T(8,128)S(1)}, f32[64,256]{1,0:T(8,128)S(1)}, u32[]{:S(2)}, u32[]{:S(2)}) collective-permute-start(f32[64,256]{1,0:T(8,128)S(1)} %constant_dynamic-slice_fusion.3), channel_id=1, source_target_pairs={{0,4},{4,0},{8,12},{12,8},{16,20},{20,16},{24,28},{28,24},{1,5},{5... | collective-permute-start | bytes 196616 | tf_op jit(solution)/shard_map/ppermute | solution.py:223
  153.4 4.0 %collective-permute-start.18 = (f32[64,256]{1,0:T(8,128)S(1)}, f32[64,256]{1,0:T(8,128)S(1)}, u32[]{:S(2)}, u32[]{:S(2)}) collective-permute-start(f32[64,256]{1,0:T(8,128)S(1)} %dynamic-slice_add_fusion.3), channel_id=1, source_target_pairs={{0,8},{4,12},{8,0},{12,4},{16,24},{20,28},{24,16},{28,20},{1,9},{5... | collective-permute-start | bytes 196616 | tf_op jit(solution)/shard_map/ppermute | solution.py:226
  160.0 2.3 %collective-permute-done.26 = f32[64,256]{1,0:T(8,128)S(1)} collective-permute-done((f32[64,256]{1,0:T(8,128)S(1)}, f32[64,256]{1,0:T(8,128)S(1)}, u32[]{:S(2)}, u32[]{:S(2)}) %collective-permute-start.26) | collective-permute-done | bytes 65568 | tf_op jit(solution)/shard_map/ppermute | solution.py:226
  162.8 2.2 %collective-permute-done.19 = f32[64,256]{1,0:T(8,128)S(1)} collective-permute-done((f32[64,256]{1,0:T(8,128)S(1)}, f32[64,256]{1,0:T(8,128)S(1)}, u32[]{:S(2)}, u32[]{:S(2)}) %collective-permute-start.19) | collective-permute-done | bytes 65568 | tf_op jit(solution)/shard_map/ppermute | solution.py:226
  166.1 2.2 %collective-permute-done.27 = f32[64,256]{1,0:T(8,128)S(1)} collective-permute-done((f32[64,256]{1,0:T(8,128)S(1)}, f32[64,256]{1,0:T(8,128)S(1)}, u32[]{:S(2)}, u32[]{:S(2)}) %collective-permute-start.27) | collective-permute-done | bytes 65568 | tf_op jit(solution)/shard_map/ppermute | solution.py:226
  170.0 2.6 %collective-permute-done.28 = f32[64,256]{1,0:T(8,128)S(1)} collective-permute-done((f32[64,256]{1,0:T(8,128)S(1)}, f32[64,256]{1,0:T(8,128)S(1)}, u32[]{:S(2)}, u32[]{:S(2)}) %collective-permute-start.28) | collective-permute-done | bytes 65568 | tf_op jit(solution)/shard_map/ppermute | solution.py:188
  172.8 1.7 collective-permute-done.21
  174.6 3.2 %collective-permute-done.29 = f32[128,256]{1,0:T(8,128)S(1)} collective-permute-done((f32[128,256]{1,0:T(8,128)S(1)}, f32[128,256]{1,0:T(8,128)S(1)}, u32[]{:S(2)}, u32[]{:S(2)}) %collective-permute-start.29) | collective-permute-done | bytes 131104 | tf_op jit(solution)/shard_map/ppermute | solution.py:188
  (395 shorter events, 54.8 us)
Async XLA Ops:
  0.6 30.6 %copy-start = (bf16[1,1,4,64,512]{4,3,2,1,0:T(8,128)(2,1)S(1)}, bf16[1,1,4,64,512]{4,3,2,1,0:T(8,128)(2,1)}, u32[]{:S(2)}) copy-start(bf16[1,1,4,64,512]{4,3,2,1,0:T(8,128)(2,1)} %param.15) | copy-start | bytes 786436
  0.6 13.1 %copy-start.1 = (bf16[16,16,256]{2,1,0:T(8,128)(2,1)S(1)}, bf16[16,16,256]{2,1,0:T(8,128)(2,1)}, u32[]{:S(2)}) copy-start(bf16[16,16,256]{2,1,0:T(8,128)(2,1)} %param.10) | copy-start | bytes 393220
  0.7 13.1 %copy-start.66 = (bf16[256,256]{1,0:T(8,128)(2,1)S(1)}, bf16[256,256]{1,0:T(8,128)(2,1)}, u32[]{:S(2)}) copy-start(bf16[256,256]{1,0:T(8,128)(2,1)} %param.11) | copy-start | bytes 393220
  0.7 13.3 %copy-start.30 = (bf16[256,256]{1,0:T(8,128)(2,1)S(1)}, bf16[256,256]{1,0:T(8,128)(2,1)}, u32[]{:S(2)}) copy-start(bf16[256,256]{1,0:T(8,128)(2,1)} %param.14) | copy-start | bytes 393220
  0.7 13.3 %copy-start.56 = (bf16[16,16,256]{2,1,0:T(8,128)(2,1)S(1)}, bf16[16,16,256]{2,1,0:T(8,128)(2,1)}, u32[]{:S(2)}) copy-start(bf16[16,16,256]{2,1,0:T(8,128)(2,1)} %param.18) | copy-start | bytes 393220
  2.5 19.4 %collective-permute-start.4 = (s32[1,2,8]{2,1,0:T(2,128)S(1)}, s32[1,2,8]{2,1,0:T(2,128)S(1)}, u32[]{:S(2)}, u32[]{:S(2)}) collective-permute-start(s32[1,2,8]{2,1,0:T(2,128)S(1)} %add_bitcast_fusion), channel_id=1, source_target_pairs={{0,16},{4,20},{8,24},{12,28},{16,0},{20,4},{24,8},{28,12},{1,17},{... | collective-permute-start | bytes 200 | tf_op jit(solution)/shard_map/ppermute | solution.py:188
  7.8 12.1 %copy-start.72 = (s32[1,1,4,2]{2,3,1,0:T(2,128)S(1)}, s32[1,1,4,2]{2,3,1,0:T(2,128)}, u32[]{:S(2)}) copy-start(s32[1,1,4,2]{2,3,1,0:T(2,128)} %param.16) | copy-start | bytes 100
  7.8 13.2 %copy-start.93 = (s32[8]{0:T(128)S(1)}, s32[8]{0:T(128)}, u32[]{:S(2)}) copy-start(s32[8]{0:T(128)} %constant.189) | copy-start | bytes 100
  7.9 27.4 %collective-permute-start.1 = (bf16[8,16,512]{2,1,0:T(8,128)(2,1)S(1)}, bf16[8,16,512]{2,1,0:T(8,128)(2,1)S(1)}, u32[]{:S(2)}, u32[]{:S(2)}) collective-permute-start(bf16[8,16,512]{2,1,0:T(8,128)(2,1)S(1)} %bitcast.521), channel_id=1, source_target_pairs={{4,0},{8,4},{12,8},{16,12},{20,16},{24,20},{28,24},{5,1},{9,5},{13... | collective-permute-start | bytes 393224 | tf_op jit(solution)/shard_map/ppermute | solution.py:27
  9.2 26.1 %collective-permute-start = (bf16[8,16,512]{2,1,0:T(8,128)(2,1)S(1)}, bf16[8,16,512]{2,1,0:T(8,128)(2,1)S(1)}, u32[]{:S(2)}, u32[]{:S(2)}) collective-permute-start(bf16[8,16,512]{2,1,0:T(8,128)(2,1)S(1)} %bitcast.520), channel_id=1, source_target_pairs={{0,4},{4,8},{8,12},{12,16},{16,20},{20,24},{24,28},{1,5},{5,9},{9,... | collective-permute-start | bytes 393224 | tf_op jit(solution)/shard_map/ppermute | solution.py:24
  14.2 17.6 %collective-permute-start.7 = (bf16[8,16,512]{2,1,0:T(8,128)(2,1)S(1)}, bf16[8,16,512]{2,1,0:T(8,128)(2,1)S(1)}, u32[]{:S(2)}, u32[]{:S(2)}) collective-permute-start(bf16[8,16,512]{2,1,0:T(8,128)(2,1)S(1)} %get-tuple-element.65), channel_id=1, source_target_pairs={{0,4},{4,8},{8,12},{12,16},{16,20},{20,24},{24,28},{1,5},{5,9},{9,... | collective-permute-start | bytes 393224 | tf_op jit(solution)/shard_map/ppermute | solution.py:24
  18.5 13.3 %collective-permute-start.8 = (bf16[8,16,512]{2,1,0:T(8,128)(2,1)S(1)}, bf16[8,16,512]{2,1,0:T(8,128)(2,1)S(1)}, u32[]{:S(2)}, u32[]{:S(2)}) collective-permute-start(bf16[8,16,512]{2,1,0:T(8,128)(2,1)S(1)} %get-tuple-element.66), channel_id=1, source_target_pairs={{4,0},{8,4},{12,8},{16,12},{20,16},{24,20},{28,24},{5,1},{9,5},{13... | collective-permute-start | bytes 393224 | tf_op jit(solution)/shard_map/ppermute | solution.py:27
  21.8 29.8 %copy-start.89 = (pred[2,2]{1,0:T(4,128)(4,1)}, pred[2,2]{1,0:T(4,128)(4,1)S(1)}, u32[]{:S(2)}) copy-start(pred[2,2]{1,0:T(4,128)(4,1)S(1)} %get-tuple-element.102) | copy-start | bytes 16
  21.9 4.3 %collective-permute-start.5 = (s32[2,2,8]{2,1,0:T(2,128)S(1)}, s32[2,2,8]{2,1,0:T(2,128)S(1)}, u32[]{:S(2)}, u32[]{:S(2)}) collective-permute-start(s32[2,2,8]{2,1,0:T(2,128)S(1)} %pad_add_fusion.2), channel_id=1, source_target_pairs={{0,8},{4,12},{8,0},{12,4},{16,24},{20,28},{24,16},{28,20},{1,9},{5... | collective-permute-start | bytes 392 | tf_op jit(solution)/shard_map/ppermute | solution.py:188
  24.7 32.5 %copy-start.55 = (bf16[2,2,64,2,128]{4,3,2,1,0:T(2,128)(2,1)}, bf16[2,2,64,2,128]{4,3,2,1,0:T(2,128)(2,1)S(1)}, u32[]{:S(2)}) copy-start(bf16[2,2,64,2,128]{4,3,2,1,0:T(2,128)(2,1)S(1)} %reshape_reshape.29) | copy-start | bytes 393220
  26.3 3.7 %collective-permute-start.6 = (s32[4,2,8]{2,1,0:T(2,128)S(1)}, s32[4,2,8]{2,1,0:T(2,128)S(1)}, u32[]{:S(2)}, u32[]{:S(2)}) collective-permute-start(s32[4,2,8]{2,1,0:T(2,128)S(1)} %pad_add_fusion.1), channel_id=1, source_target_pairs={{0,4},{4,0},{8,12},{12,8},{16,20},{20,16},{24,28},{28,24},{1,5},{5... | collective-permute-start | bytes 776 | tf_op jit(solution)/shard_map/ppermute | solution.py:188
  32.0 15.7 %collective-permute-start.9 = (bf16[32,8,512]{2,1,0:T(8,128)(2,1)S(1)}, bf16[32,8,512]{2,1,0:T(8,128)(2,1)}, u32[]{:S(2)}, u32[]{:S(2)}) collective-permute-start(bf16[32,8,512]{2,1,0:T(8,128)(2,1)S(1)} %get-tuple-element.55), channel_id=1, source_target_pairs={{0,1},{1,2},{2,3},{4,5},{5,6},{6,7},{8,9},{9,10},{10,11},{12,13},{... | collective-permute-start | bytes 786440 | tf_op jit(solution)/shard_map/ppermute | solution.py:24
  34.0 13.7 %collective-permute-start.10 = (bf16[32,8,512]{2,1,0:T(8,128)(2,1)S(1)}, bf16[32,8,512]{2,1,0:T(8,128)(2,1)}, u32[]{:S(2)}, u32[]{:S(2)}) collective-permute-start(bf16[32,8,512]{2,1,0:T(8,128)(2,1)S(1)} %get-tuple-element.56), channel_id=1, source_target_pairs={{1,0},{2,1},{3,2},{5,4},{6,5},{7,6},{9,8},{10,9},{11,10},{13,12},{... | collective-permute-start | bytes 786440 | tf_op jit(solution)/shard_map/ppermute | solution.py:27
  36.2 12.8 %collective-permute-start.2 = (bf16[32,8,512]{2,1,0:T(8,128)(2,1)}, bf16[32,8,512]{2,1,0:T(8,128)(2,1)}, u32[]{:S(2)}, u32[]{:S(2)}) collective-permute-start(bf16[32,8,512]{2,1,0:T(8,128)(2,1)} %get-tuple-element.59), channel_id=1, source_target_pairs={{0,1},{1,2},{2,3},{4,5},{5,6},{6,7},{8,9},{9,10},{10,11},{12,13},{... | collective-permute-start | bytes 786440 | tf_op jit(solution)/shard_map/ppermute | solution.py:24
  41.0 8.0 %collective-permute-start.3 = (bf16[32,8,512]{2,1,0:T(8,128)(2,1)}, bf16[32,8,512]{2,1,0:T(8,128)(2,1)}, u32[]{:S(2)}, u32[]{:S(2)}) collective-permute-start(bf16[32,8,512]{2,1,0:T(8,128)(2,1)} %get-tuple-element.60), channel_id=1, source_target_pairs={{1,0},{2,1},{3,2},{5,4},{6,5},{7,6},{9,8},{10,9},{11,10},{13,12},{... | collective-permute-start | bytes 786440 | tf_op jit(solution)/shard_map/ppermute | solution.py:27
  43.4 31.4 %all-to-all-start = ((bf16[8,2,64,512]{3,2,1,0:T(8,128)(2,1)}), bf16[8,2,64,512]{3,2,1,0:T(8,128)(2,1)}, u32[]{:S(2)}, u32[]{:S(2)}) async-start(bf16[8,2,64,512]{3,2,1,0:T(8,128)(2,1)} %broadcast_select_fusion), calls=%async_computation | async-start | bytes 2097152 | tf_op jit(solution)/shard_map/all_to_all | solution.py:250
  99.5 6.9 %copy-start.63 = (bf16[2,2,64,2,128]{4,2,3,1,0:T(8,128)(2,1)S(1)}, bf16[2,2,64,2,128]{4,2,3,1,0:T(8,128)(2,1)}, u32[]{:S(2)}) copy-start(bf16[2,2,64,2,128]{4,2,3,1,0:T(8,128)(2,1)} %get-tuple-element.131) | copy-start | bytes 393220
  100.0 6.7 %copy-start.57 = (bf16[16,16,256]{2,1,0:T(8,128)(2,1)S(1)}, bf16[16,16,256]{2,1,0:T(8,128)(2,1)}, u32[]{:S(2)}) copy-start(bf16[16,16,256]{2,1,0:T(8,128)(2,1)} %param.18) | copy-start | bytes 393220
  100.2 6.9 %copy-start.58 = (bf16[2,8,2,8,256]{4,3,2,1,0:T(8,128)(2,1)}, bf16[2,8,2,8,256]{4,3,2,1,0:T(8,128)(2,1)S(1)}, u32[]{:S(2)}) copy-start(bf16[2,8,2,8,256]{4,3,2,1,0:T(8,128)(2,1)S(1)} %copy.458) | copy-start | bytes 393220
  100.5 7.4 %collective-permute-start.12 = (f32[8,16,4]{1,0,2:T(8,128)S(1)}, f32[8,16,4]{1,0,2:T(8,128)S(1)}, u32[]{:S(2)}, u32[]{:S(2)}) collective-permute-start(f32[8,16,4]{1,0,2:T(8,128)S(1)} %slice.411), channel_id=1, source_target_pairs={{4,0},{8,4},{12,8},{16,12},{20,16},{24,20},{28,24},{5,1},{9,5},{13... | collective-permute-start | bytes 6152 | tf_op jit(solution)/shard_map/ppermute | solution.py:27
  101.9 6.0 %collective-permute-start.11 = (f32[8,16,4]{1,0,2:T(8,128)S(1)}, f32[8,16,4]{1,0,2:T(8,128)S(1)}, u32[]{:S(2)}, u32[]{:S(2)}) collective-permute-start(f32[8,16,4]{1,0,2:T(8,128)S(1)} %slice.409), channel_id=1, source_target_pairs={{0,4},{4,8},{8,12},{12,16},{16,20},{20,24},{24,28},{1,5},{5,9},{9,... | collective-permute-start | bytes 6152 | tf_op jit(solution)/shard_map/ppermute | solution.py:24
  108.0 7.0 %collective-permute-start.13 = (f32[32,8,4]{1,0,2:T(8,128)S(1)}, f32[32,8,4]{1,0,2:T(8,128)S(1)}, u32[]{:S(2)}, u32[]{:S(2)}) collective-permute-start(f32[32,8,4]{1,0,2:T(8,128)S(1)} %get-tuple-element.73), channel_id=1, source_target_pairs={{0,1},{1,2},{2,3},{4,5},{5,6},{6,7},{8,9},{9,10},{10,11},{12,13},{... | collective-permute-start | bytes 12296 | tf_op jit(solution)/shard_map/ppermute | solution.py:24
  109.3 6.8 %copy-start.39 = (bf16[2,2,8,2,8,128]{5,4,3,2,1,0:T(8,128)(2,1)S(1)}, bf16[2,2,8,2,8,128]{5,4,3,2,1,0:T(8,128)(2,1)}, u32[]{:S(2)}) copy-start(bf16[2,2,8,2,8,128]{5,4,3,2,1,0:T(8,128)(2,1)} %copy-done.38) | copy-start | bytes 393220
  109.3 6.8 %copy-start.44 = (bf16[2,2,8,2,8,128]{5,4,3,2,1,0:T(8,128)(2,1)S(1)}, bf16[2,2,8,2,8,128]{5,4,3,2,1,0:T(8,128)(2,1)}, u32[]{:S(2)}) copy-start(bf16[2,2,8,2,8,128]{5,4,3,2,1,0:T(8,128)(2,1)} %get-tuple-element.32) | copy-start | bytes 393220
  109.3 6.8 %copy-start.92 = (pred[2,2]{1,0:T(4,128)(4,1)S(1)}, pred[2,2]{1,0:T(4,128)(4,1)}, u32[]{:S(2)}) copy-start(pred[2,2]{1,0:T(4,128)(4,1)} %get-tuple-element.109) | copy-start | bytes 16
  109.3 5.7 %collective-permute-start.14 = (f32[32,8,4]{1,0,2:T(8,128)S(1)}, f32[32,8,4]{1,0,2:T(8,128)S(1)}, u32[]{:S(2)}, u32[]{:S(2)}) collective-permute-start(f32[32,8,4]{1,0,2:T(8,128)S(1)} %get-tuple-element.74), channel_id=1, source_target_pairs={{1,0},{2,1},{3,2},{5,4},{6,5},{7,6},{9,8},{10,9},{11,10},{13,12},{... | collective-permute-start | bytes 12296 | tf_op jit(solution)/shard_map/ppermute | solution.py:27
  111.7 29.1 %collective-permute-start.15 = (f32[256,256]{1,0:T(8,128)}, f32[256,256]{1,0:T(8,128)}, u32[]{:S(2)}, u32[]{:S(2)}) collective-permute-start(f32[256,256]{1,0:T(8,128)} %fusion.99), channel_id=1, source_target_pairs={{0,1},{1,0},{2,3},{3,2},{4,5},{5,4},{6,7},{7,6},{8,9},{9,8},{10,11... | collective-permute-start | bytes 786440 | tf_op jit(solution)/shard_map/ppermute | solution.py:223
  138.1 3.9 %collective-permute-start.23 = (f32[256,256]{1,0:T(8,128)S(1)}, f32[256,256]{1,0:T(8,128)S(1)}, u32[]{:S(2)}, u32[]{:S(2)}) collective-permute-start(f32[256,256]{1,0:T(8,128)S(1)} %fusion.96), channel_id=1, source_target_pairs={{0,1},{1,0},{2,3},{3,2},{4,5},{5,4},{6,7},{7,6},{8,9},{9,8},{10,11... | collective-permute-start | bytes 786440 | tf_op jit(solution)/shard_map/ppermute | solution.py:223
  141.9 6.4 %collective-permute-start.16 = (f32[128,256]{1,0:T(8,128)S(1)}, f32[128,256]{1,0:T(8,128)S(1)}, u32[]{:S(2)}, u32[]{:S(2)}) collective-permute-start(f32[128,256]{1,0:T(8,128)S(1)} %constant_dynamic-slice_fusion.2), channel_id=1, source_target_pairs={{0,2},{1,3},{2,0},{3,1},{4,6},{5,7},{6,4},{7,5},{8,10},{9,11},{10,... | collective-permute-start | bytes 393224 | tf_op jit(solution)/shard_map/ppermute | solution.py:223
  142.1 23.2 %copy-start.31 = (bf16[256,256]{1,0:T(8,128)(2,1)S(1)}, bf16[256,256]{1,0:T(8,128)(2,1)}, u32[]{:S(2)}) copy-start(bf16[256,256]{1,0:T(8,128)(2,1)} %param.14) | copy-start | bytes 393220
  142.1 8.6 %collective-permute-start.24 = (f32[128,256]{1,0:T(8,128)S(1)}, f32[128,256]{1,0:T(8,128)S(1)}, u32[]{:S(2)}, u32[]{:S(2)}) collective-permute-start(f32[128,256]{1,0:T(8,128)S(1)} %constant_dynamic-slice_fusion), channel_id=1, source_target_pairs={{0,2},{1,3},{2,0},{3,1},{4,6},{5,7},{6,4},{7,5},{8,10},{9,11},{10,... | collective-permute-start | bytes 393224 | tf_op jit(solution)/shard_map/ppermute | solution.py:223
  148.3 5.0 %collective-permute-start.17 = (f32[64,256]{1,0:T(8,128)S(1)}, f32[64,256]{1,0:T(8,128)S(1)}, u32[]{:S(2)}, u32[]{:S(2)}) collective-permute-start(f32[64,256]{1,0:T(8,128)S(1)} %constant_dynamic-slice_fusion.1), channel_id=1, source_target_pairs={{0,4},{4,0},{8,12},{12,8},{16,20},{20,16},{24,28},{28,24},{1,5},{5... | collective-permute-start | bytes 196616 | tf_op jit(solution)/shard_map/ppermute | solution.py:223
  150.8 6.6 %collective-permute-start.25 = (f32[64,256]{1,0:T(8,128)S(1)}, f32[64,256]{1,0:T(8,128)S(1)}, u32[]{:S(2)}, u32[]{:S(2)}) collective-permute-start(f32[64,256]{1,0:T(8,128)S(1)} %constant_dynamic-slice_fusion.3), channel_id=1, source_target_pairs={{0,4},{4,0},{8,12},{12,8},{16,20},{20,16},{24,28},{28,24},{1,5},{5... | collective-permute-start | bytes 196616 | tf_op jit(solution)/shard_map/ppermute | solution.py:223
  153.4 6.4 %collective-permute-start.18 = (f32[64,256]{1,0:T(8,128)S(1)}, f32[64,256]{1,0:T(8,128)S(1)}, u32[]{:S(2)}, u32[]{:S(2)}) collective-permute-start(f32[64,256]{1,0:T(8,128)S(1)} %dynamic-slice_add_fusion.3), channel_id=1, source_target_pairs={{0,8},{4,12},{8,0},{12,4},{16,24},{20,28},{24,16},{28,20},{1,9},{5... | collective-permute-start | bytes 196616 | tf_op jit(solution)/shard_map/ppermute | solution.py:226
  157.4 4.9 %collective-permute-start.26 = (f32[64,256]{1,0:T(8,128)S(1)}, f32[64,256]{1,0:T(8,128)S(1)}, u32[]{:S(2)}, u32[]{:S(2)}) collective-permute-start(f32[64,256]{1,0:T(8,128)S(1)} %dynamic-slice_add_fusion.2), channel_id=1, source_target_pairs={{0,8},{4,12},{8,0},{12,4},{16,24},{20,28},{24,16},{28,20},{1,9},{5... | collective-permute-start | bytes 196616 | tf_op jit(solution)/shard_map/ppermute | solution.py:226
  159.8 5.3 %collective-permute-start.19 = (f32[64,256]{1,0:T(8,128)S(1)}, f32[64,256]{1,0:T(8,128)S(1)}, u32[]{:S(2)}, u32[]{:S(2)}) collective-permute-start(f32[64,256]{1,0:T(8,128)S(1)} %add.446), channel_id=1, source_target_pairs={{0,16},{4,20},{8,24},{12,28},{16,0},{20,4},{24,8},{28,12},{1,17},{... | collective-permute-start | bytes 196616 | tf_op jit(solution)/shard_map/ppermute | solution.py:226
  162.3 6.0 %collective-permute-start.27 = (f32[64,256]{1,0:T(8,128)S(1)}, f32[64,256]{1,0:T(8,128)S(1)}, u32[]{:S(2)}, u32[]{:S(2)}) collective-permute-start(f32[64,256]{1,0:T(8,128)S(1)} %add.451), channel_id=1, source_target_pairs={{0,16},{4,20},{8,24},{12,28},{16,0},{20,4},{24,8},{28,12},{1,17},{... | collective-permute-start | bytes 196616 | tf_op jit(solution)/shard_map/ppermute | solution.py:226
  165.1 4.3 %collective-permute-start.20 = (f32[64,256]{1,0:T(8,128)S(1)}, f32[64,256]{1,0:T(8,128)S(1)}, u32[]{:S(2)}, u32[]{:S(2)}) collective-permute-start(f32[64,256]{1,0:T(8,128)S(1)} %add.447), channel_id=1, source_target_pairs={{0,4},{4,0},{8,12},{12,8},{16,20},{20,16},{24,28},{28,24},{1,5},{5... | collective-permute-start | bytes 196616 | tf_op jit(solution)/shard_map/ppermute | solution.py:188
  168.3 4.3 %collective-permute-start.28 = (f32[64,256]{1,0:T(8,128)S(1)}, f32[64,256]{1,0:T(8,128)S(1)}, u32[]{:S(2)}, u32[]{:S(2)}) collective-permute-start(f32[64,256]{1,0:T(8,128)S(1)} %add.452), channel_id=1, source_target_pairs={{0,4},{4,0},{8,12},{12,8},{16,20},{20,16},{24,28},{28,24},{1,5},{5... | collective-permute-start | bytes 196616 | tf_op jit(solution)/shard_map/ppermute | solution.py:188
  169.4 5.0 %collective-permute-start.21 = (f32[128,256]{1,0:T(8,128)S(1)}, f32[128,256]{1,0:T(8,128)S(1)}, u32[]{:S(2)}, u32[]{:S(2)}) collective-permute-start(f32[128,256]{1,0:T(8,128)S(1)} %pad_maximum_fusion.7), channel_id=1, source_target_pairs={{0,2},{1,3},{2,0},{3,1},{4,6},{5,7},{6,4},{7,5},{8,10},{9,11},{10,... | collective-permute-start | bytes 393224 | tf_op jit(solution)/shard_map/ppermute | solution.py:188
  172.7 5.0 %collective-permute-start.29 = (f32[128,256]{1,0:T(8,128)S(1)}, f32[128,256]{1,0:T(8,128)S(1)}, u32[]{:S(2)}, u32[]{:S(2)}) collective-permute-start(f32[128,256]{1,0:T(8,128)S(1)} %pad_maximum_fusion.8), channel_id=1, source_target_pairs={{0,2},{1,3},{2,0},{3,1},{4,6},{5,7},{6,4},{7,5},{8,10},{9,11},{10,... | collective-permute-start | bytes 393224 | tf_op jit(solution)/shard_map/ppermute | solution.py:188
  174.5 4.4 %collective-permute-start.22 = (f32[256,256]{1,0:T(8,128)S(1)}, f32[256,256]{1,0:T(8,128)S(1)}, u32[]{:S(2)}, u32[]{:S(2)}) collective-permute-start(f32[256,256]{1,0:T(8,128)S(1)} %pad_maximum_fusion.4), channel_id=1, source_target_pairs={{0,1},{1,0},{2,3},{3,2},{4,5},{5,4},{6,7},{7,6},{8,9},{9,8},{10,11... | collective-permute-start | bytes 786440 | tf_op jit(solution)/shard_map/ppermute | solution.py:188
  177.8 1.9 %collective-permute-start.30 = (f32[256,256]{1,0:T(8,128)S(1)}, f32[256,256]{1,0:T(8,128)S(1)}, u32[]{:S(2)}, u32[]{:S(2)}) collective-permute-start(f32[256,256]{1,0:T(8,128)S(1)} %pad_maximum_fusion.5), channel_id=1, source_target_pairs={{0,1},{1,0},{2,3},{3,2},{4,5},{5,4},{6,7},{7,6},{8,9},{9,8},{10,11... | collective-permute-start | bytes 786440 | tf_op jit(solution)/shard_map/ppermute | solution.py:188
  (78 other events, 148.2 us)

commit v11 on v8

--- a/solution.py
+++ b/solution.py
@@ -49,50 +49,46 @@
     return source.reshape(source.shape[:-1] + (HEADS, source.shape[-1] // HEADS))
 
 
-def key_pieces(keyval_pad, key_valid, region_keyval):
-    block_rows, block_cols = (region_keyval.shape[0], region_keyval.shape[1])
-    pieces = []
+def neighbour_set(padded_blocks, valid_blocks, block_rows, block_cols, axis):
+    parts = []
+    valid = []
     for row_off in range(3):
         for col_off in range(3):
-            key_block = keyval_pad[row_off : row_off + block_rows, col_off : col_off + block_cols]
-            valid_mask = key_valid[row_off : row_off + block_rows, col_off : col_off + block_cols]
-            pieces.append((key_block[..., :D], key_block[..., D:], valid_mask))
+            part = padded_blocks[row_off : row_off + block_rows, col_off : col_off + block_cols]
+            parts.append(part)
+            mask = valid_blocks[row_off : row_off + block_rows, col_off : col_off + block_cols]
+            valid.append(jnp.broadcast_to(mask[:, :, None], (block_rows, block_cols, BT)))
+    return jnp.concatenate(parts, axis), jnp.concatenate(valid, 2)
+
+
+def key_set(keyval_pad, key_valid, region_keyval):
+    block_rows, block_cols = (region_keyval.shape[0], region_keyval.shape[1])
+    keyvals, valid = neighbour_set(keyval_pad, key_valid, block_rows, block_cols, 2)
     merged = region_keyval.reshape(block_rows, block_cols, 2 * BT, 2 * D)
-    pieces.append(
-        (merged[..., :D], merged[..., D:], jnp.ones((block_rows, block_cols), dtype=jnp.bool_))
-    )
-    return pieces
-
-
-def piece_scores(query_heads, key_part, valid_mask):
+    keyvals = jnp.concatenate([keyvals, merged], 2)
+    valid = jnp.concatenate([valid, jnp.ones((block_rows, block_cols, 2 * BT), jnp.bool_)], 2)
+    return keyvals[..., :D], keyvals[..., D:], valid
+
+
+def set_scores(query_heads, key_part, valid):
     scores = jnp.einsum(
         "abqhe,abkhe->abhqk", query_heads, split_heads(key_part), preferred_element_type=jnp.float32
     )
     scores = scores * (1.0 / math.sqrt(HEAD_DIM))
-    return jnp.where(valid_mask[:, :, None, None, None], scores, masked_score)
+    return jnp.where(valid[:, :, None, None, :], scores, masked_score)
 
 
 def attend_forward(query_blocks, keyval_pad, key_valid, region_keyval):
     query_heads = split_heads(query_blocks)
-    pieces = key_pieces(keyval_pad, key_valid, region_keyval)
-    scores = [
-        piece_scores(query_heads, key_part, valid_mask)
-        for key_part, value_part, valid_mask in pieces
-    ]
-    row_top = jnp.max(jnp.concatenate(scores, -1), -1, keepdims=True)
-    row_total = sum(
-        (jnp.sum(jnp.exp(part_scores - row_top), -1, keepdims=True) for part_scores in scores)
-    )
+    key_part, value_part, valid = key_set(keyval_pad, key_valid, region_keyval)
+    scores = set_scores(query_heads, key_part, valid)
+    row_top = jnp.max(scores, -1, keepdims=True)
+    row_total = jnp.sum(jnp.exp(scores - row_top), -1, keepdims=True)
     log_total = row_top + jnp.log(row_total)
-    mixed_sum = jnp.zeros(query_heads.shape, jnp.float32)
-    for part_scores, (key_part, value_part, valid_mask) in zip(scores, pieces):
-        weights = jnp.exp(part_scores - log_total).astype(jnp.bfloat16)
-        mixed_sum = mixed_sum + jnp.einsum(
-            "abhqk,abkhe->abqhe",
-            weights,
-            split_heads(value_part),
-            preferred_element_type=jnp.float32,
-        )
+    weights = jnp.exp(scores - log_total).astype(jnp.bfloat16)
+    mixed_sum = jnp.einsum(
+        "abhqk,abkhe->abqhe", weights, split_heads(value_part), preferred_element_type=jnp.float32
+    )
     output = mixed_sum.reshape(query_blocks.shape).astype(jnp.bfloat16)
     return (output, log_total[..., 0])
 
@@ -102,23 +98,16 @@
 ):
     query_heads = split_heads(query_blocks)
     dout_heads = split_heads(dout_blocks)
-    accum_sum = jnp.zeros(query_heads.shape, jnp.float32)
-    for key_part, value_part, valid_mask in key_pieces(keyval_pad, key_valid, region_keyval):
-        part_scores = piece_scores(query_heads, key_part, valid_mask)
-        prob_part = jnp.exp(part_scores - log_total[..., None])
-        grad_prob = jnp.einsum(
-            "abqhe,abkhe->abhqk",
-            dout_heads,
-            split_heads(value_part),
-            preferred_element_type=jnp.float32,
-        )
-        grad_score = (prob_part * (grad_prob - delta_rows[..., None])).astype(jnp.bfloat16)
-        accum_sum = accum_sum + jnp.einsum(
-            "abhqk,abkhe->abqhe",
-            grad_score,
-            split_heads(key_part),
-            preferred_element_type=jnp.float32,
-        )
+    key_part, value_part, valid = key_set(keyval_pad, key_valid, region_keyval)
+    scores = set_scores(query_heads, key_part, valid)
+    prob = jnp.exp(scores - log_total[..., None])
+    grad_prob = jnp.einsum(
+        "abqhe,abkhe->abhqk", dout_heads, split_heads(value_part), preferred_element_type=jnp.float32
+    )
+    grad_score = (prob * (grad_prob - delta_rows[..., None])).astype(jnp.bfloat16)
+    accum_sum = jnp.einsum(
+        "abhqk,abkhe->abqhe", grad_score, split_heads(key_part), preferred_element_type=jnp.float32
+    )
     return (
         (accum_sum * (1.0 / math.sqrt(HEAD_DIM))).reshape(query_blocks.shape).astype(jnp.bfloat16)
     )
@@ -128,37 +117,27 @@
     block_rows, block_cols = (keyval_center.shape[0], keyval_center.shape[1])
     key_heads = split_heads(keyval_center[..., :D])
     value_heads = split_heads(keyval_center[..., D:])
-    grad_key = jnp.zeros(key_heads.shape, jnp.float32)
-    grad_value = jnp.zeros(key_heads.shape, jnp.float32)
-    for row_off in range(3):
-        for col_off in range(3):
-            query_heads = split_heads(
-                query_pad[row_off : row_off + block_rows, col_off : col_off + block_cols]
-            )
-            dout_heads = split_heads(
-                dout_pad[row_off : row_off + block_rows, col_off : col_off + block_cols]
-            )
-            log_part = log_pad[row_off : row_off + block_rows, col_off : col_off + block_cols]
-            delta_part = delta_pad[row_off : row_off + block_rows, col_off : col_off + block_cols]
-            valid_mask = query_valid[row_off : row_off + block_rows, col_off : col_off + block_cols]
-            part_scores = jnp.einsum(
-                "abqhe,abkhe->abhqk", query_heads, key_heads, preferred_element_type=jnp.float32
-            )
-            part_scores = part_scores * (1.0 / math.sqrt(HEAD_DIM))
-            prob_part = jnp.where(
-                valid_mask[:, :, None, None, None], jnp.exp(part_scores - log_part[..., None]), 0.0
-            )
-            grad_prob = jnp.einsum(
-                "abqhe,abkhe->abhqk", dout_heads, value_heads, preferred_element_type=jnp.float32
-            )
-            grad_score = (prob_part * (grad_prob - delta_part[..., None])).astype(jnp.bfloat16)
-            grad_key = grad_key + jnp.einsum(
-                "abhqk,abqhe->abkhe", grad_score, query_heads, preferred_element_type=jnp.float32
-            )
-            rounded_prob = prob_part.astype(jnp.bfloat16)
-            grad_value = grad_value + jnp.einsum(
-                "abhqk,abqhe->abkhe", rounded_prob, dout_heads, preferred_element_type=jnp.float32
-            )
+    queries, valid = neighbour_set(query_pad, query_valid, block_rows, block_cols, 2)
+    douts, _ = neighbour_set(dout_pad, query_valid, block_rows, block_cols, 2)
+    logs, _ = neighbour_set(log_pad, query_valid, block_rows, block_cols, 3)
+    deltas, _ = neighbour_set(delta_pad, query_valid, block_rows, block_cols, 3)
+    query_heads = split_heads(queries)
+    dout_heads = split_heads(douts)
+    scores = jnp.einsum(
+        "abqhe,abkhe->abhqk", query_heads, key_heads, preferred_element_type=jnp.float32
+    )
+    scores = scores * (1.0 / math.sqrt(HEAD_DIM))
+    prob = jnp.where(valid[:, :, None, :, None], jnp.exp(scores - logs[..., None]), 0.0)
+    grad_prob = jnp.einsum(
+        "abqhe,abkhe->abhqk", dout_heads, value_heads, preferred_element_type=jnp.float32
+    )
+    grad_score = (prob * (grad_prob - deltas[..., None])).astype(jnp.bfloat16)
+    grad_key = jnp.einsum(
+        "abhqk,abqhe->abkhe", grad_score, query_heads, preferred_element_type=jnp.float32
+    )
+    grad_value = jnp.einsum(
+        "abhqk,abqhe->abkhe", prob.astype(jnp.bfloat16), dout_heads, preferred_element_type=jnp.float32
+    )
     out_shape = (block_rows, block_cols, BT, D)
     grad_key = (grad_key * (1.0 / math.sqrt(HEAD_DIM))).reshape(out_shape).astype(jnp.bfloat16)
     return (grad_key, grad_value.reshape(out_shape).astype(jnp.bfloat16))

time: 176 us -> 145 us (0.82)
  matrix products: 49.1 us -> 16.7 us
  local copies, waits for them, and re-layouts: 19.9 us -> 23.4 us
  starting transfers between devices: 52.7 us -> 50.2 us
    dot_general x9 -> x1, matrix products: 16 us -> 2.67 us  [key_grads(): jnp.einsum('abhqk,abqhe->abkhe', grad_score, query_heads, preferred_eleme...]
    dot_general x10 -> x1, matrix products: 12.1 us -> 3.08 us  [query_grads(): jnp.einsum('abhqk,abkhe->abqhe', grad_score, split_heads(key_part), prefe...]
    dot_general x19 -> x2, matrix products: 8.82 us -> 1.12 us  [the longest x1 0.77 us: set_scores(): jnp.einsum('abqhe,abkhe->abhqk', query_heads, split_heads(key_part), pref...]
    unnamed x195 -> x70, local copies, waits for them, and re-layouts: 8.31 us -> 12 us
    slice x5 -> x2, local copies, waits for them, and re-layouts: 3.41 us -> 0.11 us  [the longest x1 0.08 us: neighbour_set(): valid_blocks[row_off:row_off + block_rows, col_off:col_off + block_cols]]
    dot_general x10 -> x1, matrix products: 3.12 us -> 1.17 us  [attend_forward(): jnp.einsum('abhqk,abkhe->abqhe', weights, split_heads(value_part), prefer...]
  transfers between devices with their start and end apart: 24 -> 24, of which waited for: 13 -> 13; matrix products, arithmetic and copies ran while one was open for 11% -> 15% of each run, Pallas kernels for 0% -> 0%
where the time goes in v11:
time: 145 us; the launch traced here: 144 us
  starting transfers between devices  50.2 us (35%)
  waiting for transfers between devices  48 us (33%)
  local copies, waits for them, and re-layouts  23.4 us (16%)
  matrix products  16.7 us (12%)
  other arithmetic  4.22 us (3%)
  between operations  1.71 us (1%)
    ppermute x6, starting transfers between devices, padded(): lax.ppermute(lax.slice_in_dim(block, block.shape[dim] - width, None, axis...  19.1 us
    ppermute x6, waiting for transfers between devices, doubling_gather(): got = lax.ppermute(joined, axis, pairs)  14.1 us
    ppermute x3, waiting for transfers between devices, tree_sum(): joined = keep + lax.ppermute(send, axis, pairs)  13.4 us
    unnamed x70, local copies, waits for them, and re-layouts  12 us
    ppermute x6, starting transfers between devices, doubling_gather(): got = lax.ppermute(joined, axis, pairs)  11.4 us
    ppermute x2, waiting for transfers between devices, tree_sum(): joined = joined + lax.ppermute(joined, axis, pairs)  8.95 us
    ppermute x6, starting transfers between devices, padded(): lax.ppermute(lax.slice_in_dim(block, 0, width, axis=dim), axis, backward)  7.92 us
    ppermute x6, waiting for transfers between devices, padded(): lax.ppermute(lax.slice_in_dim(block, 0, width, axis=dim), axis, backward)  6.5 us
  transfers between devices with their start and end apart: 24, of which 13 were waited for; matrix products, arithmetic and copies ran while one was open for 15% of the time, Pallas kernels for 0%

profile of v11, /device:TPU:0, one launch (start us, length us, event | category | flops | bytes accessed | tf_op | source)
XLA Modules:
  0.0 144.2 jit_solution(241629981467573793)
XLA Ops:
  0.7 0.8 copy.118
  2.5 4.1 %collective-permute-start.4 = (s32[1,2,8]{2,1,0:T(2,128)S(1)}, s32[1,2,8]{2,1,0:T(2,128)S(1)}, u32[]{:S(2)}, u32[]{:S(2)}) collective-permute-start(s32[1,2,8]{2,1,0:T(2,128)S(1)} %add_bitcast_fusion), channel_id=1, source_target_pairs={{0,16},{4,20},{8,24},{12,28},{16,0},{20,4},{24,8},{28,12},{1,17},{... | collective-permute-start | bytes 200 | tf_op jit(solution)/shard_map/ppermute | solution.py:167
  6.6 1.3 convolution_convert_fusion
  7.9 3.4 %collective-permute-start = (bf16[8,16,512]{2,1,0:T(8,128)(2,1)S(1)}, bf16[8,16,512]{2,1,0:T(8,128)(2,1)S(1)}, u32[]{:S(2)}, u32[]{:S(2)}) collective-permute-start(bf16[8,16,512]{2,1,0:T(8,128)(2,1)S(1)} %bitcast.274), channel_id=1, source_target_pairs={{0,4},{4,8},{8,12},{12,16},{16,20},{20,24},{24,28},{1,5},{5,9},{9,... | collective-permute-start | bytes 393224 | tf_op jit(solution)/shard_map/ppermute | solution.py:24
  11.3 1.3 collective-permute-start.1
  12.6 1.2 convolution_convert_fusion.4
  14.0 4.5 %collective-permute-start.7 = (bf16[8,16,512]{2,1,0:T(8,128)(2,1)S(1)}, bf16[8,16,512]{2,1,0:T(8,128)(2,1)S(1)}, u32[]{:S(2)}, u32[]{:S(2)}) collective-permute-start(bf16[8,16,512]{2,1,0:T(8,128)(2,1)S(1)} %get-tuple-element.42), channel_id=1, source_target_pairs={{0,4},{4,8},{8,12},{12,16},{16,20},{20,24},{24,28},{1,5},{5,9},{9,... | collective-permute-start | bytes 393224 | tf_op jit(solution)/shard_map/ppermute | solution.py:24
  18.6 1.3 collective-permute-start.8
  23.4 4.6 %collective-permute-start.5 = (s32[2,2,8]{2,1,0:T(2,128)S(1)}, s32[2,2,8]{2,1,0:T(2,128)S(1)}, u32[]{:S(2)}, u32[]{:S(2)}) collective-permute-start(s32[2,2,8]{2,1,0:T(2,128)S(1)} %pad_add_fusion.2), channel_id=1, source_target_pairs={{0,8},{4,12},{8,0},{12,4},{16,24},{20,28},{24,16},{28,20},{1,9},{5... | collective-permute-start | bytes 392 | tf_op jit(solution)/shard_map/ppermute | solution.py:167
  28.0 1.6 %collective-permute-done.5 = s32[2,2,8]{2,1,0:T(2,128)S(1)} collective-permute-done((s32[2,2,8]{2,1,0:T(2,128)S(1)}, s32[2,2,8]{2,1,0:T(2,128)S(1)}, u32[]{:S(2)}, u32[]{:S(2)}) %collective-permute-start.5) | collective-permute-done | bytes 160 | tf_op jit(solution)/shard_map/ppermute | solution.py:167
  30.2 3.0 %collective-permute-done.6 = s32[4,2,8]{2,1,0:T(2,128)S(1)} collective-permute-done((s32[4,2,8]{2,1,0:T(2,128)S(1)}, s32[4,2,8]{2,1,0:T(2,128)S(1)}, u32[]{:S(2)}, u32[]{:S(2)}) %collective-permute-start.6) | collective-permute-done | bytes 288 | tf_op jit(solution)/shard_map/ppermute | solution.py:167
  35.2 1.2 broadcast_select_fusion
  36.4 3.6 %all-to-all-start = ((bf16[8,2,64,512]{3,2,1,0:T(8,128)(2,1)}), bf16[8,2,64,512]{3,2,1,0:T(8,128)(2,1)S(1)}, u32[]{:S(2)}, u32[]{:S(2)}) async-start(bf16[8,2,64,512]{3,2,1,0:T(8,128)(2,1)} %broadcast_select_fusion), calls=%async_computation | async-start | bytes 2097152 | tf_op jit(solution)/shard_map/all_to_all | solution.py:229
  40.1 1.3 collective-permute-start.2
  41.4 1.3 collective-permute-start.3
  42.8 1.3 collective-permute-start.10
  44.1 5.4 %collective-permute-start.9 = (bf16[32,8,512]{2,1,0:T(8,128)(2,1)S(1)}, bf16[32,8,512]{2,1,0:T(8,128)(2,1)S(1)}, u32[]{:S(2)}, u32[]{:S(2)}) collective-permute-start(bf16[32,8,512]{2,1,0:T(8,128)(2,1)S(1)} %get-tuple-element.36), channel_id=1, source_target_pairs={{0,1},{1,2},{2,3},{4,5},{5,6},{6,7},{8,9},{9,10},{10,11},{12,13},{... | collective-permute-start | bytes 786440 | tf_op jit(solution)/shard_map/ppermute | solution.py:24
  57.7 5.0 %all-to-all-done = bf16[8,2,64,512]{3,2,1,0:T(8,128)(2,1)S(1)} async-done(((bf16[8,2,64,512]{3,2,1,0:T(8,128)(2,1)}), bf16[8,2,64,512]{3,2,1,0:T(8,128)(2,1)S(1)}, u32[]{:S(2)}, u32[]{:S(2)}) %all-to-all-start) | async-done | bytes 1048608 | tf_op jit(solution)/shard_map/all_to_all | solution.py:229
  63.3 1.0 select_dynamic-update-slice_fusion
  64.3 2.3 %slice_bitcast_fusion.1 = (bf16[2,2,88,2,8,128]{5,4,3,2,1,0:T(8,128)(2,1)S(1)}, bf16[2,2,88,2,8,128]{5,4,3,2,1,0:T(8,128)(2,1)S(1)}) fusion(bf16[2,2,704,512]{3,2,1,0:T(8,128)(2,1)} %select_dynamic-update-slice_fusion), kind=kLoop, calls=%fused_computation.14 | loop fusion | bytes 5767168
  67.9 1.2 multiply_reduce_fusion
  69.0 3.1 %fusion.62 = bf16[2,2,64,2,128]{4,2,3,1,0:T(8,128)(2,1)} fusion(bf16[2,2,88,2,8,128]{5,4,3,2,1,0:T(8,128)(2,1)S(1)} %get-tuple-element.6, f32[2,2,2,64,704]{4,3,2,1,0:T(8,128)S(1)} %get-tuple-element.84, bf16[2,2,88,2,8,128]{5,4,3,2,1,0:T(8,128)(2,1)} %copy-done.1, f32[2,2,2,64]{3,2,1,0:T(2,128)S(1)} %bitcast.275, f32[2,2,2,64]{3,2,1,0:T(2,128)S(1)} %log_add_fusion, ...), kind=kOutput, calls=%fused_computation.50 | convolution fusion | flops 186122240 | bytes 4591616 | tf_op jit(solution)/shard_map/abhqk,abkhe->abqhe/dot_general | solution.py:108
  72.1 1.1 copy.137
  73.6 3.1 %collective-permute-start.11 = (f32[8,16,4]{1,0,2:T(8,128)S(1)}, f32[8,16,4]{1,0,2:T(8,128)S(1)}, u32[]{:S(2)}, u32[]{:S(2)}) collective-permute-start(f32[8,16,4]{1,0,2:T(8,128)S(1)} %slice.355), channel_id=1, source_target_pairs={{0,4},{4,8},{8,12},{12,16},{16,20},{20,24},{24,28},{1,5},{5,9},{9,... | collective-permute-start | bytes 6152 | tf_op jit(solution)/shard_map/ppermute | solution.py:24
  76.7 0.9 convolution_bitcast_fusion.2
  77.9 1.3 collective-permute-start.12
  79.5 4.0 %collective-permute-done.12 = f32[8,16,4]{1,0,2:T(8,128)S(1)} collective-permute-done((f32[8,16,4]{1,0,2:T(8,128)S(1)}, f32[8,16,4]{1,0,2:T(8,128)S(1)}, u32[]{:S(2)}, u32[]{:S(2)}) %collective-permute-start.12) | collective-permute-done | bytes 2080 | tf_op jit(solution)/shard_map/ppermute | solution.py:27
  83.6 1.3 collective-permute-start.13
  84.9 1.5 %collective-permute-start.14 = (f32[32,8,4]{1,0,2:T(8,128)S(1)}, f32[32,8,4]{1,0,2:T(8,128)S(1)}, u32[]{:S(2)}, u32[]{:S(2)}) collective-permute-start(f32[32,8,4]{1,0,2:T(8,128)S(1)} %get-tuple-element.47), channel_id=1, source_target_pairs={{1,0},{2,1},{3,2},{5,4},{6,5},{7,6},{9,8},{10,9},{11,10},{13,12},{... | collective-permute-start | bytes 12296 | tf_op jit(solution)/shard_map/ppermute | solution.py:27
  86.4 0.9 fusion.116
  87.4 2.5 %collective-permute-done.14 = f32[32,8,4]{1,0,2:T(8,128)S(1)} collective-permute-done((f32[32,8,4]{1,0,2:T(8,128)S(1)}, f32[32,8,4]{1,0,2:T(8,128)S(1)}, u32[]{:S(2)}, u32[]{:S(2)}) %collective-permute-start.14) | collective-permute-done | bytes 4128 | tf_op jit(solution)/shard_map/ppermute | solution.py:27
  90.5 1.9 %fusion.9 = f32[2,2,2,576,64]{3,4,2,1,0:T(8,128)S(1)} fusion(f32[2,2,2,576]{3,2,1,0:T(2,128)S(1)} %concatenate.90, pred[2,2,576]{2,1,0:T(4,128)(4,1)S(1)} %copy-done.20, bf16[2,2,8,2,8,128]{5,4,3,2,1,0:T(8,128)(2,1)} %get-tuple-element.11, bf16[2,2,576,256]{3,2,1,0:T(8,128)(2,1)} %copy-done.19), kind=kOutput, calls=%fused_computation.20 | convolution fusion | flops 76382208 | bytes 2511104 | tf_op jit(solution)/shard_map/abqhe,abkhe->abhqk/dot_general | solution.py:126
  93.3 2.7 %fusion.57 = bf16[2,2,64,2,128]{4,2,3,1,0:T(8,128)(2,1)} fusion(f32[2,2,2,576,64]{3,4,2,1,0:T(8,128)S(1)} %fusion.9, f32[2,2,2,576]{3,2,1,0:T(2,128)S(1)} %concatenate.92, bf16[2,2,8,2,8,128]{5,4,3,2,1,0:T(8,128)(2,1)S(1)} %copy-done.18, bf16[2,2,576,256]{3,2,1,0:T(8,128)(2,1)S(1)} %copy-done.4, bf16[2,2,576,256]{3,2,1,0:T(8,128)(2,1)} %copy-done.19), kind=kOutput, calls=%fused_computation.49 | convolution fusion | flops 152010752 | bytes 3819520 | tf_op jit(solution)/shard_map/abhqk,abqhe->abkhe/dot_general | solution.py:135
  96.0 1.1 copy.149
  98.0 3.0 %collective-permute-start.15 = (f32[512,256]{1,0:T(8,128)S(1)}, f32[512,256]{1,0:T(8,128)S(1)}, u32[]{:S(2)}, u32[]{:S(2)}) collective-permute-start(f32[512,256]{1,0:T(8,128)S(1)} %constant_dynamic-slice_fusion.1), channel_id=1, source_target_pairs={{0,1},{1,0},{2,3},{3,2},{4,5},{5,4},{6,7},{7,6},{8,9},{9,8},{10,11... | collective-permute-start | bytes 1572872 | tf_op jit(solution)/shard_map/ppermute | solution.py:202
  101.0 1.5 %collective-permute-done.15 = f32[512,256]{1,0:T(8,128)S(1)} collective-permute-done((f32[512,256]{1,0:T(8,128)S(1)}, f32[512,256]{1,0:T(8,128)S(1)}, u32[]{:S(2)}, u32[]{:S(2)}) %collective-permute-start.15) | collective-permute-done | bytes 524320 | tf_op jit(solution)/shard_map/ppermute | solution.py:202
  103.0 8.4 %collective-permute-done.16 = f32[256,256]{1,0:T(8,128)S(1)} collective-permute-done((f32[256,256]{1,0:T(8,128)S(1)}, f32[256,256]{1,0:T(8,128)S(1)}, u32[]{:S(2)}, u32[]{:S(2)}) %collective-permute-start.16) | collective-permute-done | bytes 262176 | tf_op jit(solution)/shard_map/ppermute | solution.py:202
  111.4 1.6 %collective-permute-start.17 = (f32[128,256]{1,0:T(8,128)S(1)}, f32[128,256]{1,0:T(8,128)S(1)}, u32[]{:S(2)}, u32[]{:S(2)}) collective-permute-start(f32[128,256]{1,0:T(8,128)S(1)} %constant_dynamic-slice_fusion.2), channel_id=1, source_target_pairs={{0,4},{4,0},{8,12},{12,8},{16,20},{20,16},{24,28},{28,24},{1,5},{5... | collective-permute-start | bytes 393224 | tf_op jit(solution)/shard_map/ppermute | solution.py:202
  113.0 3.5 %collective-permute-done.17 = f32[128,256]{1,0:T(8,128)S(1)} collective-permute-done((f32[128,256]{1,0:T(8,128)S(1)}, f32[128,256]{1,0:T(8,128)S(1)}, u32[]{:S(2)}, u32[]{:S(2)}) %collective-permute-start.17) | collective-permute-done | bytes 131104 | tf_op jit(solution)/shard_map/ppermute | solution.py:202
  116.5 1.3 collective-permute-start.18
  117.7 3.8 %collective-permute-done.18 = f32[128,256]{1,0:T(8,128)S(1)} collective-permute-done((f32[128,256]{1,0:T(8,128)S(1)}, f32[128,256]{1,0:T(8,128)S(1)}, u32[]{:S(2)}, u32[]{:S(2)}) %collective-permute-start.18) | collective-permute-done | bytes 131104 | tf_op jit(solution)/shard_map/ppermute | solution.py:205
  121.5 2.2 %collective-permute-start.19 = (f32[128,256]{1,0:T(8,128)S(1)}, f32[128,256]{1,0:T(8,128)S(1)}, u32[]{:S(2)}, u32[]{:S(2)}) collective-permute-start(f32[128,256]{1,0:T(8,128)S(1)} %add.165), channel_id=1, source_target_pairs={{0,16},{4,20},{8,24},{12,28},{16,0},{20,4},{24,8},{28,12},{1,17},{... | collective-permute-start | bytes 393224 | tf_op jit(solution)/shard_map/ppermute | solution.py:205
  123.7 5.2 %collective-permute-done.19 = f32[128,256]{1,0:T(8,128)S(1)} collective-permute-done((f32[128,256]{1,0:T(8,128)S(1)}, f32[128,256]{1,0:T(8,128)S(1)}, u32[]{:S(2)}, u32[]{:S(2)}) %collective-permute-start.19) | collective-permute-done | bytes 131104 | tf_op jit(solution)/shard_map/ppermute | solution.py:205
  128.9 1.6 %collective-permute-start.20 = (f32[128,256]{1,0:T(8,128)S(1)}, f32[128,256]{1,0:T(8,128)S(1)}, u32[]{:S(2)}, u32[]{:S(2)}) collective-permute-start(f32[128,256]{1,0:T(8,128)S(1)} %add.166), channel_id=1, source_target_pairs={{0,4},{4,0},{8,12},{12,8},{16,20},{20,16},{24,28},{28,24},{1,5},{5... | collective-permute-start | bytes 393224 | tf_op jit(solution)/shard_map/ppermute | solution.py:167
  130.4 3.5 %collective-permute-done.20 = f32[128,256]{1,0:T(8,128)S(1)} collective-permute-done((f32[128,256]{1,0:T(8,128)S(1)}, f32[128,256]{1,0:T(8,128)S(1)}, u32[]{:S(2)}, u32[]{:S(2)}) %collective-permute-start.20) | collective-permute-done | bytes 131104 | tf_op jit(solution)/shard_map/ppermute | solution.py:167
  134.4 6.0 %collective-permute-done.21 = f32[256,256]{1,0:T(8,128)S(1)} collective-permute-done((f32[256,256]{1,0:T(8,128)S(1)}, f32[256,256]{1,0:T(8,128)S(1)}, u32[]{:S(2)}, u32[]{:S(2)}) %collective-permute-start.21) | collective-permute-done | bytes 262176 | tf_op jit(solution)/shard_map/ppermute | solution.py:167
  140.6 0.8 convolution_convert_fusion.3
  141.5 1.0 convolution_convert_fusion.1
  (203 shorter events, 23.4 us)
Async XLA Ops:
  0.6 33.9 %copy-start = (bf16[1,1,4,64,512]{4,3,2,1,0:T(8,128)(2,1)S(1)}, bf16[1,1,4,64,512]{4,3,2,1,0:T(8,128)(2,1)}, u32[]{:S(2)}) copy-start(bf16[1,1,4,64,512]{4,3,2,1,0:T(8,128)(2,1)} %param.15) | copy-start | bytes 786436
  0.6 19.6 %copy-start.22 = (s32[8]{0:T(128)S(1)}, s32[8]{0:T(128)}, u32[]{:S(2)}) copy-start(s32[8]{0:T(128)} %constant.166) | copy-start | bytes 100
  0.7 19.4 %copy-start.21 = (s32[1,1,4,2]{2,3,1,0:T(2,128)S(1)}, s32[1,1,4,2]{2,3,1,0:T(2,128)}, u32[]{:S(2)}) copy-start(s32[1,1,4,2]{2,3,1,0:T(2,128)} %param.16) | copy-start | bytes 100
  0.7 13.1 %copy-start.10 = (bf16[16,16,256]{2,1,0:T(8,128)(2,1)S(1)}, bf16[16,16,256]{2,1,0:T(8,128)(2,1)}, u32[]{:S(2)}) copy-start(bf16[16,16,256]{2,1,0:T(8,128)(2,1)} %param.18) | copy-start | bytes 393220
  0.7 13.1 %copy-start.7 = (bf16[256,256]{1,0:T(8,128)(2,1)S(1)}, bf16[256,256]{1,0:T(8,128)(2,1)}, u32[]{:S(2)}) copy-start(bf16[256,256]{1,0:T(8,128)(2,1)} %param.14) | copy-start | bytes 393220
  2.5 20.9 %collective-permute-start.4 = (s32[1,2,8]{2,1,0:T(2,128)S(1)}, s32[1,2,8]{2,1,0:T(2,128)S(1)}, u32[]{:S(2)}, u32[]{:S(2)}) collective-permute-start(s32[1,2,8]{2,1,0:T(2,128)S(1)} %add_bitcast_fusion), channel_id=1, source_target_pairs={{0,16},{4,20},{8,24},{12,28},{16,0},{20,4},{24,8},{28,12},{1,17},{... | collective-permute-start | bytes 200 | tf_op jit(solution)/shard_map/ppermute | solution.py:167
  7.9 32.1 %collective-permute-start = (bf16[8,16,512]{2,1,0:T(8,128)(2,1)S(1)}, bf16[8,16,512]{2,1,0:T(8,128)(2,1)S(1)}, u32[]{:S(2)}, u32[]{:S(2)}) collective-permute-start(bf16[8,16,512]{2,1,0:T(8,128)(2,1)S(1)} %bitcast.274), channel_id=1, source_target_pairs={{0,4},{4,8},{8,12},{12,16},{16,20},{20,24},{24,28},{1,5},{5,9},{9,... | collective-permute-start | bytes 393224 | tf_op jit(solution)/shard_map/ppermute | solution.py:24
  11.3 28.7 %collective-permute-start.1 = (bf16[8,16,512]{2,1,0:T(8,128)(2,1)S(1)}, bf16[8,16,512]{2,1,0:T(8,128)(2,1)S(1)}, u32[]{:S(2)}, u32[]{:S(2)}) collective-permute-start(bf16[8,16,512]{2,1,0:T(8,128)(2,1)S(1)} %bitcast.273), channel_id=1, source_target_pairs={{4,0},{8,4},{12,8},{16,12},{20,16},{24,20},{28,24},{5,1},{9,5},{13... | collective-permute-start | bytes 393224 | tf_op jit(solution)/shard_map/ppermute | solution.py:27
  14.0 28.7 %collective-permute-start.7 = (bf16[8,16,512]{2,1,0:T(8,128)(2,1)S(1)}, bf16[8,16,512]{2,1,0:T(8,128)(2,1)S(1)}, u32[]{:S(2)}, u32[]{:S(2)}) collective-permute-start(bf16[8,16,512]{2,1,0:T(8,128)(2,1)S(1)} %get-tuple-element.42), channel_id=1, source_target_pairs={{0,4},{4,8},{8,12},{12,16},{16,20},{20,24},{24,28},{1,5},{5,9},{9,... | collective-permute-start | bytes 393224 | tf_op jit(solution)/shard_map/ppermute | solution.py:24
  18.6 24.1 %collective-permute-start.8 = (bf16[8,16,512]{2,1,0:T(8,128)(2,1)S(1)}, bf16[8,16,512]{2,1,0:T(8,128)(2,1)S(1)}, u32[]{:S(2)}, u32[]{:S(2)}) collective-permute-start(bf16[8,16,512]{2,1,0:T(8,128)(2,1)S(1)} %get-tuple-element.43), channel_id=1, source_target_pairs={{4,0},{8,4},{12,8},{16,12},{20,16},{24,20},{28,24},{5,1},{9,5},{13... | collective-permute-start | bytes 393224 | tf_op jit(solution)/shard_map/ppermute | solution.py:27
  23.4 44.5 %copy-start.8 = (bf16[2,2,64,2,128]{4,3,2,1,0:T(2,128)(2,1)}, bf16[2,2,64,2,128]{4,3,2,1,0:T(2,128)(2,1)S(1)}, u32[]{:S(2)}) copy-start(bf16[2,2,64,2,128]{4,3,2,1,0:T(2,128)(2,1)S(1)} %reshape_reshape.32) | copy-start | bytes 393220
  23.4 6.1 %collective-permute-start.5 = (s32[2,2,8]{2,1,0:T(2,128)S(1)}, s32[2,2,8]{2,1,0:T(2,128)S(1)}, u32[]{:S(2)}, u32[]{:S(2)}) collective-permute-start(s32[2,2,8]{2,1,0:T(2,128)S(1)} %pad_add_fusion.2), channel_id=1, source_target_pairs={{0,8},{4,12},{8,0},{12,4},{16,24},{20,28},{24,16},{28,20},{1,9},{5... | collective-permute-start | bytes 392 | tf_op jit(solution)/shard_map/ppermute | solution.py:167
  29.6 3.7 %collective-permute-start.6 = (s32[4,2,8]{2,1,0:T(2,128)S(1)}, s32[4,2,8]{2,1,0:T(2,128)S(1)}, u32[]{:S(2)}, u32[]{:S(2)}) collective-permute-start(s32[4,2,8]{2,1,0:T(2,128)S(1)} %pad_add_fusion.1), channel_id=1, source_target_pairs={{0,4},{4,0},{8,12},{12,8},{16,20},{20,16},{24,28},{28,24},{1,5},{5... | collective-permute-start | bytes 776 | tf_op jit(solution)/shard_map/ppermute | solution.py:167
  36.4 26.3 %all-to-all-start = ((bf16[8,2,64,512]{3,2,1,0:T(8,128)(2,1)}), bf16[8,2,64,512]{3,2,1,0:T(8,128)(2,1)S(1)}, u32[]{:S(2)}, u32[]{:S(2)}) async-start(bf16[8,2,64,512]{3,2,1,0:T(8,128)(2,1)} %broadcast_select_fusion), calls=%async_computation | async-start | bytes 2097152 | tf_op jit(solution)/shard_map/all_to_all | solution.py:229
  40.1 9.5 %collective-permute-start.2 = (bf16[32,8,512]{2,1,0:T(8,128)(2,1)S(1)}, bf16[32,8,512]{2,1,0:T(8,128)(2,1)S(1)}, u32[]{:S(2)}, u32[]{:S(2)}) collective-permute-start(bf16[32,8,512]{2,1,0:T(8,128)(2,1)S(1)} %get-tuple-element.38), channel_id=1, source_target_pairs={{0,1},{1,2},{2,3},{4,5},{5,6},{6,7},{8,9},{9,10},{10,11},{12,13},{... | collective-permute-start | bytes 786440 | tf_op jit(solution)/shard_map/ppermute | solution.py:24
  41.4 8.2 %collective-permute-start.3 = (bf16[32,8,512]{2,1,0:T(8,128)(2,1)S(1)}, bf16[32,8,512]{2,1,0:T(8,128)(2,1)S(1)}, u32[]{:S(2)}, u32[]{:S(2)}) collective-permute-start(bf16[32,8,512]{2,1,0:T(8,128)(2,1)S(1)} %get-tuple-element.39), channel_id=1, source_target_pairs={{1,0},{2,1},{3,2},{5,4},{6,5},{7,6},{9,8},{10,9},{11,10},{13,12},{... | collective-permute-start | bytes 786440 | tf_op jit(solution)/shard_map/ppermute | solution.py:27
  42.8 9.2 %collective-permute-start.10 = (bf16[32,8,512]{2,1,0:T(8,128)(2,1)S(1)}, bf16[32,8,512]{2,1,0:T(8,128)(2,1)S(1)}, u32[]{:S(2)}, u32[]{:S(2)}) collective-permute-start(bf16[32,8,512]{2,1,0:T(8,128)(2,1)S(1)} %get-tuple-element.37), channel_id=1, source_target_pairs={{1,0},{2,1},{3,2},{5,4},{6,5},{7,6},{9,8},{10,9},{11,10},{13,12},{... | collective-permute-start | bytes 786440 | tf_op jit(solution)/shard_map/ppermute | solution.py:27
  44.1 7.9 %collective-permute-start.9 = (bf16[32,8,512]{2,1,0:T(8,128)(2,1)S(1)}, bf16[32,8,512]{2,1,0:T(8,128)(2,1)S(1)}, u32[]{:S(2)}, u32[]{:S(2)}) collective-permute-start(bf16[32,8,512]{2,1,0:T(8,128)(2,1)S(1)} %get-tuple-element.36), channel_id=1, source_target_pairs={{0,1},{1,2},{2,3},{4,5},{5,6},{6,7},{8,9},{9,10},{10,11},{12,13},{... | collective-permute-start | bytes 786440 | tf_op jit(solution)/shard_map/ppermute | solution.py:24
  52.4 4.5 %copy-start.3 = (bf16[2,2,576,256]{3,2,1,0:T(8,128)(2,1)}, bf16[2,2,576,256]{3,2,1,0:T(8,128)(2,1)S(1)}, u32[]{:S(2)}) copy-start(bf16[2,2,576,256]{3,2,1,0:T(8,128)(2,1)S(1)} %get-tuple-element.13) | copy-start | bytes 3538948
  52.5 4.5 %copy-start.19 = (bf16[2,2,576,256]{3,2,1,0:T(8,128)(2,1)}, bf16[2,2,576,256]{3,2,1,0:T(8,128)(2,1)S(1)}, u32[]{:S(2)}) copy-start(bf16[2,2,576,256]{3,2,1,0:T(8,128)(2,1)S(1)} %get-tuple-element.12) | copy-start | bytes 3538948
  64.3 2.3 %copy-start.14 = (bf16[2,2,64,2,128]{4,3,2,1,0:T(2,128)(2,1)S(1)}, bf16[2,2,64,2,128]{4,3,2,1,0:T(2,128)(2,1)}, u32[]{:S(2)}) copy-start(bf16[2,2,64,2,128]{4,3,2,1,0:T(2,128)(2,1)} %reshape_reshape.29) | copy-start | bytes 393220
  66.6 1.3 copy-start.1
  69.0 7.7 %copy-start.2 = (bf16[16,16,256]{2,1,0:T(8,128)(2,1)S(1)}, bf16[16,16,256]{2,1,0:T(8,128)(2,1)}, u32[]{:S(2)}) copy-start(bf16[16,16,256]{2,1,0:T(8,128)(2,1)} %param.10) | copy-start | bytes 393220
  72.1 7.1 %copy-start.9 = (bf16[2,2,64,2,128]{4,2,3,1,0:T(8,128)(2,1)S(1)}, bf16[2,2,64,2,128]{4,2,3,1,0:T(8,128)(2,1)}, u32[]{:S(2)}) copy-start(bf16[2,2,64,2,128]{4,2,3,1,0:T(8,128)(2,1)} %get-tuple-element.86) | copy-start | bytes 393220
  73.2 13.2 %copy-start.11 = (bf16[16,16,256]{2,1,0:T(8,128)(2,1)S(1)}, bf16[16,16,256]{2,1,0:T(8,128)(2,1)}, u32[]{:S(2)}) copy-start(bf16[16,16,256]{2,1,0:T(8,128)(2,1)} %param.18) | copy-start | bytes 393220
  73.3 5.9 %copy-start.12 = (bf16[2,8,2,8,256]{4,3,2,1,0:T(8,128)(2,1)}, bf16[2,8,2,8,256]{4,3,2,1,0:T(8,128)(2,1)S(1)}, u32[]{:S(2)}) copy-start(bf16[2,8,2,8,256]{4,3,2,1,0:T(8,128)(2,1)S(1)} %copy.138) | copy-start | bytes 393220
  73.6 5.9 %collective-permute-start.11 = (f32[8,16,4]{1,0,2:T(8,128)S(1)}, f32[8,16,4]{1,0,2:T(8,128)S(1)}, u32[]{:S(2)}, u32[]{:S(2)}) collective-permute-start(f32[8,16,4]{1,0,2:T(8,128)S(1)} %slice.355), channel_id=1, source_target_pairs={{0,4},{4,8},{8,12},{12,16},{16,20},{20,24},{24,28},{1,5},{5,9},{9,... | collective-permute-start | bytes 6152 | tf_op jit(solution)/shard_map/ppermute | solution.py:24
  77.9 5.6 %collective-permute-start.12 = (f32[8,16,4]{1,0,2:T(8,128)S(1)}, f32[8,16,4]{1,0,2:T(8,128)S(1)}, u32[]{:S(2)}, u32[]{:S(2)}) collective-permute-start(f32[8,16,4]{1,0,2:T(8,128)S(1)} %slice.357), channel_id=1, source_target_pairs={{4,0},{8,4},{12,8},{16,12},{20,16},{24,20},{28,24},{5,1},{9,5},{13... | collective-permute-start | bytes 6152 | tf_op jit(solution)/shard_map/ppermute | solution.py:27
  79.5 11.0 %copy-start.20 = (pred[2,2,576]{2,1,0:T(4,128)(4,1)S(1)}, pred[2,2,576]{2,1,0:T(4,128)(4,1)}, u32[]{:S(2)}) copy-start(pred[2,2,576]{2,1,0:T(4,128)(4,1)} %concatenate.86) | copy-start | bytes 6916
  83.6 3.7 %collective-permute-start.13 = (f32[32,8,4]{1,0,2:T(8,128)S(1)}, f32[32,8,4]{1,0,2:T(8,128)S(1)}, u32[]{:S(2)}, u32[]{:S(2)}) collective-permute-start(f32[32,8,4]{1,0,2:T(8,128)S(1)} %get-tuple-element.46), channel_id=1, source_target_pairs={{0,1},{1,2},{2,3},{4,5},{5,6},{6,7},{8,9},{9,10},{10,11},{12,13},{... | collective-permute-start | bytes 12296 | tf_op jit(solution)/shard_map/ppermute | solution.py:24
  84.9 4.9 %collective-permute-start.14 = (f32[32,8,4]{1,0,2:T(8,128)S(1)}, f32[32,8,4]{1,0,2:T(8,128)S(1)}, u32[]{:S(2)}, u32[]{:S(2)}) collective-permute-start(f32[32,8,4]{1,0,2:T(8,128)S(1)} %get-tuple-element.47), channel_id=1, source_target_pairs={{1,0},{2,1},{3,2},{5,4},{6,5},{7,6},{9,8},{10,9},{11,10},{13,12},{... | collective-permute-start | bytes 12296 | tf_op jit(solution)/shard_map/ppermute | solution.py:27
  90.4 1.9 %copy-start.4 = (bf16[2,2,576,256]{3,2,1,0:T(8,128)(2,1)S(1)}, bf16[2,2,576,256]{3,2,1,0:T(8,128)(2,1)}, u32[]{:S(2)}) copy-start(bf16[2,2,576,256]{3,2,1,0:T(8,128)(2,1)} %copy-done.3) | copy-start | bytes 3538948
  92.4 0.9 copy-start.18
  96.0 1.9 %copy-start.5 = (f32[256,256]{1,0:T(8,128)S(1)}, f32[256,256]{1,0:T(8,128)}, u32[]{:S(2)}) copy-start(f32[256,256]{1,0:T(8,128)} %convolution_bitcast_fusion.2) | copy-start | bytes 786436
  96.0 2.0 %copy-start.6 = (f32[256,256]{1,0:T(8,128)S(1)}, f32[256,256]{1,0:T(8,128)}, u32[]{:S(2)}) copy-start(f32[256,256]{1,0:T(8,128)} %fusion.116) | copy-start | bytes 786436
  98.0 4.5 %collective-permute-start.15 = (f32[512,256]{1,0:T(8,128)S(1)}, f32[512,256]{1,0:T(8,128)S(1)}, u32[]{:S(2)}, u32[]{:S(2)}) collective-permute-start(f32[512,256]{1,0:T(8,128)S(1)} %constant_dynamic-slice_fusion.1), channel_id=1, source_target_pairs={{0,1},{1,0},{2,3},{3,2},{4,5},{5,4},{6,7},{7,6},{8,9},{9,8},{10,11... | collective-permute-start | bytes 1572872 | tf_op jit(solution)/shard_map/ppermute | solution.py:202
  102.7 8.7 %collective-permute-start.16 = (f32[256,256]{1,0:T(8,128)S(1)}, f32[256,256]{1,0:T(8,128)S(1)}, u32[]{:S(2)}, u32[]{:S(2)}) collective-permute-start(f32[256,256]{1,0:T(8,128)S(1)} %constant_dynamic-slice_fusion), channel_id=1, source_target_pairs={{0,2},{1,3},{2,0},{3,1},{4,6},{5,7},{6,4},{7,5},{8,10},{9,11},{10,... | collective-permute-start | bytes 786440 | tf_op jit(solution)/shard_map/ppermute | solution.py:202
  111.4 5.0 %collective-permute-start.17 = (f32[128,256]{1,0:T(8,128)S(1)}, f32[128,256]{1,0:T(8,128)S(1)}, u32[]{:S(2)}, u32[]{:S(2)}) collective-permute-start(f32[128,256]{1,0:T(8,128)S(1)} %constant_dynamic-slice_fusion.2), channel_id=1, source_target_pairs={{0,4},{4,0},{8,12},{12,8},{16,20},{20,16},{24,28},{28,24},{1,5},{5... | collective-permute-start | bytes 393224 | tf_op jit(solution)/shard_map/ppermute | solution.py:202
  116.5 5.0 %collective-permute-start.18 = (f32[128,256]{1,0:T(8,128)S(1)}, f32[128,256]{1,0:T(8,128)S(1)}, u32[]{:S(2)}, u32[]{:S(2)}) collective-permute-start(f32[128,256]{1,0:T(8,128)S(1)} %dynamic-slice_add_fusion.2), channel_id=1, source_target_pairs={{0,8},{4,12},{8,0},{12,4},{16,24},{20,28},{24,16},{28,20},{1,9},{5... | collective-permute-start | bytes 393224 | tf_op jit(solution)/shard_map/ppermute | solution.py:205
  121.5 7.3 %collective-permute-start.19 = (f32[128,256]{1,0:T(8,128)S(1)}, f32[128,256]{1,0:T(8,128)S(1)}, u32[]{:S(2)}, u32[]{:S(2)}) collective-permute-start(f32[128,256]{1,0:T(8,128)S(1)} %add.165), channel_id=1, source_target_pairs={{0,16},{4,20},{8,24},{12,28},{16,0},{20,4},{24,8},{28,12},{1,17},{... | collective-permute-start | bytes 393224 | tf_op jit(solution)/shard_map/ppermute | solution.py:205
  128.9 5.0 %collective-permute-start.20 = (f32[128,256]{1,0:T(8,128)S(1)}, f32[128,256]{1,0:T(8,128)S(1)}, u32[]{:S(2)}, u32[]{:S(2)}) collective-permute-start(f32[128,256]{1,0:T(8,128)S(1)} %add.166), channel_id=1, source_target_pairs={{0,4},{4,0},{8,12},{12,8},{16,20},{20,16},{24,28},{28,24},{1,5},{5... | collective-permute-start | bytes 393224 | tf_op jit(solution)/shard_map/ppermute | solution.py:167
  133.9 7.5 %copy-start.13 = (bf16[2,8,2,8,256]{4,3,2,1,0:T(8,128)(2,1)S(1)}, bf16[2,8,2,8,256]{4,3,2,1,0:T(8,128)(2,1)}, u32[]{:S(2)}) copy-start(bf16[2,8,2,8,256]{4,3,2,1,0:T(8,128)(2,1)} %copy-done.12) | copy-start | bytes 393220
  133.9 7.5 %copy-start.15 = (bf16[256,256]{1,0:T(8,128)(2,1)S(1)}, bf16[256,256]{1,0:T(8,128)(2,1)}, u32[]{:S(2)}) copy-start(bf16[256,256]{1,0:T(8,128)(2,1)} %param.13) | copy-start | bytes 393220
  133.9 7.5 %copy-start.16 = (bf16[256,256]{1,0:T(8,128)(2,1)S(1)}, bf16[256,256]{1,0:T(8,128)(2,1)}, u32[]{:S(2)}) copy-start(bf16[256,256]{1,0:T(8,128)(2,1)} %param.12) | copy-start | bytes 393220
  134.0 7.5 %copy-start.17 = (bf16[256,256]{1,0:T(8,128)(2,1)S(1)}, bf16[256,256]{1,0:T(8,128)(2,1)}, u32[]{:S(2)}) copy-start(bf16[256,256]{1,0:T(8,128)(2,1)} %param.11) | copy-start | bytes 393220
  134.0 6.4 %collective-permute-start.21 = (f32[256,256]{1,0:T(8,128)S(1)}, f32[256,256]{1,0:T(8,128)S(1)}, u32[]{:S(2)}, u32[]{:S(2)}) collective-permute-start(f32[256,256]{1,0:T(8,128)S(1)} %pad_maximum_fusion.6), channel_id=1, source_target_pairs={{0,2},{1,3},{2,0},{3,1},{4,6},{5,7},{6,4},{7,5},{8,10},{9,11},{10,... | collective-permute-start | bytes 786440 | tf_op jit(solution)/shard_map/ppermute | solution.py:167
  140.5 2.0 %collective-permute-start.22 = (f32[512,256]{1,0:T(8,128)S(1)}, f32[512,256]{1,0:T(8,128)S(1)}, u32[]{:S(2)}, u32[]{:S(2)}) collective-permute-start(f32[512,256]{1,0:T(8,128)S(1)} %pad_maximum_fusion.5), channel_id=1, source_target_pairs={{0,1},{1,0},{2,3},{3,2},{4,5},{5,4},{6,7},{7,6},{8,9},{9,8},{10,11... | collective-permute-start | bytes 1572872 | tf_op jit(solution)/shard_map/ppermute | solution.py:167

commit v12 on v11

--- a/solution.py
+++ b/solution.py
@@ -27,6 +27,30 @@
         high = lax.ppermute(lax.slice_in_dim(block, 0, width, axis=dim), axis, backward)
         block = jnp.concatenate([low, block, high], axis=dim)
     return block
+
+
+def halo(block, width):
+    axes = ("gx", "gy")
+    rows_n, cols_n = lax.axis_size("gx"), lax.axis_size("gy")
+    rows, cols = block.shape[0], block.shape[1]
+    row_parts = {-1: slice(rows - width, rows), 0: slice(0, rows), 1: slice(0, width)}
+    col_parts = {-1: slice(cols - width, cols), 0: slice(0, cols), 1: slice(0, width)}
+    grid = []
+    for row_off in (-1, 0, 1):
+        line = []
+        for col_off in (-1, 0, 1):
+            piece = block[row_parts[row_off], col_parts[col_off]]
+            if row_off or col_off:
+                pairs = [
+                    ((i + row_off) * cols_n + j + col_off, i * cols_n + j)
+                    for i in range(rows_n)
+                    for j in range(cols_n)
+                    if 0 <= i + row_off < rows_n and 0 <= j + col_off < cols_n
+                ]
+                piece = lax.ppermute(piece, axes, pairs)
+            line.append(piece)
+        grid.append(jnp.concatenate(line, axis=1))
+    return jnp.concatenate(grid, axis=0)
 
 
 def to_blocks(grid_array):
@@ -259,25 +283,9 @@
         region_memory.shape[2], region_memory.shape[3], region_memory.shape[4]
     )
     fetched = fetch_regions(memory_local, owners, local_ids, "gx")
-    region_keyval = fetched.reshape(
-        block_rows, block_cols, 2, memory_local.shape[1], memory_local.shape[2]
-    )
-    query_blocks = to_blocks(queries.reshape(tile_rows, tile_cols, model_width))
-    outputs, log_totals = attend_forward(query_blocks, keyval_pad, key_valid, region_keyval)
-    attended = from_blocks(outputs).reshape(-1, model_width)
-    layer_out = jnp.dot(attended, w_out, preferred_element_type=jnp.float32).astype(jnp.bfloat16)
     grad_flat = grad_out.reshape(-1, model_width)
     d_attended = jnp.dot(grad_flat, w_out.T, preferred_element_type=jnp.float32).astype(
         jnp.bfloat16
-    )
-    grad_out_local = inner_rows(attended, grad_flat)
-    dout_blocks = to_blocks(d_attended.reshape(tile_rows, tile_cols, model_width))
-    delta_rows = jnp.sum(
-        split_heads(dout_blocks).astype(jnp.float32) * split_heads(outputs).astype(jnp.float32), -1
-    )
-    delta_rows = delta_rows.transpose(0, 1, 3, 2)
-    d_queries = query_grads(
-        query_blocks, keyval_pad, key_valid, region_keyval, log_totals, dout_blocks, delta_rows
     )
     query_grid = jnp.concatenate(
         [
@@ -287,8 +295,25 @@
         -1,
     )
     query_halo = padded(query_grid, (("gx", 0), ("gy", 1)), BSIDE)
+    fetched, query_halo = lax.optimization_barrier((fetched, query_halo))
+    region_keyval = fetched.reshape(
+        block_rows, block_cols, 2, memory_local.shape[1], memory_local.shape[2]
+    )
+    query_blocks = to_blocks(queries.reshape(tile_rows, tile_cols, model_width))
+    outputs, log_totals = attend_forward(query_blocks, keyval_pad, key_valid, region_keyval)
+    attended = from_blocks(outputs).reshape(-1, model_width)
+    layer_out = jnp.dot(attended, w_out, preferred_element_type=jnp.float32).astype(jnp.bfloat16)
+    grad_out_local = inner_rows(attended, grad_flat)
+    dout_blocks = to_blocks(d_attended.reshape(tile_rows, tile_cols, model_width))
+    delta_rows = jnp.sum(
+        split_heads(dout_blocks).astype(jnp.float32) * split_heads(outputs).astype(jnp.float32), -1
+    )
+    delta_rows = delta_rows.transpose(0, 1, 3, 2)
+    d_queries = query_grads(
+        query_blocks, keyval_pad, key_valid, region_keyval, log_totals, dout_blocks, delta_rows
+    )
     stat_grid = from_blocks(jnp.concatenate([log_totals, delta_rows], 2).transpose(0, 1, 3, 2))
-    stat_halo = padded(stat_grid, (("gx", 0), ("gy", 1)), BSIDE)
+    stat_halo = halo(stat_grid, BSIDE)
     query_all = to_blocks(query_halo)
     stat_pad = to_blocks(stat_halo).transpose(0, 1, 3, 2)
     d_keys, d_values = key_grads(

time: 145 us -> 166 us (1.14)
  starting transfers between devices: 50.2 us -> 67.6 us
  local copies, waits for them, and re-layouts: 23.4 us -> 33.1 us
  waiting for transfers between devices: 48 us -> 41.9 us
    ppermute x0 -> x8, starting transfers between devices: none -> 20.8 us  [halo(): piece = lax.ppermute(piece, axes, pairs)]
    ppermute x6 -> x4, waiting for transfers between devices: 6.5 us -> 0.01 us  [padded(): lax.ppermute(lax.slice_in_dim(block, 0, width, axis=dim), axis, backward)]
    unnamed x70 -> x50, local copies, waits for them, and re-layouts: 12 us -> 16.7 us
    ppermute x6 -> x4, starting transfers between devices: 19.1 us -> 14.7 us  [padded(): lax.ppermute(lax.slice_in_dim(block, block.shape[dim] - width, None, axis...]
    ppermute x0 -> x8, waiting for transfers between devices: none -> 3.46 us  [halo(): piece = lax.ppermute(piece, axes, pairs)]
    ppermute x3, starting transfers between devices: 4.86 us -> 7.98 us  [tree_sum(): joined = keep + lax.ppermute(send, axis, pairs)]
    ppermute x6 -> x4, starting transfers between devices: 7.92 us -> 5.17 us  [padded(): lax.ppermute(lax.slice_in_dim(block, 0, width, axis=dim), axis, backward)]
    concatenate x4, local copies, waits for them, and re-layouts: 0.96 us -> 3.53 us  [neighbour_set(): return (jnp.concatenate(parts, axis), jnp.concatenate(valid, 2))]
  transfers between devices with their start and end apart: 24 -> 28, of which waited for: 13 -> 12; matrix products, arithmetic and copies ran while one was open for 15% -> 16% of each run, Pallas kernels for 0% -> 0%
where the time goes in v12:
time: 166 us; the launch traced here: 165 us
  starting transfers between devices  67.6 us (41%)
  waiting for transfers between devices  41.9 us (25%)
  local copies, waits for them, and re-layouts  33.1 us (20%)
  matrix products  16.3 us (10%)
  other arithmetic  5.12 us (3%)
    ppermute x8, starting transfers between devices, halo(): piece = lax.ppermute(piece, axes, pairs)  20.8 us
    unnamed x50, local copies, waits for them, and re-layouts  16.7 us
    ppermute x4, starting transfers between devices, padded(): lax.ppermute(lax.slice_in_dim(block, block.shape[dim] - width, None, axis...  14.7 us
    ppermute x6, waiting for transfers between devices, doubling_gather(): got = lax.ppermute(joined, axis, pairs)  12.8 us
    ppermute x6, starting transfers between devices, doubling_gather(): got = lax.ppermute(joined, axis, pairs)  12.7 us
    ppermute x3, waiting for transfers between devices, tree_sum(): joined = keep + lax.ppermute(send, axis, pairs)  11.4 us
    ppermute x2, waiting for transfers between devices, tree_sum(): joined = joined + lax.ppermute(joined, axis, pairs)  9.64 us
    ppermute x3, starting transfers between devices, tree_sum(): joined = keep + lax.ppermute(send, axis, pairs)  7.98 us
  transfers between devices with their start and end apart: 28, of which 12 were waited for; matrix products, arithmetic and copies ran while one was open for 16% of the time, Pallas kernels for 0%

profile of v12, /device:TPU:0, one launch (start us, length us, event | category | flops | bytes accessed | tf_op | source)
XLA Modules:
  0.0 165.5 jit_solution(13583159854174682602)
XLA Ops:
  2.4 4.1 %collective-permute-start.4 = (s32[1,2,8]{2,1,0:T(2,128)S(1)}, s32[1,2,8]{2,1,0:T(2,128)S(1)}, u32[]{:S(2)}, u32[]{:S(2)}) collective-permute-start(s32[1,2,8]{2,1,0:T(2,128)S(1)} %add_bitcast_fusion), channel_id=1, source_target_pairs={{0,16},{4,20},{8,24},{12,28},{16,0},{20,4},{24,8},{28,12},{1,17},{... | collective-permute-start | bytes 200 | tf_op jit(solution)/shard_map/ppermute | solution.py:191
  6.5 1.2 convolution_convert_fusion.4
  7.7 1.2 convolution_convert_fusion.3
  8.9 3.4 %collective-permute-start.7 = (bf16[8,16,512]{2,1,0:T(8,128)(2,1)S(1)}, bf16[8,16,512]{2,1,0:T(8,128)(2,1)S(1)}, u32[]{:S(2)}, u32[]{:S(2)}) collective-permute-start(bf16[8,16,512]{2,1,0:T(8,128)(2,1)S(1)} %get-tuple-element.46), channel_id=1, source_target_pairs={{0,4},{4,8},{8,12},{12,16},{16,20},{20,24},{24,28},{1,5},{5,9},{9,... | collective-permute-start | bytes 393224 | tf_op jit(solution)/shard_map/ppermute | solution.py:24
  12.3 1.3 collective-permute-start.8
  13.6 1.3 convolution_convert_fusion
  14.9 4.6 %collective-permute-start = (bf16[8,16,512]{2,1,0:T(8,128)(2,1)S(1)}, bf16[8,16,512]{2,1,0:T(8,128)(2,1)S(1)}, u32[]{:S(2)}, u32[]{:S(2)}) collective-permute-start(bf16[8,16,512]{2,1,0:T(8,128)(2,1)S(1)} %bitcast.272), channel_id=1, source_target_pairs={{0,4},{4,8},{8,12},{12,16},{16,20},{20,24},{24,28},{1,5},{5,9},{9,... | collective-permute-start | bytes 393224 | tf_op jit(solution)/shard_map/ppermute | solution.py:24
  19.5 1.3 collective-permute-start.1
  23.2 4.6 %collective-permute-start.5 = (s32[2,2,8]{2,1,0:T(2,128)S(1)}, s32[2,2,8]{2,1,0:T(2,128)S(1)}, u32[]{:S(2)}, u32[]{:S(2)}) collective-permute-start(s32[2,2,8]{2,1,0:T(2,128)S(1)} %pad_add_fusion.2), channel_id=1, source_target_pairs={{0,8},{4,12},{8,0},{12,4},{16,24},{20,28},{24,16},{28,20},{1,9},{5... | collective-permute-start | bytes 392 | tf_op jit(solution)/shard_map/ppermute | solution.py:191
  27.8 1.6 collective-permute-done.5
  30.0 3.0 %collective-permute-done.6 = s32[4,2,8]{2,1,0:T(2,128)S(1)} collective-permute-done((s32[4,2,8]{2,1,0:T(2,128)S(1)}, s32[4,2,8]{2,1,0:T(2,128)S(1)}, u32[]{:S(2)}, u32[]{:S(2)}) %collective-permute-start.6) | collective-permute-done | bytes 288 | tf_op jit(solution)/shard_map/ppermute | solution.py:191
  34.9 1.2 broadcast_select_fusion
  36.1 3.6 %all-to-all-start = ((bf16[8,2,64,512]{3,2,1,0:T(8,128)(2,1)}), bf16[8,2,64,512]{3,2,1,0:T(8,128)(2,1)S(1)}, u32[]{:S(2)}, u32[]{:S(2)}) async-start(bf16[8,2,64,512]{3,2,1,0:T(8,128)(2,1)} %broadcast_select_fusion), calls=%async_computation | async-start | bytes 2097152 | tf_op jit(solution)/shard_map/all_to_all | solution.py:253
  39.8 1.3 collective-permute-start.2
  41.1 1.3 collective-permute-start.3
  42.5 1.3 collective-permute-start.10
  43.8 5.4 %collective-permute-start.9 = (bf16[32,8,512]{2,1,0:T(8,128)(2,1)S(1)}, bf16[32,8,512]{2,1,0:T(8,128)(2,1)S(1)}, u32[]{:S(2)}, u32[]{:S(2)}) collective-permute-start(bf16[32,8,512]{2,1,0:T(8,128)(2,1)S(1)} %get-tuple-element.40), channel_id=1, source_target_pairs={{0,1},{1,2},{2,3},{4,5},{5,6},{6,7},{8,9},{9,10},{10,11},{12,13},{... | collective-permute-start | bytes 786440 | tf_op jit(solution)/shard_map/ppermute | solution.py:24
  51.7 1.1 pad_maximum_fusion.1
  58.0 4.5 %all-to-all-done = bf16[8,2,64,512]{3,2,1,0:T(8,128)(2,1)S(1)} async-done(((bf16[8,2,64,512]{3,2,1,0:T(8,128)(2,1)}), bf16[8,2,64,512]{3,2,1,0:T(8,128)(2,1)S(1)}, u32[]{:S(2)}, u32[]{:S(2)}) %all-to-all-start) | async-done | bytes 1048608 | tf_op jit(solution)/shard_map/all_to_all | solution.py:253
  64.0 2.3 %slice_bitcast_fusion.1 = (bf16[2,2,88,2,8,128]{5,4,3,2,1,0:T(8,128)(2,1)S(1)}, bf16[2,2,88,2,8,128]{5,4,3,2,1,0:T(8,128)(2,1)S(1)}) fusion(bf16[2,2,704,512]{3,2,1,0:T(8,128)(2,1)} %constant_dynamic-update-slice_fusion), kind=kLoop, calls=%fused_computation.14 | loop fusion | bytes 5767168
  68.1 3.0 %fusion.62 = bf16[2,2,64,2,128]{4,2,3,1,0:T(8,128)(2,1)} fusion(bf16[2,2,88,2,8,128]{5,4,3,2,1,0:T(8,128)(2,1)S(1)} %get-tuple-element.10, f32[2,2,2,64,704]{4,3,2,1,0:T(8,128)S(1)} %get-tuple-element.92, bf16[2,2,88,2,8,128]{5,4,3,2,1,0:T(8,128)(2,1)} %copy-done.1, f32[2,2,2,64]{3,2,1,0:T(2,128)S(1)} %bitcast.273, f32[2,2,2,64]{3,2,1,0:T(2,128)S(1)} %log_add_fusion, ...), kind=kOutput, calls=%fused_computation.50 | convolution fusion | flops 186122240 | bytes 4591616 | tf_op jit(solution)/shard_map/abhqk,abkhe->abqhe/dot_general | solution.py:132
  72.8 1.0 copy.127
  74.2 1.3 collective-permute-start.14
  75.5 1.3 collective-permute-start.15
  76.8 5.6 %collective-permute-start.11 = (f32[8,8,4]{1,0,2:T(8,128)}, f32[8,8,4]{1,0,2:T(8,128)S(1)}, u32[]{:S(2)}, u32[]{:S(2)}) collective-permute-start(f32[8,8,4]{1,0,2:T(8,128)} %get-tuple-element.70), channel_id=1, source_target_pairs={{0,5},{1,6},{2,7},{4,9},{5,10},{6,11},{8,13},{9,14},{10,15},{12,17... | collective-permute-start | bytes 3080 | tf_op jit(solution)/shard_map/ppermute | solution.py:50
  82.4 1.3 collective-permute-start.13
  83.7 1.3 collective-permute-start.16
  91.2 1.3 collective-permute-start.18
  92.5 7.3 %collective-permute-start.12 = (f32[8,16,4]{1,0,2:T(8,128)S(1)}, f32[8,16,4]{1,0,2:T(8,128)S(1)}, u32[]{:S(2)}, u32[]{:S(2)}) collective-permute-start(f32[8,16,4]{1,0,2:T(8,128)S(1)} %slice.368), channel_id=1, source_target_pairs={{0,4},{1,5},{2,6},{3,7},{4,8},{5,9},{6,10},{7,11},{8,12},{9,13},{1... | collective-permute-start | bytes 6152 | tf_op jit(solution)/shard_map/ppermute | solution.py:50
  99.9 1.5 collective-permute-start.17
  102.1 3.4 %collective-permute-done.17 = f32[8,16,4]{1,0,2:T(8,128)S(1)} collective-permute-done((f32[8,16,4]{1,0,2:T(8,128)S(1)}, f32[8,16,4]{1,0,2:T(8,128)S(1)}, u32[]{:S(2)}, u32[]{:S(2)}) %collective-permute-start.17) | collective-permute-done | bytes 2080 | tf_op jit(solution)/shard_map/ppermute | solution.py:50
  108.1 1.9 %fusion.9 = f32[2,2,2,576,64]{3,4,2,1,0:T(8,128)S(1)} fusion(f32[2,2,2,576]{3,2,1,0:T(2,128)} %concatenate.98, pred[2,2,576]{2,1,0:T(4,128)(4,1)} %concatenate.92, bf16[2,2,8,2,8,128]{5,4,3,2,1,0:T(8,128)(2,1)} %get-tuple-element.15, bf16[2,2,576,256]{3,2,1,0:T(8,128)(2,1)} %get-tuple-element.16), kind=kOutput, calls=%fused_computation.20 | convolution fusion | flops 76382208 | bytes 2511104 | tf_op jit(solution)/shard_map/abqhe,abkhe->abhqk/dot_general | solution.py:150
  111.0 1.4 concatenate.100
  112.4 2.8 %fusion.57 = bf16[2,2,64,2,128]{4,2,3,1,0:T(8,128)(2,1)} fusion(f32[2,2,2,576,64]{3,4,2,1,0:T(8,128)S(1)} %fusion.9, f32[2,2,2,576]{3,2,1,0:T(2,128)} %concatenate.100, bf16[2,2,8,2,8,128]{5,4,3,2,1,0:T(8,128)(2,1)} %get-tuple-element.14, bf16[2,2,576,256]{3,2,1,0:T(8,128)(2,1)S(1)} %get-tuple-element.17, bf16[2,2,576,256]{3,2,1,0:T(8,128)(2,1)} %get-tuple-element.16), kind=kOutput, calls=%fused_computation.49 | convolution fusion | flops 152010752 | bytes 3819520 | tf_op jit(solution)/shard_map/abhqk,abqhe->abkhe/dot_general | solution.py:159
  116.6 1.0 copy.142
  118.1 1.2 collective-permute-start.19
  119.3 1.5 collective-permute-done.19
  120.9 3.8 %collective-permute-start.20 = (f32[256,256]{1,0:T(8,128)S(1)}, f32[256,256]{1,0:T(8,128)S(1)}, u32[]{:S(2)}, u32[]{:S(2)}) collective-permute-start(f32[256,256]{1,0:T(8,128)S(1)} %constant_dynamic-slice_fusion.1), channel_id=1, source_target_pairs={{0,2},{1,3},{2,0},{3,1},{4,6},{5,7},{6,4},{7,5},{8,10},{9,11},{10,... | collective-permute-start | bytes 786440 | tf_op jit(solution)/shard_map/ppermute | solution.py:226
  124.7 6.6 %collective-permute-done.20 = f32[256,256]{1,0:T(8,128)S(1)} collective-permute-done((f32[256,256]{1,0:T(8,128)S(1)}, f32[256,256]{1,0:T(8,128)S(1)}, u32[]{:S(2)}, u32[]{:S(2)}) %collective-permute-start.20) | collective-permute-done | bytes 262176 | tf_op jit(solution)/shard_map/ppermute | solution.py:226
  131.4 3.0 %collective-permute-start.21 = (f32[128,256]{1,0:T(8,128)S(1)}, f32[128,256]{1,0:T(8,128)S(1)}, u32[]{:S(2)}, u32[]{:S(2)}) collective-permute-start(f32[128,256]{1,0:T(8,128)S(1)} %constant_dynamic-slice_fusion), channel_id=1, source_target_pairs={{0,4},{4,0},{8,12},{12,8},{16,20},{20,16},{24,28},{28,24},{1,5},{5... | collective-permute-start | bytes 393224 | tf_op jit(solution)/shard_map/ppermute | solution.py:226
  134.4 3.3 %collective-permute-done.21 = f32[128,256]{1,0:T(8,128)S(1)} collective-permute-done((f32[128,256]{1,0:T(8,128)S(1)}, f32[128,256]{1,0:T(8,128)S(1)}, u32[]{:S(2)}, u32[]{:S(2)}) %collective-permute-start.21) | collective-permute-done | bytes 131104 | tf_op jit(solution)/shard_map/ppermute | solution.py:226
  138.6 4.1 %collective-permute-done.22 = f32[128,256]{1,0:T(8,128)S(1)} collective-permute-done((f32[128,256]{1,0:T(8,128)S(1)}, f32[128,256]{1,0:T(8,128)S(1)}, u32[]{:S(2)}, u32[]{:S(2)}) %collective-permute-start.22) | collective-permute-done | bytes 131104 | tf_op jit(solution)/shard_map/ppermute | solution.py:229
  142.8 1.8 %collective-permute-start.23 = (f32[128,256]{1,0:T(8,128)S(1)}, f32[128,256]{1,0:T(8,128)S(1)}, u32[]{:S(2)}, u32[]{:S(2)}) collective-permute-start(f32[128,256]{1,0:T(8,128)S(1)} %add.163), channel_id=1, source_target_pairs={{0,16},{4,20},{8,24},{12,28},{16,0},{20,4},{24,8},{28,12},{1,17},{... | collective-permute-start | bytes 393224 | tf_op jit(solution)/shard_map/ppermute | solution.py:229
  144.6 5.5 %collective-permute-done.23 = f32[128,256]{1,0:T(8,128)S(1)} collective-permute-done((f32[128,256]{1,0:T(8,128)S(1)}, f32[128,256]{1,0:T(8,128)S(1)}, u32[]{:S(2)}, u32[]{:S(2)}) %collective-permute-start.23) | collective-permute-done | bytes 131104 | tf_op jit(solution)/shard_map/ppermute | solution.py:229
  150.1 1.8 %collective-permute-start.24 = (f32[128,256]{1,0:T(8,128)S(1)}, f32[128,256]{1,0:T(8,128)S(1)}, u32[]{:S(2)}, u32[]{:S(2)}) collective-permute-start(f32[128,256]{1,0:T(8,128)S(1)} %add.164), channel_id=1, source_target_pairs={{0,4},{4,0},{8,12},{12,8},{16,20},{20,16},{24,28},{28,24},{1,5},{5... | collective-permute-start | bytes 393224 | tf_op jit(solution)/shard_map/ppermute | solution.py:191
  151.9 3.2 %collective-permute-done.24 = f32[128,256]{1,0:T(8,128)S(1)} collective-permute-done((f32[128,256]{1,0:T(8,128)S(1)}, f32[128,256]{1,0:T(8,128)S(1)}, u32[]{:S(2)}, u32[]{:S(2)}) %collective-permute-start.24) | collective-permute-done | bytes 131104 | tf_op jit(solution)/shard_map/ppermute | solution.py:191
  155.3 1.5 collective-permute-start.25
  156.7 4.9 %collective-permute-done.25 = f32[256,256]{1,0:T(8,128)S(1)} collective-permute-done((f32[256,256]{1,0:T(8,128)S(1)}, f32[256,256]{1,0:T(8,128)S(1)}, u32[]{:S(2)}, u32[]{:S(2)}) %collective-permute-start.25) | collective-permute-done | bytes 262176 | tf_op jit(solution)/shard_map/ppermute | solution.py:191
  (186 shorter events, 36.9 us)
Async XLA Ops:
  0.6 33.7 %copy-start = (bf16[1,1,4,64,512]{4,3,2,1,0:T(8,128)(2,1)S(1)}, bf16[1,1,4,64,512]{4,3,2,1,0:T(8,128)(2,1)}, u32[]{:S(2)}) copy-start(bf16[1,1,4,64,512]{4,3,2,1,0:T(8,128)(2,1)} %param.15) | copy-start | bytes 786436
  0.6 20.3 %copy-start.13 = (s32[8]{0:T(128)S(1)}, s32[8]{0:T(128)}, u32[]{:S(2)}) copy-start(s32[8]{0:T(128)} %constant.166) | copy-start | bytes 100
  0.7 20.3 %copy-start.12 = (s32[1,1,4,2]{2,3,1,0:T(2,128)S(1)}, s32[1,1,4,2]{2,3,1,0:T(2,128)}, u32[]{:S(2)}) copy-start(s32[1,1,4,2]{2,3,1,0:T(2,128)} %param.16) | copy-start | bytes 100
  2.4 20.7 %collective-permute-start.4 = (s32[1,2,8]{2,1,0:T(2,128)S(1)}, s32[1,2,8]{2,1,0:T(2,128)S(1)}, u32[]{:S(2)}, u32[]{:S(2)}) collective-permute-start(s32[1,2,8]{2,1,0:T(2,128)S(1)} %add_bitcast_fusion), channel_id=1, source_target_pairs={{0,16},{4,20},{8,24},{12,28},{16,0},{20,4},{24,8},{28,12},{1,17},{... | collective-permute-start | bytes 200 | tf_op jit(solution)/shard_map/ppermute | solution.py:191
  8.9 33.5 %collective-permute-start.7 = (bf16[8,16,512]{2,1,0:T(8,128)(2,1)S(1)}, bf16[8,16,512]{2,1,0:T(8,128)(2,1)S(1)}, u32[]{:S(2)}, u32[]{:S(2)}) collective-permute-start(bf16[8,16,512]{2,1,0:T(8,128)(2,1)S(1)} %get-tuple-element.46), channel_id=1, source_target_pairs={{0,4},{4,8},{8,12},{12,16},{16,20},{20,24},{24,28},{1,5},{5,9},{9,... | collective-permute-start | bytes 393224 | tf_op jit(solution)/shard_map/ppermute | solution.py:24
  12.3 30.1 %collective-permute-start.8 = (bf16[8,16,512]{2,1,0:T(8,128)(2,1)S(1)}, bf16[8,16,512]{2,1,0:T(8,128)(2,1)S(1)}, u32[]{:S(2)}, u32[]{:S(2)}) collective-permute-start(bf16[8,16,512]{2,1,0:T(8,128)(2,1)S(1)} %get-tuple-element.47), channel_id=1, source_target_pairs={{4,0},{8,4},{12,8},{16,12},{20,16},{24,20},{28,24},{5,1},{9,5},{13... | collective-permute-start | bytes 393224 | tf_op jit(solution)/shard_map/ppermute | solution.py:27
  14.9 24.7 %collective-permute-start = (bf16[8,16,512]{2,1,0:T(8,128)(2,1)S(1)}, bf16[8,16,512]{2,1,0:T(8,128)(2,1)S(1)}, u32[]{:S(2)}, u32[]{:S(2)}) collective-permute-start(bf16[8,16,512]{2,1,0:T(8,128)(2,1)S(1)} %bitcast.272), channel_id=1, source_target_pairs={{0,4},{4,8},{8,12},{12,16},{16,20},{20,24},{24,28},{1,5},{5,9},{9,... | collective-permute-start | bytes 393224 | tf_op jit(solution)/shard_map/ppermute | solution.py:24
  19.5 20.2 %collective-permute-start.1 = (bf16[8,16,512]{2,1,0:T(8,128)(2,1)S(1)}, bf16[8,16,512]{2,1,0:T(8,128)(2,1)S(1)}, u32[]{:S(2)}, u32[]{:S(2)}) collective-permute-start(bf16[8,16,512]{2,1,0:T(8,128)(2,1)S(1)} %bitcast.271), channel_id=1, source_target_pairs={{4,0},{8,4},{12,8},{16,12},{20,16},{24,20},{28,24},{5,1},{9,5},{13... | collective-permute-start | bytes 393224 | tf_op jit(solution)/shard_map/ppermute | solution.py:27
  23.2 6.1 %collective-permute-start.5 = (s32[2,2,8]{2,1,0:T(2,128)S(1)}, s32[2,2,8]{2,1,0:T(2,128)S(1)}, u32[]{:S(2)}, u32[]{:S(2)}) collective-permute-start(s32[2,2,8]{2,1,0:T(2,128)S(1)} %pad_add_fusion.2), channel_id=1, source_target_pairs={{0,8},{4,12},{8,0},{12,4},{16,24},{20,28},{24,16},{28,20},{1,9},{5... | collective-permute-start | bytes 392 | tf_op jit(solution)/shard_map/ppermute | solution.py:191
  29.3 3.7 %collective-permute-start.6 = (s32[4,2,8]{2,1,0:T(2,128)S(1)}, s32[4,2,8]{2,1,0:T(2,128)S(1)}, u32[]{:S(2)}, u32[]{:S(2)}) collective-permute-start(s32[4,2,8]{2,1,0:T(2,128)S(1)} %pad_add_fusion.1), channel_id=1, source_target_pairs={{0,4},{4,0},{8,12},{12,8},{16,20},{20,16},{24,28},{28,24},{1,5},{5... | collective-permute-start | bytes 776 | tf_op jit(solution)/shard_map/ppermute | solution.py:191
  36.1 26.3 %all-to-all-start = ((bf16[8,2,64,512]{3,2,1,0:T(8,128)(2,1)}), bf16[8,2,64,512]{3,2,1,0:T(8,128)(2,1)S(1)}, u32[]{:S(2)}, u32[]{:S(2)}) async-start(bf16[8,2,64,512]{3,2,1,0:T(8,128)(2,1)} %broadcast_select_fusion), calls=%async_computation | async-start | bytes 2097152 | tf_op jit(solution)/shard_map/all_to_all | solution.py:253
  39.8 9.5 %collective-permute-start.2 = (bf16[32,8,512]{2,1,0:T(8,128)(2,1)S(1)}, bf16[32,8,512]{2,1,0:T(8,128)(2,1)S(1)}, u32[]{:S(2)}, u32[]{:S(2)}) collective-permute-start(bf16[32,8,512]{2,1,0:T(8,128)(2,1)S(1)} %get-tuple-element.42), channel_id=1, source_target_pairs={{0,1},{1,2},{2,3},{4,5},{5,6},{6,7},{8,9},{9,10},{10,11},{12,13},{... | collective-permute-start | bytes 786440 | tf_op jit(solution)/shard_map/ppermute | solution.py:24
  41.1 8.2 %collective-permute-start.3 = (bf16[32,8,512]{2,1,0:T(8,128)(2,1)S(1)}, bf16[32,8,512]{2,1,0:T(8,128)(2,1)S(1)}, u32[]{:S(2)}, u32[]{:S(2)}) collective-permute-start(bf16[32,8,512]{2,1,0:T(8,128)(2,1)S(1)} %get-tuple-element.43), channel_id=1, source_target_pairs={{1,0},{2,1},{3,2},{5,4},{6,5},{7,6},{9,8},{10,9},{11,10},{13,12},{... | collective-permute-start | bytes 786440 | tf_op jit(solution)/shard_map/ppermute | solution.py:27
  42.5 9.2 %collective-permute-start.10 = (bf16[32,8,512]{2,1,0:T(8,128)(2,1)S(1)}, bf16[32,8,512]{2,1,0:T(8,128)(2,1)S(1)}, u32[]{:S(2)}, u32[]{:S(2)}) collective-permute-start(bf16[32,8,512]{2,1,0:T(8,128)(2,1)S(1)} %get-tuple-element.41), channel_id=1, source_target_pairs={{1,0},{2,1},{3,2},{5,4},{6,5},{7,6},{9,8},{10,9},{11,10},{13,12},{... | collective-permute-start | bytes 786440 | tf_op jit(solution)/shard_map/ppermute | solution.py:27
  43.8 7.9 %collective-permute-start.9 = (bf16[32,8,512]{2,1,0:T(8,128)(2,1)S(1)}, bf16[32,8,512]{2,1,0:T(8,128)(2,1)S(1)}, u32[]{:S(2)}, u32[]{:S(2)}) collective-permute-start(bf16[32,8,512]{2,1,0:T(8,128)(2,1)S(1)} %get-tuple-element.40), channel_id=1, source_target_pairs={{0,1},{1,2},{2,3},{4,5},{5,6},{6,7},{8,9},{9,10},{10,11},{12,13},{... | collective-permute-start | bytes 786440 | tf_op jit(solution)/shard_map/ppermute | solution.py:24
  66.3 1.2 copy-start.1
  71.1 2.8 %copy-start.3 = (bf16[16,16,256]{2,1,0:T(8,128)(2,1)S(1)}, bf16[16,16,256]{2,1,0:T(8,128)(2,1)}, u32[]{:S(2)}) copy-start(bf16[16,16,256]{2,1,0:T(8,128)(2,1)} %param.10) | copy-start | bytes 393220
  71.1 13.8 %copy-start.2 = (bf16[32,32,512]{2,1,0:T(8,128)(2,1)S(1)}, bf16[32,32,512]{2,1,0:T(8,128)(2,1)}, u32[]{:S(2)}) copy-start(bf16[32,32,512]{2,1,0:T(8,128)(2,1)} %pad_maximum_fusion.1) | copy-start | bytes 3145732
  73.9 11.0 %copy-start.6 = (bf16[2,8,2,8,256]{4,3,2,1,0:T(8,128)(2,1)}, bf16[2,8,2,8,256]{4,3,2,1,0:T(8,128)(2,1)S(1)}, u32[]{:S(2)}) copy-start(bf16[2,8,2,8,256]{4,3,2,1,0:T(8,128)(2,1)S(1)} %copy.128) | copy-start | bytes 393220
  74.2 27.9 %collective-permute-start.14 = (f32[16,8,4]{1,0,2:T(8,128)}, f32[16,8,4]{1,0,2:T(8,128)S(1)}, u32[]{:S(2)}, u32[]{:S(2)}) collective-permute-start(f32[16,8,4]{1,0,2:T(8,128)} %get-tuple-element.74), channel_id=1, source_target_pairs={{0,1},{1,2},{2,3},{4,5},{5,6},{6,7},{8,9},{9,10},{10,11},{12,13},{... | collective-permute-start | bytes 6152 | tf_op jit(solution)/shard_map/ppermute | solution.py:50
  75.5 26.6 %collective-permute-start.15 = (f32[16,8,4]{1,0,2:T(8,128)}, f32[16,8,4]{1,0,2:T(8,128)}, u32[]{:S(2)}, u32[]{:S(2)}) collective-permute-start(f32[16,8,4]{1,0,2:T(8,128)} %get-tuple-element.75), channel_id=1, source_target_pairs={{1,0},{2,1},{3,2},{5,4},{6,5},{7,6},{9,8},{10,9},{11,10},{13,12},{... | collective-permute-start | bytes 6152 | tf_op jit(solution)/shard_map/ppermute | solution.py:50
  76.8 14.5 %collective-permute-start.11 = (f32[8,8,4]{1,0,2:T(8,128)}, f32[8,8,4]{1,0,2:T(8,128)S(1)}, u32[]{:S(2)}, u32[]{:S(2)}) collective-permute-start(f32[8,8,4]{1,0,2:T(8,128)} %get-tuple-element.70), channel_id=1, source_target_pairs={{0,5},{1,6},{2,7},{4,9},{5,10},{6,11},{8,13},{9,14},{10,15},{12,17... | collective-permute-start | bytes 3080 | tf_op jit(solution)/shard_map/ppermute | solution.py:50
  82.4 10.1 %collective-permute-start.13 = (f32[8,8,4]{1,0,2:T(8,128)}, f32[8,8,4]{1,0,2:T(8,128)}, u32[]{:S(2)}, u32[]{:S(2)}) collective-permute-start(f32[8,8,4]{1,0,2:T(8,128)} %get-tuple-element.73), channel_id=1, source_target_pairs={{1,4},{2,5},{3,6},{5,8},{6,9},{7,10},{9,12},{10,13},{11,14},{13,16... | collective-permute-start | bytes 3080 | tf_op jit(solution)/shard_map/ppermute | solution.py:50
  83.7 16.2 %collective-permute-start.16 = (f32[8,8,4]{1,0,2:T(8,128)}, f32[8,8,4]{1,0,2:T(8,128)}, u32[]{:S(2)}, u32[]{:S(2)}) collective-permute-start(f32[8,8,4]{1,0,2:T(8,128)} %get-tuple-element.72), channel_id=1, source_target_pairs={{4,1},{5,2},{6,3},{8,5},{9,6},{10,7},{12,9},{13,10},{14,11},{16,13... | collective-permute-start | bytes 3080 | tf_op jit(solution)/shard_map/ppermute | solution.py:50
  84.9 1.1 copy-start.5
  87.6 3.6 %copy-start.11 = (f32[8,8,4]{1,0,2:T(8,128)S(1)}, f32[8,8,4]{1,0,2:T(8,128)}, u32[]{:S(2)}) copy-start(f32[8,8,4]{1,0,2:T(8,128)} %get-tuple-element.71) | copy-start | bytes 3076
  91.2 10.8 %collective-permute-start.18 = (f32[8,8,4]{1,0,2:T(8,128)S(1)}, f32[8,8,4]{1,0,2:T(8,128)S(1)}, u32[]{:S(2)}, u32[]{:S(2)}) collective-permute-start(f32[8,8,4]{1,0,2:T(8,128)S(1)} %copy-done.11), channel_id=1, source_target_pairs={{5,0},{6,1},{7,2},{9,4},{10,5},{11,6},{13,8},{14,9},{15,10},{17,12... | collective-permute-start | bytes 3080 | tf_op jit(solution)/shard_map/ppermute | solution.py:50
  92.5 9.5 %collective-permute-start.12 = (f32[8,16,4]{1,0,2:T(8,128)S(1)}, f32[8,16,4]{1,0,2:T(8,128)S(1)}, u32[]{:S(2)}, u32[]{:S(2)}) collective-permute-start(f32[8,16,4]{1,0,2:T(8,128)S(1)} %slice.368), channel_id=1, source_target_pairs={{0,4},{1,5},{2,6},{3,7},{4,8},{5,9},{6,10},{7,11},{8,12},{9,13},{1... | collective-permute-start | bytes 6152 | tf_op jit(solution)/shard_map/ppermute | solution.py:50
  99.9 5.6 %collective-permute-start.17 = (f32[8,16,4]{1,0,2:T(8,128)S(1)}, f32[8,16,4]{1,0,2:T(8,128)S(1)}, u32[]{:S(2)}, u32[]{:S(2)}) collective-permute-start(f32[8,16,4]{1,0,2:T(8,128)S(1)} %slice.374), channel_id=1, source_target_pairs={{4,0},{5,1},{6,2},{7,3},{8,4},{9,5},{10,6},{11,7},{12,8},{13,9},{1... | collective-permute-start | bytes 6152 | tf_op jit(solution)/shard_map/ppermute | solution.py:50
  118.1 2.7 %collective-permute-start.19 = (f32[512,256]{1,0:T(8,128)S(1)}, f32[512,256]{1,0:T(8,128)S(1)}, u32[]{:S(2)}, u32[]{:S(2)}) collective-permute-start(f32[512,256]{1,0:T(8,128)S(1)} %constant_dynamic-slice_fusion.2), channel_id=1, source_target_pairs={{0,1},{1,0},{2,3},{3,2},{4,5},{5,4},{6,7},{7,6},{8,9},{9,8},{10,11... | collective-permute-start | bytes 1572872 | tf_op jit(solution)/shard_map/ppermute | solution.py:226
  120.9 10.4 %collective-permute-start.20 = (f32[256,256]{1,0:T(8,128)S(1)}, f32[256,256]{1,0:T(8,128)S(1)}, u32[]{:S(2)}, u32[]{:S(2)}) collective-permute-start(f32[256,256]{1,0:T(8,128)S(1)} %constant_dynamic-slice_fusion.1), channel_id=1, source_target_pairs={{0,2},{1,3},{2,0},{3,1},{4,6},{5,7},{6,4},{7,5},{8,10},{9,11},{10,... | collective-permute-start | bytes 786440 | tf_op jit(solution)/shard_map/ppermute | solution.py:226
  131.4 6.3 %collective-permute-start.21 = (f32[128,256]{1,0:T(8,128)S(1)}, f32[128,256]{1,0:T(8,128)S(1)}, u32[]{:S(2)}, u32[]{:S(2)}) collective-permute-start(f32[128,256]{1,0:T(8,128)S(1)} %constant_dynamic-slice_fusion), channel_id=1, source_target_pairs={{0,4},{4,0},{8,12},{12,8},{16,20},{20,16},{24,28},{28,24},{1,5},{5... | collective-permute-start | bytes 393224 | tf_op jit(solution)/shard_map/ppermute | solution.py:226
  137.7 5.0 %collective-permute-start.22 = (f32[128,256]{1,0:T(8,128)S(1)}, f32[128,256]{1,0:T(8,128)S(1)}, u32[]{:S(2)}, u32[]{:S(2)}) collective-permute-start(f32[128,256]{1,0:T(8,128)S(1)} %dynamic-slice_add_fusion.2), channel_id=1, source_target_pairs={{0,8},{4,12},{8,0},{12,4},{16,24},{20,28},{24,16},{28,20},{1,9},{5... | collective-permute-start | bytes 393224 | tf_op jit(solution)/shard_map/ppermute | solution.py:229
  142.8 7.3 %collective-permute-start.23 = (f32[128,256]{1,0:T(8,128)S(1)}, f32[128,256]{1,0:T(8,128)S(1)}, u32[]{:S(2)}, u32[]{:S(2)}) collective-permute-start(f32[128,256]{1,0:T(8,128)S(1)} %add.163), channel_id=1, source_target_pairs={{0,16},{4,20},{8,24},{12,28},{16,0},{20,4},{24,8},{28,12},{1,17},{... | collective-permute-start | bytes 393224 | tf_op jit(solution)/shard_map/ppermute | solution.py:229
  150.1 5.0 %collective-permute-start.24 = (f32[128,256]{1,0:T(8,128)S(1)}, f32[128,256]{1,0:T(8,128)S(1)}, u32[]{:S(2)}, u32[]{:S(2)}) collective-permute-start(f32[128,256]{1,0:T(8,128)S(1)} %add.164), channel_id=1, source_target_pairs={{0,4},{4,0},{8,12},{12,8},{16,20},{20,16},{24,28},{28,24},{1,5},{5... | collective-permute-start | bytes 393224 | tf_op jit(solution)/shard_map/ppermute | solution.py:191
  155.2 6.7 %copy-start.4 = (bf16[256,256]{1,0:T(8,128)(2,1)S(1)}, bf16[256,256]{1,0:T(8,128)(2,1)}, u32[]{:S(2)}) copy-start(bf16[256,256]{1,0:T(8,128)(2,1)} %param.14) | copy-start | bytes 393220
  155.2 7.5 %copy-start.7 = (bf16[2,8,2,8,256]{4,3,2,1,0:T(8,128)(2,1)S(1)}, bf16[2,8,2,8,256]{4,3,2,1,0:T(8,128)(2,1)}, u32[]{:S(2)}) copy-start(bf16[2,8,2,8,256]{4,3,2,1,0:T(8,128)(2,1)} %copy-done.6) | copy-start | bytes 393220
  155.2 7.5 %copy-start.8 = (bf16[256,256]{1,0:T(8,128)(2,1)S(1)}, bf16[256,256]{1,0:T(8,128)(2,1)}, u32[]{:S(2)}) copy-start(bf16[256,256]{1,0:T(8,128)(2,1)} %param.13) | copy-start | bytes 393220
  155.2 7.5 %copy-start.9 = (bf16[256,256]{1,0:T(8,128)(2,1)S(1)}, bf16[256,256]{1,0:T(8,128)(2,1)}, u32[]{:S(2)}) copy-start(bf16[256,256]{1,0:T(8,128)(2,1)} %param.12) | copy-start | bytes 393220
  155.2 7.5 %copy-start.10 = (bf16[256,256]{1,0:T(8,128)(2,1)S(1)}, bf16[256,256]{1,0:T(8,128)(2,1)}, u32[]{:S(2)}) copy-start(bf16[256,256]{1,0:T(8,128)(2,1)} %param.11) | copy-start | bytes 393220
  155.3 6.4 %collective-permute-start.25 = (f32[256,256]{1,0:T(8,128)S(1)}, f32[256,256]{1,0:T(8,128)S(1)}, u32[]{:S(2)}, u32[]{:S(2)}) collective-permute-start(f32[256,256]{1,0:T(8,128)S(1)} %pad_maximum_fusion.6), channel_id=1, source_target_pairs={{0,2},{1,3},{2,0},{3,1},{4,6},{5,7},{6,4},{7,5},{8,10},{9,11},{10,... | collective-permute-start | bytes 786440 | tf_op jit(solution)/shard_map/ppermute | solution.py:191
  161.8 2.0 %collective-permute-start.26 = (f32[512,256]{1,0:T(8,128)S(1)}, f32[512,256]{1,0:T(8,128)S(1)}, u32[]{:S(2)}, u32[]{:S(2)}) collective-permute-start(f32[512,256]{1,0:T(8,128)S(1)} %pad_maximum_fusion.5), channel_id=1, source_target_pairs={{0,1},{1,0},{2,3},{3,2},{4,5},{5,4},{6,7},{7,6},{8,9},{9,8},{10,11... | collective-permute-start | bytes 1572872 | tf_op jit(solution)/shard_map/ppermute | solution.py:191

commit v13 on v11

--- a/solution.py
+++ b/solution.py
@@ -212,7 +212,7 @@
     return tuple(out)
 
 
-def fetch_regions(memory_local, owners, local_ids, axis):
+def fetch_regions(memory_local, owners, local_ids, axis, held):
     count = lax.axis_size(axis)
     entries = owners.shape[0]
     me = lax.axis_index(axis)
@@ -220,6 +220,7 @@
     earlier = order[None, :] < order[:, None]
     tables, slot_of = tree_gather(jnp.stack([owners, local_ids])[None], axis)
     tables = tables[jnp.array([slot_of(device) for device in range(count)])]
+    tables, held = lax.optimization_barrier((tables, held))
     mine = tables[:, 0] == me
     rank_here = jnp.sum(mine[:, None, :] & earlier[None], axis=2)
     wanted = mine[:, :, None] & (rank_here[:, :, None] == jnp.arange(CAP)[None, None, :])
@@ -230,7 +231,7 @@
     received = received.reshape((count * CAP,) + memory_local.shape[1:])
     same = owners[:, None] == owners[None, :]
     rank = jnp.sum(same & earlier, axis=1)
-    return jnp.take(received, owners * CAP + rank, axis=0)
+    return jnp.take(received, owners * CAP + rank, axis=0), held
 
 
 def on_device(
@@ -240,6 +241,12 @@
     block_rows, block_cols = (tile_rows // BSIDE, tile_cols // BSIDE)
     block_count = block_rows * block_cols
     flat_in = patches.reshape(-1, model_width)
+    owners = region_owner.reshape(2 * block_count)
+    local_ids = region_local.reshape(2 * block_count)
+    memory_local = region_memory.reshape(
+        region_memory.shape[2], region_memory.shape[3], region_memory.shape[4]
+    )
+    fetched, flat_in = fetch_regions(memory_local, owners, local_ids, "gx", flat_in)
     w_pair = jnp.concatenate([w_key, w_value], 1)
     queries = jnp.dot(flat_in, w_query, preferred_element_type=jnp.float32).astype(jnp.bfloat16)
     keyvals = jnp.dot(flat_in, w_pair, preferred_element_type=jnp.float32).astype(jnp.bfloat16)
@@ -253,12 +260,6 @@
     row_valid = (row_ids >= 0) & (row_ids < block_rows * gx_count)
     col_valid = (col_ids >= 0) & (col_ids < block_cols * gy_count)
     key_valid = row_valid[:, None] & col_valid[None, :]
-    owners = region_owner.reshape(2 * block_count)
-    local_ids = region_local.reshape(2 * block_count)
-    memory_local = region_memory.reshape(
-        region_memory.shape[2], region_memory.shape[3], region_memory.shape[4]
-    )
-    fetched = fetch_regions(memory_local, owners, local_ids, "gx")
     region_keyval = fetched.reshape(
         block_rows, block_cols, 2, memory_local.shape[1], memory_local.shape[2]
     )

time: 145 us -> 154 us (1.062)
  starting transfers between devices: 50.2 us -> 59.3 us
    ppermute x3, starting transfers between devices: 4.86 us -> 10.6 us  [tree_sum(): joined = keep + lax.ppermute(send, axis, pairs)]
    all_to_all x1, waiting for transfers between devices: 5 us -> 0.01 us  [fetch_regions(): received = lax.all_to_all(sent, axis, 0, 0, tiled=True)]
    ppermute x6, waiting for transfers between devices: 0.02 us -> 4.49 us  [padded(): lax.ppermute(lax.slice_in_dim(block, block.shape[dim] - width, None, axis...]
    ppermute x6, waiting for transfers between devices: 6.5 us -> 9.24 us  [padded(): lax.ppermute(lax.slice_in_dim(block, 0, width, axis=dim), axis, backward)]
    ppermute x6, starting transfers between devices: 19.1 us -> 21.5 us  [padded(): lax.ppermute(lax.slice_in_dim(block, block.shape[dim] - width, None, axis...]
    unnamed x70 -> x62, local copies, waits for them, and re-layouts: 12 us -> 11.6 us
  transfers between devices with their start and end apart: 24 -> 24, of which waited for: 13 -> 13; matrix products, arithmetic and copies ran while one was open for 15% -> 13% of each run, Pallas kernels for 0% -> 0%
where the time goes in v13:
time: 154 us; the launch traced here: 153 us
  starting transfers between devices  59.3 us (39%)
  waiting for transfers between devices  47.8 us (31%)
  local copies, waits for them, and re-layouts  22.6 us (15%)
  matrix products  16 us (10%)
  other arithmetic  5.53 us (4%)
  between operations  1.58 us (1%)
    ppermute x6, starting transfers between devices, padded(): lax.ppermute(lax.slice_in_dim(block, block.shape[dim] - width, None, axis...  21.5 us
    ppermute x6, waiting for transfers between devices, doubling_gather(): got = lax.ppermute(joined, axis, pairs)  13.3 us
    ppermute x3, waiting for transfers between devices, tree_sum(): joined = keep + lax.ppermute(send, axis, pairs)  13.1 us
    unnamed x62, local copies, waits for them, and re-layouts  11.6 us
    ppermute x3, starting transfers between devices, tree_sum(): joined = keep + lax.ppermute(send, axis, pairs)  10.6 us
    ppermute x6, starting transfers between devices, doubling_gather(): got = lax.ppermute(joined, axis, pairs)  10.2 us
    ppermute x6, waiting for transfers between devices, padded(): lax.ppermute(lax.slice_in_dim(block, 0, width, axis=dim), axis, backward)  9.24 us
    ppermute x6, starting transfers between devices, padded(): lax.ppermute(lax.slice_in_dim(block, 0, width, axis=dim), axis, backward)  7.92 us
  transfers between devices with their start and end apart: 24, of which 13 were waited for; matrix products, arithmetic and copies ran while one was open for 13% of the time, Pallas kernels for 0%

profile of v13, /device:TPU:0, one launch (start us, length us, event | category | flops | bytes accessed | tf_op | source)
XLA Modules:
  0.0 152.8 jit_solution(15482822939101081943)
XLA Ops:
  2.4 4.1 %collective-permute-start = (s32[1,2,8]{2,1,0:T(2,128)S(1)}, s32[1,2,8]{2,1,0:T(2,128)S(1)}, u32[]{:S(2)}, u32[]{:S(2)}) collective-permute-start(s32[1,2,8]{2,1,0:T(2,128)S(1)} %add_bitcast_fusion), channel_id=1, source_target_pairs={{0,16},{4,20},{8,24},{12,28},{16,0},{20,4},{24,8},{28,12},{1,17},{... | collective-permute-start | bytes 200 | tf_op jit(solution)/shard_map/ppermute | solution.py:167
  10.5 1.2 convolution_convert_fusion.2
  11.8 1.6 %collective-permute-start.1 = (s32[2,2,8]{2,1,0:T(2,128)S(1)}, s32[2,2,8]{2,1,0:T(2,128)S(1)}, u32[]{:S(2)}, u32[]{:S(2)}) collective-permute-start(s32[2,2,8]{2,1,0:T(2,128)S(1)} %pad_add_fusion.2), channel_id=1, source_target_pairs={{0,8},{4,12},{8,0},{12,4},{16,24},{20,28},{24,16},{28,20},{1,9},{5... | collective-permute-start | bytes 392 | tf_op jit(solution)/shard_map/ppermute | solution.py:167
  13.5 2.0 %collective-permute-done.1 = s32[2,2,8]{2,1,0:T(2,128)S(1)} collective-permute-done((s32[2,2,8]{2,1,0:T(2,128)S(1)}, s32[2,2,8]{2,1,0:T(2,128)S(1)}, u32[]{:S(2)}, u32[]{:S(2)}) %collective-permute-start.1) | collective-permute-done | bytes 160 | tf_op jit(solution)/shard_map/ppermute | solution.py:167
  15.5 1.6 %collective-permute-start.2 = (s32[4,2,8]{2,1,0:T(2,128)S(1)}, s32[4,2,8]{2,1,0:T(2,128)S(1)}, u32[]{:S(2)}, u32[]{:S(2)}) collective-permute-start(s32[4,2,8]{2,1,0:T(2,128)S(1)} %pad_add_fusion.1), channel_id=1, source_target_pairs={{0,4},{4,0},{8,12},{12,8},{16,20},{20,16},{24,28},{28,24},{1,5},{5... | collective-permute-start | bytes 776 | tf_op jit(solution)/shard_map/ppermute | solution.py:167
  17.0 2.1 %collective-permute-done.2 = s32[4,2,8]{2,1,0:T(2,128)S(1)} collective-permute-done((s32[4,2,8]{2,1,0:T(2,128)S(1)}, s32[4,2,8]{2,1,0:T(2,128)S(1)}, u32[]{:S(2)}, u32[]{:S(2)}) %collective-permute-start.2) | collective-permute-done | bytes 288 | tf_op jit(solution)/shard_map/ppermute | solution.py:167
  20.2 1.3 convolution_convert_fusion
  21.6 3.4 %collective-permute-start.3 = (bf16[8,16,512]{2,1,0:T(8,128)(2,1)S(1)}, bf16[8,16,512]{2,1,0:T(8,128)(2,1)S(1)}, u32[]{:S(2)}, u32[]{:S(2)}) collective-permute-start(bf16[8,16,512]{2,1,0:T(8,128)(2,1)S(1)} %bitcast.265), channel_id=1, source_target_pairs={{0,4},{4,8},{8,12},{12,16},{16,20},{20,24},{24,28},{1,5},{5,9},{9,... | collective-permute-start | bytes 393224 | tf_op jit(solution)/shard_map/ppermute | solution.py:24
  25.0 1.3 collective-permute-start.4
  27.1 1.1 broadcast_select_fusion
  28.2 5.1 %all-to-all-start = ((bf16[8,2,64,512]{3,2,1,0:T(8,128)(2,1)}), bf16[8,2,64,512]{3,2,1,0:T(8,128)(2,1)S(1)}, u32[]{:S(2)}, u32[]{:S(2)}) async-start(bf16[8,2,64,512]{3,2,1,0:T(8,128)(2,1)} %broadcast_select_fusion), calls=%async_computation | async-start | bytes 2097152 | tf_op jit(solution)/shard_map/all_to_all | solution.py:230
  34.2 3.9 %collective-permute-start.7 = (bf16[8,16,512]{2,1,0:T(8,128)(2,1)S(1)}, bf16[8,16,512]{2,1,0:T(8,128)(2,1)S(1)}, u32[]{:S(2)}, u32[]{:S(2)}) collective-permute-start(bf16[8,16,512]{2,1,0:T(8,128)(2,1)S(1)} %get-tuple-element.46), channel_id=1, source_target_pairs={{0,4},{4,8},{8,12},{12,16},{16,20},{20,24},{24,28},{1,5},{5,9},{9,... | collective-permute-start | bytes 393224 | tf_op jit(solution)/shard_map/ppermute | solution.py:24
  38.2 1.3 collective-permute-start.8
  39.6 1.3 collective-permute-start.5
  40.9 1.3 collective-permute-start.6
  42.2 4.5 %collective-permute-done.7 = bf16[8,16,512]{2,1,0:T(8,128)(2,1)S(1)} collective-permute-done((bf16[8,16,512]{2,1,0:T(8,128)(2,1)S(1)}, bf16[8,16,512]{2,1,0:T(8,128)(2,1)S(1)}, u32[]{:S(2)}, u32[]{:S(2)}) %collective-permute-start.7) | collective-permute-done | bytes 131104 | tf_op jit(solution)/shard_map/ppermute | solution.py:24
  46.8 1.3 collective-permute-start.10
  48.1 3.0 %collective-permute-start.9 = (bf16[32,8,512]{2,1,0:T(8,128)(2,1)S(1)}, bf16[32,8,512]{2,1,0:T(8,128)(2,1)S(1)}, u32[]{:S(2)}, u32[]{:S(2)}) collective-permute-start(bf16[32,8,512]{2,1,0:T(8,128)(2,1)S(1)} %get-tuple-element.40), channel_id=1, source_target_pairs={{0,1},{1,2},{2,3},{4,5},{5,6},{6,7},{8,9},{9,10},{10,11},{12,13},{... | collective-permute-start | bytes 786440 | tf_op jit(solution)/shard_map/ppermute | solution.py:24
  59.9 1.0 select_dynamic-update-slice_fusion
  60.9 2.3 %slice_bitcast_fusion.1 = (bf16[2,2,88,2,8,128]{5,4,3,2,1,0:T(8,128)(2,1)S(1)}, bf16[2,2,88,2,8,128]{5,4,3,2,1,0:T(8,128)(2,1)S(1)}) fusion(bf16[2,2,704,512]{3,2,1,0:T(8,128)(2,1)} %select_dynamic-update-slice_fusion), kind=kLoop, calls=%fused_computation.14 | loop fusion | bytes 5767168
  64.5 1.2 multiply_reduce_fusion
  65.7 3.0 %fusion.62 = bf16[2,2,64,2,128]{4,2,3,1,0:T(8,128)(2,1)} fusion(bf16[2,2,88,2,8,128]{5,4,3,2,1,0:T(8,128)(2,1)S(1)} %get-tuple-element.10, f32[2,2,2,64,704]{4,3,2,1,0:T(8,128)S(1)} %get-tuple-element.88, bf16[2,2,88,2,8,128]{5,4,3,2,1,0:T(8,128)(2,1)} %copy-done.1, f32[2,2,2,64]{3,2,1,0:T(2,128)S(1)} %bitcast.266, f32[2,2,2,64]{3,2,1,0:T(2,128)S(1)} %log_add_fusion, ...), kind=kOutput, calls=%fused_computation.47 | convolution fusion | flops 186122240 | bytes 4591616 | tf_op jit(solution)/shard_map/abhqk,abkhe->abqhe/dot_general | solution.py:108
  68.7 1.1 copy.137
  70.2 7.0 %collective-permute-start.11 = (f32[8,16,4]{1,0,2:T(8,128)S(1)}, f32[8,16,4]{1,0,2:T(8,128)S(1)}, u32[]{:S(2)}, u32[]{:S(2)}) collective-permute-start(f32[8,16,4]{1,0,2:T(8,128)S(1)} %slice.355), channel_id=1, source_target_pairs={{0,4},{4,8},{8,12},{12,16},{16,20},{20,24},{24,28},{1,5},{5,9},{9,... | collective-permute-start | bytes 6152 | tf_op jit(solution)/shard_map/ppermute | solution.py:24
  77.2 0.9 fusion.116
  78.4 1.3 collective-permute-start.12
  80.0 5.4 %collective-permute-done.12 = f32[8,16,4]{1,0,2:T(8,128)S(1)} collective-permute-done((f32[8,16,4]{1,0,2:T(8,128)S(1)}, f32[8,16,4]{1,0,2:T(8,128)S(1)}, u32[]{:S(2)}, u32[]{:S(2)}) %collective-permute-start.12) | collective-permute-done | bytes 2080 | tf_op jit(solution)/shard_map/ppermute | solution.py:27
  85.5 2.7 %collective-permute-start.13 = (f32[32,8,4]{1,0,2:T(8,128)S(1)}, f32[32,8,4]{1,0,2:T(8,128)S(1)}, u32[]{:S(2)}, u32[]{:S(2)}) collective-permute-start(f32[32,8,4]{1,0,2:T(8,128)S(1)} %get-tuple-element.50), channel_id=1, source_target_pairs={{0,1},{1,2},{2,3},{4,5},{5,6},{6,7},{8,9},{9,10},{10,11},{12,13},{... | collective-permute-start | bytes 12296 | tf_op jit(solution)/shard_map/ppermute | solution.py:24
  88.2 1.5 collective-permute-start.14
  89.7 0.9 fusion.119
  90.7 3.9 %collective-permute-done.14 = f32[32,8,4]{1,0,2:T(8,128)S(1)} collective-permute-done((f32[32,8,4]{1,0,2:T(8,128)S(1)}, f32[32,8,4]{1,0,2:T(8,128)S(1)}, u32[]{:S(2)}, u32[]{:S(2)}) %collective-permute-start.14) | collective-permute-done | bytes 4128 | tf_op jit(solution)/shard_map/ppermute | solution.py:27
  95.1 1.9 %fusion.9 = f32[2,2,2,576,64]{3,4,2,1,0:T(8,128)S(1)} fusion(f32[2,2,2,576]{3,2,1,0:T(2,128)S(1)} %concatenate.90, pred[2,2,576]{2,1,0:T(4,128)(4,1)S(1)} %copy-done.18, bf16[2,2,8,2,8,128]{5,4,3,2,1,0:T(8,128)(2,1)S(1)} %copy-done.16, bf16[2,2,576,256]{3,2,1,0:T(8,128)(2,1)} %copy-done.17), kind=kOutput, calls=%fused_computation.20 | convolution fusion | flops 76382208 | bytes 2511104 | tf_op jit(solution)/shard_map/abqhe,abkhe->abhqk/dot_general | solution.py:126
  98.2 2.0 %fusion.57 = bf16[2,2,64,2,128]{4,2,3,1,0:T(8,128)(2,1)S(1)} fusion(f32[2,2,2,576,64]{3,4,2,1,0:T(8,128)S(1)} %fusion.9, f32[2,2,2,576]{3,2,1,0:T(2,128)} %concatenate.92, bf16[2,2,8,2,8,128]{5,4,3,2,1,0:T(8,128)(2,1)S(1)} %copy-done.15, bf16[2,2,576,256]{3,2,1,0:T(8,128)(2,1)S(1)} %copy-done.4, bf16[2,2,576,256]{3,2,1,0:T(8,128)(2,1)} %copy-done.17), kind=kOutput, calls=%fused_computation.46 | convolution fusion | flops 152010752 | bytes 3819520 | tf_op jit(solution)/shard_map/abhqk,abqhe->abkhe/dot_general | solution.py:135
  101.4 3.0 %collective-permute-start.15 = (f32[512,256]{1,0:T(8,128)S(1)}, f32[512,256]{1,0:T(8,128)S(1)}, u32[]{:S(2)}, u32[]{:S(2)}) collective-permute-start(f32[512,256]{1,0:T(8,128)S(1)} %constant_dynamic-slice_fusion.1), channel_id=1, source_target_pairs={{0,1},{1,0},{2,3},{3,2},{4,5},{5,4},{6,7},{7,6},{8,9},{9,8},{10,11... | collective-permute-start | bytes 1572872 | tf_op jit(solution)/shard_map/ppermute | solution.py:202
  104.4 1.5 %collective-permute-done.15 = f32[512,256]{1,0:T(8,128)S(1)} collective-permute-done((f32[512,256]{1,0:T(8,128)S(1)}, f32[512,256]{1,0:T(8,128)S(1)}, u32[]{:S(2)}, u32[]{:S(2)}) %collective-permute-start.15) | collective-permute-done | bytes 524320 | tf_op jit(solution)/shard_map/ppermute | solution.py:202
  106.3 8.4 %collective-permute-done.16 = f32[256,256]{1,0:T(8,128)S(1)} collective-permute-done((f32[256,256]{1,0:T(8,128)S(1)}, f32[256,256]{1,0:T(8,128)S(1)}, u32[]{:S(2)}, u32[]{:S(2)}) %collective-permute-start.16) | collective-permute-done | bytes 262176 | tf_op jit(solution)/shard_map/ppermute | solution.py:202
  114.7 7.3 %collective-permute-start.17 = (f32[128,256]{1,0:T(8,128)S(1)}, f32[128,256]{1,0:T(8,128)S(1)}, u32[]{:S(2)}, u32[]{:S(2)}) collective-permute-start(f32[128,256]{1,0:T(8,128)S(1)} %constant_dynamic-slice_fusion.2), channel_id=1, source_target_pairs={{0,4},{4,0},{8,12},{12,8},{16,20},{20,16},{24,28},{28,24},{1,5},{5... | collective-permute-start | bytes 393224 | tf_op jit(solution)/shard_map/ppermute | solution.py:202
  122.0 3.2 %collective-permute-done.17 = f32[128,256]{1,0:T(8,128)S(1)} collective-permute-done((f32[128,256]{1,0:T(8,128)S(1)}, f32[128,256]{1,0:T(8,128)S(1)}, u32[]{:S(2)}, u32[]{:S(2)}) %collective-permute-start.17) | collective-permute-done | bytes 131104 | tf_op jit(solution)/shard_map/ppermute | solution.py:202
  125.2 2.8 %collective-permute-start.18 = (f32[128,256]{1,0:T(8,128)S(1)}, f32[128,256]{1,0:T(8,128)S(1)}, u32[]{:S(2)}, u32[]{:S(2)}) collective-permute-start(f32[128,256]{1,0:T(8,128)S(1)} %dynamic-slice_add_fusion.2), channel_id=1, source_target_pairs={{0,8},{4,12},{8,0},{12,4},{16,24},{20,28},{24,16},{28,20},{1,9},{5... | collective-permute-start | bytes 393224 | tf_op jit(solution)/shard_map/ppermute | solution.py:205
  128.0 3.1 %collective-permute-done.18 = f32[128,256]{1,0:T(8,128)S(1)} collective-permute-done((f32[128,256]{1,0:T(8,128)S(1)}, f32[128,256]{1,0:T(8,128)S(1)}, u32[]{:S(2)}, u32[]{:S(2)}) %collective-permute-start.18) | collective-permute-done | bytes 131104 | tf_op jit(solution)/shard_map/ppermute | solution.py:205
  131.1 1.4 collective-permute-start.19
  132.5 4.6 %collective-permute-done.19 = f32[128,256]{1,0:T(8,128)S(1)} collective-permute-done((f32[128,256]{1,0:T(8,128)S(1)}, f32[128,256]{1,0:T(8,128)S(1)}, u32[]{:S(2)}, u32[]{:S(2)}) %collective-permute-start.19) | collective-permute-done | bytes 131104 | tf_op jit(solution)/shard_map/ppermute | solution.py:205
  137.1 2.5 %collective-permute-start.20 = (f32[128,256]{1,0:T(8,128)S(1)}, f32[128,256]{1,0:T(8,128)S(1)}, u32[]{:S(2)}, u32[]{:S(2)}) collective-permute-start(f32[128,256]{1,0:T(8,128)S(1)} %add.166), channel_id=1, source_target_pairs={{0,4},{4,0},{8,12},{12,8},{16,20},{20,16},{24,28},{28,24},{1,5},{5... | collective-permute-start | bytes 393224 | tf_op jit(solution)/shard_map/ppermute | solution.py:167
  139.6 2.9 %collective-permute-done.20 = f32[128,256]{1,0:T(8,128)S(1)} collective-permute-done((f32[128,256]{1,0:T(8,128)S(1)}, f32[128,256]{1,0:T(8,128)S(1)}, u32[]{:S(2)}, u32[]{:S(2)}) %collective-permute-start.20) | collective-permute-done | bytes 131104 | tf_op jit(solution)/shard_map/ppermute | solution.py:167
  142.9 6.1 %collective-permute-done.21 = f32[256,256]{1,0:T(8,128)S(1)} collective-permute-done((f32[256,256]{1,0:T(8,128)S(1)}, f32[256,256]{1,0:T(8,128)S(1)}, u32[]{:S(2)}, u32[]{:S(2)}) %collective-permute-start.21) | collective-permute-done | bytes 262176 | tf_op jit(solution)/shard_map/ppermute | solution.py:167
  149.2 0.8 convolution_convert_fusion.3
  150.1 1.0 convolution_convert_fusion.1
  151.2 0.8 fusion.106
  (195 shorter events, 24.3 us)
Async XLA Ops:
  0.6 25.8 %copy-start = (bf16[1,1,4,64,512]{4,3,2,1,0:T(8,128)(2,1)S(1)}, bf16[1,1,4,64,512]{4,3,2,1,0:T(8,128)(2,1)}, u32[]{:S(2)}) copy-start(bf16[1,1,4,64,512]{4,3,2,1,0:T(8,128)(2,1)} %param.15) | copy-start | bytes 786436
  2.4 9.4 %collective-permute-start = (s32[1,2,8]{2,1,0:T(2,128)S(1)}, s32[1,2,8]{2,1,0:T(2,128)S(1)}, u32[]{:S(2)}, u32[]{:S(2)}) collective-permute-start(s32[1,2,8]{2,1,0:T(2,128)S(1)} %add_bitcast_fusion), channel_id=1, source_target_pairs={{0,16},{4,20},{8,24},{12,28},{16,0},{20,4},{24,8},{28,12},{1,17},{... | collective-permute-start | bytes 200 | tf_op jit(solution)/shard_map/ppermute | solution.py:167
  11.8 3.7 %collective-permute-start.1 = (s32[2,2,8]{2,1,0:T(2,128)S(1)}, s32[2,2,8]{2,1,0:T(2,128)S(1)}, u32[]{:S(2)}, u32[]{:S(2)}) collective-permute-start(s32[2,2,8]{2,1,0:T(2,128)S(1)} %pad_add_fusion.2), channel_id=1, source_target_pairs={{0,8},{4,12},{8,0},{12,4},{16,24},{20,28},{24,16},{28,20},{1,9},{5... | collective-permute-start | bytes 392 | tf_op jit(solution)/shard_map/ppermute | solution.py:167
  15.5 3.7 %collective-permute-start.2 = (s32[4,2,8]{2,1,0:T(2,128)S(1)}, s32[4,2,8]{2,1,0:T(2,128)S(1)}, u32[]{:S(2)}, u32[]{:S(2)}) collective-permute-start(s32[4,2,8]{2,1,0:T(2,128)S(1)} %pad_add_fusion.1), channel_id=1, source_target_pairs={{0,4},{4,0},{8,12},{12,8},{16,20},{20,16},{24,28},{28,24},{1,5},{5... | collective-permute-start | bytes 776 | tf_op jit(solution)/shard_map/ppermute | solution.py:167
  21.6 17.9 %collective-permute-start.3 = (bf16[8,16,512]{2,1,0:T(8,128)(2,1)S(1)}, bf16[8,16,512]{2,1,0:T(8,128)(2,1)S(1)}, u32[]{:S(2)}, u32[]{:S(2)}) collective-permute-start(bf16[8,16,512]{2,1,0:T(8,128)(2,1)S(1)} %bitcast.265), channel_id=1, source_target_pairs={{0,4},{4,8},{8,12},{12,16},{16,20},{20,24},{24,28},{1,5},{5,9},{9,... | collective-permute-start | bytes 393224 | tf_op jit(solution)/shard_map/ppermute | solution.py:24
  25.0 14.5 %collective-permute-start.4 = (bf16[8,16,512]{2,1,0:T(8,128)(2,1)S(1)}, bf16[8,16,512]{2,1,0:T(8,128)(2,1)S(1)}, u32[]{:S(2)}, u32[]{:S(2)}) collective-permute-start(bf16[8,16,512]{2,1,0:T(8,128)(2,1)S(1)} %bitcast.264), channel_id=1, source_target_pairs={{4,0},{8,4},{12,8},{16,12},{20,16},{24,20},{28,24},{5,1},{9,5},{13... | collective-permute-start | bytes 393224 | tf_op jit(solution)/shard_map/ppermute | solution.py:27
  28.2 5.1 %copy-start.2 = (bf16[16,16,256]{2,1,0:T(8,128)(2,1)S(1)}, bf16[16,16,256]{2,1,0:T(8,128)(2,1)}, u32[]{:S(2)}) copy-start(bf16[16,16,256]{2,1,0:T(8,128)(2,1)} %param.10) | copy-start | bytes 393220
  28.2 5.1 %copy-start.13 = (bf16[256,256]{1,0:T(8,128)(2,1)S(1)}, bf16[256,256]{1,0:T(8,128)(2,1)}, u32[]{:S(2)}) copy-start(bf16[256,256]{1,0:T(8,128)(2,1)} %param.11) | copy-start | bytes 393220
  28.2 31.1 %all-to-all-start = ((bf16[8,2,64,512]{3,2,1,0:T(8,128)(2,1)}), bf16[8,2,64,512]{3,2,1,0:T(8,128)(2,1)S(1)}, u32[]{:S(2)}, u32[]{:S(2)}) async-start(bf16[8,2,64,512]{3,2,1,0:T(8,128)(2,1)} %broadcast_select_fusion), calls=%async_computation | async-start | bytes 2097152 | tf_op jit(solution)/shard_map/all_to_all | solution.py:230
  34.2 12.5 %collective-permute-start.7 = (bf16[8,16,512]{2,1,0:T(8,128)(2,1)S(1)}, bf16[8,16,512]{2,1,0:T(8,128)(2,1)S(1)}, u32[]{:S(2)}, u32[]{:S(2)}) collective-permute-start(bf16[8,16,512]{2,1,0:T(8,128)(2,1)S(1)} %get-tuple-element.46), channel_id=1, source_target_pairs={{0,4},{4,8},{8,12},{12,16},{16,20},{20,24},{24,28},{1,5},{5,9},{9,... | collective-permute-start | bytes 393224 | tf_op jit(solution)/shard_map/ppermute | solution.py:24
  38.2 8.5 %collective-permute-start.8 = (bf16[8,16,512]{2,1,0:T(8,128)(2,1)S(1)}, bf16[8,16,512]{2,1,0:T(8,128)(2,1)S(1)}, u32[]{:S(2)}, u32[]{:S(2)}) collective-permute-start(bf16[8,16,512]{2,1,0:T(8,128)(2,1)S(1)} %get-tuple-element.47), channel_id=1, source_target_pairs={{4,0},{8,4},{12,8},{16,12},{20,16},{24,20},{28,24},{5,1},{9,5},{13... | collective-permute-start | bytes 393224 | tf_op jit(solution)/shard_map/ppermute | solution.py:27
  39.6 11.5 %collective-permute-start.5 = (bf16[32,8,512]{2,1,0:T(8,128)(2,1)S(1)}, bf16[32,8,512]{2,1,0:T(8,128)(2,1)S(1)}, u32[]{:S(2)}, u32[]{:S(2)}) collective-permute-start(bf16[32,8,512]{2,1,0:T(8,128)(2,1)S(1)} %get-tuple-element.42), channel_id=1, source_target_pairs={{0,1},{1,2},{2,3},{4,5},{5,6},{6,7},{8,9},{9,10},{10,11},{12,13},{... | collective-permute-start | bytes 786440 | tf_op jit(solution)/shard_map/ppermute | solution.py:24
  40.9 10.2 %collective-permute-start.6 = (bf16[32,8,512]{2,1,0:T(8,128)(2,1)S(1)}, bf16[32,8,512]{2,1,0:T(8,128)(2,1)S(1)}, u32[]{:S(2)}, u32[]{:S(2)}) collective-permute-start(bf16[32,8,512]{2,1,0:T(8,128)(2,1)S(1)} %get-tuple-element.43), channel_id=1, source_target_pairs={{1,0},{2,1},{3,2},{5,4},{6,5},{7,6},{9,8},{10,9},{11,10},{13,12},{... | collective-permute-start | bytes 786440 | tf_op jit(solution)/shard_map/ppermute | solution.py:27
  46.8 6.8 %collective-permute-start.10 = (bf16[32,8,512]{2,1,0:T(8,128)(2,1)S(1)}, bf16[32,8,512]{2,1,0:T(8,128)(2,1)S(1)}, u32[]{:S(2)}, u32[]{:S(2)}) collective-permute-start(bf16[32,8,512]{2,1,0:T(8,128)(2,1)S(1)} %get-tuple-element.41), channel_id=1, source_target_pairs={{1,0},{2,1},{3,2},{5,4},{6,5},{7,6},{9,8},{10,9},{11,10},{13,12},{... | collective-permute-start | bytes 786440 | tf_op jit(solution)/shard_map/ppermute | solution.py:27
  48.1 5.5 %collective-permute-start.9 = (bf16[32,8,512]{2,1,0:T(8,128)(2,1)S(1)}, bf16[32,8,512]{2,1,0:T(8,128)(2,1)S(1)}, u32[]{:S(2)}, u32[]{:S(2)}) collective-permute-start(bf16[32,8,512]{2,1,0:T(8,128)(2,1)S(1)} %get-tuple-element.40), channel_id=1, source_target_pairs={{0,1},{1,2},{2,3},{4,5},{5,6},{6,7},{8,9},{9,10},{10,11},{12,13},{... | collective-permute-start | bytes 786440 | tf_op jit(solution)/shard_map/ppermute | solution.py:24
  54.0 4.5 %copy-start.3 = (bf16[2,2,576,256]{3,2,1,0:T(8,128)(2,1)}, bf16[2,2,576,256]{3,2,1,0:T(8,128)(2,1)S(1)}, u32[]{:S(2)}) copy-start(bf16[2,2,576,256]{3,2,1,0:T(8,128)(2,1)S(1)} %get-tuple-element.17) | copy-start | bytes 3538948
  54.1 4.5 %copy-start.17 = (bf16[2,2,576,256]{3,2,1,0:T(8,128)(2,1)}, bf16[2,2,576,256]{3,2,1,0:T(8,128)(2,1)S(1)}, u32[]{:S(2)}) copy-start(bf16[2,2,576,256]{3,2,1,0:T(8,128)(2,1)S(1)} %get-tuple-element.16) | copy-start | bytes 3538948
  60.9 2.3 %copy-start.10 = (bf16[2,2,64,2,128]{4,3,2,1,0:T(2,128)(2,1)S(1)}, bf16[2,2,64,2,128]{4,3,2,1,0:T(2,128)(2,1)}, u32[]{:S(2)}) copy-start(bf16[2,2,64,2,128]{4,3,2,1,0:T(2,128)(2,1)} %reshape_reshape.29) | copy-start | bytes 393220
  63.2 1.3 copy-start.1
  68.7 11.0 %copy-start.8 = (bf16[2,2,64,2,128]{4,2,3,1,0:T(8,128)(2,1)S(1)}, bf16[2,2,64,2,128]{4,2,3,1,0:T(8,128)(2,1)}, u32[]{:S(2)}) copy-start(bf16[2,2,64,2,128]{4,2,3,1,0:T(8,128)(2,1)} %get-tuple-element.90) | copy-start | bytes 393220
  69.8 19.9 %copy-start.9 = (bf16[16,16,256]{2,1,0:T(8,128)(2,1)S(1)}, bf16[16,16,256]{2,1,0:T(8,128)(2,1)}, u32[]{:S(2)}) copy-start(bf16[16,16,256]{2,1,0:T(8,128)(2,1)} %param.18) | copy-start | bytes 393220
  70.2 9.8 %collective-permute-start.11 = (f32[8,16,4]{1,0,2:T(8,128)S(1)}, f32[8,16,4]{1,0,2:T(8,128)S(1)}, u32[]{:S(2)}, u32[]{:S(2)}) collective-permute-start(f32[8,16,4]{1,0,2:T(8,128)S(1)} %slice.355), channel_id=1, source_target_pairs={{0,4},{4,8},{8,12},{12,16},{16,20},{20,24},{24,28},{1,5},{5,9},{9,... | collective-permute-start | bytes 6152 | tf_op jit(solution)/shard_map/ppermute | solution.py:24
  78.4 7.0 %collective-permute-start.12 = (f32[8,16,4]{1,0,2:T(8,128)S(1)}, f32[8,16,4]{1,0,2:T(8,128)S(1)}, u32[]{:S(2)}, u32[]{:S(2)}) collective-permute-start(f32[8,16,4]{1,0,2:T(8,128)S(1)} %slice.357), channel_id=1, source_target_pairs={{4,0},{8,4},{12,8},{16,12},{20,16},{24,20},{28,24},{5,1},{9,5},{13... | collective-permute-start | bytes 6152 | tf_op jit(solution)/shard_map/ppermute | solution.py:27
  80.0 15.2 %copy-start.16 = (bf16[2,2,8,2,8,128]{5,4,3,2,1,0:T(8,128)(2,1)S(1)}, bf16[2,2,8,2,8,128]{5,4,3,2,1,0:T(8,128)(2,1)}, u32[]{:S(2)}) copy-start(bf16[2,2,8,2,8,128]{5,4,3,2,1,0:T(8,128)(2,1)} %get-tuple-element.15) | copy-start | bytes 393220
  80.0 15.2 %copy-start.18 = (pred[2,2,576]{2,1,0:T(4,128)(4,1)S(1)}, pred[2,2,576]{2,1,0:T(4,128)(4,1)}, u32[]{:S(2)}) copy-start(pred[2,2,576]{2,1,0:T(4,128)(4,1)} %concatenate.86) | copy-start | bytes 6916
  85.5 5.2 %collective-permute-start.13 = (f32[32,8,4]{1,0,2:T(8,128)S(1)}, f32[32,8,4]{1,0,2:T(8,128)S(1)}, u32[]{:S(2)}, u32[]{:S(2)}) collective-permute-start(f32[32,8,4]{1,0,2:T(8,128)S(1)} %get-tuple-element.50), channel_id=1, source_target_pairs={{0,1},{1,2},{2,3},{4,5},{5,6},{6,7},{8,9},{9,10},{10,11},{12,13},{... | collective-permute-start | bytes 12296 | tf_op jit(solution)/shard_map/ppermute | solution.py:24
  88.2 6.3 %collective-permute-start.14 = (f32[32,8,4]{1,0,2:T(8,128)S(1)}, f32[32,8,4]{1,0,2:T(8,128)S(1)}, u32[]{:S(2)}, u32[]{:S(2)}) collective-permute-start(f32[32,8,4]{1,0,2:T(8,128)S(1)} %get-tuple-element.51), channel_id=1, source_target_pairs={{1,0},{2,1},{3,2},{5,4},{6,5},{7,6},{9,8},{10,9},{11,10},{13,12},{... | collective-permute-start | bytes 12296 | tf_op jit(solution)/shard_map/ppermute | solution.py:27
  95.1 1.9 %copy-start.4 = (bf16[2,2,576,256]{3,2,1,0:T(8,128)(2,1)S(1)}, bf16[2,2,576,256]{3,2,1,0:T(8,128)(2,1)}, u32[]{:S(2)}) copy-start(bf16[2,2,576,256]{3,2,1,0:T(8,128)(2,1)} %copy-done.3) | copy-start | bytes 3538948
  97.1 1.1 copy-start.15
  100.2 1.0 copy-start.5
  100.2 1.0 copy-start.6
  101.4 4.5 %collective-permute-start.15 = (f32[512,256]{1,0:T(8,128)S(1)}, f32[512,256]{1,0:T(8,128)S(1)}, u32[]{:S(2)}, u32[]{:S(2)}) collective-permute-start(f32[512,256]{1,0:T(8,128)S(1)} %constant_dynamic-slice_fusion.1), channel_id=1, source_target_pairs={{0,1},{1,0},{2,3},{3,2},{4,5},{5,4},{6,7},{7,6},{8,9},{9,8},{10,11... | collective-permute-start | bytes 1572872 | tf_op jit(solution)/shard_map/ppermute | solution.py:202
  106.0 8.7 %collective-permute-start.16 = (f32[256,256]{1,0:T(8,128)S(1)}, f32[256,256]{1,0:T(8,128)S(1)}, u32[]{:S(2)}, u32[]{:S(2)}) collective-permute-start(f32[256,256]{1,0:T(8,128)S(1)} %constant_dynamic-slice_fusion), channel_id=1, source_target_pairs={{0,2},{1,3},{2,0},{3,1},{4,6},{5,7},{6,4},{7,5},{8,10},{9,11},{10,... | collective-permute-start | bytes 786440 | tf_op jit(solution)/shard_map/ppermute | solution.py:202
  114.7 10.5 %collective-permute-start.17 = (f32[128,256]{1,0:T(8,128)S(1)}, f32[128,256]{1,0:T(8,128)S(1)}, u32[]{:S(2)}, u32[]{:S(2)}) collective-permute-start(f32[128,256]{1,0:T(8,128)S(1)} %constant_dynamic-slice_fusion.2), channel_id=1, source_target_pairs={{0,4},{4,0},{8,12},{12,8},{16,20},{20,16},{24,28},{28,24},{1,5},{5... | collective-permute-start | bytes 393224 | tf_op jit(solution)/shard_map/ppermute | solution.py:202
  125.2 5.9 %collective-permute-start.18 = (f32[128,256]{1,0:T(8,128)S(1)}, f32[128,256]{1,0:T(8,128)S(1)}, u32[]{:S(2)}, u32[]{:S(2)}) collective-permute-start(f32[128,256]{1,0:T(8,128)S(1)} %dynamic-slice_add_fusion.2), channel_id=1, source_target_pairs={{0,8},{4,12},{8,0},{12,4},{16,24},{20,28},{24,16},{28,20},{1,9},{5... | collective-permute-start | bytes 393224 | tf_op jit(solution)/shard_map/ppermute | solution.py:205
  131.1 5.9 %collective-permute-start.19 = (f32[128,256]{1,0:T(8,128)S(1)}, f32[128,256]{1,0:T(8,128)S(1)}, u32[]{:S(2)}, u32[]{:S(2)}) collective-permute-start(f32[128,256]{1,0:T(8,128)S(1)} %add.165), channel_id=1, source_target_pairs={{0,16},{4,20},{8,24},{12,28},{16,0},{20,4},{24,8},{28,12},{1,17},{... | collective-permute-start | bytes 393224 | tf_op jit(solution)/shard_map/ppermute | solution.py:205
  137.1 5.4 %collective-permute-start.20 = (f32[128,256]{1,0:T(8,128)S(1)}, f32[128,256]{1,0:T(8,128)S(1)}, u32[]{:S(2)}, u32[]{:S(2)}) collective-permute-start(f32[128,256]{1,0:T(8,128)S(1)} %add.166), channel_id=1, source_target_pairs={{0,4},{4,0},{8,12},{12,8},{16,20},{20,16},{24,28},{28,24},{1,5},{5... | collective-permute-start | bytes 393224 | tf_op jit(solution)/shard_map/ppermute | solution.py:167
  142.5 6.7 %copy-start.7 = (bf16[256,256]{1,0:T(8,128)(2,1)S(1)}, bf16[256,256]{1,0:T(8,128)(2,1)}, u32[]{:S(2)}) copy-start(bf16[256,256]{1,0:T(8,128)(2,1)} %param.14) | copy-start | bytes 393220
  142.5 7.5 %copy-start.11 = (bf16[256,256]{1,0:T(8,128)(2,1)S(1)}, bf16[256,256]{1,0:T(8,128)(2,1)}, u32[]{:S(2)}) copy-start(bf16[256,256]{1,0:T(8,128)(2,1)} %param.13) | copy-start | bytes 393220
  142.5 7.5 %copy-start.12 = (bf16[256,256]{1,0:T(8,128)(2,1)S(1)}, bf16[256,256]{1,0:T(8,128)(2,1)}, u32[]{:S(2)}) copy-start(bf16[256,256]{1,0:T(8,128)(2,1)} %param.12) | copy-start | bytes 393220
  142.6 7.5 %copy-start.14 = (bf16[256,256]{1,0:T(8,128)(2,1)S(1)}, bf16[256,256]{1,0:T(8,128)(2,1)}, u32[]{:S(2)}) copy-start(bf16[256,256]{1,0:T(8,128)(2,1)} %param.11) | copy-start | bytes 393220
  142.6 6.4 %collective-permute-start.21 = (f32[256,256]{1,0:T(8,128)S(1)}, f32[256,256]{1,0:T(8,128)S(1)}, u32[]{:S(2)}, u32[]{:S(2)}) collective-permute-start(f32[256,256]{1,0:T(8,128)S(1)} %pad_maximum_fusion.6), channel_id=1, source_target_pairs={{0,2},{1,3},{2,0},{3,1},{4,6},{5,7},{6,4},{7,5},{8,10},{9,11},{10,... | collective-permute-start | bytes 786440 | tf_op jit(solution)/shard_map/ppermute | solution.py:167
  149.1 2.0 %collective-permute-start.22 = (f32[512,256]{1,0:T(8,128)S(1)}, f32[512,256]{1,0:T(8,128)S(1)}, u32[]{:S(2)}, u32[]{:S(2)}) collective-permute-start(f32[512,256]{1,0:T(8,128)S(1)} %pad_maximum_fusion.5), channel_id=1, source_target_pairs={{0,1},{1,0},{2,3},{3,2},{4,5},{5,4},{6,7},{7,6},{8,9},{9,8},{10,11... | collective-permute-start | bytes 1572872 | tf_op jit(solution)/shard_map/ppermute | solution.py:167

commit v14 on v11

--- a/solution.py
+++ b/solution.py
@@ -226,11 +226,15 @@
     asked = jnp.sum(jnp.where(wanted, tables[:, 1][:, :, None], 0), axis=1)
     sent = jnp.take(memory_local, asked.reshape(-1), axis=0)
     sent = sent.reshape((count, CAP) + memory_local.shape[1:])
-    received = lax.all_to_all(sent, axis, 0, 0, tiled=True)
-    received = received.reshape((count * CAP,) + memory_local.shape[1:])
+    width = memory_local.shape[-1] // 2
     same = owners[:, None] == owners[None, :]
     rank = jnp.sum(same & earlier, axis=1)
-    return jnp.take(received, owners * CAP + rank, axis=0)
+    halves = []
+    for half in (sent[..., :width], sent[..., width:]):
+        received = lax.all_to_all(half, axis, 0, 0, tiled=True)
+        received = received.reshape((count * CAP,) + half.shape[2:])
+        halves.append(jnp.take(received, owners * CAP + rank, axis=0))
+    return jnp.concatenate(halves, -1)
 
 
 def on_device(

time: 145 us -> 162 us (1.12)
  waiting for transfers between devices: 48 us -> 54.7 us
  local copies, waits for them, and re-layouts: 23.4 us -> 29.9 us
  starting transfers between devices: 50.2 us -> 55.5 us
  other arithmetic: 4.22 us -> 2.34 us
    all_to_all x1 -> x2, starting transfers between devices: 3.56 us -> 10 us  [fetch_regions(): received = lax.all_to_all(half, axis, 0, 0, tiled=True)]
    all_to_all x1 -> x2, waiting for transfers between devices: 5 us -> 11 us  [fetch_regions(): received = lax.all_to_all(half, axis, 0, 0, tiled=True)]
    gather x1 -> x2, local copies, waits for them, and re-layouts: 0.58 us -> 3.21 us  [fetch_regions(): halves.append(jnp.take(received, owners * CAP + rank, axis=0))]
    ppermute x2, starting transfers between devices: 3.42 us -> 1.55 us  [tree_sum(): joined = joined + lax.ppermute(joined, axis, pairs)]
    ppermute x2, waiting for transfers between devices: 8.95 us -> 10.8 us  [tree_sum(): joined = joined + lax.ppermute(joined, axis, pairs)]
    unnamed x70 -> x66, local copies, waits for them, and re-layouts: 12 us -> 13.4 us
  transfers between devices with their start and end apart: 24 -> 25, of which waited for: 13 -> 13; matrix products, arithmetic and copies ran while one was open for 15% -> 15% of each run, Pallas kernels for 0% -> 0%
where the time goes in v14:
time: 162 us; the launch traced here: 161 us
  starting transfers between devices  55.5 us (34%)
  waiting for transfers between devices  54.7 us (34%)
  local copies, waits for them, and re-layouts  29.9 us (18%)
  matrix products  16.6 us (10%)
  other arithmetic  2.34 us (1%)
  between operations  1.69 us (1%)
    ppermute x6, starting transfers between devices, padded(): lax.ppermute(lax.slice_in_dim(block, block.shape[dim] - width, None, axis...  19.4 us
    ppermute x6, waiting for transfers between devices, doubling_gather(): got = lax.ppermute(joined, axis, pairs)  13.9 us
    unnamed x66, local copies, waits for them, and re-layouts  13.4 us
    ppermute x3, waiting for transfers between devices, tree_sum(): joined = keep + lax.ppermute(send, axis, pairs)  13.2 us
    ppermute x6, starting transfers between devices, doubling_gather(): got = lax.ppermute(joined, axis, pairs)  11.6 us
    all_to_all x2, waiting for transfers between devices, fetch_regions(): received = lax.all_to_all(half, axis, 0, 0, tiled=True)  11 us
    ppermute x2, waiting for transfers between devices, tree_sum(): joined = joined + lax.ppermute(joined, axis, pairs)  10.8 us
    all_to_all x2, starting transfers between devices, fetch_regions(): received = lax.all_to_all(half, axis, 0, 0, tiled=True)  10 us
  transfers between devices with their start and end apart: 25, of which 13 were waited for; matrix products, arithmetic and copies ran while one was open for 15% of the time, Pallas kernels for 0%

profile of v14, /device:TPU:0, one launch (start us, length us, event | category | flops | bytes accessed | tf_op | source)
XLA Modules:
  0.0 160.6 jit_solution(8828468631591423073)
XLA Ops:
  2.4 4.1 %collective-permute-start.4 = (s32[1,2,8]{2,1,0:T(2,128)S(1)}, s32[1,2,8]{2,1,0:T(2,128)S(1)}, u32[]{:S(2)}, u32[]{:S(2)}) collective-permute-start(s32[1,2,8]{2,1,0:T(2,128)S(1)} %add_bitcast_fusion), channel_id=1, source_target_pairs={{0,16},{4,20},{8,24},{12,28},{16,0},{20,4},{24,8},{28,12},{1,17},{... | collective-permute-start | bytes 200 | tf_op jit(solution)/shard_map/ppermute | solution.py:167
  6.5 1.3 convolution_convert_fusion
  7.8 3.4 %collective-permute-start = (bf16[8,16,512]{2,1,0:T(8,128)(2,1)S(1)}, bf16[8,16,512]{2,1,0:T(8,128)(2,1)S(1)}, u32[]{:S(2)}, u32[]{:S(2)}) collective-permute-start(bf16[8,16,512]{2,1,0:T(8,128)(2,1)S(1)} %bitcast.266), channel_id=1, source_target_pairs={{0,4},{4,8},{8,12},{12,16},{16,20},{20,24},{24,28},{1,5},{5,9},{9,... | collective-permute-start | bytes 393224 | tf_op jit(solution)/shard_map/ppermute | solution.py:24
  11.2 1.3 collective-permute-start.1
  12.5 1.2 convolution_convert_fusion.4
  14.0 4.6 %collective-permute-start.7 = (bf16[8,16,512]{2,1,0:T(8,128)(2,1)S(1)}, bf16[8,16,512]{2,1,0:T(8,128)(2,1)S(1)}, u32[]{:S(2)}, u32[]{:S(2)}) collective-permute-start(bf16[8,16,512]{2,1,0:T(8,128)(2,1)S(1)} %get-tuple-element.47), channel_id=1, source_target_pairs={{0,4},{4,8},{8,12},{12,16},{16,20},{20,24},{24,28},{1,5},{5,9},{9,... | collective-permute-start | bytes 393224 | tf_op jit(solution)/shard_map/ppermute | solution.py:24
  18.5 1.3 collective-permute-start.8
  23.3 4.6 %collective-permute-start.5 = (s32[2,2,8]{2,1,0:T(2,128)S(1)}, s32[2,2,8]{2,1,0:T(2,128)S(1)}, u32[]{:S(2)}, u32[]{:S(2)}) collective-permute-start(s32[2,2,8]{2,1,0:T(2,128)S(1)} %pad_add_fusion.2), channel_id=1, source_target_pairs={{0,8},{4,12},{8,0},{12,4},{16,24},{20,28},{24,16},{28,20},{1,9},{5... | collective-permute-start | bytes 392 | tf_op jit(solution)/shard_map/ppermute | solution.py:167
  27.9 1.6 collective-permute-done.5
  30.1 3.0 %collective-permute-done.6 = s32[4,2,8]{2,1,0:T(2,128)S(1)} collective-permute-done((s32[4,2,8]{2,1,0:T(2,128)S(1)}, s32[4,2,8]{2,1,0:T(2,128)S(1)}, u32[]{:S(2)}, u32[]{:S(2)}) %collective-permute-start.6) | collective-permute-done | bytes 288 | tf_op jit(solution)/shard_map/ppermute | solution.py:167
  35.2 1.1 fusion.105
  36.3 4.1 %all-to-all-start.1 = ((bf16[8,2,64,256]{3,2,1,0:T(8,128)(2,1)}), bf16[8,2,64,256]{3,2,1,0:T(8,128)(2,1)}, u32[]{:S(2)}, u32[]{:S(2)}) async-start(bf16[8,2,64,256]{3,2,1,0:T(8,128)(2,1)} %get-tuple-element.34), calls=%async_computation.1 | async-start | bytes 1048576 | tf_op jit(solution)/shard_map/all_to_all | solution.py:234
  40.6 1.3 collective-permute-start.2
  41.9 1.3 collective-permute-start.3
  43.3 1.3 collective-permute-start.10
  44.6 5.4 %collective-permute-start.9 = (bf16[32,8,512]{2,1,0:T(8,128)(2,1)S(1)}, bf16[32,8,512]{2,1,0:T(8,128)(2,1)S(1)}, u32[]{:S(2)}, u32[]{:S(2)}) collective-permute-start(bf16[32,8,512]{2,1,0:T(8,128)(2,1)S(1)} %get-tuple-element.41), channel_id=1, source_target_pairs={{0,1},{1,2},{2,3},{4,5},{5,6},{6,7},{8,9},{9,10},{10,11},{12,13},{... | collective-permute-start | bytes 786440 | tf_op jit(solution)/shard_map/ppermute | solution.py:24
  53.7 1.0 copy-done.18
  56.9 5.9 %all-to-all-start = ((bf16[8,2,64,256]{3,2,1,0:T(8,128)(2,1)}), bf16[8,2,64,256]{3,2,1,0:T(8,128)(2,1)}, u32[]{:S(2)}, u32[]{:S(2)}) async-start(bf16[8,2,64,256]{3,2,1,0:T(8,128)(2,1)} %get-tuple-element.33), calls=%async_computation | async-start | bytes 1048576 | tf_op jit(solution)/shard_map/all_to_all | solution.py:234
  65.7 1.6 gather_fusion.3
  67.3 11.0 %all-to-all-done = bf16[8,2,64,256]{3,2,1,0:T(8,128)(2,1)} async-done(((bf16[8,2,64,256]{3,2,1,0:T(8,128)(2,1)}), bf16[8,2,64,256]{3,2,1,0:T(8,128)(2,1)}, u32[]{:S(2)}, u32[]{:S(2)}) %all-to-all-start) | async-done | bytes 524320 | tf_op jit(solution)/shard_map/all_to_all | solution.py:234
  78.2 1.6 gather_fusion.2
  80.9 2.3 %slice_bitcast_fusion.1 = (bf16[2,2,88,2,8,128]{5,4,3,2,1,0:T(8,128)(2,1)S(1)}, bf16[2,2,88,2,8,128]{5,4,3,2,1,0:T(8,128)(2,1)S(1)}) fusion(bf16[2,2,704,512]{3,2,1,0:T(8,128)(2,1)} %constant_dynamic-update-slice_fusion), kind=kLoop, calls=%fused_computation.15 | loop fusion | bytes 5767168
  84.9 1.2 multiply_reduce_fusion
  86.1 3.0 %fusion.62 = bf16[2,2,64,2,128]{4,2,3,1,0:T(8,128)(2,1)} fusion(bf16[2,2,88,2,8,128]{5,4,3,2,1,0:T(8,128)(2,1)S(1)} %get-tuple-element.9, f32[2,2,2,64,704]{4,3,2,1,0:T(8,128)S(1)} %get-tuple-element.91, bf16[2,2,88,2,8,128]{5,4,3,2,1,0:T(8,128)(2,1)} %copy-done.1, f32[2,2,2,64]{3,2,1,0:T(2,128)S(1)} %bitcast.267, f32[2,2,2,64]{3,2,1,0:T(2,128)S(1)} %log_add_fusion, ...), kind=kOutput, calls=%fused_computation.51 | convolution fusion | flops 186122240 | bytes 4591616 | tf_op jit(solution)/shard_map/abhqk,abkhe->abqhe/dot_general | solution.py:108
  89.1 1.1 copy.122
  90.5 3.4 %collective-permute-start.11 = (f32[8,16,4]{1,0,2:T(8,128)S(1)}, f32[8,16,4]{1,0,2:T(8,128)S(1)}, u32[]{:S(2)}, u32[]{:S(2)}) collective-permute-start(f32[8,16,4]{1,0,2:T(8,128)S(1)} %slice.363), channel_id=1, source_target_pairs={{0,4},{4,8},{8,12},{12,16},{16,20},{20,24},{24,28},{1,5},{5,9},{9,... | collective-permute-start | bytes 6152 | tf_op jit(solution)/shard_map/ppermute | solution.py:24
  93.9 0.9 convolution_bitcast_fusion.2
  95.1 1.3 collective-permute-start.12
  96.7 4.0 %collective-permute-done.12 = f32[8,16,4]{1,0,2:T(8,128)S(1)} collective-permute-done((f32[8,16,4]{1,0,2:T(8,128)S(1)}, f32[8,16,4]{1,0,2:T(8,128)S(1)}, u32[]{:S(2)}, u32[]{:S(2)}) %collective-permute-start.12) | collective-permute-done | bytes 2080 | tf_op jit(solution)/shard_map/ppermute | solution.py:27
  100.8 1.3 collective-permute-start.13
  102.1 1.5 collective-permute-start.14
  103.6 0.9 fusion.116
  104.6 1.7 %collective-permute-done.14 = f32[32,8,4]{1,0,2:T(8,128)S(1)} collective-permute-done((f32[32,8,4]{1,0,2:T(8,128)S(1)}, f32[32,8,4]{1,0,2:T(8,128)S(1)}, u32[]{:S(2)}, u32[]{:S(2)}) %collective-permute-start.14) | collective-permute-done | bytes 4128 | tf_op jit(solution)/shard_map/ppermute | solution.py:27
  106.9 1.9 %fusion.9 = f32[2,2,2,576,64]{3,4,2,1,0:T(8,128)S(1)} fusion(f32[2,2,2,576]{3,2,1,0:T(2,128)S(1)} %concatenate.94, pred[2,2,576]{2,1,0:T(4,128)(4,1)S(1)} %copy-done.19, bf16[2,2,8,2,8,128]{5,4,3,2,1,0:T(8,128)(2,1)} %get-tuple-element.14, bf16[2,2,576,256]{3,2,1,0:T(8,128)(2,1)} %get-tuple-element.15), kind=kOutput, calls=%fused_computation.21 | convolution fusion | flops 76382208 | bytes 2511104 | tf_op jit(solution)/shard_map/abqhe,abkhe->abhqk/dot_general | solution.py:126
  109.8 2.7 %fusion.57 = bf16[2,2,64,2,128]{4,2,3,1,0:T(8,128)(2,1)} fusion(f32[2,2,2,576,64]{3,4,2,1,0:T(8,128)S(1)} %fusion.9, f32[2,2,2,576]{3,2,1,0:T(2,128)S(1)} %concatenate.96, bf16[2,2,8,2,8,128]{5,4,3,2,1,0:T(8,128)(2,1)S(1)} %copy-done.17, bf16[2,2,576,256]{3,2,1,0:T(8,128)(2,1)S(1)} %copy-done.4, bf16[2,2,576,256]{3,2,1,0:T(8,128)(2,1)} %get-tuple-element.15), kind=kOutput, calls=%fused_computation.50 | convolution fusion | flops 152010752 | bytes 3819520 | tf_op jit(solution)/shard_map/abhqk,abqhe->abkhe/dot_general | solution.py:135
  112.4 1.1 copy.134
  114.5 3.0 %collective-permute-start.15 = (f32[512,256]{1,0:T(8,128)S(1)}, f32[512,256]{1,0:T(8,128)S(1)}, u32[]{:S(2)}, u32[]{:S(2)}) collective-permute-start(f32[512,256]{1,0:T(8,128)S(1)} %constant_dynamic-slice_fusion.1), channel_id=1, source_target_pairs={{0,1},{1,0},{2,3},{3,2},{4,5},{5,4},{6,7},{7,6},{8,9},{9,8},{10,11... | collective-permute-start | bytes 1572872 | tf_op jit(solution)/shard_map/ppermute | solution.py:202
  117.5 1.5 collective-permute-done.15
  119.4 8.4 %collective-permute-done.16 = f32[256,256]{1,0:T(8,128)S(1)} collective-permute-done((f32[256,256]{1,0:T(8,128)S(1)}, f32[256,256]{1,0:T(8,128)S(1)}, u32[]{:S(2)}, u32[]{:S(2)}) %collective-permute-start.16) | collective-permute-done | bytes 262176 | tf_op jit(solution)/shard_map/ppermute | solution.py:202
  127.9 1.7 %collective-permute-start.17 = (f32[128,256]{1,0:T(8,128)S(1)}, f32[128,256]{1,0:T(8,128)S(1)}, u32[]{:S(2)}, u32[]{:S(2)}) collective-permute-start(f32[128,256]{1,0:T(8,128)S(1)} %constant_dynamic-slice_fusion.2), channel_id=1, source_target_pairs={{0,4},{4,0},{8,12},{12,8},{16,20},{20,16},{24,28},{28,24},{1,5},{5... | collective-permute-start | bytes 393224 | tf_op jit(solution)/shard_map/ppermute | solution.py:202
  129.6 3.3 %collective-permute-done.17 = f32[128,256]{1,0:T(8,128)S(1)} collective-permute-done((f32[128,256]{1,0:T(8,128)S(1)}, f32[128,256]{1,0:T(8,128)S(1)}, u32[]{:S(2)}, u32[]{:S(2)}) %collective-permute-start.17) | collective-permute-done | bytes 131104 | tf_op jit(solution)/shard_map/ppermute | solution.py:202
  133.5 4.4 %collective-permute-done.18 = f32[128,256]{1,0:T(8,128)S(1)} collective-permute-done((f32[128,256]{1,0:T(8,128)S(1)}, f32[128,256]{1,0:T(8,128)S(1)}, u32[]{:S(2)}, u32[]{:S(2)}) %collective-permute-start.18) | collective-permute-done | bytes 131104 | tf_op jit(solution)/shard_map/ppermute | solution.py:205
  138.0 1.0 collective-permute-start.19
  138.9 6.3 %collective-permute-done.19 = f32[128,256]{1,0:T(8,128)S(1)} collective-permute-done((f32[128,256]{1,0:T(8,128)S(1)}, f32[128,256]{1,0:T(8,128)S(1)}, u32[]{:S(2)}, u32[]{:S(2)}) %collective-permute-start.19) | collective-permute-done | bytes 131104 | tf_op jit(solution)/shard_map/ppermute | solution.py:205
  145.3 1.8 %collective-permute-start.20 = (f32[128,256]{1,0:T(8,128)S(1)}, f32[128,256]{1,0:T(8,128)S(1)}, u32[]{:S(2)}, u32[]{:S(2)}) collective-permute-start(f32[128,256]{1,0:T(8,128)S(1)} %add.139), channel_id=1, source_target_pairs={{0,4},{4,0},{8,12},{12,8},{16,20},{20,16},{24,28},{28,24},{1,5},{5... | collective-permute-start | bytes 393224 | tf_op jit(solution)/shard_map/ppermute | solution.py:167
  147.1 3.3 %collective-permute-done.20 = f32[128,256]{1,0:T(8,128)S(1)} collective-permute-done((f32[128,256]{1,0:T(8,128)S(1)}, f32[128,256]{1,0:T(8,128)S(1)}, u32[]{:S(2)}, u32[]{:S(2)}) %collective-permute-start.20) | collective-permute-done | bytes 131104 | tf_op jit(solution)/shard_map/ppermute | solution.py:167
  150.9 6.0 %collective-permute-done.21 = f32[256,256]{1,0:T(8,128)S(1)} collective-permute-done((f32[256,256]{1,0:T(8,128)S(1)}, f32[256,256]{1,0:T(8,128)S(1)}, u32[]{:S(2)}, u32[]{:S(2)}) %collective-permute-start.21) | collective-permute-done | bytes 262176 | tf_op jit(solution)/shard_map/ppermute | solution.py:167
  157.9 1.0 convolution_convert_fusion.1
  (195 shorter events, 27.1 us)
Async XLA Ops:
  0.6 33.8 %copy-start = (bf16[1,1,4,64,512]{4,3,2,1,0:T(8,128)(2,1)S(1)}, bf16[1,1,4,64,512]{4,3,2,1,0:T(8,128)(2,1)}, u32[]{:S(2)}) copy-start(bf16[1,1,4,64,512]{4,3,2,1,0:T(8,128)(2,1)} %param.17) | copy-start | bytes 786436
  0.6 19.3 %copy-start.20 = (s32[8]{0:T(128)S(1)}, s32[8]{0:T(128)}, u32[]{:S(2)}) copy-start(s32[8]{0:T(128)} %constant.163) | copy-start | bytes 100
  0.7 13.1 %copy-start.11 = (bf16[16,16,256]{2,1,0:T(8,128)(2,1)S(1)}, bf16[16,16,256]{2,1,0:T(8,128)(2,1)}, u32[]{:S(2)}) copy-start(bf16[16,16,256]{2,1,0:T(8,128)(2,1)} %param.20) | copy-start | bytes 393220
  0.7 13.1 %copy-start.7 = (bf16[256,256]{1,0:T(8,128)(2,1)S(1)}, bf16[256,256]{1,0:T(8,128)(2,1)}, u32[]{:S(2)}) copy-start(bf16[256,256]{1,0:T(8,128)(2,1)} %param.16) | copy-start | bytes 393220
  2.4 20.8 %collective-permute-start.4 = (s32[1,2,8]{2,1,0:T(2,128)S(1)}, s32[1,2,8]{2,1,0:T(2,128)S(1)}, u32[]{:S(2)}, u32[]{:S(2)}) collective-permute-start(s32[1,2,8]{2,1,0:T(2,128)S(1)} %add_bitcast_fusion), channel_id=1, source_target_pairs={{0,16},{4,20},{8,24},{12,28},{16,0},{20,4},{24,8},{28,12},{1,17},{... | collective-permute-start | bytes 200 | tf_op jit(solution)/shard_map/ppermute | solution.py:167
  7.8 32.6 %collective-permute-start = (bf16[8,16,512]{2,1,0:T(8,128)(2,1)S(1)}, bf16[8,16,512]{2,1,0:T(8,128)(2,1)S(1)}, u32[]{:S(2)}, u32[]{:S(2)}) collective-permute-start(bf16[8,16,512]{2,1,0:T(8,128)(2,1)S(1)} %bitcast.266), channel_id=1, source_target_pairs={{0,4},{4,8},{8,12},{12,16},{16,20},{20,24},{24,28},{1,5},{5,9},{9,... | collective-permute-start | bytes 393224 | tf_op jit(solution)/shard_map/ppermute | solution.py:24
  11.2 29.2 %collective-permute-start.1 = (bf16[8,16,512]{2,1,0:T(8,128)(2,1)S(1)}, bf16[8,16,512]{2,1,0:T(8,128)(2,1)S(1)}, u32[]{:S(2)}, u32[]{:S(2)}) collective-permute-start(bf16[8,16,512]{2,1,0:T(8,128)(2,1)S(1)} %bitcast.265), channel_id=1, source_target_pairs={{4,0},{8,4},{12,8},{16,12},{20,16},{24,20},{28,24},{5,1},{9,5},{13... | collective-permute-start | bytes 393224 | tf_op jit(solution)/shard_map/ppermute | solution.py:27
  14.0 29.2 %collective-permute-start.7 = (bf16[8,16,512]{2,1,0:T(8,128)(2,1)S(1)}, bf16[8,16,512]{2,1,0:T(8,128)(2,1)S(1)}, u32[]{:S(2)}, u32[]{:S(2)}) collective-permute-start(bf16[8,16,512]{2,1,0:T(8,128)(2,1)S(1)} %get-tuple-element.47), channel_id=1, source_target_pairs={{0,4},{4,8},{8,12},{12,16},{16,20},{20,24},{24,28},{1,5},{5,9},{9,... | collective-permute-start | bytes 393224 | tf_op jit(solution)/shard_map/ppermute | solution.py:24
  18.5 24.7 %collective-permute-start.8 = (bf16[8,16,512]{2,1,0:T(8,128)(2,1)S(1)}, bf16[8,16,512]{2,1,0:T(8,128)(2,1)S(1)}, u32[]{:S(2)}, u32[]{:S(2)}) collective-permute-start(bf16[8,16,512]{2,1,0:T(8,128)(2,1)S(1)} %get-tuple-element.48), channel_id=1, source_target_pairs={{4,0},{8,4},{12,8},{16,12},{20,16},{24,20},{28,24},{5,1},{9,5},{13... | collective-permute-start | bytes 393224 | tf_op jit(solution)/shard_map/ppermute | solution.py:27
  23.3 6.1 %collective-permute-start.5 = (s32[2,2,8]{2,1,0:T(2,128)S(1)}, s32[2,2,8]{2,1,0:T(2,128)S(1)}, u32[]{:S(2)}, u32[]{:S(2)}) collective-permute-start(s32[2,2,8]{2,1,0:T(2,128)S(1)} %pad_add_fusion.2), channel_id=1, source_target_pairs={{0,8},{4,12},{8,0},{12,4},{16,24},{20,28},{24,16},{28,20},{1,9},{5... | collective-permute-start | bytes 392 | tf_op jit(solution)/shard_map/ppermute | solution.py:167
  29.5 3.7 %collective-permute-start.6 = (s32[4,2,8]{2,1,0:T(2,128)S(1)}, s32[4,2,8]{2,1,0:T(2,128)S(1)}, u32[]{:S(2)}, u32[]{:S(2)}) collective-permute-start(s32[4,2,8]{2,1,0:T(2,128)S(1)} %pad_add_fusion.1), channel_id=1, source_target_pairs={{0,4},{4,0},{8,12},{12,8},{16,20},{20,16},{24,28},{28,24},{1,5},{5... | collective-permute-start | bytes 776 | tf_op jit(solution)/shard_map/ppermute | solution.py:167
  36.3 20.6 %all-to-all-start.1 = ((bf16[8,2,64,256]{3,2,1,0:T(8,128)(2,1)}), bf16[8,2,64,256]{3,2,1,0:T(8,128)(2,1)}, u32[]{:S(2)}, u32[]{:S(2)}) async-start(bf16[8,2,64,256]{3,2,1,0:T(8,128)(2,1)} %get-tuple-element.34), calls=%async_computation.1 | async-start | bytes 1048576 | tf_op jit(solution)/shard_map/all_to_all | solution.py:234
  40.6 9.5 %collective-permute-start.2 = (bf16[32,8,512]{2,1,0:T(8,128)(2,1)S(1)}, bf16[32,8,512]{2,1,0:T(8,128)(2,1)S(1)}, u32[]{:S(2)}, u32[]{:S(2)}) collective-permute-start(bf16[32,8,512]{2,1,0:T(8,128)(2,1)S(1)} %get-tuple-element.43), channel_id=1, source_target_pairs={{0,1},{1,2},{2,3},{4,5},{5,6},{6,7},{8,9},{9,10},{10,11},{12,13},{... | collective-permute-start | bytes 786440 | tf_op jit(solution)/shard_map/ppermute | solution.py:24
  41.9 8.2 %collective-permute-start.3 = (bf16[32,8,512]{2,1,0:T(8,128)(2,1)S(1)}, bf16[32,8,512]{2,1,0:T(8,128)(2,1)S(1)}, u32[]{:S(2)}, u32[]{:S(2)}) collective-permute-start(bf16[32,8,512]{2,1,0:T(8,128)(2,1)S(1)} %get-tuple-element.44), channel_id=1, source_target_pairs={{1,0},{2,1},{3,2},{5,4},{6,5},{7,6},{9,8},{10,9},{11,10},{13,12},{... | collective-permute-start | bytes 786440 | tf_op jit(solution)/shard_map/ppermute | solution.py:27
  43.3 9.9 %collective-permute-start.10 = (bf16[32,8,512]{2,1,0:T(8,128)(2,1)S(1)}, bf16[32,8,512]{2,1,0:T(8,128)(2,1)S(1)}, u32[]{:S(2)}, u32[]{:S(2)}) collective-permute-start(bf16[32,8,512]{2,1,0:T(8,128)(2,1)S(1)} %get-tuple-element.42), channel_id=1, source_target_pairs={{1,0},{2,1},{3,2},{5,4},{6,5},{7,6},{9,8},{10,9},{11,10},{13,12},{... | collective-permute-start | bytes 786440 | tf_op jit(solution)/shard_map/ppermute | solution.py:27
  44.6 8.6 %collective-permute-start.9 = (bf16[32,8,512]{2,1,0:T(8,128)(2,1)S(1)}, bf16[32,8,512]{2,1,0:T(8,128)(2,1)S(1)}, u32[]{:S(2)}, u32[]{:S(2)}) collective-permute-start(bf16[32,8,512]{2,1,0:T(8,128)(2,1)S(1)} %get-tuple-element.41), channel_id=1, source_target_pairs={{0,1},{1,2},{2,3},{4,5},{5,6},{6,7},{8,9},{9,10},{10,11},{12,13},{... | collective-permute-start | bytes 786440 | tf_op jit(solution)/shard_map/ppermute | solution.py:24
  53.7 1.1 copy-start.18
  56.9 21.3 %all-to-all-start = ((bf16[8,2,64,256]{3,2,1,0:T(8,128)(2,1)}), bf16[8,2,64,256]{3,2,1,0:T(8,128)(2,1)}, u32[]{:S(2)}, u32[]{:S(2)}) async-start(bf16[8,2,64,256]{3,2,1,0:T(8,128)(2,1)} %get-tuple-element.33), calls=%async_computation | async-start | bytes 1048576 | tf_op jit(solution)/shard_map/all_to_all | solution.py:234
  63.5 16.5 %copy-start.3 = (bf16[2,2,576,256]{3,2,1,0:T(8,128)(2,1)}, bf16[2,2,576,256]{3,2,1,0:T(8,128)(2,1)S(1)}, u32[]{:S(2)}) copy-start(bf16[2,2,576,256]{3,2,1,0:T(8,128)(2,1)S(1)} %get-tuple-element.16) | copy-start | bytes 3538948
  80.9 2.3 %copy-start.13 = (bf16[2,2,64,2,128]{4,3,2,1,0:T(2,128)(2,1)S(1)}, bf16[2,2,64,2,128]{4,3,2,1,0:T(2,128)(2,1)}, u32[]{:S(2)}) copy-start(bf16[2,2,64,2,128]{4,3,2,1,0:T(2,128)(2,1)} %reshape_reshape.32) | copy-start | bytes 393220
  83.2 1.3 copy-start.1
  84.0 0.9 copy-start.9
  86.1 7.8 %copy-start.2 = (bf16[16,16,256]{2,1,0:T(8,128)(2,1)S(1)}, bf16[16,16,256]{2,1,0:T(8,128)(2,1)}, u32[]{:S(2)}) copy-start(bf16[16,16,256]{2,1,0:T(8,128)(2,1)} %param.12) | copy-start | bytes 393220
  89.1 7.3 %copy-start.10 = (bf16[2,2,64,2,128]{4,2,3,1,0:T(8,128)(2,1)S(1)}, bf16[2,2,64,2,128]{4,2,3,1,0:T(8,128)(2,1)}, u32[]{:S(2)}) copy-start(bf16[2,2,64,2,128]{4,2,3,1,0:T(8,128)(2,1)} %get-tuple-element.93) | copy-start | bytes 393220
  90.2 13.4 %copy-start.12 = (bf16[16,16,256]{2,1,0:T(8,128)(2,1)S(1)}, bf16[16,16,256]{2,1,0:T(8,128)(2,1)}, u32[]{:S(2)}) copy-start(bf16[16,16,256]{2,1,0:T(8,128)(2,1)} %param.20) | copy-start | bytes 393220
  90.5 6.2 %collective-permute-start.11 = (f32[8,16,4]{1,0,2:T(8,128)S(1)}, f32[8,16,4]{1,0,2:T(8,128)S(1)}, u32[]{:S(2)}, u32[]{:S(2)}) collective-permute-start(f32[8,16,4]{1,0,2:T(8,128)S(1)} %slice.363), channel_id=1, source_target_pairs={{0,4},{4,8},{8,12},{12,16},{16,20},{20,24},{24,28},{1,5},{5,9},{9,... | collective-permute-start | bytes 6152 | tf_op jit(solution)/shard_map/ppermute | solution.py:24
  95.1 5.6 %collective-permute-start.12 = (f32[8,16,4]{1,0,2:T(8,128)S(1)}, f32[8,16,4]{1,0,2:T(8,128)S(1)}, u32[]{:S(2)}, u32[]{:S(2)}) collective-permute-start(f32[8,16,4]{1,0,2:T(8,128)S(1)} %slice.365), channel_id=1, source_target_pairs={{4,0},{8,4},{12,8},{16,12},{20,16},{24,20},{28,24},{5,1},{9,5},{13... | collective-permute-start | bytes 6152 | tf_op jit(solution)/shard_map/ppermute | solution.py:27
  96.7 10.2 %copy-start.19 = (pred[2,2,576]{2,1,0:T(4,128)(4,1)S(1)}, pred[2,2,576]{2,1,0:T(4,128)(4,1)}, u32[]{:S(2)}) copy-start(pred[2,2,576]{2,1,0:T(4,128)(4,1)} %concatenate.90) | copy-start | bytes 6916
  100.8 3.7 %collective-permute-start.13 = (f32[32,8,4]{1,0,2:T(8,128)S(1)}, f32[32,8,4]{1,0,2:T(8,128)S(1)}, u32[]{:S(2)}, u32[]{:S(2)}) collective-permute-start(f32[32,8,4]{1,0,2:T(8,128)S(1)} %get-tuple-element.51), channel_id=1, source_target_pairs={{0,1},{1,2},{2,3},{4,5},{5,6},{6,7},{8,9},{9,10},{10,11},{12,13},{... | collective-permute-start | bytes 12296 | tf_op jit(solution)/shard_map/ppermute | solution.py:24
  102.1 4.2 %collective-permute-start.14 = (f32[32,8,4]{1,0,2:T(8,128)S(1)}, f32[32,8,4]{1,0,2:T(8,128)S(1)}, u32[]{:S(2)}, u32[]{:S(2)}) collective-permute-start(f32[32,8,4]{1,0,2:T(8,128)S(1)} %get-tuple-element.52), channel_id=1, source_target_pairs={{1,0},{2,1},{3,2},{5,4},{6,5},{7,6},{9,8},{10,9},{11,10},{13,12},{... | collective-permute-start | bytes 12296 | tf_op jit(solution)/shard_map/ppermute | solution.py:27
  106.9 1.9 %copy-start.4 = (bf16[2,2,576,256]{3,2,1,0:T(8,128)(2,1)S(1)}, bf16[2,2,576,256]{3,2,1,0:T(8,128)(2,1)}, u32[]{:S(2)}) copy-start(bf16[2,2,576,256]{3,2,1,0:T(8,128)(2,1)} %copy-done.3) | copy-start | bytes 3538948
  108.8 0.9 copy-start.17
  112.4 1.9 %copy-start.5 = (f32[256,256]{1,0:T(8,128)S(1)}, f32[256,256]{1,0:T(8,128)}, u32[]{:S(2)}) copy-start(f32[256,256]{1,0:T(8,128)} %convolution_bitcast_fusion.2) | copy-start | bytes 786436
  112.4 2.0 %copy-start.6 = (f32[256,256]{1,0:T(8,128)S(1)}, f32[256,256]{1,0:T(8,128)}, u32[]{:S(2)}) copy-start(f32[256,256]{1,0:T(8,128)} %fusion.116) | copy-start | bytes 786436
  114.5 4.5 %collective-permute-start.15 = (f32[512,256]{1,0:T(8,128)S(1)}, f32[512,256]{1,0:T(8,128)S(1)}, u32[]{:S(2)}, u32[]{:S(2)}) collective-permute-start(f32[512,256]{1,0:T(8,128)S(1)} %constant_dynamic-slice_fusion.1), channel_id=1, source_target_pairs={{0,1},{1,0},{2,3},{3,2},{4,5},{5,4},{6,7},{7,6},{8,9},{9,8},{10,11... | collective-permute-start | bytes 1572872 | tf_op jit(solution)/shard_map/ppermute | solution.py:202
  119.2 8.7 %collective-permute-start.16 = (f32[256,256]{1,0:T(8,128)S(1)}, f32[256,256]{1,0:T(8,128)S(1)}, u32[]{:S(2)}, u32[]{:S(2)}) collective-permute-start(f32[256,256]{1,0:T(8,128)S(1)} %constant_dynamic-slice_fusion), channel_id=1, source_target_pairs={{0,2},{1,3},{2,0},{3,1},{4,6},{5,7},{6,4},{7,5},{8,10},{9,11},{10,... | collective-permute-start | bytes 786440 | tf_op jit(solution)/shard_map/ppermute | solution.py:202
  127.9 5.0 %collective-permute-start.17 = (f32[128,256]{1,0:T(8,128)S(1)}, f32[128,256]{1,0:T(8,128)S(1)}, u32[]{:S(2)}, u32[]{:S(2)}) collective-permute-start(f32[128,256]{1,0:T(8,128)S(1)} %constant_dynamic-slice_fusion.2), channel_id=1, source_target_pairs={{0,4},{4,0},{8,12},{12,8},{16,20},{20,16},{24,28},{28,24},{1,5},{5... | collective-permute-start | bytes 393224 | tf_op jit(solution)/shard_map/ppermute | solution.py:202
  132.9 5.0 %collective-permute-start.18 = (f32[128,256]{1,0:T(8,128)S(1)}, f32[128,256]{1,0:T(8,128)S(1)}, u32[]{:S(2)}, u32[]{:S(2)}) collective-permute-start(f32[128,256]{1,0:T(8,128)S(1)} %dynamic-slice_add_fusion.2), channel_id=1, source_target_pairs={{0,8},{4,12},{8,0},{12,4},{16,24},{20,28},{24,16},{28,20},{1,9},{5... | collective-permute-start | bytes 393224 | tf_op jit(solution)/shard_map/ppermute | solution.py:205
  138.0 7.3 %collective-permute-start.19 = (f32[128,256]{1,0:T(8,128)S(1)}, f32[128,256]{1,0:T(8,128)S(1)}, u32[]{:S(2)}, u32[]{:S(2)}) collective-permute-start(f32[128,256]{1,0:T(8,128)S(1)} %add.138), channel_id=1, source_target_pairs={{0,16},{4,20},{8,24},{12,28},{16,0},{20,4},{24,8},{28,12},{1,17},{... | collective-permute-start | bytes 393224 | tf_op jit(solution)/shard_map/ppermute | solution.py:205
  145.3 5.0 %collective-permute-start.20 = (f32[128,256]{1,0:T(8,128)S(1)}, f32[128,256]{1,0:T(8,128)S(1)}, u32[]{:S(2)}, u32[]{:S(2)}) collective-permute-start(f32[128,256]{1,0:T(8,128)S(1)} %add.139), channel_id=1, source_target_pairs={{0,4},{4,0},{8,12},{12,8},{16,20},{20,16},{24,28},{28,24},{1,5},{5... | collective-permute-start | bytes 393224 | tf_op jit(solution)/shard_map/ppermute | solution.py:167
  150.3 6.7 %copy-start.8 = (bf16[256,256]{1,0:T(8,128)(2,1)S(1)}, bf16[256,256]{1,0:T(8,128)(2,1)}, u32[]{:S(2)}) copy-start(bf16[256,256]{1,0:T(8,128)(2,1)} %param.16) | copy-start | bytes 393220
  150.4 7.5 %copy-start.14 = (bf16[256,256]{1,0:T(8,128)(2,1)S(1)}, bf16[256,256]{1,0:T(8,128)(2,1)}, u32[]{:S(2)}) copy-start(bf16[256,256]{1,0:T(8,128)(2,1)} %param.15) | copy-start | bytes 393220
  150.4 7.5 %copy-start.15 = (bf16[256,256]{1,0:T(8,128)(2,1)S(1)}, bf16[256,256]{1,0:T(8,128)(2,1)}, u32[]{:S(2)}) copy-start(bf16[256,256]{1,0:T(8,128)(2,1)} %param.14) | copy-start | bytes 393220
  150.4 7.5 %copy-start.16 = (bf16[256,256]{1,0:T(8,128)(2,1)S(1)}, bf16[256,256]{1,0:T(8,128)(2,1)}, u32[]{:S(2)}) copy-start(bf16[256,256]{1,0:T(8,128)(2,1)} %param.13) | copy-start | bytes 393220
  150.4 6.4 %collective-permute-start.21 = (f32[256,256]{1,0:T(8,128)S(1)}, f32[256,256]{1,0:T(8,128)S(1)}, u32[]{:S(2)}, u32[]{:S(2)}) collective-permute-start(f32[256,256]{1,0:T(8,128)S(1)} %pad_maximum_fusion.7), channel_id=1, source_target_pairs={{0,2},{1,3},{2,0},{3,1},{4,6},{5,7},{6,4},{7,5},{8,10},{9,11},{10,... | collective-permute-start | bytes 786440 | tf_op jit(solution)/shard_map/ppermute | solution.py:167
  156.9 2.0 %collective-permute-start.22 = (f32[512,256]{1,0:T(8,128)S(1)}, f32[512,256]{1,0:T(8,128)S(1)}, u32[]{:S(2)}, u32[]{:S(2)}) collective-permute-start(f32[512,256]{1,0:T(8,128)S(1)} %pad_maximum_fusion.6), channel_id=1, source_target_pairs={{0,1},{1,0},{2,3},{3,2},{4,5},{5,4},{6,7},{7,6},{8,9},{9,8},{10,11... | collective-permute-start | bytes 1572872 | tf_op jit(solution)/shard_map/ppermute | solution.py:167

commit v15 on v11

--- a/solution.py
+++ b/solution.py
@@ -65,30 +65,50 @@
     block_rows, block_cols = (region_keyval.shape[0], region_keyval.shape[1])
     keyvals, valid = neighbour_set(keyval_pad, key_valid, block_rows, block_cols, 2)
     merged = region_keyval.reshape(block_rows, block_cols, 2 * BT, 2 * D)
-    keyvals = jnp.concatenate([keyvals, merged], 2)
-    valid = jnp.concatenate([valid, jnp.ones((block_rows, block_cols, 2 * BT), jnp.bool_)], 2)
-    return keyvals[..., :D], keyvals[..., D:], valid
-
-
-def set_scores(query_heads, key_part, valid):
-    scores = jnp.einsum(
-        "abqhe,abkhe->abhqk", query_heads, split_heads(key_part), preferred_element_type=jnp.float32
-    )
-    scores = scores * (1.0 / math.sqrt(HEAD_DIM))
-    return jnp.where(valid[:, :, None, None, :], scores, masked_score)
+    return (keyvals[..., :D], keyvals[..., D:], valid), (merged[..., :D], merged[..., D:])
+
+
+def set_scores(query_heads, near, region):
+    near_keys, _, valid = near
+    near_scores = jnp.einsum(
+        "abqhe,abkhe->abhqk", query_heads, split_heads(near_keys), preferred_element_type=jnp.float32
+    )
+    near_scores = jnp.where(
+        valid[:, :, None, None, :], near_scores * (1.0 / math.sqrt(HEAD_DIM)), masked_score
+    )
+    region_scores = jnp.einsum(
+        "abqhe,abkhe->abhqk", query_heads, split_heads(region[0]), preferred_element_type=jnp.float32
+    )
+    region_scores = region_scores * (1.0 / math.sqrt(HEAD_DIM))
+    return jnp.concatenate([near_scores, region_scores], -1)
+
+
+def set_sum(weights, near_part, region_part):
+    split = near_part.shape[2]
+    near_sum = jnp.einsum(
+        "abhqk,abkhe->abqhe",
+        weights[..., :split],
+        split_heads(near_part),
+        preferred_element_type=jnp.float32,
+    )
+    region_sum = jnp.einsum(
+        "abhqk,abkhe->abqhe",
+        weights[..., split:],
+        split_heads(region_part),
+        preferred_element_type=jnp.float32,
+    )
+    return near_sum + region_sum
 
 
 def attend_forward(query_blocks, keyval_pad, key_valid, region_keyval):
     query_heads = split_heads(query_blocks)
-    key_part, value_part, valid = key_set(keyval_pad, key_valid, region_keyval)
-    scores = set_scores(query_heads, key_part, valid)
+    near, region = key_set(keyval_pad, key_valid, region_keyval)
+    scores = set_scores(query_heads, near, region)
     row_top = jnp.max(scores, -1, keepdims=True)
     row_total = jnp.sum(jnp.exp(scores - row_top), -1, keepdims=True)
     log_total = row_top + jnp.log(row_total)
     weights = jnp.exp(scores - log_total).astype(jnp.bfloat16)
-    mixed_sum = jnp.einsum(
-        "abhqk,abkhe->abqhe", weights, split_heads(value_part), preferred_element_type=jnp.float32
-    )
+    mixed_sum = set_sum(weights, near[1], region[1])
     output = mixed_sum.reshape(query_blocks.shape).astype(jnp.bfloat16)
     return (output, log_total[..., 0])
 
@@ -98,16 +118,23 @@
 ):
     query_heads = split_heads(query_blocks)
     dout_heads = split_heads(dout_blocks)
-    key_part, value_part, valid = key_set(keyval_pad, key_valid, region_keyval)
-    scores = set_scores(query_heads, key_part, valid)
+    near, region = key_set(keyval_pad, key_valid, region_keyval)
+    scores = set_scores(query_heads, near, region)
     prob = jnp.exp(scores - log_total[..., None])
-    grad_prob = jnp.einsum(
-        "abqhe,abkhe->abhqk", dout_heads, split_heads(value_part), preferred_element_type=jnp.float32
+    grad_prob = jnp.concatenate(
+        [
+            jnp.einsum(
+                "abqhe,abkhe->abhqk",
+                dout_heads,
+                split_heads(part),
+                preferred_element_type=jnp.float32,
+            )
+            for part in (near[1], region[1])
+        ],
+        -1,
     )
     grad_score = (prob * (grad_prob - delta_rows[..., None])).astype(jnp.bfloat16)
-    accum_sum = jnp.einsum(
-        "abhqk,abkhe->abqhe", grad_score, split_heads(key_part), preferred_element_type=jnp.float32
-    )
+    accum_sum = set_sum(grad_score, near[0], region[0])
     return (
         (accum_sum * (1.0 / math.sqrt(HEAD_DIM))).reshape(query_blocks.shape).astype(jnp.bfloat16)
     )

time: 145 us -> 150 us (1.034)
  waiting for transfers between devices: 48 us -> 53 us
  local copies, waits for them, and re-layouts: 23.4 us -> 21.4 us
  other arithmetic: 4.22 us -> 5.84 us
  starting transfers between devices: 50.2 us -> 48.6 us
    unnamed x70 -> x75, local copies, waits for them, and re-layouts: 12 us -> 5.36 us
    all_to_all x1, waiting for transfers between devices: 5 us -> 8.32 us  [fetch_regions(): received = lax.all_to_all(sent, axis, 0, 0, tiled=True)]
    slice x0 -> x3, local copies, waits for them, and re-layouts: none -> 2.7 us  [the longest x1 1.79 us: key_set(): merged[..., D:]]
    ppermute x2, starting transfers between devices: 3.42 us -> 1.57 us  [tree_sum(): joined = joined + lax.ppermute(joined, axis, pairs)]
    dot_general x3 -> x8, matrix products: 5.01 us -> 6.83 us  [the longest x2 2.47 us: set_sum(): jnp.einsum('abhqk,abkhe->abqhe', weights[..., :split], split_heads(near_p...]
    convert_element_type x0 -> x2, other arithmetic: none -> 1.79 us  [the longest x1 1.23 us: attend_forward(): weights = jnp.exp(scores - log_total).astype(jnp.bfloat16)]
  transfers between devices with their start and end apart: 24 -> 24, of which waited for: 13 -> 13; matrix products, arithmetic and copies ran while one was open for 15% -> 10% of each run, Pallas kernels for 0% -> 0%
where the time goes in v15:
time: 150 us; the launch traced here: 149 us
  waiting for transfers between devices  53 us (35%)
  starting transfers between devices  48.6 us (32%)
  local copies, waits for them, and re-layouts  21.4 us (14%)
  matrix products  18 us (12%)
  other arithmetic  5.84 us (4%)
  between operations  1.94 us (1%)
    ppermute x6, starting transfers between devices, padded(): lax.ppermute(lax.slice_in_dim(block, block.shape[dim] - width, None, axis...  18.5 us
    ppermute x3, waiting for transfers between devices, tree_sum(): joined = keep + lax.ppermute(send, axis, pairs)  13.9 us
    ppermute x6, waiting for transfers between devices, doubling_gather(): got = lax.ppermute(joined, axis, pairs)  13.3 us
    ppermute x6, starting transfers between devices, doubling_gather(): got = lax.ppermute(joined, axis, pairs)  12 us
    ppermute x2, waiting for transfers between devices, tree_sum(): joined = joined + lax.ppermute(joined, axis, pairs)  10.2 us
    all_to_all x1, waiting for transfers between devices, fetch_regions(): received = lax.all_to_all(sent, axis, 0, 0, tiled=True)  8.32 us
    ppermute x6, starting transfers between devices, padded(): lax.ppermute(lax.slice_in_dim(block, 0, width, axis=dim), axis, backward)  7.92 us
    ppermute x6, waiting for transfers between devices, padded(): lax.ppermute(lax.slice_in_dim(block, 0, width, axis=dim), axis, backward)  7.2 us
  transfers between devices with their start and end apart: 24, of which 13 were waited for; matrix products, arithmetic and copies ran while one was open for 10% of the time, Pallas kernels for 0%

profile of v15, /device:TPU:0, one launch (start us, length us, event | category | flops | bytes accessed | tf_op | source)
XLA Modules:
  0.0 148.8 jit_solution(1582311010196036988)
XLA Ops:
  0.7 1.3 convolution_convert_fusion
  2.0 4.9 %collective-permute-start = (bf16[8,16,512]{2,1,0:T(8,128)(2,1)S(1)}, bf16[8,16,512]{2,1,0:T(8,128)(2,1)S(1)}, u32[]{:S(2)}, u32[]{:S(2)}) collective-permute-start(bf16[8,16,512]{2,1,0:T(8,128)(2,1)S(1)} %bitcast.279), channel_id=1, source_target_pairs={{0,4},{4,8},{8,12},{12,16},{16,20},{20,24},{24,28},{1,5},{5,9},{9,... | collective-permute-start | bytes 393224 | tf_op jit(solution)/shard_map/ppermute | solution.py:24
  6.9 1.3 collective-permute-start.1
  9.9 4.7 %collective-permute-start.4 = (s32[1,2,8]{2,1,0:T(2,128)S(1)}, s32[1,2,8]{2,1,0:T(2,128)S(1)}, u32[]{:S(2)}, u32[]{:S(2)}) collective-permute-start(s32[1,2,8]{2,1,0:T(2,128)S(1)} %add_bitcast_fusion), channel_id=1, source_target_pairs={{0,16},{4,20},{8,24},{12,28},{16,0},{20,4},{24,8},{28,12},{1,17},{... | collective-permute-start | bytes 200 | tf_op jit(solution)/shard_map/ppermute | solution.py:194
  14.6 1.1 convolution_convert_fusion.4
  16.0 2.5 %collective-permute-start.7 = (bf16[8,16,512]{2,1,0:T(8,128)(2,1)S(1)}, bf16[8,16,512]{2,1,0:T(8,128)(2,1)S(1)}, u32[]{:S(2)}, u32[]{:S(2)}) collective-permute-start(bf16[8,16,512]{2,1,0:T(8,128)(2,1)S(1)} %get-tuple-element.44), channel_id=1, source_target_pairs={{0,4},{4,8},{8,12},{12,16},{16,20},{20,24},{24,28},{1,5},{5,9},{9,... | collective-permute-start | bytes 393224 | tf_op jit(solution)/shard_map/ppermute | solution.py:24
  18.5 1.3 collective-permute-start.8
  21.9 4.6 %collective-permute-start.5 = (s32[2,2,8]{2,1,0:T(2,128)S(1)}, s32[2,2,8]{2,1,0:T(2,128)S(1)}, u32[]{:S(2)}, u32[]{:S(2)}) collective-permute-start(s32[2,2,8]{2,1,0:T(2,128)S(1)} %pad_add_fusion.2), channel_id=1, source_target_pairs={{0,8},{4,12},{8,0},{12,4},{16,24},{20,28},{24,16},{28,20},{1,9},{5... | collective-permute-start | bytes 392 | tf_op jit(solution)/shard_map/ppermute | solution.py:194
  26.5 1.6 %collective-permute-done.5 = s32[2,2,8]{2,1,0:T(2,128)S(1)} collective-permute-done((s32[2,2,8]{2,1,0:T(2,128)S(1)}, s32[2,2,8]{2,1,0:T(2,128)S(1)}, u32[]{:S(2)}, u32[]{:S(2)}) %collective-permute-start.5) | collective-permute-done | bytes 160 | tf_op jit(solution)/shard_map/ppermute | solution.py:194
  29.5 2.3 %collective-permute-done.6 = s32[4,2,8]{2,1,0:T(2,128)S(1)} collective-permute-done((s32[4,2,8]{2,1,0:T(2,128)S(1)}, s32[4,2,8]{2,1,0:T(2,128)S(1)}, u32[]{:S(2)}, u32[]{:S(2)}) %collective-permute-start.6) | collective-permute-done | bytes 288 | tf_op jit(solution)/shard_map/ppermute | solution.py:194
  33.7 1.1 broadcast_select_fusion
  34.8 4.3 %all-to-all-start = ((bf16[8,2,64,512]{3,2,1,0:T(8,128)(2,1)}), bf16[8,2,64,512]{3,2,1,0:T(8,128)(2,1)}, u32[]{:S(2)}, u32[]{:S(2)}) async-start(bf16[8,2,64,512]{3,2,1,0:T(8,128)(2,1)} %broadcast_select_fusion), calls=%async_computation | async-start | bytes 2097152 | tf_op jit(solution)/shard_map/all_to_all | solution.py:256
  39.2 1.3 collective-permute-start.2
  40.5 1.3 collective-permute-start.3
  41.9 1.3 collective-permute-start.10
  43.2 5.4 %collective-permute-start.9 = (bf16[32,8,512]{2,1,0:T(8,128)(2,1)S(1)}, bf16[32,8,512]{2,1,0:T(8,128)(2,1)S(1)}, u32[]{:S(2)}, u32[]{:S(2)}) collective-permute-start(bf16[32,8,512]{2,1,0:T(8,128)(2,1)S(1)} %get-tuple-element.36), channel_id=1, source_target_pairs={{0,1},{1,2},{2,3},{4,5},{5,6},{6,7},{8,9},{9,10},{10,11},{12,13},{... | collective-permute-start | bytes 786440 | tf_op jit(solution)/shard_map/ppermute | solution.py:24
  50.3 0.9 copy-done.6
  53.8 8.3 %all-to-all-done = bf16[8,2,64,512]{3,2,1,0:T(8,128)(2,1)} async-done(((bf16[8,2,64,512]{3,2,1,0:T(8,128)(2,1)}), bf16[8,2,64,512]{3,2,1,0:T(8,128)(2,1)}, u32[]{:S(2)}, u32[]{:S(2)}) %all-to-all-start) | async-done | bytes 1048608 | tf_op jit(solution)/shard_map/all_to_all | solution.py:256
  62.2 1.8 %gather_fusion.2 = bf16[8,64,512]{2,1,0:T(8,128)(2,1)S(1)} fusion(bf16[16,64,512]{2,1,0:T(8,128)(2,1)} %bitcast.15, s32[1024]{0:T(1024)S(1)} %pad_clamp_fusion), kind=kCustom, calls=%fused_computation.2 | custom fusion | bytes 1048608 | tf_op jit(solution)/shard_map/jit(_take)/gather | solution.py:260
  66.6 1.2 fusion.7
  67.8 1.8 %copy.157 = bf16[2,2,128,256]{2,3,1,0:T(8,128)(2,1)} copy(bf16[2,2,128,256]{3,2,1,0:T(8,128)(2,1)} %get-tuple-element.41) | data formatting | bytes 524288 | tf_op jit(solution)/shard_map/slice | solution.py:68
  69.6 1.2 fusion.104
  70.8 1.4 fusion.100
  72.2 2.1 %multiply_reduce_fusion = (f32[2,2,64,2]{2,3,1,0:T(2,128)S(1)}, bf16[2,2,64,2,128]{4,2,3,1,0:T(8,128)(2,1)}) fusion(bf16[2,2,64,2,128]{4,3,2,1,0:T(2,128)(2,1)S(1)} %copy-done.9, f32[2,2,2,128,64]{3,4,2,1,0:T(8,128)S(1)} %fusion.100, bf16[2,2,72,2,8,128]{5,4,3,2,1,0:T(8,128)(2,1)S(1)} %copy-done.4, bf16[2,2,2,64,704]{4,3,2,1,0:T(8,128)(2,1)} %fusion.7), kind=kOutput, calls=%fused_computation.104 | convolution fusion | flops 75890176 | bytes 2361344 | tf_op jit(solution)/shard_map/abhqk,abkhe->abqhe/dot_general | solution.py:88
  76.5 3.1 %collective-permute-start.11 = (f32[8,16,4]{1,0,2:T(8,128)S(1)}, f32[8,16,4]{1,0,2:T(8,128)S(1)}, u32[]{:S(2)}, u32[]{:S(2)}) collective-permute-start(f32[8,16,4]{1,0,2:T(8,128)S(1)} %slice.381), channel_id=1, source_target_pairs={{0,4},{4,8},{8,12},{12,16},{16,20},{20,24},{24,28},{1,5},{5,9},{9,... | collective-permute-start | bytes 6152 | tf_op jit(solution)/shard_map/ppermute | solution.py:24
  80.2 1.3 collective-permute-start.12
  81.8 4.0 %collective-permute-done.12 = f32[8,16,4]{1,0,2:T(8,128)S(1)} collective-permute-done((f32[8,16,4]{1,0,2:T(8,128)S(1)}, f32[8,16,4]{1,0,2:T(8,128)S(1)}, u32[]{:S(2)}, u32[]{:S(2)}) %collective-permute-start.12) | collective-permute-done | bytes 2080 | tf_op jit(solution)/shard_map/ppermute | solution.py:27
  85.9 1.3 collective-permute-start.13
  87.2 1.5 collective-permute-start.14
  88.9 3.2 %collective-permute-done.14 = f32[32,8,4]{1,0,2:T(8,128)S(1)} collective-permute-done((f32[32,8,4]{1,0,2:T(8,128)S(1)}, f32[32,8,4]{1,0,2:T(8,128)S(1)}, u32[]{:S(2)}, u32[]{:S(2)}) %collective-permute-start.14) | collective-permute-done | bytes 4128 | tf_op jit(solution)/shard_map/ppermute | solution.py:27
  93.9 2.0 %fusion.5 = f32[2,2,2,576,64]{3,4,2,1,0:T(8,128)S(1)} fusion(f32[2,2,2,576]{3,2,1,0:T(2,128)} %concatenate.96, pred[2,2,576]{2,1,0:T(4,128)(4,1)S(1)} %concatenate.83, bf16[2,2,8,2,8,128]{5,4,3,2,1,0:T(8,128)(2,1)} %get-tuple-element.11, bf16[2,2,576,256]{3,2,1,0:T(8,128)(2,1)} %copy-done.23), kind=kOutput, calls=%fused_computation.14 | convolution fusion | flops 76382208 | bytes 2511104 | tf_op jit(solution)/shard_map/abqhe,abkhe->abhqk/dot_general | solution.py:153
  95.9 1.0 fusion.54
  96.9 1.4 concatenate.98
  98.3 2.8 %fusion.60 = bf16[2,2,64,2,128]{4,2,3,1,0:T(8,128)(2,1)} fusion(f32[2,2,2,576,64]{3,4,2,1,0:T(8,128)S(1)} %fusion.5, f32[2,2,2,576]{3,2,1,0:T(2,128)} %concatenate.98, bf16[2,2,8,2,8,128]{5,4,3,2,1,0:T(8,128)(2,1)} %get-tuple-element.10, bf16[2,2,576,256]{3,2,1,0:T(8,128)(2,1)S(1)} %copy-done.7, bf16[2,2,576,256]{3,2,1,0:T(8,128)(2,1)} %copy-done.23), kind=kOutput, calls=%fused_computation.54 | convolution fusion | flops 152010752 | bytes 3819520 | tf_op jit(solution)/shard_map/abhqk,abqhe->abkhe/dot_general | solution.py:162
  101.1 1.1 copy.181
  103.1 3.0 %collective-permute-start.15 = (f32[512,256]{1,0:T(8,128)S(1)}, f32[512,256]{1,0:T(8,128)S(1)}, u32[]{:S(2)}, u32[]{:S(2)}) collective-permute-start(f32[512,256]{1,0:T(8,128)S(1)} %constant_dynamic-slice_fusion.1), channel_id=1, source_target_pairs={{0,1},{1,0},{2,3},{3,2},{4,5},{5,4},{6,7},{7,6},{8,9},{9,8},{10,11... | collective-permute-start | bytes 1572872 | tf_op jit(solution)/shard_map/ppermute | solution.py:229
  106.1 1.5 %collective-permute-done.15 = f32[512,256]{1,0:T(8,128)S(1)} collective-permute-done((f32[512,256]{1,0:T(8,128)S(1)}, f32[512,256]{1,0:T(8,128)S(1)}, u32[]{:S(2)}, u32[]{:S(2)}) %collective-permute-start.15) | collective-permute-done | bytes 524320 | tf_op jit(solution)/shard_map/ppermute | solution.py:229
  108.1 8.4 %collective-permute-done.16 = f32[256,256]{1,0:T(8,128)S(1)} collective-permute-done((f32[256,256]{1,0:T(8,128)S(1)}, f32[256,256]{1,0:T(8,128)S(1)}, u32[]{:S(2)}, u32[]{:S(2)}) %collective-permute-start.16) | collective-permute-done | bytes 262176 | tf_op jit(solution)/shard_map/ppermute | solution.py:229
  116.5 1.0 collective-permute-start.17
  117.5 4.0 %collective-permute-done.17 = f32[128,256]{1,0:T(8,128)S(1)} collective-permute-done((f32[128,256]{1,0:T(8,128)S(1)}, f32[128,256]{1,0:T(8,128)S(1)}, u32[]{:S(2)}, u32[]{:S(2)}) %collective-permute-start.17) | collective-permute-done | bytes 131104 | tf_op jit(solution)/shard_map/ppermute | solution.py:229
  121.6 5.0 %collective-permute-done.18 = f32[128,256]{1,0:T(8,128)S(1)} collective-permute-done((f32[128,256]{1,0:T(8,128)S(1)}, f32[128,256]{1,0:T(8,128)S(1)}, u32[]{:S(2)}, u32[]{:S(2)}) %collective-permute-start.18) | collective-permute-done | bytes 131104 | tf_op jit(solution)/shard_map/ppermute | solution.py:232
  126.6 1.5 %collective-permute-start.19 = (f32[128,256]{1,0:T(8,128)S(1)}, f32[128,256]{1,0:T(8,128)S(1)}, u32[]{:S(2)}, u32[]{:S(2)}) collective-permute-start(f32[128,256]{1,0:T(8,128)S(1)} %add.175), channel_id=1, source_target_pairs={{0,16},{4,20},{8,24},{12,28},{16,0},{20,4},{24,8},{28,12},{1,17},{... | collective-permute-start | bytes 393224 | tf_op jit(solution)/shard_map/ppermute | solution.py:232
  128.1 5.3 %collective-permute-done.19 = f32[128,256]{1,0:T(8,128)S(1)} collective-permute-done((f32[128,256]{1,0:T(8,128)S(1)}, f32[128,256]{1,0:T(8,128)S(1)}, u32[]{:S(2)}, u32[]{:S(2)}) %collective-permute-start.19) | collective-permute-done | bytes 131104 | tf_op jit(solution)/shard_map/ppermute | solution.py:232
  133.4 1.6 %collective-permute-start.20 = (f32[128,256]{1,0:T(8,128)S(1)}, f32[128,256]{1,0:T(8,128)S(1)}, u32[]{:S(2)}, u32[]{:S(2)}) collective-permute-start(f32[128,256]{1,0:T(8,128)S(1)} %add.176), channel_id=1, source_target_pairs={{0,4},{4,0},{8,12},{12,8},{16,20},{20,16},{24,28},{28,24},{1,5},{5... | collective-permute-start | bytes 393224 | tf_op jit(solution)/shard_map/ppermute | solution.py:194
  135.0 3.5 %collective-permute-done.20 = f32[128,256]{1,0:T(8,128)S(1)} collective-permute-done((f32[128,256]{1,0:T(8,128)S(1)}, f32[128,256]{1,0:T(8,128)S(1)}, u32[]{:S(2)}, u32[]{:S(2)}) %collective-permute-start.20) | collective-permute-done | bytes 131104 | tf_op jit(solution)/shard_map/ppermute | solution.py:194
  139.0 6.0 %collective-permute-done.21 = f32[256,256]{1,0:T(8,128)S(1)} collective-permute-done((f32[256,256]{1,0:T(8,128)S(1)}, f32[256,256]{1,0:T(8,128)S(1)}, u32[]{:S(2)}, u32[]{:S(2)}) %collective-permute-start.21) | collective-permute-done | bytes 262176 | tf_op jit(solution)/shard_map/ppermute | solution.py:194
  145.2 0.8 convolution_convert_fusion.3
  146.0 1.0 convolution_convert_fusion.1
  (218 shorter events, 22.7 us)
Async XLA Ops:
  0.6 32.4 %copy-start = (bf16[1,1,4,64,512]{4,3,2,1,0:T(8,128)(2,1)S(1)}, bf16[1,1,4,64,512]{4,3,2,1,0:T(8,128)(2,1)}, u32[]{:S(2)}) copy-start(bf16[1,1,4,64,512]{4,3,2,1,0:T(8,128)(2,1)} %param.15) | copy-start | bytes 786436
  0.6 15.1 %copy-start.13 = (bf16[16,16,256]{2,1,0:T(8,128)(2,1)S(1)}, bf16[16,16,256]{2,1,0:T(8,128)(2,1)}, u32[]{:S(2)}) copy-start(bf16[16,16,256]{2,1,0:T(8,128)(2,1)} %param.18) | copy-start | bytes 393220
  0.7 15.1 %copy-start.10 = (bf16[256,256]{1,0:T(8,128)(2,1)S(1)}, bf16[256,256]{1,0:T(8,128)(2,1)}, u32[]{:S(2)}) copy-start(bf16[256,256]{1,0:T(8,128)(2,1)} %param.14) | copy-start | bytes 393220
  0.7 19.3 %copy-start.24 = (s32[1,1,4,2]{2,3,1,0:T(2,128)S(1)}, s32[1,1,4,2]{2,3,1,0:T(2,128)}, u32[]{:S(2)}) copy-start(s32[1,1,4,2]{2,3,1,0:T(2,128)} %param.16) | copy-start | bytes 100
  2.0 18.4 %copy-start.25 = (s32[8]{0:T(128)S(1)}, s32[8]{0:T(128)}, u32[]{:S(2)}) copy-start(s32[8]{0:T(128)} %constant.165) | copy-start | bytes 100
  2.0 37.0 %collective-permute-start = (bf16[8,16,512]{2,1,0:T(8,128)(2,1)S(1)}, bf16[8,16,512]{2,1,0:T(8,128)(2,1)S(1)}, u32[]{:S(2)}, u32[]{:S(2)}) collective-permute-start(bf16[8,16,512]{2,1,0:T(8,128)(2,1)S(1)} %bitcast.279), channel_id=1, source_target_pairs={{0,4},{4,8},{8,12},{12,16},{16,20},{20,24},{24,28},{1,5},{5,9},{9,... | collective-permute-start | bytes 393224 | tf_op jit(solution)/shard_map/ppermute | solution.py:24
  6.9 32.2 %collective-permute-start.1 = (bf16[8,16,512]{2,1,0:T(8,128)(2,1)S(1)}, bf16[8,16,512]{2,1,0:T(8,128)(2,1)S(1)}, u32[]{:S(2)}, u32[]{:S(2)}) collective-permute-start(bf16[8,16,512]{2,1,0:T(8,128)(2,1)S(1)} %bitcast.278), channel_id=1, source_target_pairs={{4,0},{8,4},{12,8},{16,12},{20,16},{24,20},{28,24},{5,1},{9,5},{13... | collective-permute-start | bytes 393224 | tf_op jit(solution)/shard_map/ppermute | solution.py:27
  9.9 11.9 %collective-permute-start.4 = (s32[1,2,8]{2,1,0:T(2,128)S(1)}, s32[1,2,8]{2,1,0:T(2,128)S(1)}, u32[]{:S(2)}, u32[]{:S(2)}) collective-permute-start(s32[1,2,8]{2,1,0:T(2,128)S(1)} %add_bitcast_fusion), channel_id=1, source_target_pairs={{0,16},{4,20},{8,24},{12,28},{16,0},{20,4},{24,8},{28,12},{1,17},{... | collective-permute-start | bytes 200 | tf_op jit(solution)/shard_map/ppermute | solution.py:194
  16.0 25.8 %collective-permute-start.7 = (bf16[8,16,512]{2,1,0:T(8,128)(2,1)S(1)}, bf16[8,16,512]{2,1,0:T(8,128)(2,1)S(1)}, u32[]{:S(2)}, u32[]{:S(2)}) collective-permute-start(bf16[8,16,512]{2,1,0:T(8,128)(2,1)S(1)} %get-tuple-element.44), channel_id=1, source_target_pairs={{0,4},{4,8},{8,12},{12,16},{16,20},{20,24},{24,28},{1,5},{5,9},{9,... | collective-permute-start | bytes 393224 | tf_op jit(solution)/shard_map/ppermute | solution.py:24
  18.5 23.3 %collective-permute-start.8 = (bf16[8,16,512]{2,1,0:T(8,128)(2,1)S(1)}, bf16[8,16,512]{2,1,0:T(8,128)(2,1)S(1)}, u32[]{:S(2)}, u32[]{:S(2)}) collective-permute-start(bf16[8,16,512]{2,1,0:T(8,128)(2,1)S(1)} %get-tuple-element.45), channel_id=1, source_target_pairs={{4,0},{8,4},{12,8},{16,12},{20,16},{24,20},{28,24},{5,1},{9,5},{13... | collective-permute-start | bytes 393224 | tf_op jit(solution)/shard_map/ppermute | solution.py:27
  21.8 29.9 %copy-start.8 = (bf16[2,2,64,2,128]{4,3,2,1,0:T(2,128)(2,1)}, bf16[2,2,64,2,128]{4,3,2,1,0:T(2,128)(2,1)S(1)}, u32[]{:S(2)}) copy-start(bf16[2,2,64,2,128]{4,3,2,1,0:T(2,128)(2,1)S(1)} %reshape_reshape.32) | copy-start | bytes 393220
  21.9 6.2 %collective-permute-start.5 = (s32[2,2,8]{2,1,0:T(2,128)S(1)}, s32[2,2,8]{2,1,0:T(2,128)S(1)}, u32[]{:S(2)}, u32[]{:S(2)}) collective-permute-start(s32[2,2,8]{2,1,0:T(2,128)S(1)} %pad_add_fusion.2), channel_id=1, source_target_pairs={{0,8},{4,12},{8,0},{12,4},{16,24},{20,28},{24,16},{28,20},{1,9},{5... | collective-permute-start | bytes 392 | tf_op jit(solution)/shard_map/ppermute | solution.py:194
  28.1 3.7 %collective-permute-start.6 = (s32[4,2,8]{2,1,0:T(2,128)S(1)}, s32[4,2,8]{2,1,0:T(2,128)S(1)}, u32[]{:S(2)}, u32[]{:S(2)}) collective-permute-start(s32[4,2,8]{2,1,0:T(2,128)S(1)} %pad_add_fusion.1), channel_id=1, source_target_pairs={{0,4},{4,0},{8,12},{12,8},{16,20},{20,16},{24,28},{28,24},{1,5},{5... | collective-permute-start | bytes 776 | tf_op jit(solution)/shard_map/ppermute | solution.py:194
  34.8 27.4 %all-to-all-start = ((bf16[8,2,64,512]{3,2,1,0:T(8,128)(2,1)}), bf16[8,2,64,512]{3,2,1,0:T(8,128)(2,1)}, u32[]{:S(2)}, u32[]{:S(2)}) async-start(bf16[8,2,64,512]{3,2,1,0:T(8,128)(2,1)} %broadcast_select_fusion), calls=%async_computation | async-start | bytes 2097152 | tf_op jit(solution)/shard_map/all_to_all | solution.py:256
  39.2 9.5 %collective-permute-start.2 = (bf16[32,8,512]{2,1,0:T(8,128)(2,1)S(1)}, bf16[32,8,512]{2,1,0:T(8,128)(2,1)S(1)}, u32[]{:S(2)}, u32[]{:S(2)}) collective-permute-start(bf16[32,8,512]{2,1,0:T(8,128)(2,1)S(1)} %get-tuple-element.38), channel_id=1, source_target_pairs={{0,1},{1,2},{2,3},{4,5},{5,6},{6,7},{8,9},{9,10},{10,11},{12,13},{... | collective-permute-start | bytes 786440 | tf_op jit(solution)/shard_map/ppermute | solution.py:24
  40.5 8.2 %collective-permute-start.3 = (bf16[32,8,512]{2,1,0:T(8,128)(2,1)S(1)}, bf16[32,8,512]{2,1,0:T(8,128)(2,1)S(1)}, u32[]{:S(2)}, u32[]{:S(2)}) collective-permute-start(bf16[32,8,512]{2,1,0:T(8,128)(2,1)S(1)} %get-tuple-element.39), channel_id=1, source_target_pairs={{1,0},{2,1},{3,2},{5,4},{6,5},{7,6},{9,8},{10,9},{11,10},{13,12},{... | collective-permute-start | bytes 786440 | tf_op jit(solution)/shard_map/ppermute | solution.py:27
  41.9 7.8 %collective-permute-start.10 = (bf16[32,8,512]{2,1,0:T(8,128)(2,1)S(1)}, bf16[32,8,512]{2,1,0:T(8,128)(2,1)S(1)}, u32[]{:S(2)}, u32[]{:S(2)}) collective-permute-start(bf16[32,8,512]{2,1,0:T(8,128)(2,1)S(1)} %get-tuple-element.37), channel_id=1, source_target_pairs={{1,0},{2,1},{3,2},{5,4},{6,5},{7,6},{9,8},{10,9},{11,10},{13,12},{... | collective-permute-start | bytes 786440 | tf_op jit(solution)/shard_map/ppermute | solution.py:27
  43.2 6.6 %collective-permute-start.9 = (bf16[32,8,512]{2,1,0:T(8,128)(2,1)S(1)}, bf16[32,8,512]{2,1,0:T(8,128)(2,1)S(1)}, u32[]{:S(2)}, u32[]{:S(2)}) collective-permute-start(bf16[32,8,512]{2,1,0:T(8,128)(2,1)S(1)} %get-tuple-element.36), channel_id=1, source_target_pairs={{0,1},{1,2},{2,3},{4,5},{5,6},{6,7},{8,9},{9,10},{10,11},{12,13},{... | collective-permute-start | bytes 786440 | tf_op jit(solution)/shard_map/ppermute | solution.py:24
  50.3 1.5 copy-start.23
  51.8 1.0 copy-start.3
  51.8 1.4 copy-start.1
  66.5 3.0 %copy-start.9 = (bf16[2,2,64,2,128]{4,3,2,1,0:T(2,128)(2,1)S(1)}, bf16[2,2,64,2,128]{4,3,2,1,0:T(2,128)(2,1)}, u32[]{:S(2)}) copy-start(bf16[2,2,64,2,128]{4,3,2,1,0:T(2,128)(2,1)} %copy-done.8) | copy-start | bytes 393220
  69.6 2.6 %copy-start.4 = (bf16[2,2,72,2,8,128]{5,4,3,2,1,0:T(8,128)(2,1)S(1)}, bf16[2,2,72,2,8,128]{5,4,3,2,1,0:T(8,128)(2,1)}, u32[]{:S(2)}) copy-start(bf16[2,2,72,2,8,128]{5,4,3,2,1,0:T(8,128)(2,1)} %copy-done.3) | copy-start | bytes 3538948
  74.3 1.3 copy-start.2
  75.6 4.0 %copy-start.5 = (bf16[16,16,256]{2,1,0:T(8,128)(2,1)S(1)}, bf16[16,16,256]{2,1,0:T(8,128)(2,1)}, u32[]{:S(2)}) copy-start(bf16[16,16,256]{2,1,0:T(8,128)(2,1)} %param.10) | copy-start | bytes 393220
  76.0 5.5 %copy-start.20 = (bf16[2,2,64,2,128]{4,2,3,1,0:T(8,128)(2,1)S(1)}, bf16[2,2,64,2,128]{4,2,3,1,0:T(8,128)(2,1)}, u32[]{:S(2)}) copy-start(bf16[2,2,64,2,128]{4,2,3,1,0:T(8,128)(2,1)} %get-tuple-element.90) | copy-start | bytes 393220
  76.2 12.4 %copy-start.14 = (bf16[16,16,256]{2,1,0:T(8,128)(2,1)S(1)}, bf16[16,16,256]{2,1,0:T(8,128)(2,1)}, u32[]{:S(2)}) copy-start(bf16[16,16,256]{2,1,0:T(8,128)(2,1)} %param.18) | copy-start | bytes 393220
  76.3 5.2 %copy-start.15 = (bf16[2,8,2,8,256]{4,3,2,1,0:T(8,128)(2,1)}, bf16[2,8,2,8,256]{4,3,2,1,0:T(8,128)(2,1)S(1)}, u32[]{:S(2)}) copy-start(bf16[2,8,2,8,256]{4,3,2,1,0:T(8,128)(2,1)S(1)} %copy.170) | copy-start | bytes 393220
  76.5 5.2 %collective-permute-start.11 = (f32[8,16,4]{1,0,2:T(8,128)S(1)}, f32[8,16,4]{1,0,2:T(8,128)S(1)}, u32[]{:S(2)}, u32[]{:S(2)}) collective-permute-start(f32[8,16,4]{1,0,2:T(8,128)S(1)} %slice.381), channel_id=1, source_target_pairs={{0,4},{4,8},{8,12},{12,16},{16,20},{20,24},{24,28},{1,5},{5,9},{9,... | collective-permute-start | bytes 6152 | tf_op jit(solution)/shard_map/ppermute | solution.py:24
  80.2 5.6 %collective-permute-start.12 = (f32[8,16,4]{1,0,2:T(8,128)S(1)}, f32[8,16,4]{1,0,2:T(8,128)S(1)}, u32[]{:S(2)}, u32[]{:S(2)}) collective-permute-start(f32[8,16,4]{1,0,2:T(8,128)S(1)} %slice.383), channel_id=1, source_target_pairs={{4,0},{8,4},{12,8},{16,12},{20,16},{24,20},{28,24},{5,1},{9,5},{13... | collective-permute-start | bytes 6152 | tf_op jit(solution)/shard_map/ppermute | solution.py:27
  85.9 3.0 %collective-permute-start.13 = (f32[32,8,4]{1,0,2:T(8,128)S(1)}, f32[32,8,4]{1,0,2:T(8,128)S(1)}, u32[]{:S(2)}, u32[]{:S(2)}) collective-permute-start(f32[32,8,4]{1,0,2:T(8,128)S(1)} %get-tuple-element.48), channel_id=1, source_target_pairs={{0,1},{1,2},{2,3},{4,5},{5,6},{6,7},{8,9},{9,10},{10,11},{12,13},{... | collective-permute-start | bytes 12296 | tf_op jit(solution)/shard_map/ppermute | solution.py:24
  87.2 4.9 %collective-permute-start.14 = (f32[32,8,4]{1,0,2:T(8,128)S(1)}, f32[32,8,4]{1,0,2:T(8,128)S(1)}, u32[]{:S(2)}, u32[]{:S(2)}) collective-permute-start(f32[32,8,4]{1,0,2:T(8,128)S(1)} %get-tuple-element.49), channel_id=1, source_target_pairs={{1,0},{2,1},{3,2},{5,4},{6,5},{7,6},{9,8},{10,9},{11,10},{13,12},{... | collective-permute-start | bytes 12296 | tf_op jit(solution)/shard_map/ppermute | solution.py:27
  93.9 2.0 %copy-start.7 = (bf16[2,2,576,256]{3,2,1,0:T(8,128)(2,1)S(1)}, bf16[2,2,576,256]{3,2,1,0:T(8,128)(2,1)}, u32[]{:S(2)}) copy-start(bf16[2,2,576,256]{3,2,1,0:T(8,128)(2,1)} %copy-done.6) | copy-start | bytes 3538948
  95.8 1.0 copy-start.21
  101.1 1.4 copy-start.12
  103.1 4.5 %collective-permute-start.15 = (f32[512,256]{1,0:T(8,128)S(1)}, f32[512,256]{1,0:T(8,128)S(1)}, u32[]{:S(2)}, u32[]{:S(2)}) collective-permute-start(f32[512,256]{1,0:T(8,128)S(1)} %constant_dynamic-slice_fusion.1), channel_id=1, source_target_pairs={{0,1},{1,0},{2,3},{3,2},{4,5},{5,4},{6,7},{7,6},{8,9},{9,8},{10,11... | collective-permute-start | bytes 1572872 | tf_op jit(solution)/shard_map/ppermute | solution.py:229
  107.8 8.7 %collective-permute-start.16 = (f32[256,256]{1,0:T(8,128)S(1)}, f32[256,256]{1,0:T(8,128)S(1)}, u32[]{:S(2)}, u32[]{:S(2)}) collective-permute-start(f32[256,256]{1,0:T(8,128)S(1)} %constant_dynamic-slice_fusion), channel_id=1, source_target_pairs={{0,2},{1,3},{2,0},{3,1},{4,6},{5,7},{6,4},{7,5},{8,10},{9,11},{10,... | collective-permute-start | bytes 786440 | tf_op jit(solution)/shard_map/ppermute | solution.py:229
  116.5 5.0 %collective-permute-start.17 = (f32[128,256]{1,0:T(8,128)S(1)}, f32[128,256]{1,0:T(8,128)S(1)}, u32[]{:S(2)}, u32[]{:S(2)}) collective-permute-start(f32[128,256]{1,0:T(8,128)S(1)} %constant_dynamic-slice_fusion.2), channel_id=1, source_target_pairs={{0,4},{4,0},{8,12},{12,8},{16,20},{20,16},{24,28},{28,24},{1,5},{5... | collective-permute-start | bytes 393224 | tf_op jit(solution)/shard_map/ppermute | solution.py:229
  121.5 5.0 %collective-permute-start.18 = (f32[128,256]{1,0:T(8,128)S(1)}, f32[128,256]{1,0:T(8,128)S(1)}, u32[]{:S(2)}, u32[]{:S(2)}) collective-permute-start(f32[128,256]{1,0:T(8,128)S(1)} %dynamic-slice_add_fusion.2), channel_id=1, source_target_pairs={{0,8},{4,12},{8,0},{12,4},{16,24},{20,28},{24,16},{28,20},{1,9},{5... | collective-permute-start | bytes 393224 | tf_op jit(solution)/shard_map/ppermute | solution.py:232
  126.6 6.8 %collective-permute-start.19 = (f32[128,256]{1,0:T(8,128)S(1)}, f32[128,256]{1,0:T(8,128)S(1)}, u32[]{:S(2)}, u32[]{:S(2)}) collective-permute-start(f32[128,256]{1,0:T(8,128)S(1)} %add.175), channel_id=1, source_target_pairs={{0,16},{4,20},{8,24},{12,28},{16,0},{20,4},{24,8},{28,12},{1,17},{... | collective-permute-start | bytes 393224 | tf_op jit(solution)/shard_map/ppermute | solution.py:232
  133.4 5.0 %collective-permute-start.20 = (f32[128,256]{1,0:T(8,128)S(1)}, f32[128,256]{1,0:T(8,128)S(1)}, u32[]{:S(2)}, u32[]{:S(2)}) collective-permute-start(f32[128,256]{1,0:T(8,128)S(1)} %add.176), channel_id=1, source_target_pairs={{0,4},{4,0},{8,12},{12,8},{16,20},{20,16},{24,28},{28,24},{1,5},{5... | collective-permute-start | bytes 393224 | tf_op jit(solution)/shard_map/ppermute | solution.py:194
  138.4 6.7 %copy-start.11 = (bf16[256,256]{1,0:T(8,128)(2,1)S(1)}, bf16[256,256]{1,0:T(8,128)(2,1)}, u32[]{:S(2)}) copy-start(bf16[256,256]{1,0:T(8,128)(2,1)} %param.14) | copy-start | bytes 393220
  138.5 7.5 %copy-start.16 = (bf16[2,8,2,8,256]{4,3,2,1,0:T(8,128)(2,1)S(1)}, bf16[2,8,2,8,256]{4,3,2,1,0:T(8,128)(2,1)}, u32[]{:S(2)}) copy-start(bf16[2,8,2,8,256]{4,3,2,1,0:T(8,128)(2,1)} %copy-done.15) | copy-start | bytes 393220
  138.5 7.5 %copy-start.17 = (bf16[256,256]{1,0:T(8,128)(2,1)S(1)}, bf16[256,256]{1,0:T(8,128)(2,1)}, u32[]{:S(2)}) copy-start(bf16[256,256]{1,0:T(8,128)(2,1)} %param.11) | copy-start | bytes 393220
  138.5 7.5 %copy-start.18 = (bf16[256,256]{1,0:T(8,128)(2,1)S(1)}, bf16[256,256]{1,0:T(8,128)(2,1)}, u32[]{:S(2)}) copy-start(bf16[256,256]{1,0:T(8,128)(2,1)} %param.13) | copy-start | bytes 393220
  138.5 7.5 %copy-start.19 = (bf16[256,256]{1,0:T(8,128)(2,1)S(1)}, bf16[256,256]{1,0:T(8,128)(2,1)}, u32[]{:S(2)}) copy-start(bf16[256,256]{1,0:T(8,128)(2,1)} %param.12) | copy-start | bytes 393220
  138.5 6.4 %collective-permute-start.21 = (f32[256,256]{1,0:T(8,128)S(1)}, f32[256,256]{1,0:T(8,128)S(1)}, u32[]{:S(2)}, u32[]{:S(2)}) collective-permute-start(f32[256,256]{1,0:T(8,128)S(1)} %pad_maximum_fusion.7), channel_id=1, source_target_pairs={{0,2},{1,3},{2,0},{3,1},{4,6},{5,7},{6,4},{7,5},{8,10},{9,11},{10,... | collective-permute-start | bytes 786440 | tf_op jit(solution)/shard_map/ppermute | solution.py:194
  145.1 2.0 %collective-permute-start.22 = (f32[512,256]{1,0:T(8,128)S(1)}, f32[512,256]{1,0:T(8,128)S(1)}, u32[]{:S(2)}, u32[]{:S(2)}) collective-permute-start(f32[512,256]{1,0:T(8,128)S(1)} %pad_maximum_fusion.6), channel_id=1, source_target_pairs={{0,1},{1,0},{2,3},{3,2},{4,5},{5,4},{6,7},{7,6},{8,9},{9,8},{10,11... | collective-permute-start | bytes 1572872 | tf_op jit(solution)/shard_map/ppermute | solution.py:194
  (2 other events, 2.1 us)

commit v16 on v11

--- a/solution.py
+++ b/solution.py
@@ -288,7 +288,7 @@
     )
     query_halo = padded(query_grid, (("gx", 0), ("gy", 1)), BSIDE)
     stat_grid = from_blocks(jnp.concatenate([log_totals, delta_rows], 2).transpose(0, 1, 3, 2))
-    stat_halo = padded(stat_grid, (("gx", 0), ("gy", 1)), BSIDE)
+    stat_halo = padded(stat_grid, (("gy", 1), ("gx", 0)), BSIDE)
     query_all = to_blocks(query_halo)
     stat_pad = to_blocks(stat_halo).transpose(0, 1, 3, 2)
     d_keys, d_values = key_grads(

time: 145 us -> 142 us (0.979)
  waiting for transfers between devices: 48 us -> 44.5 us
    ppermute x3, waiting for transfers between devices: 13.4 us -> 11.9 us  [tree_sum(): joined = keep + lax.ppermute(send, axis, pairs)]
    unnamed x70 -> x68, local copies, waits for them, and re-layouts: 12 us -> 12 us
where the time goes in v16:
time: 142 us; the launch traced here: 141 us
  starting transfers between devices  51.1 us (36%)
  waiting for transfers between devices  44.5 us (31%)
  local copies, waits for them, and re-layouts  23.2 us (16%)
  matrix products  16.7 us (12%)
  other arithmetic  4.28 us (3%)
  between operations  1.66 us (1%)
    ppermute x6, starting transfers between devices, padded(): lax.ppermute(lax.slice_in_dim(block, block.shape[dim] - width, None, axis...  19.1 us
    ppermute x6, waiting for transfers between devices, doubling_gather(): got = lax.ppermute(joined, axis, pairs)  13.1 us
    ppermute x6, starting transfers between devices, doubling_gather(): got = lax.ppermute(joined, axis, pairs)  12.5 us
    unnamed x68, local copies, waits for them, and re-layouts  12 us
    ppermute x3, waiting for transfers between devices, tree_sum(): joined = keep + lax.ppermute(send, axis, pairs)  11.9 us
    ppermute x2, waiting for transfers between devices, tree_sum(): joined = joined + lax.ppermute(joined, axis, pairs)  8.95 us
    ppermute x6, starting transfers between devices, padded(): lax.ppermute(lax.slice_in_dim(block, 0, width, axis=dim), axis, backward)  7.93 us
    ppermute x6, waiting for transfers between devices, padded(): lax.ppermute(lax.slice_in_dim(block, 0, width, axis=dim), axis, backward)  5.55 us
  transfers between devices with their start and end apart: 24, of which 13 were waited for; matrix products, arithmetic and copies ran while one was open for 15% of the time, Pallas kernels for 0%

profile of v16, /device:TPU:0, one launch (start us, length us, event | category | flops | bytes accessed | tf_op | source)
XLA Modules:
  0.0 141.3 jit_solution(14717345665521048404)
XLA Ops:
  2.5 4.1 %collective-permute-start.4 = (s32[1,2,8]{2,1,0:T(2,128)S(1)}, s32[1,2,8]{2,1,0:T(2,128)S(1)}, u32[]{:S(2)}, u32[]{:S(2)}) collective-permute-start(s32[1,2,8]{2,1,0:T(2,128)S(1)} %add_bitcast_fusion), channel_id=1, source_target_pairs={{0,16},{4,20},{8,24},{12,28},{16,0},{20,4},{24,8},{28,12},{1,17},{... | collective-permute-start | bytes 200 | tf_op jit(solution)/shard_map/ppermute | solution.py:167
  6.6 1.3 convolution_convert_fusion
  7.9 3.4 %collective-permute-start = (bf16[8,16,512]{2,1,0:T(8,128)(2,1)S(1)}, bf16[8,16,512]{2,1,0:T(8,128)(2,1)S(1)}, u32[]{:S(2)}, u32[]{:S(2)}) collective-permute-start(bf16[8,16,512]{2,1,0:T(8,128)(2,1)S(1)} %bitcast.269), channel_id=1, source_target_pairs={{0,4},{4,8},{8,12},{12,16},{16,20},{20,24},{24,28},{1,5},{5,9},{9,... | collective-permute-start | bytes 393224 | tf_op jit(solution)/shard_map/ppermute | solution.py:24
  11.3 1.3 collective-permute-start.1
  12.6 1.2 convolution_convert_fusion.4
  14.0 4.5 %collective-permute-start.7 = (bf16[8,16,512]{2,1,0:T(8,128)(2,1)S(1)}, bf16[8,16,512]{2,1,0:T(8,128)(2,1)S(1)}, u32[]{:S(2)}, u32[]{:S(2)}) collective-permute-start(bf16[8,16,512]{2,1,0:T(8,128)(2,1)S(1)} %get-tuple-element.42), channel_id=1, source_target_pairs={{0,4},{4,8},{8,12},{12,16},{16,20},{20,24},{24,28},{1,5},{5,9},{9,... | collective-permute-start | bytes 393224 | tf_op jit(solution)/shard_map/ppermute | solution.py:24
  18.6 1.3 collective-permute-start.8
  23.4 4.6 %collective-permute-start.5 = (s32[2,2,8]{2,1,0:T(2,128)S(1)}, s32[2,2,8]{2,1,0:T(2,128)S(1)}, u32[]{:S(2)}, u32[]{:S(2)}) collective-permute-start(s32[2,2,8]{2,1,0:T(2,128)S(1)} %pad_add_fusion.2), channel_id=1, source_target_pairs={{0,8},{4,12},{8,0},{12,4},{16,24},{20,28},{24,16},{28,20},{1,9},{5... | collective-permute-start | bytes 392 | tf_op jit(solution)/shard_map/ppermute | solution.py:167
  28.0 1.6 %collective-permute-done.5 = s32[2,2,8]{2,1,0:T(2,128)S(1)} collective-permute-done((s32[2,2,8]{2,1,0:T(2,128)S(1)}, s32[2,2,8]{2,1,0:T(2,128)S(1)}, u32[]{:S(2)}, u32[]{:S(2)}) %collective-permute-start.5) | collective-permute-done | bytes 160 | tf_op jit(solution)/shard_map/ppermute | solution.py:167
  30.2 3.0 %collective-permute-done.6 = s32[4,2,8]{2,1,0:T(2,128)S(1)} collective-permute-done((s32[4,2,8]{2,1,0:T(2,128)S(1)}, s32[4,2,8]{2,1,0:T(2,128)S(1)}, u32[]{:S(2)}, u32[]{:S(2)}) %collective-permute-start.6) | collective-permute-done | bytes 288 | tf_op jit(solution)/shard_map/ppermute | solution.py:167
  35.2 1.2 broadcast_select_fusion
  36.4 3.6 %all-to-all-start = ((bf16[8,2,64,512]{3,2,1,0:T(8,128)(2,1)}), bf16[8,2,64,512]{3,2,1,0:T(8,128)(2,1)S(1)}, u32[]{:S(2)}, u32[]{:S(2)}) async-start(bf16[8,2,64,512]{3,2,1,0:T(8,128)(2,1)} %broadcast_select_fusion), calls=%async_computation | async-start | bytes 2097152 | tf_op jit(solution)/shard_map/all_to_all | solution.py:229
  40.1 1.3 collective-permute-start.2
  41.4 1.3 collective-permute-start.3
  42.8 1.3 collective-permute-start.10
  44.1 5.4 %collective-permute-start.9 = (bf16[32,8,512]{2,1,0:T(8,128)(2,1)S(1)}, bf16[32,8,512]{2,1,0:T(8,128)(2,1)S(1)}, u32[]{:S(2)}, u32[]{:S(2)}) collective-permute-start(bf16[32,8,512]{2,1,0:T(8,128)(2,1)S(1)} %get-tuple-element.36), channel_id=1, source_target_pairs={{0,1},{1,2},{2,3},{4,5},{5,6},{6,7},{8,9},{9,10},{10,11},{12,13},{... | collective-permute-start | bytes 786440 | tf_op jit(solution)/shard_map/ppermute | solution.py:24
  57.7 5.0 %all-to-all-done = bf16[8,2,64,512]{3,2,1,0:T(8,128)(2,1)S(1)} async-done(((bf16[8,2,64,512]{3,2,1,0:T(8,128)(2,1)}), bf16[8,2,64,512]{3,2,1,0:T(8,128)(2,1)S(1)}, u32[]{:S(2)}, u32[]{:S(2)}) %all-to-all-start) | async-done | bytes 1048608 | tf_op jit(solution)/shard_map/all_to_all | solution.py:229
  63.3 1.0 select_dynamic-update-slice_fusion
  64.3 2.3 %slice_bitcast_fusion.1 = (bf16[2,2,88,2,8,128]{5,4,3,2,1,0:T(8,128)(2,1)S(1)}, bf16[2,2,88,2,8,128]{5,4,3,2,1,0:T(8,128)(2,1)S(1)}) fusion(bf16[2,2,704,512]{3,2,1,0:T(8,128)(2,1)} %select_dynamic-update-slice_fusion), kind=kLoop, calls=%fused_computation.14 | loop fusion | bytes 5767168
  67.9 1.2 multiply_reduce_fusion
  69.0 3.1 %fusion.62 = bf16[2,2,64,2,128]{4,2,3,1,0:T(8,128)(2,1)} fusion(bf16[2,2,88,2,8,128]{5,4,3,2,1,0:T(8,128)(2,1)S(1)} %get-tuple-element.6, f32[2,2,2,64,704]{4,3,2,1,0:T(8,128)S(1)} %get-tuple-element.84, bf16[2,2,88,2,8,128]{5,4,3,2,1,0:T(8,128)(2,1)} %copy-done.1, f32[2,2,2,64]{3,2,1,0:T(2,128)S(1)} %bitcast.270, f32[2,2,2,64]{3,2,1,0:T(2,128)S(1)} %log_add_fusion, ...), kind=kOutput, calls=%fused_computation.50 | convolution fusion | flops 186122240 | bytes 4591616 | tf_op jit(solution)/shard_map/abhqk,abkhe->abqhe/dot_general | solution.py:108
  72.1 1.1 copy.132
  73.7 1.3 collective-permute-start.11
  75.0 1.3 collective-permute-start.12
  76.3 0.9 convolution_bitcast_fusion.2
  77.5 2.3 %collective-permute-done.12 = f32[16,8,4]{1,0,2:T(8,128)S(1)} collective-permute-done((f32[16,8,4]{1,0,2:T(8,128)S(1)}, f32[16,8,4]{1,0,2:T(8,128)S(1)}, u32[]{:S(2)}, u32[]{:S(2)}) %collective-permute-start.12) | collective-permute-done | bytes 2080 | tf_op jit(solution)/shard_map/ppermute | solution.py:27
  79.9 3.1 %collective-permute-start.13 = (f32[8,32,4]{1,0,2:T(8,128)S(1)}, f32[8,32,4]{1,0,2:T(8,128)S(1)}, u32[]{:S(2)}, u32[]{:S(2)}) collective-permute-start(f32[8,32,4]{1,0,2:T(8,128)S(1)} %get-tuple-element.64), channel_id=1, source_target_pairs={{0,4},{4,8},{8,12},{12,16},{16,20},{20,24},{24,28},{1,5},{5,9},{9,... | collective-permute-start | bytes 12296 | tf_op jit(solution)/shard_map/ppermute | solution.py:24
  83.1 1.5 %collective-permute-start.14 = (f32[8,32,4]{1,0,2:T(8,128)S(1)}, f32[8,32,4]{1,0,2:T(8,128)S(1)}, u32[]{:S(2)}, u32[]{:S(2)}) collective-permute-start(f32[8,32,4]{1,0,2:T(8,128)S(1)} %get-tuple-element.65), channel_id=1, source_target_pairs={{4,0},{8,4},{12,8},{16,12},{20,16},{24,20},{28,24},{5,1},{9,5},{13... | collective-permute-start | bytes 12296 | tf_op jit(solution)/shard_map/ppermute | solution.py:27
  84.6 0.9 fusion.116
  85.5 3.2 %collective-permute-done.14 = f32[8,32,4]{1,0,2:T(8,128)S(1)} collective-permute-done((f32[8,32,4]{1,0,2:T(8,128)S(1)}, f32[8,32,4]{1,0,2:T(8,128)S(1)}, u32[]{:S(2)}, u32[]{:S(2)}) %collective-permute-start.14) | collective-permute-done | bytes 4128 | tf_op jit(solution)/shard_map/ppermute | solution.py:27
  89.3 1.9 %fusion.9 = f32[2,2,2,576,64]{3,4,2,1,0:T(8,128)S(1)} fusion(f32[2,2,2,576]{3,2,1,0:T(2,128)S(1)} %concatenate.90, pred[2,2,576]{2,1,0:T(4,128)(4,1)S(1)} %copy-done.20, bf16[2,2,8,2,8,128]{5,4,3,2,1,0:T(8,128)(2,1)} %get-tuple-element.11, bf16[2,2,576,256]{3,2,1,0:T(8,128)(2,1)} %copy-done.19), kind=kOutput, calls=%fused_computation.20 | convolution fusion | flops 76382208 | bytes 2511104 | tf_op jit(solution)/shard_map/abqhe,abkhe->abhqk/dot_general | solution.py:126
  92.1 2.7 %fusion.57 = bf16[2,2,64,2,128]{4,2,3,1,0:T(8,128)(2,1)} fusion(f32[2,2,2,576,64]{3,4,2,1,0:T(8,128)S(1)} %fusion.9, f32[2,2,2,576]{3,2,1,0:T(2,128)S(1)} %concatenate.92, bf16[2,2,8,2,8,128]{5,4,3,2,1,0:T(8,128)(2,1)S(1)} %copy-done.18, bf16[2,2,576,256]{3,2,1,0:T(8,128)(2,1)S(1)} %copy-done.4, bf16[2,2,576,256]{3,2,1,0:T(8,128)(2,1)} %copy-done.19), kind=kOutput, calls=%fused_computation.49 | convolution fusion | flops 152010752 | bytes 3819520 | tf_op jit(solution)/shard_map/abhqk,abqhe->abkhe/dot_general | solution.py:135
  94.8 1.1 copy.142
  96.9 1.3 collective-permute-start.15
  98.2 1.5 %collective-permute-done.15 = f32[512,256]{1,0:T(8,128)S(1)} collective-permute-done((f32[512,256]{1,0:T(8,128)S(1)}, f32[512,256]{1,0:T(8,128)S(1)}, u32[]{:S(2)}, u32[]{:S(2)}) %collective-permute-start.15) | collective-permute-done | bytes 524320 | tf_op jit(solution)/shard_map/ppermute | solution.py:202
  99.8 1.8 %collective-permute-start.16 = (f32[256,256]{1,0:T(8,128)S(1)}, f32[256,256]{1,0:T(8,128)S(1)}, u32[]{:S(2)}, u32[]{:S(2)}) collective-permute-start(f32[256,256]{1,0:T(8,128)S(1)} %constant_dynamic-slice_fusion), channel_id=1, source_target_pairs={{0,2},{1,3},{2,0},{3,1},{4,6},{5,7},{6,4},{7,5},{8,10},{9,11},{10,... | collective-permute-start | bytes 786440 | tf_op jit(solution)/shard_map/ppermute | solution.py:202
  101.6 6.9 %collective-permute-done.16 = f32[256,256]{1,0:T(8,128)S(1)} collective-permute-done((f32[256,256]{1,0:T(8,128)S(1)}, f32[256,256]{1,0:T(8,128)S(1)}, u32[]{:S(2)}, u32[]{:S(2)}) %collective-permute-start.16) | collective-permute-done | bytes 262176 | tf_op jit(solution)/shard_map/ppermute | solution.py:202
  108.5 1.6 %collective-permute-start.17 = (f32[128,256]{1,0:T(8,128)S(1)}, f32[128,256]{1,0:T(8,128)S(1)}, u32[]{:S(2)}, u32[]{:S(2)}) collective-permute-start(f32[128,256]{1,0:T(8,128)S(1)} %constant_dynamic-slice_fusion.2), channel_id=1, source_target_pairs={{0,4},{4,0},{8,12},{12,8},{16,20},{20,16},{24,28},{28,24},{1,5},{5... | collective-permute-start | bytes 393224 | tf_op jit(solution)/shard_map/ppermute | solution.py:202
  110.1 3.5 %collective-permute-done.17 = f32[128,256]{1,0:T(8,128)S(1)} collective-permute-done((f32[128,256]{1,0:T(8,128)S(1)}, f32[128,256]{1,0:T(8,128)S(1)}, u32[]{:S(2)}, u32[]{:S(2)}) %collective-permute-start.17) | collective-permute-done | bytes 131104 | tf_op jit(solution)/shard_map/ppermute | solution.py:202
  113.6 1.3 collective-permute-start.18
  114.8 3.8 %collective-permute-done.18 = f32[128,256]{1,0:T(8,128)S(1)} collective-permute-done((f32[128,256]{1,0:T(8,128)S(1)}, f32[128,256]{1,0:T(8,128)S(1)}, u32[]{:S(2)}, u32[]{:S(2)}) %collective-permute-start.18) | collective-permute-done | bytes 131104 | tf_op jit(solution)/shard_map/ppermute | solution.py:205
  118.6 2.2 %collective-permute-start.19 = (f32[128,256]{1,0:T(8,128)S(1)}, f32[128,256]{1,0:T(8,128)S(1)}, u32[]{:S(2)}, u32[]{:S(2)}) collective-permute-start(f32[128,256]{1,0:T(8,128)S(1)} %add.165), channel_id=1, source_target_pairs={{0,16},{4,20},{8,24},{12,28},{16,0},{20,4},{24,8},{28,12},{1,17},{... | collective-permute-start | bytes 393224 | tf_op jit(solution)/shard_map/ppermute | solution.py:205
  120.8 5.2 %collective-permute-done.19 = f32[128,256]{1,0:T(8,128)S(1)} collective-permute-done((f32[128,256]{1,0:T(8,128)S(1)}, f32[128,256]{1,0:T(8,128)S(1)}, u32[]{:S(2)}, u32[]{:S(2)}) %collective-permute-start.19) | collective-permute-done | bytes 131104 | tf_op jit(solution)/shard_map/ppermute | solution.py:205
  126.0 1.6 %collective-permute-start.20 = (f32[128,256]{1,0:T(8,128)S(1)}, f32[128,256]{1,0:T(8,128)S(1)}, u32[]{:S(2)}, u32[]{:S(2)}) collective-permute-start(f32[128,256]{1,0:T(8,128)S(1)} %add.166), channel_id=1, source_target_pairs={{0,4},{4,0},{8,12},{12,8},{16,20},{20,16},{24,28},{28,24},{1,5},{5... | collective-permute-start | bytes 393224 | tf_op jit(solution)/shard_map/ppermute | solution.py:167
  127.6 3.5 %collective-permute-done.20 = f32[128,256]{1,0:T(8,128)S(1)} collective-permute-done((f32[128,256]{1,0:T(8,128)S(1)}, f32[128,256]{1,0:T(8,128)S(1)}, u32[]{:S(2)}, u32[]{:S(2)}) %collective-permute-start.20) | collective-permute-done | bytes 131104 | tf_op jit(solution)/shard_map/ppermute | solution.py:167
  131.1 1.5 %collective-permute-start.21 = (f32[256,256]{1,0:T(8,128)S(1)}, f32[256,256]{1,0:T(8,128)S(1)}, u32[]{:S(2)}, u32[]{:S(2)}) collective-permute-start(f32[256,256]{1,0:T(8,128)S(1)} %pad_maximum_fusion.6), channel_id=1, source_target_pairs={{0,2},{1,3},{2,0},{3,1},{4,6},{5,7},{6,4},{7,5},{8,10},{9,11},{10,... | collective-permute-start | bytes 786440 | tf_op jit(solution)/shard_map/ppermute | solution.py:167
  132.6 4.9 %collective-permute-done.21 = f32[256,256]{1,0:T(8,128)S(1)} collective-permute-done((f32[256,256]{1,0:T(8,128)S(1)}, f32[256,256]{1,0:T(8,128)S(1)}, u32[]{:S(2)}, u32[]{:S(2)}) %collective-permute-start.21) | collective-permute-done | bytes 262176 | tf_op jit(solution)/shard_map/ppermute | solution.py:167
  138.6 1.0 convolution_convert_fusion.1
  (197 shorter events, 24.2 us)
Async XLA Ops:
  0.6 33.9 %copy-start = (bf16[1,1,4,64,512]{4,3,2,1,0:T(8,128)(2,1)S(1)}, bf16[1,1,4,64,512]{4,3,2,1,0:T(8,128)(2,1)}, u32[]{:S(2)}) copy-start(bf16[1,1,4,64,512]{4,3,2,1,0:T(8,128)(2,1)} %param.15) | copy-start | bytes 786436
  0.6 19.6 %copy-start.22 = (s32[8]{0:T(128)S(1)}, s32[8]{0:T(128)}, u32[]{:S(2)}) copy-start(s32[8]{0:T(128)} %constant.166) | copy-start | bytes 100
  0.7 19.4 %copy-start.21 = (s32[1,1,4,2]{2,3,1,0:T(2,128)S(1)}, s32[1,1,4,2]{2,3,1,0:T(2,128)}, u32[]{:S(2)}) copy-start(s32[1,1,4,2]{2,3,1,0:T(2,128)} %param.16) | copy-start | bytes 100
  0.7 13.1 %copy-start.10 = (bf16[16,16,256]{2,1,0:T(8,128)(2,1)S(1)}, bf16[16,16,256]{2,1,0:T(8,128)(2,1)}, u32[]{:S(2)}) copy-start(bf16[16,16,256]{2,1,0:T(8,128)(2,1)} %param.18) | copy-start | bytes 393220
  0.7 13.1 %copy-start.7 = (bf16[256,256]{1,0:T(8,128)(2,1)S(1)}, bf16[256,256]{1,0:T(8,128)(2,1)}, u32[]{:S(2)}) copy-start(bf16[256,256]{1,0:T(8,128)(2,1)} %param.14) | copy-start | bytes 393220
  2.5 20.9 %collective-permute-start.4 = (s32[1,2,8]{2,1,0:T(2,128)S(1)}, s32[1,2,8]{2,1,0:T(2,128)S(1)}, u32[]{:S(2)}, u32[]{:S(2)}) collective-permute-start(s32[1,2,8]{2,1,0:T(2,128)S(1)} %add_bitcast_fusion), channel_id=1, source_target_pairs={{0,16},{4,20},{8,24},{12,28},{16,0},{20,4},{24,8},{28,12},{1,17},{... | collective-permute-start | bytes 200 | tf_op jit(solution)/shard_map/ppermute | solution.py:167
  7.9 32.1 %collective-permute-start = (bf16[8,16,512]{2,1,0:T(8,128)(2,1)S(1)}, bf16[8,16,512]{2,1,0:T(8,128)(2,1)S(1)}, u32[]{:S(2)}, u32[]{:S(2)}) collective-permute-start(bf16[8,16,512]{2,1,0:T(8,128)(2,1)S(1)} %bitcast.269), channel_id=1, source_target_pairs={{0,4},{4,8},{8,12},{12,16},{16,20},{20,24},{24,28},{1,5},{5,9},{9,... | collective-permute-start | bytes 393224 | tf_op jit(solution)/shard_map/ppermute | solution.py:24
  11.3 28.7 %collective-permute-start.1 = (bf16[8,16,512]{2,1,0:T(8,128)(2,1)S(1)}, bf16[8,16,512]{2,1,0:T(8,128)(2,1)S(1)}, u32[]{:S(2)}, u32[]{:S(2)}) collective-permute-start(bf16[8,16,512]{2,1,0:T(8,128)(2,1)S(1)} %bitcast.268), channel_id=1, source_target_pairs={{4,0},{8,4},{12,8},{16,12},{20,16},{24,20},{28,24},{5,1},{9,5},{13... | collective-permute-start | bytes 393224 | tf_op jit(solution)/shard_map/ppermute | solution.py:27
  14.0 28.7 %collective-permute-start.7 = (bf16[8,16,512]{2,1,0:T(8,128)(2,1)S(1)}, bf16[8,16,512]{2,1,0:T(8,128)(2,1)S(1)}, u32[]{:S(2)}, u32[]{:S(2)}) collective-permute-start(bf16[8,16,512]{2,1,0:T(8,128)(2,1)S(1)} %get-tuple-element.42), channel_id=1, source_target_pairs={{0,4},{4,8},{8,12},{12,16},{16,20},{20,24},{24,28},{1,5},{5,9},{9,... | collective-permute-start | bytes 393224 | tf_op jit(solution)/shard_map/ppermute | solution.py:24
  18.6 24.1 %collective-permute-start.8 = (bf16[8,16,512]{2,1,0:T(8,128)(2,1)S(1)}, bf16[8,16,512]{2,1,0:T(8,128)(2,1)S(1)}, u32[]{:S(2)}, u32[]{:S(2)}) collective-permute-start(bf16[8,16,512]{2,1,0:T(8,128)(2,1)S(1)} %get-tuple-element.43), channel_id=1, source_target_pairs={{4,0},{8,4},{12,8},{16,12},{20,16},{24,20},{28,24},{5,1},{9,5},{13... | collective-permute-start | bytes 393224 | tf_op jit(solution)/shard_map/ppermute | solution.py:27
  23.4 44.5 %copy-start.8 = (bf16[2,2,64,2,128]{4,3,2,1,0:T(2,128)(2,1)}, bf16[2,2,64,2,128]{4,3,2,1,0:T(2,128)(2,1)S(1)}, u32[]{:S(2)}) copy-start(bf16[2,2,64,2,128]{4,3,2,1,0:T(2,128)(2,1)S(1)} %reshape_reshape.32) | copy-start | bytes 393220
  23.4 6.1 %collective-permute-start.5 = (s32[2,2,8]{2,1,0:T(2,128)S(1)}, s32[2,2,8]{2,1,0:T(2,128)S(1)}, u32[]{:S(2)}, u32[]{:S(2)}) collective-permute-start(s32[2,2,8]{2,1,0:T(2,128)S(1)} %pad_add_fusion.2), channel_id=1, source_target_pairs={{0,8},{4,12},{8,0},{12,4},{16,24},{20,28},{24,16},{28,20},{1,9},{5... | collective-permute-start | bytes 392 | tf_op jit(solution)/shard_map/ppermute | solution.py:167
  29.6 3.7 %collective-permute-start.6 = (s32[4,2,8]{2,1,0:T(2,128)S(1)}, s32[4,2,8]{2,1,0:T(2,128)S(1)}, u32[]{:S(2)}, u32[]{:S(2)}) collective-permute-start(s32[4,2,8]{2,1,0:T(2,128)S(1)} %pad_add_fusion.1), channel_id=1, source_target_pairs={{0,4},{4,0},{8,12},{12,8},{16,20},{20,16},{24,28},{28,24},{1,5},{5... | collective-permute-start | bytes 776 | tf_op jit(solution)/shard_map/ppermute | solution.py:167
  36.4 26.3 %all-to-all-start = ((bf16[8,2,64,512]{3,2,1,0:T(8,128)(2,1)}), bf16[8,2,64,512]{3,2,1,0:T(8,128)(2,1)S(1)}, u32[]{:S(2)}, u32[]{:S(2)}) async-start(bf16[8,2,64,512]{3,2,1,0:T(8,128)(2,1)} %broadcast_select_fusion), calls=%async_computation | async-start | bytes 2097152 | tf_op jit(solution)/shard_map/all_to_all | solution.py:229
  40.1 9.5 %collective-permute-start.2 = (bf16[32,8,512]{2,1,0:T(8,128)(2,1)S(1)}, bf16[32,8,512]{2,1,0:T(8,128)(2,1)S(1)}, u32[]{:S(2)}, u32[]{:S(2)}) collective-permute-start(bf16[32,8,512]{2,1,0:T(8,128)(2,1)S(1)} %get-tuple-element.38), channel_id=1, source_target_pairs={{0,1},{1,2},{2,3},{4,5},{5,6},{6,7},{8,9},{9,10},{10,11},{12,13},{... | collective-permute-start | bytes 786440 | tf_op jit(solution)/shard_map/ppermute | solution.py:24
  41.4 8.2 %collective-permute-start.3 = (bf16[32,8,512]{2,1,0:T(8,128)(2,1)S(1)}, bf16[32,8,512]{2,1,0:T(8,128)(2,1)S(1)}, u32[]{:S(2)}, u32[]{:S(2)}) collective-permute-start(bf16[32,8,512]{2,1,0:T(8,128)(2,1)S(1)} %get-tuple-element.39), channel_id=1, source_target_pairs={{1,0},{2,1},{3,2},{5,4},{6,5},{7,6},{9,8},{10,9},{11,10},{13,12},{... | collective-permute-start | bytes 786440 | tf_op jit(solution)/shard_map/ppermute | solution.py:27
  42.8 9.2 %collective-permute-start.10 = (bf16[32,8,512]{2,1,0:T(8,128)(2,1)S(1)}, bf16[32,8,512]{2,1,0:T(8,128)(2,1)S(1)}, u32[]{:S(2)}, u32[]{:S(2)}) collective-permute-start(bf16[32,8,512]{2,1,0:T(8,128)(2,1)S(1)} %get-tuple-element.37), channel_id=1, source_target_pairs={{1,0},{2,1},{3,2},{5,4},{6,5},{7,6},{9,8},{10,9},{11,10},{13,12},{... | collective-permute-start | bytes 786440 | tf_op jit(solution)/shard_map/ppermute | solution.py:27
  44.1 7.9 %collective-permute-start.9 = (bf16[32,8,512]{2,1,0:T(8,128)(2,1)S(1)}, bf16[32,8,512]{2,1,0:T(8,128)(2,1)S(1)}, u32[]{:S(2)}, u32[]{:S(2)}) collective-permute-start(bf16[32,8,512]{2,1,0:T(8,128)(2,1)S(1)} %get-tuple-element.36), channel_id=1, source_target_pairs={{0,1},{1,2},{2,3},{4,5},{5,6},{6,7},{8,9},{9,10},{10,11},{12,13},{... | collective-permute-start | bytes 786440 | tf_op jit(solution)/shard_map/ppermute | solution.py:24
  52.4 4.5 %copy-start.3 = (bf16[2,2,576,256]{3,2,1,0:T(8,128)(2,1)}, bf16[2,2,576,256]{3,2,1,0:T(8,128)(2,1)S(1)}, u32[]{:S(2)}) copy-start(bf16[2,2,576,256]{3,2,1,0:T(8,128)(2,1)S(1)} %get-tuple-element.13) | copy-start | bytes 3538948
  52.5 4.5 %copy-start.19 = (bf16[2,2,576,256]{3,2,1,0:T(8,128)(2,1)}, bf16[2,2,576,256]{3,2,1,0:T(8,128)(2,1)S(1)}, u32[]{:S(2)}) copy-start(bf16[2,2,576,256]{3,2,1,0:T(8,128)(2,1)S(1)} %get-tuple-element.12) | copy-start | bytes 3538948
  64.3 2.3 %copy-start.14 = (bf16[2,2,64,2,128]{4,3,2,1,0:T(2,128)(2,1)S(1)}, bf16[2,2,64,2,128]{4,3,2,1,0:T(2,128)(2,1)}, u32[]{:S(2)}) copy-start(bf16[2,2,64,2,128]{4,3,2,1,0:T(2,128)(2,1)} %reshape_reshape.29) | copy-start | bytes 393220
  66.6 1.3 copy-start.1
  69.0 7.2 %copy-start.2 = (bf16[16,16,256]{2,1,0:T(8,128)(2,1)S(1)}, bf16[16,16,256]{2,1,0:T(8,128)(2,1)}, u32[]{:S(2)}) copy-start(bf16[16,16,256]{2,1,0:T(8,128)(2,1)} %param.10) | copy-start | bytes 393220
  72.1 5.1 %copy-start.9 = (bf16[2,2,64,2,128]{4,2,3,1,0:T(8,128)(2,1)S(1)}, bf16[2,2,64,2,128]{4,2,3,1,0:T(8,128)(2,1)}, u32[]{:S(2)}) copy-start(bf16[2,2,64,2,128]{4,2,3,1,0:T(8,128)(2,1)} %get-tuple-element.86) | copy-start | bytes 393220
  72.1 12.4 %copy-start.11 = (bf16[16,16,256]{2,1,0:T(8,128)(2,1)S(1)}, bf16[16,16,256]{2,1,0:T(8,128)(2,1)}, u32[]{:S(2)}) copy-start(bf16[16,16,256]{2,1,0:T(8,128)(2,1)} %param.18) | copy-start | bytes 393220
  73.3 3.9 %copy-start.12 = (bf16[2,8,2,8,256]{4,3,2,1,0:T(8,128)(2,1)}, bf16[2,8,2,8,256]{4,3,2,1,0:T(8,128)(2,1)S(1)}, u32[]{:S(2)}) copy-start(bf16[2,8,2,8,256]{4,3,2,1,0:T(8,128)(2,1)S(1)} %copy.133) | copy-start | bytes 393220
  73.7 3.8 %collective-permute-start.11 = (f32[16,8,4]{1,0,2:T(8,128)S(1)}, f32[16,8,4]{1,0,2:T(8,128)S(1)}, u32[]{:S(2)}, u32[]{:S(2)}) collective-permute-start(f32[16,8,4]{1,0,2:T(8,128)S(1)} %get-tuple-element.66), channel_id=1, source_target_pairs={{0,1},{1,2},{2,3},{4,5},{5,6},{6,7},{8,9},{9,10},{10,11},{12,13},{... | collective-permute-start | bytes 6152 | tf_op jit(solution)/shard_map/ppermute | solution.py:24
  75.0 4.9 %collective-permute-start.12 = (f32[16,8,4]{1,0,2:T(8,128)S(1)}, f32[16,8,4]{1,0,2:T(8,128)S(1)}, u32[]{:S(2)}, u32[]{:S(2)}) collective-permute-start(f32[16,8,4]{1,0,2:T(8,128)S(1)} %get-tuple-element.67), channel_id=1, source_target_pairs={{1,0},{2,1},{3,2},{5,4},{6,5},{7,6},{9,8},{10,9},{11,10},{13,12},{... | collective-permute-start | bytes 6152 | tf_op jit(solution)/shard_map/ppermute | solution.py:27
  77.4 11.9 %copy-start.20 = (pred[2,2,576]{2,1,0:T(4,128)(4,1)S(1)}, pred[2,2,576]{2,1,0:T(4,128)(4,1)}, u32[]{:S(2)}) copy-start(pred[2,2,576]{2,1,0:T(4,128)(4,1)} %concatenate.86) | copy-start | bytes 6916
  79.9 5.6 %collective-permute-start.13 = (f32[8,32,4]{1,0,2:T(8,128)S(1)}, f32[8,32,4]{1,0,2:T(8,128)S(1)}, u32[]{:S(2)}, u32[]{:S(2)}) collective-permute-start(f32[8,32,4]{1,0,2:T(8,128)S(1)} %get-tuple-element.64), channel_id=1, source_target_pairs={{0,4},{4,8},{8,12},{12,16},{16,20},{20,24},{24,28},{1,5},{5,9},{9,... | collective-permute-start | bytes 12296 | tf_op jit(solution)/shard_map/ppermute | solution.py:24
  83.1 5.6 %collective-permute-start.14 = (f32[8,32,4]{1,0,2:T(8,128)S(1)}, f32[8,32,4]{1,0,2:T(8,128)S(1)}, u32[]{:S(2)}, u32[]{:S(2)}) collective-permute-start(f32[8,32,4]{1,0,2:T(8,128)S(1)} %get-tuple-element.65), channel_id=1, source_target_pairs={{4,0},{8,4},{12,8},{16,12},{20,16},{24,20},{28,24},{5,1},{9,5},{13... | collective-permute-start | bytes 12296 | tf_op jit(solution)/shard_map/ppermute | solution.py:27
  89.3 1.9 %copy-start.4 = (bf16[2,2,576,256]{3,2,1,0:T(8,128)(2,1)S(1)}, bf16[2,2,576,256]{3,2,1,0:T(8,128)(2,1)}, u32[]{:S(2)}) copy-start(bf16[2,2,576,256]{3,2,1,0:T(8,128)(2,1)} %copy-done.3) | copy-start | bytes 3538948
  91.2 0.9 copy-start.18
  94.8 1.9 %copy-start.5 = (f32[256,256]{1,0:T(8,128)S(1)}, f32[256,256]{1,0:T(8,128)}, u32[]{:S(2)}) copy-start(f32[256,256]{1,0:T(8,128)} %convolution_bitcast_fusion.2) | copy-start | bytes 786436
  94.8 2.0 %copy-start.6 = (f32[256,256]{1,0:T(8,128)S(1)}, f32[256,256]{1,0:T(8,128)}, u32[]{:S(2)}) copy-start(f32[256,256]{1,0:T(8,128)} %fusion.116) | copy-start | bytes 786436
  96.9 2.8 %collective-permute-start.15 = (f32[512,256]{1,0:T(8,128)S(1)}, f32[512,256]{1,0:T(8,128)S(1)}, u32[]{:S(2)}, u32[]{:S(2)}) collective-permute-start(f32[512,256]{1,0:T(8,128)S(1)} %constant_dynamic-slice_fusion.1), channel_id=1, source_target_pairs={{0,1},{1,0},{2,3},{3,2},{4,5},{5,4},{6,7},{7,6},{8,9},{9,8},{10,11... | collective-permute-start | bytes 1572872 | tf_op jit(solution)/shard_map/ppermute | solution.py:202
  99.8 8.7 %collective-permute-start.16 = (f32[256,256]{1,0:T(8,128)S(1)}, f32[256,256]{1,0:T(8,128)S(1)}, u32[]{:S(2)}, u32[]{:S(2)}) collective-permute-start(f32[256,256]{1,0:T(8,128)S(1)} %constant_dynamic-slice_fusion), channel_id=1, source_target_pairs={{0,2},{1,3},{2,0},{3,1},{4,6},{5,7},{6,4},{7,5},{8,10},{9,11},{10,... | collective-permute-start | bytes 786440 | tf_op jit(solution)/shard_map/ppermute | solution.py:202
  108.5 5.0 %collective-permute-start.17 = (f32[128,256]{1,0:T(8,128)S(1)}, f32[128,256]{1,0:T(8,128)S(1)}, u32[]{:S(2)}, u32[]{:S(2)}) collective-permute-start(f32[128,256]{1,0:T(8,128)S(1)} %constant_dynamic-slice_fusion.2), channel_id=1, source_target_pairs={{0,4},{4,0},{8,12},{12,8},{16,20},{20,16},{24,28},{28,24},{1,5},{5... | collective-permute-start | bytes 393224 | tf_op jit(solution)/shard_map/ppermute | solution.py:202
  113.6 5.0 %collective-permute-start.18 = (f32[128,256]{1,0:T(8,128)S(1)}, f32[128,256]{1,0:T(8,128)S(1)}, u32[]{:S(2)}, u32[]{:S(2)}) collective-permute-start(f32[128,256]{1,0:T(8,128)S(1)} %dynamic-slice_add_fusion.2), channel_id=1, source_target_pairs={{0,8},{4,12},{8,0},{12,4},{16,24},{20,28},{24,16},{28,20},{1,9},{5... | collective-permute-start | bytes 393224 | tf_op jit(solution)/shard_map/ppermute | solution.py:205
  118.6 7.3 %collective-permute-start.19 = (f32[128,256]{1,0:T(8,128)S(1)}, f32[128,256]{1,0:T(8,128)S(1)}, u32[]{:S(2)}, u32[]{:S(2)}) collective-permute-start(f32[128,256]{1,0:T(8,128)S(1)} %add.165), channel_id=1, source_target_pairs={{0,16},{4,20},{8,24},{12,28},{16,0},{20,4},{24,8},{28,12},{1,17},{... | collective-permute-start | bytes 393224 | tf_op jit(solution)/shard_map/ppermute | solution.py:205
  126.0 5.0 %collective-permute-start.20 = (f32[128,256]{1,0:T(8,128)S(1)}, f32[128,256]{1,0:T(8,128)S(1)}, u32[]{:S(2)}, u32[]{:S(2)}) collective-permute-start(f32[128,256]{1,0:T(8,128)S(1)} %add.166), channel_id=1, source_target_pairs={{0,4},{4,0},{8,12},{12,8},{16,20},{20,16},{24,28},{28,24},{1,5},{5... | collective-permute-start | bytes 393224 | tf_op jit(solution)/shard_map/ppermute | solution.py:167
  131.0 7.5 %copy-start.13 = (bf16[2,8,2,8,256]{4,3,2,1,0:T(8,128)(2,1)S(1)}, bf16[2,8,2,8,256]{4,3,2,1,0:T(8,128)(2,1)}, u32[]{:S(2)}) copy-start(bf16[2,8,2,8,256]{4,3,2,1,0:T(8,128)(2,1)} %copy-done.12) | copy-start | bytes 393220
  131.1 7.5 %copy-start.15 = (bf16[256,256]{1,0:T(8,128)(2,1)S(1)}, bf16[256,256]{1,0:T(8,128)(2,1)}, u32[]{:S(2)}) copy-start(bf16[256,256]{1,0:T(8,128)(2,1)} %param.13) | copy-start | bytes 393220
  131.1 7.5 %copy-start.16 = (bf16[256,256]{1,0:T(8,128)(2,1)S(1)}, bf16[256,256]{1,0:T(8,128)(2,1)}, u32[]{:S(2)}) copy-start(bf16[256,256]{1,0:T(8,128)(2,1)} %param.12) | copy-start | bytes 393220
  131.1 7.5 %copy-start.17 = (bf16[256,256]{1,0:T(8,128)(2,1)S(1)}, bf16[256,256]{1,0:T(8,128)(2,1)}, u32[]{:S(2)}) copy-start(bf16[256,256]{1,0:T(8,128)(2,1)} %param.11) | copy-start | bytes 393220
  131.1 6.4 %collective-permute-start.21 = (f32[256,256]{1,0:T(8,128)S(1)}, f32[256,256]{1,0:T(8,128)S(1)}, u32[]{:S(2)}, u32[]{:S(2)}) collective-permute-start(f32[256,256]{1,0:T(8,128)S(1)} %pad_maximum_fusion.6), channel_id=1, source_target_pairs={{0,2},{1,3},{2,0},{3,1},{4,6},{5,7},{6,4},{7,5},{8,10},{9,11},{10,... | collective-permute-start | bytes 786440 | tf_op jit(solution)/shard_map/ppermute | solution.py:167
  137.6 2.0 %collective-permute-start.22 = (f32[512,256]{1,0:T(8,128)S(1)}, f32[512,256]{1,0:T(8,128)S(1)}, u32[]{:S(2)}, u32[]{:S(2)}) collective-permute-start(f32[512,256]{1,0:T(8,128)S(1)} %pad_maximum_fusion.5), channel_id=1, source_target_pairs={{0,1},{1,0},{2,3},{3,2},{4,5},{5,4},{6,7},{7,6},{8,9},{9,8},{10,11... | collective-permute-start | bytes 1572872 | tf_op jit(solution)/shard_map/ppermute | solution.py:167

commit v17 on v16

--- a/solution.py
+++ b/solution.py
@@ -244,7 +244,7 @@
     queries = jnp.dot(flat_in, w_query, preferred_element_type=jnp.float32).astype(jnp.bfloat16)
     keyvals = jnp.dot(flat_in, w_pair, preferred_element_type=jnp.float32).astype(jnp.bfloat16)
     keyvals = keyvals.reshape(tile_rows, tile_cols, 2 * model_width)
-    keyval_grid = padded(keyvals, (("gx", 0), ("gy", 1)), BSIDE)
+    keyval_grid = padded(keyvals, (("gy", 1), ("gx", 0)), BSIDE)
     keyval_pad = to_blocks(keyval_grid)
     gx_count = lax.axis_size("gx")
     gy_count = lax.axis_size("gy")
@@ -286,7 +286,7 @@
         ],
         -1,
     )
-    query_halo = padded(query_grid, (("gx", 0), ("gy", 1)), BSIDE)
+    query_halo = padded(query_grid, (("gy", 1), ("gx", 0)), BSIDE)
     stat_grid = from_blocks(jnp.concatenate([log_totals, delta_rows], 2).transpose(0, 1, 3, 2))
     stat_halo = padded(stat_grid, (("gy", 1), ("gx", 0)), BSIDE)
     query_all = to_blocks(query_halo)

time: 142 us -> 159 us (1.12)
  waiting for transfers between devices: 44.5 us -> 60.2 us
    ppermute x6, waiting for transfers between devices: 0.02 us -> 19.8 us  [padded(): lax.ppermute(lax.slice_in_dim(block, block.shape[dim] - width, None, axis...]
    all_to_all x1, waiting for transfers between devices: 5 us -> 0.01 us  [fetch_regions(): received = lax.all_to_all(sent, axis, 0, 0, tiled=True)]
    ppermute x6, starting transfers between devices: 12.5 us -> 10.5 us  [doubling_gather(): got = lax.ppermute(joined, axis, pairs)]
    ppermute x6, starting transfers between devices: 19.1 us -> 20.9 us  [padded(): lax.ppermute(lax.slice_in_dim(block, block.shape[dim] - width, None, axis...]
  transfers between devices with their start and end apart: 24 -> 24, of which waited for: 13 -> 14; matrix products, arithmetic and copies ran while one was open for 15% -> 13% of each run, Pallas kernels for 0% -> 0%
where the time goes in v17:
time: 159 us; the launch traced here: 158 us
  waiting for transfers between devices  60.2 us (38%)
  starting transfers between devices  52.2 us (33%)
  local copies, waits for them, and re-layouts  23.2 us (15%)
  matrix products  16.7 us (11%)
  other arithmetic  4.28 us (3%)
  between operations  1.63 us (1%)
    ppermute x6, starting transfers between devices, padded(): lax.ppermute(lax.slice_in_dim(block, block.shape[dim] - width, None, axis...  20.9 us
    ppermute x6, waiting for transfers between devices, padded(): lax.ppermute(lax.slice_in_dim(block, block.shape[dim] - width, None, axis...  19.8 us
    ppermute x6, waiting for transfers between devices, doubling_gather(): got = lax.ppermute(joined, axis, pairs)  12.6 us
    unnamed x68, local copies, waits for them, and re-layouts  12 us
    ppermute x3, waiting for transfers between devices, tree_sum(): joined = keep + lax.ppermute(send, axis, pairs)  11.9 us
    ppermute x6, starting transfers between devices, doubling_gather(): got = lax.ppermute(joined, axis, pairs)  10.5 us
    ppermute x2, waiting for transfers between devices, tree_sum(): joined = joined + lax.ppermute(joined, axis, pairs)  8.97 us
    ppermute x6, starting transfers between devices, padded(): lax.ppermute(lax.slice_in_dim(block, 0, width, axis=dim), axis, backward)  7.93 us
  transfers between devices with their start and end apart: 24, of which 14 were waited for; matrix products, arithmetic and copies ran while one was open for 13% of the time, Pallas kernels for 0%

profile of v17, /device:TPU:0, one launch (start us, length us, event | category | flops | bytes accessed | tf_op | source)
XLA Modules:
  0.0 158.1 jit_solution(16379206066447094607)
XLA Ops:
  2.5 4.1 %collective-permute-start.4 = (s32[1,2,8]{2,1,0:T(2,128)S(1)}, s32[1,2,8]{2,1,0:T(2,128)S(1)}, u32[]{:S(2)}, u32[]{:S(2)}) collective-permute-start(s32[1,2,8]{2,1,0:T(2,128)S(1)} %add_bitcast_fusion), channel_id=1, source_target_pairs={{0,16},{4,20},{8,24},{12,28},{16,0},{20,4},{24,8},{28,12},{1,17},{... | collective-permute-start | bytes 200 | tf_op jit(solution)/shard_map/ppermute | solution.py:167
  6.6 1.3 convolution_convert_fusion
  7.9 1.5 collective-permute-start
  9.3 1.3 collective-permute-start.1
  10.6 1.2 convolution_convert_fusion.4
  12.1 4.6 %collective-permute-start.7 = (bf16[16,8,512]{2,1,0:T(8,128)(2,1)S(1)}, bf16[16,8,512]{2,1,0:T(8,128)(2,1)S(1)}, u32[]{:S(2)}, u32[]{:S(2)}) collective-permute-start(bf16[16,8,512]{2,1,0:T(8,128)(2,1)S(1)} %get-tuple-element.42), channel_id=1, source_target_pairs={{0,1},{1,2},{2,3},{4,5},{5,6},{6,7},{8,9},{9,10},{10,11},{12,13},{... | collective-permute-start | bytes 393224 | tf_op jit(solution)/shard_map/ppermute | solution.py:24
  16.7 1.3 collective-permute-start.8
  21.6 1.6 %collective-permute-start.5 = (s32[2,2,8]{2,1,0:T(2,128)S(1)}, s32[2,2,8]{2,1,0:T(2,128)S(1)}, u32[]{:S(2)}, u32[]{:S(2)}) collective-permute-start(s32[2,2,8]{2,1,0:T(2,128)S(1)} %pad_add_fusion.2), channel_id=1, source_target_pairs={{0,8},{4,12},{8,0},{12,4},{16,24},{20,28},{24,16},{28,20},{1,9},{5... | collective-permute-start | bytes 392 | tf_op jit(solution)/shard_map/ppermute | solution.py:167
  23.2 2.0 %collective-permute-done.5 = s32[2,2,8]{2,1,0:T(2,128)S(1)} collective-permute-done((s32[2,2,8]{2,1,0:T(2,128)S(1)}, s32[2,2,8]{2,1,0:T(2,128)S(1)}, u32[]{:S(2)}, u32[]{:S(2)}) %collective-permute-start.5) | collective-permute-done | bytes 160 | tf_op jit(solution)/shard_map/ppermute | solution.py:167
  25.2 1.6 collective-permute-start.6
  26.8 2.1 %collective-permute-done.6 = s32[4,2,8]{2,1,0:T(2,128)S(1)} collective-permute-done((s32[4,2,8]{2,1,0:T(2,128)S(1)}, s32[4,2,8]{2,1,0:T(2,128)S(1)}, u32[]{:S(2)}, u32[]{:S(2)}) %collective-permute-start.6) | collective-permute-done | bytes 288 | tf_op jit(solution)/shard_map/ppermute | solution.py:167
  30.8 1.2 broadcast_select_fusion
  32.0 3.8 %all-to-all-start = ((bf16[8,2,64,512]{3,2,1,0:T(8,128)(2,1)}), bf16[8,2,64,512]{3,2,1,0:T(8,128)(2,1)S(1)}, u32[]{:S(2)}, u32[]{:S(2)}) async-start(bf16[8,2,64,512]{3,2,1,0:T(8,128)(2,1)} %broadcast_select_fusion), calls=%async_computation | async-start | bytes 2097152 | tf_op jit(solution)/shard_map/all_to_all | solution.py:229
  35.9 3.9 %collective-permute-start.2 = (bf16[8,32,512]{2,1,0:T(8,128)(2,1)S(1)}, bf16[8,32,512]{2,1,0:T(8,128)(2,1)S(1)}, u32[]{:S(2)}, u32[]{:S(2)}) collective-permute-start(bf16[8,32,512]{2,1,0:T(8,128)(2,1)S(1)} %get-tuple-element.38), channel_id=1, source_target_pairs={{0,4},{4,8},{8,12},{12,16},{16,20},{20,24},{24,28},{1,5},{5,9},{9,... | collective-permute-start | bytes 786440 | tf_op jit(solution)/shard_map/ppermute | solution.py:24
  39.8 1.3 collective-permute-start.3
  41.3 1.3 collective-permute-start.10
  42.6 5.2 %collective-permute-start.9 = (bf16[8,32,512]{2,1,0:T(8,128)(2,1)S(1)}, bf16[8,32,512]{2,1,0:T(8,128)(2,1)S(1)}, u32[]{:S(2)}, u32[]{:S(2)}) collective-permute-start(bf16[8,32,512]{2,1,0:T(8,128)(2,1)S(1)} %get-tuple-element.36), channel_id=1, source_target_pairs={{0,4},{4,8},{8,12},{12,16},{16,20},{20,24},{24,28},{1,5},{5,9},{9,... | collective-permute-start | bytes 786440 | tf_op jit(solution)/shard_map/ppermute | solution.py:24
  47.8 12.8 %collective-permute-done.2 = bf16[8,32,512]{2,1,0:T(8,128)(2,1)S(1)} collective-permute-done((bf16[8,32,512]{2,1,0:T(8,128)(2,1)S(1)}, bf16[8,32,512]{2,1,0:T(8,128)(2,1)S(1)}, u32[]{:S(2)}, u32[]{:S(2)}) %collective-permute-start.2) | collective-permute-done | bytes 262176 | tf_op jit(solution)/shard_map/ppermute | solution.py:24
  63.0 7.0 %collective-permute-done.9 = bf16[8,32,512]{2,1,0:T(8,128)(2,1)S(1)} collective-permute-done((bf16[8,32,512]{2,1,0:T(8,128)(2,1)S(1)}, bf16[8,32,512]{2,1,0:T(8,128)(2,1)S(1)}, u32[]{:S(2)}, u32[]{:S(2)}) %collective-permute-start.9) | collective-permute-done | bytes 262176 | tf_op jit(solution)/shard_map/ppermute | solution.py:24
  76.3 1.0 select_dynamic-update-slice_fusion
  77.3 2.3 %slice_bitcast_fusion.1 = (bf16[2,2,88,2,8,128]{5,4,3,2,1,0:T(8,128)(2,1)S(1)}, bf16[2,2,88,2,8,128]{5,4,3,2,1,0:T(8,128)(2,1)S(1)}) fusion(bf16[2,2,704,512]{3,2,1,0:T(8,128)(2,1)} %select_dynamic-update-slice_fusion), kind=kLoop, calls=%fused_computation.14 | loop fusion | bytes 5767168
  80.9 1.2 multiply_reduce_fusion
  82.1 3.1 %fusion.62 = bf16[2,2,64,2,128]{4,2,3,1,0:T(8,128)(2,1)} fusion(bf16[2,2,88,2,8,128]{5,4,3,2,1,0:T(8,128)(2,1)S(1)} %get-tuple-element.6, f32[2,2,2,64,704]{4,3,2,1,0:T(8,128)S(1)} %get-tuple-element.84, bf16[2,2,88,2,8,128]{5,4,3,2,1,0:T(8,128)(2,1)} %copy-done.1, f32[2,2,2,64]{3,2,1,0:T(2,128)S(1)} %bitcast.266, f32[2,2,2,64]{3,2,1,0:T(2,128)S(1)} %log_add_fusion, ...), kind=kOutput, calls=%fused_computation.50 | convolution fusion | flops 186122240 | bytes 4591616 | tf_op jit(solution)/shard_map/abhqk,abkhe->abqhe/dot_general | solution.py:108
  85.1 1.1 copy.132
  86.7 1.3 collective-permute-start.11
  88.0 1.3 collective-permute-start.12
  90.5 1.6 collective-permute-done.12
  92.2 4.4 %collective-permute-start.13 = (f32[8,32,4]{1,0,2:T(8,128)S(1)}, f32[8,32,4]{1,0,2:T(8,128)S(1)}, u32[]{:S(2)}, u32[]{:S(2)}) collective-permute-start(f32[8,32,4]{1,0,2:T(8,128)S(1)} %get-tuple-element.64), channel_id=1, source_target_pairs={{0,4},{4,8},{8,12},{12,16},{16,20},{20,24},{24,28},{1,5},{5,9},{9,... | collective-permute-start | bytes 12296 | tf_op jit(solution)/shard_map/ppermute | solution.py:24
  96.6 1.5 collective-permute-start.14
  99.0 5.4 %collective-permute-done.14 = f32[8,32,4]{1,0,2:T(8,128)S(1)} collective-permute-done((f32[8,32,4]{1,0,2:T(8,128)S(1)}, f32[8,32,4]{1,0,2:T(8,128)S(1)}, u32[]{:S(2)}, u32[]{:S(2)}) %collective-permute-start.14) | collective-permute-done | bytes 4128 | tf_op jit(solution)/shard_map/ppermute | solution.py:27
  104.9 1.9 %fusion.9 = f32[2,2,2,576,64]{3,4,2,1,0:T(8,128)S(1)} fusion(f32[2,2,2,576]{3,2,1,0:T(2,128)S(1)} %concatenate.90, pred[2,2,576]{2,1,0:T(4,128)(4,1)S(1)} %copy-done.20, bf16[2,2,8,2,8,128]{5,4,3,2,1,0:T(8,128)(2,1)} %get-tuple-element.11, bf16[2,2,576,256]{3,2,1,0:T(8,128)(2,1)} %copy-done.19), kind=kOutput, calls=%fused_computation.20 | convolution fusion | flops 76382208 | bytes 2511104 | tf_op jit(solution)/shard_map/abqhe,abkhe->abhqk/dot_general | solution.py:126
  107.8 2.7 %fusion.57 = bf16[2,2,64,2,128]{4,2,3,1,0:T(8,128)(2,1)} fusion(f32[2,2,2,576,64]{3,4,2,1,0:T(8,128)S(1)} %fusion.9, f32[2,2,2,576]{3,2,1,0:T(2,128)S(1)} %concatenate.92, bf16[2,2,8,2,8,128]{5,4,3,2,1,0:T(8,128)(2,1)S(1)} %copy-done.18, bf16[2,2,576,256]{3,2,1,0:T(8,128)(2,1)S(1)} %copy-done.4, bf16[2,2,576,256]{3,2,1,0:T(8,128)(2,1)} %copy-done.19), kind=kOutput, calls=%fused_computation.49 | convolution fusion | flops 152010752 | bytes 3819520 | tf_op jit(solution)/shard_map/abhqk,abqhe->abkhe/dot_general | solution.py:135
  110.4 1.1 copy.142
  112.5 1.5 collective-permute-start.15
  114.1 1.5 collective-permute-done.15
  115.7 1.5 collective-permute-start.16
  117.2 7.2 %collective-permute-done.16 = f32[256,256]{1,0:T(8,128)S(1)} collective-permute-done((f32[256,256]{1,0:T(8,128)S(1)}, f32[256,256]{1,0:T(8,128)S(1)}, u32[]{:S(2)}, u32[]{:S(2)}) %collective-permute-start.16) | collective-permute-done | bytes 262176 | tf_op jit(solution)/shard_map/ppermute | solution.py:202
  124.4 2.7 %collective-permute-start.17 = (f32[128,256]{1,0:T(8,128)S(1)}, f32[128,256]{1,0:T(8,128)S(1)}, u32[]{:S(2)}, u32[]{:S(2)}) collective-permute-start(f32[128,256]{1,0:T(8,128)S(1)} %constant_dynamic-slice_fusion.2), channel_id=1, source_target_pairs={{0,4},{4,0},{8,12},{12,8},{16,20},{20,16},{24,28},{28,24},{1,5},{5... | collective-permute-start | bytes 393224 | tf_op jit(solution)/shard_map/ppermute | solution.py:202
  127.1 3.2 %collective-permute-done.17 = f32[128,256]{1,0:T(8,128)S(1)} collective-permute-done((f32[128,256]{1,0:T(8,128)S(1)}, f32[128,256]{1,0:T(8,128)S(1)}, u32[]{:S(2)}, u32[]{:S(2)}) %collective-permute-start.17) | collective-permute-done | bytes 131104 | tf_op jit(solution)/shard_map/ppermute | solution.py:202
  130.4 1.5 collective-permute-start.18
  131.9 3.5 %collective-permute-done.18 = f32[128,256]{1,0:T(8,128)S(1)} collective-permute-done((f32[128,256]{1,0:T(8,128)S(1)}, f32[128,256]{1,0:T(8,128)S(1)}, u32[]{:S(2)}, u32[]{:S(2)}) %collective-permute-start.18) | collective-permute-done | bytes 131104 | tf_op jit(solution)/shard_map/ppermute | solution.py:205
  135.4 1.9 %collective-permute-start.19 = (f32[128,256]{1,0:T(8,128)S(1)}, f32[128,256]{1,0:T(8,128)S(1)}, u32[]{:S(2)}, u32[]{:S(2)}) collective-permute-start(f32[128,256]{1,0:T(8,128)S(1)} %add.165), channel_id=1, source_target_pairs={{0,16},{4,20},{8,24},{12,28},{16,0},{20,4},{24,8},{28,12},{1,17},{... | collective-permute-start | bytes 393224 | tf_op jit(solution)/shard_map/ppermute | solution.py:205
  137.3 5.5 %collective-permute-done.19 = f32[128,256]{1,0:T(8,128)S(1)} collective-permute-done((f32[128,256]{1,0:T(8,128)S(1)}, f32[128,256]{1,0:T(8,128)S(1)}, u32[]{:S(2)}, u32[]{:S(2)}) %collective-permute-start.19) | collective-permute-done | bytes 131104 | tf_op jit(solution)/shard_map/ppermute | solution.py:205
  142.8 1.8 %collective-permute-start.20 = (f32[128,256]{1,0:T(8,128)S(1)}, f32[128,256]{1,0:T(8,128)S(1)}, u32[]{:S(2)}, u32[]{:S(2)}) collective-permute-start(f32[128,256]{1,0:T(8,128)S(1)} %add.166), channel_id=1, source_target_pairs={{0,4},{4,0},{8,12},{12,8},{16,20},{20,16},{24,28},{28,24},{1,5},{5... | collective-permute-start | bytes 393224 | tf_op jit(solution)/shard_map/ppermute | solution.py:167
  144.6 3.2 %collective-permute-done.20 = f32[128,256]{1,0:T(8,128)S(1)} collective-permute-done((f32[128,256]{1,0:T(8,128)S(1)}, f32[128,256]{1,0:T(8,128)S(1)}, u32[]{:S(2)}, u32[]{:S(2)}) %collective-permute-start.20) | collective-permute-done | bytes 131104 | tf_op jit(solution)/shard_map/ppermute | solution.py:167
  147.9 1.3 collective-permute-start.21
  149.2 5.2 %collective-permute-done.21 = f32[256,256]{1,0:T(8,128)S(1)} collective-permute-done((f32[256,256]{1,0:T(8,128)S(1)}, f32[256,256]{1,0:T(8,128)S(1)}, u32[]{:S(2)}, u32[]{:S(2)}) %collective-permute-start.21) | collective-permute-done | bytes 262176 | tf_op jit(solution)/shard_map/ppermute | solution.py:167
  155.4 1.0 convolution_convert_fusion.1
  (197 shorter events, 25.4 us)
Async XLA Ops:
  0.6 29.6 %copy-start = (bf16[1,1,4,64,512]{4,3,2,1,0:T(8,128)(2,1)S(1)}, bf16[1,1,4,64,512]{4,3,2,1,0:T(8,128)(2,1)}, u32[]{:S(2)}) copy-start(bf16[1,1,4,64,512]{4,3,2,1,0:T(8,128)(2,1)} %param.15) | copy-start | bytes 786436
  0.6 17.7 %copy-start.22 = (s32[8]{0:T(128)S(1)}, s32[8]{0:T(128)}, u32[]{:S(2)}) copy-start(s32[8]{0:T(128)} %constant.166) | copy-start | bytes 100
  0.7 17.5 %copy-start.21 = (s32[1,1,4,2]{2,3,1,0:T(2,128)S(1)}, s32[1,1,4,2]{2,3,1,0:T(2,128)}, u32[]{:S(2)}) copy-start(s32[1,1,4,2]{2,3,1,0:T(2,128)} %param.16) | copy-start | bytes 100
  0.7 11.1 %copy-start.10 = (bf16[16,16,256]{2,1,0:T(8,128)(2,1)S(1)}, bf16[16,16,256]{2,1,0:T(8,128)(2,1)}, u32[]{:S(2)}) copy-start(bf16[16,16,256]{2,1,0:T(8,128)(2,1)} %param.18) | copy-start | bytes 393220
  0.7 11.1 %copy-start.7 = (bf16[256,256]{1,0:T(8,128)(2,1)S(1)}, bf16[256,256]{1,0:T(8,128)(2,1)}, u32[]{:S(2)}) copy-start(bf16[256,256]{1,0:T(8,128)(2,1)} %param.14) | copy-start | bytes 393220
  2.5 19.1 %collective-permute-start.4 = (s32[1,2,8]{2,1,0:T(2,128)S(1)}, s32[1,2,8]{2,1,0:T(2,128)S(1)}, u32[]{:S(2)}, u32[]{:S(2)}) collective-permute-start(s32[1,2,8]{2,1,0:T(2,128)S(1)} %add_bitcast_fusion), channel_id=1, source_target_pairs={{0,16},{4,20},{8,24},{12,28},{16,0},{20,4},{24,8},{28,12},{1,17},{... | collective-permute-start | bytes 200 | tf_op jit(solution)/shard_map/ppermute | solution.py:167
  7.9 27.9 %collective-permute-start = (bf16[16,8,512]{2,1,0:T(8,128)(2,1)S(1)}, bf16[16,8,512]{2,1,0:T(8,128)(2,1)S(1)}, u32[]{:S(2)}, u32[]{:S(2)}) collective-permute-start(bf16[16,8,512]{2,1,0:T(8,128)(2,1)S(1)} %get-tuple-element.44), channel_id=1, source_target_pairs={{0,1},{1,2},{2,3},{4,5},{5,6},{6,7},{8,9},{9,10},{10,11},{12,13},{... | collective-permute-start | bytes 393224 | tf_op jit(solution)/shard_map/ppermute | solution.py:24
  9.3 26.4 %collective-permute-start.1 = (bf16[16,8,512]{2,1,0:T(8,128)(2,1)S(1)}, bf16[16,8,512]{2,1,0:T(8,128)(2,1)S(1)}, u32[]{:S(2)}, u32[]{:S(2)}) collective-permute-start(bf16[16,8,512]{2,1,0:T(8,128)(2,1)S(1)} %get-tuple-element.45), channel_id=1, source_target_pairs={{1,0},{2,1},{3,2},{5,4},{6,5},{7,6},{9,8},{10,9},{11,10},{13,12},{... | collective-permute-start | bytes 393224 | tf_op jit(solution)/shard_map/ppermute | solution.py:27
  12.1 29.1 %collective-permute-start.7 = (bf16[16,8,512]{2,1,0:T(8,128)(2,1)S(1)}, bf16[16,8,512]{2,1,0:T(8,128)(2,1)S(1)}, u32[]{:S(2)}, u32[]{:S(2)}) collective-permute-start(bf16[16,8,512]{2,1,0:T(8,128)(2,1)S(1)} %get-tuple-element.42), channel_id=1, source_target_pairs={{0,1},{1,2},{2,3},{4,5},{5,6},{6,7},{8,9},{9,10},{10,11},{12,13},{... | collective-permute-start | bytes 393224 | tf_op jit(solution)/shard_map/ppermute | solution.py:24
  16.7 24.5 %collective-permute-start.8 = (bf16[16,8,512]{2,1,0:T(8,128)(2,1)S(1)}, bf16[16,8,512]{2,1,0:T(8,128)(2,1)S(1)}, u32[]{:S(2)}, u32[]{:S(2)}) collective-permute-start(bf16[16,8,512]{2,1,0:T(8,128)(2,1)S(1)} %get-tuple-element.43), channel_id=1, source_target_pairs={{1,0},{2,1},{3,2},{5,4},{6,5},{7,6},{9,8},{10,9},{11,10},{13,12},{... | collective-permute-start | bytes 393224 | tf_op jit(solution)/shard_map/ppermute | solution.py:27
  21.5 59.4 %copy-start.8 = (bf16[2,2,64,2,128]{4,3,2,1,0:T(2,128)(2,1)}, bf16[2,2,64,2,128]{4,3,2,1,0:T(2,128)(2,1)S(1)}, u32[]{:S(2)}) copy-start(bf16[2,2,64,2,128]{4,3,2,1,0:T(2,128)(2,1)S(1)} %reshape_reshape.32) | copy-start | bytes 393220
  21.6 3.7 %collective-permute-start.5 = (s32[2,2,8]{2,1,0:T(2,128)S(1)}, s32[2,2,8]{2,1,0:T(2,128)S(1)}, u32[]{:S(2)}, u32[]{:S(2)}) collective-permute-start(s32[2,2,8]{2,1,0:T(2,128)S(1)} %pad_add_fusion.2), channel_id=1, source_target_pairs={{0,8},{4,12},{8,0},{12,4},{16,24},{20,28},{24,16},{28,20},{1,9},{5... | collective-permute-start | bytes 392 | tf_op jit(solution)/shard_map/ppermute | solution.py:167
  25.2 3.7 %collective-permute-start.6 = (s32[4,2,8]{2,1,0:T(2,128)S(1)}, s32[4,2,8]{2,1,0:T(2,128)S(1)}, u32[]{:S(2)}, u32[]{:S(2)}) collective-permute-start(s32[4,2,8]{2,1,0:T(2,128)S(1)} %pad_add_fusion.1), channel_id=1, source_target_pairs={{0,4},{4,0},{8,12},{12,8},{16,20},{20,16},{24,28},{28,24},{1,5},{5... | collective-permute-start | bytes 776 | tf_op jit(solution)/shard_map/ppermute | solution.py:167
  32.0 43.7 %all-to-all-start = ((bf16[8,2,64,512]{3,2,1,0:T(8,128)(2,1)}), bf16[8,2,64,512]{3,2,1,0:T(8,128)(2,1)S(1)}, u32[]{:S(2)}, u32[]{:S(2)}) async-start(bf16[8,2,64,512]{3,2,1,0:T(8,128)(2,1)} %broadcast_select_fusion), calls=%async_computation | async-start | bytes 2097152 | tf_op jit(solution)/shard_map/all_to_all | solution.py:229
  35.9 24.7 %collective-permute-start.2 = (bf16[8,32,512]{2,1,0:T(8,128)(2,1)S(1)}, bf16[8,32,512]{2,1,0:T(8,128)(2,1)S(1)}, u32[]{:S(2)}, u32[]{:S(2)}) collective-permute-start(bf16[8,32,512]{2,1,0:T(8,128)(2,1)S(1)} %get-tuple-element.38), channel_id=1, source_target_pairs={{0,4},{4,8},{8,12},{12,16},{16,20},{20,24},{24,28},{1,5},{5,9},{9,... | collective-permute-start | bytes 786440 | tf_op jit(solution)/shard_map/ppermute | solution.py:24
  39.8 20.7 %collective-permute-start.3 = (bf16[8,32,512]{2,1,0:T(8,128)(2,1)S(1)}, bf16[8,32,512]{2,1,0:T(8,128)(2,1)S(1)}, u32[]{:S(2)}, u32[]{:S(2)}) collective-permute-start(bf16[8,32,512]{2,1,0:T(8,128)(2,1)S(1)} %get-tuple-element.39), channel_id=1, source_target_pairs={{4,0},{8,4},{12,8},{16,12},{20,16},{24,20},{28,24},{5,1},{9,5},{13... | collective-permute-start | bytes 786440 | tf_op jit(solution)/shard_map/ppermute | solution.py:27
  41.3 21.8 %collective-permute-start.10 = (bf16[8,32,512]{2,1,0:T(8,128)(2,1)S(1)}, bf16[8,32,512]{2,1,0:T(8,128)(2,1)S(1)}, u32[]{:S(2)}, u32[]{:S(2)}) collective-permute-start(bf16[8,32,512]{2,1,0:T(8,128)(2,1)S(1)} %get-tuple-element.37), channel_id=1, source_target_pairs={{4,0},{8,4},{12,8},{16,12},{20,16},{24,20},{28,24},{5,1},{9,5},{13... | collective-permute-start | bytes 786440 | tf_op jit(solution)/shard_map/ppermute | solution.py:27
  42.6 27.4 %collective-permute-start.9 = (bf16[8,32,512]{2,1,0:T(8,128)(2,1)S(1)}, bf16[8,32,512]{2,1,0:T(8,128)(2,1)S(1)}, u32[]{:S(2)}, u32[]{:S(2)}) collective-permute-start(bf16[8,32,512]{2,1,0:T(8,128)(2,1)S(1)} %get-tuple-element.36), channel_id=1, source_target_pairs={{0,4},{4,8},{8,12},{12,16},{16,20},{20,24},{24,28},{1,5},{5,9},{9,... | collective-permute-start | bytes 786440 | tf_op jit(solution)/shard_map/ppermute | solution.py:24
  70.4 4.5 %copy-start.3 = (bf16[2,2,576,256]{3,2,1,0:T(8,128)(2,1)}, bf16[2,2,576,256]{3,2,1,0:T(8,128)(2,1)S(1)}, u32[]{:S(2)}) copy-start(bf16[2,2,576,256]{3,2,1,0:T(8,128)(2,1)S(1)} %get-tuple-element.13) | copy-start | bytes 3538948
  70.5 4.5 %copy-start.19 = (bf16[2,2,576,256]{3,2,1,0:T(8,128)(2,1)}, bf16[2,2,576,256]{3,2,1,0:T(8,128)(2,1)S(1)}, u32[]{:S(2)}) copy-start(bf16[2,2,576,256]{3,2,1,0:T(8,128)(2,1)S(1)} %get-tuple-element.12) | copy-start | bytes 3538948
  77.3 2.3 %copy-start.14 = (bf16[2,2,64,2,128]{4,3,2,1,0:T(2,128)(2,1)S(1)}, bf16[2,2,64,2,128]{4,3,2,1,0:T(2,128)(2,1)}, u32[]{:S(2)}) copy-start(bf16[2,2,64,2,128]{4,3,2,1,0:T(2,128)(2,1)} %reshape_reshape.29) | copy-start | bytes 393220
  79.6 1.3 copy-start.1
  82.1 7.2 %copy-start.2 = (bf16[16,16,256]{2,1,0:T(8,128)(2,1)S(1)}, bf16[16,16,256]{2,1,0:T(8,128)(2,1)}, u32[]{:S(2)}) copy-start(bf16[16,16,256]{2,1,0:T(8,128)(2,1)} %param.10) | copy-start | bytes 393220
  85.1 5.1 %copy-start.9 = (bf16[2,2,64,2,128]{4,2,3,1,0:T(8,128)(2,1)S(1)}, bf16[2,2,64,2,128]{4,2,3,1,0:T(8,128)(2,1)}, u32[]{:S(2)}) copy-start(bf16[2,2,64,2,128]{4,2,3,1,0:T(8,128)(2,1)} %get-tuple-element.86) | copy-start | bytes 393220
  85.1 12.9 %copy-start.11 = (bf16[16,16,256]{2,1,0:T(8,128)(2,1)S(1)}, bf16[16,16,256]{2,1,0:T(8,128)(2,1)}, u32[]{:S(2)}) copy-start(bf16[16,16,256]{2,1,0:T(8,128)(2,1)} %param.18) | copy-start | bytes 393220
  86.3 3.9 %copy-start.12 = (bf16[2,8,2,8,256]{4,3,2,1,0:T(8,128)(2,1)}, bf16[2,8,2,8,256]{4,3,2,1,0:T(8,128)(2,1)S(1)}, u32[]{:S(2)}) copy-start(bf16[2,8,2,8,256]{4,3,2,1,0:T(8,128)(2,1)S(1)} %copy.133) | copy-start | bytes 393220
  86.7 3.8 %collective-permute-start.11 = (f32[16,8,4]{1,0,2:T(8,128)S(1)}, f32[16,8,4]{1,0,2:T(8,128)S(1)}, u32[]{:S(2)}, u32[]{:S(2)}) collective-permute-start(f32[16,8,4]{1,0,2:T(8,128)S(1)} %get-tuple-element.66), channel_id=1, source_target_pairs={{0,1},{1,2},{2,3},{4,5},{5,6},{6,7},{8,9},{9,10},{10,11},{12,13},{... | collective-permute-start | bytes 6152 | tf_op jit(solution)/shard_map/ppermute | solution.py:24
  88.0 4.1 %collective-permute-start.12 = (f32[16,8,4]{1,0,2:T(8,128)S(1)}, f32[16,8,4]{1,0,2:T(8,128)S(1)}, u32[]{:S(2)}, u32[]{:S(2)}) collective-permute-start(f32[16,8,4]{1,0,2:T(8,128)S(1)} %get-tuple-element.67), channel_id=1, source_target_pairs={{1,0},{2,1},{3,2},{5,4},{6,5},{7,6},{9,8},{10,9},{11,10},{13,12},{... | collective-permute-start | bytes 6152 | tf_op jit(solution)/shard_map/ppermute | solution.py:27
  90.4 14.6 %copy-start.20 = (pred[2,2,576]{2,1,0:T(4,128)(4,1)S(1)}, pred[2,2,576]{2,1,0:T(4,128)(4,1)}, u32[]{:S(2)}) copy-start(pred[2,2,576]{2,1,0:T(4,128)(4,1)} %concatenate.86) | copy-start | bytes 6916
  92.2 6.8 %collective-permute-start.13 = (f32[8,32,4]{1,0,2:T(8,128)S(1)}, f32[8,32,4]{1,0,2:T(8,128)S(1)}, u32[]{:S(2)}, u32[]{:S(2)}) collective-permute-start(f32[8,32,4]{1,0,2:T(8,128)S(1)} %get-tuple-element.64), channel_id=1, source_target_pairs={{0,4},{4,8},{8,12},{12,16},{16,20},{20,24},{24,28},{1,5},{5,9},{9,... | collective-permute-start | bytes 12296 | tf_op jit(solution)/shard_map/ppermute | solution.py:24
  96.6 7.8 %collective-permute-start.14 = (f32[8,32,4]{1,0,2:T(8,128)S(1)}, f32[8,32,4]{1,0,2:T(8,128)S(1)}, u32[]{:S(2)}, u32[]{:S(2)}) collective-permute-start(f32[8,32,4]{1,0,2:T(8,128)S(1)} %get-tuple-element.65), channel_id=1, source_target_pairs={{4,0},{8,4},{12,8},{16,12},{20,16},{24,20},{28,24},{5,1},{9,5},{13... | collective-permute-start | bytes 12296 | tf_op jit(solution)/shard_map/ppermute | solution.py:27
  104.9 1.9 %copy-start.4 = (bf16[2,2,576,256]{3,2,1,0:T(8,128)(2,1)S(1)}, bf16[2,2,576,256]{3,2,1,0:T(8,128)(2,1)}, u32[]{:S(2)}) copy-start(bf16[2,2,576,256]{3,2,1,0:T(8,128)(2,1)} %copy-done.3) | copy-start | bytes 3538948
  106.9 0.9 copy-start.18
  110.4 1.9 %copy-start.5 = (f32[256,256]{1,0:T(8,128)S(1)}, f32[256,256]{1,0:T(8,128)}, u32[]{:S(2)}) copy-start(f32[256,256]{1,0:T(8,128)} %convolution_bitcast_fusion.2) | copy-start | bytes 786436
  110.4 2.0 %copy-start.6 = (f32[256,256]{1,0:T(8,128)S(1)}, f32[256,256]{1,0:T(8,128)}, u32[]{:S(2)}) copy-start(f32[256,256]{1,0:T(8,128)} %fusion.116) | copy-start | bytes 786436
  112.5 3.1 %collective-permute-start.15 = (f32[512,256]{1,0:T(8,128)S(1)}, f32[512,256]{1,0:T(8,128)S(1)}, u32[]{:S(2)}, u32[]{:S(2)}) collective-permute-start(f32[512,256]{1,0:T(8,128)S(1)} %constant_dynamic-slice_fusion.1), channel_id=1, source_target_pairs={{0,1},{1,0},{2,3},{3,2},{4,5},{5,4},{6,7},{7,6},{8,9},{9,8},{10,11... | collective-permute-start | bytes 1572872 | tf_op jit(solution)/shard_map/ppermute | solution.py:202
  115.7 8.7 %collective-permute-start.16 = (f32[256,256]{1,0:T(8,128)S(1)}, f32[256,256]{1,0:T(8,128)S(1)}, u32[]{:S(2)}, u32[]{:S(2)}) collective-permute-start(f32[256,256]{1,0:T(8,128)S(1)} %constant_dynamic-slice_fusion), channel_id=1, source_target_pairs={{0,2},{1,3},{2,0},{3,1},{4,6},{5,7},{6,4},{7,5},{8,10},{9,11},{10,... | collective-permute-start | bytes 786440 | tf_op jit(solution)/shard_map/ppermute | solution.py:202
  124.4 5.9 %collective-permute-start.17 = (f32[128,256]{1,0:T(8,128)S(1)}, f32[128,256]{1,0:T(8,128)S(1)}, u32[]{:S(2)}, u32[]{:S(2)}) collective-permute-start(f32[128,256]{1,0:T(8,128)S(1)} %constant_dynamic-slice_fusion.2), channel_id=1, source_target_pairs={{0,4},{4,0},{8,12},{12,8},{16,20},{20,16},{24,28},{28,24},{1,5},{5... | collective-permute-start | bytes 393224 | tf_op jit(solution)/shard_map/ppermute | solution.py:202
  130.4 5.0 %collective-permute-start.18 = (f32[128,256]{1,0:T(8,128)S(1)}, f32[128,256]{1,0:T(8,128)S(1)}, u32[]{:S(2)}, u32[]{:S(2)}) collective-permute-start(f32[128,256]{1,0:T(8,128)S(1)} %dynamic-slice_add_fusion.2), channel_id=1, source_target_pairs={{0,8},{4,12},{8,0},{12,4},{16,24},{20,28},{24,16},{28,20},{1,9},{5... | collective-permute-start | bytes 393224 | tf_op jit(solution)/shard_map/ppermute | solution.py:205
  135.4 7.3 %collective-permute-start.19 = (f32[128,256]{1,0:T(8,128)S(1)}, f32[128,256]{1,0:T(8,128)S(1)}, u32[]{:S(2)}, u32[]{:S(2)}) collective-permute-start(f32[128,256]{1,0:T(8,128)S(1)} %add.165), channel_id=1, source_target_pairs={{0,16},{4,20},{8,24},{12,28},{16,0},{20,4},{24,8},{28,12},{1,17},{... | collective-permute-start | bytes 393224 | tf_op jit(solution)/shard_map/ppermute | solution.py:205
  142.8 5.0 %collective-permute-start.20 = (f32[128,256]{1,0:T(8,128)S(1)}, f32[128,256]{1,0:T(8,128)S(1)}, u32[]{:S(2)}, u32[]{:S(2)}) collective-permute-start(f32[128,256]{1,0:T(8,128)S(1)} %add.166), channel_id=1, source_target_pairs={{0,4},{4,0},{8,12},{12,8},{16,20},{20,16},{24,28},{28,24},{1,5},{5... | collective-permute-start | bytes 393224 | tf_op jit(solution)/shard_map/ppermute | solution.py:167
  147.8 7.5 %copy-start.13 = (bf16[2,8,2,8,256]{4,3,2,1,0:T(8,128)(2,1)S(1)}, bf16[2,8,2,8,256]{4,3,2,1,0:T(8,128)(2,1)}, u32[]{:S(2)}) copy-start(bf16[2,8,2,8,256]{4,3,2,1,0:T(8,128)(2,1)} %copy-done.12) | copy-start | bytes 393220
  147.8 7.5 %copy-start.15 = (bf16[256,256]{1,0:T(8,128)(2,1)S(1)}, bf16[256,256]{1,0:T(8,128)(2,1)}, u32[]{:S(2)}) copy-start(bf16[256,256]{1,0:T(8,128)(2,1)} %param.13) | copy-start | bytes 393220
  147.9 7.5 %copy-start.16 = (bf16[256,256]{1,0:T(8,128)(2,1)S(1)}, bf16[256,256]{1,0:T(8,128)(2,1)}, u32[]{:S(2)}) copy-start(bf16[256,256]{1,0:T(8,128)(2,1)} %param.12) | copy-start | bytes 393220
  147.9 7.5 %copy-start.17 = (bf16[256,256]{1,0:T(8,128)(2,1)S(1)}, bf16[256,256]{1,0:T(8,128)(2,1)}, u32[]{:S(2)}) copy-start(bf16[256,256]{1,0:T(8,128)(2,1)} %param.11) | copy-start | bytes 393220
  147.9 6.4 %collective-permute-start.21 = (f32[256,256]{1,0:T(8,128)S(1)}, f32[256,256]{1,0:T(8,128)S(1)}, u32[]{:S(2)}, u32[]{:S(2)}) collective-permute-start(f32[256,256]{1,0:T(8,128)S(1)} %pad_maximum_fusion.6), channel_id=1, source_target_pairs={{0,2},{1,3},{2,0},{3,1},{4,6},{5,7},{6,4},{7,5},{8,10},{9,11},{10,... | collective-permute-start | bytes 786440 | tf_op jit(solution)/shard_map/ppermute | solution.py:167
  154.4 2.0 %collective-permute-start.22 = (f32[512,256]{1,0:T(8,128)S(1)}, f32[512,256]{1,0:T(8,128)S(1)}, u32[]{:S(2)}, u32[]{:S(2)}) collective-permute-start(f32[512,256]{1,0:T(8,128)S(1)} %pad_maximum_fusion.5), channel_id=1, source_target_pairs={{0,1},{1,0},{2,3},{3,2},{4,5},{5,4},{6,7},{7,6},{8,9},{9,8},{10,11... | collective-permute-start | bytes 1572872 | tf_op jit(solution)/shard_map/ppermute | solution.py:167

commit v18 on v17

--- a/solution.py
+++ b/solution.py
@@ -244,7 +244,7 @@
     queries = jnp.dot(flat_in, w_query, preferred_element_type=jnp.float32).astype(jnp.bfloat16)
     keyvals = jnp.dot(flat_in, w_pair, preferred_element_type=jnp.float32).astype(jnp.bfloat16)
     keyvals = keyvals.reshape(tile_rows, tile_cols, 2 * model_width)
-    keyval_grid = padded(keyvals, (("gy", 1), ("gx", 0)), BSIDE)
+    keyval_grid = padded(keyvals, (("gx", 0), ("gy", 1)), BSIDE)
     keyval_pad = to_blocks(keyval_grid)
     gx_count = lax.axis_size("gx")
     gy_count = lax.axis_size("gy")

time: 159 us -> 151 us (0.950)
  waiting for transfers between devices: 60.2 us -> 45.7 us
  starting transfers between devices: 52.2 us -> 58.4 us
    ppermute x6, waiting for transfers between devices: 19.8 us -> 4.85 us  [padded(): lax.ppermute(lax.slice_in_dim(block, block.shape[dim] - width, None, axis...]
    ppermute x6, waiting for transfers between devices: 6.93 us -> 10.3 us  [padded(): lax.ppermute(lax.slice_in_dim(block, 0, width, axis=dim), axis, backward)]
    ppermute x6, starting transfers between devices: 10.5 us -> 12.9 us  [doubling_gather(): got = lax.ppermute(joined, axis, pairs)]
    ppermute x2, waiting for transfers between devices: 8.97 us -> 6.76 us  [tree_sum(): joined = joined + lax.ppermute(joined, axis, pairs)]
    ppermute x3, starting transfers between devices: 5.72 us -> 7.85 us  [tree_sum(): joined = keep + lax.ppermute(send, axis, pairs)]
  transfers between devices with their start and end apart: 24 -> 24, of which waited for: 14 -> 14; matrix products, arithmetic and copies ran while one was open for 13% -> 14% of each run, Pallas kernels for 0% -> 0%
where the time goes in v18:
time: 151 us; the launch traced here: 150 us
  starting transfers between devices  58.4 us (39%)
  waiting for transfers between devices  45.7 us (30%)
  local copies, waits for them, and re-layouts  23.2 us (15%)
  matrix products  16.7 us (11%)
  other arithmetic  4.29 us (3%)
  between operations  1.66 us (1%)
    ppermute x6, starting transfers between devices, padded(): lax.ppermute(lax.slice_in_dim(block, block.shape[dim] - width, None, axis...  21.6 us
    ppermute x6, starting transfers between devices, doubling_gather(): got = lax.ppermute(joined, axis, pairs)  12.9 us
    ppermute x6, waiting for transfers between devices, doubling_gather(): got = lax.ppermute(joined, axis, pairs)  12 us
    unnamed x68, local copies, waits for them, and re-layouts  12 us
    ppermute x3, waiting for transfers between devices, tree_sum(): joined = keep + lax.ppermute(send, axis, pairs)  11.8 us
    ppermute x6, waiting for transfers between devices, padded(): lax.ppermute(lax.slice_in_dim(block, 0, width, axis=dim), axis, backward)  10.3 us
    ppermute x6, starting transfers between devices, padded(): lax.ppermute(lax.slice_in_dim(block, 0, width, axis=dim), axis, backward)  7.93 us
    ppermute x3, starting transfers between devices, tree_sum(): joined = keep + lax.ppermute(send, axis, pairs)  7.85 us
  transfers between devices with their start and end apart: 24, of which 14 were waited for; matrix products, arithmetic and copies ran while one was open for 14% of the time, Pallas kernels for 0%

profile of v18, /device:TPU:0, one launch (start us, length us, event | category | flops | bytes accessed | tf_op | source)
XLA Modules:
  0.0 149.9 jit_solution(3997706590000459356)
XLA Ops:
  2.5 4.1 %collective-permute-start.4 = (s32[1,2,8]{2,1,0:T(2,128)S(1)}, s32[1,2,8]{2,1,0:T(2,128)S(1)}, u32[]{:S(2)}, u32[]{:S(2)}) collective-permute-start(s32[1,2,8]{2,1,0:T(2,128)S(1)} %add_bitcast_fusion), channel_id=1, source_target_pairs={{0,16},{4,20},{8,24},{12,28},{16,0},{20,4},{24,8},{28,12},{1,17},{... | collective-permute-start | bytes 200 | tf_op jit(solution)/shard_map/ppermute | solution.py:167
  6.6 1.3 convolution_convert_fusion
  7.9 3.4 %collective-permute-start = (bf16[8,16,512]{2,1,0:T(8,128)(2,1)S(1)}, bf16[8,16,512]{2,1,0:T(8,128)(2,1)S(1)}, u32[]{:S(2)}, u32[]{:S(2)}) collective-permute-start(bf16[8,16,512]{2,1,0:T(8,128)(2,1)S(1)} %bitcast.269), channel_id=1, source_target_pairs={{0,4},{4,8},{8,12},{12,16},{16,20},{20,24},{24,28},{1,5},{5,9},{9,... | collective-permute-start | bytes 393224 | tf_op jit(solution)/shard_map/ppermute | solution.py:24
  11.3 1.3 collective-permute-start.1
  12.6 1.2 convolution_convert_fusion.4
  14.0 1.3 collective-permute-start.7
  15.3 1.3 collective-permute-start.8
  20.2 3.7 %collective-permute-start.5 = (s32[2,2,8]{2,1,0:T(2,128)S(1)}, s32[2,2,8]{2,1,0:T(2,128)S(1)}, u32[]{:S(2)}, u32[]{:S(2)}) collective-permute-start(s32[2,2,8]{2,1,0:T(2,128)S(1)} %pad_add_fusion.2), channel_id=1, source_target_pairs={{0,8},{4,12},{8,0},{12,4},{16,24},{20,28},{24,16},{28,20},{1,9},{5... | collective-permute-start | bytes 392 | tf_op jit(solution)/shard_map/ppermute | solution.py:167
  23.9 1.6 %collective-permute-done.5 = s32[2,2,8]{2,1,0:T(2,128)S(1)} collective-permute-done((s32[2,2,8]{2,1,0:T(2,128)S(1)}, s32[2,2,8]{2,1,0:T(2,128)S(1)}, u32[]{:S(2)}, u32[]{:S(2)}) %collective-permute-start.5) | collective-permute-done | bytes 160 | tf_op jit(solution)/shard_map/ppermute | solution.py:167
  25.5 1.1 collective-permute-start.6
  26.6 2.6 %collective-permute-done.6 = s32[4,2,8]{2,1,0:T(2,128)S(1)} collective-permute-done((s32[4,2,8]{2,1,0:T(2,128)S(1)}, s32[4,2,8]{2,1,0:T(2,128)S(1)}, u32[]{:S(2)}, u32[]{:S(2)}) %collective-permute-start.6) | collective-permute-done | bytes 288 | tf_op jit(solution)/shard_map/ppermute | solution.py:167
  31.0 1.2 broadcast_select_fusion
  32.2 3.6 %all-to-all-start = ((bf16[8,2,64,512]{3,2,1,0:T(8,128)(2,1)}), bf16[8,2,64,512]{3,2,1,0:T(8,128)(2,1)S(1)}, u32[]{:S(2)}, u32[]{:S(2)}) async-start(bf16[8,2,64,512]{3,2,1,0:T(8,128)(2,1)} %broadcast_select_fusion), calls=%async_computation | async-start | bytes 2097152 | tf_op jit(solution)/shard_map/all_to_all | solution.py:229
  35.9 2.8 %collective-permute-start.2 = (bf16[32,8,512]{2,1,0:T(8,128)(2,1)S(1)}, bf16[32,8,512]{2,1,0:T(8,128)(2,1)S(1)}, u32[]{:S(2)}, u32[]{:S(2)}) collective-permute-start(bf16[32,8,512]{2,1,0:T(8,128)(2,1)S(1)} %get-tuple-element.38), channel_id=1, source_target_pairs={{0,1},{1,2},{2,3},{4,5},{5,6},{6,7},{8,9},{9,10},{10,11},{12,13},{... | collective-permute-start | bytes 786440 | tf_op jit(solution)/shard_map/ppermute | solution.py:24
  38.7 1.3 collective-permute-start.3
  40.1 1.3 collective-permute-start.10
  41.4 4.6 %collective-permute-start.9 = (bf16[8,32,512]{2,1,0:T(8,128)(2,1)S(1)}, bf16[8,32,512]{2,1,0:T(8,128)(2,1)S(1)}, u32[]{:S(2)}, u32[]{:S(2)}) collective-permute-start(bf16[8,32,512]{2,1,0:T(8,128)(2,1)S(1)} %get-tuple-element.36), channel_id=1, source_target_pairs={{0,4},{4,8},{8,12},{12,16},{16,20},{20,24},{24,28},{1,5},{5,9},{9,... | collective-permute-start | bytes 786440 | tf_op jit(solution)/shard_map/ppermute | solution.py:24
  48.4 4.4 %collective-permute-done.10 = bf16[8,32,512]{2,1,0:T(8,128)(2,1)S(1)} collective-permute-done((bf16[8,32,512]{2,1,0:T(8,128)(2,1)S(1)}, bf16[8,32,512]{2,1,0:T(8,128)(2,1)S(1)}, u32[]{:S(2)}, u32[]{:S(2)}) %collective-permute-start.10) | collective-permute-done | bytes 262176 | tf_op jit(solution)/shard_map/ppermute | solution.py:27
  52.9 4.8 %collective-permute-done.9 = bf16[8,32,512]{2,1,0:T(8,128)(2,1)S(1)} collective-permute-done((bf16[8,32,512]{2,1,0:T(8,128)(2,1)S(1)}, bf16[8,32,512]{2,1,0:T(8,128)(2,1)S(1)}, u32[]{:S(2)}, u32[]{:S(2)}) %collective-permute-start.9) | collective-permute-done | bytes 262176 | tf_op jit(solution)/shard_map/ppermute | solution.py:24
  64.0 1.0 select_dynamic-update-slice_fusion
  65.0 2.3 %slice_bitcast_fusion.1 = (bf16[2,2,88,2,8,128]{5,4,3,2,1,0:T(8,128)(2,1)S(1)}, bf16[2,2,88,2,8,128]{5,4,3,2,1,0:T(8,128)(2,1)S(1)}) fusion(bf16[2,2,704,512]{3,2,1,0:T(8,128)(2,1)} %select_dynamic-update-slice_fusion), kind=kLoop, calls=%fused_computation.14 | loop fusion | bytes 5767168
  68.6 1.2 multiply_reduce_fusion
  69.8 3.1 %fusion.62 = bf16[2,2,64,2,128]{4,2,3,1,0:T(8,128)(2,1)} fusion(bf16[2,2,88,2,8,128]{5,4,3,2,1,0:T(8,128)(2,1)S(1)} %get-tuple-element.6, f32[2,2,2,64,704]{4,3,2,1,0:T(8,128)S(1)} %get-tuple-element.84, bf16[2,2,88,2,8,128]{5,4,3,2,1,0:T(8,128)(2,1)} %copy-done.1, f32[2,2,2,64]{3,2,1,0:T(2,128)S(1)} %bitcast.270, f32[2,2,2,64]{3,2,1,0:T(2,128)S(1)} %log_add_fusion, ...), kind=kOutput, calls=%fused_computation.50 | convolution fusion | flops 186122240 | bytes 4591616 | tf_op jit(solution)/shard_map/abhqk,abkhe->abqhe/dot_general | solution.py:108
  72.9 1.1 copy.132
  74.4 5.2 %collective-permute-start.11 = (f32[16,8,4]{1,0,2:T(8,128)S(1)}, f32[16,8,4]{1,0,2:T(8,128)S(1)}, u32[]{:S(2)}, u32[]{:S(2)}) collective-permute-start(f32[16,8,4]{1,0,2:T(8,128)S(1)} %get-tuple-element.66), channel_id=1, source_target_pairs={{0,1},{1,2},{2,3},{4,5},{5,6},{6,7},{8,9},{9,10},{10,11},{12,13},{... | collective-permute-start | bytes 6152 | tf_op jit(solution)/shard_map/ppermute | solution.py:24
  79.6 1.3 collective-permute-start.12
  82.1 2.5 %collective-permute-done.12 = f32[16,8,4]{1,0,2:T(8,128)S(1)} collective-permute-done((f32[16,8,4]{1,0,2:T(8,128)S(1)}, f32[16,8,4]{1,0,2:T(8,128)S(1)}, u32[]{:S(2)}, u32[]{:S(2)}) %collective-permute-start.12) | collective-permute-done | bytes 2080 | tf_op jit(solution)/shard_map/ppermute | solution.py:27
  84.7 4.4 %collective-permute-start.13 = (f32[8,32,4]{1,0,2:T(8,128)S(1)}, f32[8,32,4]{1,0,2:T(8,128)S(1)}, u32[]{:S(2)}, u32[]{:S(2)}) collective-permute-start(f32[8,32,4]{1,0,2:T(8,128)S(1)} %get-tuple-element.64), channel_id=1, source_target_pairs={{0,4},{4,8},{8,12},{12,16},{16,20},{20,24},{24,28},{1,5},{5,9},{9,... | collective-permute-start | bytes 12296 | tf_op jit(solution)/shard_map/ppermute | solution.py:24
  89.1 1.5 collective-permute-start.14
  91.5 3.3 %collective-permute-done.14 = f32[8,32,4]{1,0,2:T(8,128)S(1)} collective-permute-done((f32[8,32,4]{1,0,2:T(8,128)S(1)}, f32[8,32,4]{1,0,2:T(8,128)S(1)}, u32[]{:S(2)}, u32[]{:S(2)}) %collective-permute-start.14) | collective-permute-done | bytes 4128 | tf_op jit(solution)/shard_map/ppermute | solution.py:27
  95.4 1.9 %fusion.9 = f32[2,2,2,576,64]{3,4,2,1,0:T(8,128)S(1)} fusion(f32[2,2,2,576]{3,2,1,0:T(2,128)S(1)} %concatenate.90, pred[2,2,576]{2,1,0:T(4,128)(4,1)S(1)} %copy-done.20, bf16[2,2,8,2,8,128]{5,4,3,2,1,0:T(8,128)(2,1)} %get-tuple-element.11, bf16[2,2,576,256]{3,2,1,0:T(8,128)(2,1)} %copy-done.19), kind=kOutput, calls=%fused_computation.20 | convolution fusion | flops 76382208 | bytes 2511104 | tf_op jit(solution)/shard_map/abqhe,abkhe->abhqk/dot_general | solution.py:126
  98.3 2.7 %fusion.57 = bf16[2,2,64,2,128]{4,2,3,1,0:T(8,128)(2,1)} fusion(f32[2,2,2,576,64]{3,4,2,1,0:T(8,128)S(1)} %fusion.9, f32[2,2,2,576]{3,2,1,0:T(2,128)S(1)} %concatenate.92, bf16[2,2,8,2,8,128]{5,4,3,2,1,0:T(8,128)(2,1)S(1)} %copy-done.18, bf16[2,2,576,256]{3,2,1,0:T(8,128)(2,1)S(1)} %copy-done.4, bf16[2,2,576,256]{3,2,1,0:T(8,128)(2,1)} %copy-done.19), kind=kOutput, calls=%fused_computation.49 | convolution fusion | flops 152010752 | bytes 3819520 | tf_op jit(solution)/shard_map/abhqk,abqhe->abkhe/dot_general | solution.py:135
  101.0 1.1 copy.142
  103.0 1.3 collective-permute-start.15
  104.3 1.5 %collective-permute-done.15 = f32[512,256]{1,0:T(8,128)S(1)} collective-permute-done((f32[512,256]{1,0:T(8,128)S(1)}, f32[512,256]{1,0:T(8,128)S(1)}, u32[]{:S(2)}, u32[]{:S(2)}) %collective-permute-start.15) | collective-permute-done | bytes 524320 | tf_op jit(solution)/shard_map/ppermute | solution.py:202
  106.0 1.6 %collective-permute-start.16 = (f32[256,256]{1,0:T(8,128)S(1)}, f32[256,256]{1,0:T(8,128)S(1)}, u32[]{:S(2)}, u32[]{:S(2)}) collective-permute-start(f32[256,256]{1,0:T(8,128)S(1)} %constant_dynamic-slice_fusion), channel_id=1, source_target_pairs={{0,2},{1,3},{2,0},{3,1},{4,6},{5,7},{6,4},{7,5},{8,10},{9,11},{10,... | collective-permute-start | bytes 786440 | tf_op jit(solution)/shard_map/ppermute | solution.py:202
  107.6 7.0 %collective-permute-done.16 = f32[256,256]{1,0:T(8,128)S(1)} collective-permute-done((f32[256,256]{1,0:T(8,128)S(1)}, f32[256,256]{1,0:T(8,128)S(1)}, u32[]{:S(2)}, u32[]{:S(2)}) %collective-permute-start.16) | collective-permute-done | bytes 262176 | tf_op jit(solution)/shard_map/ppermute | solution.py:202
  114.7 4.9 %collective-permute-start.17 = (f32[128,256]{1,0:T(8,128)S(1)}, f32[128,256]{1,0:T(8,128)S(1)}, u32[]{:S(2)}, u32[]{:S(2)}) collective-permute-start(f32[128,256]{1,0:T(8,128)S(1)} %constant_dynamic-slice_fusion.2), channel_id=1, source_target_pairs={{0,4},{4,0},{8,12},{12,8},{16,20},{20,16},{24,28},{28,24},{1,5},{5... | collective-permute-start | bytes 393224 | tf_op jit(solution)/shard_map/ppermute | solution.py:202
  119.6 3.2 %collective-permute-done.17 = f32[128,256]{1,0:T(8,128)S(1)} collective-permute-done((f32[128,256]{1,0:T(8,128)S(1)}, f32[128,256]{1,0:T(8,128)S(1)}, u32[]{:S(2)}, u32[]{:S(2)}) %collective-permute-start.17) | collective-permute-done | bytes 131104 | tf_op jit(solution)/shard_map/ppermute | solution.py:202
  122.8 2.5 %collective-permute-start.18 = (f32[128,256]{1,0:T(8,128)S(1)}, f32[128,256]{1,0:T(8,128)S(1)}, u32[]{:S(2)}, u32[]{:S(2)}) collective-permute-start(f32[128,256]{1,0:T(8,128)S(1)} %dynamic-slice_add_fusion.2), channel_id=1, source_target_pairs={{0,8},{4,12},{8,0},{12,4},{16,24},{20,28},{24,16},{28,20},{1,9},{5... | collective-permute-start | bytes 393224 | tf_op jit(solution)/shard_map/ppermute | solution.py:205
  125.3 2.9 %collective-permute-done.18 = f32[128,256]{1,0:T(8,128)S(1)} collective-permute-done((f32[128,256]{1,0:T(8,128)S(1)}, f32[128,256]{1,0:T(8,128)S(1)}, u32[]{:S(2)}, u32[]{:S(2)}) %collective-permute-start.18) | collective-permute-done | bytes 131104 | tf_op jit(solution)/shard_map/ppermute | solution.py:205
  128.3 2.1 %collective-permute-start.19 = (f32[128,256]{1,0:T(8,128)S(1)}, f32[128,256]{1,0:T(8,128)S(1)}, u32[]{:S(2)}, u32[]{:S(2)}) collective-permute-start(f32[128,256]{1,0:T(8,128)S(1)} %add.165), channel_id=1, source_target_pairs={{0,16},{4,20},{8,24},{12,28},{16,0},{20,4},{24,8},{28,12},{1,17},{... | collective-permute-start | bytes 393224 | tf_op jit(solution)/shard_map/ppermute | solution.py:205
  130.4 3.8 %collective-permute-done.19 = f32[128,256]{1,0:T(8,128)S(1)} collective-permute-done((f32[128,256]{1,0:T(8,128)S(1)}, f32[128,256]{1,0:T(8,128)S(1)}, u32[]{:S(2)}, u32[]{:S(2)}) %collective-permute-start.19) | collective-permute-done | bytes 131104 | tf_op jit(solution)/shard_map/ppermute | solution.py:205
  134.2 2.4 %collective-permute-start.20 = (f32[128,256]{1,0:T(8,128)S(1)}, f32[128,256]{1,0:T(8,128)S(1)}, u32[]{:S(2)}, u32[]{:S(2)}) collective-permute-start(f32[128,256]{1,0:T(8,128)S(1)} %add.166), channel_id=1, source_target_pairs={{0,4},{4,0},{8,12},{12,8},{16,20},{20,16},{24,28},{28,24},{1,5},{5... | collective-permute-start | bytes 393224 | tf_op jit(solution)/shard_map/ppermute | solution.py:167
  136.6 2.9 %collective-permute-done.20 = f32[128,256]{1,0:T(8,128)S(1)} collective-permute-done((f32[128,256]{1,0:T(8,128)S(1)}, f32[128,256]{1,0:T(8,128)S(1)}, u32[]{:S(2)}, u32[]{:S(2)}) %collective-permute-start.20) | collective-permute-done | bytes 131104 | tf_op jit(solution)/shard_map/ppermute | solution.py:167
  139.7 1.5 %collective-permute-start.21 = (f32[256,256]{1,0:T(8,128)S(1)}, f32[256,256]{1,0:T(8,128)S(1)}, u32[]{:S(2)}, u32[]{:S(2)}) collective-permute-start(f32[256,256]{1,0:T(8,128)S(1)} %pad_maximum_fusion.6), channel_id=1, source_target_pairs={{0,2},{1,3},{2,0},{3,1},{4,6},{5,7},{6,4},{7,5},{8,10},{9,11},{10,... | collective-permute-start | bytes 786440 | tf_op jit(solution)/shard_map/ppermute | solution.py:167
  141.2 4.9 %collective-permute-done.21 = f32[256,256]{1,0:T(8,128)S(1)} collective-permute-done((f32[256,256]{1,0:T(8,128)S(1)}, f32[256,256]{1,0:T(8,128)S(1)}, u32[]{:S(2)}, u32[]{:S(2)}) %collective-permute-start.21) | collective-permute-done | bytes 262176 | tf_op jit(solution)/shard_map/ppermute | solution.py:167
  147.1 1.0 convolution_convert_fusion.1
  (197 shorter events, 25.4 us)
Async XLA Ops:
  0.6 29.8 %copy-start = (bf16[1,1,4,64,512]{4,3,2,1,0:T(8,128)(2,1)S(1)}, bf16[1,1,4,64,512]{4,3,2,1,0:T(8,128)(2,1)}, u32[]{:S(2)}) copy-start(bf16[1,1,4,64,512]{4,3,2,1,0:T(8,128)(2,1)} %param.15) | copy-start | bytes 786436
  0.6 16.3 %copy-start.22 = (s32[8]{0:T(128)S(1)}, s32[8]{0:T(128)}, u32[]{:S(2)}) copy-start(s32[8]{0:T(128)} %constant.166) | copy-start | bytes 100
  0.7 16.1 %copy-start.21 = (s32[1,1,4,2]{2,3,1,0:T(2,128)S(1)}, s32[1,1,4,2]{2,3,1,0:T(2,128)}, u32[]{:S(2)}) copy-start(s32[1,1,4,2]{2,3,1,0:T(2,128)} %param.16) | copy-start | bytes 100
  0.7 13.1 %copy-start.10 = (bf16[16,16,256]{2,1,0:T(8,128)(2,1)S(1)}, bf16[16,16,256]{2,1,0:T(8,128)(2,1)}, u32[]{:S(2)}) copy-start(bf16[16,16,256]{2,1,0:T(8,128)(2,1)} %param.18) | copy-start | bytes 393220
  0.7 13.1 %copy-start.7 = (bf16[256,256]{1,0:T(8,128)(2,1)S(1)}, bf16[256,256]{1,0:T(8,128)(2,1)}, u32[]{:S(2)}) copy-start(bf16[256,256]{1,0:T(8,128)(2,1)} %param.14) | copy-start | bytes 393220
  2.5 17.7 %collective-permute-start.4 = (s32[1,2,8]{2,1,0:T(2,128)S(1)}, s32[1,2,8]{2,1,0:T(2,128)S(1)}, u32[]{:S(2)}, u32[]{:S(2)}) collective-permute-start(s32[1,2,8]{2,1,0:T(2,128)S(1)} %add_bitcast_fusion), channel_id=1, source_target_pairs={{0,16},{4,20},{8,24},{12,28},{16,0},{20,4},{24,8},{28,12},{1,17},{... | collective-permute-start | bytes 200 | tf_op jit(solution)/shard_map/ppermute | solution.py:167
  7.9 27.9 %collective-permute-start = (bf16[8,16,512]{2,1,0:T(8,128)(2,1)S(1)}, bf16[8,16,512]{2,1,0:T(8,128)(2,1)S(1)}, u32[]{:S(2)}, u32[]{:S(2)}) collective-permute-start(bf16[8,16,512]{2,1,0:T(8,128)(2,1)S(1)} %bitcast.269), channel_id=1, source_target_pairs={{0,4},{4,8},{8,12},{12,16},{16,20},{20,24},{24,28},{1,5},{5,9},{9,... | collective-permute-start | bytes 393224 | tf_op jit(solution)/shard_map/ppermute | solution.py:24
  11.3 24.5 %collective-permute-start.1 = (bf16[8,16,512]{2,1,0:T(8,128)(2,1)S(1)}, bf16[8,16,512]{2,1,0:T(8,128)(2,1)S(1)}, u32[]{:S(2)}, u32[]{:S(2)}) collective-permute-start(bf16[8,16,512]{2,1,0:T(8,128)(2,1)S(1)} %bitcast.268), channel_id=1, source_target_pairs={{4,0},{8,4},{12,8},{16,12},{20,16},{24,20},{28,24},{5,1},{9,5},{13... | collective-permute-start | bytes 393224 | tf_op jit(solution)/shard_map/ppermute | solution.py:27
  14.0 26.0 %collective-permute-start.7 = (bf16[16,8,512]{2,1,0:T(8,128)(2,1)S(1)}, bf16[16,8,512]{2,1,0:T(8,128)(2,1)S(1)}, u32[]{:S(2)}, u32[]{:S(2)}) collective-permute-start(bf16[16,8,512]{2,1,0:T(8,128)(2,1)S(1)} %get-tuple-element.42), channel_id=1, source_target_pairs={{0,1},{1,2},{2,3},{4,5},{5,6},{6,7},{8,9},{9,10},{10,11},{12,13},{... | collective-permute-start | bytes 393224 | tf_op jit(solution)/shard_map/ppermute | solution.py:24
  15.3 24.7 %collective-permute-start.8 = (bf16[16,8,512]{2,1,0:T(8,128)(2,1)S(1)}, bf16[16,8,512]{2,1,0:T(8,128)(2,1)S(1)}, u32[]{:S(2)}, u32[]{:S(2)}) collective-permute-start(bf16[16,8,512]{2,1,0:T(8,128)(2,1)S(1)} %get-tuple-element.43), channel_id=1, source_target_pairs={{1,0},{2,1},{3,2},{5,4},{6,5},{7,6},{9,8},{10,9},{11,10},{13,12},{... | collective-permute-start | bytes 393224 | tf_op jit(solution)/shard_map/ppermute | solution.py:27
  20.1 48.5 %copy-start.8 = (bf16[2,2,64,2,128]{4,3,2,1,0:T(2,128)(2,1)}, bf16[2,2,64,2,128]{4,3,2,1,0:T(2,128)(2,1)S(1)}, u32[]{:S(2)}) copy-start(bf16[2,2,64,2,128]{4,3,2,1,0:T(2,128)(2,1)S(1)} %reshape_reshape.32) | copy-start | bytes 393220
  20.2 5.2 %collective-permute-start.5 = (s32[2,2,8]{2,1,0:T(2,128)S(1)}, s32[2,2,8]{2,1,0:T(2,128)S(1)}, u32[]{:S(2)}, u32[]{:S(2)}) collective-permute-start(s32[2,2,8]{2,1,0:T(2,128)S(1)} %pad_add_fusion.2), channel_id=1, source_target_pairs={{0,8},{4,12},{8,0},{12,4},{16,24},{20,28},{24,16},{28,20},{1,9},{5... | collective-permute-start | bytes 392 | tf_op jit(solution)/shard_map/ppermute | solution.py:167
  25.5 3.7 %collective-permute-start.6 = (s32[4,2,8]{2,1,0:T(2,128)S(1)}, s32[4,2,8]{2,1,0:T(2,128)S(1)}, u32[]{:S(2)}, u32[]{:S(2)}) collective-permute-start(s32[4,2,8]{2,1,0:T(2,128)S(1)} %pad_add_fusion.1), channel_id=1, source_target_pairs={{0,4},{4,0},{8,12},{12,8},{16,20},{20,16},{24,28},{28,24},{1,5},{5... | collective-permute-start | bytes 776 | tf_op jit(solution)/shard_map/ppermute | solution.py:167
  32.2 31.2 %all-to-all-start = ((bf16[8,2,64,512]{3,2,1,0:T(8,128)(2,1)}), bf16[8,2,64,512]{3,2,1,0:T(8,128)(2,1)S(1)}, u32[]{:S(2)}, u32[]{:S(2)}) async-start(bf16[8,2,64,512]{3,2,1,0:T(8,128)(2,1)} %broadcast_select_fusion), calls=%async_computation | async-start | bytes 2097152 | tf_op jit(solution)/shard_map/all_to_all | solution.py:229
  35.9 10.1 %collective-permute-start.2 = (bf16[32,8,512]{2,1,0:T(8,128)(2,1)S(1)}, bf16[32,8,512]{2,1,0:T(8,128)(2,1)S(1)}, u32[]{:S(2)}, u32[]{:S(2)}) collective-permute-start(bf16[32,8,512]{2,1,0:T(8,128)(2,1)S(1)} %get-tuple-element.38), channel_id=1, source_target_pairs={{0,1},{1,2},{2,3},{4,5},{5,6},{6,7},{8,9},{9,10},{10,11},{12,13},{... | collective-permute-start | bytes 786440 | tf_op jit(solution)/shard_map/ppermute | solution.py:24
  38.7 7.3 %collective-permute-start.3 = (bf16[32,8,512]{2,1,0:T(8,128)(2,1)S(1)}, bf16[32,8,512]{2,1,0:T(8,128)(2,1)S(1)}, u32[]{:S(2)}, u32[]{:S(2)}) collective-permute-start(bf16[32,8,512]{2,1,0:T(8,128)(2,1)S(1)} %get-tuple-element.39), channel_id=1, source_target_pairs={{1,0},{2,1},{3,2},{5,4},{6,5},{7,6},{9,8},{10,9},{11,10},{13,12},{... | collective-permute-start | bytes 786440 | tf_op jit(solution)/shard_map/ppermute | solution.py:27
  40.1 12.7 %collective-permute-start.10 = (bf16[8,32,512]{2,1,0:T(8,128)(2,1)S(1)}, bf16[8,32,512]{2,1,0:T(8,128)(2,1)S(1)}, u32[]{:S(2)}, u32[]{:S(2)}) collective-permute-start(bf16[8,32,512]{2,1,0:T(8,128)(2,1)S(1)} %get-tuple-element.37), channel_id=1, source_target_pairs={{4,0},{8,4},{12,8},{16,12},{20,16},{24,20},{28,24},{5,1},{9,5},{13... | collective-permute-start | bytes 786440 | tf_op jit(solution)/shard_map/ppermute | solution.py:27
  41.4 16.3 %collective-permute-start.9 = (bf16[8,32,512]{2,1,0:T(8,128)(2,1)S(1)}, bf16[8,32,512]{2,1,0:T(8,128)(2,1)S(1)}, u32[]{:S(2)}, u32[]{:S(2)}) collective-permute-start(bf16[8,32,512]{2,1,0:T(8,128)(2,1)S(1)} %get-tuple-element.36), channel_id=1, source_target_pairs={{0,4},{4,8},{8,12},{12,16},{16,20},{20,24},{24,28},{1,5},{5,9},{9,... | collective-permute-start | bytes 786440 | tf_op jit(solution)/shard_map/ppermute | solution.py:24
  58.2 4.5 %copy-start.3 = (bf16[2,2,576,256]{3,2,1,0:T(8,128)(2,1)}, bf16[2,2,576,256]{3,2,1,0:T(8,128)(2,1)S(1)}, u32[]{:S(2)}) copy-start(bf16[2,2,576,256]{3,2,1,0:T(8,128)(2,1)S(1)} %get-tuple-element.13) | copy-start | bytes 3538948
  58.2 4.5 %copy-start.19 = (bf16[2,2,576,256]{3,2,1,0:T(8,128)(2,1)}, bf16[2,2,576,256]{3,2,1,0:T(8,128)(2,1)S(1)}, u32[]{:S(2)}) copy-start(bf16[2,2,576,256]{3,2,1,0:T(8,128)(2,1)S(1)} %get-tuple-element.12) | copy-start | bytes 3538948
  65.0 2.3 %copy-start.14 = (bf16[2,2,64,2,128]{4,3,2,1,0:T(2,128)(2,1)S(1)}, bf16[2,2,64,2,128]{4,3,2,1,0:T(2,128)(2,1)}, u32[]{:S(2)}) copy-start(bf16[2,2,64,2,128]{4,3,2,1,0:T(2,128)(2,1)} %reshape_reshape.29) | copy-start | bytes 393220
  67.3 1.3 copy-start.1
  69.8 11.1 %copy-start.2 = (bf16[16,16,256]{2,1,0:T(8,128)(2,1)S(1)}, bf16[16,16,256]{2,1,0:T(8,128)(2,1)}, u32[]{:S(2)}) copy-start(bf16[16,16,256]{2,1,0:T(8,128)(2,1)} %param.10) | copy-start | bytes 393220
  72.9 9.0 %copy-start.9 = (bf16[2,2,64,2,128]{4,2,3,1,0:T(8,128)(2,1)S(1)}, bf16[2,2,64,2,128]{4,2,3,1,0:T(8,128)(2,1)}, u32[]{:S(2)}) copy-start(bf16[2,2,64,2,128]{4,2,3,1,0:T(8,128)(2,1)} %get-tuple-element.86) | copy-start | bytes 393220
  72.9 17.7 %copy-start.11 = (bf16[16,16,256]{2,1,0:T(8,128)(2,1)S(1)}, bf16[16,16,256]{2,1,0:T(8,128)(2,1)}, u32[]{:S(2)}) copy-start(bf16[16,16,256]{2,1,0:T(8,128)(2,1)} %param.18) | copy-start | bytes 393220
  74.1 7.7 %copy-start.12 = (bf16[2,8,2,8,256]{4,3,2,1,0:T(8,128)(2,1)}, bf16[2,8,2,8,256]{4,3,2,1,0:T(8,128)(2,1)S(1)}, u32[]{:S(2)}) copy-start(bf16[2,8,2,8,256]{4,3,2,1,0:T(8,128)(2,1)S(1)} %copy.133) | copy-start | bytes 393220
  74.4 7.7 %collective-permute-start.11 = (f32[16,8,4]{1,0,2:T(8,128)S(1)}, f32[16,8,4]{1,0,2:T(8,128)S(1)}, u32[]{:S(2)}, u32[]{:S(2)}) collective-permute-start(f32[16,8,4]{1,0,2:T(8,128)S(1)} %get-tuple-element.66), channel_id=1, source_target_pairs={{0,1},{1,2},{2,3},{4,5},{5,6},{6,7},{8,9},{9,10},{10,11},{12,13},{... | collective-permute-start | bytes 6152 | tf_op jit(solution)/shard_map/ppermute | solution.py:24
  79.6 5.0 %collective-permute-start.12 = (f32[16,8,4]{1,0,2:T(8,128)S(1)}, f32[16,8,4]{1,0,2:T(8,128)S(1)}, u32[]{:S(2)}, u32[]{:S(2)}) collective-permute-start(f32[16,8,4]{1,0,2:T(8,128)S(1)} %get-tuple-element.67), channel_id=1, source_target_pairs={{1,0},{2,1},{3,2},{5,4},{6,5},{7,6},{9,8},{10,9},{11,10},{13,12},{... | collective-permute-start | bytes 6152 | tf_op jit(solution)/shard_map/ppermute | solution.py:27
  82.0 13.5 %copy-start.20 = (pred[2,2,576]{2,1,0:T(4,128)(4,1)S(1)}, pred[2,2,576]{2,1,0:T(4,128)(4,1)}, u32[]{:S(2)}) copy-start(pred[2,2,576]{2,1,0:T(4,128)(4,1)} %concatenate.86) | copy-start | bytes 6916
  84.7 6.8 %collective-permute-start.13 = (f32[8,32,4]{1,0,2:T(8,128)S(1)}, f32[8,32,4]{1,0,2:T(8,128)S(1)}, u32[]{:S(2)}, u32[]{:S(2)}) collective-permute-start(f32[8,32,4]{1,0,2:T(8,128)S(1)} %get-tuple-element.64), channel_id=1, source_target_pairs={{0,4},{4,8},{8,12},{12,16},{16,20},{20,24},{24,28},{1,5},{5,9},{9,... | collective-permute-start | bytes 12296 | tf_op jit(solution)/shard_map/ppermute | solution.py:24
  89.1 5.7 %collective-permute-start.14 = (f32[8,32,4]{1,0,2:T(8,128)S(1)}, f32[8,32,4]{1,0,2:T(8,128)S(1)}, u32[]{:S(2)}, u32[]{:S(2)}) collective-permute-start(f32[8,32,4]{1,0,2:T(8,128)S(1)} %get-tuple-element.65), channel_id=1, source_target_pairs={{4,0},{8,4},{12,8},{16,12},{20,16},{24,20},{28,24},{5,1},{9,5},{13... | collective-permute-start | bytes 12296 | tf_op jit(solution)/shard_map/ppermute | solution.py:27
  95.4 1.9 %copy-start.4 = (bf16[2,2,576,256]{3,2,1,0:T(8,128)(2,1)S(1)}, bf16[2,2,576,256]{3,2,1,0:T(8,128)(2,1)}, u32[]{:S(2)}) copy-start(bf16[2,2,576,256]{3,2,1,0:T(8,128)(2,1)} %copy-done.3) | copy-start | bytes 3538948
  97.4 0.9 copy-start.18
  100.9 1.9 %copy-start.5 = (f32[256,256]{1,0:T(8,128)S(1)}, f32[256,256]{1,0:T(8,128)}, u32[]{:S(2)}) copy-start(f32[256,256]{1,0:T(8,128)} %convolution_bitcast_fusion.2) | copy-start | bytes 786436
  100.9 2.0 %copy-start.6 = (f32[256,256]{1,0:T(8,128)S(1)}, f32[256,256]{1,0:T(8,128)}, u32[]{:S(2)}) copy-start(f32[256,256]{1,0:T(8,128)} %fusion.116) | copy-start | bytes 786436
  103.0 2.8 %collective-permute-start.15 = (f32[512,256]{1,0:T(8,128)S(1)}, f32[512,256]{1,0:T(8,128)S(1)}, u32[]{:S(2)}, u32[]{:S(2)}) collective-permute-start(f32[512,256]{1,0:T(8,128)S(1)} %constant_dynamic-slice_fusion.1), channel_id=1, source_target_pairs={{0,1},{1,0},{2,3},{3,2},{4,5},{5,4},{6,7},{7,6},{8,9},{9,8},{10,11... | collective-permute-start | bytes 1572872 | tf_op jit(solution)/shard_map/ppermute | solution.py:202
  106.0 8.7 %collective-permute-start.16 = (f32[256,256]{1,0:T(8,128)S(1)}, f32[256,256]{1,0:T(8,128)S(1)}, u32[]{:S(2)}, u32[]{:S(2)}) collective-permute-start(f32[256,256]{1,0:T(8,128)S(1)} %constant_dynamic-slice_fusion), channel_id=1, source_target_pairs={{0,2},{1,3},{2,0},{3,1},{4,6},{5,7},{6,4},{7,5},{8,10},{9,11},{10,... | collective-permute-start | bytes 786440 | tf_op jit(solution)/shard_map/ppermute | solution.py:202
  114.7 8.1 %collective-permute-start.17 = (f32[128,256]{1,0:T(8,128)S(1)}, f32[128,256]{1,0:T(8,128)S(1)}, u32[]{:S(2)}, u32[]{:S(2)}) collective-permute-start(f32[128,256]{1,0:T(8,128)S(1)} %constant_dynamic-slice_fusion.2), channel_id=1, source_target_pairs={{0,4},{4,0},{8,12},{12,8},{16,20},{20,16},{24,28},{28,24},{1,5},{5... | collective-permute-start | bytes 393224 | tf_op jit(solution)/shard_map/ppermute | solution.py:202
  122.8 5.4 %collective-permute-start.18 = (f32[128,256]{1,0:T(8,128)S(1)}, f32[128,256]{1,0:T(8,128)S(1)}, u32[]{:S(2)}, u32[]{:S(2)}) collective-permute-start(f32[128,256]{1,0:T(8,128)S(1)} %dynamic-slice_add_fusion.2), channel_id=1, source_target_pairs={{0,8},{4,12},{8,0},{12,4},{16,24},{20,28},{24,16},{28,20},{1,9},{5... | collective-permute-start | bytes 393224 | tf_op jit(solution)/shard_map/ppermute | solution.py:205
  128.3 5.9 %collective-permute-start.19 = (f32[128,256]{1,0:T(8,128)S(1)}, f32[128,256]{1,0:T(8,128)S(1)}, u32[]{:S(2)}, u32[]{:S(2)}) collective-permute-start(f32[128,256]{1,0:T(8,128)S(1)} %add.165), channel_id=1, source_target_pairs={{0,16},{4,20},{8,24},{12,28},{16,0},{20,4},{24,8},{28,12},{1,17},{... | collective-permute-start | bytes 393224 | tf_op jit(solution)/shard_map/ppermute | solution.py:205
  134.2 5.3 %collective-permute-start.20 = (f32[128,256]{1,0:T(8,128)S(1)}, f32[128,256]{1,0:T(8,128)S(1)}, u32[]{:S(2)}, u32[]{:S(2)}) collective-permute-start(f32[128,256]{1,0:T(8,128)S(1)} %add.166), channel_id=1, source_target_pairs={{0,4},{4,0},{8,12},{12,8},{16,20},{20,16},{24,28},{28,24},{1,5},{5... | collective-permute-start | bytes 393224 | tf_op jit(solution)/shard_map/ppermute | solution.py:167
  139.6 7.5 %copy-start.13 = (bf16[2,8,2,8,256]{4,3,2,1,0:T(8,128)(2,1)S(1)}, bf16[2,8,2,8,256]{4,3,2,1,0:T(8,128)(2,1)}, u32[]{:S(2)}) copy-start(bf16[2,8,2,8,256]{4,3,2,1,0:T(8,128)(2,1)} %copy-done.12) | copy-start | bytes 393220
  139.6 7.5 %copy-start.15 = (bf16[256,256]{1,0:T(8,128)(2,1)S(1)}, bf16[256,256]{1,0:T(8,128)(2,1)}, u32[]{:S(2)}) copy-start(bf16[256,256]{1,0:T(8,128)(2,1)} %param.13) | copy-start | bytes 393220
  139.6 7.5 %copy-start.16 = (bf16[256,256]{1,0:T(8,128)(2,1)S(1)}, bf16[256,256]{1,0:T(8,128)(2,1)}, u32[]{:S(2)}) copy-start(bf16[256,256]{1,0:T(8,128)(2,1)} %param.12) | copy-start | bytes 393220
  139.6 7.5 %copy-start.17 = (bf16[256,256]{1,0:T(8,128)(2,1)S(1)}, bf16[256,256]{1,0:T(8,128)(2,1)}, u32[]{:S(2)}) copy-start(bf16[256,256]{1,0:T(8,128)(2,1)} %param.11) | copy-start | bytes 393220
  139.7 6.4 %collective-permute-start.21 = (f32[256,256]{1,0:T(8,128)S(1)}, f32[256,256]{1,0:T(8,128)S(1)}, u32[]{:S(2)}, u32[]{:S(2)}) collective-permute-start(f32[256,256]{1,0:T(8,128)S(1)} %pad_maximum_fusion.6), channel_id=1, source_target_pairs={{0,2},{1,3},{2,0},{3,1},{4,6},{5,7},{6,4},{7,5},{8,10},{9,11},{10,... | collective-permute-start | bytes 786440 | tf_op jit(solution)/shard_map/ppermute | solution.py:167
  146.2 2.0 %collective-permute-start.22 = (f32[512,256]{1,0:T(8,128)S(1)}, f32[512,256]{1,0:T(8,128)S(1)}, u32[]{:S(2)}, u32[]{:S(2)}) collective-permute-start(f32[512,256]{1,0:T(8,128)S(1)} %pad_maximum_fusion.5), channel_id=1, source_target_pairs={{0,1},{1,0},{2,3},{3,2},{4,5},{5,4},{6,7},{7,6},{8,9},{9,8},{10,11... | collective-permute-start | bytes 1572872 | tf_op jit(solution)/shard_map/ppermute | solution.py:167

commit v19 on v17

--- a/solution.py
+++ b/solution.py
@@ -286,7 +286,7 @@
         ],
         -1,
     )
-    query_halo = padded(query_grid, (("gy", 1), ("gx", 0)), BSIDE)
+    query_halo = padded(query_grid, (("gx", 0), ("gy", 1)), BSIDE)
     stat_grid = from_blocks(jnp.concatenate([log_totals, delta_rows], 2).transpose(0, 1, 3, 2))
     stat_halo = padded(stat_grid, (("gy", 1), ("gx", 0)), BSIDE)
     query_all = to_blocks(query_halo)

time: 159 us -> 153 us (0.962)
  waiting for transfers between devices: 60.2 us -> 49.6 us
  starting transfers between devices: 52.2 us -> 56.7 us
    ppermute x6, waiting for transfers between devices: 19.8 us -> 13.2 us  [padded(): lax.ppermute(lax.slice_in_dim(block, block.shape[dim] - width, None, axis...]
    ppermute x3, starting transfers between devices: 5.72 us -> 8.68 us  [tree_sum(): joined = keep + lax.ppermute(send, axis, pairs)]
    ppermute x6, starting transfers between devices: 10.5 us -> 12.9 us  [doubling_gather(): got = lax.ppermute(joined, axis, pairs)]
    ppermute x2, waiting for transfers between devices: 8.97 us -> 6.76 us  [tree_sum(): joined = joined + lax.ppermute(joined, axis, pairs)]
    ppermute x6, starting transfers between devices: 20.9 us -> 19 us  [padded(): lax.ppermute(lax.slice_in_dim(block, block.shape[dim] - width, None, axis...]
  transfers between devices with their start and end apart: 24 -> 24, of which waited for: 14 -> 13; matrix products, arithmetic and copies ran while one was open for 13% -> 14% of each run, Pallas kernels for 0% -> 0%
where the time goes in v19:
time: 153 us; the launch traced here: 152 us
  starting transfers between devices  56.7 us (37%)
  waiting for transfers between devices  49.6 us (32%)
  local copies, waits for them, and re-layouts  23.2 us (15%)
  matrix products  16.7 us (11%)
  other arithmetic  4.27 us (3%)
  between operations  1.65 us (1%)
    ppermute x6, starting transfers between devices, padded(): lax.ppermute(lax.slice_in_dim(block, block.shape[dim] - width, None, axis...  19 us
    ppermute x6, waiting for transfers between devices, padded(): lax.ppermute(lax.slice_in_dim(block, block.shape[dim] - width, None, axis...  13.2 us
    ppermute x6, starting transfers between devices, doubling_gather(): got = lax.ppermute(joined, axis, pairs)  12.9 us
    ppermute x6, waiting for transfers between devices, doubling_gather(): got = lax.ppermute(joined, axis, pairs)  12 us
    unnamed x68, local copies, waits for them, and re-layouts  12 us
    ppermute x3, waiting for transfers between devices, tree_sum(): joined = keep + lax.ppermute(send, axis, pairs)  11.9 us
    ppermute x3, starting transfers between devices, tree_sum(): joined = keep + lax.ppermute(send, axis, pairs)  8.68 us
    ppermute x6, starting transfers between devices, padded(): lax.ppermute(lax.slice_in_dim(block, 0, width, axis=dim), axis, backward)  7.93 us
  transfers between devices with their start and end apart: 24, of which 13 were waited for; matrix products, arithmetic and copies ran while one was open for 14% of the time, Pallas kernels for 0%

profile of v19, /device:TPU:0, one launch (start us, length us, event | category | flops | bytes accessed | tf_op | source)
XLA Modules:
  0.0 152.0 jit_solution(16329914477640957465)
XLA Ops:
  2.5 4.1 %collective-permute-start.4 = (s32[1,2,8]{2,1,0:T(2,128)S(1)}, s32[1,2,8]{2,1,0:T(2,128)S(1)}, u32[]{:S(2)}, u32[]{:S(2)}) collective-permute-start(s32[1,2,8]{2,1,0:T(2,128)S(1)} %add_bitcast_fusion), channel_id=1, source_target_pairs={{0,16},{4,20},{8,24},{12,28},{16,0},{20,4},{24,8},{28,12},{1,17},{... | collective-permute-start | bytes 200 | tf_op jit(solution)/shard_map/ppermute | solution.py:167
  6.6 1.3 convolution_convert_fusion
  7.9 1.5 collective-permute-start
  9.3 1.3 collective-permute-start.1
  10.6 1.2 convolution_convert_fusion.4
  12.1 3.4 %collective-permute-start.7 = (bf16[8,16,512]{2,1,0:T(8,128)(2,1)S(1)}, bf16[8,16,512]{2,1,0:T(8,128)(2,1)S(1)}, u32[]{:S(2)}, u32[]{:S(2)}) collective-permute-start(bf16[8,16,512]{2,1,0:T(8,128)(2,1)S(1)} %get-tuple-element.42), channel_id=1, source_target_pairs={{0,4},{4,8},{8,12},{12,16},{16,20},{20,24},{24,28},{1,5},{5,9},{9,... | collective-permute-start | bytes 393224 | tf_op jit(solution)/shard_map/ppermute | solution.py:24
  15.5 1.3 collective-permute-start.8
  20.4 3.7 %collective-permute-start.5 = (s32[2,2,8]{2,1,0:T(2,128)S(1)}, s32[2,2,8]{2,1,0:T(2,128)S(1)}, u32[]{:S(2)}, u32[]{:S(2)}) collective-permute-start(s32[2,2,8]{2,1,0:T(2,128)S(1)} %pad_add_fusion.2), channel_id=1, source_target_pairs={{0,8},{4,12},{8,0},{12,4},{16,24},{20,28},{24,16},{28,20},{1,9},{5... | collective-permute-start | bytes 392 | tf_op jit(solution)/shard_map/ppermute | solution.py:167
  24.1 1.6 %collective-permute-done.5 = s32[2,2,8]{2,1,0:T(2,128)S(1)} collective-permute-done((s32[2,2,8]{2,1,0:T(2,128)S(1)}, s32[2,2,8]{2,1,0:T(2,128)S(1)}, u32[]{:S(2)}, u32[]{:S(2)}) %collective-permute-start.5) | collective-permute-done | bytes 160 | tf_op jit(solution)/shard_map/ppermute | solution.py:167
  25.6 1.1 collective-permute-start.6
  26.7 2.6 %collective-permute-done.6 = s32[4,2,8]{2,1,0:T(2,128)S(1)} collective-permute-done((s32[4,2,8]{2,1,0:T(2,128)S(1)}, s32[4,2,8]{2,1,0:T(2,128)S(1)}, u32[]{:S(2)}, u32[]{:S(2)}) %collective-permute-start.6) | collective-permute-done | bytes 288 | tf_op jit(solution)/shard_map/ppermute | solution.py:167
  31.2 1.2 broadcast_select_fusion
  32.4 3.6 %all-to-all-start = ((bf16[8,2,64,512]{3,2,1,0:T(8,128)(2,1)}), bf16[8,2,64,512]{3,2,1,0:T(8,128)(2,1)S(1)}, u32[]{:S(2)}, u32[]{:S(2)}) async-start(bf16[8,2,64,512]{3,2,1,0:T(8,128)(2,1)} %broadcast_select_fusion), calls=%async_computation | async-start | bytes 2097152 | tf_op jit(solution)/shard_map/all_to_all | solution.py:229
  36.1 3.8 %collective-permute-start.2 = (bf16[8,32,512]{2,1,0:T(8,128)(2,1)S(1)}, bf16[8,32,512]{2,1,0:T(8,128)(2,1)S(1)}, u32[]{:S(2)}, u32[]{:S(2)}) collective-permute-start(bf16[8,32,512]{2,1,0:T(8,128)(2,1)S(1)} %get-tuple-element.38), channel_id=1, source_target_pairs={{0,4},{4,8},{8,12},{12,16},{16,20},{20,24},{24,28},{1,5},{5,9},{9,... | collective-permute-start | bytes 786440 | tf_op jit(solution)/shard_map/ppermute | solution.py:24
  39.9 1.3 collective-permute-start.3
  41.3 1.3 collective-permute-start.10
  42.6 3.0 %collective-permute-start.9 = (bf16[32,8,512]{2,1,0:T(8,128)(2,1)S(1)}, bf16[32,8,512]{2,1,0:T(8,128)(2,1)S(1)}, u32[]{:S(2)}, u32[]{:S(2)}) collective-permute-start(bf16[32,8,512]{2,1,0:T(8,128)(2,1)S(1)} %get-tuple-element.36), channel_id=1, source_target_pairs={{0,1},{1,2},{2,3},{4,5},{5,6},{6,7},{8,9},{9,10},{10,11},{12,13},{... | collective-permute-start | bytes 786440 | tf_op jit(solution)/shard_map/ppermute | solution.py:24
  45.7 13.2 %collective-permute-done.2 = bf16[8,32,512]{2,1,0:T(8,128)(2,1)S(1)} collective-permute-done((bf16[8,32,512]{2,1,0:T(8,128)(2,1)S(1)}, bf16[8,32,512]{2,1,0:T(8,128)(2,1)S(1)}, u32[]{:S(2)}, u32[]{:S(2)}) %collective-permute-start.2) | collective-permute-done | bytes 262176 | tf_op jit(solution)/shard_map/ppermute | solution.py:24
  67.6 1.0 select_dynamic-update-slice_fusion
  68.7 2.3 %slice_bitcast_fusion.1 = (bf16[2,2,88,2,8,128]{5,4,3,2,1,0:T(8,128)(2,1)S(1)}, bf16[2,2,88,2,8,128]{5,4,3,2,1,0:T(8,128)(2,1)S(1)}) fusion(bf16[2,2,704,512]{3,2,1,0:T(8,128)(2,1)} %select_dynamic-update-slice_fusion), kind=kLoop, calls=%fused_computation.14 | loop fusion | bytes 5767168
  72.3 1.2 multiply_reduce_fusion
  73.4 3.1 %fusion.62 = bf16[2,2,64,2,128]{4,2,3,1,0:T(8,128)(2,1)} fusion(bf16[2,2,88,2,8,128]{5,4,3,2,1,0:T(8,128)(2,1)S(1)} %get-tuple-element.6, f32[2,2,2,64,704]{4,3,2,1,0:T(8,128)S(1)} %get-tuple-element.84, bf16[2,2,88,2,8,128]{5,4,3,2,1,0:T(8,128)(2,1)} %copy-done.1, f32[2,2,2,64]{3,2,1,0:T(2,128)S(1)} %bitcast.266, f32[2,2,2,64]{3,2,1,0:T(2,128)S(1)} %log_add_fusion, ...), kind=kOutput, calls=%fused_computation.50 | convolution fusion | flops 186122240 | bytes 4591616 | tf_op jit(solution)/shard_map/abhqk,abkhe->abqhe/dot_general | solution.py:108
  76.5 1.1 copy.132
  78.1 1.3 collective-permute-start.11
  79.3 1.3 collective-permute-start.12
  80.7 0.9 convolution_bitcast_fusion.2
  82.5 6.0 %collective-permute-start.13 = (f32[8,32,4]{1,0,2:T(8,128)S(1)}, f32[8,32,4]{1,0,2:T(8,128)S(1)}, u32[]{:S(2)}, u32[]{:S(2)}) collective-permute-start(f32[8,32,4]{1,0,2:T(8,128)S(1)} %get-tuple-element.64), channel_id=1, source_target_pairs={{0,4},{4,8},{8,12},{12,16},{16,20},{20,24},{24,28},{1,5},{5,9},{9,... | collective-permute-start | bytes 12296 | tf_op jit(solution)/shard_map/ppermute | solution.py:24
  88.5 1.5 collective-permute-start.14
  90.0 0.9 fusion.116
  90.9 5.0 %collective-permute-done.14 = f32[8,32,4]{1,0,2:T(8,128)S(1)} collective-permute-done((f32[8,32,4]{1,0,2:T(8,128)S(1)}, f32[8,32,4]{1,0,2:T(8,128)S(1)}, u32[]{:S(2)}, u32[]{:S(2)}) %collective-permute-start.14) | collective-permute-done | bytes 4128 | tf_op jit(solution)/shard_map/ppermute | solution.py:27
  96.5 1.9 %fusion.9 = f32[2,2,2,576,64]{3,4,2,1,0:T(8,128)S(1)} fusion(f32[2,2,2,576]{3,2,1,0:T(2,128)S(1)} %concatenate.90, pred[2,2,576]{2,1,0:T(4,128)(4,1)S(1)} %copy-done.20, bf16[2,2,8,2,8,128]{5,4,3,2,1,0:T(8,128)(2,1)} %get-tuple-element.11, bf16[2,2,576,256]{3,2,1,0:T(8,128)(2,1)} %copy-done.19), kind=kOutput, calls=%fused_computation.20 | convolution fusion | flops 76382208 | bytes 2511104 | tf_op jit(solution)/shard_map/abqhe,abkhe->abhqk/dot_general | solution.py:126
  99.4 2.7 %fusion.57 = bf16[2,2,64,2,128]{4,2,3,1,0:T(8,128)(2,1)} fusion(f32[2,2,2,576,64]{3,4,2,1,0:T(8,128)S(1)} %fusion.9, f32[2,2,2,576]{3,2,1,0:T(2,128)S(1)} %concatenate.92, bf16[2,2,8,2,8,128]{5,4,3,2,1,0:T(8,128)(2,1)S(1)} %copy-done.18, bf16[2,2,576,256]{3,2,1,0:T(8,128)(2,1)S(1)} %copy-done.4, bf16[2,2,576,256]{3,2,1,0:T(8,128)(2,1)} %copy-done.19), kind=kOutput, calls=%fused_computation.49 | convolution fusion | flops 152010752 | bytes 3819520 | tf_op jit(solution)/shard_map/abhqk,abqhe->abkhe/dot_general | solution.py:135
  102.0 1.1 copy.142
  104.1 1.5 %collective-permute-start.15 = (f32[512,256]{1,0:T(8,128)S(1)}, f32[512,256]{1,0:T(8,128)S(1)}, u32[]{:S(2)}, u32[]{:S(2)}) collective-permute-start(f32[512,256]{1,0:T(8,128)S(1)} %constant_dynamic-slice_fusion.1), channel_id=1, source_target_pairs={{0,1},{1,0},{2,3},{3,2},{4,5},{5,4},{6,7},{7,6},{8,9},{9,8},{10,11... | collective-permute-start | bytes 1572872 | tf_op jit(solution)/shard_map/ppermute | solution.py:202
  105.7 1.5 %collective-permute-done.15 = f32[512,256]{1,0:T(8,128)S(1)} collective-permute-done((f32[512,256]{1,0:T(8,128)S(1)}, f32[512,256]{1,0:T(8,128)S(1)}, u32[]{:S(2)}, u32[]{:S(2)}) %collective-permute-start.15) | collective-permute-done | bytes 524320 | tf_op jit(solution)/shard_map/ppermute | solution.py:202
  107.3 1.5 collective-permute-start.16
  108.8 7.2 %collective-permute-done.16 = f32[256,256]{1,0:T(8,128)S(1)} collective-permute-done((f32[256,256]{1,0:T(8,128)S(1)}, f32[256,256]{1,0:T(8,128)S(1)}, u32[]{:S(2)}, u32[]{:S(2)}) %collective-permute-start.16) | collective-permute-done | bytes 262176 | tf_op jit(solution)/shard_map/ppermute | solution.py:202
  116.0 5.7 %collective-permute-start.17 = (f32[128,256]{1,0:T(8,128)S(1)}, f32[128,256]{1,0:T(8,128)S(1)}, u32[]{:S(2)}, u32[]{:S(2)}) collective-permute-start(f32[128,256]{1,0:T(8,128)S(1)} %constant_dynamic-slice_fusion.2), channel_id=1, source_target_pairs={{0,4},{4,0},{8,12},{12,8},{16,20},{20,16},{24,28},{28,24},{1,5},{5... | collective-permute-start | bytes 393224 | tf_op jit(solution)/shard_map/ppermute | solution.py:202
  121.7 3.2 %collective-permute-done.17 = f32[128,256]{1,0:T(8,128)S(1)} collective-permute-done((f32[128,256]{1,0:T(8,128)S(1)}, f32[128,256]{1,0:T(8,128)S(1)}, u32[]{:S(2)}, u32[]{:S(2)}) %collective-permute-start.17) | collective-permute-done | bytes 131104 | tf_op jit(solution)/shard_map/ppermute | solution.py:202
  124.9 2.5 %collective-permute-start.18 = (f32[128,256]{1,0:T(8,128)S(1)}, f32[128,256]{1,0:T(8,128)S(1)}, u32[]{:S(2)}, u32[]{:S(2)}) collective-permute-start(f32[128,256]{1,0:T(8,128)S(1)} %dynamic-slice_add_fusion.2), channel_id=1, source_target_pairs={{0,8},{4,12},{8,0},{12,4},{16,24},{20,28},{24,16},{28,20},{1,9},{5... | collective-permute-start | bytes 393224 | tf_op jit(solution)/shard_map/ppermute | solution.py:205
  127.4 2.9 %collective-permute-done.18 = f32[128,256]{1,0:T(8,128)S(1)} collective-permute-done((f32[128,256]{1,0:T(8,128)S(1)}, f32[128,256]{1,0:T(8,128)S(1)}, u32[]{:S(2)}, u32[]{:S(2)}) %collective-permute-start.18) | collective-permute-done | bytes 131104 | tf_op jit(solution)/shard_map/ppermute | solution.py:205
  130.4 2.1 %collective-permute-start.19 = (f32[128,256]{1,0:T(8,128)S(1)}, f32[128,256]{1,0:T(8,128)S(1)}, u32[]{:S(2)}, u32[]{:S(2)}) collective-permute-start(f32[128,256]{1,0:T(8,128)S(1)} %add.165), channel_id=1, source_target_pairs={{0,16},{4,20},{8,24},{12,28},{16,0},{20,4},{24,8},{28,12},{1,17},{... | collective-permute-start | bytes 393224 | tf_op jit(solution)/shard_map/ppermute | solution.py:205
  132.5 3.8 %collective-permute-done.19 = f32[128,256]{1,0:T(8,128)S(1)} collective-permute-done((f32[128,256]{1,0:T(8,128)S(1)}, f32[128,256]{1,0:T(8,128)S(1)}, u32[]{:S(2)}, u32[]{:S(2)}) %collective-permute-start.19) | collective-permute-done | bytes 131104 | tf_op jit(solution)/shard_map/ppermute | solution.py:205
  136.3 2.4 %collective-permute-start.20 = (f32[128,256]{1,0:T(8,128)S(1)}, f32[128,256]{1,0:T(8,128)S(1)}, u32[]{:S(2)}, u32[]{:S(2)}) collective-permute-start(f32[128,256]{1,0:T(8,128)S(1)} %add.166), channel_id=1, source_target_pairs={{0,4},{4,0},{8,12},{12,8},{16,20},{20,16},{24,28},{28,24},{1,5},{5... | collective-permute-start | bytes 393224 | tf_op jit(solution)/shard_map/ppermute | solution.py:167
  138.7 2.9 %collective-permute-done.20 = f32[128,256]{1,0:T(8,128)S(1)} collective-permute-done((f32[128,256]{1,0:T(8,128)S(1)}, f32[128,256]{1,0:T(8,128)S(1)}, u32[]{:S(2)}, u32[]{:S(2)}) %collective-permute-start.20) | collective-permute-done | bytes 131104 | tf_op jit(solution)/shard_map/ppermute | solution.py:167
  141.8 1.5 %collective-permute-start.21 = (f32[256,256]{1,0:T(8,128)S(1)}, f32[256,256]{1,0:T(8,128)S(1)}, u32[]{:S(2)}, u32[]{:S(2)}) collective-permute-start(f32[256,256]{1,0:T(8,128)S(1)} %pad_maximum_fusion.6), channel_id=1, source_target_pairs={{0,2},{1,3},{2,0},{3,1},{4,6},{5,7},{6,4},{7,5},{8,10},{9,11},{10,... | collective-permute-start | bytes 786440 | tf_op jit(solution)/shard_map/ppermute | solution.py:167
  143.3 4.9 %collective-permute-done.21 = f32[256,256]{1,0:T(8,128)S(1)} collective-permute-done((f32[256,256]{1,0:T(8,128)S(1)}, f32[256,256]{1,0:T(8,128)S(1)}, u32[]{:S(2)}, u32[]{:S(2)}) %collective-permute-start.21) | collective-permute-done | bytes 262176 | tf_op jit(solution)/shard_map/ppermute | solution.py:167
  149.2 1.0 convolution_convert_fusion.1
  (197 shorter events, 24.1 us)
Async XLA Ops:
  0.6 30.0 %copy-start = (bf16[1,1,4,64,512]{4,3,2,1,0:T(8,128)(2,1)S(1)}, bf16[1,1,4,64,512]{4,3,2,1,0:T(8,128)(2,1)}, u32[]{:S(2)}) copy-start(bf16[1,1,4,64,512]{4,3,2,1,0:T(8,128)(2,1)} %param.15) | copy-start | bytes 786436
  0.6 16.5 %copy-start.22 = (s32[8]{0:T(128)S(1)}, s32[8]{0:T(128)}, u32[]{:S(2)}) copy-start(s32[8]{0:T(128)} %constant.166) | copy-start | bytes 100
  0.7 16.3 %copy-start.21 = (s32[1,1,4,2]{2,3,1,0:T(2,128)S(1)}, s32[1,1,4,2]{2,3,1,0:T(2,128)}, u32[]{:S(2)}) copy-start(s32[1,1,4,2]{2,3,1,0:T(2,128)} %param.16) | copy-start | bytes 100
  0.7 11.1 %copy-start.10 = (bf16[16,16,256]{2,1,0:T(8,128)(2,1)S(1)}, bf16[16,16,256]{2,1,0:T(8,128)(2,1)}, u32[]{:S(2)}) copy-start(bf16[16,16,256]{2,1,0:T(8,128)(2,1)} %param.18) | copy-start | bytes 393220
  0.7 11.1 %copy-start.7 = (bf16[256,256]{1,0:T(8,128)(2,1)S(1)}, bf16[256,256]{1,0:T(8,128)(2,1)}, u32[]{:S(2)}) copy-start(bf16[256,256]{1,0:T(8,128)(2,1)} %param.14) | copy-start | bytes 393220
  2.5 17.8 %collective-permute-start.4 = (s32[1,2,8]{2,1,0:T(2,128)S(1)}, s32[1,2,8]{2,1,0:T(2,128)S(1)}, u32[]{:S(2)}, u32[]{:S(2)}) collective-permute-start(s32[1,2,8]{2,1,0:T(2,128)S(1)} %add_bitcast_fusion), channel_id=1, source_target_pairs={{0,16},{4,20},{8,24},{12,28},{16,0},{20,4},{24,8},{28,12},{1,17},{... | collective-permute-start | bytes 200 | tf_op jit(solution)/shard_map/ppermute | solution.py:167
  7.9 28.1 %collective-permute-start = (bf16[16,8,512]{2,1,0:T(8,128)(2,1)S(1)}, bf16[16,8,512]{2,1,0:T(8,128)(2,1)S(1)}, u32[]{:S(2)}, u32[]{:S(2)}) collective-permute-start(bf16[16,8,512]{2,1,0:T(8,128)(2,1)S(1)} %get-tuple-element.44), channel_id=1, source_target_pairs={{0,1},{1,2},{2,3},{4,5},{5,6},{6,7},{8,9},{9,10},{10,11},{12,13},{... | collective-permute-start | bytes 393224 | tf_op jit(solution)/shard_map/ppermute | solution.py:24
  9.3 26.6 %collective-permute-start.1 = (bf16[16,8,512]{2,1,0:T(8,128)(2,1)S(1)}, bf16[16,8,512]{2,1,0:T(8,128)(2,1)S(1)}, u32[]{:S(2)}, u32[]{:S(2)}) collective-permute-start(bf16[16,8,512]{2,1,0:T(8,128)(2,1)S(1)} %get-tuple-element.45), channel_id=1, source_target_pairs={{1,0},{2,1},{3,2},{5,4},{6,5},{7,6},{9,8},{10,9},{11,10},{13,12},{... | collective-permute-start | bytes 393224 | tf_op jit(solution)/shard_map/ppermute | solution.py:27
  12.1 29.1 %collective-permute-start.7 = (bf16[8,16,512]{2,1,0:T(8,128)(2,1)S(1)}, bf16[8,16,512]{2,1,0:T(8,128)(2,1)S(1)}, u32[]{:S(2)}, u32[]{:S(2)}) collective-permute-start(bf16[8,16,512]{2,1,0:T(8,128)(2,1)S(1)} %get-tuple-element.42), channel_id=1, source_target_pairs={{0,4},{4,8},{8,12},{12,16},{16,20},{20,24},{24,28},{1,5},{5,9},{9,... | collective-permute-start | bytes 393224 | tf_op jit(solution)/shard_map/ppermute | solution.py:24
  15.5 25.7 %collective-permute-start.8 = (bf16[8,16,512]{2,1,0:T(8,128)(2,1)S(1)}, bf16[8,16,512]{2,1,0:T(8,128)(2,1)S(1)}, u32[]{:S(2)}, u32[]{:S(2)}) collective-permute-start(bf16[8,16,512]{2,1,0:T(8,128)(2,1)S(1)} %get-tuple-element.43), channel_id=1, source_target_pairs={{4,0},{8,4},{12,8},{16,12},{20,16},{24,20},{28,24},{5,1},{9,5},{13... | collective-permute-start | bytes 393224 | tf_op jit(solution)/shard_map/ppermute | solution.py:27
  20.3 51.9 %copy-start.8 = (bf16[2,2,64,2,128]{4,3,2,1,0:T(2,128)(2,1)}, bf16[2,2,64,2,128]{4,3,2,1,0:T(2,128)(2,1)S(1)}, u32[]{:S(2)}) copy-start(bf16[2,2,64,2,128]{4,3,2,1,0:T(2,128)(2,1)S(1)} %reshape_reshape.32) | copy-start | bytes 393220
  20.4 5.3 %collective-permute-start.5 = (s32[2,2,8]{2,1,0:T(2,128)S(1)}, s32[2,2,8]{2,1,0:T(2,128)S(1)}, u32[]{:S(2)}, u32[]{:S(2)}) collective-permute-start(s32[2,2,8]{2,1,0:T(2,128)S(1)} %pad_add_fusion.2), channel_id=1, source_target_pairs={{0,8},{4,12},{8,0},{12,4},{16,24},{20,28},{24,16},{28,20},{1,9},{5... | collective-permute-start | bytes 392 | tf_op jit(solution)/shard_map/ppermute | solution.py:167
  25.6 3.7 %collective-permute-start.6 = (s32[4,2,8]{2,1,0:T(2,128)S(1)}, s32[4,2,8]{2,1,0:T(2,128)S(1)}, u32[]{:S(2)}, u32[]{:S(2)}) collective-permute-start(s32[4,2,8]{2,1,0:T(2,128)S(1)} %pad_add_fusion.1), channel_id=1, source_target_pairs={{0,4},{4,0},{8,12},{12,8},{16,20},{20,16},{24,28},{28,24},{1,5},{5... | collective-permute-start | bytes 776 | tf_op jit(solution)/shard_map/ppermute | solution.py:167
  32.4 34.7 %all-to-all-start = ((bf16[8,2,64,512]{3,2,1,0:T(8,128)(2,1)}), bf16[8,2,64,512]{3,2,1,0:T(8,128)(2,1)S(1)}, u32[]{:S(2)}, u32[]{:S(2)}) async-start(bf16[8,2,64,512]{3,2,1,0:T(8,128)(2,1)} %broadcast_select_fusion), calls=%async_computation | async-start | bytes 2097152 | tf_op jit(solution)/shard_map/all_to_all | solution.py:229
  36.1 22.8 %collective-permute-start.2 = (bf16[8,32,512]{2,1,0:T(8,128)(2,1)S(1)}, bf16[8,32,512]{2,1,0:T(8,128)(2,1)S(1)}, u32[]{:S(2)}, u32[]{:S(2)}) collective-permute-start(bf16[8,32,512]{2,1,0:T(8,128)(2,1)S(1)} %get-tuple-element.38), channel_id=1, source_target_pairs={{0,4},{4,8},{8,12},{12,16},{16,20},{20,24},{24,28},{1,5},{5,9},{9,... | collective-permute-start | bytes 786440 | tf_op jit(solution)/shard_map/ppermute | solution.py:24
  39.9 19.0 %collective-permute-start.3 = (bf16[8,32,512]{2,1,0:T(8,128)(2,1)S(1)}, bf16[8,32,512]{2,1,0:T(8,128)(2,1)S(1)}, u32[]{:S(2)}, u32[]{:S(2)}) collective-permute-start(bf16[8,32,512]{2,1,0:T(8,128)(2,1)S(1)} %get-tuple-element.39), channel_id=1, source_target_pairs={{4,0},{8,4},{12,8},{16,12},{20,16},{24,20},{28,24},{5,1},{9,5},{13... | collective-permute-start | bytes 786440 | tf_op jit(solution)/shard_map/ppermute | solution.py:27
  41.3 20.0 %collective-permute-start.10 = (bf16[32,8,512]{2,1,0:T(8,128)(2,1)S(1)}, bf16[32,8,512]{2,1,0:T(8,128)(2,1)S(1)}, u32[]{:S(2)}, u32[]{:S(2)}) collective-permute-start(bf16[32,8,512]{2,1,0:T(8,128)(2,1)S(1)} %get-tuple-element.37), channel_id=1, source_target_pairs={{1,0},{2,1},{3,2},{5,4},{6,5},{7,6},{9,8},{10,9},{11,10},{13,12},{... | collective-permute-start | bytes 786440 | tf_op jit(solution)/shard_map/ppermute | solution.py:27
  42.6 18.7 %collective-permute-start.9 = (bf16[32,8,512]{2,1,0:T(8,128)(2,1)S(1)}, bf16[32,8,512]{2,1,0:T(8,128)(2,1)S(1)}, u32[]{:S(2)}, u32[]{:S(2)}) collective-permute-start(bf16[32,8,512]{2,1,0:T(8,128)(2,1)S(1)} %get-tuple-element.36), channel_id=1, source_target_pairs={{0,1},{1,2},{2,3},{4,5},{5,6},{6,7},{8,9},{9,10},{10,11},{12,13},{... | collective-permute-start | bytes 786440 | tf_op jit(solution)/shard_map/ppermute | solution.py:24
  61.8 4.5 %copy-start.3 = (bf16[2,2,576,256]{3,2,1,0:T(8,128)(2,1)}, bf16[2,2,576,256]{3,2,1,0:T(8,128)(2,1)S(1)}, u32[]{:S(2)}) copy-start(bf16[2,2,576,256]{3,2,1,0:T(8,128)(2,1)S(1)} %get-tuple-element.13) | copy-start | bytes 3538948
  61.8 4.5 %copy-start.19 = (bf16[2,2,576,256]{3,2,1,0:T(8,128)(2,1)}, bf16[2,2,576,256]{3,2,1,0:T(8,128)(2,1)S(1)}, u32[]{:S(2)}) copy-start(bf16[2,2,576,256]{3,2,1,0:T(8,128)(2,1)S(1)} %get-tuple-element.12) | copy-start | bytes 3538948
  68.7 2.3 %copy-start.14 = (bf16[2,2,64,2,128]{4,3,2,1,0:T(2,128)(2,1)S(1)}, bf16[2,2,64,2,128]{4,3,2,1,0:T(2,128)(2,1)}, u32[]{:S(2)}) copy-start(bf16[2,2,64,2,128]{4,3,2,1,0:T(2,128)(2,1)} %reshape_reshape.29) | copy-start | bytes 393220
  71.0 1.3 copy-start.1
  73.4 7.2 %copy-start.2 = (bf16[16,16,256]{2,1,0:T(8,128)(2,1)S(1)}, bf16[16,16,256]{2,1,0:T(8,128)(2,1)}, u32[]{:S(2)}) copy-start(bf16[16,16,256]{2,1,0:T(8,128)(2,1)} %param.10) | copy-start | bytes 393220
  76.5 5.1 %copy-start.9 = (bf16[2,2,64,2,128]{4,2,3,1,0:T(8,128)(2,1)S(1)}, bf16[2,2,64,2,128]{4,2,3,1,0:T(8,128)(2,1)}, u32[]{:S(2)}) copy-start(bf16[2,2,64,2,128]{4,2,3,1,0:T(8,128)(2,1)} %get-tuple-element.86) | copy-start | bytes 393220
  76.5 13.5 %copy-start.11 = (bf16[16,16,256]{2,1,0:T(8,128)(2,1)S(1)}, bf16[16,16,256]{2,1,0:T(8,128)(2,1)}, u32[]{:S(2)}) copy-start(bf16[16,16,256]{2,1,0:T(8,128)(2,1)} %param.18) | copy-start | bytes 393220
  77.7 3.9 %copy-start.12 = (bf16[2,8,2,8,256]{4,3,2,1,0:T(8,128)(2,1)}, bf16[2,8,2,8,256]{4,3,2,1,0:T(8,128)(2,1)S(1)}, u32[]{:S(2)}) copy-start(bf16[2,8,2,8,256]{4,3,2,1,0:T(8,128)(2,1)S(1)} %copy.133) | copy-start | bytes 393220
  78.1 3.8 %collective-permute-start.11 = (f32[16,8,4]{1,0,2:T(8,128)S(1)}, f32[16,8,4]{1,0,2:T(8,128)S(1)}, u32[]{:S(2)}, u32[]{:S(2)}) collective-permute-start(f32[16,8,4]{1,0,2:T(8,128)S(1)} %get-tuple-element.66), channel_id=1, source_target_pairs={{0,1},{1,2},{2,3},{4,5},{5,6},{6,7},{8,9},{9,10},{10,11},{12,13},{... | collective-permute-start | bytes 6152 | tf_op jit(solution)/shard_map/ppermute | solution.py:24
  79.3 3.1 %collective-permute-start.12 = (f32[16,8,4]{1,0,2:T(8,128)S(1)}, f32[16,8,4]{1,0,2:T(8,128)S(1)}, u32[]{:S(2)}, u32[]{:S(2)}) collective-permute-start(f32[16,8,4]{1,0,2:T(8,128)S(1)} %get-tuple-element.67), channel_id=1, source_target_pairs={{1,0},{2,1},{3,2},{5,4},{6,5},{7,6},{9,8},{10,9},{11,10},{13,12},{... | collective-permute-start | bytes 6152 | tf_op jit(solution)/shard_map/ppermute | solution.py:27
  81.7 14.8 %copy-start.20 = (pred[2,2,576]{2,1,0:T(4,128)(4,1)S(1)}, pred[2,2,576]{2,1,0:T(4,128)(4,1)}, u32[]{:S(2)}) copy-start(pred[2,2,576]{2,1,0:T(4,128)(4,1)} %concatenate.86) | copy-start | bytes 6916
  82.5 8.4 %collective-permute-start.13 = (f32[8,32,4]{1,0,2:T(8,128)S(1)}, f32[8,32,4]{1,0,2:T(8,128)S(1)}, u32[]{:S(2)}, u32[]{:S(2)}) collective-permute-start(f32[8,32,4]{1,0,2:T(8,128)S(1)} %get-tuple-element.64), channel_id=1, source_target_pairs={{0,4},{4,8},{8,12},{12,16},{16,20},{20,24},{24,28},{1,5},{5,9},{9,... | collective-permute-start | bytes 12296 | tf_op jit(solution)/shard_map/ppermute | solution.py:24
  88.5 7.4 %collective-permute-start.14 = (f32[8,32,4]{1,0,2:T(8,128)S(1)}, f32[8,32,4]{1,0,2:T(8,128)S(1)}, u32[]{:S(2)}, u32[]{:S(2)}) collective-permute-start(f32[8,32,4]{1,0,2:T(8,128)S(1)} %get-tuple-element.65), channel_id=1, source_target_pairs={{4,0},{8,4},{12,8},{16,12},{20,16},{24,20},{28,24},{5,1},{9,5},{13... | collective-permute-start | bytes 12296 | tf_op jit(solution)/shard_map/ppermute | solution.py:27
  96.5 1.9 %copy-start.4 = (bf16[2,2,576,256]{3,2,1,0:T(8,128)(2,1)S(1)}, bf16[2,2,576,256]{3,2,1,0:T(8,128)(2,1)}, u32[]{:S(2)}) copy-start(bf16[2,2,576,256]{3,2,1,0:T(8,128)(2,1)} %copy-done.3) | copy-start | bytes 3538948
  98.5 0.9 copy-start.18
  102.0 1.9 %copy-start.5 = (f32[256,256]{1,0:T(8,128)S(1)}, f32[256,256]{1,0:T(8,128)}, u32[]{:S(2)}) copy-start(f32[256,256]{1,0:T(8,128)} %convolution_bitcast_fusion.2) | copy-start | bytes 786436
  102.0 2.0 %copy-start.6 = (f32[256,256]{1,0:T(8,128)S(1)}, f32[256,256]{1,0:T(8,128)}, u32[]{:S(2)}) copy-start(f32[256,256]{1,0:T(8,128)} %fusion.116) | copy-start | bytes 786436
  104.1 3.1 %collective-permute-start.15 = (f32[512,256]{1,0:T(8,128)S(1)}, f32[512,256]{1,0:T(8,128)S(1)}, u32[]{:S(2)}, u32[]{:S(2)}) collective-permute-start(f32[512,256]{1,0:T(8,128)S(1)} %constant_dynamic-slice_fusion.1), channel_id=1, source_target_pairs={{0,1},{1,0},{2,3},{3,2},{4,5},{5,4},{6,7},{7,6},{8,9},{9,8},{10,11... | collective-permute-start | bytes 1572872 | tf_op jit(solution)/shard_map/ppermute | solution.py:202
  107.3 8.7 %collective-permute-start.16 = (f32[256,256]{1,0:T(8,128)S(1)}, f32[256,256]{1,0:T(8,128)S(1)}, u32[]{:S(2)}, u32[]{:S(2)}) collective-permute-start(f32[256,256]{1,0:T(8,128)S(1)} %constant_dynamic-slice_fusion), channel_id=1, source_target_pairs={{0,2},{1,3},{2,0},{3,1},{4,6},{5,7},{6,4},{7,5},{8,10},{9,11},{10,... | collective-permute-start | bytes 786440 | tf_op jit(solution)/shard_map/ppermute | solution.py:202
  116.0 8.9 %collective-permute-start.17 = (f32[128,256]{1,0:T(8,128)S(1)}, f32[128,256]{1,0:T(8,128)S(1)}, u32[]{:S(2)}, u32[]{:S(2)}) collective-permute-start(f32[128,256]{1,0:T(8,128)S(1)} %constant_dynamic-slice_fusion.2), channel_id=1, source_target_pairs={{0,4},{4,0},{8,12},{12,8},{16,20},{20,16},{24,28},{28,24},{1,5},{5... | collective-permute-start | bytes 393224 | tf_op jit(solution)/shard_map/ppermute | solution.py:202
  124.9 5.4 %collective-permute-start.18 = (f32[128,256]{1,0:T(8,128)S(1)}, f32[128,256]{1,0:T(8,128)S(1)}, u32[]{:S(2)}, u32[]{:S(2)}) collective-permute-start(f32[128,256]{1,0:T(8,128)S(1)} %dynamic-slice_add_fusion.2), channel_id=1, source_target_pairs={{0,8},{4,12},{8,0},{12,4},{16,24},{20,28},{24,16},{28,20},{1,9},{5... | collective-permute-start | bytes 393224 | tf_op jit(solution)/shard_map/ppermute | solution.py:205
  130.4 5.9 %collective-permute-start.19 = (f32[128,256]{1,0:T(8,128)S(1)}, f32[128,256]{1,0:T(8,128)S(1)}, u32[]{:S(2)}, u32[]{:S(2)}) collective-permute-start(f32[128,256]{1,0:T(8,128)S(1)} %add.165), channel_id=1, source_target_pairs={{0,16},{4,20},{8,24},{12,28},{16,0},{20,4},{24,8},{28,12},{1,17},{... | collective-permute-start | bytes 393224 | tf_op jit(solution)/shard_map/ppermute | solution.py:205
  136.3 5.3 %collective-permute-start.20 = (f32[128,256]{1,0:T(8,128)S(1)}, f32[128,256]{1,0:T(8,128)S(1)}, u32[]{:S(2)}, u32[]{:S(2)}) collective-permute-start(f32[128,256]{1,0:T(8,128)S(1)} %add.166), channel_id=1, source_target_pairs={{0,4},{4,0},{8,12},{12,8},{16,20},{20,16},{24,28},{28,24},{1,5},{5... | collective-permute-start | bytes 393224 | tf_op jit(solution)/shard_map/ppermute | solution.py:167
  141.7 7.5 %copy-start.13 = (bf16[2,8,2,8,256]{4,3,2,1,0:T(8,128)(2,1)S(1)}, bf16[2,8,2,8,256]{4,3,2,1,0:T(8,128)(2,1)}, u32[]{:S(2)}) copy-start(bf16[2,8,2,8,256]{4,3,2,1,0:T(8,128)(2,1)} %copy-done.12) | copy-start | bytes 393220
  141.7 7.5 %copy-start.15 = (bf16[256,256]{1,0:T(8,128)(2,1)S(1)}, bf16[256,256]{1,0:T(8,128)(2,1)}, u32[]{:S(2)}) copy-start(bf16[256,256]{1,0:T(8,128)(2,1)} %param.13) | copy-start | bytes 393220
  141.7 7.5 %copy-start.16 = (bf16[256,256]{1,0:T(8,128)(2,1)S(1)}, bf16[256,256]{1,0:T(8,128)(2,1)}, u32[]{:S(2)}) copy-start(bf16[256,256]{1,0:T(8,128)(2,1)} %param.12) | copy-start | bytes 393220
  141.7 7.5 %copy-start.17 = (bf16[256,256]{1,0:T(8,128)(2,1)S(1)}, bf16[256,256]{1,0:T(8,128)(2,1)}, u32[]{:S(2)}) copy-start(bf16[256,256]{1,0:T(8,128)(2,1)} %param.11) | copy-start | bytes 393220
  141.8 6.4 %collective-permute-start.21 = (f32[256,256]{1,0:T(8,128)S(1)}, f32[256,256]{1,0:T(8,128)S(1)}, u32[]{:S(2)}, u32[]{:S(2)}) collective-permute-start(f32[256,256]{1,0:T(8,128)S(1)} %pad_maximum_fusion.6), channel_id=1, source_target_pairs={{0,2},{1,3},{2,0},{3,1},{4,6},{5,7},{6,4},{7,5},{8,10},{9,11},{10,... | collective-permute-start | bytes 786440 | tf_op jit(solution)/shard_map/ppermute | solution.py:167
  148.3 2.0 %collective-permute-start.22 = (f32[512,256]{1,0:T(8,128)S(1)}, f32[512,256]{1,0:T(8,128)S(1)}, u32[]{:S(2)}, u32[]{:S(2)}) collective-permute-start(f32[512,256]{1,0:T(8,128)S(1)} %pad_maximum_fusion.5), channel_id=1, source_target_pairs={{0,1},{1,0},{2,3},{3,2},{4,5},{5,4},{6,7},{7,6},{8,9},{9,8},{10,11... | collective-permute-start | bytes 1572872 | tf_op jit(solution)/shard_map/ppermute | solution.py:167

commit v20 on v16

--- a/solution.py
+++ b/solution.py
@@ -175,12 +175,7 @@
     count = lax.axis_size(axis)
     if count & (count - 1):
         return lax.all_gather(block, axis, axis=0, tiled=True), lambda index: index
-    width = count.bit_length() - 1
-
-    def slot_of(index):
-        return sum(((index >> bit) & 1) << (width - 1 - bit) for bit in range(width))
-
-    return doubling_gather(block, halving_steps((axis,))), slot_of
+    return doubling_gather(block, halving_steps((axis,))[::-1]), lambda index: index
 
 
 def tree_sum(parts, axes):

time: 142 us -> 143 us (level)
  starting transfers between devices: 51.1 us -> 55.1 us
  waiting for transfers between devices: 44.5 us -> 41.8 us
    ppermute x6, starting transfers between devices: 12.5 us -> 14.3 us  [doubling_gather(): got = lax.ppermute(joined, axis, pairs)]
    all_to_all x1, starting transfers between devices: 3.56 us -> 5.21 us  [fetch_regions(): received = lax.all_to_all(sent, axis, 0, 0, tiled=True)]
    ppermute x6, waiting for transfers between devices: 13.1 us -> 11.6 us  [doubling_gather(): got = lax.ppermute(joined, axis, pairs)]
    unnamed x68 -> x66, local copies, waits for them, and re-layouts: 12 us -> 12 us
where the time goes in v20:
time: 143 us
  starting transfers between devices  55.1 us (39%)
  waiting for transfers between devices  41.8 us (29%)
  local copies, waits for them, and re-layouts  23.1 us (16%)
  matrix products  16.7 us (12%)
  other arithmetic  4.25 us (3%)
  between operations  1.64 us (1%)
    ppermute x6, starting transfers between devices, padded(): lax.ppermute(lax.slice_in_dim(block, block.shape[dim] - width, None, axis...  18.6 us
    ppermute x6, starting transfers between devices, doubling_gather(): got = lax.ppermute(joined, axis, pairs)  14.3 us
    unnamed x66, local copies, waits for them, and re-layouts  12 us
    ppermute x3, waiting for transfers between devices, tree_sum(): joined = keep + lax.ppermute(send, axis, pairs)  11.6 us
    ppermute x6, waiting for transfers between devices, doubling_gather(): got = lax.ppermute(joined, axis, pairs)  11.6 us
    ppermute x2, waiting for transfers between devices, tree_sum(): joined = joined + lax.ppermute(joined, axis, pairs)  8.41 us
    ppermute x6, starting transfers between devices, padded(): lax.ppermute(lax.slice_in_dim(block, 0, width, axis=dim), axis, backward)  7.93 us
    ppermute x6, waiting for transfers between devices, padded(): lax.ppermute(lax.slice_in_dim(block, 0, width, axis=dim), axis, backward)  5.55 us
  transfers between devices with their start and end apart: 24, of which 13 were waited for; matrix products, arithmetic and copies ran while one was open for 15% of the time, Pallas kernels for 0%

profile of v20, /device:TPU:0, one launch (start us, length us, event | category | flops | bytes accessed | tf_op | source)
XLA Modules:
  0.0 142.6 jit_solution(7011931315034117032)
XLA Ops:
  2.4 3.0 %collective-permute-start.4 = (s32[1,2,8]{2,1,0:T(2,128)S(1)}, s32[1,2,8]{2,1,0:T(2,128)S(1)}, u32[]{:S(2)}, u32[]{:S(2)}) collective-permute-start(s32[1,2,8]{2,1,0:T(2,128)S(1)} %add_bitcast_fusion), channel_id=1, source_target_pairs={{0,4},{4,0},{8,12},{12,8},{16,20},{20,16},{24,28},{28,24},{1,5},{5... | collective-permute-start | bytes 200 | tf_op jit(solution)/shard_map/ppermute | solution.py:167
  5.4 1.3 convolution_convert_fusion
  6.7 1.9 %collective-permute-start = (bf16[8,16,512]{2,1,0:T(8,128)(2,1)S(1)}, bf16[8,16,512]{2,1,0:T(8,128)(2,1)S(1)}, u32[]{:S(2)}, u32[]{:S(2)}) collective-permute-start(bf16[8,16,512]{2,1,0:T(8,128)(2,1)S(1)} %bitcast.269), channel_id=1, source_target_pairs={{0,4},{4,8},{8,12},{12,16},{16,20},{20,24},{24,28},{1,5},{5,9},{9,... | collective-permute-start | bytes 393224 | tf_op jit(solution)/shard_map/ppermute | solution.py:24
  8.7 1.3 collective-permute-start.1
  10.0 1.2 convolution_convert_fusion.4
  11.4 5.6 %collective-permute-start.7 = (bf16[8,16,512]{2,1,0:T(8,128)(2,1)S(1)}, bf16[8,16,512]{2,1,0:T(8,128)(2,1)S(1)}, u32[]{:S(2)}, u32[]{:S(2)}) collective-permute-start(bf16[8,16,512]{2,1,0:T(8,128)(2,1)S(1)} %get-tuple-element.42), channel_id=1, source_target_pairs={{0,4},{4,8},{8,12},{12,16},{16,20},{20,24},{24,28},{1,5},{5,9},{9,... | collective-permute-start | bytes 393224 | tf_op jit(solution)/shard_map/ppermute | solution.py:24
  17.0 1.3 collective-permute-start.8
  21.8 5.1 %collective-permute-start.5 = (s32[2,2,8]{2,1,0:T(2,128)S(1)}, s32[2,2,8]{2,1,0:T(2,128)S(1)}, u32[]{:S(2)}, u32[]{:S(2)}) collective-permute-start(s32[2,2,8]{2,1,0:T(2,128)S(1)} %pad_add_fusion.2), channel_id=1, source_target_pairs={{0,8},{4,12},{8,0},{12,4},{16,24},{20,28},{24,16},{28,20},{1,9},{5... | collective-permute-start | bytes 392 | tf_op jit(solution)/shard_map/ppermute | solution.py:167
  26.9 1.6 %collective-permute-done.5 = s32[2,2,8]{2,1,0:T(2,128)S(1)} collective-permute-done((s32[2,2,8]{2,1,0:T(2,128)S(1)}, s32[2,2,8]{2,1,0:T(2,128)S(1)}, u32[]{:S(2)}, u32[]{:S(2)}) %collective-permute-start.5) | collective-permute-done | bytes 160 | tf_op jit(solution)/shard_map/ppermute | solution.py:167
  28.5 3.1 %collective-permute-start.6 = (s32[4,2,8]{2,1,0:T(2,128)S(1)}, s32[4,2,8]{2,1,0:T(2,128)S(1)}, u32[]{:S(2)}, u32[]{:S(2)}) collective-permute-start(s32[4,2,8]{2,1,0:T(2,128)S(1)} %pad_add_fusion.1), channel_id=1, source_target_pairs={{0,16},{4,20},{8,24},{12,28},{16,0},{20,4},{24,8},{28,12},{1,17},{... | collective-permute-start | bytes 776 | tf_op jit(solution)/shard_map/ppermute | solution.py:167
  31.6 1.6 %collective-permute-done.6 = s32[4,2,8]{2,1,0:T(2,128)S(1)} collective-permute-done((s32[4,2,8]{2,1,0:T(2,128)S(1)}, s32[4,2,8]{2,1,0:T(2,128)S(1)}, u32[]{:S(2)}, u32[]{:S(2)}) %collective-permute-start.6) | collective-permute-done | bytes 288 | tf_op jit(solution)/shard_map/ppermute | solution.py:167
  35.1 1.2 broadcast_select_fusion
  36.2 5.2 %all-to-all-start = ((bf16[8,2,64,512]{3,2,1,0:T(8,128)(2,1)}), bf16[8,2,64,512]{3,2,1,0:T(8,128)(2,1)S(1)}, u32[]{:S(2)}, u32[]{:S(2)}) async-start(bf16[8,2,64,512]{3,2,1,0:T(8,128)(2,1)} %broadcast_select_fusion), calls=%async_computation | async-start | bytes 2097152 | tf_op jit(solution)/shard_map/all_to_all | solution.py:224
  41.6 1.3 collective-permute-start.2
  42.9 1.3 collective-permute-start.3
  44.3 1.3 collective-permute-start.10
  45.6 5.4 %collective-permute-start.9 = (bf16[32,8,512]{2,1,0:T(8,128)(2,1)S(1)}, bf16[32,8,512]{2,1,0:T(8,128)(2,1)S(1)}, u32[]{:S(2)}, u32[]{:S(2)}) collective-permute-start(bf16[32,8,512]{2,1,0:T(8,128)(2,1)S(1)} %get-tuple-element.36), channel_id=1, source_target_pairs={{0,1},{1,2},{2,3},{4,5},{5,6},{6,7},{8,9},{9,10},{10,11},{12,13},{... | collective-permute-start | bytes 786440 | tf_op jit(solution)/shard_map/ppermute | solution.py:24
  59.2 4.6 %all-to-all-done = bf16[8,2,64,512]{3,2,1,0:T(8,128)(2,1)S(1)} async-done(((bf16[8,2,64,512]{3,2,1,0:T(8,128)(2,1)}), bf16[8,2,64,512]{3,2,1,0:T(8,128)(2,1)S(1)}, u32[]{:S(2)}, u32[]{:S(2)}) %all-to-all-start) | async-done | bytes 1048608 | tf_op jit(solution)/shard_map/all_to_all | solution.py:224
  64.3 1.0 select_dynamic-update-slice_fusion
  65.3 2.3 %slice_bitcast_fusion.1 = (bf16[2,2,88,2,8,128]{5,4,3,2,1,0:T(8,128)(2,1)S(1)}, bf16[2,2,88,2,8,128]{5,4,3,2,1,0:T(8,128)(2,1)S(1)}) fusion(bf16[2,2,704,512]{3,2,1,0:T(8,128)(2,1)} %select_dynamic-update-slice_fusion), kind=kLoop, calls=%fused_computation.14 | loop fusion | bytes 5767168
  68.9 1.2 multiply_reduce_fusion
  70.1 3.1 %fusion.62 = bf16[2,2,64,2,128]{4,2,3,1,0:T(8,128)(2,1)} fusion(bf16[2,2,88,2,8,128]{5,4,3,2,1,0:T(8,128)(2,1)S(1)} %get-tuple-element.6, f32[2,2,2,64,704]{4,3,2,1,0:T(8,128)S(1)} %get-tuple-element.84, bf16[2,2,88,2,8,128]{5,4,3,2,1,0:T(8,128)(2,1)} %copy-done.1, f32[2,2,2,64]{3,2,1,0:T(2,128)S(1)} %bitcast.270, f32[2,2,2,64]{3,2,1,0:T(2,128)S(1)} %log_add_fusion, ...), kind=kOutput, calls=%fused_computation.50 | convolution fusion | flops 186122240 | bytes 4591616 | tf_op jit(solution)/shard_map/abhqk,abkhe->abqhe/dot_general | solution.py:108
  73.2 1.1 copy.132
  74.7 1.3 collective-permute-start.11
  76.0 1.3 collective-permute-start.12
  77.3 0.9 convolution_bitcast_fusion.2
  78.5 2.3 %collective-permute-done.12 = f32[16,8,4]{1,0,2:T(8,128)S(1)} collective-permute-done((f32[16,8,4]{1,0,2:T(8,128)S(1)}, f32[16,8,4]{1,0,2:T(8,128)S(1)}, u32[]{:S(2)}, u32[]{:S(2)}) %collective-permute-start.12) | collective-permute-done | bytes 2080 | tf_op jit(solution)/shard_map/ppermute | solution.py:27
  81.0 3.1 %collective-permute-start.13 = (f32[8,32,4]{1,0,2:T(8,128)S(1)}, f32[8,32,4]{1,0,2:T(8,128)S(1)}, u32[]{:S(2)}, u32[]{:S(2)}) collective-permute-start(f32[8,32,4]{1,0,2:T(8,128)S(1)} %get-tuple-element.64), channel_id=1, source_target_pairs={{0,4},{4,8},{8,12},{12,16},{16,20},{20,24},{24,28},{1,5},{5,9},{9,... | collective-permute-start | bytes 12296 | tf_op jit(solution)/shard_map/ppermute | solution.py:24
  84.1 1.5 %collective-permute-start.14 = (f32[8,32,4]{1,0,2:T(8,128)S(1)}, f32[8,32,4]{1,0,2:T(8,128)S(1)}, u32[]{:S(2)}, u32[]{:S(2)}) collective-permute-start(f32[8,32,4]{1,0,2:T(8,128)S(1)} %get-tuple-element.65), channel_id=1, source_target_pairs={{4,0},{8,4},{12,8},{16,12},{20,16},{24,20},{28,24},{5,1},{9,5},{13... | collective-permute-start | bytes 12296 | tf_op jit(solution)/shard_map/ppermute | solution.py:27
  86.5 3.2 %collective-permute-done.14 = f32[8,32,4]{1,0,2:T(8,128)S(1)} collective-permute-done((f32[8,32,4]{1,0,2:T(8,128)S(1)}, f32[8,32,4]{1,0,2:T(8,128)S(1)}, u32[]{:S(2)}, u32[]{:S(2)}) %collective-permute-start.14) | collective-permute-done | bytes 4128 | tf_op jit(solution)/shard_map/ppermute | solution.py:27
  90.3 1.9 %fusion.9 = f32[2,2,2,576,64]{3,4,2,1,0:T(8,128)S(1)} fusion(f32[2,2,2,576]{3,2,1,0:T(2,128)S(1)} %concatenate.90, pred[2,2,576]{2,1,0:T(4,128)(4,1)S(1)} %copy-done.20, bf16[2,2,8,2,8,128]{5,4,3,2,1,0:T(8,128)(2,1)} %get-tuple-element.11, bf16[2,2,576,256]{3,2,1,0:T(8,128)(2,1)} %copy-done.19), kind=kOutput, calls=%fused_computation.20 | convolution fusion | flops 76382208 | bytes 2511104 | tf_op jit(solution)/shard_map/abqhe,abkhe->abhqk/dot_general | solution.py:126
  93.1 2.7 %fusion.57 = bf16[2,2,64,2,128]{4,2,3,1,0:T(8,128)(2,1)} fusion(f32[2,2,2,576,64]{3,4,2,1,0:T(8,128)S(1)} %fusion.9, f32[2,2,2,576]{3,2,1,0:T(2,128)S(1)} %concatenate.92, bf16[2,2,8,2,8,128]{5,4,3,2,1,0:T(8,128)(2,1)S(1)} %copy-done.18, bf16[2,2,576,256]{3,2,1,0:T(8,128)(2,1)S(1)} %copy-done.4, bf16[2,2,576,256]{3,2,1,0:T(8,128)(2,1)} %copy-done.19), kind=kOutput, calls=%fused_computation.49 | convolution fusion | flops 152010752 | bytes 3819520 | tf_op jit(solution)/shard_map/abhqk,abqhe->abkhe/dot_general | solution.py:135
  95.8 1.1 copy.142
  97.9 1.3 collective-permute-start.15
  99.2 1.5 %collective-permute-done.15 = f32[512,256]{1,0:T(8,128)S(1)} collective-permute-done((f32[512,256]{1,0:T(8,128)S(1)}, f32[512,256]{1,0:T(8,128)S(1)}, u32[]{:S(2)}, u32[]{:S(2)}) %collective-permute-start.15) | collective-permute-done | bytes 524320 | tf_op jit(solution)/shard_map/ppermute | solution.py:197
  100.8 1.8 %collective-permute-start.16 = (f32[256,256]{1,0:T(8,128)S(1)}, f32[256,256]{1,0:T(8,128)S(1)}, u32[]{:S(2)}, u32[]{:S(2)}) collective-permute-start(f32[256,256]{1,0:T(8,128)S(1)} %constant_dynamic-slice_fusion), channel_id=1, source_target_pairs={{0,2},{1,3},{2,0},{3,1},{4,6},{5,7},{6,4},{7,5},{8,10},{9,11},{10,... | collective-permute-start | bytes 786440 | tf_op jit(solution)/shard_map/ppermute | solution.py:197
  102.6 6.9 %collective-permute-done.16 = f32[256,256]{1,0:T(8,128)S(1)} collective-permute-done((f32[256,256]{1,0:T(8,128)S(1)}, f32[256,256]{1,0:T(8,128)S(1)}, u32[]{:S(2)}, u32[]{:S(2)}) %collective-permute-start.16) | collective-permute-done | bytes 262176 | tf_op jit(solution)/shard_map/ppermute | solution.py:197
  109.5 2.1 %collective-permute-start.17 = (f32[128,256]{1,0:T(8,128)S(1)}, f32[128,256]{1,0:T(8,128)S(1)}, u32[]{:S(2)}, u32[]{:S(2)}) collective-permute-start(f32[128,256]{1,0:T(8,128)S(1)} %constant_dynamic-slice_fusion.2), channel_id=1, source_target_pairs={{0,4},{4,0},{8,12},{12,8},{16,20},{20,16},{24,28},{28,24},{1,5},{5... | collective-permute-start | bytes 393224 | tf_op jit(solution)/shard_map/ppermute | solution.py:197
  111.6 3.2 %collective-permute-done.17 = f32[128,256]{1,0:T(8,128)S(1)} collective-permute-done((f32[128,256]{1,0:T(8,128)S(1)}, f32[128,256]{1,0:T(8,128)S(1)}, u32[]{:S(2)}, u32[]{:S(2)}) %collective-permute-start.17) | collective-permute-done | bytes 131104 | tf_op jit(solution)/shard_map/ppermute | solution.py:197
  114.8 1.5 %collective-permute-start.18 = (f32[128,256]{1,0:T(8,128)S(1)}, f32[128,256]{1,0:T(8,128)S(1)}, u32[]{:S(2)}, u32[]{:S(2)}) collective-permute-start(f32[128,256]{1,0:T(8,128)S(1)} %dynamic-slice_add_fusion.2), channel_id=1, source_target_pairs={{0,8},{4,12},{8,0},{12,4},{16,24},{20,28},{24,16},{28,20},{1,9},{5... | collective-permute-start | bytes 393224 | tf_op jit(solution)/shard_map/ppermute | solution.py:200
  116.4 3.5 %collective-permute-done.18 = f32[128,256]{1,0:T(8,128)S(1)} collective-permute-done((f32[128,256]{1,0:T(8,128)S(1)}, f32[128,256]{1,0:T(8,128)S(1)}, u32[]{:S(2)}, u32[]{:S(2)}) %collective-permute-start.18) | collective-permute-done | bytes 131104 | tf_op jit(solution)/shard_map/ppermute | solution.py:200
  119.9 2.4 %collective-permute-start.19 = (f32[128,256]{1,0:T(8,128)S(1)}, f32[128,256]{1,0:T(8,128)S(1)}, u32[]{:S(2)}, u32[]{:S(2)}) collective-permute-start(f32[128,256]{1,0:T(8,128)S(1)} %add.165), channel_id=1, source_target_pairs={{0,16},{4,20},{8,24},{12,28},{16,0},{20,4},{24,8},{28,12},{1,17},{... | collective-permute-start | bytes 393224 | tf_op jit(solution)/shard_map/ppermute | solution.py:200
  122.3 4.9 %collective-permute-done.19 = f32[128,256]{1,0:T(8,128)S(1)} collective-permute-done((f32[128,256]{1,0:T(8,128)S(1)}, f32[128,256]{1,0:T(8,128)S(1)}, u32[]{:S(2)}, u32[]{:S(2)}) %collective-permute-start.19) | collective-permute-done | bytes 131104 | tf_op jit(solution)/shard_map/ppermute | solution.py:200
  127.2 1.8 %collective-permute-start.20 = (f32[128,256]{1,0:T(8,128)S(1)}, f32[128,256]{1,0:T(8,128)S(1)}, u32[]{:S(2)}, u32[]{:S(2)}) collective-permute-start(f32[128,256]{1,0:T(8,128)S(1)} %add.166), channel_id=1, source_target_pairs={{0,4},{4,0},{8,12},{12,8},{16,20},{20,16},{24,28},{28,24},{1,5},{5... | collective-permute-start | bytes 393224 | tf_op jit(solution)/shard_map/ppermute | solution.py:167
  129.1 3.2 %collective-permute-done.20 = f32[128,256]{1,0:T(8,128)S(1)} collective-permute-done((f32[128,256]{1,0:T(8,128)S(1)}, f32[128,256]{1,0:T(8,128)S(1)}, u32[]{:S(2)}, u32[]{:S(2)}) %collective-permute-start.20) | collective-permute-done | bytes 131104 | tf_op jit(solution)/shard_map/ppermute | solution.py:167
  132.4 1.3 collective-permute-start.21
  133.7 5.2 %collective-permute-done.21 = f32[256,256]{1,0:T(8,128)S(1)} collective-permute-done((f32[256,256]{1,0:T(8,128)S(1)}, f32[256,256]{1,0:T(8,128)S(1)}, u32[]{:S(2)}, u32[]{:S(2)}) %collective-permute-start.21) | collective-permute-done | bytes 262176 | tf_op jit(solution)/shard_map/ppermute | solution.py:167
  139.9 1.0 convolution_convert_fusion.1
  (196 shorter events, 24.5 us)
Async XLA Ops:
  0.6 33.8 %copy-start = (bf16[1,1,4,64,512]{4,3,2,1,0:T(8,128)(2,1)S(1)}, bf16[1,1,4,64,512]{4,3,2,1,0:T(8,128)(2,1)}, u32[]{:S(2)}) copy-start(bf16[1,1,4,64,512]{4,3,2,1,0:T(8,128)(2,1)} %param.15) | copy-start | bytes 786436
  0.6 17.8 %copy-start.21 = (s32[1,1,4,2]{2,3,1,0:T(2,128)S(1)}, s32[1,1,4,2]{2,3,1,0:T(2,128)}, u32[]{:S(2)}) copy-start(s32[1,1,4,2]{2,3,1,0:T(2,128)} %param.16) | copy-start | bytes 100
  0.7 10.5 %copy-start.10 = (bf16[16,16,256]{2,1,0:T(8,128)(2,1)S(1)}, bf16[16,16,256]{2,1,0:T(8,128)(2,1)}, u32[]{:S(2)}) copy-start(bf16[16,16,256]{2,1,0:T(8,128)(2,1)} %param.18) | copy-start | bytes 393220
  0.7 10.5 %copy-start.7 = (bf16[256,256]{1,0:T(8,128)(2,1)S(1)}, bf16[256,256]{1,0:T(8,128)(2,1)}, u32[]{:S(2)}) copy-start(bf16[256,256]{1,0:T(8,128)(2,1)} %param.14) | copy-start | bytes 393220
  2.4 19.4 %collective-permute-start.4 = (s32[1,2,8]{2,1,0:T(2,128)S(1)}, s32[1,2,8]{2,1,0:T(2,128)S(1)}, u32[]{:S(2)}, u32[]{:S(2)}) collective-permute-start(s32[1,2,8]{2,1,0:T(2,128)S(1)} %add_bitcast_fusion), channel_id=1, source_target_pairs={{0,4},{4,0},{8,12},{12,8},{16,20},{20,16},{24,28},{28,24},{1,5},{5... | collective-permute-start | bytes 200 | tf_op jit(solution)/shard_map/ppermute | solution.py:167
  6.7 34.7 %collective-permute-start = (bf16[8,16,512]{2,1,0:T(8,128)(2,1)S(1)}, bf16[8,16,512]{2,1,0:T(8,128)(2,1)S(1)}, u32[]{:S(2)}, u32[]{:S(2)}) collective-permute-start(bf16[8,16,512]{2,1,0:T(8,128)(2,1)S(1)} %bitcast.269), channel_id=1, source_target_pairs={{0,4},{4,8},{8,12},{12,16},{16,20},{20,24},{24,28},{1,5},{5,9},{9,... | collective-permute-start | bytes 393224 | tf_op jit(solution)/shard_map/ppermute | solution.py:24
  8.7 32.8 %collective-permute-start.1 = (bf16[8,16,512]{2,1,0:T(8,128)(2,1)S(1)}, bf16[8,16,512]{2,1,0:T(8,128)(2,1)S(1)}, u32[]{:S(2)}, u32[]{:S(2)}) collective-permute-start(bf16[8,16,512]{2,1,0:T(8,128)(2,1)S(1)} %bitcast.268), channel_id=1, source_target_pairs={{4,0},{8,4},{12,8},{16,12},{20,16},{24,20},{28,24},{5,1},{9,5},{13... | collective-permute-start | bytes 393224 | tf_op jit(solution)/shard_map/ppermute | solution.py:27
  11.4 32.8 %collective-permute-start.7 = (bf16[8,16,512]{2,1,0:T(8,128)(2,1)S(1)}, bf16[8,16,512]{2,1,0:T(8,128)(2,1)S(1)}, u32[]{:S(2)}, u32[]{:S(2)}) collective-permute-start(bf16[8,16,512]{2,1,0:T(8,128)(2,1)S(1)} %get-tuple-element.42), channel_id=1, source_target_pairs={{0,4},{4,8},{8,12},{12,16},{16,20},{20,24},{24,28},{1,5},{5,9},{9,... | collective-permute-start | bytes 393224 | tf_op jit(solution)/shard_map/ppermute | solution.py:24
  17.0 27.2 %collective-permute-start.8 = (bf16[8,16,512]{2,1,0:T(8,128)(2,1)S(1)}, bf16[8,16,512]{2,1,0:T(8,128)(2,1)S(1)}, u32[]{:S(2)}, u32[]{:S(2)}) collective-permute-start(bf16[8,16,512]{2,1,0:T(8,128)(2,1)S(1)} %get-tuple-element.43), channel_id=1, source_target_pairs={{4,0},{8,4},{12,8},{16,12},{20,16},{24,20},{28,24},{5,1},{9,5},{13... | collective-permute-start | bytes 393224 | tf_op jit(solution)/shard_map/ppermute | solution.py:27
  21.8 47.1 %copy-start.8 = (bf16[2,2,64,2,128]{4,3,2,1,0:T(2,128)(2,1)}, bf16[2,2,64,2,128]{4,3,2,1,0:T(2,128)(2,1)S(1)}, u32[]{:S(2)}) copy-start(bf16[2,2,64,2,128]{4,3,2,1,0:T(2,128)(2,1)S(1)} %reshape_reshape.32) | copy-start | bytes 393220
  21.8 6.6 %collective-permute-start.5 = (s32[2,2,8]{2,1,0:T(2,128)S(1)}, s32[2,2,8]{2,1,0:T(2,128)S(1)}, u32[]{:S(2)}, u32[]{:S(2)}) collective-permute-start(s32[2,2,8]{2,1,0:T(2,128)S(1)} %pad_add_fusion.2), channel_id=1, source_target_pairs={{0,8},{4,12},{8,0},{12,4},{16,24},{20,28},{24,16},{28,20},{1,9},{5... | collective-permute-start | bytes 392 | tf_op jit(solution)/shard_map/ppermute | solution.py:167
  28.5 4.7 %collective-permute-start.6 = (s32[4,2,8]{2,1,0:T(2,128)S(1)}, s32[4,2,8]{2,1,0:T(2,128)S(1)}, u32[]{:S(2)}, u32[]{:S(2)}) collective-permute-start(s32[4,2,8]{2,1,0:T(2,128)S(1)} %pad_add_fusion.1), channel_id=1, source_target_pairs={{0,16},{4,20},{8,24},{12,28},{16,0},{20,4},{24,8},{28,12},{1,17},{... | collective-permute-start | bytes 776 | tf_op jit(solution)/shard_map/ppermute | solution.py:167
  36.2 27.5 %all-to-all-start = ((bf16[8,2,64,512]{3,2,1,0:T(8,128)(2,1)}), bf16[8,2,64,512]{3,2,1,0:T(8,128)(2,1)S(1)}, u32[]{:S(2)}, u32[]{:S(2)}) async-start(bf16[8,2,64,512]{3,2,1,0:T(8,128)(2,1)} %broadcast_select_fusion), calls=%async_computation | async-start | bytes 2097152 | tf_op jit(solution)/shard_map/all_to_all | solution.py:224
  41.6 9.5 %collective-permute-start.2 = (bf16[32,8,512]{2,1,0:T(8,128)(2,1)S(1)}, bf16[32,8,512]{2,1,0:T(8,128)(2,1)S(1)}, u32[]{:S(2)}, u32[]{:S(2)}) collective-permute-start(bf16[32,8,512]{2,1,0:T(8,128)(2,1)S(1)} %get-tuple-element.38), channel_id=1, source_target_pairs={{0,1},{1,2},{2,3},{4,5},{5,6},{6,7},{8,9},{9,10},{10,11},{12,13},{... | collective-permute-start | bytes 786440 | tf_op jit(solution)/shard_map/ppermute | solution.py:24
  42.9 8.2 %collective-permute-start.3 = (bf16[32,8,512]{2,1,0:T(8,128)(2,1)S(1)}, bf16[32,8,512]{2,1,0:T(8,128)(2,1)S(1)}, u32[]{:S(2)}, u32[]{:S(2)}) collective-permute-start(bf16[32,8,512]{2,1,0:T(8,128)(2,1)S(1)} %get-tuple-element.39), channel_id=1, source_target_pairs={{1,0},{2,1},{3,2},{5,4},{6,5},{7,6},{9,8},{10,9},{11,10},{13,12},{... | collective-permute-start | bytes 786440 | tf_op jit(solution)/shard_map/ppermute | solution.py:27
  44.3 9.2 %collective-permute-start.10 = (bf16[32,8,512]{2,1,0:T(8,128)(2,1)S(1)}, bf16[32,8,512]{2,1,0:T(8,128)(2,1)S(1)}, u32[]{:S(2)}, u32[]{:S(2)}) collective-permute-start(bf16[32,8,512]{2,1,0:T(8,128)(2,1)S(1)} %get-tuple-element.37), channel_id=1, source_target_pairs={{1,0},{2,1},{3,2},{5,4},{6,5},{7,6},{9,8},{10,9},{11,10},{13,12},{... | collective-permute-start | bytes 786440 | tf_op jit(solution)/shard_map/ppermute | solution.py:27
  45.6 7.9 %collective-permute-start.9 = (bf16[32,8,512]{2,1,0:T(8,128)(2,1)S(1)}, bf16[32,8,512]{2,1,0:T(8,128)(2,1)S(1)}, u32[]{:S(2)}, u32[]{:S(2)}) collective-permute-start(bf16[32,8,512]{2,1,0:T(8,128)(2,1)S(1)} %get-tuple-element.36), channel_id=1, source_target_pairs={{0,1},{1,2},{2,3},{4,5},{5,6},{6,7},{8,9},{9,10},{10,11},{12,13},{... | collective-permute-start | bytes 786440 | tf_op jit(solution)/shard_map/ppermute | solution.py:24
  54.0 4.5 %copy-start.3 = (bf16[2,2,576,256]{3,2,1,0:T(8,128)(2,1)}, bf16[2,2,576,256]{3,2,1,0:T(8,128)(2,1)S(1)}, u32[]{:S(2)}) copy-start(bf16[2,2,576,256]{3,2,1,0:T(8,128)(2,1)S(1)} %get-tuple-element.13) | copy-start | bytes 3538948
  54.0 4.5 %copy-start.19 = (bf16[2,2,576,256]{3,2,1,0:T(8,128)(2,1)}, bf16[2,2,576,256]{3,2,1,0:T(8,128)(2,1)S(1)}, u32[]{:S(2)}) copy-start(bf16[2,2,576,256]{3,2,1,0:T(8,128)(2,1)S(1)} %get-tuple-element.12) | copy-start | bytes 3538948
  65.3 2.3 %copy-start.14 = (bf16[2,2,64,2,128]{4,3,2,1,0:T(2,128)(2,1)S(1)}, bf16[2,2,64,2,128]{4,3,2,1,0:T(2,128)(2,1)}, u32[]{:S(2)}) copy-start(bf16[2,2,64,2,128]{4,3,2,1,0:T(2,128)(2,1)} %reshape_reshape.29) | copy-start | bytes 393220
  67.6 1.3 copy-start.1
  70.1 7.2 %copy-start.2 = (bf16[16,16,256]{2,1,0:T(8,128)(2,1)S(1)}, bf16[16,16,256]{2,1,0:T(8,128)(2,1)}, u32[]{:S(2)}) copy-start(bf16[16,16,256]{2,1,0:T(8,128)(2,1)} %param.10) | copy-start | bytes 393220
  73.2 5.1 %copy-start.9 = (bf16[2,2,64,2,128]{4,2,3,1,0:T(8,128)(2,1)S(1)}, bf16[2,2,64,2,128]{4,2,3,1,0:T(8,128)(2,1)}, u32[]{:S(2)}) copy-start(bf16[2,2,64,2,128]{4,2,3,1,0:T(8,128)(2,1)} %get-tuple-element.86) | copy-start | bytes 393220
  73.2 12.4 %copy-start.11 = (bf16[16,16,256]{2,1,0:T(8,128)(2,1)S(1)}, bf16[16,16,256]{2,1,0:T(8,128)(2,1)}, u32[]{:S(2)}) copy-start(bf16[16,16,256]{2,1,0:T(8,128)(2,1)} %param.18) | copy-start | bytes 393220
  74.4 3.9 %copy-start.12 = (bf16[2,8,2,8,256]{4,3,2,1,0:T(8,128)(2,1)}, bf16[2,8,2,8,256]{4,3,2,1,0:T(8,128)(2,1)S(1)}, u32[]{:S(2)}) copy-start(bf16[2,8,2,8,256]{4,3,2,1,0:T(8,128)(2,1)S(1)} %copy.133) | copy-start | bytes 393220
  74.7 3.8 %collective-permute-start.11 = (f32[16,8,4]{1,0,2:T(8,128)S(1)}, f32[16,8,4]{1,0,2:T(8,128)S(1)}, u32[]{:S(2)}, u32[]{:S(2)}) collective-permute-start(f32[16,8,4]{1,0,2:T(8,128)S(1)} %get-tuple-element.66), channel_id=1, source_target_pairs={{0,1},{1,2},{2,3},{4,5},{5,6},{6,7},{8,9},{9,10},{10,11},{12,13},{... | collective-permute-start | bytes 6152 | tf_op jit(solution)/shard_map/ppermute | solution.py:24
  76.0 4.9 %collective-permute-start.12 = (f32[16,8,4]{1,0,2:T(8,128)S(1)}, f32[16,8,4]{1,0,2:T(8,128)S(1)}, u32[]{:S(2)}, u32[]{:S(2)}) collective-permute-start(f32[16,8,4]{1,0,2:T(8,128)S(1)} %get-tuple-element.67), channel_id=1, source_target_pairs={{1,0},{2,1},{3,2},{5,4},{6,5},{7,6},{9,8},{10,9},{11,10},{13,12},{... | collective-permute-start | bytes 6152 | tf_op jit(solution)/shard_map/ppermute | solution.py:27
  78.4 11.9 %copy-start.20 = (pred[2,2,576]{2,1,0:T(4,128)(4,1)S(1)}, pred[2,2,576]{2,1,0:T(4,128)(4,1)}, u32[]{:S(2)}) copy-start(pred[2,2,576]{2,1,0:T(4,128)(4,1)} %concatenate.86) | copy-start | bytes 6916
  81.0 5.5 %collective-permute-start.13 = (f32[8,32,4]{1,0,2:T(8,128)S(1)}, f32[8,32,4]{1,0,2:T(8,128)S(1)}, u32[]{:S(2)}, u32[]{:S(2)}) collective-permute-start(f32[8,32,4]{1,0,2:T(8,128)S(1)} %get-tuple-element.64), channel_id=1, source_target_pairs={{0,4},{4,8},{8,12},{12,16},{16,20},{20,24},{24,28},{1,5},{5,9},{9,... | collective-permute-start | bytes 12296 | tf_op jit(solution)/shard_map/ppermute | solution.py:24
  84.1 5.6 %collective-permute-start.14 = (f32[8,32,4]{1,0,2:T(8,128)S(1)}, f32[8,32,4]{1,0,2:T(8,128)S(1)}, u32[]{:S(2)}, u32[]{:S(2)}) collective-permute-start(f32[8,32,4]{1,0,2:T(8,128)S(1)} %get-tuple-element.65), channel_id=1, source_target_pairs={{4,0},{8,4},{12,8},{16,12},{20,16},{24,20},{28,24},{5,1},{9,5},{13... | collective-permute-start | bytes 12296 | tf_op jit(solution)/shard_map/ppermute | solution.py:27
  90.3 1.9 %copy-start.4 = (bf16[2,2,576,256]{3,2,1,0:T(8,128)(2,1)S(1)}, bf16[2,2,576,256]{3,2,1,0:T(8,128)(2,1)}, u32[]{:S(2)}) copy-start(bf16[2,2,576,256]{3,2,1,0:T(8,128)(2,1)} %copy-done.3) | copy-start | bytes 3538948
  92.2 0.9 copy-start.18
  95.8 1.9 %copy-start.5 = (f32[256,256]{1,0:T(8,128)S(1)}, f32[256,256]{1,0:T(8,128)}, u32[]{:S(2)}) copy-start(f32[256,256]{1,0:T(8,128)} %convolution_bitcast_fusion.2) | copy-start | bytes 786436
  95.8 1.9 %copy-start.6 = (f32[256,256]{1,0:T(8,128)S(1)}, f32[256,256]{1,0:T(8,128)}, u32[]{:S(2)}) copy-start(f32[256,256]{1,0:T(8,128)} %fusion.116) | copy-start | bytes 786436
  97.9 2.8 %collective-permute-start.15 = (f32[512,256]{1,0:T(8,128)S(1)}, f32[512,256]{1,0:T(8,128)S(1)}, u32[]{:S(2)}, u32[]{:S(2)}) collective-permute-start(f32[512,256]{1,0:T(8,128)S(1)} %constant_dynamic-slice_fusion.1), channel_id=1, source_target_pairs={{0,1},{1,0},{2,3},{3,2},{4,5},{5,4},{6,7},{7,6},{8,9},{9,8},{10,11... | collective-permute-start | bytes 1572872 | tf_op jit(solution)/shard_map/ppermute | solution.py:197
  100.8 8.7 %collective-permute-start.16 = (f32[256,256]{1,0:T(8,128)S(1)}, f32[256,256]{1,0:T(8,128)S(1)}, u32[]{:S(2)}, u32[]{:S(2)}) collective-permute-start(f32[256,256]{1,0:T(8,128)S(1)} %constant_dynamic-slice_fusion), channel_id=1, source_target_pairs={{0,2},{1,3},{2,0},{3,1},{4,6},{5,7},{6,4},{7,5},{8,10},{9,11},{10,... | collective-permute-start | bytes 786440 | tf_op jit(solution)/shard_map/ppermute | solution.py:197
  109.5 5.3 %collective-permute-start.17 = (f32[128,256]{1,0:T(8,128)S(1)}, f32[128,256]{1,0:T(8,128)S(1)}, u32[]{:S(2)}, u32[]{:S(2)}) collective-permute-start(f32[128,256]{1,0:T(8,128)S(1)} %constant_dynamic-slice_fusion.2), channel_id=1, source_target_pairs={{0,4},{4,0},{8,12},{12,8},{16,20},{20,16},{24,28},{28,24},{1,5},{5... | collective-permute-start | bytes 393224 | tf_op jit(solution)/shard_map/ppermute | solution.py:197
  114.8 5.0 %collective-permute-start.18 = (f32[128,256]{1,0:T(8,128)S(1)}, f32[128,256]{1,0:T(8,128)S(1)}, u32[]{:S(2)}, u32[]{:S(2)}) collective-permute-start(f32[128,256]{1,0:T(8,128)S(1)} %dynamic-slice_add_fusion.2), channel_id=1, source_target_pairs={{0,8},{4,12},{8,0},{12,4},{16,24},{20,28},{24,16},{28,20},{1,9},{5... | collective-permute-start | bytes 393224 | tf_op jit(solution)/shard_map/ppermute | solution.py:200
  119.9 7.3 %collective-permute-start.19 = (f32[128,256]{1,0:T(8,128)S(1)}, f32[128,256]{1,0:T(8,128)S(1)}, u32[]{:S(2)}, u32[]{:S(2)}) collective-permute-start(f32[128,256]{1,0:T(8,128)S(1)} %add.165), channel_id=1, source_target_pairs={{0,16},{4,20},{8,24},{12,28},{16,0},{20,4},{24,8},{28,12},{1,17},{... | collective-permute-start | bytes 393224 | tf_op jit(solution)/shard_map/ppermute | solution.py:200
  127.2 5.0 %collective-permute-start.20 = (f32[128,256]{1,0:T(8,128)S(1)}, f32[128,256]{1,0:T(8,128)S(1)}, u32[]{:S(2)}, u32[]{:S(2)}) collective-permute-start(f32[128,256]{1,0:T(8,128)S(1)} %add.166), channel_id=1, source_target_pairs={{0,4},{4,0},{8,12},{12,8},{16,20},{20,16},{24,28},{28,24},{1,5},{5... | collective-permute-start | bytes 393224 | tf_op jit(solution)/shard_map/ppermute | solution.py:167
  132.3 7.5 %copy-start.13 = (bf16[2,8,2,8,256]{4,3,2,1,0:T(8,128)(2,1)S(1)}, bf16[2,8,2,8,256]{4,3,2,1,0:T(8,128)(2,1)}, u32[]{:S(2)}) copy-start(bf16[2,8,2,8,256]{4,3,2,1,0:T(8,128)(2,1)} %copy-done.12) | copy-start | bytes 393220
  132.3 7.5 %copy-start.15 = (bf16[256,256]{1,0:T(8,128)(2,1)S(1)}, bf16[256,256]{1,0:T(8,128)(2,1)}, u32[]{:S(2)}) copy-start(bf16[256,256]{1,0:T(8,128)(2,1)} %param.13) | copy-start | bytes 393220
  132.3 7.5 %copy-start.16 = (bf16[256,256]{1,0:T(8,128)(2,1)S(1)}, bf16[256,256]{1,0:T(8,128)(2,1)}, u32[]{:S(2)}) copy-start(bf16[256,256]{1,0:T(8,128)(2,1)} %param.12) | copy-start | bytes 393220
  132.3 7.5 %copy-start.17 = (bf16[256,256]{1,0:T(8,128)(2,1)S(1)}, bf16[256,256]{1,0:T(8,128)(2,1)}, u32[]{:S(2)}) copy-start(bf16[256,256]{1,0:T(8,128)(2,1)} %param.11) | copy-start | bytes 393220
  132.4 6.4 %collective-permute-start.21 = (f32[256,256]{1,0:T(8,128)S(1)}, f32[256,256]{1,0:T(8,128)S(1)}, u32[]{:S(2)}, u32[]{:S(2)}) collective-permute-start(f32[256,256]{1,0:T(8,128)S(1)} %pad_maximum_fusion.6), channel_id=1, source_target_pairs={{0,2},{1,3},{2,0},{3,1},{4,6},{5,7},{6,4},{7,5},{8,10},{9,11},{10,... | collective-permute-start | bytes 786440 | tf_op jit(solution)/shard_map/ppermute | solution.py:167
  138.9 2.0 %collective-permute-start.22 = (f32[512,256]{1,0:T(8,128)S(1)}, f32[512,256]{1,0:T(8,128)S(1)}, u32[]{:S(2)}, u32[]{:S(2)}) collective-permute-start(f32[512,256]{1,0:T(8,128)S(1)} %pad_maximum_fusion.5), channel_id=1, source_target_pairs={{0,1},{1,0},{2,3},{3,2},{4,5},{5,4},{6,7},{7,6},{8,9},{9,8},{10,11... | collective-permute-start | bytes 1572872 | tf_op jit(solution)/shard_map/ppermute | solution.py:167
